TPU v7x, 32 devices: a whole 2x2x4 slice. The times are simulated.
32 devices in a mesh: group: 2 (over x), tm: 16 (over z, y, core).
Axes of the slice: x: 2, y: 2, z: 4, core: 2. Of those that a mesh axis runs over, the one named last changes fastest.
Arguments:
- queries: bfloat16 [4096, 2560], P(('group', 'tm')), parts along dimension 0, may hold values from -120 to 120
- keys: bfloat16 [4096, 2560], P(('group', 'tm')), parts along dimension 0, may hold values from -6 to 6
- values: bfloat16 [4096, 2560], P(('group', 'tm')), parts along dimension 0, may hold values from -6 to 6
- out_grad: bfloat16 [4096, 2560], P(('group', 'tm')), parts along dimension 0, may hold values from -6 to 6
- frame_keep: int32 [8, 3], P('group'), parts along dimension 0, may hold values from 0 to 1, as said below
- band_window: int32 [8], P('group'), parts along dimension 0, may hold values from 65 to 128
Outputs:
- query_grad: bfloat16 [4096, 2560], P(('group', 'tm')), parts along dimension 0
- key_grad: bfloat16 [4096, 2560], P(('group', 'tm')), parts along dimension 0
- value_grad: bfloat16 [4096, 2560], P(('group', 'tm')), parts along dimension 0
There are 2 independent parts, one for each index of `group`. A program takes and returns all parts, laid end to end along the dimension named above; each array names one. Nothing has to cross between parts.
Inputs may be any that keep to these rules, and one draw needn't show every extreme that they name: Every query frame attends its own frame: frame_keep[t, 1] = 1 for every t.
All inputs are finite; a program needn't handle non-finite values.
Results may differ from a plain program's by a relative error of at most 0.01.
Values may be sent and summed in bfloat16 or wider, within the bound.
No kernel may reach another device: no remote copies, remote signals or barrier semaphores. Data moves between devices by JAX's collectives and lax.ppermute only.
A program may use at most 128 MiB of HBM per device.

v0:
```python
import math

import jax
import jax.numpy as jnp
from jax import lax
from jax.sharding import PartitionSpec as P

HD = 128
QUARTERS = 4
REACH = 5


def shifted(value, axis, steps):
    count = lax.axis_size(axis)
    leading, last = (max(0, -steps), min(count, count - steps))
    return lax.ppermute(value, axis, [(source, source + steps) for source in range(leading, last)])


def allowed(query_rows, key_rows, frame_keep, band_window, frame_len):
    frame_count = frame_keep.shape[0]
    query_frame = jnp.floor_divide(query_rows, frame_len)
    key_frame = jnp.floor_divide(key_rows, frame_len)
    query_place = query_rows - query_frame * frame_len
    key_place = key_rows - key_frame * frame_len
    query_inside = (query_rows >= 0) & (query_rows < frame_count * frame_len)
    key_inside = (key_rows >= 0) & (key_rows < frame_count * frame_len)
    inside = query_inside[:, None] & key_inside[None, :]
    onehot = (query_frame[:, None] == jnp.arange(frame_count, dtype=jnp.int32)[None, :]).astype(
        jnp.int32
    )
    keep_rows = jnp.sum(onehot[:, :, None] * frame_keep[None, :, :], axis=1)
    window_rows = jnp.sum(onehot * band_window[None, :], axis=1)
    frame_gap = key_frame[None, :] - query_frame[:, None]
    kept_pair = jnp.zeros(frame_gap.shape, jnp.int32)
    for column in range(3):
        kept_pair = kept_pair + jnp.where(
            frame_gap == column - 1, keep_rows[:, column : column + 1], 0
        )
    place_gap = jnp.abs(query_place[:, None] - key_place[None, :])
    nearby = (frame_gap == 0) | (place_gap <= window_rows[:, None])
    return inside & (kept_pair > 0) & nearby


def relay_blocks(block, advance):
    gathered = {0: block}
    for course in (1, -1):
        carried = block
        for offset in range(1, REACH + 1):
            carried = advance(carried, -course)
            gathered[course * offset] = carried
    return [gathered[offset] for offset in range(-REACH, REACH + 1)]


def spread_keys(stacked):

    def advance(tensor, amount):
        return shifted(tensor, "tm", amount)

    return relay_blocks(stacked, advance)


def return_partial(tensor, amount):
    return shifted(tensor, "tm", amount)


def body(queries, keys, values, out_grad, frame_keep, band_window):
    rows_own, channel_total = queries.shape
    head_total = channel_total // HD
    group_heads = 4
    group_width = group_heads * HD
    frame_len = QUARTERS * rows_own
    block_count = 2 * REACH + 1
    inv_root = 1.0 / math.sqrt(HD)
    device = lax.axis_index("tm")
    own_rows = device * rows_own + jnp.arange(rows_own, dtype=jnp.int32)
    far_rows = (device - REACH) * rows_own + jnp.arange(block_count * rows_own, dtype=jnp.int32)
    key_blocks = spread_keys(jnp.stack([keys, values]))
    key_all = jnp.concatenate([member[0] for member in key_blocks])
    value_all = jnp.concatenate([member[1] for member in key_blocks])
    forward_mask = allowed(own_rows, far_rows, frame_keep, band_window, frame_len)
    query_parts = []
    key_parts = []
    value_parts = []
    for group_index in range(head_total // group_heads):
        lower = group_index * group_width
        upper = lower + group_width
        query_heads = queries[:, lower:upper].reshape(rows_own, group_heads, HD)
        grad_heads = out_grad[:, lower:upper].reshape(rows_own, group_heads, HD)
        key_heads = key_all[:, lower:upper].reshape(-1, group_heads, HD)
        value_heads = value_all[:, lower:upper].reshape(-1, group_heads, HD)
        scores = (
            jnp.einsum("qhd,khd->hqk", query_heads, key_heads, preferred_element_type=jnp.float32)
            * inv_root
        )
        masked = jnp.where(forward_mask[None], scores, -1e30)
        highest = jnp.max(masked, axis=2, keepdims=True)
        total_mass = jnp.sum(jnp.exp(masked - highest), axis=2, keepdims=True)
        log_total = highest + jnp.log(total_mass)
        attn_prob = jnp.exp(masked - log_total)
        prob_low = attn_prob.astype(jnp.bfloat16)
        attended = jnp.einsum(
            "hqk,khd->qhd", prob_low, value_heads, preferred_element_type=jnp.float32
        )
        delta_sum = jnp.sum(grad_heads.astype(jnp.float32) * attended, axis=2)
        prob_grad = jnp.einsum(
            "qhd,khd->hqk", grad_heads, value_heads, preferred_element_type=jnp.float32
        )
        score_grad = (attn_prob * (prob_grad - delta_sum.T[:, :, None])).astype(jnp.bfloat16)
        query_part = (
            jnp.einsum("hqk,khd->qhd", score_grad, key_heads, preferred_element_type=jnp.float32)
            * inv_root
        )
        query_parts.append(query_part.reshape(rows_own, group_width))
        key_part = (
            jnp.einsum("hqk,qhd->khd", score_grad, query_heads, preferred_element_type=jnp.float32)
            * inv_root
        )
        value_part = jnp.einsum(
            "hqk,qhd->khd", prob_low, grad_heads, preferred_element_type=jnp.float32
        )
        key_parts.append(key_part.reshape(-1, group_width).astype(jnp.bfloat16))
        value_parts.append(value_part.reshape(-1, group_width).astype(jnp.bfloat16))
    query_grad = jnp.concatenate(query_parts, axis=1).astype(jnp.bfloat16)
    partials = jnp.stack([jnp.concatenate(key_parts, axis=1), jnp.concatenate(value_parts, axis=1)])
    summed = partials[:, REACH * rows_own : (REACH + 1) * rows_own].astype(jnp.float32)
    for position in range(block_count):
        amount = position - REACH
        if amount != 0:
            section = partials[:, position * rows_own : (position + 1) * rows_own]
            summed = summed + return_partial(section, amount).astype(jnp.float32)
    key_grad = summed[0].astype(jnp.bfloat16)
    value_grad = summed[1].astype(jnp.bfloat16)
    return (query_grad, key_grad, value_grad)


def solution(mesh):
    placed = (
        P(("group", "tm"), None),
        P(("group", "tm"), None),
        P(("group", "tm"), None),
        P(("group", "tm"), None),
        P("group", None),
        P("group"),
    )
    return jax.shard_map(
        body,
        mesh=mesh,
        in_specs=placed,
        out_specs=(P(("group", "tm"), None), P(("group", "tm"), None), P(("group", "tm"), None)),
        check_vma=False,
    )
```

profile of v0, /device:TPU:7, one launch (start us, length us, event | category | flops | bytes accessed | tf_op | source)
XLA Modules:
  0.0 463.4 jit_solution(6017277781914965745)
XLA Ops:
  3.7 3.7 collective-permute-start
  7.4 1.9 collective-permute-start.5
  9.3 12.6 %collective-permute-done = bf16[2,128,2560]{1,2,0:T(8,128)(2,1)S(1)} collective-permute-done((bf16[2,128,2560]{1,2,0:T(8,128)(2,1)S(1)}, bf16[2,128,2560]{1,2,0:T(8,128)(2,1)S(1)}, u32[]{:S(2)}, u32[]{:S(2)}) %collective-permute-start) | collective-permute-done | bytes 1310752 | tf_op jit(solution)/shard_map/ppermute | solution.py:16
  22.0 5.3 %collective-permute-start.1 = (bf16[2,128,2560]{1,2,0:T(8,128)(2,1)S(1)}, bf16[2,128,2560]{1,2,0:T(8,128)(2,1)S(1)}, u32[]{:S(2)}, u32[]{:S(2)}) collective-permute-start(bf16[2,128,2560]{1,2,0:T(8,128)(2,1)S(1)} %collective-permute-done), channel_id=1, source_target_pairs={{0,1},{1,2},{2,3},{3,4},{4,5},{5,6},{6,7},{7,8},{8,9},{9,10},{10,1... | collective-permute-start | bytes 3932168 | tf_op jit(solution)/shard_map/ppermute | solution.py:16
  27.3 13.8 %collective-permute-start.6 = (bf16[2,128,2560]{1,2,0:T(8,128)(2,1)S(1)}, bf16[2,128,2560]{1,2,0:T(8,128)(2,1)}, u32[]{:S(2)}, u32[]{:S(2)}) collective-permute-start(bf16[2,128,2560]{1,2,0:T(8,128)(2,1)S(1)} %collective-permute-done.5), channel_id=1, source_target_pairs={{1,0},{2,1},{3,2},{4,3},{5,4},{6,5},{7,6},{8,7},{9,8},{10,9},{11,1... | collective-permute-start | bytes 3932168 | tf_op jit(solution)/shard_map/ppermute | solution.py:16
  41.9 5.3 %collective-permute-start.2 = (bf16[2,128,2560]{1,2,0:T(8,128)(2,1)S(1)}, bf16[2,128,2560]{1,2,0:T(8,128)(2,1)}, u32[]{:S(2)}, u32[]{:S(2)}) collective-permute-start(bf16[2,128,2560]{1,2,0:T(8,128)(2,1)S(1)} %collective-permute-done.1), channel_id=1, source_target_pairs={{0,1},{1,2},{2,3},{3,4},{4,5},{5,6},{6,7},{7,8},{8,9},{9,10},{10,1... | collective-permute-start | bytes 3932168 | tf_op jit(solution)/shard_map/ppermute | solution.py:16
  47.2 9.7 %collective-permute-done.6 = bf16[2,128,2560]{1,2,0:T(8,128)(2,1)} collective-permute-done((bf16[2,128,2560]{1,2,0:T(8,128)(2,1)S(1)}, bf16[2,128,2560]{1,2,0:T(8,128)(2,1)}, u32[]{:S(2)}, u32[]{:S(2)}) %collective-permute-start.6) | collective-permute-done | bytes 1310752 | tf_op jit(solution)/shard_map/ppermute | solution.py:16
  56.9 17.2 %collective-permute-start.7 = (bf16[2,128,2560]{1,2,0:T(8,128)(2,1)}, bf16[2,128,2560]{1,2,0:T(8,128)(2,1)}, u32[]{:S(2)}, u32[]{:S(2)}) collective-permute-start(bf16[2,128,2560]{1,2,0:T(8,128)(2,1)} %collective-permute-done.6), channel_id=1, source_target_pairs={{1,0},{2,1},{3,2},{4,3},{5,4},{6,5},{7,6},{8,7},{9,8},{10,9},{11,1... | collective-permute-start | bytes 3932168 | tf_op jit(solution)/shard_map/ppermute | solution.py:16
  74.8 1.9 collective-permute-start.3
  77.7 1.9 fusion.111
  85.0 1.7 copy.265
  86.7 2.7 collective-permute-done.7
  89.4 27.7 %collective-permute-start.8 = (bf16[2,128,2560]{1,2,0:T(8,128)(2,1)}, bf16[2,128,2560]{1,2,0:T(8,128)(2,1)S(1)}, u32[]{:S(2)}, u32[]{:S(2)}) collective-permute-start(bf16[2,128,2560]{1,2,0:T(8,128)(2,1)} %collective-permute-done.7), channel_id=1, source_target_pairs={{1,0},{2,1},{3,2},{4,3},{5,4},{6,5},{7,6},{8,7},{9,8},{10,9},{11,1... | collective-permute-start | bytes 3932168 | tf_op jit(solution)/shard_map/ppermute | solution.py:16
  117.2 1.9 collective-permute-start.4
  120.5 11.1 %collective-permute-done.8 = bf16[2,128,2560]{1,2,0:T(8,128)(2,1)S(1)} collective-permute-done((bf16[2,128,2560]{1,2,0:T(8,128)(2,1)}, bf16[2,128,2560]{1,2,0:T(8,128)(2,1)S(1)}, u32[]{:S(2)}, u32[]{:S(2)}) %collective-permute-start.8) | collective-permute-done | bytes 1310752 | tf_op jit(solution)/shard_map/ppermute | solution.py:16
  131.6 10.4 %collective-permute-start.9 = (bf16[2,128,2560]{1,2,0:T(8,128)(2,1)S(1)}, bf16[2,128,2560]{1,2,0:T(8,128)(2,1)S(1)}, u32[]{:S(2)}, u32[]{:S(2)}) collective-permute-start(bf16[2,128,2560]{1,2,0:T(8,128)(2,1)S(1)} %collective-permute-done.8), channel_id=1, source_target_pairs={{1,0},{2,1},{3,2},{4,3},{5,4},{6,5},{7,6},{8,7},{9,8},{10,9},{11,1... | collective-permute-start | bytes 3932168 | tf_op jit(solution)/shard_map/ppermute | solution.py:16
  142.3 1.7 fusion.80
  144.0 1.7 fusion.79
  147.0 1.6 fusion.75
  148.6 1.6 fusion.74
  150.5 4.9 %collective-permute-done.9 = bf16[2,128,2560]{1,2,0:T(8,128)(2,1)S(1)} collective-permute-done((bf16[2,128,2560]{1,2,0:T(8,128)(2,1)S(1)}, bf16[2,128,2560]{1,2,0:T(8,128)(2,1)S(1)}, u32[]{:S(2)}, u32[]{:S(2)}) %collective-permute-start.9) | collective-permute-done | bytes 1310752 | tf_op jit(solution)/shard_map/ppermute | solution.py:16
  155.7 2.9 copy-done.13
  158.6 3.6 fusion.110
  164.7 1.7 convolution_convert_fusion.4
  169.2 1.8 convolution_convert_fusion.3
  171.6 2.1 fusion.23
  175.2 1.7 convolution_convert_fusion.2
  177.6 2.0 fusion.22
  180.9 1.7 convolution_convert_fusion.1
  183.3 2.1 fusion.21
  186.6 1.7 convolution_convert_fusion
  189.0 2.1 fusion.20
  191.1 1.7 fusion.34
  192.8 2.8 copy.192
  195.6 2.8 constant_dynamic-update-slice_fusion.11
  198.4 1.7 fusion.33
  200.1 2.5 copy.195
  202.6 3.0 fusion.32
  205.7 2.5 copy.198
  208.2 3.0 fusion.31
  211.2 2.5 copy.201
  213.7 3.0 fusion.30
  216.7 2.5 copy.204
  219.3 1.6 constant_dynamic-update-slice_fusion.16
  228.2 3.8 copy-done
  232.0 4.7 %fusion.42 = (bf16[2,128,2560]{1,2,0:T(8,128)(2,1)}, bf16[2,128,2560]{1,2,0:T(8,128)(2,1)}, bf16[2,128,2560]{1,2,0:T(8,128)(2,1)}, bf16[2,128,2560]{1,2,0:T(8,12...) fusion(bf16[1,1408,2560]{1,2,0:T(8,128)(2,1)S(1)} %bitcast.295,, ...), kind=kLoop, calls=%fused_computation.96 | loop fusion | flops 23592960 | bytes 26214400 | tf_op jit(solution)/shard_map/stack | solution.py:124
  236.7 18.2 %collective-permute-start.19 = (bf16[2,128,2560]{1,2,0:T(8,128)(2,1)S(1)}, bf16[2,128,2560]{1,2,0:T(8,128)(2,1)S(1)}, u32[]{:S(2)}, u32[]{:S(2)}) collective-permute-start(bf16[2,128,2560]{1,2,0:T(8,128)(2,1)S(1)} %get-tuple-element.17), channel_id=1, source_target_pairs={{0,5},{1,6},{2,7},{3,8},{4,9},{5,10},{6,11},{7,12},{8,13},{9,14},{... | collective-permute-start | bytes 3932168 | tf_op jit(solution)/shard_map/ppermute | solution.py:16
  255.1 2.6 collective-permute-start.18
  257.7 10.1 %collective-permute-start.17 = (bf16[2,128,2560]{1,2,0:T(8,128)(2,1)S(1)}, bf16[2,128,2560]{1,2,0:T(8,128)(2,1)S(1)}, u32[]{:S(2)}, u32[]{:S(2)}) collective-permute-start(bf16[2,128,2560]{1,2,0:T(8,128)(2,1)S(1)} %get-tuple-element.16), channel_id=1, source_target_pairs={{0,3},{1,4},{2,5},{3,6},{4,7},{5,8},{6,9},{7,10},{8,11},{9,12},{10... | collective-permute-start | bytes 3932168 | tf_op jit(solution)/shard_map/ppermute | solution.py:16
  267.8 2.5 collective-permute-start.16
  270.4 3.0 collective-permute-start.15
  274.5 2.5 collective-permute-done.19
  277.0 15.2 %collective-permute-start.14 = (bf16[2,128,2560]{1,2,0:T(8,128)(2,1)}, bf16[2,128,2560]{1,2,0:T(8,128)(2,1)}, u32[]{:S(2)}, u32[]{:S(2)}) collective-permute-start(bf16[2,128,2560]{1,2,0:T(8,128)(2,1)} %get-tuple-element.13), channel_id=1, source_target_pairs={{1,0},{2,1},{3,2},{4,3},{5,4},{6,5},{7,6},{8,7},{9,8},{10,9},{11,1... | collective-permute-start | bytes 3932168 | tf_op jit(solution)/shard_map/ppermute | solution.py:16
  292.1 12.9 %collective-permute-done.18 = bf16[2,128,2560]{1,2,0:T(8,128)(2,1)S(1)} collective-permute-done((bf16[2,128,2560]{1,2,0:T(8,128)(2,1)S(1)}, bf16[2,128,2560]{1,2,0:T(8,128)(2,1)S(1)}, u32[]{:S(2)}, u32[]{:S(2)}) %collective-permute-start.18) | collective-permute-done | bytes 1310752 | tf_op jit(solution)/shard_map/ppermute | solution.py:16
  305.1 7.4 %collective-permute-start.13 = (bf16[2,128,2560]{1,2,0:T(8,128)(2,1)}, bf16[2,128,2560]{1,2,0:T(8,128)(2,1)}, u32[]{:S(2)}, u32[]{:S(2)}) collective-permute-start(bf16[2,128,2560]{1,2,0:T(8,128)(2,1)} %get-tuple-element.12), channel_id=1, source_target_pairs={{2,0},{3,1},{4,2},{5,3},{6,4},{7,5},{8,6},{9,7},{10,8},{11,9},{12,... | collective-permute-start | bytes 3932168 | tf_op jit(solution)/shard_map/ppermute | solution.py:16
  312.4 20.7 %collective-permute-done.17 = bf16[2,128,2560]{1,2,0:T(8,128)(2,1)S(1)} collective-permute-done((bf16[2,128,2560]{1,2,0:T(8,128)(2,1)S(1)}, bf16[2,128,2560]{1,2,0:T(8,128)(2,1)S(1)}, u32[]{:S(2)}, u32[]{:S(2)}) %collective-permute-start.17) | collective-permute-done | bytes 1310752 | tf_op jit(solution)/shard_map/ppermute | solution.py:16
  333.1 1.9 collective-permute-start.12
  335.1 26.2 %collective-permute-done.16 = bf16[2,128,2560]{1,2,0:T(8,128)(2,1)S(1)} collective-permute-done((bf16[2,128,2560]{1,2,0:T(8,128)(2,1)S(1)}, bf16[2,128,2560]{1,2,0:T(8,128)(2,1)S(1)}, u32[]{:S(2)}, u32[]{:S(2)}) %collective-permute-start.16) | collective-permute-done | bytes 1310752 | tf_op jit(solution)/shard_map/ppermute | solution.py:16
  362.6 19.2 %collective-permute-done.15 = bf16[2,128,2560]{1,2,0:T(8,128)(2,1)S(1)} collective-permute-done((bf16[2,128,2560]{1,2,0:T(8,128)(2,1)S(1)}, bf16[2,128,2560]{1,2,0:T(8,128)(2,1)S(1)}, u32[]{:S(2)}, u32[]{:S(2)}) %collective-permute-start.15) | collective-permute-done | bytes 1310752 | tf_op jit(solution)/shard_map/ppermute | solution.py:16
  384.0 1.9 fusion.58
  386.0 2.0 fusion.59
  388.3 10.4 %collective-permute-done.11 = bf16[2,128,2560]{1,2,0:T(8,128)(2,1)} collective-permute-done((bf16[2,128,2560]{1,2,0:T(8,128)(2,1)}, bf16[2,128,2560]{1,2,0:T(8,128)(2,1)}, u32[]{:S(2)}, u32[]{:S(2)}) %collective-permute-start.11) | collective-permute-done | bytes 1310752 | tf_op jit(solution)/shard_map/ppermute | solution.py:16
  398.7 56.2 %collective-permute-done.10 = bf16[2,128,2560]{1,2,0:T(8,128)(2,1)} collective-permute-done((bf16[2,128,2560]{1,2,0:T(8,128)(2,1)}, bf16[2,128,2560]{1,2,0:T(8,128)(2,1)}, u32[]{:S(2)}, u32[]{:S(2)}) %collective-permute-start.10) | collective-permute-done | bytes 1310752 | tf_op jit(solution)/shard_map/ppermute | solution.py:16
  454.9 5.8 %add_convert_fusion = bf16[2,128,2560]{1,2,0:T(8,128)(2,1)S(1)} fusion(bf16[2,128,2560]{1,2,0:T(8,128)(2,1)S(1)} %copy-done.23, bf16[2,128,2560]{1,2,0:T(8,128)(2,1)} %copy-done.24, bf16[2,128,2560]{1,2,0:T(8,128)(2,1)} %copy-done.25, bf16[2,128,2560]{1,2,0:T(8,128)(2,1)} %copy-done.26, bf16[2,128,2560]{1,2,0:T(8,128)(2,1)} %copy-done.27, ...), kind=kLoop, calls=%fused_computation.85 | loop fusion | flops 15073280 | bytes 28835840 | tf_op jit(solution)/shard_map/convert.1
  (173 shorter events, 40.5 us)
Async XLA Ops:
  0.6 76.1 %copy-start.38 = (bf16[128,2560]{1,0:T(8,128)(2,1)S(1)}, bf16[128,2560]{1,0:T(8,128)(2,1)}, u32[]{:S(2)}) copy-start(bf16[128,2560]{1,0:T(8,128)(2,1)} %param.9) | copy-start | bytes 1966084
  3.5 76.8 %copy-start.42 = (s32[4,3]{1,0:T(4,128)S(1)}, s32[4,3]{1,0:T(4,128)}, u32[]{:S(2)}) copy-start(s32[4,3]{1,0:T(4,128)} %param.10) | copy-start | bytes 148
  3.7 18.3 %collective-permute-start = (bf16[2,128,2560]{1,2,0:T(8,128)(2,1)S(1)}, bf16[2,128,2560]{1,2,0:T(8,128)(2,1)S(1)}, u32[]{:S(2)}, u32[]{:S(2)}) collective-permute-start(bf16[2,128,2560]{1,2,0:T(8,128)(2,1)S(1)} %pad_maximum_fusion.1), channel_id=1, source_target_pairs={{0,1},{1,2},{2,3},{3,4},{4,5},{5,6},{6,7},{7,8},{8,9},{9,10},{10,1... | collective-permute-start | bytes 3932168 | tf_op jit(solution)/shard_map/ppermute | solution.py:16
  7.4 19.9 %collective-permute-start.5 = (bf16[2,128,2560]{1,2,0:T(8,128)(2,1)S(1)}, bf16[2,128,2560]{1,2,0:T(8,128)(2,1)S(1)}, u32[]{:S(2)}, u32[]{:S(2)}) collective-permute-start(bf16[2,128,2560]{1,2,0:T(8,128)(2,1)S(1)} %pad_maximum_fusion.1), channel_id=1, source_target_pairs={{1,0},{2,1},{3,2},{4,3},{5,4},{6,5},{7,6},{8,7},{9,8},{10,9},{11,1... | collective-permute-start | bytes 3932168 | tf_op jit(solution)/shard_map/ppermute | solution.py:16
  22.0 35.0 %copy-start.28 = (bf16[2,128,2560]{1,2,0:T(8,128)(2,1)}, bf16[2,128,2560]{1,2,0:T(8,128)(2,1)S(1)}, u32[]{:S(2)}) copy-start(bf16[2,128,2560]{1,2,0:T(8,128)(2,1)S(1)} %collective-permute-done) | copy-start | bytes 3932164
  22.0 19.9 %collective-permute-start.1 = (bf16[2,128,2560]{1,2,0:T(8,128)(2,1)S(1)}, bf16[2,128,2560]{1,2,0:T(8,128)(2,1)S(1)}, u32[]{:S(2)}, u32[]{:S(2)}) collective-permute-start(bf16[2,128,2560]{1,2,0:T(8,128)(2,1)S(1)} %collective-permute-done), channel_id=1, source_target_pairs={{0,1},{1,2},{2,3},{3,4},{4,5},{5,6},{6,7},{7,8},{8,9},{9,10},{10,1... | collective-permute-start | bytes 3932168 | tf_op jit(solution)/shard_map/ppermute | solution.py:16
  27.3 29.6 %collective-permute-start.6 = (bf16[2,128,2560]{1,2,0:T(8,128)(2,1)S(1)}, bf16[2,128,2560]{1,2,0:T(8,128)(2,1)}, u32[]{:S(2)}, u32[]{:S(2)}) collective-permute-start(bf16[2,128,2560]{1,2,0:T(8,128)(2,1)S(1)} %collective-permute-done.5), channel_id=1, source_target_pairs={{1,0},{2,1},{3,2},{4,3},{5,4},{6,5},{7,6},{8,7},{9,8},{10,9},{11,1... | collective-permute-start | bytes 3932168 | tf_op jit(solution)/shard_map/ppermute | solution.py:16
  41.9 32.3 %copy-start.30 = (bf16[2,128,2560]{1,2,0:T(8,128)(2,1)}, bf16[2,128,2560]{1,2,0:T(8,128)(2,1)S(1)}, u32[]{:S(2)}) copy-start(bf16[2,128,2560]{1,2,0:T(8,128)(2,1)S(1)} %collective-permute-done.1) | copy-start | bytes 3932164
  41.9 33.0 %collective-permute-start.2 = (bf16[2,128,2560]{1,2,0:T(8,128)(2,1)S(1)}, bf16[2,128,2560]{1,2,0:T(8,128)(2,1)}, u32[]{:S(2)}, u32[]{:S(2)}) collective-permute-start(bf16[2,128,2560]{1,2,0:T(8,128)(2,1)S(1)} %collective-permute-done.1), channel_id=1, source_target_pairs={{0,1},{1,2},{2,3},{3,4},{4,5},{5,6},{6,7},{7,8},{8,9},{9,10},{10,1... | collective-permute-start | bytes 3932168 | tf_op jit(solution)/shard_map/ppermute | solution.py:16
  56.9 32.5 %collective-permute-start.7 = (bf16[2,128,2560]{1,2,0:T(8,128)(2,1)}, bf16[2,128,2560]{1,2,0:T(8,128)(2,1)}, u32[]{:S(2)}, u32[]{:S(2)}) collective-permute-start(bf16[2,128,2560]{1,2,0:T(8,128)(2,1)} %collective-permute-done.6), channel_id=1, source_target_pairs={{1,0},{2,1},{3,2},{4,3},{5,4},{6,5},{7,6},{8,7},{9,8},{10,9},{11,1... | collective-permute-start | bytes 3932168 | tf_op jit(solution)/shard_map/ppermute | solution.py:16
  74.8 42.3 %collective-permute-start.3 = (bf16[2,128,2560]{1,2,0:T(8,128)(2,1)}, bf16[2,128,2560]{1,2,0:T(8,128)(2,1)}, u32[]{:S(2)}, u32[]{:S(2)}) collective-permute-start(bf16[2,128,2560]{1,2,0:T(8,128)(2,1)} %collective-permute-done.2), channel_id=1, source_target_pairs={{0,1},{1,2},{2,3},{3,4},{4,5},{5,6},{6,7},{7,8},{8,9},{9,10},{10,1... | collective-permute-start | bytes 3932168 | tf_op jit(solution)/shard_map/ppermute | solution.py:16
  76.8 42.4 %copy-start.43 = (s32[4]{0:T(128)S(1)}, s32[4]{0:T(128)}, u32[]{:S(2)}) copy-start(s32[4]{0:T(128)} %param.11) | copy-start | bytes 52
  77.6 6.4 %copy-start.40 = (bf16[128,512]{1,0:T(8,128)(2,1)S(1)}, bf16[128,512]{1,0:T(8,128)(2,1)}, u32[]{:S(2)}) copy-start(bf16[128,512]{1,0:T(8,128)(2,1)} %get-tuple-element.56) | copy-start | bytes 393220
  77.6 7.3 %copy-start.39 = (bf16[128,512]{1,0:T(8,128)(2,1)S(1)}, bf16[128,512]{1,0:T(8,128)(2,1)}, u32[]{:S(2)}) copy-start(bf16[128,512]{1,0:T(8,128)(2,1)} %get-tuple-element.55) | copy-start | bytes 393220
  89.4 42.2 %collective-permute-start.8 = (bf16[2,128,2560]{1,2,0:T(8,128)(2,1)}, bf16[2,128,2560]{1,2,0:T(8,128)(2,1)S(1)}, u32[]{:S(2)}, u32[]{:S(2)}) collective-permute-start(bf16[2,128,2560]{1,2,0:T(8,128)(2,1)} %collective-permute-done.7), channel_id=1, source_target_pairs={{1,0},{2,1},{3,2},{4,3},{5,4},{6,5},{7,6},{8,7},{9,8},{10,9},{11,1... | collective-permute-start | bytes 3932168 | tf_op jit(solution)/shard_map/ppermute | solution.py:16
  117.2 24.9 %collective-permute-start.4 = (bf16[2,128,2560]{1,2,0:T(8,128)(2,1)}, bf16[2,128,2560]{1,2,0:T(8,128)(2,1)S(1)}, u32[]{:S(2)}, u32[]{:S(2)}) collective-permute-start(bf16[2,128,2560]{1,2,0:T(8,128)(2,1)} %collective-permute-done.3), channel_id=1, source_target_pairs={{0,1},{1,2},{2,3},{3,4},{4,5},{5,6},{6,7},{7,8},{8,9},{9,10},{10,1... | collective-permute-start | bytes 3932168 | tf_op jit(solution)/shard_map/ppermute | solution.py:16
  131.6 23.8 %collective-permute-start.9 = (bf16[2,128,2560]{1,2,0:T(8,128)(2,1)S(1)}, bf16[2,128,2560]{1,2,0:T(8,128)(2,1)S(1)}, u32[]{:S(2)}, u32[]{:S(2)}) collective-permute-start(bf16[2,128,2560]{1,2,0:T(8,128)(2,1)S(1)} %collective-permute-done.8), channel_id=1, source_target_pairs={{1,0},{2,1},{3,2},{4,3},{5,4},{6,5},{7,6},{8,7},{9,8},{10,9},{11,1... | collective-permute-start | bytes 3932168 | tf_op jit(solution)/shard_map/ppermute | solution.py:16
  142.3 3.4 copy-start.31
  144.0 2.0 copy-start.29
  155.7 2.9 copy-start.13
  162.3 1.2 copy-start.6
  162.3 5.7 %copy-start.4 = (bf16[1408,512]{0,1:T(8,128)(2,1)}, bf16[1408,512]{0,1:T(8,128)(2,1)S(1)}, u32[]{:S(2)}) copy-start(bf16[1408,512]{0,1:T(8,128)(2,1)S(1)} %get-tuple-element.26) | copy-start | bytes 4325380
  162.3 11.5 %copy-start.2 = (bf16[1408,512]{0,1:T(8,128)(2,1)}, bf16[1408,512]{0,1:T(8,128)(2,1)S(1)}, u32[]{:S(2)}) copy-start(bf16[1408,512]{0,1:T(8,128)(2,1)S(1)} %get-tuple-element.25) | copy-start | bytes 4325380
  162.3 1.1 copy-start.32
  167.0 0.9 copy-start.33
  168.0 23.2 %copy-start.9 = (bf16[4,128,1408]{1,2,0:T(8,128)(2,1)}, bf16[4,128,1408]{1,2,0:T(8,128)(2,1)S(1)}, u32[]{:S(2)}) copy-start(bf16[4,128,1408]{1,2,0:T(8,128)(2,1)S(1)} %fusion.24) | copy-start | bytes 4325380
  171.6 2.1 copy-start.35
  177.6 2.0 copy-start.36
  183.3 2.1 copy-start.37
  192.8 5.5 %copy-start.34 = (bf16[128,512]{0,1:T(8,128)(2,1)S(1)}, bf16[128,512]{0,1:T(8,128)(2,1)}, u32[]{:S(2)}) copy-start(bf16[128,512]{0,1:T(8,128)(2,1)} %copy.259) | copy-start | bytes 393220
  195.6 2.8 copy-start.11
  219.3 1.8 copy-start.14
  219.3 3.0 copy-start.15
  221.1 2.4 copy-start.16
  222.3 2.5 copy-start.17
  223.5 2.5 copy-start.18
  224.8 2.0 copy-start.19
  226.0 1.5 copy-start.20
  226.2 1.7 copy-start.21
  226.8 5.2 %copy-start = (bf16[1408,2560]{0,1:T(8,128)(2,1)S(1)}, bf16[1408,2560]{0,1:T(8,128)(2,1)}, u32[]{:S(2)}) copy-start(bf16[1408,2560]{0,1:T(8,128)(2,1)} %constant_dynamic-update-slice_fusion.7) | copy-start | bytes 21626884
  228.1 26.7 %copy-start.1 = (bf16[1408,2560]{0,1:T(8,128)(2,1)}, bf16[1408,2560]{0,1:T(8,128)(2,1)S(1)}, u32[]{:S(2)}) copy-start(bf16[1408,2560]{0,1:T(8,128)(2,1)S(1)} %constant_dynamic-update-slice_fusion.12) | copy-start | bytes 21626884
  236.7 36.7 %copy-start.7 = (bf16[1408,512]{0,1:T(8,128)(2,1)S(1)}, bf16[1408,512]{0,1:T(8,128)(2,1)}, u32[]{:S(2)}) copy-start(bf16[1408,512]{0,1:T(8,128)(2,1)} %copy-done.6) | copy-start | bytes 4325380
  236.7 36.7 %copy-start.10 = (bf16[4,128,1408]{1,2,0:T(8,128)(2,1)S(1)}, bf16[4,128,1408]{1,2,0:T(8,128)(2,1)}, u32[]{:S(2)}) copy-start(bf16[4,128,1408]{1,2,0:T(8,128)(2,1)} %copy-done.9) | copy-start | bytes 4325380
  236.7 40.3 %collective-permute-start.19 = (bf16[2,128,2560]{1,2,0:T(8,128)(2,1)S(1)}, bf16[2,128,2560]{1,2,0:T(8,128)(2,1)S(1)}, u32[]{:S(2)}, u32[]{:S(2)}) collective-permute-start(bf16[2,128,2560]{1,2,0:T(8,128)(2,1)S(1)} %get-tuple-element.17), channel_id=1, source_target_pairs={{0,5},{1,6},{2,7},{3,8},{4,9},{5,10},{6,11},{7,12},{8,13},{9,14},{... | collective-permute-start | bytes 3932168 | tf_op jit(solution)/shard_map/ppermute | solution.py:16
  255.0 18.9 %copy-start.5 = (bf16[1408,512]{0,1:T(8,128)(2,1)S(1)}, bf16[1408,512]{0,1:T(8,128)(2,1)}, u32[]{:S(2)}) copy-start(bf16[1408,512]{0,1:T(8,128)(2,1)} %copy-done.4) | copy-start | bytes 4325380
  255.1 18.9 %copy-start.12 = (bf16[4,128,1408]{1,2,0:T(8,128)(2,1)S(1)}, bf16[4,128,1408]{1,2,0:T(8,128)(2,1)}, u32[]{:S(2)}) copy-start(bf16[4,128,1408]{1,2,0:T(8,128)(2,1)} %fusion.23) | copy-start | bytes 4325380
  255.1 50.0 %collective-permute-start.18 = (bf16[2,128,2560]{1,2,0:T(8,128)(2,1)S(1)}, bf16[2,128,2560]{1,2,0:T(8,128)(2,1)S(1)}, u32[]{:S(2)}, u32[]{:S(2)}) collective-permute-start(bf16[2,128,2560]{1,2,0:T(8,128)(2,1)S(1)} %fusion.40), channel_id=1, source_target_pairs={{0,4},{1,5},{2,6},{3,7},{4,8},{5,9},{6,10},{7,11},{8,12},{9,13},{1... | collective-permute-start | bytes 3932168 | tf_op jit(solution)/shard_map/ppermute | solution.py:16
  257.7 75.4 %collective-permute-start.17 = (bf16[2,128,2560]{1,2,0:T(8,128)(2,1)S(1)}, bf16[2,128,2560]{1,2,0:T(8,128)(2,1)S(1)}, u32[]{:S(2)}, u32[]{:S(2)}) collective-permute-start(bf16[2,128,2560]{1,2,0:T(8,128)(2,1)S(1)} %get-tuple-element.16), channel_id=1, source_target_pairs={{0,3},{1,4},{2,5},{3,6},{4,7},{5,8},{6,9},{7,10},{8,11},{9,12},{10... | collective-permute-start | bytes 3932168 | tf_op jit(solution)/shard_map/ppermute | solution.py:16
  267.8 93.5 %collective-permute-start.16 = (bf16[2,128,2560]{1,2,0:T(8,128)(2,1)S(1)}, bf16[2,128,2560]{1,2,0:T(8,128)(2,1)S(1)}, u32[]{:S(2)}, u32[]{:S(2)}) collective-permute-start(bf16[2,128,2560]{1,2,0:T(8,128)(2,1)S(1)} %get-tuple-element.15), channel_id=1, source_target_pairs={{0,2},{1,3},{2,4},{3,5},{4,6},{5,7},{6,8},{7,9},{8,10},{9,11},{10,... | collective-permute-start | bytes 3932168 | tf_op jit(solution)/shard_map/ppermute | solution.py:16
  270.3 112.7 %copy-start.3 = (bf16[1408,512]{0,1:T(8,128)(2,1)S(1)}, bf16[1408,512]{0,1:T(8,128)(2,1)}, u32[]{:S(2)}) copy-start(bf16[1408,512]{0,1:T(8,128)(2,1)} %copy-done.2) | copy-start | bytes 4325380
  270.4 112.7 %copy-start.8 = (bf16[4,128,1408]{1,2,0:T(8,128)(2,1)S(1)}, bf16[4,128,1408]{1,2,0:T(8,128)(2,1)}, u32[]{:S(2)}) copy-start(bf16[4,128,1408]{1,2,0:T(8,128)(2,1)} %fusion.22) | copy-start | bytes 4325380
  270.4 111.4 %collective-permute-start.15 = (bf16[2,128,2560]{1,2,0:T(8,128)(2,1)S(1)}, bf16[2,128,2560]{1,2,0:T(8,128)(2,1)S(1)}, u32[]{:S(2)}, u32[]{:S(2)}) collective-permute-start(bf16[2,128,2560]{1,2,0:T(8,128)(2,1)S(1)} %get-tuple-element.14), channel_id=1, source_target_pairs={{0,1},{1,2},{2,3},{3,4},{4,5},{5,6},{6,7},{7,8},{8,9},{9,10},{10,1... | collective-permute-start | bytes 3932168 | tf_op jit(solution)/shard_map/ppermute | solution.py:16
  277.0 106.6 %copy-start.22 = (bf16[2,128,2560]{1,2,0:T(8,128)(2,1)}, bf16[2,128,2560]{1,2,0:T(8,128)(2,1)S(1)}, u32[]{:S(2)}) copy-start(bf16[2,128,2560]{1,2,0:T(8,128)(2,1)S(1)} %collective-permute-done.19) | copy-start | bytes 3932164
  277.0 111.3 %collective-permute-start.14 = (bf16[2,128,2560]{1,2,0:T(8,128)(2,1)}, bf16[2,128,2560]{1,2,0:T(8,128)(2,1)}, u32[]{:S(2)}, u32[]{:S(2)}) collective-permute-start(bf16[2,128,2560]{1,2,0:T(8,128)(2,1)} %get-tuple-element.13), channel_id=1, source_target_pairs={{1,0},{2,1},{3,2},{4,3},{5,4},{6,5},{7,6},{8,7},{9,8},{10,9},{11,1... | collective-permute-start | bytes 3932168 | tf_op jit(solution)/shard_map/ppermute | solution.py:16
  305.1 78.6 %copy-start.24 = (bf16[2,128,2560]{1,2,0:T(8,128)(2,1)}, bf16[2,128,2560]{1,2,0:T(8,128)(2,1)S(1)}, u32[]{:S(2)}) copy-start(bf16[2,128,2560]{1,2,0:T(8,128)(2,1)S(1)} %collective-permute-done.18) | copy-start | bytes 3932164
  305.1 83.2 %collective-permute-start.13 = (bf16[2,128,2560]{1,2,0:T(8,128)(2,1)}, bf16[2,128,2560]{1,2,0:T(8,128)(2,1)}, u32[]{:S(2)}, u32[]{:S(2)}) collective-permute-start(bf16[2,128,2560]{1,2,0:T(8,128)(2,1)} %get-tuple-element.12), channel_id=1, source_target_pairs={{2,0},{3,1},{4,2},{5,3},{6,4},{7,5},{8,6},{9,7},{10,8},{11,9},{12,... | collective-permute-start | bytes 3932168 | tf_op jit(solution)/shard_map/ppermute | solution.py:16
  333.1 50.5 %copy-start.25 = (bf16[2,128,2560]{1,2,0:T(8,128)(2,1)}, bf16[2,128,2560]{1,2,0:T(8,128)(2,1)S(1)}, u32[]{:S(2)}) copy-start(bf16[2,128,2560]{1,2,0:T(8,128)(2,1)S(1)} %collective-permute-done.17) | copy-start | bytes 3932164
  333.1 55.1 %collective-permute-start.12 = (bf16[2,128,2560]{1,2,0:T(8,128)(2,1)}, bf16[2,128,2560]{1,2,0:T(8,128)(2,1)}, u32[]{:S(2)}, u32[]{:S(2)}) collective-permute-start(bf16[2,128,2560]{1,2,0:T(8,128)(2,1)} %get-tuple-element.11), channel_id=1, source_target_pairs={{3,0},{4,1},{5,2},{6,3},{7,4},{8,5},{9,6},{10,7},{11,8},{12,9},{13... | collective-permute-start | bytes 3932168 | tf_op jit(solution)/shard_map/ppermute | solution.py:16
  361.3 22.4 %copy-start.26 = (bf16[2,128,2560]{1,2,0:T(8,128)(2,1)}, bf16[2,128,2560]{1,2,0:T(8,128)(2,1)S(1)}, u32[]{:S(2)}) copy-start(bf16[2,128,2560]{1,2,0:T(8,128)(2,1)S(1)} %collective-permute-done.16) | copy-start | bytes 3932164
  361.3 37.4 %collective-permute-start.11 = (bf16[2,128,2560]{1,2,0:T(8,128)(2,1)}, bf16[2,128,2560]{1,2,0:T(8,128)(2,1)}, u32[]{:S(2)}, u32[]{:S(2)}) collective-permute-start(bf16[2,128,2560]{1,2,0:T(8,128)(2,1)} %get-tuple-element.10), channel_id=1, source_target_pairs={{4,0},{5,1},{6,2},{7,3},{8,4},{9,5},{10,6},{11,7},{12,8},{13,9},{1... | collective-permute-start | bytes 3932168 | tf_op jit(solution)/shard_map/ppermute | solution.py:16
  381.8 1.9 copy-start.27
  381.8 73.1 %collective-permute-start.10 = (bf16[2,128,2560]{1,2,0:T(8,128)(2,1)}, bf16[2,128,2560]{1,2,0:T(8,128)(2,1)}, u32[]{:S(2)}, u32[]{:S(2)}) collective-permute-start(bf16[2,128,2560]{1,2,0:T(8,128)(2,1)} %get-tuple-element.9), channel_id=1, source_target_pairs={{5,0},{6,1},{7,2},{8,3},{9,4},{10,5},{11,6},{12,7},{13,8},{14,9},{... | collective-permute-start | bytes 3932168 | tf_op jit(solution)/shard_map/ppermute | solution.py:16
  385.9 69.0 %copy-start.23 = (bf16[2,128,2560]{1,2,0:T(8,128)(2,1)S(1)}, bf16[2,128,2560]{1,2,0:T(8,128)(2,1)}, u32[]{:S(2)}) copy-start(bf16[2,128,2560]{1,2,0:T(8,128)(2,1)} %copy-done.22) | copy-start | bytes 3932164
  388.2 10.5 %copy-start.41 = (bf16[128,2560]{1,0:T(8,128)(2,1)}, bf16[128,2560]{1,0:T(8,128)(2,1)S(1)}, u32[]{:S(2)}) copy-start(bf16[128,2560]{1,0:T(8,128)(2,1)S(1)} %constant_dynamic-update-slice_fusion.2) | copy-start | bytes 1966084
where the time goes:
time: 468 us; the launch traced here: 463 us
  waiting for transfers between devices  191 us (41%)
  starting transfers between devices  153 us (33%)
  local copies, waits for them, and re-layouts  60.4 us (13%)
  matrix products  43.4 us (9%)
  other arithmetic  14.2 us (3%)
    ppermute x20, waiting for transfers between devices, shifted(): lax.ppermute(value, axis, [(source, source + steps) for source in range(l...  191 us
    ppermute x20, starting transfers between devices, shifted(): lax.ppermute(value, axis, [(source, source + steps) for source in range(l...  153 us
    unnamed x125, local copies, waits for them, and re-layouts  38.2 us
    convert_element_type x5, local copies, waits for them, and re-layouts, body(): key_parts.append(key_part.reshape(-1, group_width).astype(jnp.bfloat16))  12.9 us
    dot_general x5, matrix products, body(): jnp.einsum('hqk,qhd->khd', score_grad, query_heads, preferred_element_typ...  12.5 us
  transfers between devices with their start and end apart: 20, of which 14 were waited for; matrix products, arithmetic and copies ran while one was open for 6% of the time, Pallas kernels for 0%

commit v1 on v0

--- a/solution.py
+++ b/solution.py
@@ -7,13 +7,42 @@
 
 HD = 128
 QUARTERS = 4
-REACH = 5
 
 
-def shifted(value, axis, steps):
-    count = lax.axis_size(axis)
-    leading, last = (max(0, -steps), min(count, count - steps))
-    return lax.ppermute(value, axis, [(source, source + steps) for source in range(leading, last)])
+def send(value, pairs):
+    return lax.ppermute(value, "tm", pairs)
+
+
+def pairs_of(count, target):
+    pairs = []
+    for source in range(count):
+        dest = target(source)
+        if dest is not None and 0 <= dest < count:
+            pairs.append((source, dest))
+    return pairs
+
+
+def route(count):
+    core = pairs_of(count, lambda t: t ^ 1)
+    cross = pairs_of(count, lambda t: t ^ 2)
+    down = pairs_of(count, lambda t: t - QUARTERS)
+    up = pairs_of(count, lambda t: t + QUARTERS)
+
+    def diag(step):
+        def target(t):
+            q = t % QUARTERS
+            if q == 0:
+                return t + step * QUARTERS + 1
+            if q == QUARTERS - 1:
+                return t + step * QUARTERS - 1
+            return None
+
+        return pairs_of(count, target)
+
+    diag_up = diag(1)
+    diag_down = diag(-1)
+    back = lambda pairs: [(dest, source) for source, dest in pairs]
+    return core, cross, down, up, diag_up, diag_down, back
 
 
 def allowed(query_rows, key_rows, frame_keep, band_window, frame_len):
@@ -41,42 +70,49 @@
     return inside & (kept_pair > 0) & nearby
 
 
-def relay_blocks(block, advance):
-    gathered = {0: block}
-    for course in (1, -1):
-        carried = block
-        for offset in range(1, REACH + 1):
-            carried = advance(carried, -course)
-            gathered[course * offset] = carried
-    return [gathered[offset] for offset in range(-REACH, REACH + 1)]
-
-
-def spread_keys(stacked):
-
-    def advance(tensor, amount):
-        return shifted(tensor, "tm", amount)
-
-    return relay_blocks(stacked, advance)
-
-
-def return_partial(tensor, amount):
-    return shifted(tensor, "tm", amount)
-
-
 def body(queries, keys, values, out_grad, frame_keep, band_window):
     rows_own, channel_total = queries.shape
     head_total = channel_total // HD
     group_heads = 4
     group_width = group_heads * HD
     frame_len = QUARTERS * rows_own
-    block_count = 2 * REACH + 1
     inv_root = 1.0 / math.sqrt(HD)
+    count = lax.axis_size("tm")
+    core, cross, down, up, diag_up, diag_down, back = route(count)
     device = lax.axis_index("tm")
-    own_rows = device * rows_own + jnp.arange(rows_own, dtype=jnp.int32)
-    far_rows = (device - REACH) * rows_own + jnp.arange(block_count * rows_own, dtype=jnp.int32)
-    key_blocks = spread_keys(jnp.stack([keys, values]))
-    key_all = jnp.concatenate([member[0] for member in key_blocks])
-    value_all = jnp.concatenate([member[1] for member in key_blocks])
+    quarter = device % QUARTERS
+    partner = device ^ 1
+
+    own = jnp.stack([keys, values])
+    from_core = send(own, core)
+    from_cross = send(own, cross)
+    from_below = send(own, up)
+    from_above = send(own, down)
+    relayed = send(jnp.stack([from_cross, from_below, from_above]), core)
+    diag_from_below = send(from_cross, diag_up)
+    diag_from_above = send(from_cross, diag_down)
+    slots = [own, from_core, from_cross, from_below, from_above,
+             relayed[0], relayed[1], relayed[2], diag_from_below, diag_from_above]
+    middle = (quarter == 1) | (quarter == 2)
+    diag_quarter = QUARTERS - 1 - quarter
+    absent = jnp.int32(-(1 << 20))
+    sources = [
+        device,
+        partner,
+        device ^ 2,
+        device - QUARTERS,
+        device + QUARTERS,
+        device ^ 3,
+        partner - QUARTERS,
+        partner + QUARTERS,
+        jnp.where(middle, device - quarter - QUARTERS + diag_quarter, absent),
+        jnp.where(middle, device - quarter + QUARTERS + diag_quarter, absent),
+    ]
+    base_rows = jnp.arange(rows_own, dtype=jnp.int32)
+    far_rows = jnp.concatenate([source * rows_own + base_rows for source in sources])
+    own_rows = device * rows_own + base_rows
+    key_all = jnp.concatenate([member[0] for member in slots])
+    value_all = jnp.concatenate([member[1] for member in slots])
     forward_mask = allowed(own_rows, far_rows, frame_keep, band_window, frame_len)
     query_parts = []
     key_parts = []
@@ -122,12 +158,18 @@
         value_parts.append(value_part.reshape(-1, group_width).astype(jnp.bfloat16))
     query_grad = jnp.concatenate(query_parts, axis=1).astype(jnp.bfloat16)
     partials = jnp.stack([jnp.concatenate(key_parts, axis=1), jnp.concatenate(value_parts, axis=1)])
-    summed = partials[:, REACH * rows_own : (REACH + 1) * rows_own].astype(jnp.float32)
-    for position in range(block_count):
-        amount = position - REACH
-        if amount != 0:
-            section = partials[:, position * rows_own : (position + 1) * rows_own]
-            summed = summed + return_partial(section, amount).astype(jnp.float32)
+    part = [partials[:, slot * rows_own : (slot + 1) * rows_own] for slot in range(len(slots))]
+    wide = lambda tensor: tensor.astype(jnp.float32)
+    to_partner = send(jnp.stack([part[1], part[5], part[6], part[7]]), core)
+    diag_back_below = send(part[8], back(diag_up))
+    diag_back_above = send(part[9], back(diag_down))
+    cross_sum = wide(part[2]) + wide(to_partner[1]) + wide(diag_back_below) + wide(diag_back_above)
+    below_sum = wide(part[3]) + wide(to_partner[2])
+    above_sum = wide(part[4]) + wide(to_partner[3])
+    got_cross = send(cross_sum.astype(jnp.bfloat16), cross)
+    got_below = send(below_sum.astype(jnp.bfloat16), down)
+    got_above = send(above_sum.astype(jnp.bfloat16), up)
+    summed = wide(part[0]) + wide(to_partner[0]) + wide(got_cross) + wide(got_below) + wide(got_above)
     key_grad = summed[0].astype(jnp.bfloat16)
     value_grad = summed[1].astype(jnp.bfloat16)
     return (query_grad, key_grad, value_grad)

time: 468 us -> 211 us (0.45)
  the two profiles are of different devices: /device:TPU:7 before, /device:TPU:0 now
where the time goes in v1:
time: 211 us; the launch traced here: 210 us
  waiting for transfers between devices  69.8 us (33%)
  local copies, waits for them, and re-layouts  58.3 us (28%)
  matrix products  40.9 us (19%)
  starting transfers between devices  22 us (10%)
  other arithmetic  17.2 us (8%)
    ppermute x13, waiting for transfers between devices, send(): return lax.ppermute(value, 'tm', pairs)  69.8 us
    unnamed x98, local copies, waits for them, and re-layouts  35.9 us
    ppermute x13, starting transfers between devices, send(): return lax.ppermute(value, 'tm', pairs)  22 us
    convert_element_type x5, local copies, waits for them, and re-layouts, body(): key_parts.append(key_part.reshape(-1, group_width).astype(jnp.bfloat16))  12.2 us
    dot_general x5, matrix products, body(): jnp.einsum('hqk,qhd->khd', score_grad, query_heads, preferred_element_typ...  12 us
    dot_general x5, matrix products, body(): jnp.einsum('qhd,khd->hqk', grad_heads, value_heads, preferred_element_typ...  8.66 us
    dot_general x5, matrix products, body(): jnp.einsum('hqk,qhd->khd', prob_low, grad_heads, preferred_element_type=j...  8.09 us
    dot_general x5, matrix products, body(): jnp.einsum('hqk,khd->qhd', score_grad, key_heads, preferred_element_type=...  5.12 us
  transfers between devices with their start and end apart: 13, of which 7 were waited for; matrix products, arithmetic and copies ran while one was open for 13% of the time, Pallas kernels for 0%

profile of v1, /device:TPU:0, one launch (start us, length us, event | category | flops | bytes accessed | tf_op | source)
XLA Modules:
  0.0 209.6 jit_solution(7612259962295256339)
XLA Ops:
  0.6 1.5 copy.142
  2.1 1.4 copy.141
  3.5 1.2 pad_maximum_fusion.3
  5.2 2.5 %collective-permute-start.1 = (bf16[2,128,2560]{1,2,0:T(8,128)(2,1)}, bf16[2,128,2560]{1,2,0:T(8,128)(2,1)S(1)}, u32[]{:S(2)}, u32[]{:S(2)}) collective-permute-start(bf16[2,128,2560]{1,2,0:T(8,128)(2,1)} %pad_maximum_fusion.3), channel_id=1, source_target_pairs={{0,2},{1,3},{2,0},{3,1},{4,6},{5,7},{6,4},{7,5},{8,10},{9,11},{10,... | collective-permute-start | bytes 3932168 | tf_op jit(solution)/shard_map/ppermute | solution.py:13
  7.7 4.5 %collective-permute-start.2 = (bf16[2,128,2560]{1,2,0:T(8,128)(2,1)}, bf16[2,128,2560]{1,2,0:T(8,128)(2,1)}, u32[]{:S(2)}, u32[]{:S(2)}) collective-permute-start(bf16[2,128,2560]{1,2,0:T(8,128)(2,1)} %pad_maximum_fusion.3), channel_id=1, source_target_pairs={{0,4},{1,5},{2,6},{3,7},{4,8},{5,9},{6,10},{7,11},{8,12},{9,13},{1... | collective-permute-start | bytes 3932168 | tf_op jit(solution)/shard_map/ppermute | solution.py:13
  12.3 1.3 collective-permute-start.3
  15.6 2.0 fusion.117
  18.7 1.0 copy.262
  20.7 1.7 copy.263
  22.3 1.0 copy.266
  23.4 1.7 copy.265
  26.0 11.4 %collective-permute-done.1 = bf16[2,128,2560]{1,2,0:T(8,128)(2,1)S(1)} collective-permute-done((bf16[2,128,2560]{1,2,0:T(8,128)(2,1)}, bf16[2,128,2560]{1,2,0:T(8,128)(2,1)S(1)}, u32[]{:S(2)}, u32[]{:S(2)}) %collective-permute-start.1) | collective-permute-done | bytes 1310752 | tf_op jit(solution)/shard_map/ppermute | solution.py:13
  37.4 2.5 %collective-permute-done.2 = bf16[2,128,2560]{1,2,0:T(8,128)(2,1)} collective-permute-done((bf16[2,128,2560]{1,2,0:T(8,128)(2,1)}, bf16[2,128,2560]{1,2,0:T(8,128)(2,1)}, u32[]{:S(2)}, u32[]{:S(2)}) %collective-permute-start.2) | collective-permute-done | bytes 1310752 | tf_op jit(solution)/shard_map/ppermute | solution.py:13
  40.0 5.2 %collective-permute-done.3 = bf16[2,128,2560]{1,2,0:T(8,128)(2,1)} collective-permute-done((bf16[2,128,2560]{1,2,0:T(8,128)(2,1)}, bf16[2,128,2560]{1,2,0:T(8,128)(2,1)}, u32[]{:S(2)}, u32[]{:S(2)}) %collective-permute-start.3) | collective-permute-done | bytes 1310752 | tf_op jit(solution)/shard_map/ppermute | solution.py:13
  45.1 1.9 pad_maximum_fusion.1
  47.7 1.1 fusion.100
  48.8 2.3 %collective-permute-start.5 = (bf16[2,128,2560]{1,2,0:T(8,128)(2,1)S(1)}, bf16[2,128,2560]{1,2,0:T(8,128)(2,1)S(1)}, u32[]{:S(2)}, u32[]{:S(2)}) collective-permute-start(bf16[2,128,2560]{1,2,0:T(8,128)(2,1)S(1)} %collective-permute-done.1), channel_id=1, source_target_pairs={{0,5},{3,6},{4,9},{7,10},{8,13},{11,14},{16,21},{19,22},{20,25},{2... | collective-permute-start | bytes 3932168 | tf_op jit(solution)/shard_map/ppermute | solution.py:13
  51.1 0.9 collective-permute-start.6
  52.1 1.6 fusion.90
  54.0 1.6 fusion.88
  55.6 1.6 fusion.87
  58.1 8.0 %collective-permute-done.5 = bf16[2,128,2560]{1,2,0:T(8,128)(2,1)S(1)} collective-permute-done((bf16[2,128,2560]{1,2,0:T(8,128)(2,1)S(1)}, bf16[2,128,2560]{1,2,0:T(8,128)(2,1)S(1)}, u32[]{:S(2)}, u32[]{:S(2)}) %collective-permute-start.5) | collective-permute-done | bytes 1310752 | tf_op jit(solution)/shard_map/ppermute | solution.py:13
  66.8 2.7 %copy-done.13 = bf16[1280,2560]{0,1:T(8,128)(2,1)} copy-done((bf16[1280,2560]{0,1:T(8,128)(2,1)}, bf16[1280,2560]{0,1:T(8,128)(2,1)S(1)}, u32[]{:S(2)}) %copy-start.13) | copy-done | bytes 6553624
  70.0 4.7 %fusion.115 = (bf16[1280,512]{0,1:T(8,128)(2,1)S(1)}, bf16[1280,512]{0,1:T(8,128)(2,1)S(1)}, bf16[1280,512]{0,1:T(8,128)(2,1)S(1)}, bf16[1280,512]{0,1:T(8,128)(2,1)S(1)}, bf16[1280,512]{0,1:T(8,128)(2,1)S(1)}) fusion(bf16[1280,2560]{0,1:T(8,128)(2,1)} %copy-done.13), kind=kLoop, calls=%fused_computation.251 | loop fusion | bytes 13107200 | tf_op jit(solution)/shard_map/slice | solution.py:126
  75.9 1.6 convolution_convert_fusion.4
  80.1 1.6 convolution_convert_fusion.3
  82.3 1.9 fusion.23
  85.4 1.6 convolution_convert_fusion.2
  87.8 2.0 fusion.22
  91.0 1.6 convolution_convert_fusion.1
  93.2 2.0 fusion.21
  96.4 1.6 convolution_convert_fusion
  98.6 1.9 fusion.20
  100.6 1.6 fusion.34
  102.1 2.5 %copy.192 = bf16[1280,4,128]{0,2,1:T(8,128)(2,1)} copy(bf16[1280,4,128]{2,0,1:T(8,128)(2,1)} %fusion.34) | data formatting | bytes 2621440 | tf_op jit(solution)/shard_map/convert_element_type | solution.py:157
  104.6 2.6 %constant_dynamic-update-slice_fusion.12 = bf16[1280,2560]{0,1:T(8,128)(2,1)} fusion(bf16[1280,512]{0,1:T(8,128)(2,1)} %bitcast.354), kind=kLoop, calls=%fused_computation.208 | loop fusion | bytes 2621440
  107.2 1.6 fusion.33
  108.8 2.5 %copy.195 = bf16[1280,4,128]{0,2,1:T(8,128)(2,1)} copy(bf16[1280,4,128]{2,0,1:T(8,128)(2,1)} %fusion.33) | data formatting | bytes 2621440 | tf_op jit(solution)/shard_map/convert_element_type | solution.py:157
  111.3 2.9 %fusion.32 = bf16[1280,4,128]{2,0,1:T(8,128)(2,1)} fusion(bf16[4,128,1280]{1,2,0:T(8,128)(2,1)} %fusion.22, bf16[128,4,128]{0,2,1:T(8,128)(2,1)S(1)} %bitcast.376), kind=kOutput, calls=%fused_computation.72 | convolution fusion | flops 169082880 | bytes 2752512 | tf_op jit(solution)/shard_map/hqk,qhd->khd/dot_general | solution.py:151
  114.2 2.5 %copy.198 = bf16[1280,4,128]{0,2,1:T(8,128)(2,1)} copy(bf16[1280,4,128]{2,0,1:T(8,128)(2,1)} %fusion.32) | data formatting | bytes 2621440 | tf_op jit(solution)/shard_map/convert_element_type | solution.py:157
  116.6 2.9 %fusion.31 = bf16[1280,4,128]{2,0,1:T(8,128)(2,1)} fusion(bf16[4,128,1280]{1,2,0:T(8,128)(2,1)} %fusion.21, bf16[128,4,128]{0,2,1:T(8,128)(2,1)S(1)} %bitcast.378), kind=kOutput, calls=%fused_computation.71 | convolution fusion | flops 169082880 | bytes 2752512 | tf_op jit(solution)/shard_map/hqk,qhd->khd/dot_general | solution.py:151
  119.5 2.5 %copy.201 = bf16[1280,4,128]{0,2,1:T(8,128)(2,1)} copy(bf16[1280,4,128]{2,0,1:T(8,128)(2,1)} %fusion.31) | data formatting | bytes 2621440 | tf_op jit(solution)/shard_map/convert_element_type | solution.py:157
  122.0 3.0 %fusion.30 = bf16[1280,4,128]{2,0,1:T(8,128)(2,1)} fusion(bf16[4,128,1280]{1,2,0:T(8,128)(2,1)} %fusion.20, bf16[128,4,128]{0,2,1:T(8,128)(2,1)S(1)} %bitcast.380), kind=kOutput, calls=%fused_computation.70 | convolution fusion | flops 169082880 | bytes 2752512 | tf_op jit(solution)/shard_map/hqk,qhd->khd/dot_general | solution.py:151
  124.9 2.4 %copy.204 = bf16[1280,4,128]{0,2,1:T(8,128)(2,1)} copy(bf16[1280,4,128]{2,0,1:T(8,128)(2,1)} %fusion.30) | data formatting | bytes 2621440 | tf_op jit(solution)/shard_map/convert_element_type | solution.py:157
  127.3 1.6 constant_dynamic-update-slice_fusion.17
  129.1 1.2 constant_dynamic-update-slice_fusion.11
  130.3 1.2 constant_dynamic-update-slice_fusion.10
  131.5 1.1 constant_dynamic-update-slice_fusion.9
  132.6 1.2 constant_dynamic-update-slice_fusion.8
  135.7 3.7 %copy-done = bf16[1280,2560]{0,1:T(8,128)(2,1)S(1)} copy-done((bf16[1280,2560]{0,1:T(8,128)(2,1)S(1)}, bf16[1280,2560]{0,1:T(8,128)(2,1)}, u32[]{:S(2)}) %copy-start) | copy-done | bytes 6553624
  139.5 1.0 fusion.56
  141.5 3.0 %collective-permute-start.7 = (bf16[4,2,128,2560]{2,3,1,0:T(8,128)(2,1)S(1)}, bf16[4,2,128,2560]{2,3,1,0:T(8,128)(2,1)S(1)}, u32[]{:S(2)}, u32[]{:S(2)}) collective-permute-start(bf16[4,2,128,2560]{2,3,1,0:T(8,128)(2,1)S(1)} %pad_maximum_fusion), channel_id=1, source_target_pairs={{0,1},{1,0},{2,3},{3,2},{4,5},{5,4},{6,7},{7,6},{8,9},{9,8},{10,11... | collective-permute-start | bytes 15728648 | tf_op jit(solution)/shard_map/ppermute | solution.py:13
  145.2 1.3 collective-permute-start.8
  147.5 17.1 %collective-permute-done.8 = bf16[2,128,2560]{1,2,0:T(8,128)(2,1)S(1)} collective-permute-done((bf16[2,128,2560]{1,2,0:T(8,128)(2,1)S(1)}, bf16[2,128,2560]{1,2,0:T(8,128)(2,1)S(1)}, u32[]{:S(2)}, u32[]{:S(2)}) %collective-permute-start.8) | collective-permute-done | bytes 1310752 | tf_op jit(solution)/shard_map/ppermute | solution.py:13
  164.7 3.4 %fusion.39 = (bf16[2,128,2560]{1,2,0:T(8,128)(2,1)}, bf16[2,128,2560]{1,2,0:T(8,128)(2,1)}, bf16[2,128,2560]{1,2,0:T(8,128)(2,1)}) fusion(bf16[2,128,2560]{1,2,0:T(8,128)(2,1)S(1)} %collective-permute-done.9, bf16[2,128,2560]{1,2,0:T(8,128)(2,1)S(1)} %collective-permute-done.8, bf16[1,1280,2560]{1,2,0:T(8,128)(2,1)S(1)} %bitcast.321, ...), kind=kLoop, calls=%fused_computation.82 | loop fusion | flops 16384000 | bytes 23592960 | tf_op jit(solution)/shard_map/convert_element_type | solution.py:169
  168.3 3.5 %collective-permute-start.12 = (bf16[2,128,2560]{1,2,0:T(8,128)(2,1)}, bf16[2,128,2560]{1,2,0:T(8,128)(2,1)}, u32[]{:S(2)}, u32[]{:S(2)}) collective-permute-start(bf16[2,128,2560]{1,2,0:T(8,128)(2,1)} %get-tuple-element.10), channel_id=1, source_target_pairs={{0,4},{1,5},{2,6},{3,7},{4,8},{5,9},{6,10},{7,11},{8,12},{9,13},{1... | collective-permute-start | bytes 3932168 | tf_op jit(solution)/shard_map/ppermute | solution.py:13
  171.8 1.3 collective-permute-start.11
  174.1 1.8 fusion.70
  176.0 1.8 fusion.71
  178.1 20.3 %collective-permute-done.12 = bf16[2,128,2560]{1,2,0:T(8,128)(2,1)} collective-permute-done((bf16[2,128,2560]{1,2,0:T(8,128)(2,1)}, bf16[2,128,2560]{1,2,0:T(8,128)(2,1)}, u32[]{:S(2)}, u32[]{:S(2)}) %collective-permute-start.12) | collective-permute-done | bytes 1310752 | tf_op jit(solution)/shard_map/ppermute | solution.py:13
  198.4 5.2 %collective-permute-done.11 = bf16[2,128,2560]{1,2,0:T(8,128)(2,1)} collective-permute-done((bf16[2,128,2560]{1,2,0:T(8,128)(2,1)}, bf16[2,128,2560]{1,2,0:T(8,128)(2,1)}, u32[]{:S(2)}, u32[]{:S(2)}) %collective-permute-start.11) | collective-permute-done | bytes 1310752 | tf_op jit(solution)/shard_map/ppermute | solution.py:13
  203.6 3.8 %fusion.43 = bf16[2,128,2560]{1,2,0:T(8,128)(2,1)S(1)} fusion(bf16[2,128,2560]{1,2,0:T(8,128)(2,1)} %collective-permute-done.12, bf16[2,128,2560]{1,2,0:T(8,128)(2,1)} %collective-permute-done.11, bf16[2,128,2560]{1,2,0:T(8,128)(2,1)} %collective-permute-done.10, bf16[1,1280,2560]{1,2,0:T(8,128)(2,1)} %bitcast.322, bf16[1,1280,2560]{1,2,0:T(8,128)(2,1)} %bitcast.317, ...), kind=kLoop, calls=%fused_computation.87 | loop fusion | flops 7208960 | bytes 19660800 | tf_op jit(solution)/shard_map/convert.5
  207.5 1.1 copy.210
  208.6 1.1 copy.211
  (145 shorter events, 24.5 us)
Async XLA Ops:
  0.6 14.1 %copy-start.26 = (bf16[128,2560]{1,0:T(8,128)(2,1)S(1)}, bf16[128,2560]{1,0:T(8,128)(2,1)}, u32[]{:S(2)}) copy-start(bf16[128,2560]{1,0:T(8,128)(2,1)} %param.9) | copy-start | bytes 1966084
  4.7 47.3 %collective-permute-start = (bf16[2,128,2560]{1,2,0:T(8,128)(2,1)}, bf16[2,128,2560]{1,2,0:T(8,128)(2,1)}, u32[]{:S(2)}, u32[]{:S(2)}) collective-permute-start(bf16[2,128,2560]{1,2,0:T(8,128)(2,1)} %pad_maximum_fusion.3), channel_id=1, source_target_pairs={{0,1},{1,0},{2,3},{3,2},{4,5},{5,4},{6,7},{7,6},{8,9},{9,8},{10,11... | collective-permute-start | bytes 3932168 | tf_op jit(solution)/shard_map/ppermute | solution.py:13
  5.2 32.2 %collective-permute-start.1 = (bf16[2,128,2560]{1,2,0:T(8,128)(2,1)}, bf16[2,128,2560]{1,2,0:T(8,128)(2,1)S(1)}, u32[]{:S(2)}, u32[]{:S(2)}) collective-permute-start(bf16[2,128,2560]{1,2,0:T(8,128)(2,1)} %pad_maximum_fusion.3), channel_id=1, source_target_pairs={{0,2},{1,3},{2,0},{3,1},{4,6},{5,7},{6,4},{7,5},{8,10},{9,11},{10,... | collective-permute-start | bytes 3932168 | tf_op jit(solution)/shard_map/ppermute | solution.py:13
  7.7 32.2 %collective-permute-start.2 = (bf16[2,128,2560]{1,2,0:T(8,128)(2,1)}, bf16[2,128,2560]{1,2,0:T(8,128)(2,1)}, u32[]{:S(2)}, u32[]{:S(2)}) collective-permute-start(bf16[2,128,2560]{1,2,0:T(8,128)(2,1)} %pad_maximum_fusion.3), channel_id=1, source_target_pairs={{0,4},{1,5},{2,6},{3,7},{4,8},{5,9},{6,10},{7,11},{8,12},{9,13},{1... | collective-permute-start | bytes 3932168 | tf_op jit(solution)/shard_map/ppermute | solution.py:13
  12.3 32.8 %collective-permute-start.3 = (bf16[2,128,2560]{1,2,0:T(8,128)(2,1)}, bf16[2,128,2560]{1,2,0:T(8,128)(2,1)}, u32[]{:S(2)}, u32[]{:S(2)}) collective-permute-start(bf16[2,128,2560]{1,2,0:T(8,128)(2,1)} %pad_maximum_fusion.3), channel_id=1, source_target_pairs={{4,0},{5,1},{6,2},{7,3},{8,4},{9,5},{10,6},{11,7},{12,8},{13,9},{1... | collective-permute-start | bytes 3932168 | tf_op jit(solution)/shard_map/ppermute | solution.py:13
  15.5 5.1 %copy-start.27 = (bf16[128,512]{1,0:T(8,128)(2,1)S(1)}, bf16[128,512]{1,0:T(8,128)(2,1)}, u32[]{:S(2)}) copy-start(bf16[128,512]{1,0:T(8,128)(2,1)} %get-tuple-element.54) | copy-start | bytes 393220
  47.0 0.6 copy-start.29
  47.1 0.7 copy-start.30
  47.1 10.1 %collective-permute-start.4 = (bf16[3,2,128,2560]{2,3,1,0:T(8,128)(2,1)S(1)}, bf16[3,2,128,2560]{2,3,1,0:T(8,128)(2,1)S(1)}, u32[]{:S(2)}, u32[]{:S(2)}) collective-permute-start(bf16[3,2,128,2560]{2,3,1,0:T(8,128)(2,1)S(1)} %pad_maximum_fusion.1), channel_id=1, source_target_pairs={{0,1},{1,0},{2,3},{3,2},{4,5},{5,4},{6,7},{7,6},{8,9},{9,8},{10,11... | collective-permute-start | bytes 11796488 | tf_op jit(solution)/shard_map/ppermute | solution.py:13
  48.8 17.3 %collective-permute-start.5 = (bf16[2,128,2560]{1,2,0:T(8,128)(2,1)S(1)}, bf16[2,128,2560]{1,2,0:T(8,128)(2,1)S(1)}, u32[]{:S(2)}, u32[]{:S(2)}) collective-permute-start(bf16[2,128,2560]{1,2,0:T(8,128)(2,1)S(1)} %collective-permute-done.1), channel_id=1, source_target_pairs={{0,5},{3,6},{4,9},{7,10},{8,13},{11,14},{16,21},{19,22},{20,25},{2... | collective-permute-start | bytes 3932168 | tf_op jit(solution)/shard_map/ppermute | solution.py:13
  51.1 15.3 %collective-permute-start.6 = (bf16[2,128,2560]{1,2,0:T(8,128)(2,1)S(1)}, bf16[2,128,2560]{1,2,0:T(8,128)(2,1)S(1)}, u32[]{:S(2)}, u32[]{:S(2)}) collective-permute-start(bf16[2,128,2560]{1,2,0:T(8,128)(2,1)S(1)} %collective-permute-done.1), channel_id=1, source_target_pairs={{4,1},{7,2},{8,5},{11,6},{12,9},{15,10},{20,17},{23,18},{24,21},{2... | collective-permute-start | bytes 3932168 | tf_op jit(solution)/shard_map/ppermute | solution.py:13
  66.8 2.7 %copy-start.13 = (bf16[1280,2560]{0,1:T(8,128)(2,1)}, bf16[1280,2560]{0,1:T(8,128)(2,1)S(1)}, u32[]{:S(2)}) copy-start(bf16[1280,2560]{0,1:T(8,128)(2,1)S(1)} %get-tuple-element.36) | copy-start | bytes 19660804
  69.9 4.8 %copy-start.6 = (bf16[1280,512]{0,1:T(8,128)(2,1)}, bf16[1280,512]{0,1:T(8,128)(2,1)S(1)}, u32[]{:S(2)}) copy-start(bf16[1280,512]{0,1:T(8,128)(2,1)S(1)} %get-tuple-element.27) | copy-start | bytes 3932164
  70.0 9.0 %copy-start.4 = (bf16[1280,512]{0,1:T(8,128)(2,1)}, bf16[1280,512]{0,1:T(8,128)(2,1)S(1)}, u32[]{:S(2)}) copy-start(bf16[1280,512]{0,1:T(8,128)(2,1)S(1)} %get-tuple-element.26) | copy-start | bytes 3932164
  70.0 14.2 %copy-start.2 = (bf16[1280,512]{0,1:T(8,128)(2,1)}, bf16[1280,512]{0,1:T(8,128)(2,1)S(1)}, u32[]{:S(2)}) copy-start(bf16[1280,512]{0,1:T(8,128)(2,1)S(1)} %get-tuple-element.25) | copy-start | bytes 3932164
  78.9 21.6 %copy-start.9 = (bf16[4,128,1280]{1,2,0:T(8,128)(2,1)}, bf16[4,128,1280]{1,2,0:T(8,128)(2,1)S(1)}, u32[]{:S(2)}) copy-start(bf16[4,128,1280]{1,2,0:T(8,128)(2,1)S(1)} %fusion.24) | copy-start | bytes 3932164
  82.3 1.9 copy-start.23
  87.8 2.0 copy-start.24
  93.2 2.0 copy-start.25
  104.6 2.6 %copy-start.11 = (bf16[4,128,1280]{1,2,0:T(8,128)(2,1)S(1)}, bf16[4,128,1280]{1,2,0:T(8,128)(2,1)}, u32[]{:S(2)}) copy-start(bf16[4,128,1280]{1,2,0:T(8,128)(2,1)} %fusion.23) | copy-start | bytes 3932164
  127.3 1.7 copy-start.19
  127.3 3.0 %copy-start.20 = (bf16[1280,4,128]{0,2,1:T(8,128)(2,1)S(1)}, bf16[1280,4,128]{0,2,1:T(8,128)(2,1)}, u32[]{:S(2)}) copy-start(bf16[1280,4,128]{0,2,1:T(8,128)(2,1)} %copy.198) | copy-start | bytes 3932164
  129.1 2.4 %copy-start.21 = (bf16[1280,4,128]{0,2,1:T(8,128)(2,1)S(1)}, bf16[1280,4,128]{0,2,1:T(8,128)(2,1)}, u32[]{:S(2)}) copy-start(bf16[1280,4,128]{0,2,1:T(8,128)(2,1)} %copy.201) | copy-start | bytes 3932164
  130.3 2.3 %copy-start.22 = (bf16[1280,4,128]{0,2,1:T(8,128)(2,1)S(1)}, bf16[1280,4,128]{0,2,1:T(8,128)(2,1)}, u32[]{:S(2)}) copy-start(bf16[1280,4,128]{0,2,1:T(8,128)(2,1)} %copy.204) | copy-start | bytes 3932164
  131.5 2.4 %copy-start.15 = (bf16[4,1280,128]{1,2,0:T(8,128)(2,1)S(1)}, bf16[4,1280,128]{1,2,0:T(8,128)(2,1)}, u32[]{:S(2)}) copy-start(bf16[4,1280,128]{1,2,0:T(8,128)(2,1)} %convolution_convert_fusion.3) | copy-start | bytes 3932164
  132.6 1.9 copy-start.16
  133.8 1.4 copy-start.17
  133.9 1.7 copy-start.18
  134.5 5.0 %copy-start = (bf16[1280,2560]{0,1:T(8,128)(2,1)S(1)}, bf16[1280,2560]{0,1:T(8,128)(2,1)}, u32[]{:S(2)}) copy-start(bf16[1280,2560]{0,1:T(8,128)(2,1)} %constant_dynamic-update-slice_fusion.8) | copy-start | bytes 19660804
  135.7 28.9 %copy-start.1 = (bf16[1280,2560]{0,1:T(8,128)(2,1)}, bf16[1280,2560]{0,1:T(8,128)(2,1)S(1)}, u32[]{:S(2)}) copy-start(bf16[1280,2560]{0,1:T(8,128)(2,1)S(1)} %constant_dynamic-update-slice_fusion.13) | copy-start | bytes 19660804
  140.5 6.0 %copy-start.7 = (bf16[1280,512]{0,1:T(8,128)(2,1)S(1)}, bf16[1280,512]{0,1:T(8,128)(2,1)}, u32[]{:S(2)}) copy-start(bf16[1280,512]{0,1:T(8,128)(2,1)} %copy-done.6) | copy-start | bytes 3932164
  140.5 6.0 %copy-start.10 = (bf16[4,128,1280]{1,2,0:T(8,128)(2,1)S(1)}, bf16[4,128,1280]{1,2,0:T(8,128)(2,1)}, u32[]{:S(2)}) copy-start(bf16[4,128,1280]{1,2,0:T(8,128)(2,1)} %copy-done.9) | copy-start | bytes 3932164
  141.4 5.5 %copy-start.5 = (bf16[1280,512]{0,1:T(8,128)(2,1)S(1)}, bf16[1280,512]{0,1:T(8,128)(2,1)}, u32[]{:S(2)}) copy-start(bf16[1280,512]{0,1:T(8,128)(2,1)} %copy-done.4) | copy-start | bytes 3932164
  141.5 5.5 %copy-start.12 = (bf16[4,128,1280]{1,2,0:T(8,128)(2,1)S(1)}, bf16[4,128,1280]{1,2,0:T(8,128)(2,1)}, u32[]{:S(2)}) copy-start(bf16[4,128,1280]{1,2,0:T(8,128)(2,1)} %fusion.23) | copy-start | bytes 3932164
  141.5 23.2 %collective-permute-start.7 = (bf16[4,2,128,2560]{2,3,1,0:T(8,128)(2,1)S(1)}, bf16[4,2,128,2560]{2,3,1,0:T(8,128)(2,1)S(1)}, u32[]{:S(2)}, u32[]{:S(2)}) collective-permute-start(bf16[4,2,128,2560]{2,3,1,0:T(8,128)(2,1)S(1)} %pad_maximum_fusion), channel_id=1, source_target_pairs={{0,1},{1,0},{2,3},{3,2},{4,5},{5,4},{6,7},{7,6},{8,9},{9,8},{10,11... | collective-permute-start | bytes 15728648 | tf_op jit(solution)/shard_map/ppermute | solution.py:13
  144.4 3.1 %collective-permute-start.9 = (bf16[2,128,2560]{1,2,0:T(8,128)(2,1)S(1)}, bf16[2,128,2560]{1,2,0:T(8,128)(2,1)S(1)}, u32[]{:S(2)}, u32[]{:S(2)}) collective-permute-start(bf16[2,128,2560]{1,2,0:T(8,128)(2,1)S(1)} %get-tuple-element.17), channel_id=1, source_target_pairs={{1,4},{2,7},{5,8},{6,11},{9,12},{10,15},{17,20},{18,23},{21,24},{2... | collective-permute-start | bytes 3932168 | tf_op jit(solution)/shard_map/ppermute | solution.py:13
  145.2 19.5 %collective-permute-start.8 = (bf16[2,128,2560]{1,2,0:T(8,128)(2,1)S(1)}, bf16[2,128,2560]{1,2,0:T(8,128)(2,1)S(1)}, u32[]{:S(2)}, u32[]{:S(2)}) collective-permute-start(bf16[2,128,2560]{1,2,0:T(8,128)(2,1)S(1)} %get-tuple-element.12), channel_id=1, source_target_pairs={{5,0},{6,3},{9,4},{10,7},{13,8},{14,11},{21,16},{22,19},{25,20},{2... | collective-permute-start | bytes 3932168 | tf_op jit(solution)/shard_map/ppermute | solution.py:13
  147.5 25.7 %copy-start.3 = (bf16[1280,512]{0,1:T(8,128)(2,1)S(1)}, bf16[1280,512]{0,1:T(8,128)(2,1)}, u32[]{:S(2)}) copy-start(bf16[1280,512]{0,1:T(8,128)(2,1)} %copy-done.2) | copy-start | bytes 3932164
  147.5 25.7 %copy-start.8 = (bf16[4,128,1280]{1,2,0:T(8,128)(2,1)S(1)}, bf16[4,128,1280]{1,2,0:T(8,128)(2,1)}, u32[]{:S(2)}) copy-start(bf16[4,128,1280]{1,2,0:T(8,128)(2,1)} %fusion.22) | copy-start | bytes 3932164
  164.7 3.7 %copy-start.14 = (bf16[4,2,128,2560]{2,3,1,0:T(8,128)(2,1)}, bf16[4,2,128,2560]{2,3,1,0:T(8,128)(2,1)S(1)}, u32[]{:S(2)}) copy-start(bf16[4,2,128,2560]{2,3,1,0:T(8,128)(2,1)S(1)} %collective-permute-done.7) | copy-start | bytes 15728644
  168.3 30.1 %collective-permute-start.12 = (bf16[2,128,2560]{1,2,0:T(8,128)(2,1)}, bf16[2,128,2560]{1,2,0:T(8,128)(2,1)}, u32[]{:S(2)}, u32[]{:S(2)}) collective-permute-start(bf16[2,128,2560]{1,2,0:T(8,128)(2,1)} %get-tuple-element.10), channel_id=1, source_target_pairs={{0,4},{1,5},{2,6},{3,7},{4,8},{5,9},{6,10},{7,11},{8,12},{9,13},{1... | collective-permute-start | bytes 3932168 | tf_op jit(solution)/shard_map/ppermute | solution.py:13
  171.8 31.8 %collective-permute-start.11 = (bf16[2,128,2560]{1,2,0:T(8,128)(2,1)}, bf16[2,128,2560]{1,2,0:T(8,128)(2,1)}, u32[]{:S(2)}, u32[]{:S(2)}) collective-permute-start(bf16[2,128,2560]{1,2,0:T(8,128)(2,1)} %get-tuple-element.11), channel_id=1, source_target_pairs={{4,0},{5,1},{6,2},{7,3},{8,4},{9,5},{10,6},{11,7},{12,8},{13,9},{1... | collective-permute-start | bytes 3932168 | tf_op jit(solution)/shard_map/ppermute | solution.py:13
  173.1 30.5 %collective-permute-start.10 = (bf16[2,128,2560]{1,2,0:T(8,128)(2,1)}, bf16[2,128,2560]{1,2,0:T(8,128)(2,1)}, u32[]{:S(2)}, u32[]{:S(2)}) collective-permute-start(bf16[2,128,2560]{1,2,0:T(8,128)(2,1)} %get-tuple-element.9), channel_id=1, source_target_pairs={{0,2},{1,3},{2,0},{3,1},{4,6},{5,7},{6,4},{7,5},{8,10},{9,11},{10,... | collective-permute-start | bytes 3932168 | tf_op jit(solution)/shard_map/ppermute | solution.py:13
  178.1 29.3 %copy-start.28 = (bf16[128,2560]{1,0:T(8,128)(2,1)}, bf16[128,2560]{1,0:T(8,128)(2,1)S(1)}, u32[]{:S(2)}) copy-start(bf16[128,2560]{1,0:T(8,128)(2,1)S(1)} %constant_dynamic-update-slice_fusion.3) | copy-start | bytes 1966084

commit v2 on v1

--- a/solution.py
+++ b/solution.py
@@ -3,6 +3,7 @@
 import jax
 import jax.numpy as jnp
 from jax import lax
+from jax.experimental import pallas as pl
 from jax.sharding import PartitionSpec as P
 
 HD = 128
@@ -70,11 +71,66 @@
     return inside & (kept_pair > 0) & nearby
 
 
+def attention_backward(mask, queries, out_grad, inputs, slot_in, out_lead, slot_out, inv_root):
+    rows, channels = queries.shape
+    heads = channels // HD
+    slots = len(slot_in)
+    n_in = len(inputs)
+
+    def kernel(mask_ref, q_ref, g_ref, *refs):
+        in_refs = refs[:n_in]
+        dq_ref = refs[n_in]
+        out_refs = refs[n_in + 1 :]
+        k = jnp.concatenate([in_refs[i][lead + (0,)] for i, lead in slot_in], axis=0)
+        v = jnp.concatenate([in_refs[i][lead + (1,)] for i, lead in slot_in], axis=0)
+        q = q_ref[...]
+        g = g_ref[...]
+        nt = (((1,), (1,)), ((), ()))
+        tn = (((0,), (0,)), ((), ()))
+        scores = lax.dot_general(q, k, nt, preferred_element_type=jnp.float32) * inv_root
+        masked = jnp.where(mask_ref[...] != 0, scores, -1e30)
+        highest = jnp.max(masked, axis=1, keepdims=True)
+        total_mass = jnp.sum(jnp.exp(masked - highest), axis=1, keepdims=True)
+        log_total = highest + jnp.log(total_mass)
+        prob = jnp.exp(masked - log_total)
+        prob_low = prob.astype(jnp.bfloat16)
+        attended = jnp.dot(prob_low, v, preferred_element_type=jnp.float32)
+        delta = jnp.sum(g.astype(jnp.float32) * attended, axis=1, keepdims=True)
+        prob_grad = lax.dot_general(g, v, nt, preferred_element_type=jnp.float32)
+        score_grad = (prob * (prob_grad - delta)).astype(jnp.bfloat16)
+        dq = jnp.dot(score_grad, k, preferred_element_type=jnp.float32) * inv_root
+        dq_ref[...] = dq.astype(dq_ref.dtype)
+        dk = lax.dot_general(score_grad, q, tn, preferred_element_type=jnp.float32) * inv_root
+        dv = lax.dot_general(prob_low, g, tn, preferred_element_type=jnp.float32)
+        for slot, (i, lead) in enumerate(slot_out):
+            out_refs[i][lead + (0,)] = dk[slot * rows : (slot + 1) * rows].astype(jnp.bfloat16)
+            out_refs[i][lead + (1,)] = dv[slot * rows : (slot + 1) * rows].astype(jnp.bfloat16)
+
+    def head_spec(lead_shape):
+        zeros = (0,) * len(lead_shape)
+        return pl.BlockSpec(lead_shape + (2, rows, HD), lambda h: zeros + (0, 0, h))
+
+    in_specs = [
+        pl.BlockSpec((rows, slots * rows), lambda h: (0, 0)),
+        pl.BlockSpec((rows, HD), lambda h: (0, h)),
+        pl.BlockSpec((rows, HD), lambda h: (0, h)),
+    ] + [head_spec(tuple(x.shape[:-3])) for x in inputs]
+    out_specs = [pl.BlockSpec((rows, HD), lambda h: (0, h))] + [head_spec(lead) for lead in out_lead]
+    out_shape = [jax.ShapeDtypeStruct((rows, channels), jnp.bfloat16)] + [
+        jax.ShapeDtypeStruct(lead + (2, rows, channels), jnp.bfloat16) for lead in out_lead
+    ]
+    results = pl.pallas_call(
+        kernel,
+        grid=(heads,),
+        in_specs=in_specs,
+        out_specs=out_specs,
+        out_shape=out_shape,
+    )(mask, queries, out_grad, *inputs)
+    return results[0], results[1:]
+
+
 def body(queries, keys, values, out_grad, frame_keep, band_window):
     rows_own, channel_total = queries.shape
-    head_total = channel_total // HD
-    group_heads = 4
-    group_width = group_heads * HD
     frame_len = QUARTERS * rows_own
     inv_root = 1.0 / math.sqrt(HD)
     count = lax.axis_size("tm")
@@ -111,65 +167,26 @@
     base_rows = jnp.arange(rows_own, dtype=jnp.int32)
     far_rows = jnp.concatenate([source * rows_own + base_rows for source in sources])
     own_rows = device * rows_own + base_rows
-    key_all = jnp.concatenate([member[0] for member in slots])
-    value_all = jnp.concatenate([member[1] for member in slots])
-    forward_mask = allowed(own_rows, far_rows, frame_keep, band_window, frame_len)
-    query_parts = []
-    key_parts = []
-    value_parts = []
-    for group_index in range(head_total // group_heads):
-        lower = group_index * group_width
-        upper = lower + group_width
-        query_heads = queries[:, lower:upper].reshape(rows_own, group_heads, HD)
-        grad_heads = out_grad[:, lower:upper].reshape(rows_own, group_heads, HD)
-        key_heads = key_all[:, lower:upper].reshape(-1, group_heads, HD)
-        value_heads = value_all[:, lower:upper].reshape(-1, group_heads, HD)
-        scores = (
-            jnp.einsum("qhd,khd->hqk", query_heads, key_heads, preferred_element_type=jnp.float32)
-            * inv_root
-        )
-        masked = jnp.where(forward_mask[None], scores, -1e30)
-        highest = jnp.max(masked, axis=2, keepdims=True)
-        total_mass = jnp.sum(jnp.exp(masked - highest), axis=2, keepdims=True)
-        log_total = highest + jnp.log(total_mass)
-        attn_prob = jnp.exp(masked - log_total)
-        prob_low = attn_prob.astype(jnp.bfloat16)
-        attended = jnp.einsum(
-            "hqk,khd->qhd", prob_low, value_heads, preferred_element_type=jnp.float32
-        )
-        delta_sum = jnp.sum(grad_heads.astype(jnp.float32) * attended, axis=2)
-        prob_grad = jnp.einsum(
-            "qhd,khd->hqk", grad_heads, value_heads, preferred_element_type=jnp.float32
-        )
-        score_grad = (attn_prob * (prob_grad - delta_sum.T[:, :, None])).astype(jnp.bfloat16)
-        query_part = (
-            jnp.einsum("hqk,khd->qhd", score_grad, key_heads, preferred_element_type=jnp.float32)
-            * inv_root
-        )
-        query_parts.append(query_part.reshape(rows_own, group_width))
-        key_part = (
-            jnp.einsum("hqk,qhd->khd", score_grad, query_heads, preferred_element_type=jnp.float32)
-            * inv_root
-        )
-        value_part = jnp.einsum(
-            "hqk,qhd->khd", prob_low, grad_heads, preferred_element_type=jnp.float32
-        )
-        key_parts.append(key_part.reshape(-1, group_width).astype(jnp.bfloat16))
-        value_parts.append(value_part.reshape(-1, group_width).astype(jnp.bfloat16))
-    query_grad = jnp.concatenate(query_parts, axis=1).astype(jnp.bfloat16)
-    partials = jnp.stack([jnp.concatenate(key_parts, axis=1), jnp.concatenate(value_parts, axis=1)])
-    part = [partials[:, slot * rows_own : (slot + 1) * rows_own] for slot in range(len(slots))]
+    forward_mask = allowed(own_rows, far_rows, frame_keep, band_window, frame_len).astype(jnp.int32)
+    inputs = [own, from_core, from_cross, from_below, from_above, relayed, diag_from_below, diag_from_above]
+    slot_in = [(0, ()), (1, ()), (2, ()), (3, ()), (4, ()), (5, (0,)), (5, (1,)), (5, (2,)), (6, ()), (7, ())]
+    out_lead = [(), (4,), (), (), (), (), ()]
+    slot_out = [(0, ()), (1, (0,)), (2, ()), (3, ()), (4, ()), (1, (1,)), (1, (2,)), (1, (3,)), (5, ()), (6, ())]
+    query_grad, outs = attention_backward(
+        forward_mask, queries, out_grad, inputs, slot_in, out_lead, slot_out, inv_root
+    )
+    own_part, to_core, cross_part, below_part, above_part, diag_b_part, diag_a_part = outs
     wide = lambda tensor: tensor.astype(jnp.float32)
-    to_partner = send(jnp.stack([part[1], part[5], part[6], part[7]]), core)
-    diag_back_below = send(part[8], back(diag_up))
-    diag_back_above = send(part[9], back(diag_down))
-    cross_sum = wide(part[2]) + wide(to_partner[1]) + wide(diag_back_below) + wide(diag_back_above)
-    below_sum = wide(part[3]) + wide(to_partner[2])
-    above_sum = wide(part[4]) + wide(to_partner[3])
+    to_partner = send(to_core, core)
+    diag_back_below = send(diag_b_part, back(diag_up))
+    diag_back_above = send(diag_a_part, back(diag_down))
+    cross_sum = wide(cross_part) + wide(to_partner[1]) + wide(diag_back_below) + wide(diag_back_above)
+    below_sum = wide(below_part) + wide(to_partner[2])
+    above_sum = wide(above_part) + wide(to_partner[3])
     got_cross = send(cross_sum.astype(jnp.bfloat16), cross)
     got_below = send(below_sum.astype(jnp.bfloat16), down)
     got_above = send(above_sum.astype(jnp.bfloat16), up)
-    summed = wide(part[0]) + wide(to_partner[0]) + wide(got_cross) + wide(got_below) + wide(got_above)
+    summed = wide(own_part) + wide(to_partner[0]) + wide(got_cross) + wide(got_below) + wide(got_above)
     key_grad = summed[0].astype(jnp.bfloat16)
     value_grad = summed[1].astype(jnp.bfloat16)
     return (query_grad, key_grad, value_grad)

time: 211 us -> 155 us (0.73)
  local copies, waits for them, and re-layouts: 58.3 us -> 1.26 us
  matrix products: 40.9 us -> 0 us
  Pallas kernels: 0 us -> 27.2 us
  waiting for transfers between devices: 69.8 us -> 89 us
  other arithmetic: 17.2 us -> 9.74 us
  starting transfers between devices: 22 us -> 25.6 us
    dot_general x30 -> x0, matrix products: 40.9 us -> none  [the longest x5 12 us: body(): jnp.einsum('hqk,qhd->khd', score_grad, query_heads, preferred_element_typ...]
    unnamed x98 -> x15, local copies, waits for them, and re-layouts: 35.9 us -> 0.12 us
    pallas_call x0 -> x1, Pallas kernels: none -> 27.2 us  [attention_backward(): pl.pallas_call(kernel, grid=(heads,), in_specs=in_specs, out_specs=out_sp...]
    ppermute x13, waiting for transfers between devices: 69.8 us -> 89 us  [send(): return lax.ppermute(value, 'tm', pairs)]
    convert_element_type x5 -> x0, local copies, waits for them, and re-layouts: 12.2 us -> none  [body(): key_parts.append(key_part.reshape(-1, group_width).astype(jnp.bfloat16))]
    slice x4 -> x0, local copies, waits for them, and re-layouts: 7.86 us -> none  [the longest x1 4.72 us: body(): value_heads = value_all[:, lower:upper].reshape(-1, group_heads, HD)]
    another operation x3 -> x1, other arithmetic: 5.71 us -> 0.81 us
    ppermute x13, starting transfers between devices: 22 us -> 25.6 us  [send(): return lax.ppermute(value, 'tm', pairs)]
  transfers between devices with their start and end apart: 13 -> 13, of which waited for: 7 -> 9; matrix products, arithmetic and copies ran while one was open for 13% -> 1% of each run, Pallas kernels for 0% -> 0%
where the time goes in v2:
time: 155 us; the launch traced here: 154 us
  waiting for transfers between devices  89 us (57%)
  Pallas kernels  27.2 us (18%)
  starting transfers between devices  25.6 us (17%)
  other arithmetic  9.74 us (6%)
    ppermute x13, waiting for transfers between devices, send(): return lax.ppermute(value, 'tm', pairs)  89 us
    pallas_call x1, Pallas kernels, attention_backward(): pl.pallas_call(kernel, grid=(heads,), in_specs=in_specs, out_specs=out_sp...  27.2 us
    ppermute x13, starting transfers between devices, send(): return lax.ppermute(value, 'tm', pairs)  25.6 us
    convert_element_type x1, other arithmetic, body(): got_cross = send(cross_sum.astype(jnp.bfloat16), cross)  3.58 us
  transfers between devices with their start and end apart: 13, of which 9 were waited for; matrix products, arithmetic and copies ran while one was open for 1% of the time, Pallas kernels for 0%

profile of v2, /device:TPU:0, one launch (start us, length us, event | category | flops | bytes accessed | tf_op | source)
XLA Modules:
  0.0 153.7 jit_solution(5798313466018600596)
XLA Ops:
  0.6 1.4 pad_maximum_fusion.1.refs_0_
  2.0 0.0 copy-start
  2.0 1.3 collective-permute-start.3
  3.4 5.7 %collective-permute-start.2 = (bf16[2,128,2560]{2,1,0:T(8,128)(2,1)S(1)}, bf16[2,128,2560]{2,1,0:T(8,128)(2,1)S(1)}, u32[]{:S(2)}, u32[]{:S(2)}) collective-permute-start(bf16[2,128,2560]{2,1,0:T(8,128)(2,1)S(1)} %pad_maximum_fusion.1.refs_0_), channel_id=1, source_target_pairs={{0,4},{1,5},{2,6},{3,7},{4,8},{5,9},{6,10},{7,11},{8,12},{9,13},{1... | collective-permute-start | bytes 3932168 | tf_op jit(solution)/shard_map/ppermute | solution.py:14
  9.0 2.0 %collective-permute-start.1 = (bf16[2,128,2560]{2,1,0:T(8,128)(2,1)S(1)}, bf16[2,128,2560]{2,1,0:T(8,128)(2,1)S(1)}, u32[]{:S(2)}, u32[]{:S(2)}) collective-permute-start(bf16[2,128,2560]{2,1,0:T(8,128)(2,1)S(1)} %pad_maximum_fusion.1.refs_0_), channel_id=1, source_target_pairs={{0,2},{1,3},{2,0},{3,1},{4,6},{5,7},{6,4},{7,5},{8,10},{9,11},{10,... | collective-permute-start | bytes 3932168 | tf_op jit(solution)/shard_map/ppermute | solution.py:14
  11.0 24.7 %collective-permute-done.3.refs_4_ = bf16[2,128,2560]{2,1,0:T(8,128)(2,1)S(1)} collective-permute-done((bf16[2,128,2560]{2,1,0:T(8,128)(2,1)S(1)}, bf16[2,128,2560]{2,1,0:T(8,128)(2,1)S(1)}, u32[]{:S(2)}, u32[]{:S(2)}) %collective-permute-start.3) | collective-permute-done | bytes 1310752 | tf_op jit(solution)/shard_map/ppermute | solution.py:14
  35.8 0.0 copy-start.1
  35.8 1.2 collective-permute-done.2.refs_3_
  37.0 0.0 copy-start.2
  37.0 2.4 %collective-permute-done.1.refs_2_ = bf16[2,128,2560]{2,1,0:T(8,128)(2,1)S(1)} collective-permute-done((bf16[2,128,2560]{2,1,0:T(8,128)(2,1)S(1)}, bf16[2,128,2560]{2,1,0:T(8,128)(2,1)S(1)}, u32[]{:S(2)}, u32[]{:S(2)}) %collective-permute-start.1) | collective-permute-done | bytes 1310752 | tf_op jit(solution)/shard_map/ppermute | solution.py:14
  39.3 0.0 copy-start.3
  39.3 0.0 copy-start.6
  39.3 0.0 copy-start.5
  39.3 2.3 %pad_maximum_fusion = bf16[3,2,128,2560]{3,2,1,0:T(8,128)(2,1)} fusion(bf16[1,2,128,2560]{3,2,1,0:T(8,128)(2,1)S(1)} %bitcast.35, bf16[1,2,128,2560]{3,2,1,0:T(8,128)(2,1)S(1)} %bitcast.36, bf16[1,2,128,2560]{3,2,1,0:T(8,128)(2,1)S(1)} %bitcast.37), kind=kLoop, calls=%fused_computation | loop fusion | flops 3932160 | bytes 7864320 | tf_op jit(solution)/shard_map/stack | solution.py:147
  41.6 0.0 copy-done.1
  41.6 0.0 copy-done.2
  41.6 0.0 collective-permute-start.4
  41.6 0.0 copy-done
  41.6 0.5 collective-permute-start
  42.3 0.0 copy-done.6
  42.3 0.1 select_reduce_fusion
  42.4 1.7 %collective-permute-start.6 = (bf16[2,128,2560]{2,1,0:T(8,128)(2,1)S(1)}, bf16[2,128,2560]{2,1,0:T(8,128)(2,1)}, u32[]{:S(2)}, u32[]{:S(2)}) collective-permute-start(bf16[2,128,2560]{2,1,0:T(8,128)(2,1)S(1)} %collective-permute-done.1.refs_2_), channel_id=1, source_target_pairs={{4,1},{7,2},{8,5},{11,6},{12,9},{15,10},{20,17},{23,18},{24,21},{2... | collective-permute-start | bytes 3932168 | tf_op jit(solution)/shard_map/ppermute | solution.py:14
  44.1 0.0 copy-done.3
  44.1 3.9 %collective-permute-start.5 = (bf16[2,128,2560]{2,1,0:T(8,128)(2,1)S(1)}, bf16[2,128,2560]{2,1,0:T(8,128)(2,1)}, u32[]{:S(2)}, u32[]{:S(2)}) collective-permute-start(bf16[2,128,2560]{2,1,0:T(8,128)(2,1)S(1)} %collective-permute-done.1.refs_2_), channel_id=1, source_target_pairs={{0,5},{3,6},{4,9},{7,10},{8,13},{11,14},{16,21},{19,22},{20,25},{2... | collective-permute-start | bytes 3932168 | tf_op jit(solution)/shard_map/ppermute | solution.py:14
  48.0 0.0 copy-done.5
  48.0 0.1 copy.9
  48.1 0.1 multiply_reduce_fusion
  48.2 1.4 fusion.15.mask_ref
  49.6 1.0 collective-permute-done.refs_1_
  50.6 0.0 collective-permute-done.6.refs_7_
  50.6 11.4 %collective-permute-done.5.refs_6_ = bf16[2,128,2560]{2,1,0:T(8,128)(2,1)} collective-permute-done((bf16[2,128,2560]{2,1,0:T(8,128)(2,1)S(1)}, bf16[2,128,2560]{2,1,0:T(8,128)(2,1)}, u32[]{:S(2)}, u32[]{:S(2)}) %collective-permute-start.5) | collective-permute-done | bytes 1310752 | tf_op jit(solution)/shard_map/ppermute | solution.py:14
  62.0 0.0 collective-permute-done.4.refs_5_
  62.0 27.2 %shard_map.85 = (bf16[128,2560]{1,0:T(8,128)(2,1)}, bf16[2,128,2560]{2,1,0:T(8,128)(2,1)}, bf16[4,2,128,2560]{3,2,1,0:T(8,128)(2,1)}, bf16[2,128,2560]{2,1,0:T(8...) custom-call(s32[128,1280]{1,0:T(8,128)} %fusion.15.mask_ref, ...), custom_call_target="tpu_custom_call" | custom-call | tf_op jit(solution)/shard_map/pallas_call | solution.py:122
  89.2 0.1 collective-permute-start.7
  89.3 1.3 collective-permute-start.8
  90.6 0.7 collective-permute-start.9
  91.4 17.1 %collective-permute-done.8 = bf16[2,128,2560]{2,1,0:T(8,128)(2,1)S(1)} collective-permute-done((bf16[2,128,2560]{2,1,0:T(8,128)(2,1)}, bf16[2,128,2560]{2,1,0:T(8,128)(2,1)S(1)}, u32[]{:S(2)}, u32[]{:S(2)}) %collective-permute-start.8) | collective-permute-done | bytes 1310752 | tf_op jit(solution)/shard_map/ppermute | solution.py:14
  108.4 0.0 collective-permute-done.9
  108.4 0.0 collective-permute-done.7
  108.4 0.0 copy-start.4
  108.5 3.6 %fusion.4 = (bf16[2,128,2560]{2,1,0:T(8,128)(2,1)S(1)}, bf16[2,128,2560]{2,1,0:T(8,128)(2,1)S(1)}, bf16[2,128,2560]{2,1,0:T(8,128)(2,1)S(1)}) fusion(bf16[2,128,2560]{2,1,0:T(8,128)(2,1)S(1)} %collective-permute-done.9, bf16[2,128,2560]{2,1,0:T(8,128)(2,1)S(1)} %collective-permute-done.8, bf16[2,128,2560]{2,1,0:T(8,128)(2,1)} %get-tuple-element.14, ...), kind=kLoop, calls=%fused_computation.8 | loop fusion | flops 10485760 | bytes 14417920 | tf_op jit(solution)/shard_map/convert_element_type | solution.py:186
  112.0 3.5 %collective-permute-start.10 = (bf16[2,128,2560]{2,1,0:T(8,128)(2,1)S(1)}, bf16[2,128,2560]{2,1,0:T(8,128)(2,1)S(1)}, u32[]{:S(2)}, u32[]{:S(2)}) collective-permute-start(bf16[2,128,2560]{2,1,0:T(8,128)(2,1)S(1)} %get-tuple-element.19), channel_id=1, source_target_pairs={{0,2},{1,3},{2,0},{3,1},{4,6},{5,7},{6,4},{7,5},{8,10},{9,11},{10,... | collective-permute-start | bytes 3932168 | tf_op jit(solution)/shard_map/ppermute | solution.py:14
  115.5 3.6 %collective-permute-start.12 = (bf16[2,128,2560]{2,1,0:T(8,128)(2,1)S(1)}, bf16[2,128,2560]{2,1,0:T(8,128)(2,1)S(1)}, u32[]{:S(2)}, u32[]{:S(2)}) collective-permute-start(bf16[2,128,2560]{2,1,0:T(8,128)(2,1)S(1)} %get-tuple-element.20), channel_id=1, source_target_pairs={{0,4},{1,5},{2,6},{3,7},{4,8},{5,9},{6,10},{7,11},{8,12},{9,13},{1... | collective-permute-start | bytes 3932168 | tf_op jit(solution)/shard_map/ppermute | solution.py:14
  119.2 1.3 collective-permute-start.11
  120.5 23.7 %collective-permute-done.10 = bf16[2,128,2560]{2,1,0:T(8,128)(2,1)S(1)} collective-permute-done((bf16[2,128,2560]{2,1,0:T(8,128)(2,1)S(1)}, bf16[2,128,2560]{2,1,0:T(8,128)(2,1)S(1)}, u32[]{:S(2)}, u32[]{:S(2)}) %collective-permute-start.10) | collective-permute-done | bytes 1310752 | tf_op jit(solution)/shard_map/ppermute | solution.py:14
  144.2 3.3 %collective-permute-done.12 = bf16[2,128,2560]{2,1,0:T(8,128)(2,1)S(1)} collective-permute-done((bf16[2,128,2560]{2,1,0:T(8,128)(2,1)S(1)}, bf16[2,128,2560]{2,1,0:T(8,128)(2,1)S(1)}, u32[]{:S(2)}, u32[]{:S(2)}) %collective-permute-start.12) | collective-permute-done | bytes 1310752 | tf_op jit(solution)/shard_map/ppermute | solution.py:14
  147.5 4.2 %collective-permute-done.11 = bf16[2,128,2560]{2,1,0:T(8,128)(2,1)S(1)} collective-permute-done((bf16[2,128,2560]{2,1,0:T(8,128)(2,1)S(1)}, bf16[2,128,2560]{2,1,0:T(8,128)(2,1)S(1)}, u32[]{:S(2)}, u32[]{:S(2)}) %collective-permute-start.11) | collective-permute-done | bytes 1310752 | tf_op jit(solution)/shard_map/ppermute | solution.py:14
  151.7 0.0 copy-done.4
  151.7 0.8 fusion.8
  152.5 1.1 slice_bitcast_fusion.4
  (17 shorter events, 0.1 us)
Async XLA Ops:
  2.0 39.6 %copy-start = (bf16[2,128,2560]{2,1,0:T(8,128)(2,1)}, bf16[2,128,2560]{2,1,0:T(8,128)(2,1)S(1)}, u32[]{:S(2)}) copy-start(bf16[2,128,2560]{2,1,0:T(8,128)(2,1)S(1)} %pad_maximum_fusion.1.refs_0_) | copy-start | bytes 3932164
  2.0 33.7 %collective-permute-start.3 = (bf16[2,128,2560]{2,1,0:T(8,128)(2,1)S(1)}, bf16[2,128,2560]{2,1,0:T(8,128)(2,1)S(1)}, u32[]{:S(2)}, u32[]{:S(2)}) collective-permute-start(bf16[2,128,2560]{2,1,0:T(8,128)(2,1)S(1)} %pad_maximum_fusion.1.refs_0_), channel_id=1, source_target_pairs={{4,0},{5,1},{6,2},{7,3},{8,4},{9,5},{10,6},{11,7},{12,8},{13,9},{1... | collective-permute-start | bytes 3932168 | tf_op jit(solution)/shard_map/ppermute | solution.py:14
  3.4 33.6 %collective-permute-start.2 = (bf16[2,128,2560]{2,1,0:T(8,128)(2,1)S(1)}, bf16[2,128,2560]{2,1,0:T(8,128)(2,1)S(1)}, u32[]{:S(2)}, u32[]{:S(2)}) collective-permute-start(bf16[2,128,2560]{2,1,0:T(8,128)(2,1)S(1)} %pad_maximum_fusion.1.refs_0_), channel_id=1, source_target_pairs={{0,4},{1,5},{2,6},{3,7},{4,8},{5,9},{6,10},{7,11},{8,12},{9,13},{1... | collective-permute-start | bytes 3932168 | tf_op jit(solution)/shard_map/ppermute | solution.py:14
  9.0 30.3 %collective-permute-start.1 = (bf16[2,128,2560]{2,1,0:T(8,128)(2,1)S(1)}, bf16[2,128,2560]{2,1,0:T(8,128)(2,1)S(1)}, u32[]{:S(2)}, u32[]{:S(2)}) collective-permute-start(bf16[2,128,2560]{2,1,0:T(8,128)(2,1)S(1)} %pad_maximum_fusion.1.refs_0_), channel_id=1, source_target_pairs={{0,2},{1,3},{2,0},{3,1},{4,6},{5,7},{6,4},{7,5},{8,10},{9,11},{10,... | collective-permute-start | bytes 3932168 | tf_op jit(solution)/shard_map/ppermute | solution.py:14
  35.8 5.8 %copy-start.1 = (bf16[2,128,2560]{2,1,0:T(8,128)(2,1)}, bf16[2,128,2560]{2,1,0:T(8,128)(2,1)S(1)}, u32[]{:S(2)}) copy-start(bf16[2,128,2560]{2,1,0:T(8,128)(2,1)S(1)} %collective-permute-done.3.refs_4_) | copy-start | bytes 3932164
  37.0 4.6 %copy-start.2 = (bf16[2,128,2560]{2,1,0:T(8,128)(2,1)}, bf16[2,128,2560]{2,1,0:T(8,128)(2,1)S(1)}, u32[]{:S(2)}) copy-start(bf16[2,128,2560]{2,1,0:T(8,128)(2,1)S(1)} %collective-permute-done.2.refs_3_) | copy-start | bytes 3932164
  39.3 4.8 %copy-start.3 = (bf16[2,128,2560]{2,1,0:T(8,128)(2,1)}, bf16[2,128,2560]{2,1,0:T(8,128)(2,1)S(1)}, u32[]{:S(2)}) copy-start(bf16[2,128,2560]{2,1,0:T(8,128)(2,1)S(1)} %collective-permute-done.1.refs_2_) | copy-start | bytes 3932164
  39.3 2.9 %copy-start.6 = (s32[4]{0:T(128)S(1)}, s32[4]{0:T(128)}, u32[]{:S(2)}) copy-start(s32[4]{0:T(128)} %param.11) | copy-start | bytes 52
  39.3 8.6 %copy-start.5 = (s32[4,3]{1,0:T(4,128)S(1)}, s32[4,3]{1,0:T(4,128)}, u32[]{:S(2)}) copy-start(s32[4,3]{1,0:T(4,128)} %param.10) | copy-start | bytes 148
  41.6 20.4 %collective-permute-start.4 = (bf16[3,2,128,2560]{3,2,1,0:T(8,128)(2,1)}, bf16[3,2,128,2560]{3,2,1,0:T(8,128)(2,1)}, u32[]{:S(2)}, u32[]{:S(2)}) collective-permute-start(bf16[3,2,128,2560]{3,2,1,0:T(8,128)(2,1)} %pad_maximum_fusion), channel_id=1, source_target_pairs={{0,1},{1,0},{2,3},{3,2},{4,5},{5,4},{6,7},{7,6},{8,9},{9,8},{10,11... | collective-permute-start | bytes 11796488 | tf_op jit(solution)/shard_map/ppermute | solution.py:14
  41.6 9.0 %collective-permute-start = (bf16[2,128,2560]{2,1,0:T(8,128)(2,1)S(1)}, bf16[2,128,2560]{2,1,0:T(8,128)(2,1)}, u32[]{:S(2)}, u32[]{:S(2)}) collective-permute-start(bf16[2,128,2560]{2,1,0:T(8,128)(2,1)S(1)} %pad_maximum_fusion.1.refs_0_), channel_id=1, source_target_pairs={{0,1},{1,0},{2,3},{3,2},{4,5},{5,4},{6,7},{7,6},{8,9},{9,8},{10,11... | collective-permute-start | bytes 3932168 | tf_op jit(solution)/shard_map/ppermute | solution.py:14
  42.4 8.2 %collective-permute-start.6 = (bf16[2,128,2560]{2,1,0:T(8,128)(2,1)S(1)}, bf16[2,128,2560]{2,1,0:T(8,128)(2,1)}, u32[]{:S(2)}, u32[]{:S(2)}) collective-permute-start(bf16[2,128,2560]{2,1,0:T(8,128)(2,1)S(1)} %collective-permute-done.1.refs_2_), channel_id=1, source_target_pairs={{4,1},{7,2},{8,5},{11,6},{12,9},{15,10},{20,17},{23,18},{24,21},{2... | collective-permute-start | bytes 3932168 | tf_op jit(solution)/shard_map/ppermute | solution.py:14
  44.1 17.9 %collective-permute-start.5 = (bf16[2,128,2560]{2,1,0:T(8,128)(2,1)S(1)}, bf16[2,128,2560]{2,1,0:T(8,128)(2,1)}, u32[]{:S(2)}, u32[]{:S(2)}) collective-permute-start(bf16[2,128,2560]{2,1,0:T(8,128)(2,1)S(1)} %collective-permute-done.1.refs_2_), channel_id=1, source_target_pairs={{0,5},{3,6},{4,9},{7,10},{8,13},{11,14},{16,21},{19,22},{20,25},{2... | collective-permute-start | bytes 3932168 | tf_op jit(solution)/shard_map/ppermute | solution.py:14
  89.2 19.2 %collective-permute-start.7 = (bf16[4,2,128,2560]{3,2,1,0:T(8,128)(2,1)}, bf16[4,2,128,2560]{3,2,1,0:T(8,128)(2,1)S(1)}, u32[]{:S(2)}, u32[]{:S(2)}) collective-permute-start(bf16[4,2,128,2560]{3,2,1,0:T(8,128)(2,1)} %get-tuple-element.13), channel_id=1, source_target_pairs={{0,1},{1,0},{2,3},{3,2},{4,5},{5,4},{6,7},{7,6},{8,9},{9,8},{10,11... | collective-permute-start | bytes 15728648 | tf_op jit(solution)/shard_map/ppermute | solution.py:14
  89.3 19.1 %collective-permute-start.8 = (bf16[2,128,2560]{2,1,0:T(8,128)(2,1)}, bf16[2,128,2560]{2,1,0:T(8,128)(2,1)S(1)}, u32[]{:S(2)}, u32[]{:S(2)}) collective-permute-start(bf16[2,128,2560]{2,1,0:T(8,128)(2,1)} %get-tuple-element.15), channel_id=1, source_target_pairs={{5,0},{6,3},{9,4},{10,7},{13,8},{14,11},{21,16},{22,19},{25,20},{2... | collective-permute-start | bytes 3932168 | tf_op jit(solution)/shard_map/ppermute | solution.py:14
  90.6 17.8 %collective-permute-start.9 = (bf16[2,128,2560]{2,1,0:T(8,128)(2,1)}, bf16[2,128,2560]{2,1,0:T(8,128)(2,1)S(1)}, u32[]{:S(2)}, u32[]{:S(2)}) collective-permute-start(bf16[2,128,2560]{2,1,0:T(8,128)(2,1)} %get-tuple-element.16), channel_id=1, source_target_pairs={{1,4},{2,7},{5,8},{6,11},{9,12},{10,15},{17,20},{18,23},{21,24},{2... | collective-permute-start | bytes 3932168 | tf_op jit(solution)/shard_map/ppermute | solution.py:14
  108.4 43.3 %copy-start.4 = (bf16[2,128,2560]{2,1,0:T(8,128)(2,1)S(1)}, bf16[2,128,2560]{2,1,0:T(8,128)(2,1)}, u32[]{:S(2)}) copy-start(bf16[2,128,2560]{2,1,0:T(8,128)(2,1)} %get-tuple-element.12) | copy-start | bytes 3932164
  112.0 32.2 %collective-permute-start.10 = (bf16[2,128,2560]{2,1,0:T(8,128)(2,1)S(1)}, bf16[2,128,2560]{2,1,0:T(8,128)(2,1)S(1)}, u32[]{:S(2)}, u32[]{:S(2)}) collective-permute-start(bf16[2,128,2560]{2,1,0:T(8,128)(2,1)S(1)} %get-tuple-element.19), channel_id=1, source_target_pairs={{0,2},{1,3},{2,0},{3,1},{4,6},{5,7},{6,4},{7,5},{8,10},{9,11},{10,... | collective-permute-start | bytes 3932168 | tf_op jit(solution)/shard_map/ppermute | solution.py:14
  115.5 32.0 %collective-permute-start.12 = (bf16[2,128,2560]{2,1,0:T(8,128)(2,1)S(1)}, bf16[2,128,2560]{2,1,0:T(8,128)(2,1)S(1)}, u32[]{:S(2)}, u32[]{:S(2)}) collective-permute-start(bf16[2,128,2560]{2,1,0:T(8,128)(2,1)S(1)} %get-tuple-element.20), channel_id=1, source_target_pairs={{0,4},{1,5},{2,6},{3,7},{4,8},{5,9},{6,10},{7,11},{8,12},{9,13},{1... | collective-permute-start | bytes 3932168 | tf_op jit(solution)/shard_map/ppermute | solution.py:14
  119.2 32.6 %collective-permute-start.11 = (bf16[2,128,2560]{2,1,0:T(8,128)(2,1)S(1)}, bf16[2,128,2560]{2,1,0:T(8,128)(2,1)S(1)}, u32[]{:S(2)}, u32[]{:S(2)}) collective-permute-start(bf16[2,128,2560]{2,1,0:T(8,128)(2,1)S(1)} %get-tuple-element.21), channel_id=1, source_target_pairs={{4,0},{5,1},{6,2},{7,3},{8,4},{9,5},{10,6},{11,7},{12,8},{13,9},{1... | collective-permute-start | bytes 3932168 | tf_op jit(solution)/shard_map/ppermute | solution.py:14

commit v3 on v2

--- a/solution.py
+++ b/solution.py
@@ -8,6 +8,7 @@
 
 HD = 128
 QUARTERS = 4
+CHUNKS = 2
 
 
 def send(value, pairs):
@@ -71,8 +72,8 @@
     return inside & (kept_pair > 0) & nearby
 
 
-def attention_backward(mask, queries, out_grad, inputs, slot_in, out_lead, slot_out, inv_root):
-    rows, channels = queries.shape
+def attention_backward(mask, queries, out_grad, inputs, slot_in, out_lead, slot_out, inv_root, offset):
+    rows, channels = inputs[0].shape[-2:]
     heads = channels // HD
     slots = len(slot_in)
     n_in = len(inputs)
@@ -112,8 +113,8 @@
 
     in_specs = [
         pl.BlockSpec((rows, slots * rows), lambda h: (0, 0)),
-        pl.BlockSpec((rows, HD), lambda h: (0, h)),
-        pl.BlockSpec((rows, HD), lambda h: (0, h)),
+        pl.BlockSpec((rows, HD), lambda h: (0, h + offset)),
+        pl.BlockSpec((rows, HD), lambda h: (0, h + offset)),
     ] + [head_spec(tuple(x.shape[:-3])) for x in inputs]
     out_specs = [pl.BlockSpec((rows, HD), lambda h: (0, h))] + [head_spec(lead) for lead in out_lead]
     out_shape = [jax.ShapeDtypeStruct((rows, channels), jnp.bfloat16)] + [
@@ -125,20 +126,17 @@
         in_specs=in_specs,
         out_specs=out_specs,
         out_shape=out_shape,
+        cost_estimate=pl.CostEstimate(
+            flops=12 * heads * rows * slots * rows * HD,
+            transcendentals=2 * heads * rows * slots * rows,
+            bytes_accessed=2 * 4 * slots * rows * channels + 6 * rows * channels + 4 * rows * slots * rows,
+        ),
     )(mask, queries, out_grad, *inputs)
     return results[0], results[1:]
 
 
-def body(queries, keys, values, out_grad, frame_keep, band_window):
-    rows_own, channel_total = queries.shape
-    frame_len = QUARTERS * rows_own
-    inv_root = 1.0 / math.sqrt(HD)
-    count = lax.axis_size("tm")
+def exchange_chunk(forward_mask, queries, out_grad, keys, values, head_offset, inv_root, count):
     core, cross, down, up, diag_up, diag_down, back = route(count)
-    device = lax.axis_index("tm")
-    quarter = device % QUARTERS
-    partner = device ^ 1
-
     own = jnp.stack([keys, values])
     from_core = send(own, core)
     from_cross = send(own, cross)
@@ -147,8 +145,37 @@
     relayed = send(jnp.stack([from_cross, from_below, from_above]), core)
     diag_from_below = send(from_cross, diag_up)
     diag_from_above = send(from_cross, diag_down)
-    slots = [own, from_core, from_cross, from_below, from_above,
-             relayed[0], relayed[1], relayed[2], diag_from_below, diag_from_above]
+    inputs = [own, from_core, from_cross, from_below, from_above, relayed, diag_from_below, diag_from_above]
+    slot_in = [(0, ()), (1, ()), (2, ()), (3, ()), (4, ()), (5, (0,)), (5, (1,)), (5, (2,)), (6, ()), (7, ())]
+    out_lead = [(), (4,), (), (), (), (), ()]
+    slot_out = [(0, ()), (1, (0,)), (2, ()), (3, ()), (4, ()), (1, (1,)), (1, (2,)), (1, (3,)), (5, ()), (6, ())]
+    query_grad, outs = attention_backward(
+        forward_mask, queries, out_grad, inputs, slot_in, out_lead, slot_out, inv_root, head_offset
+    )
+    own_part, to_core, cross_part, below_part, above_part, diag_b_part, diag_a_part = outs
+    wide = lambda tensor: tensor.astype(jnp.float32)
+    to_partner = send(to_core, core)
+    diag_back_below = send(diag_b_part, back(diag_up))
+    diag_back_above = send(diag_a_part, back(diag_down))
+    cross_sum = wide(cross_part) + wide(to_partner[1]) + wide(diag_back_below) + wide(diag_back_above)
+    below_sum = wide(below_part) + wide(to_partner[2])
+    above_sum = wide(above_part) + wide(to_partner[3])
+    got_cross = send(cross_sum.astype(jnp.bfloat16), cross)
+    got_below = send(below_sum.astype(jnp.bfloat16), down)
+    got_above = send(above_sum.astype(jnp.bfloat16), up)
+    summed = wide(own_part) + wide(to_partner[0]) + wide(got_cross) + wide(got_below) + wide(got_above)
+    return query_grad, summed[0].astype(jnp.bfloat16), summed[1].astype(jnp.bfloat16)
+
+
+def body(queries, keys, values, out_grad, frame_keep, band_window):
+    rows_own, channel_total = queries.shape
+    frame_len = QUARTERS * rows_own
+    inv_root = 1.0 / math.sqrt(HD)
+    count = lax.axis_size("tm")
+    device = lax.axis_index("tm")
+    quarter = device % QUARTERS
+    partner = device ^ 1
+
     middle = (quarter == 1) | (quarter == 2)
     diag_quarter = QUARTERS - 1 - quarter
     absent = jnp.int32(-(1 << 20))
@@ -168,27 +195,20 @@
     far_rows = jnp.concatenate([source * rows_own + base_rows for source in sources])
     own_rows = device * rows_own + base_rows
     forward_mask = allowed(own_rows, far_rows, frame_keep, band_window, frame_len).astype(jnp.int32)
-    inputs = [own, from_core, from_cross, from_below, from_above, relayed, diag_from_below, diag_from_above]
-    slot_in = [(0, ()), (1, ()), (2, ()), (3, ()), (4, ()), (5, (0,)), (5, (1,)), (5, (2,)), (6, ()), (7, ())]
-    out_lead = [(), (4,), (), (), (), (), ()]
-    slot_out = [(0, ()), (1, (0,)), (2, ()), (3, ()), (4, ()), (1, (1,)), (1, (2,)), (1, (3,)), (5, ()), (6, ())]
-    query_grad, outs = attention_backward(
-        forward_mask, queries, out_grad, inputs, slot_in, out_lead, slot_out, inv_root
-    )
-    own_part, to_core, cross_part, below_part, above_part, diag_b_part, diag_a_part = outs
-    wide = lambda tensor: tensor.astype(jnp.float32)
-    to_partner = send(to_core, core)
-    diag_back_below = send(diag_b_part, back(diag_up))
-    diag_back_above = send(diag_a_part, back(diag_down))
-    cross_sum = wide(cross_part) + wide(to_partner[1]) + wide(diag_back_below) + wide(diag_back_above)
-    below_sum = wide(below_part) + wide(to_partner[2])
-    above_sum = wide(above_part) + wide(to_partner[3])
-    got_cross = send(cross_sum.astype(jnp.bfloat16), cross)
-    got_below = send(below_sum.astype(jnp.bfloat16), down)
-    got_above = send(above_sum.astype(jnp.bfloat16), up)
-    summed = wide(own_part) + wide(to_partner[0]) + wide(got_cross) + wide(got_below) + wide(got_above)
-    key_grad = summed[0].astype(jnp.bfloat16)
-    value_grad = summed[1].astype(jnp.bfloat16)
+    heads = channel_total // HD
+    chunk_heads = heads // CHUNKS if heads % CHUNKS == 0 else heads
+    width = chunk_heads * HD
+    grads = []
+    for first in range(0, channel_total, width):
+        grads.append(
+            exchange_chunk(
+                forward_mask, queries, out_grad, keys[:, first : first + width],
+                values[:, first : first + width], first // HD, inv_root, count,
+            )
+        )
+    query_grad = jnp.concatenate([grad[0] for grad in grads], axis=1)
+    key_grad = jnp.concatenate([grad[1] for grad in grads], axis=1)
+    value_grad = jnp.concatenate([grad[2] for grad in grads], axis=1)
     return (query_grad, key_grad, value_grad)
 
 

time: 155 us -> 148 us (0.955)
  waiting for transfers between devices: 89 us -> 54.4 us
  starting transfers between devices: 25.6 us -> 47.3 us
  other arithmetic: 9.74 us -> 12.5 us
  Pallas kernels: 27.2 us -> 29.8 us
    ppermute x13 -> x26, waiting for transfers between devices: 89 us -> 54.4 us  [send(): return lax.ppermute(value, 'tm', pairs)]
    ppermute x13 -> x26, starting transfers between devices: 25.6 us -> 47.3 us  [send(): return lax.ppermute(value, 'tm', pairs)]
    concatenate x0 -> x3, other arithmetic: none -> 3.71 us  [the longest x1 1.95 us: body(): query_grad = jnp.concatenate([grad[0] for grad in grads], axis=1)]
    pallas_call x1 -> x2, Pallas kernels: 27.2 us -> 29.8 us  [attention_backward(): pl.pallas_call(kernel, grid=(heads,), in_specs=in_specs, out_specs=out_sp...]
    convert_element_type x1 -> x2, other arithmetic: 3.58 us -> 1.4 us  [exchange_chunk(): got_cross = send(cross_sum.astype(jnp.bfloat16), cross)]
    another operation x3 -> x6, other arithmetic: 4.47 us -> 5.69 us  [the longest x2 4.72 us: exchange_chunk(): relayed = send(jnp.stack([from_cross, from_below, from_above]), core)]
  transfers between devices with their start and end apart: 13 -> 26, of which waited for: 9 -> 15; matrix products, arithmetic and copies ran while one was open for 1% -> 7% of each run, Pallas kernels for 0% -> 20%
where the time goes in v3:
time: 148 us; the launch traced here: 147 us
  waiting for transfers between devices  54.4 us (37%)
  starting transfers between devices  47.3 us (32%)
  Pallas kernels  29.8 us (20%)
  other arithmetic  12.5 us (8%)
  local copies, waits for them, and re-layouts  1.6 us (1%)
    ppermute x26, waiting for transfers between devices, send(): return lax.ppermute(value, 'tm', pairs)  54.4 us
    ppermute x26, starting transfers between devices, send(): return lax.ppermute(value, 'tm', pairs)  47.3 us
    pallas_call x2, Pallas kernels, attention_backward(): pl.pallas_call(kernel, grid=(heads,), in_specs=in_specs, out_specs=out_sp...  29.8 us
    another operation x2, other arithmetic, exchange_chunk(): relayed = send(jnp.stack([from_cross, from_below, from_above]), core)  4.72 us
  transfers between devices with their start and end apart: 26, of which 15 were waited for; matrix products, arithmetic and copies ran while one was open for 7% of the time, Pallas kernels for 20%

profile of v3, /device:TPU:0, one launch (start us, length us, event | category | flops | bytes accessed | tf_op | source)
XLA Modules:
  0.0 146.7 jit_solution(645915871290396043)
XLA Ops:
  0.6 1.4 slice_bitcast_fusion.14
  2.0 0.0 copy-start.11
  2.0 0.1 pad_maximum_fusion.2.refs_0_
  2.1 0.0 copy-start.7
  2.1 3.1 %collective-permute-start.1 = (bf16[2,128,1280]{2,1,0:T(8,128)(2,1)S(1)}, bf16[2,128,1280]{2,1,0:T(8,128)(2,1)}, u32[]{:S(2)}, u32[]{:S(2)}) collective-permute-start(bf16[2,128,1280]{2,1,0:T(8,128)(2,1)S(1)} %pad_maximum_fusion.2.refs_0_), channel_id=1, source_target_pairs={{0,2},{1,3},{2,0},{3,1},{4,6},{5,7},{6,4},{7,5},{8,10},{9,11},{10,... | collective-permute-start | bytes 1966088 | tf_op jit(solution)/shard_map/ppermute | solution.py:15
  5.1 4.3 %collective-permute-start.2 = (bf16[2,128,1280]{2,1,0:T(8,128)(2,1)S(1)}, bf16[2,128,1280]{2,1,0:T(8,128)(2,1)}, u32[]{:S(2)}, u32[]{:S(2)}) collective-permute-start(bf16[2,128,1280]{2,1,0:T(8,128)(2,1)S(1)} %pad_maximum_fusion.2.refs_0_), channel_id=1, source_target_pairs={{0,4},{1,5},{2,6},{3,7},{4,8},{5,9},{6,10},{7,11},{8,12},{9,13},{1... | collective-permute-start | bytes 1966088 | tf_op jit(solution)/shard_map/ppermute | solution.py:15
  9.5 1.3 collective-permute-start.3
  10.8 0.1 pad_maximum_fusion.3.refs_0_
  10.8 0.0 copy-start.6
  10.9 0.6 collective-permute-start.8
  11.4 5.4 %collective-permute-start.9 = (bf16[2,128,1280]{2,1,0:T(8,128)(2,1)S(1)}, bf16[2,128,1280]{2,1,0:T(8,128)(2,1)}, u32[]{:S(2)}, u32[]{:S(2)}) collective-permute-start(bf16[2,128,1280]{2,1,0:T(8,128)(2,1)S(1)} %pad_maximum_fusion.3.refs_0_), channel_id=1, source_target_pairs={{0,4},{1,5},{2,6},{3,7},{4,8},{5,9},{6,10},{7,11},{8,12},{9,13},{1... | collective-permute-start | bytes 1966088 | tf_op jit(solution)/shard_map/ppermute | solution.py:15
  16.9 0.1 select_reduce_fusion
  17.0 3.8 %collective-permute-done.1.refs_2_ = bf16[2,128,1280]{2,1,0:T(8,128)(2,1)} collective-permute-done((bf16[2,128,1280]{2,1,0:T(8,128)(2,1)S(1)}, bf16[2,128,1280]{2,1,0:T(8,128)(2,1)}, u32[]{:S(2)}, u32[]{:S(2)}) %collective-permute-start.1) | collective-permute-done | bytes 655392 | tf_op jit(solution)/shard_map/ppermute | solution.py:15
  20.8 1.3 collective-permute-start.10
  22.2 1.6 %collective-permute-done.2.refs_3_ = bf16[2,128,1280]{2,1,0:T(8,128)(2,1)} collective-permute-done((bf16[2,128,1280]{2,1,0:T(8,128)(2,1)S(1)}, bf16[2,128,1280]{2,1,0:T(8,128)(2,1)}, u32[]{:S(2)}, u32[]{:S(2)}) %collective-permute-start.2) | collective-permute-done | bytes 655392 | tf_op jit(solution)/shard_map/ppermute | solution.py:15
  23.7 5.3 %collective-permute-done.3.refs_4_ = bf16[2,128,1280]{2,1,0:T(8,128)(2,1)} collective-permute-done((bf16[2,128,1280]{2,1,0:T(8,128)(2,1)S(1)}, bf16[2,128,1280]{2,1,0:T(8,128)(2,1)}, u32[]{:S(2)}, u32[]{:S(2)}) %collective-permute-start.3) | collective-permute-done | bytes 655392 | tf_op jit(solution)/shard_map/ppermute | solution.py:15
  29.1 1.7 %pad_maximum_fusion = bf16[3,2,128,1280]{3,2,1,0:T(8,128)(2,1)S(1)} fusion(bf16[1,2,128,1280]{3,2,1,0:T(8,128)(2,1)} %bitcast.7, bf16[1,2,128,1280]{3,2,1,0:T(8,128)(2,1)} %bitcast.6, bf16[1,2,128,1280]{3,2,1,0:T(8,128)(2,1)} %bitcast.5), kind=kLoop, calls=%fused_computation | loop fusion | flops 1966080 | bytes 3932160 | tf_op jit(solution)/shard_map/stack | solution.py:145
  30.8 0.1 collective-permute-start.4
  30.9 3.1 %collective-permute-done.8.refs_2_ = bf16[2,128,1280]{2,1,0:T(8,128)(2,1)} collective-permute-done((bf16[2,128,1280]{2,1,0:T(8,128)(2,1)S(1)}, bf16[2,128,1280]{2,1,0:T(8,128)(2,1)}, u32[]{:S(2)}, u32[]{:S(2)}) %collective-permute-start.8) | collective-permute-done | bytes 655392 | tf_op jit(solution)/shard_map/ppermute | solution.py:15
  34.0 2.3 %collective-permute-done.9.refs_3_ = bf16[2,128,1280]{2,1,0:T(8,128)(2,1)} collective-permute-done((bf16[2,128,1280]{2,1,0:T(8,128)(2,1)S(1)}, bf16[2,128,1280]{2,1,0:T(8,128)(2,1)}, u32[]{:S(2)}, u32[]{:S(2)}) %collective-permute-start.9) | collective-permute-done | bytes 655392 | tf_op jit(solution)/shard_map/ppermute | solution.py:15
  36.4 5.1 %collective-permute-done.10.refs_4_ = bf16[2,128,1280]{2,1,0:T(8,128)(2,1)} collective-permute-done((bf16[2,128,1280]{2,1,0:T(8,128)(2,1)S(1)}, bf16[2,128,1280]{2,1,0:T(8,128)(2,1)}, u32[]{:S(2)}, u32[]{:S(2)}) %collective-permute-start.10) | collective-permute-done | bytes 655392 | tf_op jit(solution)/shard_map/ppermute | solution.py:15
  41.4 3.0 %pad_maximum_fusion.1 = bf16[3,2,128,1280]{3,2,1,0:T(8,128)(2,1)} fusion(bf16[1,2,128,1280]{3,2,1,0:T(8,128)(2,1)} %bitcast.12, bf16[1,2,128,1280]{3,2,1,0:T(8,128)(2,1)} %bitcast.11, bf16[1,2,128,1280]{3,2,1,0:T(8,128)(2,1)} %bitcast.10), kind=kLoop, calls=%fused_computation.1 | loop fusion | flops 1966080 | bytes 3932160 | tf_op jit(solution)/shard_map/stack | solution.py:145
  44.5 0.0 collective-permute-start.11
  44.5 0.1 copy.9
  44.6 0.1 multiply_reduce_fusion
  44.7 3.6 %collective-permute-start.5 = (bf16[2,128,1280]{2,1,0:T(8,128)(2,1)}, bf16[2,128,1280]{2,1,0:T(8,128)(2,1)}, u32[]{:S(2)}, u32[]{:S(2)}) collective-permute-start(bf16[2,128,1280]{2,1,0:T(8,128)(2,1)} %collective-permute-done.1.refs_2_), channel_id=1, source_target_pairs={{0,5},{3,6},{4,9},{7,10},{8,13},{11,14},{16,21},{19,22},{20,25},{2... | collective-permute-start | bytes 1966088 | tf_op jit(solution)/shard_map/ppermute | solution.py:15
  48.3 1.5 %collective-permute-start.6 = (bf16[2,128,1280]{2,1,0:T(8,128)(2,1)}, bf16[2,128,1280]{2,1,0:T(8,128)(2,1)}, u32[]{:S(2)}, u32[]{:S(2)}) collective-permute-start(bf16[2,128,1280]{2,1,0:T(8,128)(2,1)} %collective-permute-done.1.refs_2_), channel_id=1, source_target_pairs={{4,1},{7,2},{8,5},{11,6},{12,9},{15,10},{20,17},{23,18},{24,21},{2... | collective-permute-start | bytes 1966088 | tf_op jit(solution)/shard_map/ppermute | solution.py:15
  49.8 1.4 fusion.24.mask_ref
  51.2 0.0 collective-permute-done.refs_1_
  51.2 4.6 %collective-permute-done.5.refs_6_ = bf16[2,128,1280]{2,1,0:T(8,128)(2,1)} collective-permute-done((bf16[2,128,1280]{2,1,0:T(8,128)(2,1)}, bf16[2,128,1280]{2,1,0:T(8,128)(2,1)}, u32[]{:S(2)}, u32[]{:S(2)}) %collective-permute-start.5) | collective-permute-done | bytes 655392 | tf_op jit(solution)/shard_map/ppermute | solution.py:15
  55.8 4.7 %collective-permute-start.12 = (bf16[2,128,1280]{2,1,0:T(8,128)(2,1)}, bf16[2,128,1280]{2,1,0:T(8,128)(2,1)}, u32[]{:S(2)}, u32[]{:S(2)}) collective-permute-start(bf16[2,128,1280]{2,1,0:T(8,128)(2,1)} %collective-permute-done.8.refs_2_), channel_id=1, source_target_pairs={{0,5},{3,6},{4,9},{7,10},{8,13},{11,14},{16,21},{19,22},{20,25},{2... | collective-permute-start | bytes 1966088 | tf_op jit(solution)/shard_map/ppermute | solution.py:15
  60.5 0.0 collective-permute-done.6.refs_7_
  60.5 1.5 %collective-permute-start.13 = (bf16[2,128,1280]{2,1,0:T(8,128)(2,1)}, bf16[2,128,1280]{2,1,0:T(8,128)(2,1)}, u32[]{:S(2)}, u32[]{:S(2)}) collective-permute-start(bf16[2,128,1280]{2,1,0:T(8,128)(2,1)} %collective-permute-done.8.refs_2_), channel_id=1, source_target_pairs={{4,1},{7,2},{8,5},{11,6},{12,9},{15,10},{20,17},{23,18},{24,21},{2... | collective-permute-start | bytes 1966088 | tf_op jit(solution)/shard_map/ppermute | solution.py:15
  62.0 14.8 %shard_map.85 = (bf16[128,1280]{1,0:T(8,128)(2,1)}, bf16[2,128,1280]{2,1,0:T(8,128)(2,1)}, bf16[4,2,128,1280]{3,2,1,0:T(8,128)(2,1)}, bf16[2,128,1280]{2,1,0:T(8...) custom-call(s32[128,1280]{1,0:T(8,128)} %fusion.24.mask_ref, ...), custom_call_target="tpu_custom_call" | custom-call | flops 2516582400 | bytes 14745600 | tf_op jit(solution)/shard_map/pallas_call | solution.py:123
  76.8 0.1 collective-permute-start.14
  76.9 0.0 collective-permute-done.7.refs_1_
  76.9 0.0 collective-permute-done.12.refs_6_
  76.9 15.0 %shard_map.86 = (bf16[128,1280]{1,0:T(8,128)(2,1)}, bf16[2,128,1280]{2,1,0:T(8,128)(2,1)}, bf16[4,2,128,1280]{3,2,1,0:T(8,128)(2,1)}, bf16[2,128,1280]{2,1,0:T(8...) custom-call(s32[128,1280]{1,0:T(8,128)} %fusion.24.mask_ref, ...), custom_call_target="tpu_custom_call" | custom-call | flops 2516582400 | bytes 14745600 | tf_op jit(solution)/shard_map/pallas_call | solution.py:123
  91.9 0.5 collective-permute-start.20
  92.5 1.3 collective-permute-start.15
  93.8 0.7 collective-permute-start.16
  94.5 1.3 collective-permute-start.21
  95.8 2.0 %pad_maximum_fusion.4 = bf16[128,2560]{1,0:T(8,128)(2,1)} fusion(bf16[128,1280]{1,0:T(8,128)(2,1)} %get-tuple-element.20, bf16[128,1280]{1,0:T(8,128)(2,1)} %get-tuple-element.19), kind=kLoop, calls=%fused_computation.46 | loop fusion | flops 1310720 | bytes 1310720 | tf_op jit(solution)/shard_map/concatenate | solution.py:209
  97.7 6.9 %collective-permute-done.15 = bf16[2,128,1280]{2,1,0:T(8,128)(2,1)S(1)} collective-permute-done((bf16[2,128,1280]{2,1,0:T(8,128)(2,1)}, bf16[2,128,1280]{2,1,0:T(8,128)(2,1)S(1)}, u32[]{:S(2)}, u32[]{:S(2)}) %collective-permute-start.15) | collective-permute-done | bytes 655392 | tf_op jit(solution)/shard_map/ppermute | solution.py:15
  104.6 0.7 collective-permute-start.22
  105.3 0.7 fusion.13
  106.1 3.6 %collective-permute-start.17 = (bf16[2,128,1280]{2,1,0:T(8,128)(2,1)S(1)}, bf16[2,128,1280]{2,1,0:T(8,128)(2,1)S(1)}, u32[]{:S(2)}, u32[]{:S(2)}) collective-permute-start(bf16[2,128,1280]{2,1,0:T(8,128)(2,1)S(1)} %get-tuple-element.35), channel_id=1, source_target_pairs={{0,2},{1,3},{2,0},{3,1},{4,6},{5,7},{6,4},{7,5},{8,10},{9,11},{10,... | collective-permute-start | bytes 1966088 | tf_op jit(solution)/shard_map/ppermute | solution.py:15
  109.7 1.3 collective-permute-start.18
  111.0 0.6 collective-permute-done.21
  111.6 4.1 %collective-permute-start.19 = (bf16[2,128,1280]{2,1,0:T(8,128)(2,1)S(1)}, bf16[2,128,1280]{2,1,0:T(8,128)(2,1)S(1)}, u32[]{:S(2)}, u32[]{:S(2)}) collective-permute-start(bf16[2,128,1280]{2,1,0:T(8,128)(2,1)S(1)} %get-tuple-element.36), channel_id=1, source_target_pairs={{0,4},{1,5},{2,6},{3,7},{4,8},{5,9},{6,10},{7,11},{8,12},{9,13},{1... | collective-permute-start | bytes 1966088 | tf_op jit(solution)/shard_map/ppermute | solution.py:15
  115.8 0.7 fusion.4
  116.5 1.5 %collective-permute-start.23 = (bf16[2,128,1280]{2,1,0:T(8,128)(2,1)S(1)}, bf16[2,128,1280]{2,1,0:T(8,128)(2,1)S(1)}, u32[]{:S(2)}, u32[]{:S(2)}) collective-permute-start(bf16[2,128,1280]{2,1,0:T(8,128)(2,1)S(1)} %get-tuple-element.38), channel_id=1, source_target_pairs={{0,2},{1,3},{2,0},{3,1},{4,6},{5,7},{6,4},{7,5},{8,10},{9,11},{10,... | collective-permute-start | bytes 1966088 | tf_op jit(solution)/shard_map/ppermute | solution.py:15
  118.0 1.3 collective-permute-start.24
  119.3 5.5 %collective-permute-done.17 = bf16[2,128,1280]{2,1,0:T(8,128)(2,1)S(1)} collective-permute-done((bf16[2,128,1280]{2,1,0:T(8,128)(2,1)S(1)}, bf16[2,128,1280]{2,1,0:T(8,128)(2,1)S(1)}, u32[]{:S(2)}, u32[]{:S(2)}) %collective-permute-start.17) | collective-permute-done | bytes 655392 | tf_op jit(solution)/shard_map/ppermute | solution.py:15
  124.8 3.6 %collective-permute-start.25 = (bf16[2,128,1280]{2,1,0:T(8,128)(2,1)S(1)}, bf16[2,128,1280]{2,1,0:T(8,128)(2,1)S(1)}, u32[]{:S(2)}, u32[]{:S(2)}) collective-permute-start(bf16[2,128,1280]{2,1,0:T(8,128)(2,1)S(1)} %get-tuple-element.39), channel_id=1, source_target_pairs={{0,4},{1,5},{2,6},{3,7},{4,8},{5,9},{6,10},{7,11},{8,12},{9,13},{1... | collective-permute-start | bytes 1966088 | tf_op jit(solution)/shard_map/ppermute | solution.py:15
  128.5 0.7 collective-permute-done.18
  129.2 1.6 %collective-permute-done.19 = bf16[2,128,1280]{2,1,0:T(8,128)(2,1)S(1)} collective-permute-done((bf16[2,128,1280]{2,1,0:T(8,128)(2,1)S(1)}, bf16[2,128,1280]{2,1,0:T(8,128)(2,1)S(1)}, u32[]{:S(2)}, u32[]{:S(2)}) %collective-permute-start.19) | collective-permute-done | bytes 655392 | tf_op jit(solution)/shard_map/ppermute | solution.py:15
  130.8 0.4 fusion.17
  131.3 7.0 %collective-permute-done.23 = bf16[2,128,1280]{2,1,0:T(8,128)(2,1)S(1)} collective-permute-done((bf16[2,128,1280]{2,1,0:T(8,128)(2,1)S(1)}, bf16[2,128,1280]{2,1,0:T(8,128)(2,1)S(1)}, u32[]{:S(2)}, u32[]{:S(2)}) %collective-permute-start.23) | collective-permute-done | bytes 655392 | tf_op jit(solution)/shard_map/ppermute | solution.py:15
  138.3 4.0 %collective-permute-done.24 = bf16[2,128,1280]{2,1,0:T(8,128)(2,1)S(1)} collective-permute-done((bf16[2,128,1280]{2,1,0:T(8,128)(2,1)S(1)}, bf16[2,128,1280]{2,1,0:T(8,128)(2,1)S(1)}, u32[]{:S(2)}, u32[]{:S(2)}) %collective-permute-start.24) | collective-permute-done | bytes 655392 | tf_op jit(solution)/shard_map/ppermute | solution.py:15
  142.3 2.2 %collective-permute-done.25 = bf16[2,128,1280]{2,1,0:T(8,128)(2,1)S(1)} collective-permute-done((bf16[2,128,1280]{2,1,0:T(8,128)(2,1)S(1)}, bf16[2,128,1280]{2,1,0:T(8,128)(2,1)S(1)}, u32[]{:S(2)}, u32[]{:S(2)}) %collective-permute-start.25) | collective-permute-done | bytes 655392 | tf_op jit(solution)/shard_map/ppermute | solution.py:15
  144.5 0.4 fusion.8
  145.0 0.9 pad_maximum_fusion.6
  145.9 0.9 pad_maximum_fusion.5
  (49 shorter events, 0.3 us)
Async XLA Ops:
  2.0 14.9 %copy-start.11 = (s32[4]{0:T(128)S(1)}, s32[4]{0:T(128)}, u32[]{:S(2)}) copy-start(s32[4]{0:T(128)} %param.11) | copy-start | bytes 52
  2.1 28.7 %copy-start.7 = (bf16[2,128,1280]{2,1,0:T(8,128)(2,1)}, bf16[2,128,1280]{2,1,0:T(8,128)(2,1)S(1)}, u32[]{:S(2)}) copy-start(bf16[2,128,1280]{2,1,0:T(8,128)(2,1)S(1)} %pad_maximum_fusion.2.refs_0_) | copy-start | bytes 1966084
  2.1 18.7 %collective-permute-start.1 = (bf16[2,128,1280]{2,1,0:T(8,128)(2,1)S(1)}, bf16[2,128,1280]{2,1,0:T(8,128)(2,1)}, u32[]{:S(2)}, u32[]{:S(2)}) collective-permute-start(bf16[2,128,1280]{2,1,0:T(8,128)(2,1)S(1)} %pad_maximum_fusion.2.refs_0_), channel_id=1, source_target_pairs={{0,2},{1,3},{2,0},{3,1},{4,6},{5,7},{6,4},{7,5},{8,10},{9,11},{10,... | collective-permute-start | bytes 1966088 | tf_op jit(solution)/shard_map/ppermute | solution.py:15
  5.1 18.6 %collective-permute-start.2 = (bf16[2,128,1280]{2,1,0:T(8,128)(2,1)S(1)}, bf16[2,128,1280]{2,1,0:T(8,128)(2,1)}, u32[]{:S(2)}, u32[]{:S(2)}) collective-permute-start(bf16[2,128,1280]{2,1,0:T(8,128)(2,1)S(1)} %pad_maximum_fusion.2.refs_0_), channel_id=1, source_target_pairs={{0,4},{1,5},{2,6},{3,7},{4,8},{5,9},{6,10},{7,11},{8,12},{9,13},{1... | collective-permute-start | bytes 1966088 | tf_op jit(solution)/shard_map/ppermute | solution.py:15
  9.5 19.6 %collective-permute-start.3 = (bf16[2,128,1280]{2,1,0:T(8,128)(2,1)S(1)}, bf16[2,128,1280]{2,1,0:T(8,128)(2,1)}, u32[]{:S(2)}, u32[]{:S(2)}) collective-permute-start(bf16[2,128,1280]{2,1,0:T(8,128)(2,1)S(1)} %pad_maximum_fusion.2.refs_0_), channel_id=1, source_target_pairs={{4,0},{5,1},{6,2},{7,3},{8,4},{9,5},{10,6},{11,7},{12,8},{13,9},{1... | collective-permute-start | bytes 1966088 | tf_op jit(solution)/shard_map/ppermute | solution.py:15
  10.8 40.4 %copy-start.6 = (bf16[2,128,1280]{2,1,0:T(8,128)(2,1)}, bf16[2,128,1280]{2,1,0:T(8,128)(2,1)S(1)}, u32[]{:S(2)}) copy-start(bf16[2,128,1280]{2,1,0:T(8,128)(2,1)S(1)} %pad_maximum_fusion.3.refs_0_) | copy-start | bytes 1966084
  10.9 23.2 %collective-permute-start.8 = (bf16[2,128,1280]{2,1,0:T(8,128)(2,1)S(1)}, bf16[2,128,1280]{2,1,0:T(8,128)(2,1)}, u32[]{:S(2)}, u32[]{:S(2)}) collective-permute-start(bf16[2,128,1280]{2,1,0:T(8,128)(2,1)S(1)} %pad_maximum_fusion.3.refs_0_), channel_id=1, source_target_pairs={{0,2},{1,3},{2,0},{3,1},{4,6},{5,7},{6,4},{7,5},{8,10},{9,11},{10,... | collective-permute-start | bytes 1966088 | tf_op jit(solution)/shard_map/ppermute | solution.py:15
  11.4 24.9 %collective-permute-start.9 = (bf16[2,128,1280]{2,1,0:T(8,128)(2,1)S(1)}, bf16[2,128,1280]{2,1,0:T(8,128)(2,1)}, u32[]{:S(2)}, u32[]{:S(2)}) collective-permute-start(bf16[2,128,1280]{2,1,0:T(8,128)(2,1)S(1)} %pad_maximum_fusion.3.refs_0_), channel_id=1, source_target_pairs={{0,4},{1,5},{2,6},{3,7},{4,8},{5,9},{6,10},{7,11},{8,12},{9,13},{1... | collective-permute-start | bytes 1966088 | tf_op jit(solution)/shard_map/ppermute | solution.py:15
  20.8 20.6 %collective-permute-start.10 = (bf16[2,128,1280]{2,1,0:T(8,128)(2,1)S(1)}, bf16[2,128,1280]{2,1,0:T(8,128)(2,1)}, u32[]{:S(2)}, u32[]{:S(2)}) collective-permute-start(bf16[2,128,1280]{2,1,0:T(8,128)(2,1)S(1)} %pad_maximum_fusion.3.refs_0_), channel_id=1, source_target_pairs={{4,0},{5,1},{6,2},{7,3},{8,4},{9,5},{10,6},{11,7},{12,8},{13,9},{1... | collective-permute-start | bytes 1966088 | tf_op jit(solution)/shard_map/ppermute | solution.py:15
  23.7 27.5 %collective-permute-start = (bf16[2,128,1280]{2,1,0:T(8,128)(2,1)S(1)}, bf16[2,128,1280]{2,1,0:T(8,128)(2,1)}, u32[]{:S(2)}, u32[]{:S(2)}) collective-permute-start(bf16[2,128,1280]{2,1,0:T(8,128)(2,1)S(1)} %pad_maximum_fusion.2.refs_0_), channel_id=1, source_target_pairs={{0,1},{1,0},{2,3},{3,2},{4,5},{5,4},{6,7},{7,6},{8,9},{9,8},{10,11... | collective-permute-start | bytes 1966088 | tf_op jit(solution)/shard_map/ppermute | solution.py:15
  30.8 31.2 %collective-permute-start.4 = (bf16[3,2,128,1280]{3,2,1,0:T(8,128)(2,1)S(1)}, bf16[3,2,128,1280]{3,2,1,0:T(8,128)(2,1)}, u32[]{:S(2)}, u32[]{:S(2)}) collective-permute-start(bf16[3,2,128,1280]{3,2,1,0:T(8,128)(2,1)S(1)} %pad_maximum_fusion), channel_id=1, source_target_pairs={{0,1},{1,0},{2,3},{3,2},{4,5},{5,4},{6,7},{7,6},{8,9},{9,8},{10,11... | collective-permute-start | bytes 5898248 | tf_op jit(solution)/shard_map/ppermute | solution.py:15
  41.4 3.0 %copy-start.10 = (s32[4,3]{1,0:T(4,128)S(1)}, s32[4,3]{1,0:T(4,128)}, u32[]{:S(2)}) copy-start(s32[4,3]{1,0:T(4,128)} %param.10) | copy-start | bytes 148
  44.5 32.5 %collective-permute-start.11 = (bf16[3,2,128,1280]{3,2,1,0:T(8,128)(2,1)}, bf16[3,2,128,1280]{3,2,1,0:T(8,128)(2,1)}, u32[]{:S(2)}, u32[]{:S(2)}) collective-permute-start(bf16[3,2,128,1280]{3,2,1,0:T(8,128)(2,1)} %pad_maximum_fusion.1), channel_id=1, source_target_pairs={{0,1},{1,0},{2,3},{3,2},{4,5},{5,4},{6,7},{7,6},{8,9},{9,8},{10,11... | collective-permute-start | bytes 5898248 | tf_op jit(solution)/shard_map/ppermute | solution.py:15
  44.7 11.2 %collective-permute-start.5 = (bf16[2,128,1280]{2,1,0:T(8,128)(2,1)}, bf16[2,128,1280]{2,1,0:T(8,128)(2,1)}, u32[]{:S(2)}, u32[]{:S(2)}) collective-permute-start(bf16[2,128,1280]{2,1,0:T(8,128)(2,1)} %collective-permute-done.1.refs_2_), channel_id=1, source_target_pairs={{0,5},{3,6},{4,9},{7,10},{8,13},{11,14},{16,21},{19,22},{20,25},{2... | collective-permute-start | bytes 1966088 | tf_op jit(solution)/shard_map/ppermute | solution.py:15
  48.3 12.2 %collective-permute-start.6 = (bf16[2,128,1280]{2,1,0:T(8,128)(2,1)}, bf16[2,128,1280]{2,1,0:T(8,128)(2,1)}, u32[]{:S(2)}, u32[]{:S(2)}) collective-permute-start(bf16[2,128,1280]{2,1,0:T(8,128)(2,1)} %collective-permute-done.1.refs_2_), channel_id=1, source_target_pairs={{4,1},{7,2},{8,5},{11,6},{12,9},{15,10},{20,17},{23,18},{24,21},{2... | collective-permute-start | bytes 1966088 | tf_op jit(solution)/shard_map/ppermute | solution.py:15
  51.2 25.7 %collective-permute-start.7 = (bf16[2,128,1280]{2,1,0:T(8,128)(2,1)S(1)}, bf16[2,128,1280]{2,1,0:T(8,128)(2,1)}, u32[]{:S(2)}, u32[]{:S(2)}) collective-permute-start(bf16[2,128,1280]{2,1,0:T(8,128)(2,1)S(1)} %pad_maximum_fusion.3.refs_0_), channel_id=1, source_target_pairs={{0,1},{1,0},{2,3},{3,2},{4,5},{5,4},{6,7},{7,6},{8,9},{9,8},{10,11... | collective-permute-start | bytes 1966088 | tf_op jit(solution)/shard_map/ppermute | solution.py:15
  55.8 21.0 %collective-permute-start.12 = (bf16[2,128,1280]{2,1,0:T(8,128)(2,1)}, bf16[2,128,1280]{2,1,0:T(8,128)(2,1)}, u32[]{:S(2)}, u32[]{:S(2)}) collective-permute-start(bf16[2,128,1280]{2,1,0:T(8,128)(2,1)} %collective-permute-done.8.refs_2_), channel_id=1, source_target_pairs={{0,5},{3,6},{4,9},{7,10},{8,13},{11,14},{16,21},{19,22},{20,25},{2... | collective-permute-start | bytes 1966088 | tf_op jit(solution)/shard_map/ppermute | solution.py:15
  60.5 16.4 %collective-permute-start.13 = (bf16[2,128,1280]{2,1,0:T(8,128)(2,1)}, bf16[2,128,1280]{2,1,0:T(8,128)(2,1)}, u32[]{:S(2)}, u32[]{:S(2)}) collective-permute-start(bf16[2,128,1280]{2,1,0:T(8,128)(2,1)} %collective-permute-done.8.refs_2_), channel_id=1, source_target_pairs={{4,1},{7,2},{8,5},{11,6},{12,9},{15,10},{20,17},{23,18},{24,21},{2... | collective-permute-start | bytes 1966088 | tf_op jit(solution)/shard_map/ppermute | solution.py:15
  76.8 28.5 %collective-permute-start.14 = (bf16[4,2,128,1280]{3,2,1,0:T(8,128)(2,1)}, bf16[4,2,128,1280]{3,2,1,0:T(8,128)(2,1)S(1)}, u32[]{:S(2)}, u32[]{:S(2)}) collective-permute-start(bf16[4,2,128,1280]{3,2,1,0:T(8,128)(2,1)} %get-tuple-element.22), channel_id=1, source_target_pairs={{0,1},{1,0},{2,3},{3,2},{4,5},{5,4},{6,7},{7,6},{8,9},{9,8},{10,11... | collective-permute-start | bytes 7864328 | tf_op jit(solution)/shard_map/ppermute | solution.py:15
  76.9 28.4 %copy-start.2 = (bf16[2,128,1280]{2,1,0:T(8,128)(2,1)S(1)}, bf16[2,128,1280]{2,1,0:T(8,128)(2,1)}, u32[]{:S(2)}) copy-start(bf16[2,128,1280]{2,1,0:T(8,128)(2,1)} %get-tuple-element.27) | copy-start | bytes 1966084
  91.9 13.4 %copy-start = (bf16[2,128,1280]{2,1,0:T(8,128)(2,1)S(1)}, bf16[2,128,1280]{2,1,0:T(8,128)(2,1)}, u32[]{:S(2)}) copy-start(bf16[2,128,1280]{2,1,0:T(8,128)(2,1)} %get-tuple-element.23) | copy-start | bytes 1966084
  91.9 13.4 %copy-start.1 = (bf16[2,128,1280]{2,1,0:T(8,128)(2,1)S(1)}, bf16[2,128,1280]{2,1,0:T(8,128)(2,1)}, u32[]{:S(2)}) copy-start(bf16[2,128,1280]{2,1,0:T(8,128)(2,1)} %get-tuple-element.26) | copy-start | bytes 1966084
  91.9 23.8 %collective-permute-start.20 = (bf16[4,2,128,1280]{3,2,1,0:T(8,128)(2,1)}, bf16[4,2,128,1280]{3,2,1,0:T(8,128)(2,1)S(1)}, u32[]{:S(2)}, u32[]{:S(2)}) collective-permute-start(bf16[4,2,128,1280]{3,2,1,0:T(8,128)(2,1)} %get-tuple-element.29), channel_id=1, source_target_pairs={{0,1},{1,0},{2,3},{3,2},{4,5},{5,4},{6,7},{7,6},{8,9},{9,8},{10,11... | collective-permute-start | bytes 7864328 | tf_op jit(solution)/shard_map/ppermute | solution.py:15
  92.5 12.1 %collective-permute-start.15 = (bf16[2,128,1280]{2,1,0:T(8,128)(2,1)}, bf16[2,128,1280]{2,1,0:T(8,128)(2,1)S(1)}, u32[]{:S(2)}, u32[]{:S(2)}) collective-permute-start(bf16[2,128,1280]{2,1,0:T(8,128)(2,1)} %get-tuple-element.24), channel_id=1, source_target_pairs={{5,0},{6,3},{9,4},{10,7},{13,8},{14,11},{21,16},{22,19},{25,20},{2... | collective-permute-start | bytes 1966088 | tf_op jit(solution)/shard_map/ppermute | solution.py:15
  93.8 11.5 %collective-permute-start.16 = (bf16[2,128,1280]{2,1,0:T(8,128)(2,1)}, bf16[2,128,1280]{2,1,0:T(8,128)(2,1)S(1)}, u32[]{:S(2)}, u32[]{:S(2)}) collective-permute-start(bf16[2,128,1280]{2,1,0:T(8,128)(2,1)} %get-tuple-element.25), channel_id=1, source_target_pairs={{1,4},{2,7},{5,8},{6,11},{9,12},{10,15},{17,20},{18,23},{21,24},{2... | collective-permute-start | bytes 1966088 | tf_op jit(solution)/shard_map/ppermute | solution.py:15
  94.5 17.1 %collective-permute-start.21 = (bf16[2,128,1280]{2,1,0:T(8,128)(2,1)}, bf16[2,128,1280]{2,1,0:T(8,128)(2,1)S(1)}, u32[]{:S(2)}, u32[]{:S(2)}) collective-permute-start(bf16[2,128,1280]{2,1,0:T(8,128)(2,1)} %get-tuple-element.31), channel_id=1, source_target_pairs={{5,0},{6,3},{9,4},{10,7},{13,8},{14,11},{21,16},{22,19},{25,20},{2... | collective-permute-start | bytes 1966088 | tf_op jit(solution)/shard_map/ppermute | solution.py:15
  104.6 11.2 %collective-permute-start.22 = (bf16[2,128,1280]{2,1,0:T(8,128)(2,1)}, bf16[2,128,1280]{2,1,0:T(8,128)(2,1)S(1)}, u32[]{:S(2)}, u32[]{:S(2)}) collective-permute-start(bf16[2,128,1280]{2,1,0:T(8,128)(2,1)} %get-tuple-element.32), channel_id=1, source_target_pairs={{1,4},{2,7},{5,8},{6,11},{9,12},{10,15},{17,20},{18,23},{21,24},{2... | collective-permute-start | bytes 1966088 | tf_op jit(solution)/shard_map/ppermute | solution.py:15
  105.3 10.4 %copy-start.3 = (bf16[2,128,1280]{2,1,0:T(8,128)(2,1)S(1)}, bf16[2,128,1280]{2,1,0:T(8,128)(2,1)}, u32[]{:S(2)}) copy-start(bf16[2,128,1280]{2,1,0:T(8,128)(2,1)} %get-tuple-element.30) | copy-start | bytes 1966084
  105.3 10.4 %copy-start.4 = (bf16[2,128,1280]{2,1,0:T(8,128)(2,1)S(1)}, bf16[2,128,1280]{2,1,0:T(8,128)(2,1)}, u32[]{:S(2)}) copy-start(bf16[2,128,1280]{2,1,0:T(8,128)(2,1)} %get-tuple-element.33) | copy-start | bytes 1966084
  105.3 10.4 %copy-start.5 = (bf16[2,128,1280]{2,1,0:T(8,128)(2,1)S(1)}, bf16[2,128,1280]{2,1,0:T(8,128)(2,1)}, u32[]{:S(2)}) copy-start(bf16[2,128,1280]{2,1,0:T(8,128)(2,1)} %get-tuple-element.34) | copy-start | bytes 1966084
  106.1 18.8 %collective-permute-start.17 = (bf16[2,128,1280]{2,1,0:T(8,128)(2,1)S(1)}, bf16[2,128,1280]{2,1,0:T(8,128)(2,1)S(1)}, u32[]{:S(2)}, u32[]{:S(2)}) collective-permute-start(bf16[2,128,1280]{2,1,0:T(8,128)(2,1)S(1)} %get-tuple-element.35), channel_id=1, source_target_pairs={{0,2},{1,3},{2,0},{3,1},{4,6},{5,7},{6,4},{7,5},{8,10},{9,11},{10,... | collective-permute-start | bytes 1966088 | tf_op jit(solution)/shard_map/ppermute | solution.py:15
  109.7 19.5 %collective-permute-start.18 = (bf16[2,128,1280]{2,1,0:T(8,128)(2,1)S(1)}, bf16[2,128,1280]{2,1,0:T(8,128)(2,1)S(1)}, u32[]{:S(2)}, u32[]{:S(2)}) collective-permute-start(bf16[2,128,1280]{2,1,0:T(8,128)(2,1)S(1)} %get-tuple-element.37), channel_id=1, source_target_pairs={{4,0},{5,1},{6,2},{7,3},{8,4},{9,5},{10,6},{11,7},{12,8},{13,9},{1... | collective-permute-start | bytes 1966088 | tf_op jit(solution)/shard_map/ppermute | solution.py:15
  111.6 19.2 %collective-permute-start.19 = (bf16[2,128,1280]{2,1,0:T(8,128)(2,1)S(1)}, bf16[2,128,1280]{2,1,0:T(8,128)(2,1)S(1)}, u32[]{:S(2)}, u32[]{:S(2)}) collective-permute-start(bf16[2,128,1280]{2,1,0:T(8,128)(2,1)S(1)} %get-tuple-element.36), channel_id=1, source_target_pairs={{0,4},{1,5},{2,6},{3,7},{4,8},{5,9},{6,10},{7,11},{8,12},{9,13},{1... | collective-permute-start | bytes 1966088 | tf_op jit(solution)/shard_map/ppermute | solution.py:15
  115.8 15.0 %copy-start.8 = (bf16[2,128,1280]{2,1,0:T(8,128)(2,1)S(1)}, bf16[2,128,1280]{2,1,0:T(8,128)(2,1)}, u32[]{:S(2)}) copy-start(bf16[2,128,1280]{2,1,0:T(8,128)(2,1)} %get-tuple-element.21) | copy-start | bytes 1966084
  116.5 21.8 %collective-permute-start.23 = (bf16[2,128,1280]{2,1,0:T(8,128)(2,1)S(1)}, bf16[2,128,1280]{2,1,0:T(8,128)(2,1)S(1)}, u32[]{:S(2)}, u32[]{:S(2)}) collective-permute-start(bf16[2,128,1280]{2,1,0:T(8,128)(2,1)S(1)} %get-tuple-element.38), channel_id=1, source_target_pairs={{0,2},{1,3},{2,0},{3,1},{4,6},{5,7},{6,4},{7,5},{8,10},{9,11},{10,... | collective-permute-start | bytes 1966088 | tf_op jit(solution)/shard_map/ppermute | solution.py:15
  118.0 24.3 %collective-permute-start.24 = (bf16[2,128,1280]{2,1,0:T(8,128)(2,1)S(1)}, bf16[2,128,1280]{2,1,0:T(8,128)(2,1)S(1)}, u32[]{:S(2)}, u32[]{:S(2)}) collective-permute-start(bf16[2,128,1280]{2,1,0:T(8,128)(2,1)S(1)} %get-tuple-element.40), channel_id=1, source_target_pairs={{4,0},{5,1},{6,2},{7,3},{8,4},{9,5},{10,6},{11,7},{12,8},{13,9},{1... | collective-permute-start | bytes 1966088 | tf_op jit(solution)/shard_map/ppermute | solution.py:15
  124.8 19.7 %collective-permute-start.25 = (bf16[2,128,1280]{2,1,0:T(8,128)(2,1)S(1)}, bf16[2,128,1280]{2,1,0:T(8,128)(2,1)S(1)}, u32[]{:S(2)}, u32[]{:S(2)}) collective-permute-start(bf16[2,128,1280]{2,1,0:T(8,128)(2,1)S(1)} %get-tuple-element.39), channel_id=1, source_target_pairs={{0,4},{1,5},{2,6},{3,7},{4,8},{5,9},{6,10},{7,11},{8,12},{9,13},{1... | collective-permute-start | bytes 1966088 | tf_op jit(solution)/shard_map/ppermute | solution.py:15
  131.2 13.3 %copy-start.9 = (bf16[2,128,1280]{2,1,0:T(8,128)(2,1)S(1)}, bf16[2,128,1280]{2,1,0:T(8,128)(2,1)}, u32[]{:S(2)}) copy-start(bf16[2,128,1280]{2,1,0:T(8,128)(2,1)} %get-tuple-element.28) | copy-start | bytes 1966084

commit v4 on v3

--- a/solution.py
+++ b/solution.py
@@ -135,36 +135,67 @@
     return results[0], results[1:]
 
 
-def exchange_chunk(forward_mask, queries, out_grad, keys, values, head_offset, inv_root, count):
-    core, cross, down, up, diag_up, diag_down, back = route(count)
-    own = jnp.stack([keys, values])
+def forward_relay(own, count, after):
+    core, cross, down, up, diag_up, diag_down, back = route(count)
+    if after is not None:
+        own, _ = lax.optimization_barrier((own, after))
     from_core = send(own, core)
     from_cross = send(own, cross)
     from_below = send(own, up)
     from_above = send(own, down)
-    relayed = send(jnp.stack([from_cross, from_below, from_above]), core)
+    return [own, from_core, from_cross, from_below, from_above]
+
+
+def forward_second(first, count, after):
+    core, cross, down, up, diag_up, diag_down, back = route(count)
+    own, from_core, from_cross, from_below, from_above = first
+    ahead = jnp.stack([from_cross, from_below, from_above])
+    if after is not None:
+        (ahead, from_cross), _ = lax.optimization_barrier(((ahead, from_cross), after))
+    relayed = send(ahead, core)
     diag_from_below = send(from_cross, diag_up)
     diag_from_above = send(from_cross, diag_down)
-    inputs = [own, from_core, from_cross, from_below, from_above, relayed, diag_from_below, diag_from_above]
+    return first + [relayed, diag_from_below, diag_from_above]
+
+
+def chunk_kernel(forward_mask, queries, out_grad, inputs, head_offset, inv_root):
     slot_in = [(0, ()), (1, ()), (2, ()), (3, ()), (4, ()), (5, (0,)), (5, (1,)), (5, (2,)), (6, ()), (7, ())]
     out_lead = [(), (4,), (), (), (), (), ()]
     slot_out = [(0, ()), (1, (0,)), (2, ()), (3, ()), (4, ()), (1, (1,)), (1, (2,)), (1, (3,)), (5, ()), (6, ())]
-    query_grad, outs = attention_backward(
+    return attention_backward(
         forward_mask, queries, out_grad, inputs, slot_in, out_lead, slot_out, inv_root, head_offset
     )
+
+
+def return_first(outs, count, after):
+    core, cross, down, up, diag_up, diag_down, back = route(count)
     own_part, to_core, cross_part, below_part, above_part, diag_b_part, diag_a_part = outs
-    wide = lambda tensor: tensor.astype(jnp.float32)
+    if after is not None:
+        (to_core, diag_b_part, diag_a_part), _ = lax.optimization_barrier(
+            ((to_core, diag_b_part, diag_a_part), after)
+        )
     to_partner = send(to_core, core)
     diag_back_below = send(diag_b_part, back(diag_up))
     diag_back_above = send(diag_a_part, back(diag_down))
+    return [to_partner, diag_back_below, diag_back_above]
+
+
+def return_second(outs, first, count, after):
+    core, cross, down, up, diag_up, diag_down, back = route(count)
+    own_part, to_core, cross_part, below_part, above_part, diag_b_part, diag_a_part = outs
+    to_partner, diag_back_below, diag_back_above = first
+    wide = lambda tensor: tensor.astype(jnp.float32)
     cross_sum = wide(cross_part) + wide(to_partner[1]) + wide(diag_back_below) + wide(diag_back_above)
     below_sum = wide(below_part) + wide(to_partner[2])
     above_sum = wide(above_part) + wide(to_partner[3])
-    got_cross = send(cross_sum.astype(jnp.bfloat16), cross)
-    got_below = send(below_sum.astype(jnp.bfloat16), down)
-    got_above = send(above_sum.astype(jnp.bfloat16), up)
+    sums = (cross_sum.astype(jnp.bfloat16), below_sum.astype(jnp.bfloat16), above_sum.astype(jnp.bfloat16))
+    if after is not None:
+        sums, _ = lax.optimization_barrier((sums, after))
+    got_cross = send(sums[0], cross)
+    got_below = send(sums[1], down)
+    got_above = send(sums[2], up)
     summed = wide(own_part) + wide(to_partner[0]) + wide(got_cross) + wide(got_below) + wide(got_above)
-    return query_grad, summed[0].astype(jnp.bfloat16), summed[1].astype(jnp.bfloat16)
+    return [got_cross, got_below, got_above], summed
 
 
 def body(queries, keys, values, out_grad, frame_keep, band_window):
@@ -198,14 +229,24 @@
     heads = channel_total // HD
     chunk_heads = heads // CHUNKS if heads % CHUNKS == 0 else heads
     width = chunk_heads * HD
-    grads = []
-    for first in range(0, channel_total, width):
-        grads.append(
-            exchange_chunk(
-                forward_mask, queries, out_grad, keys[:, first : first + width],
-                values[:, first : first + width], first // HD, inv_root, count,
-            )
-        )
+    starts = list(range(0, channel_total, width))
+    firsts, seconds, outs, backs, sums, dqs = [], [], [], [], [], []
+    for c, first in enumerate(starts):
+        own = jnp.stack([keys[:, first : first + width], values[:, first : first + width]])
+        firsts.append(forward_relay(own, count, firsts[c - 1][1:] if c else None))
+    for c in range(len(starts)):
+        seconds.append(forward_second(firsts[c], count, seconds[c - 1][5:] if c else None))
+    for c, first in enumerate(starts):
+        dq, parts = chunk_kernel(forward_mask, queries, out_grad, seconds[c], first // HD, inv_root)
+        dqs.append(dq)
+        outs.append(parts)
+    for c in range(len(starts)):
+        backs.append(return_first(outs[c], count, backs[c - 1] if c else None))
+    got = None
+    for c in range(len(starts)):
+        got, summed = return_second(outs[c], backs[c], count, got)
+        sums.append(summed)
+    grads = [(dqs[c], sums[c][0].astype(jnp.bfloat16), sums[c][1].astype(jnp.bfloat16)) for c in range(len(starts))]
     query_grad = jnp.concatenate([grad[0] for grad in grads], axis=1)
     key_grad = jnp.concatenate([grad[1] for grad in grads], axis=1)
     value_grad = jnp.concatenate([grad[2] for grad in grads], axis=1)

time: 148 us -> 151 us (1.020)
  waiting for transfers between devices: 54.4 us -> 50.4 us
  starting transfers between devices: 47.3 us -> 50.9 us
  local copies, waits for them, and re-layouts: 1.6 us -> 4.16 us
    ppermute x26, waiting for transfers between devices: 54.4 us -> 50.4 us  [send(): return lax.ppermute(value, 'tm', pairs)]
    ppermute x26, starting transfers between devices: 47.3 us -> 50.9 us  [send(): return lax.ppermute(value, 'tm', pairs)]
    unnamed x25 -> x41, local copies, waits for them, and re-layouts: 0.15 us -> 2.71 us
  transfers between devices with their start and end apart: 26 -> 26, of which waited for: 15 -> 12; matrix products, arithmetic and copies ran while one was open for 7% -> 8% of each run, Pallas kernels for 20% -> 20%
where the time goes in v4:
time: 151 us; the launch traced here: 150 us
  starting transfers between devices  50.9 us (34%)
  waiting for transfers between devices  50.4 us (33%)
  Pallas kernels  29.7 us (20%)
  other arithmetic  13.4 us (9%)
  local copies, waits for them, and re-layouts  4.16 us (3%)
    ppermute x26, starting transfers between devices, send(): return lax.ppermute(value, 'tm', pairs)  50.9 us
    ppermute x26, waiting for transfers between devices, send(): return lax.ppermute(value, 'tm', pairs)  50.4 us
    pallas_call x2, Pallas kernels, attention_backward(): pl.pallas_call(kernel, grid=(heads,), in_specs=in_specs, out_specs=out_sp...  29.7 us
    another operation x2, other arithmetic, forward_second(): ahead = jnp.stack([from_cross, from_below, from_above])  3.42 us
  transfers between devices with their start and end apart: 26, of which 12 were waited for; matrix products, arithmetic and copies ran while one was open for 8% of the time, Pallas kernels for 20%

profile of v4, /device:TPU:0, one launch (start us, length us, event | category | flops | bytes accessed | tf_op | source)
XLA Modules:
  0.0 149.7 jit_solution(7493998307166084241)
XLA Ops:
  0.6 1.4 slice_bitcast_fusion.14
  2.0 0.1 pad_maximum_fusion.2.refs_0_
  2.1 0.0 copy-start.6
  2.1 1.3 collective-permute-start.3
  3.4 5.6 %collective-permute-start.2 = (bf16[2,128,1280]{2,1,0:T(8,128)(2,1)S(1)}, bf16[2,128,1280]{2,1,0:T(8,128)(2,1)S(1)}, u32[]{:S(2)}, u32[]{:S(2)}) collective-permute-start(bf16[2,128,1280]{2,1,0:T(8,128)(2,1)S(1)} %pad_maximum_fusion.2.refs_0_), channel_id=1, source_target_pairs={{0,4},{1,5},{2,6},{3,7},{4,8},{5,9},{6,10},{7,11},{8,12},{9,13},{1... | collective-permute-start | bytes 1966088 | tf_op jit(solution)/shard_map/ppermute | solution.py:15
  9.0 2.0 %collective-permute-start.1 = (bf16[2,128,1280]{2,1,0:T(8,128)(2,1)S(1)}, bf16[2,128,1280]{2,1,0:T(8,128)(2,1)S(1)}, u32[]{:S(2)}, u32[]{:S(2)}) collective-permute-start(bf16[2,128,1280]{2,1,0:T(8,128)(2,1)S(1)} %pad_maximum_fusion.2.refs_0_), channel_id=1, source_target_pairs={{0,2},{1,3},{2,0},{3,1},{4,6},{5,7},{6,4},{7,5},{8,10},{9,11},{10,... | collective-permute-start | bytes 1966088 | tf_op jit(solution)/shard_map/ppermute | solution.py:15
  11.2 10.6 %collective-permute-done.3.refs_4_ = bf16[2,128,1280]{2,1,0:T(8,128)(2,1)S(1)} collective-permute-done((bf16[2,128,1280]{2,1,0:T(8,128)(2,1)S(1)}, bf16[2,128,1280]{2,1,0:T(8,128)(2,1)S(1)}, u32[]{:S(2)}, u32[]{:S(2)}) %collective-permute-start.3) | collective-permute-done | bytes 655392 | tf_op jit(solution)/shard_map/ppermute | solution.py:15
  21.8 1.2 collective-permute-done.2.refs_3_
  22.9 2.3 %collective-permute-done.1.refs_2_ = bf16[2,128,1280]{2,1,0:T(8,128)(2,1)S(1)} collective-permute-done((bf16[2,128,1280]{2,1,0:T(8,128)(2,1)S(1)}, bf16[2,128,1280]{2,1,0:T(8,128)(2,1)S(1)}, u32[]{:S(2)}, u32[]{:S(2)}) %collective-permute-start.1) | collective-permute-done | bytes 655392 | tf_op jit(solution)/shard_map/ppermute | solution.py:15
  25.3 0.8 copy-done.9
  26.1 1.7 %pad_maximum_fusion = bf16[3,2,128,1280]{3,2,1,0:T(8,128)(2,1)S(1)} fusion(bf16[1,2,128,1280]{3,2,1,0:T(8,128)(2,1)} %bitcast.68, bf16[1,2,128,1280]{3,2,1,0:T(8,128)(2,1)} %bitcast.69, bf16[1,2,128,1280]{3,2,1,0:T(8,128)(2,1)} %bitcast.70), kind=kLoop, calls=%fused_computation | loop fusion | flops 1966080 | bytes 3932160 | tf_op jit(solution)/shard_map/stack | solution.py:152
  27.9 0.1 collective-permute-start.4
  28.0 0.1 copy.9
  28.1 0.1 select_reduce_fusion
  28.2 0.1 multiply_reduce_fusion
  28.3 0.7 collective-permute-start.6
  29.0 0.9 pad_maximum_fusion.3.refs_0_
  29.9 4.3 %collective-permute-start.5 = (bf16[2,128,1280]{2,1,0:T(8,128)(2,1)S(1)}, bf16[2,128,1280]{2,1,0:T(8,128)(2,1)S(1)}, u32[]{:S(2)}, u32[]{:S(2)}) collective-permute-start(bf16[2,128,1280]{2,1,0:T(8,128)(2,1)S(1)} %copy-done.10), channel_id=1, source_target_pairs={{0,5},{3,6},{4,9},{7,10},{8,13},{11,14},{16,21},{19,22},{20,25},{2... | collective-permute-start | bytes 1966088 | tf_op jit(solution)/shard_map/ppermute | solution.py:15
  34.2 0.0 collective-permute-done.refs_1_
  34.2 1.3 collective-permute-start.10
  35.5 5.4 %collective-permute-start.9 = (bf16[2,128,1280]{2,1,0:T(8,128)(2,1)}, bf16[2,128,1280]{2,1,0:T(8,128)(2,1)}, u32[]{:S(2)}, u32[]{:S(2)}) collective-permute-start(bf16[2,128,1280]{2,1,0:T(8,128)(2,1)} %pad_maximum_fusion.3.refs_0_), channel_id=1, source_target_pairs={{0,4},{1,5},{2,6},{3,7},{4,8},{5,9},{6,10},{7,11},{8,12},{9,13},{1... | collective-permute-start | bytes 1966088 | tf_op jit(solution)/shard_map/ppermute | solution.py:15
  40.9 0.0 collective-permute-done.6.refs_7_
  40.9 4.5 %collective-permute-start.8 = (bf16[2,128,1280]{2,1,0:T(8,128)(2,1)}, bf16[2,128,1280]{2,1,0:T(8,128)(2,1)}, u32[]{:S(2)}, u32[]{:S(2)}) collective-permute-start(bf16[2,128,1280]{2,1,0:T(8,128)(2,1)} %pad_maximum_fusion.3.refs_0_), channel_id=1, source_target_pairs={{0,2},{1,3},{2,0},{3,1},{4,6},{5,7},{6,4},{7,5},{8,10},{9,11},{10,... | collective-permute-start | bytes 1966088 | tf_op jit(solution)/shard_map/ppermute | solution.py:15
  45.5 1.4 fusion.24.mask_ref
  46.9 0.0 collective-permute-done.5.refs_6_
  46.9 0.9 copy-done.15
  47.7 14.8 %shard_map.85 = (bf16[128,1280]{1,0:T(8,128)(2,1)}, bf16[2,128,1280]{2,1,0:T(8,128)(2,1)}, bf16[4,2,128,1280]{3,2,1,0:T(8,128)(2,1)}, bf16[2,128,1280]{2,1,0:T(8...) custom-call(s32[128,1280]{1,0:T(8,128)} %fusion.24.mask_ref, ...), custom_call_target="tpu_custom_call" | custom-call | flops 2516582400 | bytes 14745600 | tf_op jit(solution)/shard_map/pallas_call | solution.py:123
  62.5 0.1 collective-permute-start.14
  62.6 0.0 collective-permute-done.9.refs_3_
  62.6 0.0 collective-permute-done.8.refs_2_
  62.7 1.7 %pad_maximum_fusion.1 = bf16[3,2,128,1280]{3,2,1,0:T(8,128)(2,1)S(1)} fusion(bf16[1,2,128,1280]{3,2,1,0:T(8,128)(2,1)} %bitcast.12, bf16[1,2,128,1280]{3,2,1,0:T(8,128)(2,1)} %bitcast.11, bf16[1,2,128,1280]{3,2,1,0:T(8,128)(2,1)} %bitcast.10), kind=kLoop, calls=%fused_computation.1 | loop fusion | flops 1966080 | bytes 3932160 | tf_op jit(solution)/shard_map/stack | solution.py:152
  64.4 0.5 collective-permute-start.11
  64.9 0.1 collective-permute-start.7
  65.0 0.7 collective-permute-start.13
  65.7 4.3 %collective-permute-start.12 = (bf16[2,128,1280]{2,1,0:T(8,128)(2,1)}, bf16[2,128,1280]{2,1,0:T(8,128)(2,1)S(1)}, u32[]{:S(2)}, u32[]{:S(2)}) collective-permute-start(bf16[2,128,1280]{2,1,0:T(8,128)(2,1)} %collective-permute-done.8.refs_2_), channel_id=1, source_target_pairs={{0,5},{3,6},{4,9},{7,10},{8,13},{11,14},{16,21},{19,22},{20,25},{2... | collective-permute-start | bytes 1966088 | tf_op jit(solution)/shard_map/ppermute | solution.py:15
  70.0 1.4 collective-permute-done.7.refs_1_
  71.5 1.3 collective-permute-start.15
  72.8 0.0 collective-permute-done.13.refs_7_
  72.8 1.5 %collective-permute-start.16 = (bf16[2,128,1280]{2,1,0:T(8,128)(2,1)}, bf16[2,128,1280]{2,1,0:T(8,128)(2,1)}, u32[]{:S(2)}, u32[]{:S(2)}) collective-permute-start(bf16[2,128,1280]{2,1,0:T(8,128)(2,1)} %get-tuple-element.37), channel_id=1, source_target_pairs={{1,4},{2,7},{5,8},{6,11},{9,12},{10,15},{17,20},{18,23},{21,24},{2... | collective-permute-start | bytes 1966088 | tf_op jit(solution)/shard_map/ppermute | solution.py:15
  74.3 4.1 %collective-permute-done.12.refs_6_ = bf16[2,128,1280]{2,1,0:T(8,128)(2,1)S(1)} collective-permute-done((bf16[2,128,1280]{2,1,0:T(8,128)(2,1)}, bf16[2,128,1280]{2,1,0:T(8,128)(2,1)S(1)}, u32[]{:S(2)}, u32[]{:S(2)}) %collective-permute-start.12) | collective-permute-done | bytes 655392 | tf_op jit(solution)/shard_map/ppermute | solution.py:15
  78.4 0.8 copy-done.18
  79.2 14.9 %shard_map.86 = (bf16[128,1280]{1,0:T(8,128)(2,1)}, bf16[2,128,1280]{2,1,0:T(8,128)(2,1)}, bf16[4,2,128,1280]{3,2,1,0:T(8,128)(2,1)}, bf16[2,128,1280]{2,1,0:T(8...) custom-call(s32[128,1280]{1,0:T(8,128)} %fusion.24.mask_ref, ...), custom_call_target="tpu_custom_call" | custom-call | flops 2516582400 | bytes 14745600 | tf_op jit(solution)/shard_map/pallas_call | solution.py:123
  94.2 3.0 %collective-permute-start.20 = (bf16[4,2,128,1280]{3,2,1,0:T(8,128)(2,1)}, bf16[4,2,128,1280]{3,2,1,0:T(8,128)(2,1)S(1)}, u32[]{:S(2)}, u32[]{:S(2)}) collective-permute-start(bf16[4,2,128,1280]{3,2,1,0:T(8,128)(2,1)} %get-tuple-element.44), channel_id=1, source_target_pairs={{0,1},{1,0},{2,3},{3,2},{4,5},{5,4},{6,7},{7,6},{8,9},{9,8},{10,11... | collective-permute-start | bytes 7864328 | tf_op jit(solution)/shard_map/ppermute | solution.py:15
  97.3 1.9 %pad_maximum_fusion.4 = bf16[128,2560]{1,0:T(8,128)(2,1)} fusion(bf16[128,1280]{1,0:T(8,128)(2,1)} %get-tuple-element.32, bf16[128,1280]{1,0:T(8,128)(2,1)} %get-tuple-element.28), kind=kLoop, calls=%fused_computation.46 | loop fusion | flops 1310720 | bytes 1310720 | tf_op jit(solution)/shard_map/concatenate | solution.py:250
  99.2 1.3 collective-permute-start.21
  100.5 0.7 collective-permute-start.22
  101.3 2.1 %fusion.9 = (bf16[2,128,1280]{2,1,0:T(8,128)(2,1)S(1)}, bf16[2,128,1280]{2,1,0:T(8,128)(2,1)S(1)}, bf16[2,128,1280]{2,1,0:T(8,128)(2,1)S(1)}) fusion(bf16[2,128,1280]{2,1,0:T(8,128)(2,1)S(1)} %copy-done.2, bf16[4,2,128,1280]{3,2,1,0:T(8,128)(2,1)S(1)} %collective-permute-done.14, bf16[2,128,1280]{2,1,0:T(8,128)(2,1)S(1)} %copy-done.1, ...), kind=kLoop, calls=%fused_computation.16 | loop fusion | flops 5242880 | bytes 7208960 | tf_op jit(solution)/shard_map/convert_element_type | solution.py:191
  103.3 4.3 %collective-permute-start.19 = (bf16[2,128,1280]{2,1,0:T(8,128)(2,1)S(1)}, bf16[2,128,1280]{2,1,0:T(8,128)(2,1)S(1)}, u32[]{:S(2)}, u32[]{:S(2)}) collective-permute-start(bf16[2,128,1280]{2,1,0:T(8,128)(2,1)S(1)} %get-tuple-element.53), channel_id=1, source_target_pairs={{0,4},{1,5},{2,6},{3,7},{4,8},{5,9},{6,10},{7,11},{8,12},{9,13},{1... | collective-permute-start | bytes 1966088 | tf_op jit(solution)/shard_map/ppermute | solution.py:15
  107.6 1.3 collective-permute-start.18
  108.9 2.4 %collective-permute-done.21 = bf16[2,128,1280]{2,1,0:T(8,128)(2,1)S(1)} collective-permute-done((bf16[2,128,1280]{2,1,0:T(8,128)(2,1)}, bf16[2,128,1280]{2,1,0:T(8,128)(2,1)S(1)}, u32[]{:S(2)}, u32[]{:S(2)}) %collective-permute-start.21) | collective-permute-done | bytes 655392 | tf_op jit(solution)/shard_map/ppermute | solution.py:15
  111.4 0.7 fusion
  112.0 10.6 %collective-permute-done.19 = bf16[2,128,1280]{2,1,0:T(8,128)(2,1)S(1)} collective-permute-done((bf16[2,128,1280]{2,1,0:T(8,128)(2,1)S(1)}, bf16[2,128,1280]{2,1,0:T(8,128)(2,1)S(1)}, u32[]{:S(2)}, u32[]{:S(2)}) %collective-permute-start.19) | collective-permute-done | bytes 655392 | tf_op jit(solution)/shard_map/ppermute | solution.py:15
  122.7 3.4 %collective-permute-done.18 = bf16[2,128,1280]{2,1,0:T(8,128)(2,1)S(1)} collective-permute-done((bf16[2,128,1280]{2,1,0:T(8,128)(2,1)S(1)}, bf16[2,128,1280]{2,1,0:T(8,128)(2,1)S(1)}, u32[]{:S(2)}, u32[]{:S(2)}) %collective-permute-start.18) | collective-permute-done | bytes 655392 | tf_op jit(solution)/shard_map/ppermute | solution.py:15
  126.1 1.5 %collective-permute-done.17 = bf16[2,128,1280]{2,1,0:T(8,128)(2,1)S(1)} collective-permute-done((bf16[2,128,1280]{2,1,0:T(8,128)(2,1)S(1)}, bf16[2,128,1280]{2,1,0:T(8,128)(2,1)S(1)}, u32[]{:S(2)}, u32[]{:S(2)}) %collective-permute-start.17) | collective-permute-done | bytes 655392 | tf_op jit(solution)/shard_map/ppermute | solution.py:15
  127.6 0.3 collective-permute-start.23
  127.9 1.3 collective-permute-start.24
  129.2 4.9 %collective-permute-start.25 = (bf16[2,128,1280]{2,1,0:T(8,128)(2,1)S(1)}, bf16[2,128,1280]{2,1,0:T(8,128)(2,1)S(1)}, u32[]{:S(2)}, u32[]{:S(2)}) collective-permute-start(bf16[2,128,1280]{2,1,0:T(8,128)(2,1)S(1)} %get-tuple-element.52), channel_id=1, source_target_pairs={{0,4},{1,5},{2,6},{3,7},{4,8},{5,9},{6,10},{7,11},{8,12},{9,13},{1... | collective-permute-start | bytes 1966088 | tf_op jit(solution)/shard_map/ppermute | solution.py:15
  134.1 0.4 fusion.17
  134.6 9.2 %collective-permute-done.23 = bf16[2,128,1280]{2,1,0:T(8,128)(2,1)S(1)} collective-permute-done((bf16[2,128,1280]{2,1,0:T(8,128)(2,1)S(1)}, bf16[2,128,1280]{2,1,0:T(8,128)(2,1)S(1)}, u32[]{:S(2)}, u32[]{:S(2)}) %collective-permute-start.23) | collective-permute-done | bytes 655392 | tf_op jit(solution)/shard_map/ppermute | solution.py:15
  143.9 2.4 %collective-permute-done.24 = bf16[2,128,1280]{2,1,0:T(8,128)(2,1)S(1)} collective-permute-done((bf16[2,128,1280]{2,1,0:T(8,128)(2,1)S(1)}, bf16[2,128,1280]{2,1,0:T(8,128)(2,1)S(1)}, u32[]{:S(2)}, u32[]{:S(2)}) %collective-permute-start.24) | collective-permute-done | bytes 655392 | tf_op jit(solution)/shard_map/ppermute | solution.py:15
  146.3 1.2 collective-permute-done.25
  147.4 0.4 fusion.8
  147.9 0.9 pad_maximum_fusion.6
  148.8 0.9 pad_maximum_fusion.5
  (65 shorter events, 0.3 us)
Async XLA Ops:
  2.1 25.8 %copy-start.6 = (bf16[2,128,1280]{2,1,0:T(8,128)(2,1)}, bf16[2,128,1280]{2,1,0:T(8,128)(2,1)S(1)}, u32[]{:S(2)}) copy-start(bf16[2,128,1280]{2,1,0:T(8,128)(2,1)S(1)} %pad_maximum_fusion.2.refs_0_) | copy-start | bytes 1966084
  2.1 19.7 %collective-permute-start.3 = (bf16[2,128,1280]{2,1,0:T(8,128)(2,1)S(1)}, bf16[2,128,1280]{2,1,0:T(8,128)(2,1)S(1)}, u32[]{:S(2)}, u32[]{:S(2)}) collective-permute-start(bf16[2,128,1280]{2,1,0:T(8,128)(2,1)S(1)} %pad_maximum_fusion.2.refs_0_), channel_id=1, source_target_pairs={{4,0},{5,1},{6,2},{7,3},{8,4},{9,5},{10,6},{11,7},{12,8},{13,9},{1... | collective-permute-start | bytes 1966088 | tf_op jit(solution)/shard_map/ppermute | solution.py:15
  3.4 19.6 %collective-permute-start.2 = (bf16[2,128,1280]{2,1,0:T(8,128)(2,1)S(1)}, bf16[2,128,1280]{2,1,0:T(8,128)(2,1)S(1)}, u32[]{:S(2)}, u32[]{:S(2)}) collective-permute-start(bf16[2,128,1280]{2,1,0:T(8,128)(2,1)S(1)} %pad_maximum_fusion.2.refs_0_), channel_id=1, source_target_pairs={{0,4},{1,5},{2,6},{3,7},{4,8},{5,9},{6,10},{7,11},{8,12},{9,13},{1... | collective-permute-start | bytes 1966088 | tf_op jit(solution)/shard_map/ppermute | solution.py:15
  9.0 16.3 %collective-permute-start.1 = (bf16[2,128,1280]{2,1,0:T(8,128)(2,1)S(1)}, bf16[2,128,1280]{2,1,0:T(8,128)(2,1)S(1)}, u32[]{:S(2)}, u32[]{:S(2)}) collective-permute-start(bf16[2,128,1280]{2,1,0:T(8,128)(2,1)S(1)} %pad_maximum_fusion.2.refs_0_), channel_id=1, source_target_pairs={{0,2},{1,3},{2,0},{3,1},{4,6},{5,7},{6,4},{7,5},{8,10},{9,11},{10,... | collective-permute-start | bytes 1966088 | tf_op jit(solution)/shard_map/ppermute | solution.py:15
  11.0 23.2 %collective-permute-start = (bf16[2,128,1280]{2,1,0:T(8,128)(2,1)S(1)}, bf16[2,128,1280]{2,1,0:T(8,128)(2,1)}, u32[]{:S(2)}, u32[]{:S(2)}) collective-permute-start(bf16[2,128,1280]{2,1,0:T(8,128)(2,1)S(1)} %pad_maximum_fusion.2.refs_0_), channel_id=1, source_target_pairs={{0,1},{1,0},{2,3},{3,2},{4,5},{5,4},{6,7},{7,6},{8,9},{9,8},{10,11... | collective-permute-start | bytes 1966088 | tf_op jit(solution)/shard_map/ppermute | solution.py:15
  21.8 3.5 %copy-start.7 = (bf16[2,128,1280]{2,1,0:T(8,128)(2,1)}, bf16[2,128,1280]{2,1,0:T(8,128)(2,1)S(1)}, u32[]{:S(2)}) copy-start(bf16[2,128,1280]{2,1,0:T(8,128)(2,1)S(1)} %collective-permute-done.3.refs_4_) | copy-start | bytes 1966084
  22.9 2.3 %copy-start.8 = (bf16[2,128,1280]{2,1,0:T(8,128)(2,1)}, bf16[2,128,1280]{2,1,0:T(8,128)(2,1)S(1)}, u32[]{:S(2)}) copy-start(bf16[2,128,1280]{2,1,0:T(8,128)(2,1)S(1)} %collective-permute-done.2.refs_3_) | copy-start | bytes 1966084
  25.3 0.8 copy-start.9
  26.1 1.8 %copy-start.13 = (s32[4,3]{1,0:T(4,128)S(1)}, s32[4,3]{1,0:T(4,128)}, u32[]{:S(2)}) copy-start(s32[4,3]{1,0:T(4,128)} %param.10) | copy-start | bytes 148
  26.1 2.0 %copy-start.19 = (s32[4]{0:T(128)S(1)}, s32[4]{0:T(128)}, u32[]{:S(2)}) copy-start(s32[4]{0:T(128)} %param.11) | copy-start | bytes 52
  27.9 19.9 %collective-permute-start.4 = (bf16[3,2,128,1280]{3,2,1,0:T(8,128)(2,1)S(1)}, bf16[3,2,128,1280]{3,2,1,0:T(8,128)(2,1)}, u32[]{:S(2)}, u32[]{:S(2)}) collective-permute-start(bf16[3,2,128,1280]{3,2,1,0:T(8,128)(2,1)S(1)} %pad_maximum_fusion), channel_id=1, source_target_pairs={{0,1},{1,0},{2,3},{3,2},{4,5},{5,4},{6,7},{7,6},{8,9},{9,8},{10,11... | collective-permute-start | bytes 5898248 | tf_op jit(solution)/shard_map/ppermute | solution.py:15
  28.1 1.8 %copy-start.10 = (bf16[2,128,1280]{2,1,0:T(8,128)(2,1)S(1)}, bf16[2,128,1280]{2,1,0:T(8,128)(2,1)}, u32[]{:S(2)}) copy-start(bf16[2,128,1280]{2,1,0:T(8,128)(2,1)} %copy-done.9) | copy-start | bytes 1966084
  28.3 12.7 %collective-permute-start.6 = (bf16[2,128,1280]{2,1,0:T(8,128)(2,1)}, bf16[2,128,1280]{2,1,0:T(8,128)(2,1)S(1)}, u32[]{:S(2)}, u32[]{:S(2)}) collective-permute-start(bf16[2,128,1280]{2,1,0:T(8,128)(2,1)} %copy-done.9), channel_id=1, source_target_pairs={{4,1},{7,2},{8,5},{11,6},{12,9},{15,10},{20,17},{23,18},{24,21},{2... | collective-permute-start | bytes 1966088 | tf_op jit(solution)/shard_map/ppermute | solution.py:15
  29.9 17.0 %collective-permute-start.5 = (bf16[2,128,1280]{2,1,0:T(8,128)(2,1)S(1)}, bf16[2,128,1280]{2,1,0:T(8,128)(2,1)S(1)}, u32[]{:S(2)}, u32[]{:S(2)}) collective-permute-start(bf16[2,128,1280]{2,1,0:T(8,128)(2,1)S(1)} %copy-done.10), channel_id=1, source_target_pairs={{0,5},{3,6},{4,9},{7,10},{8,13},{11,14},{16,21},{19,22},{20,25},{2... | collective-permute-start | bytes 1966088 | tf_op jit(solution)/shard_map/ppermute | solution.py:15
  34.2 28.4 %collective-permute-start.10 = (bf16[2,128,1280]{2,1,0:T(8,128)(2,1)}, bf16[2,128,1280]{2,1,0:T(8,128)(2,1)}, u32[]{:S(2)}, u32[]{:S(2)}) collective-permute-start(bf16[2,128,1280]{2,1,0:T(8,128)(2,1)} %pad_maximum_fusion.3.refs_0_), channel_id=1, source_target_pairs={{4,0},{5,1},{6,2},{7,3},{8,4},{9,5},{10,6},{11,7},{12,8},{13,9},{1... | collective-permute-start | bytes 1966088 | tf_op jit(solution)/shard_map/ppermute | solution.py:15
  35.5 27.1 %collective-permute-start.9 = (bf16[2,128,1280]{2,1,0:T(8,128)(2,1)}, bf16[2,128,1280]{2,1,0:T(8,128)(2,1)}, u32[]{:S(2)}, u32[]{:S(2)}) collective-permute-start(bf16[2,128,1280]{2,1,0:T(8,128)(2,1)} %pad_maximum_fusion.3.refs_0_), channel_id=1, source_target_pairs={{0,4},{1,5},{2,6},{3,7},{4,8},{5,9},{6,10},{7,11},{8,12},{9,13},{1... | collective-permute-start | bytes 1966088 | tf_op jit(solution)/shard_map/ppermute | solution.py:15
  40.9 5.9 %copy-start.14 = (bf16[2,128,1280]{2,1,0:T(8,128)(2,1)}, bf16[2,128,1280]{2,1,0:T(8,128)(2,1)S(1)}, u32[]{:S(2)}) copy-start(bf16[2,128,1280]{2,1,0:T(8,128)(2,1)S(1)} %collective-permute-done.6.refs_7_) | copy-start | bytes 1966084
  40.9 21.7 %collective-permute-start.8 = (bf16[2,128,1280]{2,1,0:T(8,128)(2,1)}, bf16[2,128,1280]{2,1,0:T(8,128)(2,1)}, u32[]{:S(2)}, u32[]{:S(2)}) collective-permute-start(bf16[2,128,1280]{2,1,0:T(8,128)(2,1)} %pad_maximum_fusion.3.refs_0_), channel_id=1, source_target_pairs={{0,2},{1,3},{2,0},{3,1},{4,6},{5,7},{6,4},{7,5},{8,10},{9,11},{10,... | collective-permute-start | bytes 1966088 | tf_op jit(solution)/shard_map/ppermute | solution.py:15
  46.9 0.9 copy-start.15
  62.5 31.7 %collective-permute-start.14 = (bf16[4,2,128,1280]{3,2,1,0:T(8,128)(2,1)}, bf16[4,2,128,1280]{3,2,1,0:T(8,128)(2,1)S(1)}, u32[]{:S(2)}, u32[]{:S(2)}) collective-permute-start(bf16[4,2,128,1280]{3,2,1,0:T(8,128)(2,1)} %get-tuple-element.34), channel_id=1, source_target_pairs={{0,1},{1,0},{2,3},{3,2},{4,5},{5,4},{6,7},{7,6},{8,9},{9,8},{10,11... | collective-permute-start | bytes 7864328 | tf_op jit(solution)/shard_map/ppermute | solution.py:15
  64.4 14.9 %collective-permute-start.11 = (bf16[3,2,128,1280]{3,2,1,0:T(8,128)(2,1)S(1)}, bf16[3,2,128,1280]{3,2,1,0:T(8,128)(2,1)}, u32[]{:S(2)}, u32[]{:S(2)}) collective-permute-start(bf16[3,2,128,1280]{3,2,1,0:T(8,128)(2,1)S(1)} %pad_maximum_fusion.1), channel_id=1, source_target_pairs={{0,1},{1,0},{2,3},{3,2},{4,5},{5,4},{6,7},{7,6},{8,9},{9,8},{10,11... | collective-permute-start | bytes 5898248 | tf_op jit(solution)/shard_map/ppermute | solution.py:15
  64.9 6.6 %collective-permute-start.7 = (bf16[2,128,1280]{2,1,0:T(8,128)(2,1)}, bf16[2,128,1280]{2,1,0:T(8,128)(2,1)S(1)}, u32[]{:S(2)}, u32[]{:S(2)}) collective-permute-start(bf16[2,128,1280]{2,1,0:T(8,128)(2,1)} %pad_maximum_fusion.3.refs_0_), channel_id=1, source_target_pairs={{0,1},{1,0},{2,3},{3,2},{4,5},{5,4},{6,7},{7,6},{8,9},{9,8},{10,11... | collective-permute-start | bytes 1966088 | tf_op jit(solution)/shard_map/ppermute | solution.py:15
  65.0 7.8 %collective-permute-start.13 = (bf16[2,128,1280]{2,1,0:T(8,128)(2,1)}, bf16[2,128,1280]{2,1,0:T(8,128)(2,1)S(1)}, u32[]{:S(2)}, u32[]{:S(2)}) collective-permute-start(bf16[2,128,1280]{2,1,0:T(8,128)(2,1)} %collective-permute-done.8.refs_2_), channel_id=1, source_target_pairs={{4,1},{7,2},{8,5},{11,6},{12,9},{15,10},{20,17},{23,18},{24,21},{2... | collective-permute-start | bytes 1966088 | tf_op jit(solution)/shard_map/ppermute | solution.py:15
  65.7 12.7 %collective-permute-start.12 = (bf16[2,128,1280]{2,1,0:T(8,128)(2,1)}, bf16[2,128,1280]{2,1,0:T(8,128)(2,1)S(1)}, u32[]{:S(2)}, u32[]{:S(2)}) collective-permute-start(bf16[2,128,1280]{2,1,0:T(8,128)(2,1)} %collective-permute-done.8.refs_2_), channel_id=1, source_target_pairs={{0,5},{3,6},{4,9},{7,10},{8,13},{11,14},{16,21},{19,22},{20,25},{2... | collective-permute-start | bytes 1966088 | tf_op jit(solution)/shard_map/ppermute | solution.py:15
  71.5 6.9 %copy-start.16 = (bf16[2,128,1280]{2,1,0:T(8,128)(2,1)}, bf16[2,128,1280]{2,1,0:T(8,128)(2,1)S(1)}, u32[]{:S(2)}) copy-start(bf16[2,128,1280]{2,1,0:T(8,128)(2,1)S(1)} %collective-permute-done.7.refs_1_) | copy-start | bytes 1966084
  71.5 22.7 %collective-permute-start.15 = (bf16[2,128,1280]{2,1,0:T(8,128)(2,1)}, bf16[2,128,1280]{2,1,0:T(8,128)(2,1)}, u32[]{:S(2)}, u32[]{:S(2)}) collective-permute-start(bf16[2,128,1280]{2,1,0:T(8,128)(2,1)} %get-tuple-element.36), channel_id=1, source_target_pairs={{5,0},{6,3},{9,4},{10,7},{13,8},{14,11},{21,16},{22,19},{25,20},{2... | collective-permute-start | bytes 1966088 | tf_op jit(solution)/shard_map/ppermute | solution.py:15
  72.8 5.6 %copy-start.17 = (bf16[2,128,1280]{2,1,0:T(8,128)(2,1)}, bf16[2,128,1280]{2,1,0:T(8,128)(2,1)S(1)}, u32[]{:S(2)}) copy-start(bf16[2,128,1280]{2,1,0:T(8,128)(2,1)S(1)} %collective-permute-done.13.refs_7_) | copy-start | bytes 1966084
  72.8 21.4 %collective-permute-start.16 = (bf16[2,128,1280]{2,1,0:T(8,128)(2,1)}, bf16[2,128,1280]{2,1,0:T(8,128)(2,1)}, u32[]{:S(2)}, u32[]{:S(2)}) collective-permute-start(bf16[2,128,1280]{2,1,0:T(8,128)(2,1)} %get-tuple-element.37), channel_id=1, source_target_pairs={{1,4},{2,7},{5,8},{6,11},{9,12},{10,15},{17,20},{18,23},{21,24},{2... | collective-permute-start | bytes 1966088 | tf_op jit(solution)/shard_map/ppermute | solution.py:15
  78.4 0.8 copy-start.18
  79.2 22.0 %copy-start.2 = (bf16[2,128,1280]{2,1,0:T(8,128)(2,1)S(1)}, bf16[2,128,1280]{2,1,0:T(8,128)(2,1)}, u32[]{:S(2)}) copy-start(bf16[2,128,1280]{2,1,0:T(8,128)(2,1)} %get-tuple-element.39) | copy-start | bytes 1966084
  94.2 7.0 %copy-start = (bf16[2,128,1280]{2,1,0:T(8,128)(2,1)S(1)}, bf16[2,128,1280]{2,1,0:T(8,128)(2,1)}, u32[]{:S(2)}) copy-start(bf16[2,128,1280]{2,1,0:T(8,128)(2,1)} %get-tuple-element.35) | copy-start | bytes 1966084
  94.2 7.0 %copy-start.1 = (bf16[2,128,1280]{2,1,0:T(8,128)(2,1)S(1)}, bf16[2,128,1280]{2,1,0:T(8,128)(2,1)}, u32[]{:S(2)}) copy-start(bf16[2,128,1280]{2,1,0:T(8,128)(2,1)} %get-tuple-element.38) | copy-start | bytes 1966084
  94.2 17.1 %collective-permute-start.20 = (bf16[4,2,128,1280]{3,2,1,0:T(8,128)(2,1)}, bf16[4,2,128,1280]{3,2,1,0:T(8,128)(2,1)S(1)}, u32[]{:S(2)}, u32[]{:S(2)}) collective-permute-start(bf16[4,2,128,1280]{3,2,1,0:T(8,128)(2,1)} %get-tuple-element.44), channel_id=1, source_target_pairs={{0,1},{1,0},{2,3},{3,2},{4,5},{5,4},{6,7},{7,6},{8,9},{9,8},{10,11... | collective-permute-start | bytes 7864328 | tf_op jit(solution)/shard_map/ppermute | solution.py:15
  99.2 12.1 %collective-permute-start.21 = (bf16[2,128,1280]{2,1,0:T(8,128)(2,1)}, bf16[2,128,1280]{2,1,0:T(8,128)(2,1)S(1)}, u32[]{:S(2)}, u32[]{:S(2)}) collective-permute-start(bf16[2,128,1280]{2,1,0:T(8,128)(2,1)} %get-tuple-element.46), channel_id=1, source_target_pairs={{5,0},{6,3},{9,4},{10,7},{13,8},{14,11},{21,16},{22,19},{25,20},{2... | collective-permute-start | bytes 1966088 | tf_op jit(solution)/shard_map/ppermute | solution.py:15
  100.5 10.8 %collective-permute-start.22 = (bf16[2,128,1280]{2,1,0:T(8,128)(2,1)}, bf16[2,128,1280]{2,1,0:T(8,128)(2,1)S(1)}, u32[]{:S(2)}, u32[]{:S(2)}) collective-permute-start(bf16[2,128,1280]{2,1,0:T(8,128)(2,1)} %get-tuple-element.47), channel_id=1, source_target_pairs={{1,4},{2,7},{5,8},{6,11},{9,12},{10,15},{17,20},{18,23},{21,24},{2... | collective-permute-start | bytes 1966088 | tf_op jit(solution)/shard_map/ppermute | solution.py:15
  101.2 10.1 %copy-start.3 = (bf16[2,128,1280]{2,1,0:T(8,128)(2,1)S(1)}, bf16[2,128,1280]{2,1,0:T(8,128)(2,1)}, u32[]{:S(2)}) copy-start(bf16[2,128,1280]{2,1,0:T(8,128)(2,1)} %get-tuple-element.45) | copy-start | bytes 1966084
  101.2 10.1 %copy-start.4 = (bf16[2,128,1280]{2,1,0:T(8,128)(2,1)S(1)}, bf16[2,128,1280]{2,1,0:T(8,128)(2,1)}, u32[]{:S(2)}) copy-start(bf16[2,128,1280]{2,1,0:T(8,128)(2,1)} %get-tuple-element.48) | copy-start | bytes 1966084
  101.2 10.1 %copy-start.5 = (bf16[2,128,1280]{2,1,0:T(8,128)(2,1)S(1)}, bf16[2,128,1280]{2,1,0:T(8,128)(2,1)}, u32[]{:S(2)}) copy-start(bf16[2,128,1280]{2,1,0:T(8,128)(2,1)} %get-tuple-element.49) | copy-start | bytes 1966084
  103.3 19.3 %collective-permute-start.19 = (bf16[2,128,1280]{2,1,0:T(8,128)(2,1)S(1)}, bf16[2,128,1280]{2,1,0:T(8,128)(2,1)S(1)}, u32[]{:S(2)}, u32[]{:S(2)}) collective-permute-start(bf16[2,128,1280]{2,1,0:T(8,128)(2,1)S(1)} %get-tuple-element.53), channel_id=1, source_target_pairs={{0,4},{1,5},{2,6},{3,7},{4,8},{5,9},{6,10},{7,11},{8,12},{9,13},{1... | collective-permute-start | bytes 1966088 | tf_op jit(solution)/shard_map/ppermute | solution.py:15
  107.6 18.5 %collective-permute-start.18 = (bf16[2,128,1280]{2,1,0:T(8,128)(2,1)S(1)}, bf16[2,128,1280]{2,1,0:T(8,128)(2,1)S(1)}, u32[]{:S(2)}, u32[]{:S(2)}) collective-permute-start(bf16[2,128,1280]{2,1,0:T(8,128)(2,1)S(1)} %get-tuple-element.54), channel_id=1, source_target_pairs={{4,0},{5,1},{6,2},{7,3},{8,4},{9,5},{10,6},{11,7},{12,8},{13,9},{1... | collective-permute-start | bytes 1966088 | tf_op jit(solution)/shard_map/ppermute | solution.py:15
  111.3 16.3 %collective-permute-start.17 = (bf16[2,128,1280]{2,1,0:T(8,128)(2,1)S(1)}, bf16[2,128,1280]{2,1,0:T(8,128)(2,1)S(1)}, u32[]{:S(2)}, u32[]{:S(2)}) collective-permute-start(bf16[2,128,1280]{2,1,0:T(8,128)(2,1)S(1)} %get-tuple-element.55), channel_id=1, source_target_pairs={{0,2},{1,3},{2,0},{3,1},{4,6},{5,7},{6,4},{7,5},{8,10},{9,11},{10,... | collective-permute-start | bytes 1966088 | tf_op jit(solution)/shard_map/ppermute | solution.py:15
  111.3 22.8 %copy-start.11 = (bf16[2,128,1280]{2,1,0:T(8,128)(2,1)S(1)}, bf16[2,128,1280]{2,1,0:T(8,128)(2,1)}, u32[]{:S(2)}) copy-start(bf16[2,128,1280]{2,1,0:T(8,128)(2,1)} %get-tuple-element.33) | copy-start | bytes 1966084
  127.6 16.3 %collective-permute-start.23 = (bf16[2,128,1280]{2,1,0:T(8,128)(2,1)S(1)}, bf16[2,128,1280]{2,1,0:T(8,128)(2,1)S(1)}, u32[]{:S(2)}, u32[]{:S(2)}) collective-permute-start(bf16[2,128,1280]{2,1,0:T(8,128)(2,1)S(1)} %get-tuple-element.50), channel_id=1, source_target_pairs={{0,2},{1,3},{2,0},{3,1},{4,6},{5,7},{6,4},{7,5},{8,10},{9,11},{10,... | collective-permute-start | bytes 1966088 | tf_op jit(solution)/shard_map/ppermute | solution.py:15
  127.9 18.4 %collective-permute-start.24 = (bf16[2,128,1280]{2,1,0:T(8,128)(2,1)S(1)}, bf16[2,128,1280]{2,1,0:T(8,128)(2,1)S(1)}, u32[]{:S(2)}, u32[]{:S(2)}) collective-permute-start(bf16[2,128,1280]{2,1,0:T(8,128)(2,1)S(1)} %get-tuple-element.51), channel_id=1, source_target_pairs={{4,0},{5,1},{6,2},{7,3},{8,4},{9,5},{10,6},{11,7},{12,8},{13,9},{1... | collective-permute-start | bytes 1966088 | tf_op jit(solution)/shard_map/ppermute | solution.py:15
  129.2 18.3 %collective-permute-start.25 = (bf16[2,128,1280]{2,1,0:T(8,128)(2,1)S(1)}, bf16[2,128,1280]{2,1,0:T(8,128)(2,1)S(1)}, u32[]{:S(2)}, u32[]{:S(2)}) collective-permute-start(bf16[2,128,1280]{2,1,0:T(8,128)(2,1)S(1)} %get-tuple-element.52), channel_id=1, source_target_pairs={{0,4},{1,5},{2,6},{3,7},{4,8},{5,9},{6,10},{7,11},{8,12},{9,13},{1... | collective-permute-start | bytes 1966088 | tf_op jit(solution)/shard_map/ppermute | solution.py:15
  134.6 12.9 %copy-start.12 = (bf16[2,128,1280]{2,1,0:T(8,128)(2,1)S(1)}, bf16[2,128,1280]{2,1,0:T(8,128)(2,1)}, u32[]{:S(2)}) copy-start(bf16[2,128,1280]{2,1,0:T(8,128)(2,1)} %get-tuple-element.40) | copy-start | bytes 1966084

commit v5 on v4

--- a/solution.py
+++ b/solution.py
@@ -8,7 +8,7 @@
 
 HD = 128
 QUARTERS = 4
-CHUNKS = 2
+CHUNKS = 4
 
 
 def send(value, pairs):

time: 151 us -> 198 us (1.31)
  starting transfers between devices: 50.9 us -> 97.3 us
  waiting for transfers between devices: 50.4 us -> 43.1 us
  Pallas kernels: 29.7 us -> 34.5 us
  local copies, waits for them, and re-layouts: 4.16 us -> 6.19 us
    ppermute x26 -> x52, starting transfers between devices: 50.9 us -> 97.3 us  [send(): return lax.ppermute(value, 'tm', pairs)]
    ppermute x26 -> x52, waiting for transfers between devices: 50.4 us -> 43.1 us  [send(): return lax.ppermute(value, 'tm', pairs)]
    pallas_call x2 -> x4, Pallas kernels: 29.7 us -> 34.5 us  [attention_backward(): pl.pallas_call(kernel, grid=(heads,), in_specs=in_specs, out_specs=out_sp...]
    another operation x2 -> x4, other arithmetic: 3.42 us -> 0.52 us  [forward_second(): ahead = jnp.stack([from_cross, from_below, from_above])]
    convert_element_type x2 -> x4, other arithmetic: 2.76 us -> 5.33 us  [return_second(): above_sum.astype(jnp.bfloat16)]
  transfers between devices with their start and end apart: 26 -> 52, of which waited for: 12 -> 20; matrix products, arithmetic and copies ran while one was open for 8% -> 6% of each run, Pallas kernels for 20% -> 18%
where the time goes in v5:
time: 198 us; the launch traced here: 196 us
  starting transfers between devices  97.3 us (49%)
  waiting for transfers between devices  43.1 us (22%)
  Pallas kernels  34.5 us (17%)
  other arithmetic  13.2 us (7%)
  local copies, waits for them, and re-layouts  6.19 us (3%)
  between operations  2.03 us (1%)
    ppermute x52, starting transfers between devices, send(): return lax.ppermute(value, 'tm', pairs)  97.3 us
    ppermute x52, waiting for transfers between devices, send(): return lax.ppermute(value, 'tm', pairs)  43.1 us
    pallas_call x4, Pallas kernels, attention_backward(): pl.pallas_call(kernel, grid=(heads,), in_specs=in_specs, out_specs=out_sp...  34.5 us
    convert_element_type x4, other arithmetic, return_second(): above_sum.astype(jnp.bfloat16)  5.33 us
  transfers between devices with their start and end apart: 52, of which 20 were waited for; matrix products, arithmetic and copies ran while one was open for 6% of the time, Pallas kernels for 18%

profile of v5, /device:TPU:0, one launch (start us, length us, event | category | flops | bytes accessed | tf_op | source)
XLA Modules:
  0.0 196.2 jit_solution(13460587841213064177)
XLA Ops:
  0.6 2.3 %slice_bitcast_fusion.30 = (bf16[1,128,640]{2,1,0:T(8,128)(2,1)S(1)}, bf16[1,128,640]{2,1,0:T(8,128)(2,1)S(1)}, bf16[1,128,640]{2,1,0:T(8,128)(2,1)S(1)}, bf16[1...) fusion(bf16[128,2560]{1,0:T(8,128)(2,1)} %param.8, ...), kind=kLoop, calls=%fused_computation.105 | loop fusion | bytes 2621440 | tf_op jit(solution)/shard_map/stack | solution.py:235
  3.0 3.1 %collective-permute-start.1 = (bf16[2,128,640]{2,1,0:T(8,128)(2,1)S(1)}, bf16[2,128,640]{2,1,0:T(8,128)(2,1)S(1)}, u32[]{:S(2)}, u32[]{:S(2)}) collective-permute-start(bf16[2,128,640]{2,1,0:T(8,128)(2,1)S(1)} %pad_maximum_fusion.7.refs_0_), channel_id=1, source_target_pairs={{0,2},{1,3},{2,0},{3,1},{4,6},{5,7},{6,4},{7,5},{8,10},{9,11},{10,... | collective-permute-start | bytes 983048 | tf_op jit(solution)/shard_map/ppermute | solution.py:15
  6.0 3.5 %collective-permute-start.2 = (bf16[2,128,640]{2,1,0:T(8,128)(2,1)S(1)}, bf16[2,128,640]{2,1,0:T(8,128)(2,1)S(1)}, u32[]{:S(2)}, u32[]{:S(2)}) collective-permute-start(bf16[2,128,640]{2,1,0:T(8,128)(2,1)S(1)} %pad_maximum_fusion.7.refs_0_), channel_id=1, source_target_pairs={{0,4},{1,5},{2,6},{3,7},{4,8},{5,9},{6,10},{7,11},{8,12},{9,13},{1... | collective-permute-start | bytes 983048 | tf_op jit(solution)/shard_map/ppermute | solution.py:15
  9.5 1.3 collective-permute-start.3
  11.4 2.4 %collective-permute-done.1.refs_2_ = bf16[2,128,640]{2,1,0:T(8,128)(2,1)S(1)} collective-permute-done((bf16[2,128,640]{2,1,0:T(8,128)(2,1)S(1)}, bf16[2,128,640]{2,1,0:T(8,128)(2,1)S(1)}, u32[]{:S(2)}, u32[]{:S(2)}) %collective-permute-start.1) | collective-permute-done | bytes 327712 | tf_op jit(solution)/shard_map/ppermute | solution.py:15
  13.7 2.4 %collective-permute-done.2.refs_3_ = bf16[2,128,640]{2,1,0:T(8,128)(2,1)S(1)} collective-permute-done((bf16[2,128,640]{2,1,0:T(8,128)(2,1)S(1)}, bf16[2,128,640]{2,1,0:T(8,128)(2,1)S(1)}, u32[]{:S(2)}, u32[]{:S(2)}) %collective-permute-start.2) | collective-permute-done | bytes 327712 | tf_op jit(solution)/shard_map/ppermute | solution.py:15
  16.2 4.1 %collective-permute-done.3.refs_4_ = bf16[2,128,640]{2,1,0:T(8,128)(2,1)S(1)} collective-permute-done((bf16[2,128,640]{2,1,0:T(8,128)(2,1)S(1)}, bf16[2,128,640]{2,1,0:T(8,128)(2,1)S(1)}, u32[]{:S(2)}, u32[]{:S(2)}) %collective-permute-start.3) | collective-permute-done | bytes 327712 | tf_op jit(solution)/shard_map/ppermute | solution.py:15
  21.0 3.2 %collective-permute-start.5 = (bf16[2,128,640]{2,1,0:T(8,128)(2,1)S(1)}, bf16[2,128,640]{2,1,0:T(8,128)(2,1)S(1)}, u32[]{:S(2)}, u32[]{:S(2)}) collective-permute-start(bf16[2,128,640]{2,1,0:T(8,128)(2,1)S(1)} %collective-permute-done.1.refs_2_), channel_id=1, source_target_pairs={{0,5},{3,6},{4,9},{7,10},{8,13},{11,14},{16,21},{19,22},{20,25},{2... | collective-permute-start | bytes 983048 | tf_op jit(solution)/shard_map/ppermute | solution.py:15
  24.4 3.5 %collective-permute-start.9 = (bf16[2,128,640]{2,1,0:T(8,128)(2,1)S(1)}, bf16[2,128,640]{2,1,0:T(8,128)(2,1)S(1)}, u32[]{:S(2)}, u32[]{:S(2)}) collective-permute-start(bf16[2,128,640]{2,1,0:T(8,128)(2,1)S(1)} %pad_maximum_fusion.8.refs_0_), channel_id=1, source_target_pairs={{0,4},{1,5},{2,6},{3,7},{4,8},{5,9},{6,10},{7,11},{8,12},{9,13},{1... | collective-permute-start | bytes 983048 | tf_op jit(solution)/shard_map/ppermute | solution.py:15
  27.9 1.3 collective-permute-start.10
  29.9 1.4 fusion.42.mask_ref
  32.1 1.0 copy-done.16
  33.1 8.6 %shard_map.85 = (bf16[128,640]{1,0:T(8,128)(2,1)}, bf16[2,128,640]{2,1,0:T(8,128)(2,1)}, bf16[4,2,128,640]{3,2,1,0:T(8,128)(2,1)}, bf16[2,128,640]{2,1,0:T(8,128...) custom-call(s32[128,1280]{1,0:T(8,128)} %fusion.42.mask_ref, ...), custom_call_target="tpu_custom_call" | custom-call | flops 1258291200 | bytes 7700480 | tf_op jit(solution)/shard_map/pallas_call | solution.py:123
  41.7 11.7 %collective-permute-start.28 = (bf16[4,2,128,640]{3,2,1,0:T(8,128)(2,1)}, bf16[4,2,128,640]{3,2,1,0:T(8,128)(2,1)}, u32[]{:S(2)}, u32[]{:S(2)}) collective-permute-start(bf16[4,2,128,640]{3,2,1,0:T(8,128)(2,1)} %get-tuple-element.76), channel_id=1, source_target_pairs={{0,1},{1,0},{2,3},{3,2},{4,5},{5,4},{6,7},{7,6},{8,9},{9,8},{10,11... | collective-permute-start | bytes 3932168 | tf_op jit(solution)/shard_map/ppermute | solution.py:15
  54.2 1.3 collective-permute-start.29
  55.4 4.3 %collective-permute-start.12 = (bf16[2,128,640]{2,1,0:T(8,128)(2,1)S(1)}, bf16[2,128,640]{2,1,0:T(8,128)(2,1)S(1)}, u32[]{:S(2)}, u32[]{:S(2)}) collective-permute-start(bf16[2,128,640]{2,1,0:T(8,128)(2,1)S(1)} %collective-permute-done.8.refs_2_), channel_id=1, source_target_pairs={{0,5},{3,6},{4,9},{7,10},{8,13},{11,14},{16,21},{19,22},{20,25},{2... | collective-permute-start | bytes 983048 | tf_op jit(solution)/shard_map/ppermute | solution.py:15
  60.5 2.1 %collective-permute-done.29 = bf16[2,128,640]{2,1,0:T(8,128)(2,1)S(1)} collective-permute-done((bf16[2,128,640]{2,1,0:T(8,128)(2,1)S(1)}, bf16[2,128,640]{2,1,0:T(8,128)(2,1)S(1)}, u32[]{:S(2)}, u32[]{:S(2)}) %collective-permute-start.29) | collective-permute-done | bytes 327712 | tf_op jit(solution)/shard_map/ppermute | solution.py:15
  62.5 1.4 collective-permute-start.30
  64.3 2.5 %collective-permute-start.15 = (bf16[2,128,640]{2,1,0:T(8,128)(2,1)S(1)}, bf16[2,128,640]{2,1,0:T(8,128)(2,1)S(1)}, u32[]{:S(2)}, u32[]{:S(2)}) collective-permute-start(bf16[2,128,640]{2,1,0:T(8,128)(2,1)S(1)} %pad_maximum_fusion.9.refs_0_), channel_id=1, source_target_pairs={{0,2},{1,3},{2,0},{3,1},{4,6},{5,7},{6,4},{7,5},{8,10},{9,11},{10,... | collective-permute-start | bytes 983048 | tf_op jit(solution)/shard_map/ppermute | solution.py:15
  66.9 2.2 %collective-permute-start.16 = (bf16[2,128,640]{2,1,0:T(8,128)(2,1)S(1)}, bf16[2,128,640]{2,1,0:T(8,128)(2,1)S(1)}, u32[]{:S(2)}, u32[]{:S(2)}) collective-permute-start(bf16[2,128,640]{2,1,0:T(8,128)(2,1)S(1)} %pad_maximum_fusion.9.refs_0_), channel_id=1, source_target_pairs={{0,4},{1,5},{2,6},{3,7},{4,8},{5,9},{6,10},{7,11},{8,12},{9,13},{1... | collective-permute-start | bytes 983048 | tf_op jit(solution)/shard_map/ppermute | solution.py:15
  69.1 1.3 collective-permute-start.17
  70.4 8.6 %shard_map.86 = (bf16[128,640]{1,0:T(8,128)(2,1)}, bf16[2,128,640]{2,1,0:T(8,128)(2,1)}, bf16[4,2,128,640]{3,2,1,0:T(8,128)(2,1)}, bf16[2,128,640]{2,1,0:T(8,128...) custom-call(s32[128,1280]{1,0:T(8,128)} %fusion.42.mask_ref, ...), custom_call_target="tpu_custom_call" | custom-call | flops 1258291200 | bytes 7700480 | tf_op jit(solution)/shard_map/pallas_call | solution.py:123
  79.1 0.9 collective-permute-start.34
  80.1 1.5 collective-permute-done.17.refs_4_
  82.2 2.5 %collective-permute-start.19 = (bf16[2,128,640]{2,1,0:T(8,128)(2,1)S(1)}, bf16[2,128,640]{2,1,0:T(8,128)(2,1)S(1)}, u32[]{:S(2)}, u32[]{:S(2)}) collective-permute-start(bf16[2,128,640]{2,1,0:T(8,128)(2,1)S(1)} %collective-permute-done.15.refs_2_), channel_id=1, source_target_pairs={{0,5},{3,6},{4,9},{7,10},{8,13},{11,14},{16,21},{19,22},{20,25},{2... | collective-permute-start | bytes 983048 | tf_op jit(solution)/shard_map/ppermute | solution.py:15
  85.5 1.3 collective-permute-start.35
  86.8 2.5 %collective-permute-done.19.refs_6_ = bf16[2,128,640]{2,1,0:T(8,128)(2,1)S(1)} collective-permute-done((bf16[2,128,640]{2,1,0:T(8,128)(2,1)S(1)}, bf16[2,128,640]{2,1,0:T(8,128)(2,1)S(1)}, u32[]{:S(2)}, u32[]{:S(2)}) %collective-permute-start.19) | collective-permute-done | bytes 327712 | tf_op jit(solution)/shard_map/ppermute | solution.py:15
  89.3 1.4 collective-permute-start.36
  90.9 2.1 %collective-permute-start.22 = (bf16[2,128,640]{2,1,0:T(8,128)(2,1)S(1)}, bf16[2,128,640]{2,1,0:T(8,128)(2,1)S(1)}, u32[]{:S(2)}, u32[]{:S(2)}) collective-permute-start(bf16[2,128,640]{2,1,0:T(8,128)(2,1)S(1)} %pad_maximum_fusion.10.refs_0_), channel_id=1, source_target_pairs={{0,2},{1,3},{2,0},{3,1},{4,6},{5,7},{6,4},{7,5},{8,10},{9,11},{10,... | collective-permute-start | bytes 983048 | tf_op jit(solution)/shard_map/ppermute | solution.py:15
  93.0 2.2 %collective-permute-done.35 = bf16[2,128,640]{2,1,0:T(8,128)(2,1)} collective-permute-done((bf16[2,128,640]{2,1,0:T(8,128)(2,1)S(1)}, bf16[2,128,640]{2,1,0:T(8,128)(2,1)}, u32[]{:S(2)}, u32[]{:S(2)}) %collective-permute-start.35) | collective-permute-done | bytes 327712 | tf_op jit(solution)/shard_map/ppermute | solution.py:15
  95.2 3.5 %collective-permute-start.23 = (bf16[2,128,640]{2,1,0:T(8,128)(2,1)S(1)}, bf16[2,128,640]{2,1,0:T(8,128)(2,1)S(1)}, u32[]{:S(2)}, u32[]{:S(2)}) collective-permute-start(bf16[2,128,640]{2,1,0:T(8,128)(2,1)S(1)} %pad_maximum_fusion.10.refs_0_), channel_id=1, source_target_pairs={{0,4},{1,5},{2,6},{3,7},{4,8},{5,9},{6,10},{7,11},{8,12},{9,13},{1... | collective-permute-start | bytes 983048 | tf_op jit(solution)/shard_map/ppermute | solution.py:15
  98.7 1.3 collective-permute-start.24
  100.0 8.6 %shard_map.87 = (bf16[128,640]{1,0:T(8,128)(2,1)}, bf16[2,128,640]{2,1,0:T(8,128)(2,1)}, bf16[4,2,128,640]{3,2,1,0:T(8,128)(2,1)}, bf16[2,128,640]{2,1,0:T(8,128...) custom-call(s32[128,1280]{1,0:T(8,128)} %fusion.42.mask_ref, ...), custom_call_target="tpu_custom_call" | custom-call | flops 1258291200 | bytes 7700480 | tf_op jit(solution)/shard_map/pallas_call | solution.py:123
  110.3 1.7 fusion.32
  112.0 1.3 collective-permute-start.32
  113.3 5.2 %collective-permute-start.33 = (bf16[2,128,640]{2,1,0:T(8,128)(2,1)S(1)}, bf16[2,128,640]{2,1,0:T(8,128)(2,1)S(1)}, u32[]{:S(2)}, u32[]{:S(2)}) collective-permute-start(bf16[2,128,640]{2,1,0:T(8,128)(2,1)S(1)} %get-tuple-element.121), channel_id=1, source_target_pairs={{0,4},{1,5},{2,6},{3,7},{4,8},{5,9},{6,10},{7,11},{8,12},{9,13},{1... | collective-permute-start | bytes 983048 | tf_op jit(solution)/shard_map/ppermute | solution.py:15
  118.5 2.4 %collective-permute-done.31 = bf16[2,128,640]{2,1,0:T(8,128)(2,1)S(1)} collective-permute-done((bf16[2,128,640]{2,1,0:T(8,128)(2,1)S(1)}, bf16[2,128,640]{2,1,0:T(8,128)(2,1)S(1)}, u32[]{:S(2)}, u32[]{:S(2)}) %collective-permute-start.31) | collective-permute-done | bytes 327712 | tf_op jit(solution)/shard_map/ppermute | solution.py:15
  121.0 2.9 %collective-permute-done.32 = bf16[2,128,640]{2,1,0:T(8,128)(2,1)S(1)} collective-permute-done((bf16[2,128,640]{2,1,0:T(8,128)(2,1)S(1)}, bf16[2,128,640]{2,1,0:T(8,128)(2,1)S(1)}, u32[]{:S(2)}, u32[]{:S(2)}) %collective-permute-start.32) | collective-permute-done | bytes 327712 | tf_op jit(solution)/shard_map/ppermute | solution.py:15
  123.9 1.8 collective-permute-start.26
  126.4 1.2 fusion.40
  127.6 1.3 collective-permute-start.41
  128.9 1.3 collective-permute-done.26.refs_6_
  130.3 1.4 collective-permute-start.42
  132.4 8.6 %shard_map.88 = (bf16[128,640]{1,0:T(8,128)(2,1)}, bf16[2,128,640]{2,1,0:T(8,128)(2,1)}, bf16[4,2,128,640]{3,2,1,0:T(8,128)(2,1)}, bf16[2,128,640]{2,1,0:T(8,128...) custom-call(s32[128,1280]{1,0:T(8,128)} %fusion.42.mask_ref, ...), custom_call_target="tpu_custom_call" | custom-call | flops 1258291200 | bytes 7700480 | tf_op jit(solution)/shard_map/pallas_call | solution.py:123
  141.1 3.6 %collective-permute-start.46 = (bf16[4,2,128,640]{3,2,1,0:T(8,128)(2,1)}, bf16[4,2,128,640]{3,2,1,0:T(8,128)(2,1)S(1)}, u32[]{:S(2)}, u32[]{:S(2)}) collective-permute-start(bf16[4,2,128,640]{3,2,1,0:T(8,128)(2,1)} %get-tuple-element.112), channel_id=1, source_target_pairs={{0,1},{1,0},{2,3},{3,2},{4,5},{5,4},{6,7},{7,6},{8,9},{9,8},{10,11... | collective-permute-start | bytes 3932168 | tf_op jit(solution)/shard_map/ppermute | solution.py:15
  144.7 1.9 fusion.23
  147.4 1.3 collective-permute-start.38
  148.7 4.9 %collective-permute-start.39 = (bf16[2,128,640]{2,1,0:T(8,128)(2,1)S(1)}, bf16[2,128,640]{2,1,0:T(8,128)(2,1)S(1)}, u32[]{:S(2)}, u32[]{:S(2)}) collective-permute-start(bf16[2,128,640]{2,1,0:T(8,128)(2,1)S(1)} %get-tuple-element.94), channel_id=1, source_target_pairs={{0,4},{1,5},{2,6},{3,7},{4,8},{5,9},{6,10},{7,11},{8,12},{9,13},{1... | collective-permute-start | bytes 983048 | tf_op jit(solution)/shard_map/ppermute | solution.py:15
  153.6 0.9 pad_maximum_fusion.4
  154.5 1.4 collective-permute-start.47
  156.3 3.2 %collective-permute-done.38 = bf16[2,128,640]{2,1,0:T(8,128)(2,1)S(1)} collective-permute-done((bf16[2,128,640]{2,1,0:T(8,128)(2,1)S(1)}, bf16[2,128,640]{2,1,0:T(8,128)(2,1)S(1)}, u32[]{:S(2)}, u32[]{:S(2)}) %collective-permute-start.38) | collective-permute-done | bytes 327712 | tf_op jit(solution)/shard_map/ppermute | solution.py:15
  159.5 1.2 collective-permute-done.39
  160.7 1.2 fusion.31
  162.7 1.5 fusion.14
  164.1 2.6 %collective-permute-start.43 = (bf16[2,128,640]{2,1,0:T(8,128)(2,1)S(1)}, bf16[2,128,640]{2,1,0:T(8,128)(2,1)S(1)}, u32[]{:S(2)}, u32[]{:S(2)}) collective-permute-start(bf16[2,128,640]{2,1,0:T(8,128)(2,1)S(1)} %get-tuple-element.105), channel_id=1, source_target_pairs={{0,2},{1,3},{2,0},{3,1},{4,6},{5,7},{6,4},{7,5},{8,10},{9,11},{10,... | collective-permute-start | bytes 983048 | tf_op jit(solution)/shard_map/ppermute | solution.py:15
  166.7 1.3 collective-permute-start.44
  168.0 5.0 %collective-permute-start.45 = (bf16[2,128,640]{2,1,0:T(8,128)(2,1)S(1)}, bf16[2,128,640]{2,1,0:T(8,128)(2,1)S(1)}, u32[]{:S(2)}, u32[]{:S(2)}) collective-permute-start(bf16[2,128,640]{2,1,0:T(8,128)(2,1)S(1)} %get-tuple-element.107), channel_id=1, source_target_pairs={{0,4},{1,5},{2,6},{3,7},{4,8},{5,9},{6,10},{7,11},{8,12},{9,13},{1... | collective-permute-start | bytes 983048 | tf_op jit(solution)/shard_map/ppermute | solution.py:15
  174.2 5.4 %collective-permute-done.44 = bf16[2,128,640]{2,1,0:T(8,128)(2,1)S(1)} collective-permute-done((bf16[2,128,640]{2,1,0:T(8,128)(2,1)S(1)}, bf16[2,128,640]{2,1,0:T(8,128)(2,1)S(1)}, u32[]{:S(2)}, u32[]{:S(2)}) %collective-permute-start.44) | collective-permute-done | bytes 327712 | tf_op jit(solution)/shard_map/ppermute | solution.py:15
  179.7 1.2 collective-permute-done.45
  180.8 1.3 collective-permute-start.50
  182.1 5.0 %collective-permute-start.51 = (bf16[2,128,640]{2,1,0:T(8,128)(2,1)S(1)}, bf16[2,128,640]{2,1,0:T(8,128)(2,1)S(1)}, u32[]{:S(2)}, u32[]{:S(2)}) collective-permute-start(bf16[2,128,640]{2,1,0:T(8,128)(2,1)S(1)} %get-tuple-element.120), channel_id=1, source_target_pairs={{0,4},{1,5},{2,6},{3,7},{4,8},{5,9},{6,10},{7,11},{8,12},{9,13},{1... | collective-permute-start | bytes 983048 | tf_op jit(solution)/shard_map/ppermute | solution.py:15
  187.5 2.8 %collective-permute-done.49 = bf16[2,128,640]{2,1,0:T(8,128)(2,1)S(1)} collective-permute-done((bf16[2,128,640]{2,1,0:T(8,128)(2,1)S(1)}, bf16[2,128,640]{2,1,0:T(8,128)(2,1)S(1)}, u32[]{:S(2)}, u32[]{:S(2)}) %collective-permute-start.49) | collective-permute-done | bytes 327712 | tf_op jit(solution)/shard_map/ppermute | solution.py:15
  190.3 2.8 %collective-permute-done.50 = bf16[2,128,640]{2,1,0:T(8,128)(2,1)S(1)} collective-permute-done((bf16[2,128,640]{2,1,0:T(8,128)(2,1)S(1)}, bf16[2,128,640]{2,1,0:T(8,128)(2,1)S(1)}, u32[]{:S(2)}, u32[]{:S(2)}) %collective-permute-start.50) | collective-permute-done | bytes 327712 | tf_op jit(solution)/shard_map/ppermute | solution.py:15
  193.0 1.2 collective-permute-done.51
  (211 shorter events, 14.1 us)
Async XLA Ops:
  2.9 17.6 %copy-start.60 = (s32[4]{0:T(128)S(1)}, s32[4]{0:T(128)}, u32[]{:S(2)}) copy-start(s32[4]{0:T(128)} %param.11) | copy-start | bytes 52
  3.0 17.7 %copy-start = (bf16[2,128,640]{2,1,0:T(8,128)(2,1)}, bf16[2,128,640]{2,1,0:T(8,128)(2,1)S(1)}, u32[]{:S(2)}) copy-start(bf16[2,128,640]{2,1,0:T(8,128)(2,1)S(1)} %pad_maximum_fusion.7.refs_0_) | copy-start | bytes 983044
  3.0 10.8 %collective-permute-start.1 = (bf16[2,128,640]{2,1,0:T(8,128)(2,1)S(1)}, bf16[2,128,640]{2,1,0:T(8,128)(2,1)S(1)}, u32[]{:S(2)}, u32[]{:S(2)}) collective-permute-start(bf16[2,128,640]{2,1,0:T(8,128)(2,1)S(1)} %pad_maximum_fusion.7.refs_0_), channel_id=1, source_target_pairs={{0,2},{1,3},{2,0},{3,1},{4,6},{5,7},{6,4},{7,5},{8,10},{9,11},{10,... | collective-permute-start | bytes 983048 | tf_op jit(solution)/shard_map/ppermute | solution.py:15
  6.0 10.1 %collective-permute-start.2 = (bf16[2,128,640]{2,1,0:T(8,128)(2,1)S(1)}, bf16[2,128,640]{2,1,0:T(8,128)(2,1)S(1)}, u32[]{:S(2)}, u32[]{:S(2)}) collective-permute-start(bf16[2,128,640]{2,1,0:T(8,128)(2,1)S(1)} %pad_maximum_fusion.7.refs_0_), channel_id=1, source_target_pairs={{0,4},{1,5},{2,6},{3,7},{4,8},{5,9},{6,10},{7,11},{8,12},{9,13},{1... | collective-permute-start | bytes 983048 | tf_op jit(solution)/shard_map/ppermute | solution.py:15
  9.5 10.8 %collective-permute-start.3 = (bf16[2,128,640]{2,1,0:T(8,128)(2,1)S(1)}, bf16[2,128,640]{2,1,0:T(8,128)(2,1)S(1)}, u32[]{:S(2)}, u32[]{:S(2)}) collective-permute-start(bf16[2,128,640]{2,1,0:T(8,128)(2,1)S(1)} %pad_maximum_fusion.7.refs_0_), channel_id=1, source_target_pairs={{4,0},{5,1},{6,2},{7,3},{8,4},{9,5},{10,6},{11,7},{12,8},{13,9},{1... | collective-permute-start | bytes 983048 | tf_op jit(solution)/shard_map/ppermute | solution.py:15
  10.8 13.5 %collective-permute-start = (bf16[2,128,640]{2,1,0:T(8,128)(2,1)S(1)}, bf16[2,128,640]{2,1,0:T(8,128)(2,1)S(1)}, u32[]{:S(2)}, u32[]{:S(2)}) collective-permute-start(bf16[2,128,640]{2,1,0:T(8,128)(2,1)S(1)} %pad_maximum_fusion.7.refs_0_), channel_id=1, source_target_pairs={{0,1},{1,0},{2,3},{3,2},{4,5},{5,4},{6,7},{7,6},{8,9},{9,8},{10,11... | collective-permute-start | bytes 983048 | tf_op jit(solution)/shard_map/ppermute | solution.py:15
  13.7 15.5 %copy-start.4 = (bf16[2,128,640]{2,1,0:T(8,128)(2,1)}, bf16[2,128,640]{2,1,0:T(8,128)(2,1)S(1)}, u32[]{:S(2)}) copy-start(bf16[2,128,640]{2,1,0:T(8,128)(2,1)S(1)} %collective-permute-done.1.refs_2_) | copy-start | bytes 983044
  20.4 11.7 %collective-permute-start.4 = (bf16[3,2,128,640]{3,2,1,0:T(8,128)(2,1)S(1)}, bf16[3,2,128,640]{3,2,1,0:T(8,128)(2,1)S(1)}, u32[]{:S(2)}, u32[]{:S(2)}) collective-permute-start(bf16[3,2,128,640]{3,2,1,0:T(8,128)(2,1)S(1)} %pad_maximum_fusion), channel_id=1, source_target_pairs={{0,1},{1,0},{2,3},{3,2},{4,5},{5,4},{6,7},{7,6},{8,9},{9,8},{10,11... | collective-permute-start | bytes 2949128 | tf_op jit(solution)/shard_map/ppermute | solution.py:15
  21.0 32.6 %copy-start.2 = (bf16[2,128,640]{2,1,0:T(8,128)(2,1)}, bf16[2,128,640]{2,1,0:T(8,128)(2,1)S(1)}, u32[]{:S(2)}) copy-start(bf16[2,128,640]{2,1,0:T(8,128)(2,1)S(1)} %pad_maximum_fusion.8.refs_0_) | copy-start | bytes 983044
  21.0 8.2 %collective-permute-start.5 = (bf16[2,128,640]{2,1,0:T(8,128)(2,1)S(1)}, bf16[2,128,640]{2,1,0:T(8,128)(2,1)S(1)}, u32[]{:S(2)}, u32[]{:S(2)}) collective-permute-start(bf16[2,128,640]{2,1,0:T(8,128)(2,1)S(1)} %collective-permute-done.1.refs_2_), channel_id=1, source_target_pairs={{0,5},{3,6},{4,9},{7,10},{8,13},{11,14},{16,21},{19,22},{20,25},{2... | collective-permute-start | bytes 983048 | tf_op jit(solution)/shard_map/ppermute | solution.py:15
  24.3 29.1 %collective-permute-start.8 = (bf16[2,128,640]{2,1,0:T(8,128)(2,1)S(1)}, bf16[2,128,640]{2,1,0:T(8,128)(2,1)S(1)}, u32[]{:S(2)}, u32[]{:S(2)}) collective-permute-start(bf16[2,128,640]{2,1,0:T(8,128)(2,1)S(1)} %pad_maximum_fusion.8.refs_0_), channel_id=1, source_target_pairs={{0,2},{1,3},{2,0},{3,1},{4,6},{5,7},{6,4},{7,5},{8,10},{9,11},{10,... | collective-permute-start | bytes 983048 | tf_op jit(solution)/shard_map/ppermute | solution.py:15
  24.4 29.0 %collective-permute-start.9 = (bf16[2,128,640]{2,1,0:T(8,128)(2,1)S(1)}, bf16[2,128,640]{2,1,0:T(8,128)(2,1)S(1)}, u32[]{:S(2)}, u32[]{:S(2)}) collective-permute-start(bf16[2,128,640]{2,1,0:T(8,128)(2,1)S(1)} %pad_maximum_fusion.8.refs_0_), channel_id=1, source_target_pairs={{0,4},{1,5},{2,6},{3,7},{4,8},{5,9},{6,10},{7,11},{8,12},{9,13},{1... | collective-permute-start | bytes 983048 | tf_op jit(solution)/shard_map/ppermute | solution.py:15
  27.9 25.5 %collective-permute-start.10 = (bf16[2,128,640]{2,1,0:T(8,128)(2,1)S(1)}, bf16[2,128,640]{2,1,0:T(8,128)(2,1)S(1)}, u32[]{:S(2)}, u32[]{:S(2)}) collective-permute-start(bf16[2,128,640]{2,1,0:T(8,128)(2,1)S(1)} %pad_maximum_fusion.8.refs_0_), channel_id=1, source_target_pairs={{4,0},{5,1},{6,2},{7,3},{8,4},{9,5},{10,6},{11,7},{12,8},{13,9},{1... | collective-permute-start | bytes 983048 | tf_op jit(solution)/shard_map/ppermute | solution.py:15
  29.3 2.1 %collective-permute-start.6 = (bf16[2,128,640]{2,1,0:T(8,128)(2,1)S(1)}, bf16[2,128,640]{2,1,0:T(8,128)(2,1)S(1)}, u32[]{:S(2)}, u32[]{:S(2)}) collective-permute-start(bf16[2,128,640]{2,1,0:T(8,128)(2,1)S(1)} %collective-permute-done.1.refs_2_), channel_id=1, source_target_pairs={{4,1},{7,2},{8,5},{11,6},{12,9},{15,10},{20,17},{23,18},{24,21},{2... | collective-permute-start | bytes 983048 | tf_op jit(solution)/shard_map/ppermute | solution.py:15
  41.6 22.3 %copy-start.20 = (bf16[1,128,640]{2,1,0:T(8,128)(2,1)S(1)}, bf16[1,128,640]{2,1,0:T(8,128)(2,1)}, u32[]{:S(2)}) copy-start(bf16[1,128,640]{2,1,0:T(8,128)(2,1)} %get-tuple-element.140) | copy-start | bytes 491524
  41.6 22.3 %copy-start.21 = (bf16[1,128,640]{2,1,0:T(8,128)(2,1)S(1)}, bf16[1,128,640]{2,1,0:T(8,128)(2,1)}, u32[]{:S(2)}) copy-start(bf16[1,128,640]{2,1,0:T(8,128)(2,1)} %get-tuple-element.156) | copy-start | bytes 491524
  41.7 37.4 %collective-permute-start.28 = (bf16[4,2,128,640]{3,2,1,0:T(8,128)(2,1)}, bf16[4,2,128,640]{3,2,1,0:T(8,128)(2,1)}, u32[]{:S(2)}, u32[]{:S(2)}) collective-permute-start(bf16[4,2,128,640]{3,2,1,0:T(8,128)(2,1)} %get-tuple-element.76), channel_id=1, source_target_pairs={{0,1},{1,0},{2,3},{3,2},{4,5},{5,4},{6,7},{7,6},{8,9},{9,8},{10,11... | collective-permute-start | bytes 3932168 | tf_op jit(solution)/shard_map/ppermute | solution.py:15
  53.6 15.5 %collective-permute-start.11 = (bf16[3,2,128,640]{3,2,1,0:T(8,128)(2,1)S(1)}, bf16[3,2,128,640]{3,2,1,0:T(8,128)(2,1)S(1)}, u32[]{:S(2)}, u32[]{:S(2)}) collective-permute-start(bf16[3,2,128,640]{3,2,1,0:T(8,128)(2,1)S(1)} %pad_maximum_fusion.1), channel_id=1, source_target_pairs={{0,1},{1,0},{2,3},{3,2},{4,5},{5,4},{6,7},{7,6},{8,9},{9,8},{10,11... | collective-permute-start | bytes 2949128 | tf_op jit(solution)/shard_map/ppermute | solution.py:15
  53.7 6.1 %collective-permute-start.7 = (bf16[2,128,640]{2,1,0:T(8,128)(2,1)S(1)}, bf16[2,128,640]{2,1,0:T(8,128)(2,1)S(1)}, u32[]{:S(2)}, u32[]{:S(2)}) collective-permute-start(bf16[2,128,640]{2,1,0:T(8,128)(2,1)S(1)} %pad_maximum_fusion.8.refs_0_), channel_id=1, source_target_pairs={{0,1},{1,0},{2,3},{3,2},{4,5},{5,4},{6,7},{7,6},{8,9},{9,8},{10,11... | collective-permute-start | bytes 983048 | tf_op jit(solution)/shard_map/ppermute | solution.py:15
  54.2 8.4 %collective-permute-start.29 = (bf16[2,128,640]{2,1,0:T(8,128)(2,1)S(1)}, bf16[2,128,640]{2,1,0:T(8,128)(2,1)S(1)}, u32[]{:S(2)}, u32[]{:S(2)}) collective-permute-start(bf16[2,128,640]{2,1,0:T(8,128)(2,1)S(1)} %copy-done.59), channel_id=1, source_target_pairs={{5,0},{6,3},{9,4},{10,7},{13,8},{14,11},{21,16},{22,19},{25,20},{2... | collective-permute-start | bytes 983048 | tf_op jit(solution)/shard_map/ppermute | solution.py:15
  55.4 8.9 %collective-permute-start.12 = (bf16[2,128,640]{2,1,0:T(8,128)(2,1)S(1)}, bf16[2,128,640]{2,1,0:T(8,128)(2,1)S(1)}, u32[]{:S(2)}, u32[]{:S(2)}) collective-permute-start(bf16[2,128,640]{2,1,0:T(8,128)(2,1)S(1)} %collective-permute-done.8.refs_2_), channel_id=1, source_target_pairs={{0,5},{3,6},{4,9},{7,10},{8,13},{11,14},{16,21},{19,22},{20,25},{2... | collective-permute-start | bytes 983048 | tf_op jit(solution)/shard_map/ppermute | solution.py:15
  59.8 7.1 %collective-permute-start.13 = (bf16[2,128,640]{2,1,0:T(8,128)(2,1)S(1)}, bf16[2,128,640]{2,1,0:T(8,128)(2,1)S(1)}, u32[]{:S(2)}, u32[]{:S(2)}) collective-permute-start(bf16[2,128,640]{2,1,0:T(8,128)(2,1)S(1)} %collective-permute-done.8.refs_2_), channel_id=1, source_target_pairs={{4,1},{7,2},{8,5},{11,6},{12,9},{15,10},{20,17},{23,18},{24,21},{2... | collective-permute-start | bytes 983048 | tf_op jit(solution)/shard_map/ppermute | solution.py:15
  62.5 16.5 %collective-permute-start.30 = (bf16[2,128,640]{2,1,0:T(8,128)(2,1)}, bf16[2,128,640]{2,1,0:T(8,128)(2,1)}, u32[]{:S(2)}, u32[]{:S(2)}) collective-permute-start(bf16[2,128,640]{2,1,0:T(8,128)(2,1)} %get-tuple-element.79), channel_id=1, source_target_pairs={{1,4},{2,7},{5,8},{6,11},{9,12},{10,15},{17,20},{18,23},{21,24},{2... | collective-permute-start | bytes 983048 | tf_op jit(solution)/shard_map/ppermute | solution.py:15
  64.0 17.8 %copy-start.3 = (bf16[2,128,640]{2,1,0:T(8,128)(2,1)}, bf16[2,128,640]{2,1,0:T(8,128)(2,1)S(1)}, u32[]{:S(2)}) copy-start(bf16[2,128,640]{2,1,0:T(8,128)(2,1)S(1)} %pad_maximum_fusion.9.refs_0_) | copy-start | bytes 983044
  64.3 15.7 %collective-permute-start.15 = (bf16[2,128,640]{2,1,0:T(8,128)(2,1)S(1)}, bf16[2,128,640]{2,1,0:T(8,128)(2,1)S(1)}, u32[]{:S(2)}, u32[]{:S(2)}) collective-permute-start(bf16[2,128,640]{2,1,0:T(8,128)(2,1)S(1)} %pad_maximum_fusion.9.refs_0_), channel_id=1, source_target_pairs={{0,2},{1,3},{2,0},{3,1},{4,6},{5,7},{6,4},{7,5},{8,10},{9,11},{10,... | collective-permute-start | bytes 983048 | tf_op jit(solution)/shard_map/ppermute | solution.py:15
  66.9 13.2 %collective-permute-start.16 = (bf16[2,128,640]{2,1,0:T(8,128)(2,1)S(1)}, bf16[2,128,640]{2,1,0:T(8,128)(2,1)S(1)}, u32[]{:S(2)}, u32[]{:S(2)}) collective-permute-start(bf16[2,128,640]{2,1,0:T(8,128)(2,1)S(1)} %pad_maximum_fusion.9.refs_0_), channel_id=1, source_target_pairs={{0,4},{1,5},{2,6},{3,7},{4,8},{5,9},{6,10},{7,11},{8,12},{9,13},{1... | collective-permute-start | bytes 983048 | tf_op jit(solution)/shard_map/ppermute | solution.py:15
  69.1 12.4 %collective-permute-start.17 = (bf16[2,128,640]{2,1,0:T(8,128)(2,1)S(1)}, bf16[2,128,640]{2,1,0:T(8,128)(2,1)S(1)}, u32[]{:S(2)}, u32[]{:S(2)}) collective-permute-start(bf16[2,128,640]{2,1,0:T(8,128)(2,1)S(1)} %pad_maximum_fusion.9.refs_0_), channel_id=1, source_target_pairs={{4,0},{5,1},{6,2},{7,3},{8,4},{9,5},{10,6},{11,7},{12,8},{13,9},{1... | collective-permute-start | bytes 983048 | tf_op jit(solution)/shard_map/ppermute | solution.py:15
  79.1 29.6 %collective-permute-start.34 = (bf16[4,2,128,640]{3,2,1,0:T(8,128)(2,1)}, bf16[4,2,128,640]{3,2,1,0:T(8,128)(2,1)}, u32[]{:S(2)}, u32[]{:S(2)}) collective-permute-start(bf16[4,2,128,640]{3,2,1,0:T(8,128)(2,1)} %get-tuple-element.86), channel_id=1, source_target_pairs={{0,1},{1,0},{2,3},{3,2},{4,5},{5,4},{6,7},{7,6},{8,9},{9,8},{10,11... | collective-permute-start | bytes 3932168 | tf_op jit(solution)/shard_map/ppermute | solution.py:15
  81.7 17.0 %collective-permute-start.18 = (bf16[3,2,128,640]{3,2,1,0:T(8,128)(2,1)S(1)}, bf16[3,2,128,640]{3,2,1,0:T(8,128)(2,1)S(1)}, u32[]{:S(2)}, u32[]{:S(2)}) collective-permute-start(bf16[3,2,128,640]{3,2,1,0:T(8,128)(2,1)S(1)} %pad_maximum_fusion.2), channel_id=1, source_target_pairs={{0,1},{1,0},{2,3},{3,2},{4,5},{5,4},{6,7},{7,6},{8,9},{9,8},{10,11... | collective-permute-start | bytes 2949128 | tf_op jit(solution)/shard_map/ppermute | solution.py:15
  81.8 3.7 %collective-permute-start.14 = (bf16[2,128,640]{2,1,0:T(8,128)(2,1)S(1)}, bf16[2,128,640]{2,1,0:T(8,128)(2,1)S(1)}, u32[]{:S(2)}, u32[]{:S(2)}) collective-permute-start(bf16[2,128,640]{2,1,0:T(8,128)(2,1)S(1)} %pad_maximum_fusion.9.refs_0_), channel_id=1, source_target_pairs={{0,1},{1,0},{2,3},{3,2},{4,5},{5,4},{6,7},{7,6},{8,9},{9,8},{10,11... | collective-permute-start | bytes 983048 | tf_op jit(solution)/shard_map/ppermute | solution.py:15
  82.2 7.1 %collective-permute-start.19 = (bf16[2,128,640]{2,1,0:T(8,128)(2,1)S(1)}, bf16[2,128,640]{2,1,0:T(8,128)(2,1)S(1)}, u32[]{:S(2)}, u32[]{:S(2)}) collective-permute-start(bf16[2,128,640]{2,1,0:T(8,128)(2,1)S(1)} %collective-permute-done.15.refs_2_), channel_id=1, source_target_pairs={{0,5},{3,6},{4,9},{7,10},{8,13},{11,14},{16,21},{19,22},{20,25},{2... | collective-permute-start | bytes 983048 | tf_op jit(solution)/shard_map/ppermute | solution.py:15
  84.8 6.1 %collective-permute-start.20 = (bf16[2,128,640]{2,1,0:T(8,128)(2,1)S(1)}, bf16[2,128,640]{2,1,0:T(8,128)(2,1)S(1)}, u32[]{:S(2)}, u32[]{:S(2)}) collective-permute-start(bf16[2,128,640]{2,1,0:T(8,128)(2,1)S(1)} %collective-permute-done.15.refs_2_), channel_id=1, source_target_pairs={{4,1},{7,2},{8,5},{11,6},{12,9},{15,10},{20,17},{23,18},{24,21},{2... | collective-permute-start | bytes 983048 | tf_op jit(solution)/shard_map/ppermute | solution.py:15
  85.5 9.7 %collective-permute-start.35 = (bf16[2,128,640]{2,1,0:T(8,128)(2,1)S(1)}, bf16[2,128,640]{2,1,0:T(8,128)(2,1)}, u32[]{:S(2)}, u32[]{:S(2)}) collective-permute-start(bf16[2,128,640]{2,1,0:T(8,128)(2,1)S(1)} %copy-done.58), channel_id=1, source_target_pairs={{5,0},{6,3},{9,4},{10,7},{13,8},{14,11},{21,16},{22,19},{25,20},{2... | collective-permute-start | bytes 983048 | tf_op jit(solution)/shard_map/ppermute | solution.py:15
  89.3 19.3 %collective-permute-start.36 = (bf16[2,128,640]{2,1,0:T(8,128)(2,1)}, bf16[2,128,640]{2,1,0:T(8,128)(2,1)}, u32[]{:S(2)}, u32[]{:S(2)}) collective-permute-start(bf16[2,128,640]{2,1,0:T(8,128)(2,1)} %get-tuple-element.89), channel_id=1, source_target_pairs={{1,4},{2,7},{5,8},{6,11},{9,12},{10,15},{17,20},{18,23},{21,24},{2... | collective-permute-start | bytes 983048 | tf_op jit(solution)/shard_map/ppermute | solution.py:15
  90.8 30.1 %copy-start.1 = (bf16[2,128,640]{2,1,0:T(8,128)(2,1)}, bf16[2,128,640]{2,1,0:T(8,128)(2,1)S(1)}, u32[]{:S(2)}) copy-start(bf16[2,128,640]{2,1,0:T(8,128)(2,1)S(1)} %pad_maximum_fusion.10.refs_0_) | copy-start | bytes 983044
  90.9 17.9 %collective-permute-start.22 = (bf16[2,128,640]{2,1,0:T(8,128)(2,1)S(1)}, bf16[2,128,640]{2,1,0:T(8,128)(2,1)S(1)}, u32[]{:S(2)}, u32[]{:S(2)}) collective-permute-start(bf16[2,128,640]{2,1,0:T(8,128)(2,1)S(1)} %pad_maximum_fusion.10.refs_0_), channel_id=1, source_target_pairs={{0,2},{1,3},{2,0},{3,1},{4,6},{5,7},{6,4},{7,5},{8,10},{9,11},{10,... | collective-permute-start | bytes 983048 | tf_op jit(solution)/shard_map/ppermute | solution.py:15
  95.2 13.6 %collective-permute-start.23 = (bf16[2,128,640]{2,1,0:T(8,128)(2,1)S(1)}, bf16[2,128,640]{2,1,0:T(8,128)(2,1)S(1)}, u32[]{:S(2)}, u32[]{:S(2)}) collective-permute-start(bf16[2,128,640]{2,1,0:T(8,128)(2,1)S(1)} %pad_maximum_fusion.10.refs_0_), channel_id=1, source_target_pairs={{0,4},{1,5},{2,6},{3,7},{4,8},{5,9},{6,10},{7,11},{8,12},{9,13},{1... | collective-permute-start | bytes 983048 | tf_op jit(solution)/shard_map/ppermute | solution.py:15
  98.7 10.1 %collective-permute-start.24 = (bf16[2,128,640]{2,1,0:T(8,128)(2,1)S(1)}, bf16[2,128,640]{2,1,0:T(8,128)(2,1)S(1)}, u32[]{:S(2)}, u32[]{:S(2)}) collective-permute-start(bf16[2,128,640]{2,1,0:T(8,128)(2,1)S(1)} %pad_maximum_fusion.10.refs_0_), channel_id=1, source_target_pairs={{4,0},{5,1},{6,2},{7,3},{8,4},{9,5},{10,6},{11,7},{12,8},{13,9},{1... | collective-permute-start | bytes 983048 | tf_op jit(solution)/shard_map/ppermute | solution.py:15
  108.7 32.4 %collective-permute-start.40 = (bf16[4,2,128,640]{3,2,1,0:T(8,128)(2,1)}, bf16[4,2,128,640]{3,2,1,0:T(8,128)(2,1)S(1)}, u32[]{:S(2)}, u32[]{:S(2)}) collective-permute-start(bf16[4,2,128,640]{3,2,1,0:T(8,128)(2,1)} %get-tuple-element.99), channel_id=1, source_target_pairs={{0,1},{1,0},{2,3},{3,2},{4,5},{5,4},{6,7},{7,6},{8,9},{9,8},{10,11... | collective-permute-start | bytes 3932168 | tf_op jit(solution)/shard_map/ppermute | solution.py:15
  108.8 16.9 %copy-start.7 = (bf16[2,128,640]{2,1,0:T(8,128)(2,1)}, bf16[2,128,640]{2,1,0:T(8,128)(2,1)S(1)}, u32[]{:S(2)}) copy-start(bf16[2,128,640]{2,1,0:T(8,128)(2,1)S(1)} %collective-permute-done.22.refs_2_) | copy-start | bytes 983044
  109.0 22.7 %collective-permute-start.25 = (bf16[3,2,128,640]{3,2,1,0:T(8,128)(2,1)S(1)}, bf16[3,2,128,640]{3,2,1,0:T(8,128)(2,1)}, u32[]{:S(2)}, u32[]{:S(2)}) collective-permute-start(bf16[3,2,128,640]{3,2,1,0:T(8,128)(2,1)S(1)} %pad_maximum_fusion.3), channel_id=1, source_target_pairs={{0,1},{1,0},{2,3},{3,2},{4,5},{5,4},{6,7},{7,6},{8,9},{9,8},{10,11... | collective-permute-start | bytes 2949128 | tf_op jit(solution)/shard_map/ppermute | solution.py:15
  110.3 16.1 %copy-start.49 = (bf16[2,128,640]{2,1,0:T(8,128)(2,1)S(1)}, bf16[2,128,640]{2,1,0:T(8,128)(2,1)}, u32[]{:S(2)}) copy-start(bf16[2,128,640]{2,1,0:T(8,128)(2,1)} %get-tuple-element.75) | copy-start | bytes 983044
  112.0 9.0 %collective-permute-start.31 = (bf16[2,128,640]{2,1,0:T(8,128)(2,1)S(1)}, bf16[2,128,640]{2,1,0:T(8,128)(2,1)S(1)}, u32[]{:S(2)}, u32[]{:S(2)}) collective-permute-start(bf16[2,128,640]{2,1,0:T(8,128)(2,1)S(1)} %get-tuple-element.123), channel_id=1, source_target_pairs={{0,2},{1,3},{2,0},{3,1},{4,6},{5,7},{6,4},{7,5},{8,10},{9,11},{10,... | collective-permute-start | bytes 983048 | tf_op jit(solution)/shard_map/ppermute | solution.py:15
  112.0 11.8 %collective-permute-start.32 = (bf16[2,128,640]{2,1,0:T(8,128)(2,1)S(1)}, bf16[2,128,640]{2,1,0:T(8,128)(2,1)S(1)}, u32[]{:S(2)}, u32[]{:S(2)}) collective-permute-start(bf16[2,128,640]{2,1,0:T(8,128)(2,1)S(1)} %get-tuple-element.122), channel_id=1, source_target_pairs={{4,0},{5,1},{6,2},{7,3},{8,4},{9,5},{10,6},{11,7},{12,8},{13,9},{1... | collective-permute-start | bytes 983048 | tf_op jit(solution)/shard_map/ppermute | solution.py:15
  113.3 12.4 %collective-permute-start.33 = (bf16[2,128,640]{2,1,0:T(8,128)(2,1)S(1)}, bf16[2,128,640]{2,1,0:T(8,128)(2,1)S(1)}, u32[]{:S(2)}, u32[]{:S(2)}) collective-permute-start(bf16[2,128,640]{2,1,0:T(8,128)(2,1)S(1)} %get-tuple-element.121), channel_id=1, source_target_pairs={{0,4},{1,5},{2,6},{3,7},{4,8},{5,9},{6,10},{7,11},{8,12},{9,13},{1... | collective-permute-start | bytes 983048 | tf_op jit(solution)/shard_map/ppermute | solution.py:15
  121.0 6.6 %collective-permute-start.21 = (bf16[2,128,640]{2,1,0:T(8,128)(2,1)S(1)}, bf16[2,128,640]{2,1,0:T(8,128)(2,1)S(1)}, u32[]{:S(2)}, u32[]{:S(2)}) collective-permute-start(bf16[2,128,640]{2,1,0:T(8,128)(2,1)S(1)} %pad_maximum_fusion.10.refs_0_), channel_id=1, source_target_pairs={{0,1},{1,0},{2,3},{3,2},{4,5},{5,4},{6,7},{7,6},{8,9},{9,8},{10,11... | collective-permute-start | bytes 983048 | tf_op jit(solution)/shard_map/ppermute | solution.py:15
  123.9 6.4 %collective-permute-start.26 = (bf16[2,128,640]{2,1,0:T(8,128)(2,1)S(1)}, bf16[2,128,640]{2,1,0:T(8,128)(2,1)S(1)}, u32[]{:S(2)}, u32[]{:S(2)}) collective-permute-start(bf16[2,128,640]{2,1,0:T(8,128)(2,1)S(1)} %collective-permute-done.22.refs_2_), channel_id=1, source_target_pairs={{0,5},{3,6},{4,9},{7,10},{8,13},{11,14},{16,21},{19,22},{20,25},{2... | collective-permute-start | bytes 983048 | tf_op jit(solution)/shard_map/ppermute | solution.py:15
  125.7 6.0 %collective-permute-start.27 = (bf16[2,128,640]{2,1,0:T(8,128)(2,1)S(1)}, bf16[2,128,640]{2,1,0:T(8,128)(2,1)S(1)}, u32[]{:S(2)}, u32[]{:S(2)}) collective-permute-start(bf16[2,128,640]{2,1,0:T(8,128)(2,1)S(1)} %collective-permute-done.22.refs_2_), channel_id=1, source_target_pairs={{4,1},{7,2},{8,5},{11,6},{12,9},{15,10},{20,17},{23,18},{24,21},{2... | collective-permute-start | bytes 983048 | tf_op jit(solution)/shard_map/ppermute | solution.py:15
  127.6 13.4 %collective-permute-start.41 = (bf16[2,128,640]{2,1,0:T(8,128)(2,1)}, bf16[2,128,640]{2,1,0:T(8,128)(2,1)}, u32[]{:S(2)}, u32[]{:S(2)}) collective-permute-start(bf16[2,128,640]{2,1,0:T(8,128)(2,1)} %get-tuple-element.101), channel_id=1, source_target_pairs={{5,0},{6,3},{9,4},{10,7},{13,8},{14,11},{21,16},{22,19},{25,20},{2... | collective-permute-start | bytes 983048 | tf_op jit(solution)/shard_map/ppermute | solution.py:15
  130.3 10.8 %collective-permute-start.42 = (bf16[2,128,640]{2,1,0:T(8,128)(2,1)}, bf16[2,128,640]{2,1,0:T(8,128)(2,1)}, u32[]{:S(2)}, u32[]{:S(2)}) collective-permute-start(bf16[2,128,640]{2,1,0:T(8,128)(2,1)} %get-tuple-element.102), channel_id=1, source_target_pairs={{1,4},{2,7},{5,8},{6,11},{9,12},{10,15},{17,20},{18,23},{21,24},{2... | collective-permute-start | bytes 983048 | tf_op jit(solution)/shard_map/ppermute | solution.py:15
  141.1 32.0 %collective-permute-start.46 = (bf16[4,2,128,640]{3,2,1,0:T(8,128)(2,1)}, bf16[4,2,128,640]{3,2,1,0:T(8,128)(2,1)S(1)}, u32[]{:S(2)}, u32[]{:S(2)}) collective-permute-start(bf16[4,2,128,640]{3,2,1,0:T(8,128)(2,1)} %get-tuple-element.112), channel_id=1, source_target_pairs={{0,1},{1,0},{2,3},{3,2},{4,5},{5,4},{6,7},{7,6},{8,9},{9,8},{10,11... | collective-permute-start | bytes 3932168 | tf_op jit(solution)/shard_map/ppermute | solution.py:15
  146.6 14.1 %copy-start.47 = (bf16[2,128,640]{2,1,0:T(8,128)(2,1)S(1)}, bf16[2,128,640]{2,1,0:T(8,128)(2,1)}, u32[]{:S(2)}) copy-start(bf16[2,128,640]{2,1,0:T(8,128)(2,1)} %get-tuple-element.82) | copy-start | bytes 983044
  146.6 9.7 %collective-permute-start.37 = (bf16[2,128,640]{2,1,0:T(8,128)(2,1)S(1)}, bf16[2,128,640]{2,1,0:T(8,128)(2,1)S(1)}, u32[]{:S(2)}, u32[]{:S(2)}) collective-permute-start(bf16[2,128,640]{2,1,0:T(8,128)(2,1)S(1)} %get-tuple-element.92), channel_id=1, source_target_pairs={{0,2},{1,3},{2,0},{3,1},{4,6},{5,7},{6,4},{7,5},{8,10},{9,11},{10,... | collective-permute-start | bytes 983048 | tf_op jit(solution)/shard_map/ppermute | solution.py:15
  147.4 12.1 %collective-permute-start.38 = (bf16[2,128,640]{2,1,0:T(8,128)(2,1)S(1)}, bf16[2,128,640]{2,1,0:T(8,128)(2,1)S(1)}, u32[]{:S(2)}, u32[]{:S(2)}) collective-permute-start(bf16[2,128,640]{2,1,0:T(8,128)(2,1)S(1)} %get-tuple-element.93), channel_id=1, source_target_pairs={{4,0},{5,1},{6,2},{7,3},{8,4},{9,5},{10,6},{11,7},{12,8},{13,9},{1... | collective-permute-start | bytes 983048 | tf_op jit(solution)/shard_map/ppermute | solution.py:15
  148.7 12.0 %collective-permute-start.39 = (bf16[2,128,640]{2,1,0:T(8,128)(2,1)S(1)}, bf16[2,128,640]{2,1,0:T(8,128)(2,1)S(1)}, u32[]{:S(2)}, u32[]{:S(2)}) collective-permute-start(bf16[2,128,640]{2,1,0:T(8,128)(2,1)S(1)} %get-tuple-element.94), channel_id=1, source_target_pairs={{0,4},{1,5},{2,6},{3,7},{4,8},{5,9},{6,10},{7,11},{8,12},{9,13},{1... | collective-permute-start | bytes 983048 | tf_op jit(solution)/shard_map/ppermute | solution.py:15
  154.5 13.5 %collective-permute-start.47 = (bf16[2,128,640]{2,1,0:T(8,128)(2,1)S(1)}, bf16[2,128,640]{2,1,0:T(8,128)(2,1)S(1)}, u32[]{:S(2)}, u32[]{:S(2)}) collective-permute-start(bf16[2,128,640]{2,1,0:T(8,128)(2,1)S(1)} %copy-done.57), channel_id=1, source_target_pairs={{5,0},{6,3},{9,4},{10,7},{13,8},{14,11},{21,16},{22,19},{25,20},{2... | collective-permute-start | bytes 983048 | tf_op jit(solution)/shard_map/ppermute | solution.py:15
  161.9 11.2 %collective-permute-start.48 = (bf16[2,128,640]{2,1,0:T(8,128)(2,1)S(1)}, bf16[2,128,640]{2,1,0:T(8,128)(2,1)S(1)}, u32[]{:S(2)}, u32[]{:S(2)}) collective-permute-start(bf16[2,128,640]{2,1,0:T(8,128)(2,1)S(1)} %copy-done.56), channel_id=1, source_target_pairs={{1,4},{2,7},{5,8},{6,11},{9,12},{10,15},{17,20},{18,23},{21,24},{2... | collective-permute-start | bytes 983048 | tf_op jit(solution)/shard_map/ppermute | solution.py:15
  164.1 10.1 %collective-permute-start.43 = (bf16[2,128,640]{2,1,0:T(8,128)(2,1)S(1)}, bf16[2,128,640]{2,1,0:T(8,128)(2,1)S(1)}, u32[]{:S(2)}, u32[]{:S(2)}) collective-permute-start(bf16[2,128,640]{2,1,0:T(8,128)(2,1)S(1)} %get-tuple-element.105), channel_id=1, source_target_pairs={{0,2},{1,3},{2,0},{3,1},{4,6},{5,7},{6,4},{7,5},{8,10},{9,11},{10,... | collective-permute-start | bytes 983048 | tf_op jit(solution)/shard_map/ppermute | solution.py:15
  166.7 12.9 %collective-permute-start.44 = (bf16[2,128,640]{2,1,0:T(8,128)(2,1)S(1)}, bf16[2,128,640]{2,1,0:T(8,128)(2,1)S(1)}, u32[]{:S(2)}, u32[]{:S(2)}) collective-permute-start(bf16[2,128,640]{2,1,0:T(8,128)(2,1)S(1)} %get-tuple-element.106), channel_id=1, source_target_pairs={{4,0},{5,1},{6,2},{7,3},{8,4},{9,5},{10,6},{11,7},{12,8},{13,9},{1... | collective-permute-start | bytes 983048 | tf_op jit(solution)/shard_map/ppermute | solution.py:15
  168.0 12.8 %collective-permute-start.45 = (bf16[2,128,640]{2,1,0:T(8,128)(2,1)S(1)}, bf16[2,128,640]{2,1,0:T(8,128)(2,1)S(1)}, u32[]{:S(2)}, u32[]{:S(2)}) collective-permute-start(bf16[2,128,640]{2,1,0:T(8,128)(2,1)S(1)} %get-tuple-element.107), channel_id=1, source_target_pairs={{0,4},{1,5},{2,6},{3,7},{4,8},{5,9},{6,10},{7,11},{8,12},{9,13},{1... | collective-permute-start | bytes 983048 | tf_op jit(solution)/shard_map/ppermute | solution.py:15
  173.2 14.0 %copy-start.48 = (bf16[2,128,640]{2,1,0:T(8,128)(2,1)S(1)}, bf16[2,128,640]{2,1,0:T(8,128)(2,1)}, u32[]{:S(2)}) copy-start(bf16[2,128,640]{2,1,0:T(8,128)(2,1)} %get-tuple-element.95) | copy-start | bytes 983044
  180.8 9.4 %collective-permute-start.49 = (bf16[2,128,640]{2,1,0:T(8,128)(2,1)S(1)}, bf16[2,128,640]{2,1,0:T(8,128)(2,1)S(1)}, u32[]{:S(2)}, u32[]{:S(2)}) collective-permute-start(bf16[2,128,640]{2,1,0:T(8,128)(2,1)S(1)} %get-tuple-element.118), channel_id=1, source_target_pairs={{0,2},{1,3},{2,0},{3,1},{4,6},{5,7},{6,4},{7,5},{8,10},{9,11},{10,... | collective-permute-start | bytes 983048 | tf_op jit(solution)/shard_map/ppermute | solution.py:15
  180.8 12.2 %collective-permute-start.50 = (bf16[2,128,640]{2,1,0:T(8,128)(2,1)S(1)}, bf16[2,128,640]{2,1,0:T(8,128)(2,1)S(1)}, u32[]{:S(2)}, u32[]{:S(2)}) collective-permute-start(bf16[2,128,640]{2,1,0:T(8,128)(2,1)S(1)} %get-tuple-element.119), channel_id=1, source_target_pairs={{4,0},{5,1},{6,2},{7,3},{8,4},{9,5},{10,6},{11,7},{12,8},{13,9},{1... | collective-permute-start | bytes 983048 | tf_op jit(solution)/shard_map/ppermute | solution.py:15
  182.1 12.1 %collective-permute-start.51 = (bf16[2,128,640]{2,1,0:T(8,128)(2,1)S(1)}, bf16[2,128,640]{2,1,0:T(8,128)(2,1)S(1)}, u32[]{:S(2)}, u32[]{:S(2)}) collective-permute-start(bf16[2,128,640]{2,1,0:T(8,128)(2,1)S(1)} %get-tuple-element.120), channel_id=1, source_target_pairs={{0,4},{1,5},{2,6},{3,7},{4,8},{5,9},{6,10},{7,11},{8,12},{9,13},{1... | collective-permute-start | bytes 983048 | tf_op jit(solution)/shard_map/ppermute | solution.py:15
  (49 other events, 318.7 us)

commit v6 on v4

--- a/solution.py
+++ b/solution.py
@@ -139,17 +139,16 @@
     core, cross, down, up, diag_up, diag_down, back = route(count)
     if after is not None:
         own, _ = lax.optimization_barrier((own, after))
-    from_core = send(own, core)
     from_cross = send(own, cross)
     from_below = send(own, up)
     from_above = send(own, down)
-    return [own, from_core, from_cross, from_below, from_above]
+    return [own, from_cross, from_below, from_above]
 
 
 def forward_second(first, count, after):
     core, cross, down, up, diag_up, diag_down, back = route(count)
-    own, from_core, from_cross, from_below, from_above = first
-    ahead = jnp.stack([from_cross, from_below, from_above])
+    own, from_cross, from_below, from_above = first
+    ahead = jnp.stack([own, from_cross, from_below, from_above])
     if after is not None:
         (ahead, from_cross), _ = lax.optimization_barrier(((ahead, from_cross), after))
     relayed = send(ahead, core)
@@ -159,7 +158,7 @@
 
 
 def chunk_kernel(forward_mask, queries, out_grad, inputs, head_offset, inv_root):
-    slot_in = [(0, ()), (1, ()), (2, ()), (3, ()), (4, ()), (5, (0,)), (5, (1,)), (5, (2,)), (6, ()), (7, ())]
+    slot_in = [(0, ()), (4, (0,)), (1, ()), (2, ()), (3, ()), (4, (1,)), (4, (2,)), (4, (3,)), (5, ()), (6, ())]
     out_lead = [(), (4,), (), (), (), (), ()]
     slot_out = [(0, ()), (1, (0,)), (2, ()), (3, ()), (4, ()), (1, (1,)), (1, (2,)), (1, (3,)), (5, ()), (6, ())]
     return attention_backward(
@@ -235,13 +234,15 @@
         own = jnp.stack([keys[:, first : first + width], values[:, first : first + width]])
         firsts.append(forward_relay(own, count, firsts[c - 1][1:] if c else None))
     for c in range(len(starts)):
-        seconds.append(forward_second(firsts[c], count, seconds[c - 1][5:] if c else None))
+        seconds.append(forward_second(firsts[c], count, seconds[c - 1][4:] if c else None))
     for c, first in enumerate(starts):
-        dq, parts = chunk_kernel(forward_mask, queries, out_grad, seconds[c], first // HD, inv_root)
+        inputs = seconds[c]
+        if c:
+            inputs, _ = lax.optimization_barrier((inputs, backs[c - 1]))
+        dq, parts = chunk_kernel(forward_mask, queries, out_grad, inputs, first // HD, inv_root)
         dqs.append(dq)
         outs.append(parts)
-    for c in range(len(starts)):
-        backs.append(return_first(outs[c], count, backs[c - 1] if c else None))
+        backs.append(return_first(parts, count, backs[c - 1] if c else None))
     got = None
     for c in range(len(starts)):
         got, summed = return_second(outs[c], backs[c], count, got)

time: 151 us -> 171 us (1.13)
  waiting for transfers between devices: 50.4 us -> 66.3 us
  starting transfers between devices: 50.9 us -> 53.9 us
  local copies, waits for them, and re-layouts: 4.16 us -> 6.54 us
  other arithmetic: 13.4 us -> 11.6 us
    ppermute x26 -> x24, waiting for transfers between devices: 50.4 us -> 66.3 us  [send(): return lax.ppermute(value, 'tm', pairs)]
    ppermute x26 -> x24, starting transfers between devices: 50.9 us -> 53.9 us  [send(): return lax.ppermute(value, 'tm', pairs)]
    unnamed x41 -> x51, local copies, waits for them, and re-layouts: 2.71 us -> 5.09 us
    another operation x4 -> x5, other arithmetic: 4.25 us -> 3.76 us  [the longest x2 3.42 us: forward_second(): ahead = jnp.stack([from_cross, from_below, from_above])]
  transfers between devices with their start and end apart: 26 -> 24, of which waited for: 12 -> 13; matrix products, arithmetic and copies ran while one was open for 8% -> 5% of each run, Pallas kernels for 20% -> 9%
where the time goes in v6:
time: 171 us; the launch traced here: 169 us
  waiting for transfers between devices  66.3 us (39%)
  starting transfers between devices  53.9 us (32%)
  Pallas kernels  29.6 us (17%)
  other arithmetic  11.6 us (7%)
  local copies, waits for them, and re-layouts  6.54 us (4%)
    ppermute x24, waiting for transfers between devices, send(): return lax.ppermute(value, 'tm', pairs)  66.3 us
    ppermute x24, starting transfers between devices, send(): return lax.ppermute(value, 'tm', pairs)  53.9 us
    pallas_call x2, Pallas kernels, attention_backward(): pl.pallas_call(kernel, grid=(heads,), in_specs=in_specs, out_specs=out_sp...  29.6 us
    unnamed x51, local copies, waits for them, and re-layouts  5.09 us
    convert_element_type x2, other arithmetic, return_second(): above_sum.astype(jnp.bfloat16)  3.47 us
  transfers between devices with their start and end apart: 24, of which 13 were waited for; matrix products, arithmetic and copies ran while one was open for 5% of the time, Pallas kernels for 9%

profile of v6, /device:TPU:0, one launch (start us, length us, event | category | flops | bytes accessed | tf_op | source)
XLA Modules:
  0.0 169.1 jit_solution(9171101012331215297)
XLA Ops:
  0.6 1.4 slice_bitcast_fusion.14
  2.0 0.0 copy-start.19
  2.0 0.1 fusion.29
  2.1 1.3 collective-permute-start.2
  3.4 5.6 %collective-permute-start.1 = (bf16[2,128,1280]{2,1,0:T(8,128)(2,1)S(1)}, bf16[2,128,1280]{2,1,0:T(8,128)(2,1)S(1)}, u32[]{:S(2)}, u32[]{:S(2)}) collective-permute-start(bf16[2,128,1280]{2,1,0:T(8,128)(2,1)S(1)} %get-tuple-element.78.refs_0_), channel_id=1, source_target_pairs={{0,4},{1,5},{2,6},{3,7},{4,8},{5,9},{6,10},{7,11},{8,12},{9,13},{1... | collective-permute-start | bytes 1966088 | tf_op jit(solution)/shard_map/ppermute | solution.py:15
  9.0 2.0 %collective-permute-start = (bf16[2,128,1280]{2,1,0:T(8,128)(2,1)S(1)}, bf16[2,128,1280]{2,1,0:T(8,128)(2,1)}, u32[]{:S(2)}, u32[]{:S(2)}) collective-permute-start(bf16[2,128,1280]{2,1,0:T(8,128)(2,1)S(1)} %get-tuple-element.78.refs_0_), channel_id=1, source_target_pairs={{0,2},{1,3},{2,0},{3,1},{4,6},{5,7},{6,4},{7,5},{8,10},{9,11},{10,... | collective-permute-start | bytes 1966088 | tf_op jit(solution)/shard_map/ppermute | solution.py:15
  11.1 0.1 copy.9
  11.3 10.5 %collective-permute-done.2.refs_3_ = bf16[2,128,1280]{2,1,0:T(8,128)(2,1)S(1)} collective-permute-done((bf16[2,128,1280]{2,1,0:T(8,128)(2,1)S(1)}, bf16[2,128,1280]{2,1,0:T(8,128)(2,1)S(1)}, u32[]{:S(2)}, u32[]{:S(2)}) %collective-permute-start.2) | collective-permute-done | bytes 655392 | tf_op jit(solution)/shard_map/ppermute | solution.py:15
  21.8 1.2 collective-permute-done.1.refs_2_
  23.0 2.4 %collective-permute-done.refs_1_ = bf16[2,128,1280]{2,1,0:T(8,128)(2,1)} collective-permute-done((bf16[2,128,1280]{2,1,0:T(8,128)(2,1)S(1)}, bf16[2,128,1280]{2,1,0:T(8,128)(2,1)}, u32[]{:S(2)}, u32[]{:S(2)}) %collective-permute-start) | collective-permute-done | bytes 655392 | tf_op jit(solution)/shard_map/ppermute | solution.py:15
  25.4 1.4 pad_maximum_fusion
  26.9 0.1 collective-permute-start.3
  27.0 0.1 select_reduce_fusion
  27.1 0.1 multiply_reduce_fusion
  27.2 0.1 pad_maximum_fusion.3.refs_0_
  27.3 0.0 copy-start
  27.3 1.3 collective-permute-start.8
  28.6 4.6 %collective-permute-start.7 = (bf16[2,128,1280]{2,1,0:T(8,128)(2,1)S(1)}, bf16[2,128,1280]{2,1,0:T(8,128)(2,1)S(1)}, u32[]{:S(2)}, u32[]{:S(2)}) collective-permute-start(bf16[2,128,1280]{2,1,0:T(8,128)(2,1)S(1)} %pad_maximum_fusion.3.refs_0_), channel_id=1, source_target_pairs={{0,4},{1,5},{2,6},{3,7},{4,8},{5,9},{6,10},{7,11},{8,12},{9,13},{1... | collective-permute-start | bytes 1966088 | tf_op jit(solution)/shard_map/ppermute | solution.py:15
  33.2 1.7 %collective-permute-start.6 = (bf16[2,128,1280]{2,1,0:T(8,128)(2,1)S(1)}, bf16[2,128,1280]{2,1,0:T(8,128)(2,1)S(1)}, u32[]{:S(2)}, u32[]{:S(2)}) collective-permute-start(bf16[2,128,1280]{2,1,0:T(8,128)(2,1)S(1)} %pad_maximum_fusion.3.refs_0_), channel_id=1, source_target_pairs={{0,2},{1,3},{2,0},{3,1},{4,6},{5,7},{6,4},{7,5},{8,10},{9,11},{10,... | collective-permute-start | bytes 1966088 | tf_op jit(solution)/shard_map/ppermute | solution.py:15
  35.0 1.5 collective-permute-start.5
  36.5 9.8 %collective-permute-done.8.refs_3_ = bf16[2,128,1280]{2,1,0:T(8,128)(2,1)S(1)} collective-permute-done((bf16[2,128,1280]{2,1,0:T(8,128)(2,1)S(1)}, bf16[2,128,1280]{2,1,0:T(8,128)(2,1)S(1)}, u32[]{:S(2)}, u32[]{:S(2)}) %collective-permute-start.8) | collective-permute-done | bytes 655392 | tf_op jit(solution)/shard_map/ppermute | solution.py:15
  46.3 2.9 %collective-permute-start.4 = (bf16[2,128,1280]{2,1,0:T(8,128)(2,1)}, bf16[2,128,1280]{2,1,0:T(8,128)(2,1)S(1)}, u32[]{:S(2)}, u32[]{:S(2)}) collective-permute-start(bf16[2,128,1280]{2,1,0:T(8,128)(2,1)} %collective-permute-done.refs_1_), channel_id=1, source_target_pairs={{0,5},{3,6},{4,9},{7,10},{8,13},{11,14},{16,21},{19,22},{20,25},{2... | collective-permute-start | bytes 1966088 | tf_op jit(solution)/shard_map/ppermute | solution.py:15
  49.2 1.4 fusion.24.mask_ref
  50.6 0.0 copy-start.5
  50.6 0.3 pad_maximum_fusion.1
  50.9 0.5 copy-done.4
  51.4 0.2 copy-done.5
  51.6 5.9 %collective-permute-done.4.refs_5_ = bf16[2,128,1280]{2,1,0:T(8,128)(2,1)S(1)} collective-permute-done((bf16[2,128,1280]{2,1,0:T(8,128)(2,1)}, bf16[2,128,1280]{2,1,0:T(8,128)(2,1)S(1)}, u32[]{:S(2)}, u32[]{:S(2)}) %collective-permute-start.4) | collective-permute-done | bytes 655392 | tf_op jit(solution)/shard_map/ppermute | solution.py:15
  57.5 0.9 copy-done.21
  58.4 1.5 copy-done.20
  59.9 14.7 %shard_map.85 = (bf16[128,1280]{1,0:T(8,128)(2,1)}, bf16[2,128,1280]{2,1,0:T(8,128)(2,1)}, bf16[4,2,128,1280]{3,2,1,0:T(8,128)(2,1)}, bf16[2,128,1280]{2,1,0:T(8...) custom-call(s32[128,1280]{1,0:T(8,128)} %fusion.24.mask_ref, ...), custom_call_target="tpu_custom_call" | custom-call | flops 2516582400 | bytes 14745600 | tf_op jit(solution)/shard_map/pallas_call | solution.py:123
  74.6 0.6 collective-permute-start.12
  75.2 0.7 collective-permute-start.11
  75.9 4.3 %collective-permute-start.10 = (bf16[2,128,1280]{2,1,0:T(8,128)(2,1)S(1)}, bf16[2,128,1280]{2,1,0:T(8,128)(2,1)S(1)}, u32[]{:S(2)}, u32[]{:S(2)}) collective-permute-start(bf16[2,128,1280]{2,1,0:T(8,128)(2,1)S(1)} %copy-done.6), channel_id=1, source_target_pairs={{0,5},{3,6},{4,9},{7,10},{8,13},{11,14},{16,21},{19,22},{20,25},{2... | collective-permute-start | bytes 1966088 | tf_op jit(solution)/shard_map/ppermute | solution.py:15
  80.2 1.3 collective-permute-start.13
  81.5 0.8 copy-done.22
  82.4 0.7 collective-permute-start.14
  83.1 5.2 %collective-permute-done.10.refs_5_ = bf16[2,128,1280]{2,1,0:T(8,128)(2,1)S(1)} collective-permute-done((bf16[2,128,1280]{2,1,0:T(8,128)(2,1)S(1)}, bf16[2,128,1280]{2,1,0:T(8,128)(2,1)S(1)}, u32[]{:S(2)}, u32[]{:S(2)}) %collective-permute-start.10) | collective-permute-done | bytes 655392 | tf_op jit(solution)/shard_map/ppermute | solution.py:15
  88.3 6.0 %collective-permute-done.13 = bf16[2,128,1280]{2,1,0:T(8,128)(2,1)S(1)} collective-permute-done((bf16[2,128,1280]{2,1,0:T(8,128)(2,1)}, bf16[2,128,1280]{2,1,0:T(8,128)(2,1)S(1)}, u32[]{:S(2)}, u32[]{:S(2)}) %collective-permute-start.13) | collective-permute-done | bytes 655392 | tf_op jit(solution)/shard_map/ppermute | solution.py:15
  94.3 0.9 copy-done.10
  95.2 0.2 copy-done.12
  95.4 14.9 %shard_map.86 = (bf16[128,1280]{1,0:T(8,128)(2,1)}, bf16[2,128,1280]{2,1,0:T(8,128)(2,1)}, bf16[4,2,128,1280]{3,2,1,0:T(8,128)(2,1)}, bf16[2,128,1280]{2,1,0:T(8...) custom-call(s32[128,1280]{1,0:T(8,128)} %fusion.24.mask_ref, ...), custom_call_target="tpu_custom_call" | custom-call | flops 2516582400 | bytes 14745600 | tf_op jit(solution)/shard_map/pallas_call | solution.py:123
  110.2 5.0 %collective-permute-start.18 = (bf16[4,2,128,1280]{3,2,1,0:T(8,128)(2,1)}, bf16[4,2,128,1280]{3,2,1,0:T(8,128)(2,1)S(1)}, u32[]{:S(2)}, u32[]{:S(2)}) collective-permute-start(bf16[4,2,128,1280]{3,2,1,0:T(8,128)(2,1)} %get-tuple-element.58), channel_id=1, source_target_pairs={{0,1},{1,0},{2,3},{3,2},{4,5},{5,4},{6,7},{7,6},{8,9},{9,8},{10,11... | collective-permute-start | bytes 7864328 | tf_op jit(solution)/shard_map/ppermute | solution.py:15
  115.2 1.3 collective-permute-start.19
  116.5 0.7 collective-permute-start.20
  117.3 2.8 %fusion.9 = (bf16[2,128,1280]{2,1,0:T(8,128)(2,1)S(1)}, bf16[2,128,1280]{2,1,0:T(8,128)(2,1)S(1)}, bf16[2,128,1280]{2,1,0:T(8,128)(2,1)S(1)}) fusion(bf16[2,128,1280]{2,1,0:T(8,128)(2,1)} %get-tuple-element.53, bf16[4,2,128,1280]{3,2,1,0:T(8,128)(2,1)} %collective-permute-done.12, bf16[2,128,1280]{2,1,0:T(8,128)(2,1)} %get-tuple-element.52, ...), kind=kLoop, calls=%fused_computation.16 | loop fusion | flops 5242880 | bytes 7208960 | tf_op jit(solution)/shard_map/convert_element_type | solution.py:190
  120.1 5.4 %collective-permute-start.17 = (bf16[2,128,1280]{2,1,0:T(8,128)(2,1)S(1)}, bf16[2,128,1280]{2,1,0:T(8,128)(2,1)S(1)}, u32[]{:S(2)}, u32[]{:S(2)}) collective-permute-start(bf16[2,128,1280]{2,1,0:T(8,128)(2,1)S(1)} %get-tuple-element.67), channel_id=1, source_target_pairs={{0,4},{1,5},{2,6},{3,7},{4,8},{5,9},{6,10},{7,11},{8,12},{9,13},{1... | collective-permute-start | bytes 1966088 | tf_op jit(solution)/shard_map/ppermute | solution.py:15
  125.5 1.3 collective-permute-start.16
  126.8 0.9 pad_maximum_fusion.4
  127.7 5.2 %collective-permute-start.15 = (bf16[2,128,1280]{2,1,0:T(8,128)(2,1)S(1)}, bf16[2,128,1280]{2,1,0:T(8,128)(2,1)S(1)}, u32[]{:S(2)}, u32[]{:S(2)}) collective-permute-start(bf16[2,128,1280]{2,1,0:T(8,128)(2,1)S(1)} %get-tuple-element.69), channel_id=1, source_target_pairs={{0,2},{1,3},{2,0},{3,1},{4,6},{5,7},{6,4},{7,5},{8,10},{9,11},{10,... | collective-permute-start | bytes 1966088 | tf_op jit(solution)/shard_map/ppermute | solution.py:15
  132.9 0.7 fusion
  133.6 7.0 %collective-permute-done.17 = bf16[2,128,1280]{2,1,0:T(8,128)(2,1)S(1)} collective-permute-done((bf16[2,128,1280]{2,1,0:T(8,128)(2,1)S(1)}, bf16[2,128,1280]{2,1,0:T(8,128)(2,1)S(1)}, u32[]{:S(2)}, u32[]{:S(2)}) %collective-permute-start.17) | collective-permute-done | bytes 655392 | tf_op jit(solution)/shard_map/ppermute | solution.py:15
  140.6 3.6 %collective-permute-done.16 = bf16[2,128,1280]{2,1,0:T(8,128)(2,1)S(1)} collective-permute-done((bf16[2,128,1280]{2,1,0:T(8,128)(2,1)S(1)}, bf16[2,128,1280]{2,1,0:T(8,128)(2,1)S(1)}, u32[]{:S(2)}, u32[]{:S(2)}) %collective-permute-start.16) | collective-permute-done | bytes 655392 | tf_op jit(solution)/shard_map/ppermute | solution.py:15
  144.2 3.4 %collective-permute-done.15 = bf16[2,128,1280]{2,1,0:T(8,128)(2,1)S(1)} collective-permute-done((bf16[2,128,1280]{2,1,0:T(8,128)(2,1)S(1)}, bf16[2,128,1280]{2,1,0:T(8,128)(2,1)S(1)}, u32[]{:S(2)}, u32[]{:S(2)}) %collective-permute-start.15) | collective-permute-done | bytes 655392 | tf_op jit(solution)/shard_map/ppermute | solution.py:15
  147.6 0.3 collective-permute-start.21
  147.9 1.3 collective-permute-start.22
  149.2 4.9 %collective-permute-start.23 = (bf16[2,128,1280]{2,1,0:T(8,128)(2,1)S(1)}, bf16[2,128,1280]{2,1,0:T(8,128)(2,1)S(1)}, u32[]{:S(2)}, u32[]{:S(2)}) collective-permute-start(bf16[2,128,1280]{2,1,0:T(8,128)(2,1)S(1)} %get-tuple-element.66), channel_id=1, source_target_pairs={{0,4},{1,5},{2,6},{3,7},{4,8},{5,9},{6,10},{7,11},{8,12},{9,13},{1... | collective-permute-start | bytes 1966088 | tf_op jit(solution)/shard_map/ppermute | solution.py:15
  154.1 1.5 fusion.17
  155.7 7.8 %collective-permute-done.21 = bf16[2,128,1280]{2,1,0:T(8,128)(2,1)S(1)} collective-permute-done((bf16[2,128,1280]{2,1,0:T(8,128)(2,1)S(1)}, bf16[2,128,1280]{2,1,0:T(8,128)(2,1)S(1)}, u32[]{:S(2)}, u32[]{:S(2)}) %collective-permute-start.21) | collective-permute-done | bytes 655392 | tf_op jit(solution)/shard_map/ppermute | solution.py:15
  163.5 2.2 %collective-permute-done.22 = bf16[2,128,1280]{2,1,0:T(8,128)(2,1)S(1)} collective-permute-done((bf16[2,128,1280]{2,1,0:T(8,128)(2,1)S(1)}, bf16[2,128,1280]{2,1,0:T(8,128)(2,1)S(1)}, u32[]{:S(2)}, u32[]{:S(2)}) %collective-permute-start.22) | collective-permute-done | bytes 655392 | tf_op jit(solution)/shard_map/ppermute | solution.py:15
  165.7 1.2 collective-permute-done.23
  166.9 0.4 fusion.8
  167.4 0.9 pad_maximum_fusion.6
  168.3 0.9 pad_maximum_fusion.5
  (71 shorter events, 0.3 us)
Async XLA Ops:
  2.0 9.1 %copy-start.19 = (s32[4,3]{1,0:T(4,128)S(1)}, s32[4,3]{1,0:T(4,128)}, u32[]{:S(2)}) copy-start(s32[4,3]{1,0:T(4,128)} %param.10) | copy-start | bytes 148
  2.1 24.7 %copy-start.14 = (bf16[2,128,1280]{2,1,0:T(8,128)(2,1)}, bf16[2,128,1280]{2,1,0:T(8,128)(2,1)S(1)}, u32[]{:S(2)}) copy-start(bf16[2,128,1280]{2,1,0:T(8,128)(2,1)S(1)} %get-tuple-element.78.refs_0_) | copy-start | bytes 1966084
  2.1 19.7 %collective-permute-start.2 = (bf16[2,128,1280]{2,1,0:T(8,128)(2,1)S(1)}, bf16[2,128,1280]{2,1,0:T(8,128)(2,1)S(1)}, u32[]{:S(2)}, u32[]{:S(2)}) collective-permute-start(bf16[2,128,1280]{2,1,0:T(8,128)(2,1)S(1)} %get-tuple-element.78.refs_0_), channel_id=1, source_target_pairs={{4,0},{5,1},{6,2},{7,3},{8,4},{9,5},{10,6},{11,7},{12,8},{13,9},{1... | collective-permute-start | bytes 1966088 | tf_op jit(solution)/shard_map/ppermute | solution.py:15
  3.4 19.6 %collective-permute-start.1 = (bf16[2,128,1280]{2,1,0:T(8,128)(2,1)S(1)}, bf16[2,128,1280]{2,1,0:T(8,128)(2,1)S(1)}, u32[]{:S(2)}, u32[]{:S(2)}) collective-permute-start(bf16[2,128,1280]{2,1,0:T(8,128)(2,1)S(1)} %get-tuple-element.78.refs_0_), channel_id=1, source_target_pairs={{0,4},{1,5},{2,6},{3,7},{4,8},{5,9},{6,10},{7,11},{8,12},{9,13},{1... | collective-permute-start | bytes 1966088 | tf_op jit(solution)/shard_map/ppermute | solution.py:15
  9.0 16.4 %collective-permute-start = (bf16[2,128,1280]{2,1,0:T(8,128)(2,1)S(1)}, bf16[2,128,1280]{2,1,0:T(8,128)(2,1)}, u32[]{:S(2)}, u32[]{:S(2)}) collective-permute-start(bf16[2,128,1280]{2,1,0:T(8,128)(2,1)S(1)} %get-tuple-element.78.refs_0_), channel_id=1, source_target_pairs={{0,2},{1,3},{2,0},{3,1},{4,6},{5,7},{6,4},{7,5},{8,10},{9,11},{10,... | collective-permute-start | bytes 1966088 | tf_op jit(solution)/shard_map/ppermute | solution.py:15
  21.8 5.1 %copy-start.1 = (bf16[2,128,1280]{2,1,0:T(8,128)(2,1)}, bf16[2,128,1280]{2,1,0:T(8,128)(2,1)S(1)}, u32[]{:S(2)}) copy-start(bf16[2,128,1280]{2,1,0:T(8,128)(2,1)S(1)} %collective-permute-done.2.refs_3_) | copy-start | bytes 1966084
  23.0 3.9 %copy-start.2 = (bf16[2,128,1280]{2,1,0:T(8,128)(2,1)}, bf16[2,128,1280]{2,1,0:T(8,128)(2,1)S(1)}, u32[]{:S(2)}) copy-start(bf16[2,128,1280]{2,1,0:T(8,128)(2,1)S(1)} %collective-permute-done.1.refs_2_) | copy-start | bytes 1966084
  25.4 1.6 copy-start.24
  26.9 30.7 %collective-permute-start.3 = (bf16[4,2,128,1280]{3,2,1,0:T(8,128)(2,1)S(1)}, bf16[4,2,128,1280]{3,2,1,0:T(8,128)(2,1)S(1)}, u32[]{:S(2)}, u32[]{:S(2)}) collective-permute-start(bf16[4,2,128,1280]{3,2,1,0:T(8,128)(2,1)S(1)} %pad_maximum_fusion), channel_id=1, source_target_pairs={{0,1},{1,0},{2,3},{3,2},{4,5},{5,4},{6,7},{7,6},{8,9},{9,8},{10,11... | collective-permute-start | bytes 7864328 | tf_op jit(solution)/shard_map/ppermute | solution.py:15
  27.3 23.7 %copy-start = (bf16[2,128,1280]{2,1,0:T(8,128)(2,1)}, bf16[2,128,1280]{2,1,0:T(8,128)(2,1)S(1)}, u32[]{:S(2)}) copy-start(bf16[2,128,1280]{2,1,0:T(8,128)(2,1)S(1)} %pad_maximum_fusion.3.refs_0_) | copy-start | bytes 1966084
  27.3 19.0 %collective-permute-start.8 = (bf16[2,128,1280]{2,1,0:T(8,128)(2,1)S(1)}, bf16[2,128,1280]{2,1,0:T(8,128)(2,1)S(1)}, u32[]{:S(2)}, u32[]{:S(2)}) collective-permute-start(bf16[2,128,1280]{2,1,0:T(8,128)(2,1)S(1)} %pad_maximum_fusion.3.refs_0_), channel_id=1, source_target_pairs={{4,0},{5,1},{6,2},{7,3},{8,4},{9,5},{10,6},{11,7},{12,8},{13,9},{1... | collective-permute-start | bytes 1966088 | tf_op jit(solution)/shard_map/ppermute | solution.py:15
  28.6 22.0 %collective-permute-start.7 = (bf16[2,128,1280]{2,1,0:T(8,128)(2,1)S(1)}, bf16[2,128,1280]{2,1,0:T(8,128)(2,1)S(1)}, u32[]{:S(2)}, u32[]{:S(2)}) collective-permute-start(bf16[2,128,1280]{2,1,0:T(8,128)(2,1)S(1)} %pad_maximum_fusion.3.refs_0_), channel_id=1, source_target_pairs={{0,4},{1,5},{2,6},{3,7},{4,8},{5,9},{6,10},{7,11},{8,12},{9,13},{1... | collective-permute-start | bytes 1966088 | tf_op jit(solution)/shard_map/ppermute | solution.py:15
  33.2 17.4 %collective-permute-start.6 = (bf16[2,128,1280]{2,1,0:T(8,128)(2,1)S(1)}, bf16[2,128,1280]{2,1,0:T(8,128)(2,1)S(1)}, u32[]{:S(2)}, u32[]{:S(2)}) collective-permute-start(bf16[2,128,1280]{2,1,0:T(8,128)(2,1)S(1)} %pad_maximum_fusion.3.refs_0_), channel_id=1, source_target_pairs={{0,2},{1,3},{2,0},{3,1},{4,6},{5,7},{6,4},{7,5},{8,10},{9,11},{10,... | collective-permute-start | bytes 1966088 | tf_op jit(solution)/shard_map/ppermute | solution.py:15
  35.0 16.7 %collective-permute-start.5 = (bf16[2,128,1280]{2,1,0:T(8,128)(2,1)}, bf16[2,128,1280]{2,1,0:T(8,128)(2,1)}, u32[]{:S(2)}, u32[]{:S(2)}) collective-permute-start(bf16[2,128,1280]{2,1,0:T(8,128)(2,1)} %collective-permute-done.refs_1_), channel_id=1, source_target_pairs={{4,1},{7,2},{8,5},{11,6},{12,9},{15,10},{20,17},{23,18},{24,21},{2... | collective-permute-start | bytes 1966088 | tf_op jit(solution)/shard_map/ppermute | solution.py:15
  46.3 4.7 %copy-start.3 = (bf16[2,128,1280]{2,1,0:T(8,128)(2,1)}, bf16[2,128,1280]{2,1,0:T(8,128)(2,1)S(1)}, u32[]{:S(2)}) copy-start(bf16[2,128,1280]{2,1,0:T(8,128)(2,1)S(1)} %collective-permute-done.8.refs_3_) | copy-start | bytes 1966084
  46.3 11.2 %collective-permute-start.4 = (bf16[2,128,1280]{2,1,0:T(8,128)(2,1)}, bf16[2,128,1280]{2,1,0:T(8,128)(2,1)S(1)}, u32[]{:S(2)}, u32[]{:S(2)}) collective-permute-start(bf16[2,128,1280]{2,1,0:T(8,128)(2,1)} %collective-permute-done.refs_1_), channel_id=1, source_target_pairs={{0,5},{3,6},{4,9},{7,10},{8,13},{11,14},{16,21},{19,22},{20,25},{2... | collective-permute-start | bytes 1966088 | tf_op jit(solution)/shard_map/ppermute | solution.py:15
  50.6 0.8 copy-start.4
  50.6 1.0 copy-start.5
  51.6 23.5 %copy-start.6 = (bf16[2,128,1280]{2,1,0:T(8,128)(2,1)S(1)}, bf16[2,128,1280]{2,1,0:T(8,128)(2,1)}, u32[]{:S(2)}) copy-start(bf16[2,128,1280]{2,1,0:T(8,128)(2,1)} %copy-done.5) | copy-start | bytes 1966084
  57.5 0.9 copy-start.21
  58.4 1.5 copy-start.20
  59.9 34.4 %collective-permute-start.9 = (bf16[4,2,128,1280]{3,2,1,0:T(8,128)(2,1)S(1)}, bf16[4,2,128,1280]{3,2,1,0:T(8,128)(2,1)}, u32[]{:S(2)}, u32[]{:S(2)}) collective-permute-start(bf16[4,2,128,1280]{3,2,1,0:T(8,128)(2,1)S(1)} %pad_maximum_fusion.1), channel_id=1, source_target_pairs={{0,1},{1,0},{2,3},{3,2},{4,5},{5,4},{6,7},{7,6},{8,9},{9,8},{10,11... | collective-permute-start | bytes 7864328 | tf_op jit(solution)/shard_map/ppermute | solution.py:15
  74.6 20.8 %collective-permute-start.12 = (bf16[4,2,128,1280]{3,2,1,0:T(8,128)(2,1)}, bf16[4,2,128,1280]{3,2,1,0:T(8,128)(2,1)}, u32[]{:S(2)}, u32[]{:S(2)}) collective-permute-start(bf16[4,2,128,1280]{3,2,1,0:T(8,128)(2,1)} %get-tuple-element.39), channel_id=1, source_target_pairs={{0,1},{1,0},{2,3},{3,2},{4,5},{5,4},{6,7},{7,6},{8,9},{9,8},{10,11... | collective-permute-start | bytes 7864328 | tf_op jit(solution)/shard_map/ppermute | solution.py:15
  75.2 6.4 %collective-permute-start.11 = (bf16[2,128,1280]{2,1,0:T(8,128)(2,1)S(1)}, bf16[2,128,1280]{2,1,0:T(8,128)(2,1)S(1)}, u32[]{:S(2)}, u32[]{:S(2)}) collective-permute-start(bf16[2,128,1280]{2,1,0:T(8,128)(2,1)S(1)} %copy-done.6), channel_id=1, source_target_pairs={{4,1},{7,2},{8,5},{11,6},{12,9},{15,10},{20,17},{23,18},{24,21},{2... | collective-permute-start | bytes 1966088 | tf_op jit(solution)/shard_map/ppermute | solution.py:15
  75.9 12.4 %collective-permute-start.10 = (bf16[2,128,1280]{2,1,0:T(8,128)(2,1)S(1)}, bf16[2,128,1280]{2,1,0:T(8,128)(2,1)S(1)}, u32[]{:S(2)}, u32[]{:S(2)}) collective-permute-start(bf16[2,128,1280]{2,1,0:T(8,128)(2,1)S(1)} %copy-done.6), channel_id=1, source_target_pairs={{0,5},{3,6},{4,9},{7,10},{8,13},{11,14},{16,21},{19,22},{20,25},{2... | collective-permute-start | bytes 1966088 | tf_op jit(solution)/shard_map/ppermute | solution.py:15
  80.2 14.1 %collective-permute-start.13 = (bf16[2,128,1280]{2,1,0:T(8,128)(2,1)}, bf16[2,128,1280]{2,1,0:T(8,128)(2,1)S(1)}, u32[]{:S(2)}, u32[]{:S(2)}) collective-permute-start(bf16[2,128,1280]{2,1,0:T(8,128)(2,1)} %get-tuple-element.40), channel_id=1, source_target_pairs={{5,0},{6,3},{9,4},{10,7},{13,8},{14,11},{21,16},{22,19},{25,20},{2... | collective-permute-start | bytes 1966088 | tf_op jit(solution)/shard_map/ppermute | solution.py:15
  81.5 0.8 copy-start.22
  82.4 11.9 %collective-permute-start.14 = (bf16[2,128,1280]{2,1,0:T(8,128)(2,1)}, bf16[2,128,1280]{2,1,0:T(8,128)(2,1)S(1)}, u32[]{:S(2)}, u32[]{:S(2)}) collective-permute-start(bf16[2,128,1280]{2,1,0:T(8,128)(2,1)} %get-tuple-element.41), channel_id=1, source_target_pairs={{1,4},{2,7},{5,8},{6,11},{9,12},{10,15},{17,20},{18,23},{21,24},{2... | collective-permute-start | bytes 1966088 | tf_op jit(solution)/shard_map/ppermute | solution.py:15
  88.3 6.0 %copy-start.23 = (bf16[2,128,1280]{2,1,0:T(8,128)(2,1)}, bf16[2,128,1280]{2,1,0:T(8,128)(2,1)S(1)}, u32[]{:S(2)}) copy-start(bf16[2,128,1280]{2,1,0:T(8,128)(2,1)S(1)} %collective-permute-done.10.refs_5_) | copy-start | bytes 1966084
  94.3 0.9 copy-start.10
  94.3 1.1 copy-start.12
  95.4 21.9 %copy-start.11 = (bf16[2,128,1280]{2,1,0:T(8,128)(2,1)S(1)}, bf16[2,128,1280]{2,1,0:T(8,128)(2,1)}, u32[]{:S(2)}) copy-start(bf16[2,128,1280]{2,1,0:T(8,128)(2,1)} %copy-done.10) | copy-start | bytes 1966084
  95.4 21.9 %copy-start.13 = (bf16[2,128,1280]{2,1,0:T(8,128)(2,1)S(1)}, bf16[2,128,1280]{2,1,0:T(8,128)(2,1)}, u32[]{:S(2)}) copy-start(bf16[2,128,1280]{2,1,0:T(8,128)(2,1)} %copy-done.12) | copy-start | bytes 1966084
  110.2 22.7 %collective-permute-start.18 = (bf16[4,2,128,1280]{3,2,1,0:T(8,128)(2,1)}, bf16[4,2,128,1280]{3,2,1,0:T(8,128)(2,1)S(1)}, u32[]{:S(2)}, u32[]{:S(2)}) collective-permute-start(bf16[4,2,128,1280]{3,2,1,0:T(8,128)(2,1)} %get-tuple-element.58), channel_id=1, source_target_pairs={{0,1},{1,0},{2,3},{3,2},{4,5},{5,4},{6,7},{7,6},{8,9},{9,8},{10,11... | collective-permute-start | bytes 7864328 | tf_op jit(solution)/shard_map/ppermute | solution.py:15
  115.2 12.5 %collective-permute-start.19 = (bf16[2,128,1280]{2,1,0:T(8,128)(2,1)}, bf16[2,128,1280]{2,1,0:T(8,128)(2,1)S(1)}, u32[]{:S(2)}, u32[]{:S(2)}) collective-permute-start(bf16[2,128,1280]{2,1,0:T(8,128)(2,1)} %get-tuple-element.60), channel_id=1, source_target_pairs={{5,0},{6,3},{9,4},{10,7},{13,8},{14,11},{21,16},{22,19},{25,20},{2... | collective-permute-start | bytes 1966088 | tf_op jit(solution)/shard_map/ppermute | solution.py:15
  116.5 16.4 %collective-permute-start.20 = (bf16[2,128,1280]{2,1,0:T(8,128)(2,1)}, bf16[2,128,1280]{2,1,0:T(8,128)(2,1)S(1)}, u32[]{:S(2)}, u32[]{:S(2)}) collective-permute-start(bf16[2,128,1280]{2,1,0:T(8,128)(2,1)} %get-tuple-element.61), channel_id=1, source_target_pairs={{1,4},{2,7},{5,8},{6,11},{9,12},{10,15},{17,20},{18,23},{21,24},{2... | collective-permute-start | bytes 1966088 | tf_op jit(solution)/shard_map/ppermute | solution.py:15
  117.3 9.6 %copy-start.17 = (bf16[128,1280]{1,0:T(8,128)(2,1)S(1)}, bf16[128,1280]{1,0:T(8,128)(2,1)}, u32[]{:S(2)}) copy-start(bf16[128,1280]{1,0:T(8,128)(2,1)} %get-tuple-element.35) | copy-start | bytes 983044
  117.3 9.6 %copy-start.18 = (bf16[128,1280]{1,0:T(8,128)(2,1)S(1)}, bf16[128,1280]{1,0:T(8,128)(2,1)}, u32[]{:S(2)}) copy-start(bf16[128,1280]{1,0:T(8,128)(2,1)} %get-tuple-element.49) | copy-start | bytes 983044
  117.3 15.6 %copy-start.9 = (bf16[2,128,1280]{2,1,0:T(8,128)(2,1)S(1)}, bf16[2,128,1280]{2,1,0:T(8,128)(2,1)}, u32[]{:S(2)}) copy-start(bf16[2,128,1280]{2,1,0:T(8,128)(2,1)} %get-tuple-element.63) | copy-start | bytes 1966084
  120.1 12.8 %copy-start.7 = (bf16[2,128,1280]{2,1,0:T(8,128)(2,1)S(1)}, bf16[2,128,1280]{2,1,0:T(8,128)(2,1)}, u32[]{:S(2)}) copy-start(bf16[2,128,1280]{2,1,0:T(8,128)(2,1)} %get-tuple-element.59) | copy-start | bytes 1966084
  120.1 12.8 %copy-start.8 = (bf16[2,128,1280]{2,1,0:T(8,128)(2,1)S(1)}, bf16[2,128,1280]{2,1,0:T(8,128)(2,1)}, u32[]{:S(2)}) copy-start(bf16[2,128,1280]{2,1,0:T(8,128)(2,1)} %get-tuple-element.62) | copy-start | bytes 1966084
  120.1 20.5 %collective-permute-start.17 = (bf16[2,128,1280]{2,1,0:T(8,128)(2,1)S(1)}, bf16[2,128,1280]{2,1,0:T(8,128)(2,1)S(1)}, u32[]{:S(2)}, u32[]{:S(2)}) collective-permute-start(bf16[2,128,1280]{2,1,0:T(8,128)(2,1)S(1)} %get-tuple-element.67), channel_id=1, source_target_pairs={{0,4},{1,5},{2,6},{3,7},{4,8},{5,9},{6,10},{7,11},{8,12},{9,13},{1... | collective-permute-start | bytes 1966088 | tf_op jit(solution)/shard_map/ppermute | solution.py:15
  125.5 18.7 %collective-permute-start.16 = (bf16[2,128,1280]{2,1,0:T(8,128)(2,1)S(1)}, bf16[2,128,1280]{2,1,0:T(8,128)(2,1)S(1)}, u32[]{:S(2)}, u32[]{:S(2)}) collective-permute-start(bf16[2,128,1280]{2,1,0:T(8,128)(2,1)S(1)} %get-tuple-element.68), channel_id=1, source_target_pairs={{4,0},{5,1},{6,2},{7,3},{8,4},{9,5},{10,6},{11,7},{12,8},{13,9},{1... | collective-permute-start | bytes 1966088 | tf_op jit(solution)/shard_map/ppermute | solution.py:15
  127.7 19.9 %collective-permute-start.15 = (bf16[2,128,1280]{2,1,0:T(8,128)(2,1)S(1)}, bf16[2,128,1280]{2,1,0:T(8,128)(2,1)S(1)}, u32[]{:S(2)}, u32[]{:S(2)}) collective-permute-start(bf16[2,128,1280]{2,1,0:T(8,128)(2,1)S(1)} %get-tuple-element.69), channel_id=1, source_target_pairs={{0,2},{1,3},{2,0},{3,1},{4,6},{5,7},{6,4},{7,5},{8,10},{9,11},{10,... | collective-permute-start | bytes 1966088 | tf_op jit(solution)/shard_map/ppermute | solution.py:15
  132.9 21.2 %copy-start.15 = (bf16[2,128,1280]{2,1,0:T(8,128)(2,1)S(1)}, bf16[2,128,1280]{2,1,0:T(8,128)(2,1)}, u32[]{:S(2)}) copy-start(bf16[2,128,1280]{2,1,0:T(8,128)(2,1)} %get-tuple-element.50) | copy-start | bytes 1966084
  147.6 15.9 %collective-permute-start.21 = (bf16[2,128,1280]{2,1,0:T(8,128)(2,1)S(1)}, bf16[2,128,1280]{2,1,0:T(8,128)(2,1)S(1)}, u32[]{:S(2)}, u32[]{:S(2)}) collective-permute-start(bf16[2,128,1280]{2,1,0:T(8,128)(2,1)S(1)} %get-tuple-element.64), channel_id=1, source_target_pairs={{0,2},{1,3},{2,0},{3,1},{4,6},{5,7},{6,4},{7,5},{8,10},{9,11},{10,... | collective-permute-start | bytes 1966088 | tf_op jit(solution)/shard_map/ppermute | solution.py:15
  147.9 17.8 %collective-permute-start.22 = (bf16[2,128,1280]{2,1,0:T(8,128)(2,1)S(1)}, bf16[2,128,1280]{2,1,0:T(8,128)(2,1)S(1)}, u32[]{:S(2)}, u32[]{:S(2)}) collective-permute-start(bf16[2,128,1280]{2,1,0:T(8,128)(2,1)S(1)} %get-tuple-element.65), channel_id=1, source_target_pairs={{4,0},{5,1},{6,2},{7,3},{8,4},{9,5},{10,6},{11,7},{12,8},{13,9},{1... | collective-permute-start | bytes 1966088 | tf_op jit(solution)/shard_map/ppermute | solution.py:15
  149.2 17.7 %collective-permute-start.23 = (bf16[2,128,1280]{2,1,0:T(8,128)(2,1)S(1)}, bf16[2,128,1280]{2,1,0:T(8,128)(2,1)S(1)}, u32[]{:S(2)}, u32[]{:S(2)}) collective-permute-start(bf16[2,128,1280]{2,1,0:T(8,128)(2,1)S(1)} %get-tuple-element.66), channel_id=1, source_target_pairs={{0,4},{1,5},{2,6},{3,7},{4,8},{5,9},{6,10},{7,11},{8,12},{9,13},{1... | collective-permute-start | bytes 1966088 | tf_op jit(solution)/shard_map/ppermute | solution.py:15
  155.6 11.3 %copy-start.16 = (bf16[2,128,1280]{2,1,0:T(8,128)(2,1)S(1)}, bf16[2,128,1280]{2,1,0:T(8,128)(2,1)}, u32[]{:S(2)}) copy-start(bf16[2,128,1280]{2,1,0:T(8,128)(2,1)} %get-tuple-element.54) | copy-start | bytes 1966084

commit v7 on v4

--- a/solution.py
+++ b/solution.py
@@ -9,6 +9,7 @@
 HD = 128
 QUARTERS = 4
 CHUNKS = 2
+STEP_HEADS = 2
 
 
 def send(value, pairs):
@@ -82,47 +83,50 @@
         in_refs = refs[:n_in]
         dq_ref = refs[n_in]
         out_refs = refs[n_in + 1 :]
-        k = jnp.concatenate([in_refs[i][lead + (0,)] for i, lead in slot_in], axis=0)
-        v = jnp.concatenate([in_refs[i][lead + (1,)] for i, lead in slot_in], axis=0)
-        q = q_ref[...]
-        g = g_ref[...]
         nt = (((1,), (1,)), ((), ()))
         tn = (((0,), (0,)), ((), ()))
-        scores = lax.dot_general(q, k, nt, preferred_element_type=jnp.float32) * inv_root
-        masked = jnp.where(mask_ref[...] != 0, scores, -1e30)
-        highest = jnp.max(masked, axis=1, keepdims=True)
-        total_mass = jnp.sum(jnp.exp(masked - highest), axis=1, keepdims=True)
-        log_total = highest + jnp.log(total_mass)
-        prob = jnp.exp(masked - log_total)
-        prob_low = prob.astype(jnp.bfloat16)
-        attended = jnp.dot(prob_low, v, preferred_element_type=jnp.float32)
-        delta = jnp.sum(g.astype(jnp.float32) * attended, axis=1, keepdims=True)
-        prob_grad = lax.dot_general(g, v, nt, preferred_element_type=jnp.float32)
-        score_grad = (prob * (prob_grad - delta)).astype(jnp.bfloat16)
-        dq = jnp.dot(score_grad, k, preferred_element_type=jnp.float32) * inv_root
-        dq_ref[...] = dq.astype(dq_ref.dtype)
-        dk = lax.dot_general(score_grad, q, tn, preferred_element_type=jnp.float32) * inv_root
-        dv = lax.dot_general(prob_low, g, tn, preferred_element_type=jnp.float32)
-        for slot, (i, lead) in enumerate(slot_out):
-            out_refs[i][lead + (0,)] = dk[slot * rows : (slot + 1) * rows].astype(jnp.bfloat16)
-            out_refs[i][lead + (1,)] = dv[slot * rows : (slot + 1) * rows].astype(jnp.bfloat16)
+        for j in range(STEP_HEADS):
+            cols = slice(j * HD, (j + 1) * HD)
+            k = jnp.concatenate([in_refs[i][lead + (0, slice(None), cols)] for i, lead in slot_in], axis=0)
+            v = jnp.concatenate([in_refs[i][lead + (1, slice(None), cols)] for i, lead in slot_in], axis=0)
+            q = q_ref[:, cols]
+            g = g_ref[:, cols]
+            scores = lax.dot_general(q, k, nt, preferred_element_type=jnp.float32) * inv_root
+            masked = jnp.where(mask_ref[...] != 0, scores, -1e30)
+            highest = jnp.max(masked, axis=1, keepdims=True)
+            total_mass = jnp.sum(jnp.exp(masked - highest), axis=1, keepdims=True)
+            log_total = highest + jnp.log(total_mass)
+            prob = jnp.exp(masked - log_total)
+            prob_low = prob.astype(jnp.bfloat16)
+            attended = jnp.dot(prob_low, v, preferred_element_type=jnp.float32)
+            delta = jnp.sum(g.astype(jnp.float32) * attended, axis=1, keepdims=True)
+            prob_grad = lax.dot_general(g, v, nt, preferred_element_type=jnp.float32)
+            score_grad = (prob * (prob_grad - delta)).astype(jnp.bfloat16)
+            dq = jnp.dot(score_grad, k, preferred_element_type=jnp.float32) * inv_root
+            dq_ref[:, cols] = dq.astype(dq_ref.dtype)
+            dk = lax.dot_general(score_grad, q, tn, preferred_element_type=jnp.float32) * inv_root
+            dv = lax.dot_general(prob_low, g, tn, preferred_element_type=jnp.float32)
+            for slot, (i, lead) in enumerate(slot_out):
+                part = slice(slot * rows, (slot + 1) * rows)
+                out_refs[i][lead + (0, slice(None), cols)] = dk[part].astype(jnp.bfloat16)
+                out_refs[i][lead + (1, slice(None), cols)] = dv[part].astype(jnp.bfloat16)
 
     def head_spec(lead_shape):
         zeros = (0,) * len(lead_shape)
-        return pl.BlockSpec(lead_shape + (2, rows, HD), lambda h: zeros + (0, 0, h))
+        return pl.BlockSpec(lead_shape + (2, rows, STEP_HEADS * HD), lambda h: zeros + (0, 0, h))
 
     in_specs = [
         pl.BlockSpec((rows, slots * rows), lambda h: (0, 0)),
-        pl.BlockSpec((rows, HD), lambda h: (0, h + offset)),
-        pl.BlockSpec((rows, HD), lambda h: (0, h + offset)),
+        pl.BlockSpec((rows, STEP_HEADS * HD), lambda h: (0, h + offset // STEP_HEADS)),
+        pl.BlockSpec((rows, STEP_HEADS * HD), lambda h: (0, h + offset // STEP_HEADS)),
     ] + [head_spec(tuple(x.shape[:-3])) for x in inputs]
-    out_specs = [pl.BlockSpec((rows, HD), lambda h: (0, h))] + [head_spec(lead) for lead in out_lead]
+    out_specs = [pl.BlockSpec((rows, STEP_HEADS * HD), lambda h: (0, h))] + [head_spec(lead) for lead in out_lead]
     out_shape = [jax.ShapeDtypeStruct((rows, channels), jnp.bfloat16)] + [
         jax.ShapeDtypeStruct(lead + (2, rows, channels), jnp.bfloat16) for lead in out_lead
     ]
     results = pl.pallas_call(
         kernel,
-        grid=(heads,),
+        grid=(heads // STEP_HEADS,),
         in_specs=in_specs,
         out_specs=out_specs,
         out_shape=out_shape,
@@ -233,18 +237,18 @@
     firsts, seconds, outs, backs, sums, dqs = [], [], [], [], [], []
     for c, first in enumerate(starts):
         own = jnp.stack([keys[:, first : first + width], values[:, first : first + width]])
-        firsts.append(forward_relay(own, count, firsts[c - 1][1:] if c else None))
+        firsts.append(forward_relay(own, count, None))
     for c in range(len(starts)):
-        seconds.append(forward_second(firsts[c], count, seconds[c - 1][5:] if c else None))
+        seconds.append(forward_second(firsts[c], count, None))
     for c, first in enumerate(starts):
         dq, parts = chunk_kernel(forward_mask, queries, out_grad, seconds[c], first // HD, inv_root)
         dqs.append(dq)
         outs.append(parts)
     for c in range(len(starts)):
-        backs.append(return_first(outs[c], count, backs[c - 1] if c else None))
+        backs.append(return_first(outs[c], count, None))
     got = None
     for c in range(len(starts)):
-        got, summed = return_second(outs[c], backs[c], count, got)
+        got, summed = return_second(outs[c], backs[c], count, None)
         sums.append(summed)
     grads = [(dqs[c], sums[c][0].astype(jnp.bfloat16), sums[c][1].astype(jnp.bfloat16)) for c in range(len(starts))]
     query_grad = jnp.concatenate([grad[0] for grad in grads], axis=1)

time: 151 us -> 146 us (0.967)
  waiting for transfers between devices: 50.4 us -> 54.5 us
  starting transfers between devices: 50.9 us -> 47.2 us
  local copies, waits for them, and re-layouts: 4.16 us -> 1.6 us
    ppermute x26, waiting for transfers between devices: 50.4 us -> 54.5 us  [send(): return lax.ppermute(value, 'tm', pairs)]
    ppermute x26, starting transfers between devices: 50.9 us -> 47.2 us  [send(): return lax.ppermute(value, 'tm', pairs)]
    unnamed x41 -> x25, local copies, waits for them, and re-layouts: 2.71 us -> 0.15 us
  transfers between devices with their start and end apart: 26 -> 26, of which waited for: 12 -> 15; matrix products, arithmetic and copies ran while one was open for 8% -> 7% of each run, Pallas kernels for 20% -> 19%
where the time goes in v7:
time: 146 us; the launch traced here: 145 us
  waiting for transfers between devices  54.5 us (37%)
  starting transfers between devices  47.2 us (32%)
  Pallas kernels  28.2 us (19%)
  other arithmetic  12.5 us (9%)
  local copies, waits for them, and re-layouts  1.6 us (1%)
    ppermute x26, waiting for transfers between devices, send(): return lax.ppermute(value, 'tm', pairs)  54.5 us
    ppermute x26, starting transfers between devices, send(): return lax.ppermute(value, 'tm', pairs)  47.2 us
    pallas_call x2, Pallas kernels, attention_backward(): pl.pallas_call(kernel, grid=(heads // STEP_HEADS,), in_specs=in_specs, ou...  28.2 us
    another operation x2, other arithmetic, forward_second(): ahead = jnp.stack([from_cross, from_below, from_above])  4.72 us
  transfers between devices with their start and end apart: 26, of which 15 were waited for; matrix products, arithmetic and copies ran while one was open for 7% of the time, Pallas kernels for 19%

profile of v7, /device:TPU:0, one launch (start us, length us, event | category | flops | bytes accessed | tf_op | source)
XLA Modules:
  0.0 145.1 jit_solution(16141935165642301362)
XLA Ops:
  0.6 1.4 slice_bitcast_fusion.14
  2.0 0.0 copy-start.11
  2.0 0.1 pad_maximum_fusion.2.refs_0_
  2.1 0.0 copy-start.7
  2.1 3.1 %collective-permute-start.1 = (bf16[2,128,1280]{2,1,0:T(8,128)(2,1)S(1)}, bf16[2,128,1280]{2,1,0:T(8,128)(2,1)}, u32[]{:S(2)}, u32[]{:S(2)}) collective-permute-start(bf16[2,128,1280]{2,1,0:T(8,128)(2,1)S(1)} %pad_maximum_fusion.2.refs_0_), channel_id=1, source_target_pairs={{0,2},{1,3},{2,0},{3,1},{4,6},{5,7},{6,4},{7,5},{8,10},{9,11},{10,... | collective-permute-start | bytes 1966088 | tf_op jit(solution)/shard_map/ppermute | solution.py:16
  5.1 4.3 %collective-permute-start.2 = (bf16[2,128,1280]{2,1,0:T(8,128)(2,1)S(1)}, bf16[2,128,1280]{2,1,0:T(8,128)(2,1)}, u32[]{:S(2)}, u32[]{:S(2)}) collective-permute-start(bf16[2,128,1280]{2,1,0:T(8,128)(2,1)S(1)} %pad_maximum_fusion.2.refs_0_), channel_id=1, source_target_pairs={{0,4},{1,5},{2,6},{3,7},{4,8},{5,9},{6,10},{7,11},{8,12},{9,13},{1... | collective-permute-start | bytes 1966088 | tf_op jit(solution)/shard_map/ppermute | solution.py:16
  9.5 1.3 collective-permute-start.3
  10.8 0.1 pad_maximum_fusion.3.refs_0_
  10.8 0.0 copy-start.6
  10.9 0.6 collective-permute-start.8
  11.4 5.4 %collective-permute-start.9 = (bf16[2,128,1280]{2,1,0:T(8,128)(2,1)S(1)}, bf16[2,128,1280]{2,1,0:T(8,128)(2,1)}, u32[]{:S(2)}, u32[]{:S(2)}) collective-permute-start(bf16[2,128,1280]{2,1,0:T(8,128)(2,1)S(1)} %pad_maximum_fusion.3.refs_0_), channel_id=1, source_target_pairs={{0,4},{1,5},{2,6},{3,7},{4,8},{5,9},{6,10},{7,11},{8,12},{9,13},{1... | collective-permute-start | bytes 1966088 | tf_op jit(solution)/shard_map/ppermute | solution.py:16
  16.9 0.1 select_reduce_fusion
  17.0 3.8 %collective-permute-done.1.refs_2_ = bf16[2,128,1280]{2,1,0:T(8,128)(2,1)} collective-permute-done((bf16[2,128,1280]{2,1,0:T(8,128)(2,1)S(1)}, bf16[2,128,1280]{2,1,0:T(8,128)(2,1)}, u32[]{:S(2)}, u32[]{:S(2)}) %collective-permute-start.1) | collective-permute-done | bytes 655392 | tf_op jit(solution)/shard_map/ppermute | solution.py:16
  20.8 1.3 collective-permute-start.10
  22.2 1.6 %collective-permute-done.2.refs_3_ = bf16[2,128,1280]{2,1,0:T(8,128)(2,1)} collective-permute-done((bf16[2,128,1280]{2,1,0:T(8,128)(2,1)S(1)}, bf16[2,128,1280]{2,1,0:T(8,128)(2,1)}, u32[]{:S(2)}, u32[]{:S(2)}) %collective-permute-start.2) | collective-permute-done | bytes 655392 | tf_op jit(solution)/shard_map/ppermute | solution.py:16
  23.7 5.3 %collective-permute-done.3.refs_4_ = bf16[2,128,1280]{2,1,0:T(8,128)(2,1)} collective-permute-done((bf16[2,128,1280]{2,1,0:T(8,128)(2,1)S(1)}, bf16[2,128,1280]{2,1,0:T(8,128)(2,1)}, u32[]{:S(2)}, u32[]{:S(2)}) %collective-permute-start.3) | collective-permute-done | bytes 655392 | tf_op jit(solution)/shard_map/ppermute | solution.py:16
  29.1 1.7 %pad_maximum_fusion = bf16[3,2,128,1280]{3,2,1,0:T(8,128)(2,1)S(1)} fusion(bf16[1,2,128,1280]{3,2,1,0:T(8,128)(2,1)} %bitcast.7, bf16[1,2,128,1280]{3,2,1,0:T(8,128)(2,1)} %bitcast.6, bf16[1,2,128,1280]{3,2,1,0:T(8,128)(2,1)} %bitcast.5), kind=kLoop, calls=%fused_computation | loop fusion | flops 1966080 | bytes 3932160 | tf_op jit(solution)/shard_map/stack | solution.py:156
  30.8 0.1 collective-permute-start.4
  30.9 3.1 %collective-permute-done.8.refs_2_ = bf16[2,128,1280]{2,1,0:T(8,128)(2,1)} collective-permute-done((bf16[2,128,1280]{2,1,0:T(8,128)(2,1)S(1)}, bf16[2,128,1280]{2,1,0:T(8,128)(2,1)}, u32[]{:S(2)}, u32[]{:S(2)}) %collective-permute-start.8) | collective-permute-done | bytes 655392 | tf_op jit(solution)/shard_map/ppermute | solution.py:16
  34.0 2.3 %collective-permute-done.9.refs_3_ = bf16[2,128,1280]{2,1,0:T(8,128)(2,1)} collective-permute-done((bf16[2,128,1280]{2,1,0:T(8,128)(2,1)S(1)}, bf16[2,128,1280]{2,1,0:T(8,128)(2,1)}, u32[]{:S(2)}, u32[]{:S(2)}) %collective-permute-start.9) | collective-permute-done | bytes 655392 | tf_op jit(solution)/shard_map/ppermute | solution.py:16
  36.4 5.1 %collective-permute-done.10.refs_4_ = bf16[2,128,1280]{2,1,0:T(8,128)(2,1)} collective-permute-done((bf16[2,128,1280]{2,1,0:T(8,128)(2,1)S(1)}, bf16[2,128,1280]{2,1,0:T(8,128)(2,1)}, u32[]{:S(2)}, u32[]{:S(2)}) %collective-permute-start.10) | collective-permute-done | bytes 655392 | tf_op jit(solution)/shard_map/ppermute | solution.py:16
  41.4 3.0 %pad_maximum_fusion.1 = bf16[3,2,128,1280]{3,2,1,0:T(8,128)(2,1)} fusion(bf16[1,2,128,1280]{3,2,1,0:T(8,128)(2,1)} %bitcast.12, bf16[1,2,128,1280]{3,2,1,0:T(8,128)(2,1)} %bitcast.11, bf16[1,2,128,1280]{3,2,1,0:T(8,128)(2,1)} %bitcast.10), kind=kLoop, calls=%fused_computation.1 | loop fusion | flops 1966080 | bytes 3932160 | tf_op jit(solution)/shard_map/stack | solution.py:156
  44.5 0.0 collective-permute-start.11
  44.5 0.1 copy.9
  44.6 0.1 multiply_reduce_fusion
  44.7 3.6 %collective-permute-start.5 = (bf16[2,128,1280]{2,1,0:T(8,128)(2,1)}, bf16[2,128,1280]{2,1,0:T(8,128)(2,1)}, u32[]{:S(2)}, u32[]{:S(2)}) collective-permute-start(bf16[2,128,1280]{2,1,0:T(8,128)(2,1)} %collective-permute-done.1.refs_2_), channel_id=1, source_target_pairs={{0,5},{3,6},{4,9},{7,10},{8,13},{11,14},{16,21},{19,22},{20,25},{2... | collective-permute-start | bytes 1966088 | tf_op jit(solution)/shard_map/ppermute | solution.py:16
  48.3 1.5 %collective-permute-start.6 = (bf16[2,128,1280]{2,1,0:T(8,128)(2,1)}, bf16[2,128,1280]{2,1,0:T(8,128)(2,1)}, u32[]{:S(2)}, u32[]{:S(2)}) collective-permute-start(bf16[2,128,1280]{2,1,0:T(8,128)(2,1)} %collective-permute-done.1.refs_2_), channel_id=1, source_target_pairs={{4,1},{7,2},{8,5},{11,6},{12,9},{15,10},{20,17},{23,18},{24,21},{2... | collective-permute-start | bytes 1966088 | tf_op jit(solution)/shard_map/ppermute | solution.py:16
  49.8 1.4 fusion.24.mask_ref
  51.2 0.0 collective-permute-done.refs_1_
  51.2 4.6 %collective-permute-done.5.refs_6_ = bf16[2,128,1280]{2,1,0:T(8,128)(2,1)} collective-permute-done((bf16[2,128,1280]{2,1,0:T(8,128)(2,1)}, bf16[2,128,1280]{2,1,0:T(8,128)(2,1)}, u32[]{:S(2)}, u32[]{:S(2)}) %collective-permute-start.5) | collective-permute-done | bytes 655392 | tf_op jit(solution)/shard_map/ppermute | solution.py:16
  55.8 4.7 %collective-permute-start.12 = (bf16[2,128,1280]{2,1,0:T(8,128)(2,1)}, bf16[2,128,1280]{2,1,0:T(8,128)(2,1)}, u32[]{:S(2)}, u32[]{:S(2)}) collective-permute-start(bf16[2,128,1280]{2,1,0:T(8,128)(2,1)} %collective-permute-done.8.refs_2_), channel_id=1, source_target_pairs={{0,5},{3,6},{4,9},{7,10},{8,13},{11,14},{16,21},{19,22},{20,25},{2... | collective-permute-start | bytes 1966088 | tf_op jit(solution)/shard_map/ppermute | solution.py:16
  60.5 0.0 collective-permute-done.6.refs_7_
  60.5 1.5 %collective-permute-start.13 = (bf16[2,128,1280]{2,1,0:T(8,128)(2,1)}, bf16[2,128,1280]{2,1,0:T(8,128)(2,1)}, u32[]{:S(2)}, u32[]{:S(2)}) collective-permute-start(bf16[2,128,1280]{2,1,0:T(8,128)(2,1)} %collective-permute-done.8.refs_2_), channel_id=1, source_target_pairs={{4,1},{7,2},{8,5},{11,6},{12,9},{15,10},{20,17},{23,18},{24,21},{2... | collective-permute-start | bytes 1966088 | tf_op jit(solution)/shard_map/ppermute | solution.py:16
  62.0 14.1 %shard_map.85 = (bf16[128,1280]{1,0:T(8,128)(2,1)}, bf16[2,128,1280]{2,1,0:T(8,128)(2,1)}, bf16[4,2,128,1280]{3,2,1,0:T(8,128)(2,1)}, bf16[2,128,1280]{2,1,0:T(8...) custom-call(s32[128,1280]{1,0:T(8,128)} %fusion.24.mask_ref, ...), custom_call_target="tpu_custom_call" | custom-call | flops 2516582400 | bytes 14745600 | tf_op jit(solution)/shard_map/pallas_call | solution.py:127
  76.1 0.1 collective-permute-start.14
  76.2 0.0 collective-permute-done.12.refs_6_
  76.2 0.0 collective-permute-done.13.refs_7_
  76.2 14.2 %shard_map.86 = (bf16[128,1280]{1,0:T(8,128)(2,1)}, bf16[2,128,1280]{2,1,0:T(8,128)(2,1)}, bf16[4,2,128,1280]{3,2,1,0:T(8,128)(2,1)}, bf16[2,128,1280]{2,1,0:T(8...) custom-call(s32[128,1280]{1,0:T(8,128)} %fusion.24.mask_ref, ...), custom_call_target="tpu_custom_call" | custom-call | flops 2516582400 | bytes 14745600 | tf_op jit(solution)/shard_map/pallas_call | solution.py:127
  90.4 0.5 collective-permute-start.20
  90.9 1.3 collective-permute-start.15
  92.2 0.7 collective-permute-start.16
  92.9 1.3 collective-permute-start.21
  94.2 2.0 %pad_maximum_fusion.4 = bf16[128,2560]{1,0:T(8,128)(2,1)} fusion(bf16[128,1280]{1,0:T(8,128)(2,1)} %get-tuple-element.20, bf16[128,1280]{1,0:T(8,128)(2,1)} %get-tuple-element.19), kind=kLoop, calls=%fused_computation.46 | loop fusion | flops 1310720 | bytes 1310720 | tf_op jit(solution)/shard_map/concatenate | solution.py:254
  96.2 6.9 %collective-permute-done.15 = bf16[2,128,1280]{2,1,0:T(8,128)(2,1)S(1)} collective-permute-done((bf16[2,128,1280]{2,1,0:T(8,128)(2,1)}, bf16[2,128,1280]{2,1,0:T(8,128)(2,1)S(1)}, u32[]{:S(2)}, u32[]{:S(2)}) %collective-permute-start.15) | collective-permute-done | bytes 655392 | tf_op jit(solution)/shard_map/ppermute | solution.py:16
  103.0 0.7 collective-permute-start.22
  103.8 0.7 fusion.13
  104.5 3.6 %collective-permute-start.17 = (bf16[2,128,1280]{2,1,0:T(8,128)(2,1)S(1)}, bf16[2,128,1280]{2,1,0:T(8,128)(2,1)S(1)}, u32[]{:S(2)}, u32[]{:S(2)}) collective-permute-start(bf16[2,128,1280]{2,1,0:T(8,128)(2,1)S(1)} %get-tuple-element.35), channel_id=1, source_target_pairs={{0,2},{1,3},{2,0},{3,1},{4,6},{5,7},{6,4},{7,5},{8,10},{9,11},{10,... | collective-permute-start | bytes 1966088 | tf_op jit(solution)/shard_map/ppermute | solution.py:16
  108.1 1.3 collective-permute-start.18
  109.4 0.6 collective-permute-done.21
  110.1 4.1 %collective-permute-start.19 = (bf16[2,128,1280]{2,1,0:T(8,128)(2,1)S(1)}, bf16[2,128,1280]{2,1,0:T(8,128)(2,1)S(1)}, u32[]{:S(2)}, u32[]{:S(2)}) collective-permute-start(bf16[2,128,1280]{2,1,0:T(8,128)(2,1)S(1)} %get-tuple-element.36), channel_id=1, source_target_pairs={{0,4},{1,5},{2,6},{3,7},{4,8},{5,9},{6,10},{7,11},{8,12},{9,13},{1... | collective-permute-start | bytes 1966088 | tf_op jit(solution)/shard_map/ppermute | solution.py:16
  114.2 0.7 fusion.4
  114.9 1.5 %collective-permute-start.23 = (bf16[2,128,1280]{2,1,0:T(8,128)(2,1)S(1)}, bf16[2,128,1280]{2,1,0:T(8,128)(2,1)S(1)}, u32[]{:S(2)}, u32[]{:S(2)}) collective-permute-start(bf16[2,128,1280]{2,1,0:T(8,128)(2,1)S(1)} %get-tuple-element.38), channel_id=1, source_target_pairs={{0,2},{1,3},{2,0},{3,1},{4,6},{5,7},{6,4},{7,5},{8,10},{9,11},{10,... | collective-permute-start | bytes 1966088 | tf_op jit(solution)/shard_map/ppermute | solution.py:16
  116.4 1.3 collective-permute-start.24
  117.7 5.5 %collective-permute-done.17 = bf16[2,128,1280]{2,1,0:T(8,128)(2,1)S(1)} collective-permute-done((bf16[2,128,1280]{2,1,0:T(8,128)(2,1)S(1)}, bf16[2,128,1280]{2,1,0:T(8,128)(2,1)S(1)}, u32[]{:S(2)}, u32[]{:S(2)}) %collective-permute-start.17) | collective-permute-done | bytes 655392 | tf_op jit(solution)/shard_map/ppermute | solution.py:16
  123.2 3.6 %collective-permute-start.25 = (bf16[2,128,1280]{2,1,0:T(8,128)(2,1)S(1)}, bf16[2,128,1280]{2,1,0:T(8,128)(2,1)S(1)}, u32[]{:S(2)}, u32[]{:S(2)}) collective-permute-start(bf16[2,128,1280]{2,1,0:T(8,128)(2,1)S(1)} %get-tuple-element.39), channel_id=1, source_target_pairs={{0,4},{1,5},{2,6},{3,7},{4,8},{5,9},{6,10},{7,11},{8,12},{9,13},{1... | collective-permute-start | bytes 1966088 | tf_op jit(solution)/shard_map/ppermute | solution.py:16
  126.9 0.7 collective-permute-done.18
  127.6 1.6 %collective-permute-done.19 = bf16[2,128,1280]{2,1,0:T(8,128)(2,1)S(1)} collective-permute-done((bf16[2,128,1280]{2,1,0:T(8,128)(2,1)S(1)}, bf16[2,128,1280]{2,1,0:T(8,128)(2,1)S(1)}, u32[]{:S(2)}, u32[]{:S(2)}) %collective-permute-start.19) | collective-permute-done | bytes 655392 | tf_op jit(solution)/shard_map/ppermute | solution.py:16
  129.2 0.4 fusion.17
  129.7 7.0 %collective-permute-done.23 = bf16[2,128,1280]{2,1,0:T(8,128)(2,1)S(1)} collective-permute-done((bf16[2,128,1280]{2,1,0:T(8,128)(2,1)S(1)}, bf16[2,128,1280]{2,1,0:T(8,128)(2,1)S(1)}, u32[]{:S(2)}, u32[]{:S(2)}) %collective-permute-start.23) | collective-permute-done | bytes 655392 | tf_op jit(solution)/shard_map/ppermute | solution.py:16
  136.7 4.0 %collective-permute-done.24 = bf16[2,128,1280]{2,1,0:T(8,128)(2,1)S(1)} collective-permute-done((bf16[2,128,1280]{2,1,0:T(8,128)(2,1)S(1)}, bf16[2,128,1280]{2,1,0:T(8,128)(2,1)S(1)}, u32[]{:S(2)}, u32[]{:S(2)}) %collective-permute-start.24) | collective-permute-done | bytes 655392 | tf_op jit(solution)/shard_map/ppermute | solution.py:16
  140.7 2.2 %collective-permute-done.25 = bf16[2,128,1280]{2,1,0:T(8,128)(2,1)S(1)} collective-permute-done((bf16[2,128,1280]{2,1,0:T(8,128)(2,1)S(1)}, bf16[2,128,1280]{2,1,0:T(8,128)(2,1)S(1)}, u32[]{:S(2)}, u32[]{:S(2)}) %collective-permute-start.25) | collective-permute-done | bytes 655392 | tf_op jit(solution)/shard_map/ppermute | solution.py:16
  142.9 0.4 fusion.8
  143.4 0.9 pad_maximum_fusion.6
  144.3 0.9 pad_maximum_fusion.5
  (49 shorter events, 0.3 us)
Async XLA Ops:
  2.0 14.9 %copy-start.11 = (s32[4]{0:T(128)S(1)}, s32[4]{0:T(128)}, u32[]{:S(2)}) copy-start(s32[4]{0:T(128)} %param.11) | copy-start | bytes 52
  2.1 28.7 %copy-start.7 = (bf16[2,128,1280]{2,1,0:T(8,128)(2,1)}, bf16[2,128,1280]{2,1,0:T(8,128)(2,1)S(1)}, u32[]{:S(2)}) copy-start(bf16[2,128,1280]{2,1,0:T(8,128)(2,1)S(1)} %pad_maximum_fusion.2.refs_0_) | copy-start | bytes 1966084
  2.1 18.7 %collective-permute-start.1 = (bf16[2,128,1280]{2,1,0:T(8,128)(2,1)S(1)}, bf16[2,128,1280]{2,1,0:T(8,128)(2,1)}, u32[]{:S(2)}, u32[]{:S(2)}) collective-permute-start(bf16[2,128,1280]{2,1,0:T(8,128)(2,1)S(1)} %pad_maximum_fusion.2.refs_0_), channel_id=1, source_target_pairs={{0,2},{1,3},{2,0},{3,1},{4,6},{5,7},{6,4},{7,5},{8,10},{9,11},{10,... | collective-permute-start | bytes 1966088 | tf_op jit(solution)/shard_map/ppermute | solution.py:16
  5.1 18.6 %collective-permute-start.2 = (bf16[2,128,1280]{2,1,0:T(8,128)(2,1)S(1)}, bf16[2,128,1280]{2,1,0:T(8,128)(2,1)}, u32[]{:S(2)}, u32[]{:S(2)}) collective-permute-start(bf16[2,128,1280]{2,1,0:T(8,128)(2,1)S(1)} %pad_maximum_fusion.2.refs_0_), channel_id=1, source_target_pairs={{0,4},{1,5},{2,6},{3,7},{4,8},{5,9},{6,10},{7,11},{8,12},{9,13},{1... | collective-permute-start | bytes 1966088 | tf_op jit(solution)/shard_map/ppermute | solution.py:16
  9.5 19.6 %collective-permute-start.3 = (bf16[2,128,1280]{2,1,0:T(8,128)(2,1)S(1)}, bf16[2,128,1280]{2,1,0:T(8,128)(2,1)}, u32[]{:S(2)}, u32[]{:S(2)}) collective-permute-start(bf16[2,128,1280]{2,1,0:T(8,128)(2,1)S(1)} %pad_maximum_fusion.2.refs_0_), channel_id=1, source_target_pairs={{4,0},{5,1},{6,2},{7,3},{8,4},{9,5},{10,6},{11,7},{12,8},{13,9},{1... | collective-permute-start | bytes 1966088 | tf_op jit(solution)/shard_map/ppermute | solution.py:16
  10.8 40.4 %copy-start.6 = (bf16[2,128,1280]{2,1,0:T(8,128)(2,1)}, bf16[2,128,1280]{2,1,0:T(8,128)(2,1)S(1)}, u32[]{:S(2)}) copy-start(bf16[2,128,1280]{2,1,0:T(8,128)(2,1)S(1)} %pad_maximum_fusion.3.refs_0_) | copy-start | bytes 1966084
  10.9 23.2 %collective-permute-start.8 = (bf16[2,128,1280]{2,1,0:T(8,128)(2,1)S(1)}, bf16[2,128,1280]{2,1,0:T(8,128)(2,1)}, u32[]{:S(2)}, u32[]{:S(2)}) collective-permute-start(bf16[2,128,1280]{2,1,0:T(8,128)(2,1)S(1)} %pad_maximum_fusion.3.refs_0_), channel_id=1, source_target_pairs={{0,2},{1,3},{2,0},{3,1},{4,6},{5,7},{6,4},{7,5},{8,10},{9,11},{10,... | collective-permute-start | bytes 1966088 | tf_op jit(solution)/shard_map/ppermute | solution.py:16
  11.4 24.9 %collective-permute-start.9 = (bf16[2,128,1280]{2,1,0:T(8,128)(2,1)S(1)}, bf16[2,128,1280]{2,1,0:T(8,128)(2,1)}, u32[]{:S(2)}, u32[]{:S(2)}) collective-permute-start(bf16[2,128,1280]{2,1,0:T(8,128)(2,1)S(1)} %pad_maximum_fusion.3.refs_0_), channel_id=1, source_target_pairs={{0,4},{1,5},{2,6},{3,7},{4,8},{5,9},{6,10},{7,11},{8,12},{9,13},{1... | collective-permute-start | bytes 1966088 | tf_op jit(solution)/shard_map/ppermute | solution.py:16
  20.8 20.6 %collective-permute-start.10 = (bf16[2,128,1280]{2,1,0:T(8,128)(2,1)S(1)}, bf16[2,128,1280]{2,1,0:T(8,128)(2,1)}, u32[]{:S(2)}, u32[]{:S(2)}) collective-permute-start(bf16[2,128,1280]{2,1,0:T(8,128)(2,1)S(1)} %pad_maximum_fusion.3.refs_0_), channel_id=1, source_target_pairs={{4,0},{5,1},{6,2},{7,3},{8,4},{9,5},{10,6},{11,7},{12,8},{13,9},{1... | collective-permute-start | bytes 1966088 | tf_op jit(solution)/shard_map/ppermute | solution.py:16
  23.7 27.5 %collective-permute-start = (bf16[2,128,1280]{2,1,0:T(8,128)(2,1)S(1)}, bf16[2,128,1280]{2,1,0:T(8,128)(2,1)}, u32[]{:S(2)}, u32[]{:S(2)}) collective-permute-start(bf16[2,128,1280]{2,1,0:T(8,128)(2,1)S(1)} %pad_maximum_fusion.2.refs_0_), channel_id=1, source_target_pairs={{0,1},{1,0},{2,3},{3,2},{4,5},{5,4},{6,7},{7,6},{8,9},{9,8},{10,11... | collective-permute-start | bytes 1966088 | tf_op jit(solution)/shard_map/ppermute | solution.py:16
  30.8 31.2 %collective-permute-start.4 = (bf16[3,2,128,1280]{3,2,1,0:T(8,128)(2,1)S(1)}, bf16[3,2,128,1280]{3,2,1,0:T(8,128)(2,1)}, u32[]{:S(2)}, u32[]{:S(2)}) collective-permute-start(bf16[3,2,128,1280]{3,2,1,0:T(8,128)(2,1)S(1)} %pad_maximum_fusion), channel_id=1, source_target_pairs={{0,1},{1,0},{2,3},{3,2},{4,5},{5,4},{6,7},{7,6},{8,9},{9,8},{10,11... | collective-permute-start | bytes 5898248 | tf_op jit(solution)/shard_map/ppermute | solution.py:16
  41.4 3.0 %copy-start.10 = (s32[4,3]{1,0:T(4,128)S(1)}, s32[4,3]{1,0:T(4,128)}, u32[]{:S(2)}) copy-start(s32[4,3]{1,0:T(4,128)} %param.10) | copy-start | bytes 148
  44.5 31.7 %collective-permute-start.11 = (bf16[3,2,128,1280]{3,2,1,0:T(8,128)(2,1)}, bf16[3,2,128,1280]{3,2,1,0:T(8,128)(2,1)}, u32[]{:S(2)}, u32[]{:S(2)}) collective-permute-start(bf16[3,2,128,1280]{3,2,1,0:T(8,128)(2,1)} %pad_maximum_fusion.1), channel_id=1, source_target_pairs={{0,1},{1,0},{2,3},{3,2},{4,5},{5,4},{6,7},{7,6},{8,9},{9,8},{10,11... | collective-permute-start | bytes 5898248 | tf_op jit(solution)/shard_map/ppermute | solution.py:16
  44.7 11.2 %collective-permute-start.5 = (bf16[2,128,1280]{2,1,0:T(8,128)(2,1)}, bf16[2,128,1280]{2,1,0:T(8,128)(2,1)}, u32[]{:S(2)}, u32[]{:S(2)}) collective-permute-start(bf16[2,128,1280]{2,1,0:T(8,128)(2,1)} %collective-permute-done.1.refs_2_), channel_id=1, source_target_pairs={{0,5},{3,6},{4,9},{7,10},{8,13},{11,14},{16,21},{19,22},{20,25},{2... | collective-permute-start | bytes 1966088 | tf_op jit(solution)/shard_map/ppermute | solution.py:16
  48.3 12.2 %collective-permute-start.6 = (bf16[2,128,1280]{2,1,0:T(8,128)(2,1)}, bf16[2,128,1280]{2,1,0:T(8,128)(2,1)}, u32[]{:S(2)}, u32[]{:S(2)}) collective-permute-start(bf16[2,128,1280]{2,1,0:T(8,128)(2,1)} %collective-permute-done.1.refs_2_), channel_id=1, source_target_pairs={{4,1},{7,2},{8,5},{11,6},{12,9},{15,10},{20,17},{23,18},{24,21},{2... | collective-permute-start | bytes 1966088 | tf_op jit(solution)/shard_map/ppermute | solution.py:16
  51.2 24.9 %collective-permute-start.7 = (bf16[2,128,1280]{2,1,0:T(8,128)(2,1)S(1)}, bf16[2,128,1280]{2,1,0:T(8,128)(2,1)}, u32[]{:S(2)}, u32[]{:S(2)}) collective-permute-start(bf16[2,128,1280]{2,1,0:T(8,128)(2,1)S(1)} %pad_maximum_fusion.3.refs_0_), channel_id=1, source_target_pairs={{0,1},{1,0},{2,3},{3,2},{4,5},{5,4},{6,7},{7,6},{8,9},{9,8},{10,11... | collective-permute-start | bytes 1966088 | tf_op jit(solution)/shard_map/ppermute | solution.py:16
  55.8 20.3 %collective-permute-start.12 = (bf16[2,128,1280]{2,1,0:T(8,128)(2,1)}, bf16[2,128,1280]{2,1,0:T(8,128)(2,1)}, u32[]{:S(2)}, u32[]{:S(2)}) collective-permute-start(bf16[2,128,1280]{2,1,0:T(8,128)(2,1)} %collective-permute-done.8.refs_2_), channel_id=1, source_target_pairs={{0,5},{3,6},{4,9},{7,10},{8,13},{11,14},{16,21},{19,22},{20,25},{2... | collective-permute-start | bytes 1966088 | tf_op jit(solution)/shard_map/ppermute | solution.py:16
  60.5 15.7 %collective-permute-start.13 = (bf16[2,128,1280]{2,1,0:T(8,128)(2,1)}, bf16[2,128,1280]{2,1,0:T(8,128)(2,1)}, u32[]{:S(2)}, u32[]{:S(2)}) collective-permute-start(bf16[2,128,1280]{2,1,0:T(8,128)(2,1)} %collective-permute-done.8.refs_2_), channel_id=1, source_target_pairs={{4,1},{7,2},{8,5},{11,6},{12,9},{15,10},{20,17},{23,18},{24,21},{2... | collective-permute-start | bytes 1966088 | tf_op jit(solution)/shard_map/ppermute | solution.py:16
  76.1 27.7 %collective-permute-start.14 = (bf16[4,2,128,1280]{3,2,1,0:T(8,128)(2,1)}, bf16[4,2,128,1280]{3,2,1,0:T(8,128)(2,1)S(1)}, u32[]{:S(2)}, u32[]{:S(2)}) collective-permute-start(bf16[4,2,128,1280]{3,2,1,0:T(8,128)(2,1)} %get-tuple-element.22), channel_id=1, source_target_pairs={{0,1},{1,0},{2,3},{3,2},{4,5},{5,4},{6,7},{7,6},{8,9},{9,8},{10,11... | collective-permute-start | bytes 7864328 | tf_op jit(solution)/shard_map/ppermute | solution.py:16
  76.2 27.6 %copy-start.2 = (bf16[2,128,1280]{2,1,0:T(8,128)(2,1)S(1)}, bf16[2,128,1280]{2,1,0:T(8,128)(2,1)}, u32[]{:S(2)}) copy-start(bf16[2,128,1280]{2,1,0:T(8,128)(2,1)} %get-tuple-element.27) | copy-start | bytes 1966084
  90.4 13.4 %copy-start = (bf16[2,128,1280]{2,1,0:T(8,128)(2,1)S(1)}, bf16[2,128,1280]{2,1,0:T(8,128)(2,1)}, u32[]{:S(2)}) copy-start(bf16[2,128,1280]{2,1,0:T(8,128)(2,1)} %get-tuple-element.23) | copy-start | bytes 1966084
  90.4 13.4 %copy-start.1 = (bf16[2,128,1280]{2,1,0:T(8,128)(2,1)S(1)}, bf16[2,128,1280]{2,1,0:T(8,128)(2,1)}, u32[]{:S(2)}) copy-start(bf16[2,128,1280]{2,1,0:T(8,128)(2,1)} %get-tuple-element.26) | copy-start | bytes 1966084
  90.4 23.8 %collective-permute-start.20 = (bf16[4,2,128,1280]{3,2,1,0:T(8,128)(2,1)}, bf16[4,2,128,1280]{3,2,1,0:T(8,128)(2,1)S(1)}, u32[]{:S(2)}, u32[]{:S(2)}) collective-permute-start(bf16[4,2,128,1280]{3,2,1,0:T(8,128)(2,1)} %get-tuple-element.29), channel_id=1, source_target_pairs={{0,1},{1,0},{2,3},{3,2},{4,5},{5,4},{6,7},{7,6},{8,9},{9,8},{10,11... | collective-permute-start | bytes 7864328 | tf_op jit(solution)/shard_map/ppermute | solution.py:16
  90.9 12.1 %collective-permute-start.15 = (bf16[2,128,1280]{2,1,0:T(8,128)(2,1)}, bf16[2,128,1280]{2,1,0:T(8,128)(2,1)S(1)}, u32[]{:S(2)}, u32[]{:S(2)}) collective-permute-start(bf16[2,128,1280]{2,1,0:T(8,128)(2,1)} %get-tuple-element.24), channel_id=1, source_target_pairs={{5,0},{6,3},{9,4},{10,7},{13,8},{14,11},{21,16},{22,19},{25,20},{2... | collective-permute-start | bytes 1966088 | tf_op jit(solution)/shard_map/ppermute | solution.py:16
  92.2 11.5 %collective-permute-start.16 = (bf16[2,128,1280]{2,1,0:T(8,128)(2,1)}, bf16[2,128,1280]{2,1,0:T(8,128)(2,1)S(1)}, u32[]{:S(2)}, u32[]{:S(2)}) collective-permute-start(bf16[2,128,1280]{2,1,0:T(8,128)(2,1)} %get-tuple-element.25), channel_id=1, source_target_pairs={{1,4},{2,7},{5,8},{6,11},{9,12},{10,15},{17,20},{18,23},{21,24},{2... | collective-permute-start | bytes 1966088 | tf_op jit(solution)/shard_map/ppermute | solution.py:16
  92.9 17.1 %collective-permute-start.21 = (bf16[2,128,1280]{2,1,0:T(8,128)(2,1)}, bf16[2,128,1280]{2,1,0:T(8,128)(2,1)S(1)}, u32[]{:S(2)}, u32[]{:S(2)}) collective-permute-start(bf16[2,128,1280]{2,1,0:T(8,128)(2,1)} %get-tuple-element.31), channel_id=1, source_target_pairs={{5,0},{6,3},{9,4},{10,7},{13,8},{14,11},{21,16},{22,19},{25,20},{2... | collective-permute-start | bytes 1966088 | tf_op jit(solution)/shard_map/ppermute | solution.py:16
  103.0 11.1 %collective-permute-start.22 = (bf16[2,128,1280]{2,1,0:T(8,128)(2,1)}, bf16[2,128,1280]{2,1,0:T(8,128)(2,1)S(1)}, u32[]{:S(2)}, u32[]{:S(2)}) collective-permute-start(bf16[2,128,1280]{2,1,0:T(8,128)(2,1)} %get-tuple-element.32), channel_id=1, source_target_pairs={{1,4},{2,7},{5,8},{6,11},{9,12},{10,15},{17,20},{18,23},{21,24},{2... | collective-permute-start | bytes 1966088 | tf_op jit(solution)/shard_map/ppermute | solution.py:16
  103.8 10.4 %copy-start.3 = (bf16[2,128,1280]{2,1,0:T(8,128)(2,1)S(1)}, bf16[2,128,1280]{2,1,0:T(8,128)(2,1)}, u32[]{:S(2)}) copy-start(bf16[2,128,1280]{2,1,0:T(8,128)(2,1)} %get-tuple-element.30) | copy-start | bytes 1966084
  103.8 10.4 %copy-start.4 = (bf16[2,128,1280]{2,1,0:T(8,128)(2,1)S(1)}, bf16[2,128,1280]{2,1,0:T(8,128)(2,1)}, u32[]{:S(2)}) copy-start(bf16[2,128,1280]{2,1,0:T(8,128)(2,1)} %get-tuple-element.33) | copy-start | bytes 1966084
  103.8 10.4 %copy-start.5 = (bf16[2,128,1280]{2,1,0:T(8,128)(2,1)S(1)}, bf16[2,128,1280]{2,1,0:T(8,128)(2,1)}, u32[]{:S(2)}) copy-start(bf16[2,128,1280]{2,1,0:T(8,128)(2,1)} %get-tuple-element.34) | copy-start | bytes 1966084
  104.5 18.7 %collective-permute-start.17 = (bf16[2,128,1280]{2,1,0:T(8,128)(2,1)S(1)}, bf16[2,128,1280]{2,1,0:T(8,128)(2,1)S(1)}, u32[]{:S(2)}, u32[]{:S(2)}) collective-permute-start(bf16[2,128,1280]{2,1,0:T(8,128)(2,1)S(1)} %get-tuple-element.35), channel_id=1, source_target_pairs={{0,2},{1,3},{2,0},{3,1},{4,6},{5,7},{6,4},{7,5},{8,10},{9,11},{10,... | collective-permute-start | bytes 1966088 | tf_op jit(solution)/shard_map/ppermute | solution.py:16
  108.1 19.5 %collective-permute-start.18 = (bf16[2,128,1280]{2,1,0:T(8,128)(2,1)S(1)}, bf16[2,128,1280]{2,1,0:T(8,128)(2,1)S(1)}, u32[]{:S(2)}, u32[]{:S(2)}) collective-permute-start(bf16[2,128,1280]{2,1,0:T(8,128)(2,1)S(1)} %get-tuple-element.37), channel_id=1, source_target_pairs={{4,0},{5,1},{6,2},{7,3},{8,4},{9,5},{10,6},{11,7},{12,8},{13,9},{1... | collective-permute-start | bytes 1966088 | tf_op jit(solution)/shard_map/ppermute | solution.py:16
  110.1 19.2 %collective-permute-start.19 = (bf16[2,128,1280]{2,1,0:T(8,128)(2,1)S(1)}, bf16[2,128,1280]{2,1,0:T(8,128)(2,1)S(1)}, u32[]{:S(2)}, u32[]{:S(2)}) collective-permute-start(bf16[2,128,1280]{2,1,0:T(8,128)(2,1)S(1)} %get-tuple-element.36), channel_id=1, source_target_pairs={{0,4},{1,5},{2,6},{3,7},{4,8},{5,9},{6,10},{7,11},{8,12},{9,13},{1... | collective-permute-start | bytes 1966088 | tf_op jit(solution)/shard_map/ppermute | solution.py:16
  114.2 15.0 %copy-start.8 = (bf16[2,128,1280]{2,1,0:T(8,128)(2,1)S(1)}, bf16[2,128,1280]{2,1,0:T(8,128)(2,1)}, u32[]{:S(2)}) copy-start(bf16[2,128,1280]{2,1,0:T(8,128)(2,1)} %get-tuple-element.21) | copy-start | bytes 1966084
  114.9 21.8 %collective-permute-start.23 = (bf16[2,128,1280]{2,1,0:T(8,128)(2,1)S(1)}, bf16[2,128,1280]{2,1,0:T(8,128)(2,1)S(1)}, u32[]{:S(2)}, u32[]{:S(2)}) collective-permute-start(bf16[2,128,1280]{2,1,0:T(8,128)(2,1)S(1)} %get-tuple-element.38), channel_id=1, source_target_pairs={{0,2},{1,3},{2,0},{3,1},{4,6},{5,7},{6,4},{7,5},{8,10},{9,11},{10,... | collective-permute-start | bytes 1966088 | tf_op jit(solution)/shard_map/ppermute | solution.py:16
  116.4 24.3 %collective-permute-start.24 = (bf16[2,128,1280]{2,1,0:T(8,128)(2,1)S(1)}, bf16[2,128,1280]{2,1,0:T(8,128)(2,1)S(1)}, u32[]{:S(2)}, u32[]{:S(2)}) collective-permute-start(bf16[2,128,1280]{2,1,0:T(8,128)(2,1)S(1)} %get-tuple-element.40), channel_id=1, source_target_pairs={{4,0},{5,1},{6,2},{7,3},{8,4},{9,5},{10,6},{11,7},{12,8},{13,9},{1... | collective-permute-start | bytes 1966088 | tf_op jit(solution)/shard_map/ppermute | solution.py:16
  123.2 19.7 %collective-permute-start.25 = (bf16[2,128,1280]{2,1,0:T(8,128)(2,1)S(1)}, bf16[2,128,1280]{2,1,0:T(8,128)(2,1)S(1)}, u32[]{:S(2)}, u32[]{:S(2)}) collective-permute-start(bf16[2,128,1280]{2,1,0:T(8,128)(2,1)S(1)} %get-tuple-element.39), channel_id=1, source_target_pairs={{0,4},{1,5},{2,6},{3,7},{4,8},{5,9},{6,10},{7,11},{8,12},{9,13},{1... | collective-permute-start | bytes 1966088 | tf_op jit(solution)/shard_map/ppermute | solution.py:16
  129.6 13.3 %copy-start.9 = (bf16[2,128,1280]{2,1,0:T(8,128)(2,1)S(1)}, bf16[2,128,1280]{2,1,0:T(8,128)(2,1)}, u32[]{:S(2)}) copy-start(bf16[2,128,1280]{2,1,0:T(8,128)(2,1)} %get-tuple-element.28) | copy-start | bytes 1966084

commit v8 on v7

--- a/solution.py
+++ b/solution.py
@@ -141,12 +141,14 @@
 
 def forward_relay(own, count, after):
     core, cross, down, up, diag_up, diag_down, back = route(count)
-    if after is not None:
-        own, _ = lax.optimization_barrier((own, after))
+    own_cross = own_links = own
+    if after is not None:
+        own_cross, _ = lax.optimization_barrier((own, after[0]))
+        own_links, _ = lax.optimization_barrier((own, after[1]))
     from_core = send(own, core)
-    from_cross = send(own, cross)
-    from_below = send(own, up)
-    from_above = send(own, down)
+    from_cross = send(own_cross, cross)
+    from_below = send(own_links, up)
+    from_above = send(own_links, down)
     return [own, from_core, from_cross, from_below, from_above]
 
 
@@ -237,8 +239,8 @@
     firsts, seconds, outs, backs, sums, dqs = [], [], [], [], [], []
     for c, first in enumerate(starts):
         own = jnp.stack([keys[:, first : first + width], values[:, first : first + width]])
-        firsts.append(forward_relay(own, count, None))
-    for c in range(len(starts)):
+        after = (firsts[c - 1][2], seconds[c - 1][6:]) if c else None
+        firsts.append(forward_relay(own, count, after))
         seconds.append(forward_second(firsts[c], count, None))
     for c, first in enumerate(starts):
         dq, parts = chunk_kernel(forward_mask, queries, out_grad, seconds[c], first // HD, inv_root)

time: 146 us -> 149 us (1.021)
  waiting for transfers between devices: 54.5 us -> 57.4 us
    ppermute x26, waiting for transfers between devices: 54.5 us -> 57.4 us  [send(): return lax.ppermute(value, 'tm', pairs)]
  transfers between devices with their start and end apart: 26 -> 26, of which waited for: 15 -> 12; matrix products, arithmetic and copies ran while one was open for 7% -> 7% of each run, Pallas kernels for 19% -> 19%
where the time goes in v8:
time: 149 us; the launch traced here: 148 us
  waiting for transfers between devices  57.4 us (39%)
  starting transfers between devices  47.2 us (32%)
  Pallas kernels  28.2 us (19%)
  other arithmetic  12.5 us (8%)
  local copies, waits for them, and re-layouts  1.61 us (1%)
    ppermute x26, waiting for transfers between devices, send(): return lax.ppermute(value, 'tm', pairs)  57.4 us
    ppermute x26, starting transfers between devices, send(): return lax.ppermute(value, 'tm', pairs)  47.2 us
    pallas_call x2, Pallas kernels, attention_backward(): pl.pallas_call(kernel, grid=(heads // STEP_HEADS,), in_specs=in_specs, ou...  28.2 us
    another operation x2, other arithmetic, forward_second(): ahead = jnp.stack([from_cross, from_below, from_above])  4.77 us
  transfers between devices with their start and end apart: 26, of which 12 were waited for; matrix products, arithmetic and copies ran while one was open for 7% of the time, Pallas kernels for 19%

profile of v8, /device:TPU:0, one launch (start us, length us, event | category | flops | bytes accessed | tf_op | source)
XLA Modules:
  0.0 148.1 jit_solution(17402860814364634341)
XLA Ops:
  0.6 1.4 slice_bitcast_fusion.14
  2.0 0.0 copy-start.14
  2.0 0.1 pad_maximum_fusion.2.refs_0_
  2.1 0.0 copy-start.6
  2.1 3.1 %collective-permute-start.1 = (bf16[2,128,1280]{2,1,0:T(8,128)(2,1)S(1)}, bf16[2,128,1280]{2,1,0:T(8,128)(2,1)S(1)}, u32[]{:S(2)}, u32[]{:S(2)}) collective-permute-start(bf16[2,128,1280]{2,1,0:T(8,128)(2,1)S(1)} %pad_maximum_fusion.2.refs_0_), channel_id=1, source_target_pairs={{0,2},{1,3},{2,0},{3,1},{4,6},{5,7},{6,4},{7,5},{8,10},{9,11},{10,... | collective-permute-start | bytes 1966088 | tf_op jit(solution)/shard_map/ppermute | solution.py:16
  5.1 4.3 %collective-permute-start.2 = (bf16[2,128,1280]{2,1,0:T(8,128)(2,1)S(1)}, bf16[2,128,1280]{2,1,0:T(8,128)(2,1)}, u32[]{:S(2)}, u32[]{:S(2)}) collective-permute-start(bf16[2,128,1280]{2,1,0:T(8,128)(2,1)S(1)} %pad_maximum_fusion.2.refs_0_), channel_id=1, source_target_pairs={{0,4},{1,5},{2,6},{3,7},{4,8},{5,9},{6,10},{7,11},{8,12},{9,13},{1... | collective-permute-start | bytes 1966088 | tf_op jit(solution)/shard_map/ppermute | solution.py:16
  9.5 1.3 collective-permute-start.3
  10.9 9.0 %collective-permute-done.1.refs_2_ = bf16[2,128,1280]{2,1,0:T(8,128)(2,1)S(1)} collective-permute-done((bf16[2,128,1280]{2,1,0:T(8,128)(2,1)S(1)}, bf16[2,128,1280]{2,1,0:T(8,128)(2,1)S(1)}, u32[]{:S(2)}, u32[]{:S(2)}) %collective-permute-start.1) | collective-permute-done | bytes 655392 | tf_op jit(solution)/shard_map/ppermute | solution.py:16
  19.9 2.4 %collective-permute-start.5 = (bf16[2,128,1280]{2,1,0:T(8,128)(2,1)S(1)}, bf16[2,128,1280]{2,1,0:T(8,128)(2,1)S(1)}, u32[]{:S(2)}, u32[]{:S(2)}) collective-permute-start(bf16[2,128,1280]{2,1,0:T(8,128)(2,1)S(1)} %collective-permute-done.1.refs_2_), channel_id=1, source_target_pairs={{0,5},{3,6},{4,9},{7,10},{8,13},{11,14},{16,21},{19,22},{20,25},{2... | collective-permute-start | bytes 1966088 | tf_op jit(solution)/shard_map/ppermute | solution.py:16
  22.3 0.7 collective-permute-start.6
  23.1 0.1 select_reduce_fusion
  23.2 0.1 pad_maximum_fusion.3.refs_0_
  23.2 0.0 copy-start.7
  23.2 0.7 collective-permute-start.8
  23.9 6.4 %collective-permute-done.5.refs_6_ = bf16[2,128,1280]{2,1,0:T(8,128)(2,1)S(1)} collective-permute-done((bf16[2,128,1280]{2,1,0:T(8,128)(2,1)S(1)}, bf16[2,128,1280]{2,1,0:T(8,128)(2,1)S(1)}, u32[]{:S(2)}, u32[]{:S(2)}) %collective-permute-start.5) | collective-permute-done | bytes 655392 | tf_op jit(solution)/shard_map/ppermute | solution.py:16
  30.4 6.2 %collective-permute-start.9 = (bf16[2,128,1280]{2,1,0:T(8,128)(2,1)S(1)}, bf16[2,128,1280]{2,1,0:T(8,128)(2,1)}, u32[]{:S(2)}, u32[]{:S(2)}) collective-permute-start(bf16[2,128,1280]{2,1,0:T(8,128)(2,1)S(1)} %pad_maximum_fusion.3.refs_0_), channel_id=1, source_target_pairs={{0,4},{1,5},{2,6},{3,7},{4,8},{5,9},{6,10},{7,11},{8,12},{9,13},{1... | collective-permute-start | bytes 1966088 | tf_op jit(solution)/shard_map/ppermute | solution.py:16
  36.6 1.3 collective-permute-start.10
  37.9 0.0 collective-permute-done.2.refs_3_
  37.9 1.5 collective-permute-start
  39.4 1.7 %pad_maximum_fusion = bf16[3,2,128,1280]{3,2,1,0:T(8,128)(2,1)S(1)} fusion(bf16[1,2,128,1280]{3,2,1,0:T(8,128)(2,1)} %bitcast.7, bf16[1,2,128,1280]{3,2,1,0:T(8,128)(2,1)} %bitcast.6, bf16[1,2,128,1280]{3,2,1,0:T(8,128)(2,1)} %bitcast.68), kind=kLoop, calls=%fused_computation | loop fusion | flops 1966080 | bytes 3932160 | tf_op jit(solution)/shard_map/stack | solution.py:158
  41.1 0.1 collective-permute-start.4
  41.2 0.0 collective-permute-done.8.refs_2_
  41.2 0.5 collective-permute-start.7
  41.8 8.4 %collective-permute-done.9.refs_3_ = bf16[2,128,1280]{2,1,0:T(8,128)(2,1)} collective-permute-done((bf16[2,128,1280]{2,1,0:T(8,128)(2,1)S(1)}, bf16[2,128,1280]{2,1,0:T(8,128)(2,1)}, u32[]{:S(2)}, u32[]{:S(2)}) %collective-permute-start.9) | collective-permute-done | bytes 655392 | tf_op jit(solution)/shard_map/ppermute | solution.py:16
  50.1 5.6 %collective-permute-done.10.refs_4_ = bf16[2,128,1280]{2,1,0:T(8,128)(2,1)} collective-permute-done((bf16[2,128,1280]{2,1,0:T(8,128)(2,1)S(1)}, bf16[2,128,1280]{2,1,0:T(8,128)(2,1)}, u32[]{:S(2)}, u32[]{:S(2)}) %collective-permute-start.10) | collective-permute-done | bytes 655392 | tf_op jit(solution)/shard_map/ppermute | solution.py:16
  55.7 3.1 %pad_maximum_fusion.1 = bf16[3,2,128,1280]{3,2,1,0:T(8,128)(2,1)} fusion(bf16[1,2,128,1280]{3,2,1,0:T(8,128)(2,1)} %bitcast.12, bf16[1,2,128,1280]{3,2,1,0:T(8,128)(2,1)} %bitcast.11, bf16[1,2,128,1280]{3,2,1,0:T(8,128)(2,1)} %bitcast.10), kind=kLoop, calls=%fused_computation.1 | loop fusion | flops 1966080 | bytes 3932160 | tf_op jit(solution)/shard_map/stack | solution.py:158
  58.8 0.3 collective-permute-start.11
  59.1 0.1 copy.9
  59.2 0.1 multiply_reduce_fusion
  59.3 1.4 fusion.24.mask_ref
  60.7 2.6 %collective-permute-start.12 = (bf16[2,128,1280]{2,1,0:T(8,128)(2,1)}, bf16[2,128,1280]{2,1,0:T(8,128)(2,1)}, u32[]{:S(2)}, u32[]{:S(2)}) collective-permute-start(bf16[2,128,1280]{2,1,0:T(8,128)(2,1)} %collective-permute-done.8.refs_2_), channel_id=1, source_target_pairs={{0,5},{3,6},{4,9},{7,10},{8,13},{11,14},{16,21},{19,22},{20,25},{2... | collective-permute-start | bytes 1966088 | tf_op jit(solution)/shard_map/ppermute | solution.py:16
  63.3 0.0 collective-permute-done.refs_1_
  63.3 1.5 %collective-permute-start.13 = (bf16[2,128,1280]{2,1,0:T(8,128)(2,1)}, bf16[2,128,1280]{2,1,0:T(8,128)(2,1)}, u32[]{:S(2)}, u32[]{:S(2)}) collective-permute-start(bf16[2,128,1280]{2,1,0:T(8,128)(2,1)} %collective-permute-done.8.refs_2_), channel_id=1, source_target_pairs={{4,1},{7,2},{8,5},{11,6},{12,9},{15,10},{20,17},{23,18},{24,21},{2... | collective-permute-start | bytes 1966088 | tf_op jit(solution)/shard_map/ppermute | solution.py:16
  64.8 0.0 collective-permute-done.4.refs_5_
  64.8 14.0 %shard_map.85 = (bf16[128,1280]{1,0:T(8,128)(2,1)}, bf16[2,128,1280]{2,1,0:T(8,128)(2,1)}, bf16[4,2,128,1280]{3,2,1,0:T(8,128)(2,1)}, bf16[2,128,1280]{2,1,0:T(8...) custom-call(s32[128,1280]{1,0:T(8,128)} %fusion.24.mask_ref, ...), custom_call_target="tpu_custom_call" | custom-call | flops 2516582400 | bytes 14745600 | tf_op jit(solution)/shard_map/pallas_call | solution.py:127
  78.8 0.1 collective-permute-start.14
  78.9 0.0 collective-permute-done.13.refs_7_
  78.9 14.1 %shard_map.86 = (bf16[128,1280]{1,0:T(8,128)(2,1)}, bf16[2,128,1280]{2,1,0:T(8,128)(2,1)}, bf16[4,2,128,1280]{3,2,1,0:T(8,128)(2,1)}, bf16[2,128,1280]{2,1,0:T(8...) custom-call(s32[128,1280]{1,0:T(8,128)} %fusion.24.mask_ref, ...), custom_call_target="tpu_custom_call" | custom-call | flops 2516582400 | bytes 14745600 | tf_op jit(solution)/shard_map/pallas_call | solution.py:127
  93.1 0.5 collective-permute-start.20
  93.6 1.3 collective-permute-start.15
  94.9 0.7 collective-permute-start.16
  95.6 1.3 collective-permute-start.21
  96.9 2.0 %pad_maximum_fusion.4 = bf16[128,2560]{1,0:T(8,128)(2,1)} fusion(bf16[128,1280]{1,0:T(8,128)(2,1)} %get-tuple-element.24, bf16[128,1280]{1,0:T(8,128)(2,1)} %get-tuple-element.21), kind=kLoop, calls=%fused_computation.46 | loop fusion | flops 1310720 | bytes 1310720 | tf_op jit(solution)/shard_map/concatenate | solution.py:256
  98.9 6.9 %collective-permute-done.15 = bf16[2,128,1280]{2,1,0:T(8,128)(2,1)S(1)} collective-permute-done((bf16[2,128,1280]{2,1,0:T(8,128)(2,1)}, bf16[2,128,1280]{2,1,0:T(8,128)(2,1)S(1)}, u32[]{:S(2)}, u32[]{:S(2)}) %collective-permute-start.15) | collective-permute-done | bytes 655392 | tf_op jit(solution)/shard_map/ppermute | solution.py:16
  105.7 0.7 collective-permute-start.22
  106.5 0.7 fusion.13
  107.2 4.0 %collective-permute-start.17 = (bf16[2,128,1280]{2,1,0:T(8,128)(2,1)S(1)}, bf16[2,128,1280]{2,1,0:T(8,128)(2,1)S(1)}, u32[]{:S(2)}, u32[]{:S(2)}) collective-permute-start(bf16[2,128,1280]{2,1,0:T(8,128)(2,1)S(1)} %get-tuple-element.39), channel_id=1, source_target_pairs={{0,2},{1,3},{2,0},{3,1},{4,6},{5,7},{6,4},{7,5},{8,10},{9,11},{10,... | collective-permute-start | bytes 1966088 | tf_op jit(solution)/shard_map/ppermute | solution.py:16
  111.3 1.3 collective-permute-start.18
  112.5 0.2 collective-permute-done.21
  112.8 4.4 %collective-permute-start.19 = (bf16[2,128,1280]{2,1,0:T(8,128)(2,1)S(1)}, bf16[2,128,1280]{2,1,0:T(8,128)(2,1)S(1)}, u32[]{:S(2)}, u32[]{:S(2)}) collective-permute-start(bf16[2,128,1280]{2,1,0:T(8,128)(2,1)S(1)} %get-tuple-element.40), channel_id=1, source_target_pairs={{0,4},{1,5},{2,6},{3,7},{4,8},{5,9},{6,10},{7,11},{8,12},{9,13},{1... | collective-permute-start | bytes 1966088 | tf_op jit(solution)/shard_map/ppermute | solution.py:16
  117.2 0.7 fusion.4
  117.9 1.8 %collective-permute-start.23 = (bf16[2,128,1280]{2,1,0:T(8,128)(2,1)S(1)}, bf16[2,128,1280]{2,1,0:T(8,128)(2,1)S(1)}, u32[]{:S(2)}, u32[]{:S(2)}) collective-permute-start(bf16[2,128,1280]{2,1,0:T(8,128)(2,1)S(1)} %get-tuple-element.42), channel_id=1, source_target_pairs={{0,2},{1,3},{2,0},{3,1},{4,6},{5,7},{6,4},{7,5},{8,10},{9,11},{10,... | collective-permute-start | bytes 1966088 | tf_op jit(solution)/shard_map/ppermute | solution.py:16
  119.8 1.3 collective-permute-start.24
  121.0 5.3 %collective-permute-done.17 = bf16[2,128,1280]{2,1,0:T(8,128)(2,1)S(1)} collective-permute-done((bf16[2,128,1280]{2,1,0:T(8,128)(2,1)S(1)}, bf16[2,128,1280]{2,1,0:T(8,128)(2,1)S(1)}, u32[]{:S(2)}, u32[]{:S(2)}) %collective-permute-start.17) | collective-permute-done | bytes 655392 | tf_op jit(solution)/shard_map/ppermute | solution.py:16
  126.4 3.4 %collective-permute-start.25 = (bf16[2,128,1280]{2,1,0:T(8,128)(2,1)S(1)}, bf16[2,128,1280]{2,1,0:T(8,128)(2,1)S(1)}, u32[]{:S(2)}, u32[]{:S(2)}) collective-permute-start(bf16[2,128,1280]{2,1,0:T(8,128)(2,1)S(1)} %get-tuple-element.43), channel_id=1, source_target_pairs={{0,4},{1,5},{2,6},{3,7},{4,8},{5,9},{6,10},{7,11},{8,12},{9,13},{1... | collective-permute-start | bytes 1966088 | tf_op jit(solution)/shard_map/ppermute | solution.py:16
  129.8 0.9 collective-permute-done.18
  130.7 1.5 collective-permute-done.19
  132.2 0.4 fusion.17
  132.7 7.4 %collective-permute-done.23 = bf16[2,128,1280]{2,1,0:T(8,128)(2,1)S(1)} collective-permute-done((bf16[2,128,1280]{2,1,0:T(8,128)(2,1)S(1)}, bf16[2,128,1280]{2,1,0:T(8,128)(2,1)S(1)}, u32[]{:S(2)}, u32[]{:S(2)}) %collective-permute-start.23) | collective-permute-done | bytes 655392 | tf_op jit(solution)/shard_map/ppermute | solution.py:16
  140.1 3.6 %collective-permute-done.24 = bf16[2,128,1280]{2,1,0:T(8,128)(2,1)S(1)} collective-permute-done((bf16[2,128,1280]{2,1,0:T(8,128)(2,1)S(1)}, bf16[2,128,1280]{2,1,0:T(8,128)(2,1)S(1)}, u32[]{:S(2)}, u32[]{:S(2)}) %collective-permute-start.24) | collective-permute-done | bytes 655392 | tf_op jit(solution)/shard_map/ppermute | solution.py:16
  143.6 2.2 %collective-permute-done.25 = bf16[2,128,1280]{2,1,0:T(8,128)(2,1)S(1)} collective-permute-done((bf16[2,128,1280]{2,1,0:T(8,128)(2,1)S(1)}, bf16[2,128,1280]{2,1,0:T(8,128)(2,1)S(1)}, u32[]{:S(2)}, u32[]{:S(2)}) %collective-permute-start.25) | collective-permute-done | bytes 655392 | tf_op jit(solution)/shard_map/ppermute | solution.py:16
  145.8 0.4 fusion.8
  146.3 0.9 pad_maximum_fusion.6
  147.2 0.9 pad_maximum_fusion.5
  (55 shorter events, 0.3 us)
Async XLA Ops:
  2.0 21.1 %copy-start.14 = (s32[4]{0:T(128)S(1)}, s32[4]{0:T(128)}, u32[]{:S(2)}) copy-start(s32[4]{0:T(128)} %param.11) | copy-start | bytes 52
  2.1 39.0 %copy-start.6 = (bf16[2,128,1280]{2,1,0:T(8,128)(2,1)}, bf16[2,128,1280]{2,1,0:T(8,128)(2,1)S(1)}, u32[]{:S(2)}) copy-start(bf16[2,128,1280]{2,1,0:T(8,128)(2,1)S(1)} %pad_maximum_fusion.2.refs_0_) | copy-start | bytes 1966084
  2.1 17.8 %collective-permute-start.1 = (bf16[2,128,1280]{2,1,0:T(8,128)(2,1)S(1)}, bf16[2,128,1280]{2,1,0:T(8,128)(2,1)S(1)}, u32[]{:S(2)}, u32[]{:S(2)}) collective-permute-start(bf16[2,128,1280]{2,1,0:T(8,128)(2,1)S(1)} %pad_maximum_fusion.2.refs_0_), channel_id=1, source_target_pairs={{0,2},{1,3},{2,0},{3,1},{4,6},{5,7},{6,4},{7,5},{8,10},{9,11},{10,... | collective-permute-start | bytes 1966088 | tf_op jit(solution)/shard_map/ppermute | solution.py:16
  5.1 32.8 %collective-permute-start.2 = (bf16[2,128,1280]{2,1,0:T(8,128)(2,1)S(1)}, bf16[2,128,1280]{2,1,0:T(8,128)(2,1)}, u32[]{:S(2)}, u32[]{:S(2)}) collective-permute-start(bf16[2,128,1280]{2,1,0:T(8,128)(2,1)S(1)} %pad_maximum_fusion.2.refs_0_), channel_id=1, source_target_pairs={{0,4},{1,5},{2,6},{3,7},{4,8},{5,9},{6,10},{7,11},{8,12},{9,13},{1... | collective-permute-start | bytes 1966088 | tf_op jit(solution)/shard_map/ppermute | solution.py:16
  9.5 29.9 %collective-permute-start.3 = (bf16[2,128,1280]{2,1,0:T(8,128)(2,1)S(1)}, bf16[2,128,1280]{2,1,0:T(8,128)(2,1)}, u32[]{:S(2)}, u32[]{:S(2)}) collective-permute-start(bf16[2,128,1280]{2,1,0:T(8,128)(2,1)S(1)} %pad_maximum_fusion.2.refs_0_), channel_id=1, source_target_pairs={{4,0},{5,1},{6,2},{7,3},{8,4},{9,5},{10,6},{11,7},{12,8},{13,9},{1... | collective-permute-start | bytes 1966088 | tf_op jit(solution)/shard_map/ppermute | solution.py:16
  19.9 19.5 %copy-start.8 = (bf16[2,128,1280]{2,1,0:T(8,128)(2,1)}, bf16[2,128,1280]{2,1,0:T(8,128)(2,1)S(1)}, u32[]{:S(2)}) copy-start(bf16[2,128,1280]{2,1,0:T(8,128)(2,1)S(1)} %collective-permute-done.1.refs_2_) | copy-start | bytes 1966084
  19.9 10.5 %collective-permute-start.5 = (bf16[2,128,1280]{2,1,0:T(8,128)(2,1)S(1)}, bf16[2,128,1280]{2,1,0:T(8,128)(2,1)S(1)}, u32[]{:S(2)}, u32[]{:S(2)}) collective-permute-start(bf16[2,128,1280]{2,1,0:T(8,128)(2,1)S(1)} %collective-permute-done.1.refs_2_), channel_id=1, source_target_pairs={{0,5},{3,6},{4,9},{7,10},{8,13},{11,14},{16,21},{19,22},{20,25},{2... | collective-permute-start | bytes 1966088 | tf_op jit(solution)/shard_map/ppermute | solution.py:16
  22.3 8.1 %collective-permute-start.6 = (bf16[2,128,1280]{2,1,0:T(8,128)(2,1)S(1)}, bf16[2,128,1280]{2,1,0:T(8,128)(2,1)S(1)}, u32[]{:S(2)}, u32[]{:S(2)}) collective-permute-start(bf16[2,128,1280]{2,1,0:T(8,128)(2,1)S(1)} %collective-permute-done.1.refs_2_), channel_id=1, source_target_pairs={{4,1},{7,2},{8,5},{11,6},{12,9},{15,10},{20,17},{23,18},{24,21},{2... | collective-permute-start | bytes 1966088 | tf_op jit(solution)/shard_map/ppermute | solution.py:16
  23.2 18.0 %copy-start.7 = (bf16[2,128,1280]{2,1,0:T(8,128)(2,1)}, bf16[2,128,1280]{2,1,0:T(8,128)(2,1)S(1)}, u32[]{:S(2)}) copy-start(bf16[2,128,1280]{2,1,0:T(8,128)(2,1)S(1)} %pad_maximum_fusion.3.refs_0_) | copy-start | bytes 1966084
  23.2 18.0 %collective-permute-start.8 = (bf16[2,128,1280]{2,1,0:T(8,128)(2,1)S(1)}, bf16[2,128,1280]{2,1,0:T(8,128)(2,1)}, u32[]{:S(2)}, u32[]{:S(2)}) collective-permute-start(bf16[2,128,1280]{2,1,0:T(8,128)(2,1)S(1)} %pad_maximum_fusion.3.refs_0_), channel_id=1, source_target_pairs={{0,2},{1,3},{2,0},{3,1},{4,6},{5,7},{6,4},{7,5},{8,10},{9,11},{10,... | collective-permute-start | bytes 1966088 | tf_op jit(solution)/shard_map/ppermute | solution.py:16
  30.4 9.0 %copy-start.12 = (bf16[2,128,1280]{2,1,0:T(8,128)(2,1)}, bf16[2,128,1280]{2,1,0:T(8,128)(2,1)S(1)}, u32[]{:S(2)}) copy-start(bf16[2,128,1280]{2,1,0:T(8,128)(2,1)S(1)} %collective-permute-done.5.refs_6_) | copy-start | bytes 1966084
  30.4 6.2 %copy-start.13 = (bf16[2,128,1280]{2,1,0:T(8,128)(2,1)}, bf16[2,128,1280]{2,1,0:T(8,128)(2,1)S(1)}, u32[]{:S(2)}) copy-start(bf16[2,128,1280]{2,1,0:T(8,128)(2,1)S(1)} %collective-permute-done.6.refs_7_) | copy-start | bytes 1966084
  30.4 19.8 %collective-permute-start.9 = (bf16[2,128,1280]{2,1,0:T(8,128)(2,1)S(1)}, bf16[2,128,1280]{2,1,0:T(8,128)(2,1)}, u32[]{:S(2)}, u32[]{:S(2)}) collective-permute-start(bf16[2,128,1280]{2,1,0:T(8,128)(2,1)S(1)} %pad_maximum_fusion.3.refs_0_), channel_id=1, source_target_pairs={{0,4},{1,5},{2,6},{3,7},{4,8},{5,9},{6,10},{7,11},{8,12},{9,13},{1... | collective-permute-start | bytes 1966088 | tf_op jit(solution)/shard_map/ppermute | solution.py:16
  36.6 19.2 %collective-permute-start.10 = (bf16[2,128,1280]{2,1,0:T(8,128)(2,1)S(1)}, bf16[2,128,1280]{2,1,0:T(8,128)(2,1)}, u32[]{:S(2)}, u32[]{:S(2)}) collective-permute-start(bf16[2,128,1280]{2,1,0:T(8,128)(2,1)S(1)} %pad_maximum_fusion.3.refs_0_), channel_id=1, source_target_pairs={{4,0},{5,1},{6,2},{7,3},{8,4},{9,5},{10,6},{11,7},{12,8},{13,9},{1... | collective-permute-start | bytes 1966088 | tf_op jit(solution)/shard_map/ppermute | solution.py:16
  37.9 25.4 %collective-permute-start = (bf16[2,128,1280]{2,1,0:T(8,128)(2,1)S(1)}, bf16[2,128,1280]{2,1,0:T(8,128)(2,1)}, u32[]{:S(2)}, u32[]{:S(2)}) collective-permute-start(bf16[2,128,1280]{2,1,0:T(8,128)(2,1)S(1)} %pad_maximum_fusion.2.refs_0_), channel_id=1, source_target_pairs={{0,1},{1,0},{2,3},{3,2},{4,5},{5,4},{6,7},{7,6},{8,9},{9,8},{10,11... | collective-permute-start | bytes 1966088 | tf_op jit(solution)/shard_map/ppermute | solution.py:16
  41.1 23.7 %collective-permute-start.4 = (bf16[3,2,128,1280]{3,2,1,0:T(8,128)(2,1)S(1)}, bf16[3,2,128,1280]{3,2,1,0:T(8,128)(2,1)}, u32[]{:S(2)}, u32[]{:S(2)}) collective-permute-start(bf16[3,2,128,1280]{3,2,1,0:T(8,128)(2,1)S(1)} %pad_maximum_fusion), channel_id=1, source_target_pairs={{0,1},{1,0},{2,3},{3,2},{4,5},{5,4},{6,7},{7,6},{8,9},{9,8},{10,11... | collective-permute-start | bytes 5898248 | tf_op jit(solution)/shard_map/ppermute | solution.py:16
  41.2 37.6 %collective-permute-start.7 = (bf16[2,128,1280]{2,1,0:T(8,128)(2,1)S(1)}, bf16[2,128,1280]{2,1,0:T(8,128)(2,1)}, u32[]{:S(2)}, u32[]{:S(2)}) collective-permute-start(bf16[2,128,1280]{2,1,0:T(8,128)(2,1)S(1)} %pad_maximum_fusion.3.refs_0_), channel_id=1, source_target_pairs={{0,1},{1,0},{2,3},{3,2},{4,5},{5,4},{6,7},{7,6},{8,9},{9,8},{10,11... | collective-permute-start | bytes 1966088 | tf_op jit(solution)/shard_map/ppermute | solution.py:16
  55.7 3.3 %copy-start.11 = (s32[4,3]{1,0:T(4,128)S(1)}, s32[4,3]{1,0:T(4,128)}, u32[]{:S(2)}) copy-start(s32[4,3]{1,0:T(4,128)} %param.10) | copy-start | bytes 148
  58.8 20.1 %collective-permute-start.11 = (bf16[3,2,128,1280]{3,2,1,0:T(8,128)(2,1)}, bf16[3,2,128,1280]{3,2,1,0:T(8,128)(2,1)}, u32[]{:S(2)}, u32[]{:S(2)}) collective-permute-start(bf16[3,2,128,1280]{3,2,1,0:T(8,128)(2,1)} %pad_maximum_fusion.1), channel_id=1, source_target_pairs={{0,1},{1,0},{2,3},{3,2},{4,5},{5,4},{6,7},{7,6},{8,9},{9,8},{10,11... | collective-permute-start | bytes 5898248 | tf_op jit(solution)/shard_map/ppermute | solution.py:16
  60.7 18.2 %collective-permute-start.12 = (bf16[2,128,1280]{2,1,0:T(8,128)(2,1)}, bf16[2,128,1280]{2,1,0:T(8,128)(2,1)}, u32[]{:S(2)}, u32[]{:S(2)}) collective-permute-start(bf16[2,128,1280]{2,1,0:T(8,128)(2,1)} %collective-permute-done.8.refs_2_), channel_id=1, source_target_pairs={{0,5},{3,6},{4,9},{7,10},{8,13},{11,14},{16,21},{19,22},{20,25},{2... | collective-permute-start | bytes 1966088 | tf_op jit(solution)/shard_map/ppermute | solution.py:16
  63.3 15.6 %collective-permute-start.13 = (bf16[2,128,1280]{2,1,0:T(8,128)(2,1)}, bf16[2,128,1280]{2,1,0:T(8,128)(2,1)}, u32[]{:S(2)}, u32[]{:S(2)}) collective-permute-start(bf16[2,128,1280]{2,1,0:T(8,128)(2,1)} %collective-permute-done.8.refs_2_), channel_id=1, source_target_pairs={{4,1},{7,2},{8,5},{11,6},{12,9},{15,10},{20,17},{23,18},{24,21},{2... | collective-permute-start | bytes 1966088 | tf_op jit(solution)/shard_map/ppermute | solution.py:16
  78.8 27.7 %collective-permute-start.14 = (bf16[4,2,128,1280]{3,2,1,0:T(8,128)(2,1)}, bf16[4,2,128,1280]{3,2,1,0:T(8,128)(2,1)S(1)}, u32[]{:S(2)}, u32[]{:S(2)}) collective-permute-start(bf16[4,2,128,1280]{3,2,1,0:T(8,128)(2,1)} %get-tuple-element.26), channel_id=1, source_target_pairs={{0,1},{1,0},{2,3},{3,2},{4,5},{5,4},{6,7},{7,6},{8,9},{9,8},{10,11... | collective-permute-start | bytes 7864328 | tf_op jit(solution)/shard_map/ppermute | solution.py:16
  78.9 27.5 %copy-start.2 = (bf16[2,128,1280]{2,1,0:T(8,128)(2,1)S(1)}, bf16[2,128,1280]{2,1,0:T(8,128)(2,1)}, u32[]{:S(2)}) copy-start(bf16[2,128,1280]{2,1,0:T(8,128)(2,1)} %get-tuple-element.31) | copy-start | bytes 1966084
  93.1 13.4 %copy-start = (bf16[2,128,1280]{2,1,0:T(8,128)(2,1)S(1)}, bf16[2,128,1280]{2,1,0:T(8,128)(2,1)}, u32[]{:S(2)}) copy-start(bf16[2,128,1280]{2,1,0:T(8,128)(2,1)} %get-tuple-element.27) | copy-start | bytes 1966084
  93.1 13.4 %copy-start.1 = (bf16[2,128,1280]{2,1,0:T(8,128)(2,1)S(1)}, bf16[2,128,1280]{2,1,0:T(8,128)(2,1)}, u32[]{:S(2)}) copy-start(bf16[2,128,1280]{2,1,0:T(8,128)(2,1)} %get-tuple-element.30) | copy-start | bytes 1966084
  93.1 24.1 %collective-permute-start.20 = (bf16[4,2,128,1280]{3,2,1,0:T(8,128)(2,1)}, bf16[4,2,128,1280]{3,2,1,0:T(8,128)(2,1)S(1)}, u32[]{:S(2)}, u32[]{:S(2)}) collective-permute-start(bf16[4,2,128,1280]{3,2,1,0:T(8,128)(2,1)} %get-tuple-element.33), channel_id=1, source_target_pairs={{0,1},{1,0},{2,3},{3,2},{4,5},{5,4},{6,7},{7,6},{8,9},{9,8},{10,11... | collective-permute-start | bytes 7864328 | tf_op jit(solution)/shard_map/ppermute | solution.py:16
  93.6 12.1 %collective-permute-start.15 = (bf16[2,128,1280]{2,1,0:T(8,128)(2,1)}, bf16[2,128,1280]{2,1,0:T(8,128)(2,1)S(1)}, u32[]{:S(2)}, u32[]{:S(2)}) collective-permute-start(bf16[2,128,1280]{2,1,0:T(8,128)(2,1)} %get-tuple-element.28), channel_id=1, source_target_pairs={{5,0},{6,3},{9,4},{10,7},{13,8},{14,11},{21,16},{22,19},{25,20},{2... | collective-permute-start | bytes 1966088 | tf_op jit(solution)/shard_map/ppermute | solution.py:16
  94.9 11.5 %collective-permute-start.16 = (bf16[2,128,1280]{2,1,0:T(8,128)(2,1)}, bf16[2,128,1280]{2,1,0:T(8,128)(2,1)S(1)}, u32[]{:S(2)}, u32[]{:S(2)}) collective-permute-start(bf16[2,128,1280]{2,1,0:T(8,128)(2,1)} %get-tuple-element.29), channel_id=1, source_target_pairs={{1,4},{2,7},{5,8},{6,11},{9,12},{10,15},{17,20},{18,23},{21,24},{2... | collective-permute-start | bytes 1966088 | tf_op jit(solution)/shard_map/ppermute | solution.py:16
  95.6 17.1 %collective-permute-start.21 = (bf16[2,128,1280]{2,1,0:T(8,128)(2,1)}, bf16[2,128,1280]{2,1,0:T(8,128)(2,1)S(1)}, u32[]{:S(2)}, u32[]{:S(2)}) collective-permute-start(bf16[2,128,1280]{2,1,0:T(8,128)(2,1)} %get-tuple-element.35), channel_id=1, source_target_pairs={{5,0},{6,3},{9,4},{10,7},{13,8},{14,11},{21,16},{22,19},{25,20},{2... | collective-permute-start | bytes 1966088 | tf_op jit(solution)/shard_map/ppermute | solution.py:16
  105.7 11.4 %collective-permute-start.22 = (bf16[2,128,1280]{2,1,0:T(8,128)(2,1)}, bf16[2,128,1280]{2,1,0:T(8,128)(2,1)S(1)}, u32[]{:S(2)}, u32[]{:S(2)}) collective-permute-start(bf16[2,128,1280]{2,1,0:T(8,128)(2,1)} %get-tuple-element.36), channel_id=1, source_target_pairs={{1,4},{2,7},{5,8},{6,11},{9,12},{10,15},{17,20},{18,23},{21,24},{2... | collective-permute-start | bytes 1966088 | tf_op jit(solution)/shard_map/ppermute | solution.py:16
  106.5 10.7 %copy-start.3 = (bf16[2,128,1280]{2,1,0:T(8,128)(2,1)S(1)}, bf16[2,128,1280]{2,1,0:T(8,128)(2,1)}, u32[]{:S(2)}) copy-start(bf16[2,128,1280]{2,1,0:T(8,128)(2,1)} %get-tuple-element.34) | copy-start | bytes 1966084
  106.5 10.7 %copy-start.4 = (bf16[2,128,1280]{2,1,0:T(8,128)(2,1)S(1)}, bf16[2,128,1280]{2,1,0:T(8,128)(2,1)}, u32[]{:S(2)}) copy-start(bf16[2,128,1280]{2,1,0:T(8,128)(2,1)} %get-tuple-element.37) | copy-start | bytes 1966084
  106.5 10.7 %copy-start.5 = (bf16[2,128,1280]{2,1,0:T(8,128)(2,1)S(1)}, bf16[2,128,1280]{2,1,0:T(8,128)(2,1)}, u32[]{:S(2)}) copy-start(bf16[2,128,1280]{2,1,0:T(8,128)(2,1)} %get-tuple-element.38) | copy-start | bytes 1966084
  107.2 19.1 %collective-permute-start.17 = (bf16[2,128,1280]{2,1,0:T(8,128)(2,1)S(1)}, bf16[2,128,1280]{2,1,0:T(8,128)(2,1)S(1)}, u32[]{:S(2)}, u32[]{:S(2)}) collective-permute-start(bf16[2,128,1280]{2,1,0:T(8,128)(2,1)S(1)} %get-tuple-element.39), channel_id=1, source_target_pairs={{0,2},{1,3},{2,0},{3,1},{4,6},{5,7},{6,4},{7,5},{8,10},{9,11},{10,... | collective-permute-start | bytes 1966088 | tf_op jit(solution)/shard_map/ppermute | solution.py:16
  111.3 19.5 %collective-permute-start.18 = (bf16[2,128,1280]{2,1,0:T(8,128)(2,1)S(1)}, bf16[2,128,1280]{2,1,0:T(8,128)(2,1)S(1)}, u32[]{:S(2)}, u32[]{:S(2)}) collective-permute-start(bf16[2,128,1280]{2,1,0:T(8,128)(2,1)S(1)} %get-tuple-element.41), channel_id=1, source_target_pairs={{4,0},{5,1},{6,2},{7,3},{8,4},{9,5},{10,6},{11,7},{12,8},{13,9},{1... | collective-permute-start | bytes 1966088 | tf_op jit(solution)/shard_map/ppermute | solution.py:16
  112.8 19.4 %collective-permute-start.19 = (bf16[2,128,1280]{2,1,0:T(8,128)(2,1)S(1)}, bf16[2,128,1280]{2,1,0:T(8,128)(2,1)S(1)}, u32[]{:S(2)}, u32[]{:S(2)}) collective-permute-start(bf16[2,128,1280]{2,1,0:T(8,128)(2,1)S(1)} %get-tuple-element.40), channel_id=1, source_target_pairs={{0,4},{1,5},{2,6},{3,7},{4,8},{5,9},{6,10},{7,11},{8,12},{9,13},{1... | collective-permute-start | bytes 1966088 | tf_op jit(solution)/shard_map/ppermute | solution.py:16
  117.2 15.0 %copy-start.9 = (bf16[2,128,1280]{2,1,0:T(8,128)(2,1)S(1)}, bf16[2,128,1280]{2,1,0:T(8,128)(2,1)}, u32[]{:S(2)}) copy-start(bf16[2,128,1280]{2,1,0:T(8,128)(2,1)} %get-tuple-element.25) | copy-start | bytes 1966084
  117.9 22.2 %collective-permute-start.23 = (bf16[2,128,1280]{2,1,0:T(8,128)(2,1)S(1)}, bf16[2,128,1280]{2,1,0:T(8,128)(2,1)S(1)}, u32[]{:S(2)}, u32[]{:S(2)}) collective-permute-start(bf16[2,128,1280]{2,1,0:T(8,128)(2,1)S(1)} %get-tuple-element.42), channel_id=1, source_target_pairs={{0,2},{1,3},{2,0},{3,1},{4,6},{5,7},{6,4},{7,5},{8,10},{9,11},{10,... | collective-permute-start | bytes 1966088 | tf_op jit(solution)/shard_map/ppermute | solution.py:16
  119.8 23.9 %collective-permute-start.24 = (bf16[2,128,1280]{2,1,0:T(8,128)(2,1)S(1)}, bf16[2,128,1280]{2,1,0:T(8,128)(2,1)S(1)}, u32[]{:S(2)}, u32[]{:S(2)}) collective-permute-start(bf16[2,128,1280]{2,1,0:T(8,128)(2,1)S(1)} %get-tuple-element.44), channel_id=1, source_target_pairs={{4,0},{5,1},{6,2},{7,3},{8,4},{9,5},{10,6},{11,7},{12,8},{13,9},{1... | collective-permute-start | bytes 1966088 | tf_op jit(solution)/shard_map/ppermute | solution.py:16
  126.4 19.4 %collective-permute-start.25 = (bf16[2,128,1280]{2,1,0:T(8,128)(2,1)S(1)}, bf16[2,128,1280]{2,1,0:T(8,128)(2,1)S(1)}, u32[]{:S(2)}, u32[]{:S(2)}) collective-permute-start(bf16[2,128,1280]{2,1,0:T(8,128)(2,1)S(1)} %get-tuple-element.43), channel_id=1, source_target_pairs={{0,4},{1,5},{2,6},{3,7},{4,8},{5,9},{6,10},{7,11},{8,12},{9,13},{1... | collective-permute-start | bytes 1966088 | tf_op jit(solution)/shard_map/ppermute | solution.py:16
  132.6 13.2 %copy-start.10 = (bf16[2,128,1280]{2,1,0:T(8,128)(2,1)S(1)}, bf16[2,128,1280]{2,1,0:T(8,128)(2,1)}, u32[]{:S(2)}) copy-start(bf16[2,128,1280]{2,1,0:T(8,128)(2,1)} %get-tuple-element.32) | copy-start | bytes 1966084

commit v9 on v7

--- a/solution.py
+++ b/solution.py
@@ -73,9 +73,8 @@
     return inside & (kept_pair > 0) & nearby
 
 
-def attention_backward(mask, queries, out_grad, inputs, slot_in, out_lead, slot_out, inv_root, offset):
-    rows, channels = inputs[0].shape[-2:]
-    heads = channels // HD
+def attention_backward(mask, queries, out_grad, inputs, slot_in, out_lead, slot_out, inv_root, offset, heads):
+    rows, channels = queries.shape[0], heads * HD
     slots = len(slot_in)
     n_in = len(inputs)
 
@@ -111,15 +110,15 @@
                 out_refs[i][lead + (0, slice(None), cols)] = dk[part].astype(jnp.bfloat16)
                 out_refs[i][lead + (1, slice(None), cols)] = dv[part].astype(jnp.bfloat16)
 
-    def head_spec(lead_shape):
+    def head_spec(lead_shape, shift=0):
         zeros = (0,) * len(lead_shape)
-        return pl.BlockSpec(lead_shape + (2, rows, STEP_HEADS * HD), lambda h: zeros + (0, 0, h))
+        return pl.BlockSpec(lead_shape + (2, rows, STEP_HEADS * HD), lambda h: zeros + (0, 0, h + shift))
 
     in_specs = [
         pl.BlockSpec((rows, slots * rows), lambda h: (0, 0)),
         pl.BlockSpec((rows, STEP_HEADS * HD), lambda h: (0, h + offset // STEP_HEADS)),
         pl.BlockSpec((rows, STEP_HEADS * HD), lambda h: (0, h + offset // STEP_HEADS)),
-    ] + [head_spec(tuple(x.shape[:-3])) for x in inputs]
+    ] + [head_spec(tuple(x.shape[:-3]), offset // STEP_HEADS) for x in inputs]
     out_specs = [pl.BlockSpec((rows, STEP_HEADS * HD), lambda h: (0, h))] + [head_spec(lead) for lead in out_lead]
     out_shape = [jax.ShapeDtypeStruct((rows, channels), jnp.bfloat16)] + [
         jax.ShapeDtypeStruct(lead + (2, rows, channels), jnp.bfloat16) for lead in out_lead
@@ -162,12 +161,12 @@
     return first + [relayed, diag_from_below, diag_from_above]
 
 
-def chunk_kernel(forward_mask, queries, out_grad, inputs, head_offset, inv_root):
+def chunk_kernel(forward_mask, queries, out_grad, inputs, head_offset, inv_root, heads):
     slot_in = [(0, ()), (1, ()), (2, ()), (3, ()), (4, ()), (5, (0,)), (5, (1,)), (5, (2,)), (6, ()), (7, ())]
     out_lead = [(), (4,), (), (), (), (), ()]
     slot_out = [(0, ()), (1, (0,)), (2, ()), (3, ()), (4, ()), (1, (1,)), (1, (2,)), (1, (3,)), (5, ()), (6, ())]
     return attention_backward(
-        forward_mask, queries, out_grad, inputs, slot_in, out_lead, slot_out, inv_root, head_offset
+        forward_mask, queries, out_grad, inputs, slot_in, out_lead, slot_out, inv_root, head_offset, heads
     )
 
 
@@ -234,14 +233,11 @@
     chunk_heads = heads // CHUNKS if heads % CHUNKS == 0 else heads
     width = chunk_heads * HD
     starts = list(range(0, channel_total, width))
-    firsts, seconds, outs, backs, sums, dqs = [], [], [], [], [], []
+    outs, backs, sums, dqs = [], [], [], []
+    own = jnp.stack([keys, values])
+    received = forward_second(forward_relay(own, count, None), count, None)
     for c, first in enumerate(starts):
-        own = jnp.stack([keys[:, first : first + width], values[:, first : first + width]])
-        firsts.append(forward_relay(own, count, None))
-    for c in range(len(starts)):
-        seconds.append(forward_second(firsts[c], count, None))
-    for c, first in enumerate(starts):
-        dq, parts = chunk_kernel(forward_mask, queries, out_grad, seconds[c], first // HD, inv_root)
+        dq, parts = chunk_kernel(forward_mask, queries, out_grad, received, first // HD, inv_root, chunk_heads)
         dqs.append(dq)
         outs.append(parts)
     for c in range(len(starts)):

time: 146 us -> 147 us (level)
  waiting for transfers between devices: 54.5 us -> 73.1 us
  starting transfers between devices: 47.2 us -> 32.8 us
    ppermute x26 -> x19, waiting for transfers between devices: 54.5 us -> 73.1 us  [send(): return lax.ppermute(value, 'tm', pairs)]
    ppermute x26 -> x19, starting transfers between devices: 47.2 us -> 32.8 us  [send(): return lax.ppermute(value, 'tm', pairs)]
    another operation x2 -> x1, other arithmetic: 4.72 us -> 2.29 us  [forward_second(): ahead = jnp.stack([from_cross, from_below, from_above])]
  transfers between devices with their start and end apart: 26 -> 19, of which waited for: 15 -> 13; matrix products, arithmetic and copies ran while one was open for 7% -> 4% of each run, Pallas kernels for 19% -> 10%
where the time goes in v9:
time: 147 us
  waiting for transfers between devices  73.1 us (50%)
  starting transfers between devices  32.8 us (22%)
  Pallas kernels  28.1 us (19%)
  other arithmetic  11.3 us (8%)
    ppermute x19, waiting for transfers between devices, send(): return lax.ppermute(value, 'tm', pairs)  73.1 us
    ppermute x19, starting transfers between devices, send(): return lax.ppermute(value, 'tm', pairs)  32.8 us
    pallas_call x2, Pallas kernels, attention_backward(): pl.pallas_call(kernel, grid=(heads // STEP_HEADS,), in_specs=in_specs, ou...  28.1 us
  transfers between devices with their start and end apart: 19, of which 13 were waited for; matrix products, arithmetic and copies ran while one was open for 4% of the time, Pallas kernels for 10%

profile of v9, /device:TPU:0, one launch (start us, length us, event | category | flops | bytes accessed | tf_op | source)
XLA Modules:
  0.0 146.6 jit_solution(11436532921355913644)
XLA Ops:
  0.6 1.4 pad_maximum_fusion.1.refs_0_
  2.0 0.0 copy-start
  2.0 3.1 %collective-permute-start.1 = (bf16[2,128,2560]{2,1,0:T(8,128)(2,1)S(1)}, bf16[2,128,2560]{2,1,0:T(8,128)(2,1)S(1)}, u32[]{:S(2)}, u32[]{:S(2)}) collective-permute-start(bf16[2,128,2560]{2,1,0:T(8,128)(2,1)S(1)} %pad_maximum_fusion.1.refs_0_), channel_id=1, source_target_pairs={{0,2},{1,3},{2,0},{3,1},{4,6},{5,7},{6,4},{7,5},{8,10},{9,11},{10,... | collective-permute-start | bytes 3932168 | tf_op jit(solution)/shard_map/ppermute | solution.py:16
  5.1 3.6 %collective-permute-start.2 = (bf16[2,128,2560]{2,1,0:T(8,128)(2,1)S(1)}, bf16[2,128,2560]{2,1,0:T(8,128)(2,1)S(1)}, u32[]{:S(2)}, u32[]{:S(2)}) collective-permute-start(bf16[2,128,2560]{2,1,0:T(8,128)(2,1)S(1)} %pad_maximum_fusion.1.refs_0_), channel_id=1, source_target_pairs={{0,4},{1,5},{2,6},{3,7},{4,8},{5,9},{6,10},{7,11},{8,12},{9,13},{1... | collective-permute-start | bytes 3932168 | tf_op jit(solution)/shard_map/ppermute | solution.py:16
  8.7 1.3 collective-permute-start.3
  10.0 23.9 %collective-permute-done.1.refs_2_ = bf16[2,128,2560]{2,1,0:T(8,128)(2,1)S(1)} collective-permute-done((bf16[2,128,2560]{2,1,0:T(8,128)(2,1)S(1)}, bf16[2,128,2560]{2,1,0:T(8,128)(2,1)S(1)}, u32[]{:S(2)}, u32[]{:S(2)}) %collective-permute-start.1) | collective-permute-done | bytes 1310752 | tf_op jit(solution)/shard_map/ppermute | solution.py:16
  33.9 2.4 %collective-permute-done.2.refs_3_ = bf16[2,128,2560]{2,1,0:T(8,128)(2,1)S(1)} collective-permute-done((bf16[2,128,2560]{2,1,0:T(8,128)(2,1)S(1)}, bf16[2,128,2560]{2,1,0:T(8,128)(2,1)S(1)}, u32[]{:S(2)}, u32[]{:S(2)}) %collective-permute-start.2) | collective-permute-done | bytes 1310752 | tf_op jit(solution)/shard_map/ppermute | solution.py:16
  36.3 4.2 %collective-permute-done.3.refs_4_ = bf16[2,128,2560]{2,1,0:T(8,128)(2,1)S(1)} collective-permute-done((bf16[2,128,2560]{2,1,0:T(8,128)(2,1)S(1)}, bf16[2,128,2560]{2,1,0:T(8,128)(2,1)S(1)}, u32[]{:S(2)}, u32[]{:S(2)}) %collective-permute-start.3) | collective-permute-done | bytes 1310752 | tf_op jit(solution)/shard_map/ppermute | solution.py:16
  40.5 2.3 %pad_maximum_fusion = bf16[3,2,128,2560]{3,2,1,0:T(8,128)(2,1)} fusion(bf16[1,2,128,2560]{3,2,1,0:T(8,128)(2,1)S(1)} %bitcast.61, bf16[1,2,128,2560]{3,2,1,0:T(8,128)(2,1)S(1)} %bitcast.60, bf16[1,2,128,2560]{3,2,1,0:T(8,128)(2,1)S(1)} %bitcast.59), kind=kLoop, calls=%fused_computation | loop fusion | flops 3932160 | bytes 7864320 | tf_op jit(solution)/shard_map/stack | solution.py:155
  42.8 0.0 copy-done.3
  42.8 0.0 collective-permute-start.4
  42.8 0.5 collective-permute-start
  43.5 0.1 select_reduce_fusion
  43.6 4.1 %collective-permute-start.5 = (bf16[2,128,2560]{2,1,0:T(8,128)(2,1)S(1)}, bf16[2,128,2560]{2,1,0:T(8,128)(2,1)}, u32[]{:S(2)}, u32[]{:S(2)}) collective-permute-start(bf16[2,128,2560]{2,1,0:T(8,128)(2,1)S(1)} %collective-permute-done.1.refs_2_), channel_id=1, source_target_pairs={{0,5},{3,6},{4,9},{7,10},{8,13},{11,14},{16,21},{19,22},{20,25},{2... | collective-permute-start | bytes 3932168 | tf_op jit(solution)/shard_map/ppermute | solution.py:16
  47.7 1.7 %collective-permute-start.6 = (bf16[2,128,2560]{2,1,0:T(8,128)(2,1)S(1)}, bf16[2,128,2560]{2,1,0:T(8,128)(2,1)}, u32[]{:S(2)}, u32[]{:S(2)}) collective-permute-start(bf16[2,128,2560]{2,1,0:T(8,128)(2,1)S(1)} %collective-permute-done.1.refs_2_), channel_id=1, source_target_pairs={{4,1},{7,2},{8,5},{11,6},{12,9},{15,10},{20,17},{23,18},{24,21},{2... | collective-permute-start | bytes 3932168 | tf_op jit(solution)/shard_map/ppermute | solution.py:16
  49.5 0.1 copy.9
  49.6 0.1 multiply_reduce_fusion
  49.7 1.4 fusion.24.mask_ref
  51.1 0.7 collective-permute-done.refs_1_
  51.8 9.9 %collective-permute-done.5.refs_6_ = bf16[2,128,2560]{2,1,0:T(8,128)(2,1)} collective-permute-done((bf16[2,128,2560]{2,1,0:T(8,128)(2,1)S(1)}, bf16[2,128,2560]{2,1,0:T(8,128)(2,1)}, u32[]{:S(2)}, u32[]{:S(2)}) %collective-permute-start.5) | collective-permute-done | bytes 1310752 | tf_op jit(solution)/shard_map/ppermute | solution.py:16
  61.8 0.0 collective-permute-done.6.refs_7_
  61.8 0.0 collective-permute-done.4.refs_5_
  61.8 14.1 %shard_map.85 = (bf16[128,1280]{1,0:T(8,128)(2,1)}, bf16[2,128,1280]{2,1,0:T(8,128)(2,1)}, bf16[4,2,128,1280]{3,2,1,0:T(8,128)(2,1)}, bf16[2,128,1280]{2,1,0:T(8...) custom-call(s32[128,1280]{1,0:T(8,128)} %fusion.24.mask_ref, ...), custom_call_target="tpu_custom_call" | custom-call | flops 2516582400 | bytes 14745600 | tf_op jit(solution)/shard_map/pallas_call | solution.py:126
  75.9 4.4 %collective-permute-start.7 = (bf16[4,2,128,1280]{3,2,1,0:T(8,128)(2,1)}, bf16[4,2,128,1280]{3,2,1,0:T(8,128)(2,1)S(1)}, u32[]{:S(2)}, u32[]{:S(2)}) collective-permute-start(bf16[4,2,128,1280]{3,2,1,0:T(8,128)(2,1)} %get-tuple-element.22), channel_id=1, source_target_pairs={{0,1},{1,0},{2,3},{3,2},{4,5},{5,4},{6,7},{7,6},{8,9},{9,8},{10,11... | collective-permute-start | bytes 7864328 | tf_op jit(solution)/shard_map/ppermute | solution.py:16
  80.3 14.0 %shard_map.86 = (bf16[128,1280]{1,0:T(8,128)(2,1)}, bf16[2,128,1280]{2,1,0:T(8,128)(2,1)}, bf16[4,2,128,1280]{3,2,1,0:T(8,128)(2,1)}, bf16[2,128,1280]{2,1,0:T(8...) custom-call(s32[128,1280]{1,0:T(8,128)} %fusion.24.mask_ref, ...), custom_call_target="tpu_custom_call" | custom-call | flops 2516582400 | bytes 14745600 | tf_op jit(solution)/shard_map/pallas_call | solution.py:126
  94.3 0.1 collective-permute-start.13
  94.4 1.4 collective-permute-start.8
  95.8 0.7 collective-permute-start.9
  96.6 1.3 collective-permute-start.14
  97.9 2.0 %pad_maximum_fusion.2 = bf16[128,2560]{1,0:T(8,128)(2,1)} fusion(bf16[128,1280]{1,0:T(8,128)(2,1)} %get-tuple-element.20, bf16[128,1280]{1,0:T(8,128)(2,1)} %get-tuple-element.19), kind=kLoop, calls=%fused_computation.44 | loop fusion | flops 1310720 | bytes 1310720 | tf_op jit(solution)/shard_map/concatenate | solution.py:250
  99.8 6.9 %collective-permute-done.8 = bf16[2,128,1280]{2,1,0:T(8,128)(2,1)S(1)} collective-permute-done((bf16[2,128,1280]{2,1,0:T(8,128)(2,1)}, bf16[2,128,1280]{2,1,0:T(8,128)(2,1)S(1)}, u32[]{:S(2)}, u32[]{:S(2)}) %collective-permute-start.8) | collective-permute-done | bytes 655392 | tf_op jit(solution)/shard_map/ppermute | solution.py:16
  106.7 0.7 collective-permute-start.15
  107.4 0.0 collective-permute-done.9
  107.4 0.0 collective-permute-done.7
  107.4 0.0 copy-done.9
  107.4 0.0 copy-done.7
  107.4 0.0 copy-done.8
  107.4 0.0 copy-start.4
  107.4 0.0 copy-start.5
  107.4 0.0 copy-start.6
  107.4 0.7 fusion.13
  108.2 1.4 collective-permute-start.10
  109.5 1.3 collective-permute-start.11
  110.8 2.9 %collective-permute-done.14 = bf16[2,128,1280]{2,1,0:T(8,128)(2,1)S(1)} collective-permute-done((bf16[2,128,1280]{2,1,0:T(8,128)(2,1)}, bf16[2,128,1280]{2,1,0:T(8,128)(2,1)S(1)}, u32[]{:S(2)}, u32[]{:S(2)}) %collective-permute-start.14) | collective-permute-done | bytes 655392 | tf_op jit(solution)/shard_map/ppermute | solution.py:16
  113.7 1.9 %collective-permute-start.12 = (bf16[2,128,1280]{2,1,0:T(8,128)(2,1)S(1)}, bf16[2,128,1280]{2,1,0:T(8,128)(2,1)S(1)}, u32[]{:S(2)}, u32[]{:S(2)}) collective-permute-start(bf16[2,128,1280]{2,1,0:T(8,128)(2,1)S(1)} %get-tuple-element.36), channel_id=1, source_target_pairs={{0,4},{1,5},{2,6},{3,7},{4,8},{5,9},{6,10},{7,11},{8,12},{9,13},{1... | collective-permute-start | bytes 1966088 | tf_op jit(solution)/shard_map/ppermute | solution.py:16
  115.6 0.0 collective-permute-done.15
  115.6 0.0 collective-permute-done.13
  115.6 0.0 copy-done.4
  115.6 0.0 copy-done.5
  115.6 0.7 fusion.4
  116.3 1.5 %collective-permute-start.16 = (bf16[2,128,1280]{2,1,0:T(8,128)(2,1)S(1)}, bf16[2,128,1280]{2,1,0:T(8,128)(2,1)S(1)}, u32[]{:S(2)}, u32[]{:S(2)}) collective-permute-start(bf16[2,128,1280]{2,1,0:T(8,128)(2,1)S(1)} %get-tuple-element.38), channel_id=1, source_target_pairs={{0,2},{1,3},{2,0},{3,1},{4,6},{5,7},{6,4},{7,5},{8,10},{9,11},{10,... | collective-permute-start | bytes 1966088 | tf_op jit(solution)/shard_map/ppermute | solution.py:16
  117.8 1.3 collective-permute-start.17
  119.1 6.4 %collective-permute-done.10 = bf16[2,128,1280]{2,1,0:T(8,128)(2,1)S(1)} collective-permute-done((bf16[2,128,1280]{2,1,0:T(8,128)(2,1)S(1)}, bf16[2,128,1280]{2,1,0:T(8,128)(2,1)S(1)}, u32[]{:S(2)}, u32[]{:S(2)}) %collective-permute-start.10) | collective-permute-done | bytes 655392 | tf_op jit(solution)/shard_map/ppermute | solution.py:16
  125.5 2.6 %collective-permute-start.18 = (bf16[2,128,1280]{2,1,0:T(8,128)(2,1)S(1)}, bf16[2,128,1280]{2,1,0:T(8,128)(2,1)S(1)}, u32[]{:S(2)}, u32[]{:S(2)}) collective-permute-start(bf16[2,128,1280]{2,1,0:T(8,128)(2,1)S(1)} %get-tuple-element.39), channel_id=1, source_target_pairs={{0,4},{1,5},{2,6},{3,7},{4,8},{5,9},{6,10},{7,11},{8,12},{9,13},{1... | collective-permute-start | bytes 1966088 | tf_op jit(solution)/shard_map/ppermute | solution.py:16
  128.1 1.0 collective-permute-done.11
  129.0 1.6 %collective-permute-done.12 = bf16[2,128,1280]{2,1,0:T(8,128)(2,1)S(1)} collective-permute-done((bf16[2,128,1280]{2,1,0:T(8,128)(2,1)S(1)}, bf16[2,128,1280]{2,1,0:T(8,128)(2,1)S(1)}, u32[]{:S(2)}, u32[]{:S(2)}) %collective-permute-start.12) | collective-permute-done | bytes 655392 | tf_op jit(solution)/shard_map/ppermute | solution.py:16
  130.6 0.4 fusion.17
  131.1 0.0 copy-start.10
  131.1 8.4 %collective-permute-done.16 = bf16[2,128,1280]{2,1,0:T(8,128)(2,1)S(1)} collective-permute-done((bf16[2,128,1280]{2,1,0:T(8,128)(2,1)S(1)}, bf16[2,128,1280]{2,1,0:T(8,128)(2,1)S(1)}, u32[]{:S(2)}, u32[]{:S(2)}) %collective-permute-start.16) | collective-permute-done | bytes 655392 | tf_op jit(solution)/shard_map/ppermute | solution.py:16
  139.5 2.6 %collective-permute-done.17 = bf16[2,128,1280]{2,1,0:T(8,128)(2,1)S(1)} collective-permute-done((bf16[2,128,1280]{2,1,0:T(8,128)(2,1)S(1)}, bf16[2,128,1280]{2,1,0:T(8,128)(2,1)S(1)}, u32[]{:S(2)}, u32[]{:S(2)}) %collective-permute-start.17) | collective-permute-done | bytes 655392 | tf_op jit(solution)/shard_map/ppermute | solution.py:16
  142.1 2.2 %collective-permute-done.18 = bf16[2,128,1280]{2,1,0:T(8,128)(2,1)S(1)} collective-permute-done((bf16[2,128,1280]{2,1,0:T(8,128)(2,1)S(1)}, bf16[2,128,1280]{2,1,0:T(8,128)(2,1)S(1)}, u32[]{:S(2)}, u32[]{:S(2)}) %collective-permute-start.18) | collective-permute-done | bytes 655392 | tf_op jit(solution)/shard_map/ppermute | solution.py:16
  144.3 0.4 fusion.8
  144.8 0.9 pad_maximum_fusion.4
  145.7 0.9 pad_maximum_fusion.3
  (36 shorter events, 0.2 us)
Async XLA Ops:
  2.0 40.8 %copy-start = (bf16[2,128,2560]{2,1,0:T(8,128)(2,1)}, bf16[2,128,2560]{2,1,0:T(8,128)(2,1)S(1)}, u32[]{:S(2)}) copy-start(bf16[2,128,2560]{2,1,0:T(8,128)(2,1)S(1)} %pad_maximum_fusion.1.refs_0_) | copy-start | bytes 3932164
  2.0 31.8 %collective-permute-start.1 = (bf16[2,128,2560]{2,1,0:T(8,128)(2,1)S(1)}, bf16[2,128,2560]{2,1,0:T(8,128)(2,1)S(1)}, u32[]{:S(2)}, u32[]{:S(2)}) collective-permute-start(bf16[2,128,2560]{2,1,0:T(8,128)(2,1)S(1)} %pad_maximum_fusion.1.refs_0_), channel_id=1, source_target_pairs={{0,2},{1,3},{2,0},{3,1},{4,6},{5,7},{6,4},{7,5},{8,10},{9,11},{10,... | collective-permute-start | bytes 3932168 | tf_op jit(solution)/shard_map/ppermute | solution.py:16
  5.1 31.2 %collective-permute-start.2 = (bf16[2,128,2560]{2,1,0:T(8,128)(2,1)S(1)}, bf16[2,128,2560]{2,1,0:T(8,128)(2,1)S(1)}, u32[]{:S(2)}, u32[]{:S(2)}) collective-permute-start(bf16[2,128,2560]{2,1,0:T(8,128)(2,1)S(1)} %pad_maximum_fusion.1.refs_0_), channel_id=1, source_target_pairs={{0,4},{1,5},{2,6},{3,7},{4,8},{5,9},{6,10},{7,11},{8,12},{9,13},{1... | collective-permute-start | bytes 3932168 | tf_op jit(solution)/shard_map/ppermute | solution.py:16
  8.7 31.9 %collective-permute-start.3 = (bf16[2,128,2560]{2,1,0:T(8,128)(2,1)S(1)}, bf16[2,128,2560]{2,1,0:T(8,128)(2,1)S(1)}, u32[]{:S(2)}, u32[]{:S(2)}) collective-permute-start(bf16[2,128,2560]{2,1,0:T(8,128)(2,1)S(1)} %pad_maximum_fusion.1.refs_0_), channel_id=1, source_target_pairs={{4,0},{5,1},{6,2},{7,3},{8,4},{9,5},{10,6},{11,7},{12,8},{13,9},{1... | collective-permute-start | bytes 3932168 | tf_op jit(solution)/shard_map/ppermute | solution.py:16
  33.9 13.9 %copy-start.1 = (bf16[2,128,2560]{2,1,0:T(8,128)(2,1)}, bf16[2,128,2560]{2,1,0:T(8,128)(2,1)S(1)}, u32[]{:S(2)}) copy-start(bf16[2,128,2560]{2,1,0:T(8,128)(2,1)S(1)} %collective-permute-done.1.refs_2_) | copy-start | bytes 3932164
  36.3 6.5 %copy-start.2 = (bf16[2,128,2560]{2,1,0:T(8,128)(2,1)}, bf16[2,128,2560]{2,1,0:T(8,128)(2,1)S(1)}, u32[]{:S(2)}) copy-start(bf16[2,128,2560]{2,1,0:T(8,128)(2,1)S(1)} %collective-permute-done.2.refs_3_) | copy-start | bytes 3932164
  40.5 2.3 %copy-start.3 = (bf16[2,128,2560]{2,1,0:T(8,128)(2,1)}, bf16[2,128,2560]{2,1,0:T(8,128)(2,1)S(1)}, u32[]{:S(2)}) copy-start(bf16[2,128,2560]{2,1,0:T(8,128)(2,1)S(1)} %collective-permute-done.3.refs_4_) | copy-start | bytes 3932164
  40.5 3.0 %copy-start.13 = (s32[4]{0:T(128)S(1)}, s32[4]{0:T(128)}, u32[]{:S(2)}) copy-start(s32[4]{0:T(128)} %param.11) | copy-start | bytes 52
  40.5 9.0 %copy-start.12 = (s32[4,3]{1,0:T(4,128)S(1)}, s32[4,3]{1,0:T(4,128)}, u32[]{:S(2)}) copy-start(s32[4,3]{1,0:T(4,128)} %param.10) | copy-start | bytes 148
  42.8 19.0 %collective-permute-start.4 = (bf16[3,2,128,2560]{3,2,1,0:T(8,128)(2,1)}, bf16[3,2,128,2560]{3,2,1,0:T(8,128)(2,1)}, u32[]{:S(2)}, u32[]{:S(2)}) collective-permute-start(bf16[3,2,128,2560]{3,2,1,0:T(8,128)(2,1)} %pad_maximum_fusion), channel_id=1, source_target_pairs={{0,1},{1,0},{2,3},{3,2},{4,5},{5,4},{6,7},{7,6},{8,9},{9,8},{10,11... | collective-permute-start | bytes 11796488 | tf_op jit(solution)/shard_map/ppermute | solution.py:16
  42.8 9.0 %collective-permute-start = (bf16[2,128,2560]{2,1,0:T(8,128)(2,1)S(1)}, bf16[2,128,2560]{2,1,0:T(8,128)(2,1)}, u32[]{:S(2)}, u32[]{:S(2)}) collective-permute-start(bf16[2,128,2560]{2,1,0:T(8,128)(2,1)S(1)} %pad_maximum_fusion.1.refs_0_), channel_id=1, source_target_pairs={{0,1},{1,0},{2,3},{3,2},{4,5},{5,4},{6,7},{7,6},{8,9},{9,8},{10,11... | collective-permute-start | bytes 3932168 | tf_op jit(solution)/shard_map/ppermute | solution.py:16
  43.6 18.2 %collective-permute-start.5 = (bf16[2,128,2560]{2,1,0:T(8,128)(2,1)S(1)}, bf16[2,128,2560]{2,1,0:T(8,128)(2,1)}, u32[]{:S(2)}, u32[]{:S(2)}) collective-permute-start(bf16[2,128,2560]{2,1,0:T(8,128)(2,1)S(1)} %collective-permute-done.1.refs_2_), channel_id=1, source_target_pairs={{0,5},{3,6},{4,9},{7,10},{8,13},{11,14},{16,21},{19,22},{20,25},{2... | collective-permute-start | bytes 3932168 | tf_op jit(solution)/shard_map/ppermute | solution.py:16
  47.7 14.0 %collective-permute-start.6 = (bf16[2,128,2560]{2,1,0:T(8,128)(2,1)S(1)}, bf16[2,128,2560]{2,1,0:T(8,128)(2,1)}, u32[]{:S(2)}, u32[]{:S(2)}) collective-permute-start(bf16[2,128,2560]{2,1,0:T(8,128)(2,1)S(1)} %collective-permute-done.1.refs_2_), channel_id=1, source_target_pairs={{4,1},{7,2},{8,5},{11,6},{12,9},{15,10},{20,17},{23,18},{24,21},{2... | collective-permute-start | bytes 3932168 | tf_op jit(solution)/shard_map/ppermute | solution.py:16
  75.9 31.5 %collective-permute-start.7 = (bf16[4,2,128,1280]{3,2,1,0:T(8,128)(2,1)}, bf16[4,2,128,1280]{3,2,1,0:T(8,128)(2,1)S(1)}, u32[]{:S(2)}, u32[]{:S(2)}) collective-permute-start(bf16[4,2,128,1280]{3,2,1,0:T(8,128)(2,1)} %get-tuple-element.22), channel_id=1, source_target_pairs={{0,1},{1,0},{2,3},{3,2},{4,5},{5,4},{6,7},{7,6},{8,9},{9,8},{10,11... | collective-permute-start | bytes 7864328 | tf_op jit(solution)/shard_map/ppermute | solution.py:16
  80.3 27.1 %copy-start.9 = (bf16[2,128,1280]{2,1,0:T(8,128)(2,1)S(1)}, bf16[2,128,1280]{2,1,0:T(8,128)(2,1)}, u32[]{:S(2)}) copy-start(bf16[2,128,1280]{2,1,0:T(8,128)(2,1)} %get-tuple-element.27) | copy-start | bytes 1966084
  94.3 13.1 %copy-start.7 = (bf16[2,128,1280]{2,1,0:T(8,128)(2,1)S(1)}, bf16[2,128,1280]{2,1,0:T(8,128)(2,1)}, u32[]{:S(2)}) copy-start(bf16[2,128,1280]{2,1,0:T(8,128)(2,1)} %get-tuple-element.23) | copy-start | bytes 1966084
  94.3 13.1 %copy-start.8 = (bf16[2,128,1280]{2,1,0:T(8,128)(2,1)S(1)}, bf16[2,128,1280]{2,1,0:T(8,128)(2,1)}, u32[]{:S(2)}) copy-start(bf16[2,128,1280]{2,1,0:T(8,128)(2,1)} %get-tuple-element.26) | copy-start | bytes 1966084
  94.3 21.3 %collective-permute-start.13 = (bf16[4,2,128,1280]{3,2,1,0:T(8,128)(2,1)}, bf16[4,2,128,1280]{3,2,1,0:T(8,128)(2,1)S(1)}, u32[]{:S(2)}, u32[]{:S(2)}) collective-permute-start(bf16[4,2,128,1280]{3,2,1,0:T(8,128)(2,1)} %get-tuple-element.29), channel_id=1, source_target_pairs={{0,1},{1,0},{2,3},{3,2},{4,5},{5,4},{6,7},{7,6},{8,9},{9,8},{10,11... | collective-permute-start | bytes 7864328 | tf_op jit(solution)/shard_map/ppermute | solution.py:16
  94.4 12.2 %collective-permute-start.8 = (bf16[2,128,1280]{2,1,0:T(8,128)(2,1)}, bf16[2,128,1280]{2,1,0:T(8,128)(2,1)S(1)}, u32[]{:S(2)}, u32[]{:S(2)}) collective-permute-start(bf16[2,128,1280]{2,1,0:T(8,128)(2,1)} %get-tuple-element.24), channel_id=1, source_target_pairs={{5,0},{6,3},{9,4},{10,7},{13,8},{14,11},{21,16},{22,19},{25,20},{2... | collective-permute-start | bytes 1966088 | tf_op jit(solution)/shard_map/ppermute | solution.py:16
  95.8 11.5 %collective-permute-start.9 = (bf16[2,128,1280]{2,1,0:T(8,128)(2,1)}, bf16[2,128,1280]{2,1,0:T(8,128)(2,1)S(1)}, u32[]{:S(2)}, u32[]{:S(2)}) collective-permute-start(bf16[2,128,1280]{2,1,0:T(8,128)(2,1)} %get-tuple-element.25), channel_id=1, source_target_pairs={{1,4},{2,7},{5,8},{6,11},{9,12},{10,15},{17,20},{18,23},{21,24},{2... | collective-permute-start | bytes 1966088 | tf_op jit(solution)/shard_map/ppermute | solution.py:16
  96.6 17.1 %collective-permute-start.14 = (bf16[2,128,1280]{2,1,0:T(8,128)(2,1)}, bf16[2,128,1280]{2,1,0:T(8,128)(2,1)S(1)}, u32[]{:S(2)}, u32[]{:S(2)}) collective-permute-start(bf16[2,128,1280]{2,1,0:T(8,128)(2,1)} %get-tuple-element.31), channel_id=1, source_target_pairs={{5,0},{6,3},{9,4},{10,7},{13,8},{14,11},{21,16},{22,19},{25,20},{2... | collective-permute-start | bytes 1966088 | tf_op jit(solution)/shard_map/ppermute | solution.py:16
  106.7 8.9 %collective-permute-start.15 = (bf16[2,128,1280]{2,1,0:T(8,128)(2,1)}, bf16[2,128,1280]{2,1,0:T(8,128)(2,1)S(1)}, u32[]{:S(2)}, u32[]{:S(2)}) collective-permute-start(bf16[2,128,1280]{2,1,0:T(8,128)(2,1)} %get-tuple-element.32), channel_id=1, source_target_pairs={{1,4},{2,7},{5,8},{6,11},{9,12},{10,15},{17,20},{18,23},{21,24},{2... | collective-permute-start | bytes 1966088 | tf_op jit(solution)/shard_map/ppermute | solution.py:16
  107.4 8.2 %copy-start.4 = (bf16[2,128,1280]{2,1,0:T(8,128)(2,1)S(1)}, bf16[2,128,1280]{2,1,0:T(8,128)(2,1)}, u32[]{:S(2)}) copy-start(bf16[2,128,1280]{2,1,0:T(8,128)(2,1)} %get-tuple-element.30) | copy-start | bytes 1966084
  107.4 8.2 %copy-start.5 = (bf16[2,128,1280]{2,1,0:T(8,128)(2,1)S(1)}, bf16[2,128,1280]{2,1,0:T(8,128)(2,1)}, u32[]{:S(2)}) copy-start(bf16[2,128,1280]{2,1,0:T(8,128)(2,1)} %get-tuple-element.33) | copy-start | bytes 1966084
  107.4 8.2 %copy-start.6 = (bf16[2,128,1280]{2,1,0:T(8,128)(2,1)S(1)}, bf16[2,128,1280]{2,1,0:T(8,128)(2,1)}, u32[]{:S(2)}) copy-start(bf16[2,128,1280]{2,1,0:T(8,128)(2,1)} %get-tuple-element.34) | copy-start | bytes 1966084
  108.2 17.3 %collective-permute-start.10 = (bf16[2,128,1280]{2,1,0:T(8,128)(2,1)S(1)}, bf16[2,128,1280]{2,1,0:T(8,128)(2,1)S(1)}, u32[]{:S(2)}, u32[]{:S(2)}) collective-permute-start(bf16[2,128,1280]{2,1,0:T(8,128)(2,1)S(1)} %get-tuple-element.35), channel_id=1, source_target_pairs={{0,2},{1,3},{2,0},{3,1},{4,6},{5,7},{6,4},{7,5},{8,10},{9,11},{10,... | collective-permute-start | bytes 1966088 | tf_op jit(solution)/shard_map/ppermute | solution.py:16
  109.5 19.5 %collective-permute-start.11 = (bf16[2,128,1280]{2,1,0:T(8,128)(2,1)S(1)}, bf16[2,128,1280]{2,1,0:T(8,128)(2,1)S(1)}, u32[]{:S(2)}, u32[]{:S(2)}) collective-permute-start(bf16[2,128,1280]{2,1,0:T(8,128)(2,1)S(1)} %get-tuple-element.37), channel_id=1, source_target_pairs={{4,0},{5,1},{6,2},{7,3},{8,4},{9,5},{10,6},{11,7},{12,8},{13,9},{1... | collective-permute-start | bytes 1966088 | tf_op jit(solution)/shard_map/ppermute | solution.py:16
  113.7 17.0 %collective-permute-start.12 = (bf16[2,128,1280]{2,1,0:T(8,128)(2,1)S(1)}, bf16[2,128,1280]{2,1,0:T(8,128)(2,1)S(1)}, u32[]{:S(2)}, u32[]{:S(2)}) collective-permute-start(bf16[2,128,1280]{2,1,0:T(8,128)(2,1)S(1)} %get-tuple-element.36), channel_id=1, source_target_pairs={{0,4},{1,5},{2,6},{3,7},{4,8},{5,9},{6,10},{7,11},{8,12},{9,13},{1... | collective-permute-start | bytes 1966088 | tf_op jit(solution)/shard_map/ppermute | solution.py:16
  115.6 15.0 %copy-start.11 = (bf16[2,128,1280]{2,1,0:T(8,128)(2,1)S(1)}, bf16[2,128,1280]{2,1,0:T(8,128)(2,1)}, u32[]{:S(2)}) copy-start(bf16[2,128,1280]{2,1,0:T(8,128)(2,1)} %get-tuple-element.21) | copy-start | bytes 1966084
  116.3 23.2 %collective-permute-start.16 = (bf16[2,128,1280]{2,1,0:T(8,128)(2,1)S(1)}, bf16[2,128,1280]{2,1,0:T(8,128)(2,1)S(1)}, u32[]{:S(2)}, u32[]{:S(2)}) collective-permute-start(bf16[2,128,1280]{2,1,0:T(8,128)(2,1)S(1)} %get-tuple-element.38), channel_id=1, source_target_pairs={{0,2},{1,3},{2,0},{3,1},{4,6},{5,7},{6,4},{7,5},{8,10},{9,11},{10,... | collective-permute-start | bytes 1966088 | tf_op jit(solution)/shard_map/ppermute | solution.py:16
  117.8 24.3 %collective-permute-start.17 = (bf16[2,128,1280]{2,1,0:T(8,128)(2,1)S(1)}, bf16[2,128,1280]{2,1,0:T(8,128)(2,1)S(1)}, u32[]{:S(2)}, u32[]{:S(2)}) collective-permute-start(bf16[2,128,1280]{2,1,0:T(8,128)(2,1)S(1)} %get-tuple-element.40), channel_id=1, source_target_pairs={{4,0},{5,1},{6,2},{7,3},{8,4},{9,5},{10,6},{11,7},{12,8},{13,9},{1... | collective-permute-start | bytes 1966088 | tf_op jit(solution)/shard_map/ppermute | solution.py:16
  125.5 18.8 %collective-permute-start.18 = (bf16[2,128,1280]{2,1,0:T(8,128)(2,1)S(1)}, bf16[2,128,1280]{2,1,0:T(8,128)(2,1)S(1)}, u32[]{:S(2)}, u32[]{:S(2)}) collective-permute-start(bf16[2,128,1280]{2,1,0:T(8,128)(2,1)S(1)} %get-tuple-element.39), channel_id=1, source_target_pairs={{0,4},{1,5},{2,6},{3,7},{4,8},{5,9},{6,10},{7,11},{8,12},{9,13},{1... | collective-permute-start | bytes 1966088 | tf_op jit(solution)/shard_map/ppermute | solution.py:16
  131.1 13.3 %copy-start.10 = (bf16[2,128,1280]{2,1,0:T(8,128)(2,1)S(1)}, bf16[2,128,1280]{2,1,0:T(8,128)(2,1)}, u32[]{:S(2)}) copy-start(bf16[2,128,1280]{2,1,0:T(8,128)(2,1)} %get-tuple-element.28) | copy-start | bytes 1966084

commit v10 on v7

--- a/solution.py
+++ b/solution.py
@@ -234,22 +234,34 @@
     chunk_heads = heads // CHUNKS if heads % CHUNKS == 0 else heads
     width = chunk_heads * HD
     starts = list(range(0, channel_total, width))
-    firsts, seconds, outs, backs, sums, dqs = [], [], [], [], [], []
-    for c, first in enumerate(starts):
-        own = jnp.stack([keys[:, first : first + width], values[:, first : first + width]])
-        firsts.append(forward_relay(own, count, None))
-    for c in range(len(starts)):
-        seconds.append(forward_second(firsts[c], count, None))
-    for c, first in enumerate(starts):
-        dq, parts = chunk_kernel(forward_mask, queries, out_grad, seconds[c], first // HD, inv_root)
-        dqs.append(dq)
-        outs.append(parts)
-    for c in range(len(starts)):
-        backs.append(return_first(outs[c], count, None))
-    got = None
-    for c in range(len(starts)):
-        got, summed = return_second(outs[c], backs[c], count, None)
-        sums.append(summed)
+    chunks = len(starts)
+    state = {"own": [jnp.stack([keys[:, f : f + width], values[:, f : f + width]]) for f in starts]}
+    state["first"], state["second"], state["parts"], state["back"] = {}, {}, {}, {}
+    state["dq"], state["sum"] = {}, {}
+    for tick in range(chunks + 4):
+        step = {}
+        for c in range(chunks):
+            lag = tick - c
+            if lag == 0:
+                step[("first", c)] = forward_relay(state["own"][c], count, None)
+            elif lag == 1:
+                step[("second", c)] = forward_second(state["first"][c], count, None)
+            elif lag == 2:
+                dq, parts = chunk_kernel(
+                    forward_mask, queries, out_grad, state["second"][c], starts[c] // HD, inv_root
+                )
+                step[("dq", c)] = dq
+                step[("parts", c)] = parts
+            elif lag == 3:
+                step[("back", c)] = return_first(state["parts"][c], count, None)
+            elif lag == 4:
+                step[("sum", c)] = return_second(state["parts"][c], state["back"][c], count, None)[1]
+        for (kind, c), value in step.items():
+            state[kind][c] = value
+        if tick < chunks + 3:
+            state = lax.optimization_barrier(state)
+    sums = [state["sum"][c] for c in range(chunks)]
+    dqs = [state["dq"][c] for c in range(chunks)]
     grads = [(dqs[c], sums[c][0].astype(jnp.bfloat16), sums[c][1].astype(jnp.bfloat16)) for c in range(len(starts))]
     query_grad = jnp.concatenate([grad[0] for grad in grads], axis=1)
     key_grad = jnp.concatenate([grad[1] for grad in grads], axis=1)

time: 146 us -> 156 us (1.068)
  waiting for transfers between devices: 54.5 us -> 66.3 us
  other arithmetic: 12.5 us -> 8.72 us
    ppermute x26, waiting for transfers between devices: 54.5 us -> 66.3 us  [send(): return lax.ppermute(value, 'tm', pairs)]
    another operation x2, other arithmetic: 4.72 us -> 0.43 us  [forward_second(): ahead = jnp.stack([from_cross, from_below, from_above])]
    convert_element_type x2, other arithmetic: 1.4 us -> 3 us  [return_second(): cross_sum.astype(jnp.bfloat16)]
  transfers between devices with their start and end apart: 26 -> 26, of which waited for: 15 -> 13; matrix products, arithmetic and copies ran while one was open for 7% -> 4% of each run, Pallas kernels for 19% -> 18%
where the time goes in v10:
time: 156 us; the launch traced here: 155 us
  waiting for transfers between devices  66.3 us (42%)
  starting transfers between devices  47.8 us (31%)
  Pallas kernels  28.1 us (18%)
  other arithmetic  8.72 us (6%)
  local copies, waits for them, and re-layouts  3.09 us (2%)
    ppermute x26, waiting for transfers between devices, send(): return lax.ppermute(value, 'tm', pairs)  66.3 us
    ppermute x26, starting transfers between devices, send(): return lax.ppermute(value, 'tm', pairs)  47.8 us
    pallas_call x2, Pallas kernels, attention_backward(): pl.pallas_call(kernel, grid=(heads // STEP_HEADS,), in_specs=in_specs, ou...  28.1 us
  transfers between devices with their start and end apart: 26, of which 13 were waited for; matrix products, arithmetic and copies ran while one was open for 4% of the time, Pallas kernels for 18%

profile of v10, /device:TPU:0, one launch (start us, length us, event | category | flops | bytes accessed | tf_op | source)
XLA Modules:
  0.0 155.2 jit_solution(14220404834618024897)
XLA Ops:
  0.6 1.4 slice_bitcast_fusion.4
  2.0 0.1 pad_maximum_fusion.2.refs_0_
  2.1 0.6 collective-permute-start
  2.6 2.6 %collective-permute-start.1 = (bf16[2,128,1280]{2,1,0:T(8,128)(2,1)S(1)}, bf16[2,128,1280]{2,1,0:T(8,128)(2,1)S(1)}, u32[]{:S(2)}, u32[]{:S(2)}) collective-permute-start(bf16[2,128,1280]{2,1,0:T(8,128)(2,1)S(1)} %pad_maximum_fusion.2.refs_0_), channel_id=1, source_target_pairs={{0,2},{1,3},{2,0},{3,1},{4,6},{5,7},{6,4},{7,5},{8,10},{9,11},{10,... | collective-permute-start | bytes 1966088 | tf_op jit(solution)/shard_map/ppermute | solution.py:16
  5.2 3.5 %collective-permute-start.2 = (bf16[2,128,1280]{2,1,0:T(8,128)(2,1)S(1)}, bf16[2,128,1280]{2,1,0:T(8,128)(2,1)S(1)}, u32[]{:S(2)}, u32[]{:S(2)}) collective-permute-start(bf16[2,128,1280]{2,1,0:T(8,128)(2,1)S(1)} %pad_maximum_fusion.2.refs_0_), channel_id=1, source_target_pairs={{0,4},{1,5},{2,6},{3,7},{4,8},{5,9},{6,10},{7,11},{8,12},{9,13},{1... | collective-permute-start | bytes 1966088 | tf_op jit(solution)/shard_map/ppermute | solution.py:16
  8.7 1.3 collective-permute-start.3
  10.0 0.1 pad_maximum_fusion.3.refs_0_
  10.1 0.0 copy-start.4
  10.1 10.4 %collective-permute-done.1.refs_2_ = bf16[2,128,1280]{2,1,0:T(8,128)(2,1)S(1)} collective-permute-done((bf16[2,128,1280]{2,1,0:T(8,128)(2,1)S(1)}, bf16[2,128,1280]{2,1,0:T(8,128)(2,1)S(1)}, u32[]{:S(2)}, u32[]{:S(2)}) %collective-permute-start.1) | collective-permute-done | bytes 655392 | tf_op jit(solution)/shard_map/ppermute | solution.py:16
  20.5 2.4 %collective-permute-done.2.refs_3_ = bf16[2,128,1280]{2,1,0:T(8,128)(2,1)S(1)} collective-permute-done((bf16[2,128,1280]{2,1,0:T(8,128)(2,1)S(1)}, bf16[2,128,1280]{2,1,0:T(8,128)(2,1)S(1)}, u32[]{:S(2)}, u32[]{:S(2)}) %collective-permute-start.2) | collective-permute-done | bytes 655392 | tf_op jit(solution)/shard_map/ppermute | solution.py:16
  23.0 4.2 %collective-permute-done.3.refs_4_ = bf16[2,128,1280]{2,1,0:T(8,128)(2,1)S(1)} collective-permute-done((bf16[2,128,1280]{2,1,0:T(8,128)(2,1)S(1)}, bf16[2,128,1280]{2,1,0:T(8,128)(2,1)S(1)}, u32[]{:S(2)}, u32[]{:S(2)}) %collective-permute-start.3) | collective-permute-done | bytes 655392 | tf_op jit(solution)/shard_map/ppermute | solution.py:16
  27.1 0.2 pad_maximum_fusion
  27.4 0.6 copy-done.9
  28.0 0.0 collective-permute-start.8
  28.0 0.5 collective-permute-start.4
  28.5 0.5 collective-permute-start.5
  29.0 3.5 %collective-permute-start.6 = (bf16[2,128,1280]{2,1,0:T(8,128)(2,1)S(1)}, bf16[2,128,1280]{2,1,0:T(8,128)(2,1)S(1)}, u32[]{:S(2)}, u32[]{:S(2)}) collective-permute-start(bf16[2,128,1280]{2,1,0:T(8,128)(2,1)S(1)} %pad_maximum_fusion.3.refs_0_), channel_id=1, source_target_pairs={{0,4},{1,5},{2,6},{3,7},{4,8},{5,9},{6,10},{7,11},{8,12},{9,13},{1... | collective-permute-start | bytes 1966088 | tf_op jit(solution)/shard_map/ppermute | solution.py:16
  32.5 1.3 collective-permute-start.7
  33.8 0.0 collective-permute-done.4.refs_1_
  33.8 0.7 collective-permute-start.10
  34.6 10.6 %collective-permute-done.5.refs_2_ = bf16[2,128,1280]{2,1,0:T(8,128)(2,1)S(1)} collective-permute-done((bf16[2,128,1280]{2,1,0:T(8,128)(2,1)S(1)}, bf16[2,128,1280]{2,1,0:T(8,128)(2,1)S(1)}, u32[]{:S(2)}, u32[]{:S(2)}) %collective-permute-start.5) | collective-permute-done | bytes 655392 | tf_op jit(solution)/shard_map/ppermute | solution.py:16
  45.1 2.2 %collective-permute-start.9 = (bf16[2,128,1280]{2,1,0:T(8,128)(2,1)}, bf16[2,128,1280]{2,1,0:T(8,128)(2,1)S(1)}, u32[]{:S(2)}, u32[]{:S(2)}) collective-permute-start(bf16[2,128,1280]{2,1,0:T(8,128)(2,1)} %copy-done.7), channel_id=1, source_target_pairs={{0,5},{3,6},{4,9},{7,10},{8,13},{11,14},{16,21},{19,22},{20,25},{2... | collective-permute-start | bytes 1966088 | tf_op jit(solution)/shard_map/ppermute | solution.py:16
  47.4 0.0 collective-permute-done.6.refs_3_
  47.5 3.0 %collective-permute-done.7.refs_4_ = bf16[2,128,1280]{2,1,0:T(8,128)(2,1)S(1)} collective-permute-done((bf16[2,128,1280]{2,1,0:T(8,128)(2,1)S(1)}, bf16[2,128,1280]{2,1,0:T(8,128)(2,1)S(1)}, u32[]{:S(2)}, u32[]{:S(2)}) %collective-permute-start.7) | collective-permute-done | bytes 655392 | tf_op jit(solution)/shard_map/ppermute | solution.py:16
  50.5 0.0 collective-permute-done.10.refs_7_
  50.5 5.2 %collective-permute-done.9.refs_6_ = bf16[2,128,1280]{2,1,0:T(8,128)(2,1)S(1)} collective-permute-done((bf16[2,128,1280]{2,1,0:T(8,128)(2,1)}, bf16[2,128,1280]{2,1,0:T(8,128)(2,1)S(1)}, u32[]{:S(2)}, u32[]{:S(2)}) %collective-permute-start.9) | collective-permute-done | bytes 655392 | tf_op jit(solution)/shard_map/ppermute | solution.py:16
  55.7 0.9 copy-done.19
  56.6 0.2 pad_maximum_fusion.1
  56.8 1.9 %collective-permute-start.11 = (bf16[3,2,128,1280]{3,2,1,0:T(8,128)(2,1)S(1)}, bf16[3,2,128,1280]{3,2,1,0:T(8,128)(2,1)}, u32[]{:S(2)}, u32[]{:S(2)}) collective-permute-start(bf16[3,2,128,1280]{3,2,1,0:T(8,128)(2,1)S(1)} %pad_maximum_fusion.1), channel_id=1, source_target_pairs={{0,1},{1,0},{2,3},{3,2},{4,5},{5,4},{6,7},{7,6},{8,9},{9,8},{10,11... | collective-permute-start | bytes 5898248 | tf_op jit(solution)/shard_map/ppermute | solution.py:16
  58.8 0.1 copy.9
  58.9 0.1 select_reduce_fusion
  59.0 0.1 multiply_reduce_fusion
  59.1 4.3 %collective-permute-start.12 = (bf16[2,128,1280]{2,1,0:T(8,128)(2,1)S(1)}, bf16[2,128,1280]{2,1,0:T(8,128)(2,1)}, u32[]{:S(2)}, u32[]{:S(2)}) collective-permute-start(bf16[2,128,1280]{2,1,0:T(8,128)(2,1)S(1)} %collective-permute-done.5.refs_2_), channel_id=1, source_target_pairs={{0,5},{3,6},{4,9},{7,10},{8,13},{11,14},{16,21},{19,22},{20,25},{2... | collective-permute-start | bytes 1966088 | tf_op jit(solution)/shard_map/ppermute | solution.py:16
  63.4 1.5 collective-permute-start.13
  64.8 1.4 fusion.23.mask_ref
  66.2 14.0 %shard_map.85 = (bf16[128,1280]{1,0:T(8,128)(2,1)}, bf16[2,128,1280]{2,1,0:T(8,128)(2,1)}, bf16[4,2,128,1280]{3,2,1,0:T(8,128)(2,1)}, bf16[2,128,1280]{2,1,0:T(8...) custom-call(s32[128,1280]{1,0:T(8,128)} %fusion.23.mask_ref, ...), custom_call_target="tpu_custom_call" | custom-call | flops 2516582400 | bytes 14745600 | tf_op jit(solution)/shard_map/pallas_call | solution.py:127
  80.2 0.0 collective-permute-done.12.refs_6_
  80.3 0.1 collective-permute-start.14
  80.3 1.4 collective-permute-start.15
  81.8 1.5 collective-permute-start.16
  83.3 14.1 %shard_map.86 = (bf16[128,1280]{1,0:T(8,128)(2,1)}, bf16[2,128,1280]{2,1,0:T(8,128)(2,1)}, bf16[4,2,128,1280]{3,2,1,0:T(8,128)(2,1)}, bf16[2,128,1280]{2,1,0:T(8...) custom-call(s32[128,1280]{1,0:T(8,128)} %fusion.23.mask_ref, ...), custom_call_target="tpu_custom_call" | custom-call | flops 2516582400 | bytes 14745600 | tf_op jit(solution)/shard_map/pallas_call | solution.py:127
  97.5 2.5 %collective-permute-start.17 = (bf16[4,2,128,1280]{3,2,1,0:T(8,128)(2,1)}, bf16[4,2,128,1280]{3,2,1,0:T(8,128)(2,1)S(1)}, u32[]{:S(2)}, u32[]{:S(2)}) collective-permute-start(bf16[4,2,128,1280]{3,2,1,0:T(8,128)(2,1)} %get-tuple-element.134), channel_id=1, source_target_pairs={{0,1},{1,0},{2,3},{3,2},{4,5},{5,4},{6,7},{7,6},{8,9},{9,8},{10,11... | collective-permute-start | bytes 7864328 | tf_op jit(solution)/shard_map/ppermute | solution.py:16
  100.0 2.3 %fusion.13 = (bf16[2,128,1280]{2,1,0:T(8,128)(2,1)S(1)}, bf16[2,128,1280]{2,1,0:T(8,128)(2,1)S(1)}, bf16[2,128,1280]{2,1,0:T(8,128)(2,1)S(1)}) fusion(bf16[2,128,1280]{2,1,0:T(8,128)(2,1)} %collective-permute-done.16, bf16[2,128,1280]{2,1,0:T(8,128)(2,1)} %collective-permute-done.15, bf16[2,128,1280]{2,1,0:T(8,128)(2,1)S(1)} %copy-done.3, ...), kind=kLoop, calls=%fused_computation.22 | loop fusion | flops 5242880 | bytes 7208960 | tf_op jit(solution)/shard_map/convert_element_type | solution.py:195
  102.3 1.8 %collective-permute-start.20 = (bf16[2,128,1280]{2,1,0:T(8,128)(2,1)S(1)}, bf16[2,128,1280]{2,1,0:T(8,128)(2,1)S(1)}, u32[]{:S(2)}, u32[]{:S(2)}) collective-permute-start(bf16[2,128,1280]{2,1,0:T(8,128)(2,1)S(1)} %get-tuple-element.160), channel_id=1, source_target_pairs={{0,2},{1,3},{2,0},{3,1},{4,6},{5,7},{6,4},{7,5},{8,10},{9,11},{10,... | collective-permute-start | bytes 1966088 | tf_op jit(solution)/shard_map/ppermute | solution.py:16
  104.1 1.3 collective-permute-start.21
  105.4 4.7 %collective-permute-start.22 = (bf16[2,128,1280]{2,1,0:T(8,128)(2,1)S(1)}, bf16[2,128,1280]{2,1,0:T(8,128)(2,1)S(1)}, u32[]{:S(2)}, u32[]{:S(2)}) collective-permute-start(bf16[2,128,1280]{2,1,0:T(8,128)(2,1)S(1)} %get-tuple-element.161), channel_id=1, source_target_pairs={{0,4},{1,5},{2,6},{3,7},{4,8},{5,9},{6,10},{7,11},{8,12},{9,13},{1... | collective-permute-start | bytes 1966088 | tf_op jit(solution)/shard_map/ppermute | solution.py:16
  110.1 1.3 collective-permute-start.18
  111.4 7.9 %collective-permute-done.20 = bf16[2,128,1280]{2,1,0:T(8,128)(2,1)S(1)} collective-permute-done((bf16[2,128,1280]{2,1,0:T(8,128)(2,1)S(1)}, bf16[2,128,1280]{2,1,0:T(8,128)(2,1)S(1)}, u32[]{:S(2)}, u32[]{:S(2)}) %collective-permute-start.20) | collective-permute-done | bytes 655392 | tf_op jit(solution)/shard_map/ppermute | solution.py:16
  119.3 0.7 collective-permute-start.19
  120.0 3.5 %collective-permute-done.21 = bf16[2,128,1280]{2,1,0:T(8,128)(2,1)S(1)} collective-permute-done((bf16[2,128,1280]{2,1,0:T(8,128)(2,1)S(1)}, bf16[2,128,1280]{2,1,0:T(8,128)(2,1)S(1)}, u32[]{:S(2)}, u32[]{:S(2)}) %collective-permute-start.21) | collective-permute-done | bytes 655392 | tf_op jit(solution)/shard_map/ppermute | solution.py:16
  123.5 1.2 collective-permute-done.22
  124.8 0.4 fusion.16
  125.2 4.7 %collective-permute-done.18 = bf16[2,128,1280]{2,1,0:T(8,128)(2,1)S(1)} collective-permute-done((bf16[2,128,1280]{2,1,0:T(8,128)(2,1)S(1)}, bf16[2,128,1280]{2,1,0:T(8,128)(2,1)S(1)}, u32[]{:S(2)}, u32[]{:S(2)}) %collective-permute-start.18) | collective-permute-done | bytes 655392 | tf_op jit(solution)/shard_map/ppermute | solution.py:16
  129.9 0.7 fusion.4
  130.6 2.3 %collective-permute-start.23 = (bf16[2,128,1280]{2,1,0:T(8,128)(2,1)S(1)}, bf16[2,128,1280]{2,1,0:T(8,128)(2,1)S(1)}, u32[]{:S(2)}, u32[]{:S(2)}) collective-permute-start(bf16[2,128,1280]{2,1,0:T(8,128)(2,1)S(1)} %get-tuple-element.157), channel_id=1, source_target_pairs={{0,2},{1,3},{2,0},{3,1},{4,6},{5,7},{6,4},{7,5},{8,10},{9,11},{10,... | collective-permute-start | bytes 1966088 | tf_op jit(solution)/shard_map/ppermute | solution.py:16
  132.9 1.3 collective-permute-start.24
  134.2 4.7 %collective-permute-start.25 = (bf16[2,128,1280]{2,1,0:T(8,128)(2,1)S(1)}, bf16[2,128,1280]{2,1,0:T(8,128)(2,1)S(1)}, u32[]{:S(2)}, u32[]{:S(2)}) collective-permute-start(bf16[2,128,1280]{2,1,0:T(8,128)(2,1)S(1)} %get-tuple-element.158), channel_id=1, source_target_pairs={{0,4},{1,5},{2,6},{3,7},{4,8},{5,9},{6,10},{7,11},{8,12},{9,13},{1... | collective-permute-start | bytes 1966088 | tf_op jit(solution)/shard_map/ppermute | solution.py:16
  138.9 0.9 pad_maximum_fusion.4
  139.9 8.3 %collective-permute-done.23 = bf16[2,128,1280]{2,1,0:T(8,128)(2,1)S(1)} collective-permute-done((bf16[2,128,1280]{2,1,0:T(8,128)(2,1)S(1)}, bf16[2,128,1280]{2,1,0:T(8,128)(2,1)S(1)}, u32[]{:S(2)}, u32[]{:S(2)}) %collective-permute-start.23) | collective-permute-done | bytes 655392 | tf_op jit(solution)/shard_map/ppermute | solution.py:16
  148.2 3.5 %collective-permute-done.24 = bf16[2,128,1280]{2,1,0:T(8,128)(2,1)S(1)} collective-permute-done((bf16[2,128,1280]{2,1,0:T(8,128)(2,1)S(1)}, bf16[2,128,1280]{2,1,0:T(8,128)(2,1)S(1)}, u32[]{:S(2)}, u32[]{:S(2)}) %collective-permute-start.24) | collective-permute-done | bytes 655392 | tf_op jit(solution)/shard_map/ppermute | solution.py:16
  151.7 1.3 collective-permute-done.25
  153.0 0.4 fusion.8
  153.5 0.9 pad_maximum_fusion.6
  154.4 0.9 pad_maximum_fusion.5
  (71 shorter events, 0.3 us)
Async XLA Ops:
  2.1 25.3 %copy-start.5 = (bf16[2,128,1280]{2,1,0:T(8,128)(2,1)}, bf16[2,128,1280]{2,1,0:T(8,128)(2,1)S(1)}, u32[]{:S(2)}) copy-start(bf16[2,128,1280]{2,1,0:T(8,128)(2,1)S(1)} %pad_maximum_fusion.2.refs_0_) | copy-start | bytes 1966084
  2.1 8.0 %collective-permute-start = (bf16[2,128,1280]{2,1,0:T(8,128)(2,1)S(1)}, bf16[2,128,1280]{2,1,0:T(8,128)(2,1)S(1)}, u32[]{:S(2)}, u32[]{:S(2)}) collective-permute-start(bf16[2,128,1280]{2,1,0:T(8,128)(2,1)S(1)} %pad_maximum_fusion.2.refs_0_), channel_id=1, source_target_pairs={{0,1},{1,0},{2,3},{3,2},{4,5},{5,4},{6,7},{7,6},{8,9},{9,8},{10,11... | collective-permute-start | bytes 1966088 | tf_op jit(solution)/shard_map/ppermute | solution.py:16
  2.6 17.9 %collective-permute-start.1 = (bf16[2,128,1280]{2,1,0:T(8,128)(2,1)S(1)}, bf16[2,128,1280]{2,1,0:T(8,128)(2,1)S(1)}, u32[]{:S(2)}, u32[]{:S(2)}) collective-permute-start(bf16[2,128,1280]{2,1,0:T(8,128)(2,1)S(1)} %pad_maximum_fusion.2.refs_0_), channel_id=1, source_target_pairs={{0,2},{1,3},{2,0},{3,1},{4,6},{5,7},{6,4},{7,5},{8,10},{9,11},{10,... | collective-permute-start | bytes 1966088 | tf_op jit(solution)/shard_map/ppermute | solution.py:16
  5.2 17.8 %collective-permute-start.2 = (bf16[2,128,1280]{2,1,0:T(8,128)(2,1)S(1)}, bf16[2,128,1280]{2,1,0:T(8,128)(2,1)S(1)}, u32[]{:S(2)}, u32[]{:S(2)}) collective-permute-start(bf16[2,128,1280]{2,1,0:T(8,128)(2,1)S(1)} %pad_maximum_fusion.2.refs_0_), channel_id=1, source_target_pairs={{0,4},{1,5},{2,6},{3,7},{4,8},{5,9},{6,10},{7,11},{8,12},{9,13},{1... | collective-permute-start | bytes 1966088 | tf_op jit(solution)/shard_map/ppermute | solution.py:16
  8.7 18.4 %collective-permute-start.3 = (bf16[2,128,1280]{2,1,0:T(8,128)(2,1)S(1)}, bf16[2,128,1280]{2,1,0:T(8,128)(2,1)S(1)}, u32[]{:S(2)}, u32[]{:S(2)}) collective-permute-start(bf16[2,128,1280]{2,1,0:T(8,128)(2,1)S(1)} %pad_maximum_fusion.2.refs_0_), channel_id=1, source_target_pairs={{4,0},{5,1},{6,2},{7,3},{8,4},{9,5},{10,6},{11,7},{12,8},{13,9},{1... | collective-permute-start | bytes 1966088 | tf_op jit(solution)/shard_map/ppermute | solution.py:16
  10.1 22.4 %copy-start.4 = (bf16[2,128,1280]{2,1,0:T(8,128)(2,1)}, bf16[2,128,1280]{2,1,0:T(8,128)(2,1)S(1)}, u32[]{:S(2)}) copy-start(bf16[2,128,1280]{2,1,0:T(8,128)(2,1)S(1)} %pad_maximum_fusion.3.refs_0_) | copy-start | bytes 1966084
  10.1 17.0 %copy-start.17 = (bf16[2,128,1280]{2,1,0:T(8,128)(2,1)}, bf16[2,128,1280]{2,1,0:T(8,128)(2,1)S(1)}, u32[]{:S(2)}) copy-start(bf16[2,128,1280]{2,1,0:T(8,128)(2,1)S(1)} %collective-permute-done.refs_1_) | copy-start | bytes 1966084
  20.5 6.8 %copy-start.7 = (bf16[2,128,1280]{2,1,0:T(8,128)(2,1)}, bf16[2,128,1280]{2,1,0:T(8,128)(2,1)S(1)}, u32[]{:S(2)}) copy-start(bf16[2,128,1280]{2,1,0:T(8,128)(2,1)S(1)} %collective-permute-done.1.refs_2_) | copy-start | bytes 1966084
  23.0 4.4 %copy-start.8 = (bf16[2,128,1280]{2,1,0:T(8,128)(2,1)}, bf16[2,128,1280]{2,1,0:T(8,128)(2,1)S(1)}, u32[]{:S(2)}) copy-start(bf16[2,128,1280]{2,1,0:T(8,128)(2,1)S(1)} %collective-permute-done.2.refs_3_) | copy-start | bytes 1966084
  27.1 0.8 copy-start.9
  28.0 27.8 %collective-permute-start.8 = (bf16[3,2,128,1280]{3,2,1,0:T(8,128)(2,1)S(1)}, bf16[3,2,128,1280]{3,2,1,0:T(8,128)(2,1)}, u32[]{:S(2)}, u32[]{:S(2)}) collective-permute-start(bf16[3,2,128,1280]{3,2,1,0:T(8,128)(2,1)S(1)} %pad_maximum_fusion), channel_id=1, source_target_pairs={{0,1},{1,0},{2,3},{3,2},{4,5},{5,4},{6,7},{7,6},{8,9},{9,8},{10,11... | collective-permute-start | bytes 5898248 | tf_op jit(solution)/shard_map/ppermute | solution.py:16
  28.0 5.9 %collective-permute-start.4 = (bf16[2,128,1280]{2,1,0:T(8,128)(2,1)S(1)}, bf16[2,128,1280]{2,1,0:T(8,128)(2,1)}, u32[]{:S(2)}, u32[]{:S(2)}) collective-permute-start(bf16[2,128,1280]{2,1,0:T(8,128)(2,1)S(1)} %pad_maximum_fusion.3.refs_0_), channel_id=1, source_target_pairs={{0,1},{1,0},{2,3},{3,2},{4,5},{5,4},{6,7},{7,6},{8,9},{9,8},{10,11... | collective-permute-start | bytes 1966088 | tf_op jit(solution)/shard_map/ppermute | solution.py:16
  28.5 16.6 %collective-permute-start.5 = (bf16[2,128,1280]{2,1,0:T(8,128)(2,1)S(1)}, bf16[2,128,1280]{2,1,0:T(8,128)(2,1)S(1)}, u32[]{:S(2)}, u32[]{:S(2)}) collective-permute-start(bf16[2,128,1280]{2,1,0:T(8,128)(2,1)S(1)} %pad_maximum_fusion.3.refs_0_), channel_id=1, source_target_pairs={{0,2},{1,3},{2,0},{3,1},{4,6},{5,7},{6,4},{7,5},{8,10},{9,11},{10,... | collective-permute-start | bytes 1966088 | tf_op jit(solution)/shard_map/ppermute | solution.py:16
  29.0 18.4 %collective-permute-start.6 = (bf16[2,128,1280]{2,1,0:T(8,128)(2,1)S(1)}, bf16[2,128,1280]{2,1,0:T(8,128)(2,1)S(1)}, u32[]{:S(2)}, u32[]{:S(2)}) collective-permute-start(bf16[2,128,1280]{2,1,0:T(8,128)(2,1)S(1)} %pad_maximum_fusion.3.refs_0_), channel_id=1, source_target_pairs={{0,4},{1,5},{2,6},{3,7},{4,8},{5,9},{6,10},{7,11},{8,12},{9,13},{1... | collective-permute-start | bytes 1966088 | tf_op jit(solution)/shard_map/ppermute | solution.py:16
  32.5 18.0 %collective-permute-start.7 = (bf16[2,128,1280]{2,1,0:T(8,128)(2,1)S(1)}, bf16[2,128,1280]{2,1,0:T(8,128)(2,1)S(1)}, u32[]{:S(2)}, u32[]{:S(2)}) collective-permute-start(bf16[2,128,1280]{2,1,0:T(8,128)(2,1)S(1)} %pad_maximum_fusion.3.refs_0_), channel_id=1, source_target_pairs={{4,0},{5,1},{6,2},{7,3},{8,4},{9,5},{10,6},{11,7},{12,8},{13,9},{1... | collective-permute-start | bytes 1966088 | tf_op jit(solution)/shard_map/ppermute | solution.py:16
  33.8 16.7 %collective-permute-start.10 = (bf16[2,128,1280]{2,1,0:T(8,128)(2,1)}, bf16[2,128,1280]{2,1,0:T(8,128)(2,1)S(1)}, u32[]{:S(2)}, u32[]{:S(2)}) collective-permute-start(bf16[2,128,1280]{2,1,0:T(8,128)(2,1)} %copy-done.7), channel_id=1, source_target_pairs={{4,1},{7,2},{8,5},{11,6},{12,9},{15,10},{20,17},{23,18},{24,21},{2... | collective-permute-start | bytes 1966088 | tf_op jit(solution)/shard_map/ppermute | solution.py:16
  45.1 18.2 %copy-start.6 = (bf16[2,128,1280]{2,1,0:T(8,128)(2,1)}, bf16[2,128,1280]{2,1,0:T(8,128)(2,1)S(1)}, u32[]{:S(2)}) copy-start(bf16[2,128,1280]{2,1,0:T(8,128)(2,1)S(1)} %collective-permute-done.5.refs_2_) | copy-start | bytes 1966084
  45.1 10.6 %collective-permute-start.9 = (bf16[2,128,1280]{2,1,0:T(8,128)(2,1)}, bf16[2,128,1280]{2,1,0:T(8,128)(2,1)S(1)}, u32[]{:S(2)}, u32[]{:S(2)}) collective-permute-start(bf16[2,128,1280]{2,1,0:T(8,128)(2,1)} %copy-done.7), channel_id=1, source_target_pairs={{0,5},{3,6},{4,9},{7,10},{8,13},{11,14},{16,21},{19,22},{20,25},{2... | collective-permute-start | bytes 1966088 | tf_op jit(solution)/shard_map/ppermute | solution.py:16
  47.5 9.4 %copy-start.10 = (bf16[2,128,1280]{2,1,0:T(8,128)(2,1)}, bf16[2,128,1280]{2,1,0:T(8,128)(2,1)S(1)}, u32[]{:S(2)}) copy-start(bf16[2,128,1280]{2,1,0:T(8,128)(2,1)S(1)} %collective-permute-done.6.refs_3_) | copy-start | bytes 1966084
  50.5 6.3 %copy-start.11 = (bf16[2,128,1280]{2,1,0:T(8,128)(2,1)}, bf16[2,128,1280]{2,1,0:T(8,128)(2,1)S(1)}, u32[]{:S(2)}) copy-start(bf16[2,128,1280]{2,1,0:T(8,128)(2,1)S(1)} %collective-permute-done.7.refs_4_) | copy-start | bytes 1966084
  50.5 5.2 %copy-start.18 = (bf16[2,128,1280]{2,1,0:T(8,128)(2,1)}, bf16[2,128,1280]{2,1,0:T(8,128)(2,1)S(1)}, u32[]{:S(2)}) copy-start(bf16[2,128,1280]{2,1,0:T(8,128)(2,1)S(1)} %collective-permute-done.10.refs_7_) | copy-start | bytes 1966084
  55.7 0.9 copy-start.19
  56.6 2.2 %copy-start.16 = (s32[4,3]{1,0:T(4,128)S(1)}, s32[4,3]{1,0:T(4,128)}, u32[]{:S(2)}) copy-start(s32[4,3]{1,0:T(4,128)} %param.10) | copy-start | bytes 148
  56.6 2.3 %copy-start.22 = (s32[4]{0:T(128)S(1)}, s32[4]{0:T(128)}, u32[]{:S(2)}) copy-start(s32[4]{0:T(128)} %param.11) | copy-start | bytes 52
  56.8 23.4 %collective-permute-start.11 = (bf16[3,2,128,1280]{3,2,1,0:T(8,128)(2,1)S(1)}, bf16[3,2,128,1280]{3,2,1,0:T(8,128)(2,1)}, u32[]{:S(2)}, u32[]{:S(2)}) collective-permute-start(bf16[3,2,128,1280]{3,2,1,0:T(8,128)(2,1)S(1)} %pad_maximum_fusion.1), channel_id=1, source_target_pairs={{0,1},{1,0},{2,3},{3,2},{4,5},{5,4},{6,7},{7,6},{8,9},{9,8},{10,11... | collective-permute-start | bytes 5898248 | tf_op jit(solution)/shard_map/ppermute | solution.py:16
  59.1 21.1 %collective-permute-start.12 = (bf16[2,128,1280]{2,1,0:T(8,128)(2,1)S(1)}, bf16[2,128,1280]{2,1,0:T(8,128)(2,1)}, u32[]{:S(2)}, u32[]{:S(2)}) collective-permute-start(bf16[2,128,1280]{2,1,0:T(8,128)(2,1)S(1)} %collective-permute-done.5.refs_2_), channel_id=1, source_target_pairs={{0,5},{3,6},{4,9},{7,10},{8,13},{11,14},{16,21},{19,22},{20,25},{2... | collective-permute-start | bytes 1966088 | tf_op jit(solution)/shard_map/ppermute | solution.py:16
  63.4 16.9 %collective-permute-start.13 = (bf16[2,128,1280]{2,1,0:T(8,128)(2,1)S(1)}, bf16[2,128,1280]{2,1,0:T(8,128)(2,1)}, u32[]{:S(2)}, u32[]{:S(2)}) collective-permute-start(bf16[2,128,1280]{2,1,0:T(8,128)(2,1)S(1)} %collective-permute-done.5.refs_2_), channel_id=1, source_target_pairs={{4,1},{7,2},{8,5},{11,6},{12,9},{15,10},{20,17},{23,18},{24,21},{2... | collective-permute-start | bytes 1966088 | tf_op jit(solution)/shard_map/ppermute | solution.py:16
  80.3 19.7 %copy-start.3 = (bf16[2,128,1280]{2,1,0:T(8,128)(2,1)S(1)}, bf16[2,128,1280]{2,1,0:T(8,128)(2,1)}, u32[]{:S(2)}) copy-start(bf16[2,128,1280]{2,1,0:T(8,128)(2,1)} %get-tuple-element.140) | copy-start | bytes 1966084
  80.3 17.2 %collective-permute-start.14 = (bf16[4,2,128,1280]{3,2,1,0:T(8,128)(2,1)}, bf16[4,2,128,1280]{3,2,1,0:T(8,128)(2,1)S(1)}, u32[]{:S(2)}, u32[]{:S(2)}) collective-permute-start(bf16[4,2,128,1280]{3,2,1,0:T(8,128)(2,1)} %get-tuple-element.107), channel_id=1, source_target_pairs={{0,1},{1,0},{2,3},{3,2},{4,5},{5,4},{6,7},{7,6},{8,9},{9,8},{10,11... | collective-permute-start | bytes 7864328 | tf_op jit(solution)/shard_map/ppermute | solution.py:16
  80.3 17.1 %collective-permute-start.15 = (bf16[2,128,1280]{2,1,0:T(8,128)(2,1)}, bf16[2,128,1280]{2,1,0:T(8,128)(2,1)}, u32[]{:S(2)}, u32[]{:S(2)}) collective-permute-start(bf16[2,128,1280]{2,1,0:T(8,128)(2,1)} %get-tuple-element.108), channel_id=1, source_target_pairs={{5,0},{6,3},{9,4},{10,7},{13,8},{14,11},{21,16},{22,19},{25,20},{2... | collective-permute-start | bytes 1966088 | tf_op jit(solution)/shard_map/ppermute | solution.py:16
  81.8 15.7 %collective-permute-start.16 = (bf16[2,128,1280]{2,1,0:T(8,128)(2,1)}, bf16[2,128,1280]{2,1,0:T(8,128)(2,1)}, u32[]{:S(2)}, u32[]{:S(2)}) collective-permute-start(bf16[2,128,1280]{2,1,0:T(8,128)(2,1)} %get-tuple-element.109), channel_id=1, source_target_pairs={{1,4},{2,7},{5,8},{6,11},{9,12},{10,15},{17,20},{18,23},{21,24},{2... | collective-permute-start | bytes 1966088 | tf_op jit(solution)/shard_map/ppermute | solution.py:16
  97.5 12.6 %copy-start.21 = (bf16[2,128,1280]{2,1,0:T(8,128)(2,1)S(1)}, bf16[2,128,1280]{2,1,0:T(8,128)(2,1)}, u32[]{:S(2)}) copy-start(bf16[2,128,1280]{2,1,0:T(8,128)(2,1)} %get-tuple-element.135) | copy-start | bytes 1966084
  97.5 21.9 %copy-start.20 = (bf16[2,128,1280]{2,1,0:T(8,128)(2,1)S(1)}, bf16[2,128,1280]{2,1,0:T(8,128)(2,1)}, u32[]{:S(2)}) copy-start(bf16[2,128,1280]{2,1,0:T(8,128)(2,1)} %get-tuple-element.136) | copy-start | bytes 1966084
  97.5 27.3 %copy-start.13 = (bf16[2,128,1280]{2,1,0:T(8,128)(2,1)S(1)}, bf16[2,128,1280]{2,1,0:T(8,128)(2,1)}, u32[]{:S(2)}) copy-start(bf16[2,128,1280]{2,1,0:T(8,128)(2,1)} %get-tuple-element.139) | copy-start | bytes 1966084
  97.5 32.4 %collective-permute-start.17 = (bf16[4,2,128,1280]{3,2,1,0:T(8,128)(2,1)}, bf16[4,2,128,1280]{3,2,1,0:T(8,128)(2,1)S(1)}, u32[]{:S(2)}, u32[]{:S(2)}) collective-permute-start(bf16[4,2,128,1280]{3,2,1,0:T(8,128)(2,1)} %get-tuple-element.134), channel_id=1, source_target_pairs={{0,1},{1,0},{2,3},{3,2},{4,5},{5,4},{6,7},{7,6},{8,9},{9,8},{10,11... | collective-permute-start | bytes 7864328 | tf_op jit(solution)/shard_map/ppermute | solution.py:16
  102.3 17.0 %collective-permute-start.20 = (bf16[2,128,1280]{2,1,0:T(8,128)(2,1)S(1)}, bf16[2,128,1280]{2,1,0:T(8,128)(2,1)S(1)}, u32[]{:S(2)}, u32[]{:S(2)}) collective-permute-start(bf16[2,128,1280]{2,1,0:T(8,128)(2,1)S(1)} %get-tuple-element.160), channel_id=1, source_target_pairs={{0,2},{1,3},{2,0},{3,1},{4,6},{5,7},{6,4},{7,5},{8,10},{9,11},{10,... | collective-permute-start | bytes 1966088 | tf_op jit(solution)/shard_map/ppermute | solution.py:16
  104.1 19.5 %collective-permute-start.21 = (bf16[2,128,1280]{2,1,0:T(8,128)(2,1)S(1)}, bf16[2,128,1280]{2,1,0:T(8,128)(2,1)S(1)}, u32[]{:S(2)}, u32[]{:S(2)}) collective-permute-start(bf16[2,128,1280]{2,1,0:T(8,128)(2,1)S(1)} %get-tuple-element.162), channel_id=1, source_target_pairs={{4,0},{5,1},{6,2},{7,3},{8,4},{9,5},{10,6},{11,7},{12,8},{13,9},{1... | collective-permute-start | bytes 1966088 | tf_op jit(solution)/shard_map/ppermute | solution.py:16
  105.3 24.6 %copy-start = (bf16[2,128,1280]{2,1,0:T(8,128)(2,1)S(1)}, bf16[2,128,1280]{2,1,0:T(8,128)(2,1)}, u32[]{:S(2)}) copy-start(bf16[2,128,1280]{2,1,0:T(8,128)(2,1)} %get-tuple-element.152) | copy-start | bytes 1966084
  105.4 24.6 %copy-start.1 = (bf16[2,128,1280]{2,1,0:T(8,128)(2,1)S(1)}, bf16[2,128,1280]{2,1,0:T(8,128)(2,1)}, u32[]{:S(2)}) copy-start(bf16[2,128,1280]{2,1,0:T(8,128)(2,1)} %get-tuple-element.155) | copy-start | bytes 1966084
  105.4 24.6 %copy-start.2 = (bf16[2,128,1280]{2,1,0:T(8,128)(2,1)S(1)}, bf16[2,128,1280]{2,1,0:T(8,128)(2,1)}, u32[]{:S(2)}) copy-start(bf16[2,128,1280]{2,1,0:T(8,128)(2,1)} %get-tuple-element.156) | copy-start | bytes 1966084
  105.4 19.4 %collective-permute-start.22 = (bf16[2,128,1280]{2,1,0:T(8,128)(2,1)S(1)}, bf16[2,128,1280]{2,1,0:T(8,128)(2,1)S(1)}, u32[]{:S(2)}, u32[]{:S(2)}) collective-permute-start(bf16[2,128,1280]{2,1,0:T(8,128)(2,1)S(1)} %get-tuple-element.161), channel_id=1, source_target_pairs={{0,4},{1,5},{2,6},{3,7},{4,8},{5,9},{6,10},{7,11},{8,12},{9,13},{1... | collective-permute-start | bytes 1966088 | tf_op jit(solution)/shard_map/ppermute | solution.py:16
  110.1 19.8 %collective-permute-start.18 = (bf16[2,128,1280]{2,1,0:T(8,128)(2,1)S(1)}, bf16[2,128,1280]{2,1,0:T(8,128)(2,1)S(1)}, u32[]{:S(2)}, u32[]{:S(2)}) collective-permute-start(bf16[2,128,1280]{2,1,0:T(8,128)(2,1)S(1)} %copy-done.21), channel_id=1, source_target_pairs={{5,0},{6,3},{9,4},{10,7},{13,8},{14,11},{21,16},{22,19},{25,20},{2... | collective-permute-start | bytes 1966088 | tf_op jit(solution)/shard_map/ppermute | solution.py:16
  119.3 10.6 %collective-permute-start.19 = (bf16[2,128,1280]{2,1,0:T(8,128)(2,1)S(1)}, bf16[2,128,1280]{2,1,0:T(8,128)(2,1)S(1)}, u32[]{:S(2)}, u32[]{:S(2)}) collective-permute-start(bf16[2,128,1280]{2,1,0:T(8,128)(2,1)S(1)} %copy-done.20), channel_id=1, source_target_pairs={{1,4},{2,7},{5,8},{6,11},{9,12},{10,15},{17,20},{18,23},{21,24},{2... | collective-permute-start | bytes 1966088 | tf_op jit(solution)/shard_map/ppermute | solution.py:16
  125.2 13.7 %copy-start.14 = (bf16[128,1280]{1,0:T(8,128)(2,1)S(1)}, bf16[128,1280]{1,0:T(8,128)(2,1)}, u32[]{:S(2)}) copy-start(bf16[128,1280]{1,0:T(8,128)(2,1)} %get-tuple-element.147) | copy-start | bytes 983044
  125.2 13.7 %copy-start.15 = (bf16[128,1280]{1,0:T(8,128)(2,1)S(1)}, bf16[128,1280]{1,0:T(8,128)(2,1)}, u32[]{:S(2)}) copy-start(bf16[128,1280]{1,0:T(8,128)(2,1)} %get-tuple-element.148) | copy-start | bytes 983044
  130.6 17.6 %collective-permute-start.23 = (bf16[2,128,1280]{2,1,0:T(8,128)(2,1)S(1)}, bf16[2,128,1280]{2,1,0:T(8,128)(2,1)S(1)}, u32[]{:S(2)}, u32[]{:S(2)}) collective-permute-start(bf16[2,128,1280]{2,1,0:T(8,128)(2,1)S(1)} %get-tuple-element.157), channel_id=1, source_target_pairs={{0,2},{1,3},{2,0},{3,1},{4,6},{5,7},{6,4},{7,5},{8,10},{9,11},{10,... | collective-permute-start | bytes 1966088 | tf_op jit(solution)/shard_map/ppermute | solution.py:16
  132.9 18.8 %collective-permute-start.24 = (bf16[2,128,1280]{2,1,0:T(8,128)(2,1)S(1)}, bf16[2,128,1280]{2,1,0:T(8,128)(2,1)S(1)}, u32[]{:S(2)}, u32[]{:S(2)}) collective-permute-start(bf16[2,128,1280]{2,1,0:T(8,128)(2,1)S(1)} %get-tuple-element.159), channel_id=1, source_target_pairs={{4,0},{5,1},{6,2},{7,3},{8,4},{9,5},{10,6},{11,7},{12,8},{13,9},{1... | collective-permute-start | bytes 1966088 | tf_op jit(solution)/shard_map/ppermute | solution.py:16
  134.2 18.9 %copy-start.12 = (bf16[2,128,1280]{2,1,0:T(8,128)(2,1)S(1)}, bf16[2,128,1280]{2,1,0:T(8,128)(2,1)}, u32[]{:S(2)}) copy-start(bf16[2,128,1280]{2,1,0:T(8,128)(2,1)} %get-tuple-element.150) | copy-start | bytes 1966084
  134.2 18.8 %collective-permute-start.25 = (bf16[2,128,1280]{2,1,0:T(8,128)(2,1)S(1)}, bf16[2,128,1280]{2,1,0:T(8,128)(2,1)S(1)}, u32[]{:S(2)}, u32[]{:S(2)}) collective-permute-start(bf16[2,128,1280]{2,1,0:T(8,128)(2,1)S(1)} %get-tuple-element.158), channel_id=1, source_target_pairs={{0,4},{1,5},{2,6},{3,7},{4,8},{5,9},{6,10},{7,11},{8,12},{9,13},{1... | collective-permute-start | bytes 1966088 | tf_op jit(solution)/shard_map/ppermute | solution.py:16

commit v11 on v7

--- a/solution.py
+++ b/solution.py
@@ -244,16 +244,12 @@
         dq, parts = chunk_kernel(forward_mask, queries, out_grad, seconds[c], first // HD, inv_root)
         dqs.append(dq)
         outs.append(parts)
-    for c in range(len(starts)):
-        backs.append(return_first(outs[c], count, None))
-    got = None
-    for c in range(len(starts)):
-        got, summed = return_second(outs[c], backs[c], count, None)
-        sums.append(summed)
-    grads = [(dqs[c], sums[c][0].astype(jnp.bfloat16), sums[c][1].astype(jnp.bfloat16)) for c in range(len(starts))]
-    query_grad = jnp.concatenate([grad[0] for grad in grads], axis=1)
-    key_grad = jnp.concatenate([grad[1] for grad in grads], axis=1)
-    value_grad = jnp.concatenate([grad[2] for grad in grads], axis=1)
+    joined = [jnp.concatenate([part[i] for part in outs], axis=-1) for i in range(len(outs[0]))]
+    back_all = return_first(joined, count, None)
+    summed = return_second(joined, back_all, count, None)[1]
+    query_grad = jnp.concatenate(dqs, axis=1)
+    key_grad = summed[0].astype(jnp.bfloat16)
+    value_grad = summed[1].astype(jnp.bfloat16)
     return (query_grad, key_grad, value_grad)
 
 

time: 146 us -> 155 us (1.062)
  waiting for transfers between devices: 54.5 us -> 72.8 us
  starting transfers between devices: 47.2 us -> 36.8 us
  local copies, waits for them, and re-layouts: 1.6 us -> 3.63 us
    ppermute x26 -> x20, waiting for transfers between devices: 54.5 us -> 72.8 us  [send(): return lax.ppermute(value, 'tm', pairs)]
    ppermute x26 -> x20, starting transfers between devices: 47.2 us -> 36.8 us  [send(): return lax.ppermute(value, 'tm', pairs)]
    concatenate x3 -> x4, other arithmetic: 3.71 us -> 3.32 us  [the longest x3 2.44 us: body(): jnp.concatenate([part[i] for part in outs], axis=-1)]
  transfers between devices with their start and end apart: 26 -> 20, of which waited for: 15 -> 10; matrix products, arithmetic and copies ran while one was open for 7% -> 5% of each run, Pallas kernels for 19% -> 9%
where the time goes in v11:
time: 155 us
  waiting for transfers between devices  72.8 us (47%)
  starting transfers between devices  36.8 us (24%)
  Pallas kernels  28.2 us (18%)
  other arithmetic  12 us (8%)
  local copies, waits for them, and re-layouts  3.63 us (2%)
    ppermute x20, waiting for transfers between devices, send(): return lax.ppermute(value, 'tm', pairs)  72.8 us
    ppermute x20, starting transfers between devices, send(): return lax.ppermute(value, 'tm', pairs)  36.8 us
    pallas_call x2, Pallas kernels, attention_backward(): pl.pallas_call(kernel, grid=(heads // STEP_HEADS,), in_specs=in_specs, ou...  28.2 us
    another operation x2, other arithmetic, forward_second(): ahead = jnp.stack([from_cross, from_below, from_above])  4.72 us
  transfers between devices with their start and end apart: 20, of which 10 were waited for; matrix products, arithmetic and copies ran while one was open for 5% of the time, Pallas kernels for 9%

profile of v11, /device:TPU:0, one launch (start us, length us, event | category | flops | bytes accessed | tf_op | source)
XLA Modules:
  0.0 154.6 jit_solution(9523948747368971535)
XLA Ops:
  0.6 1.4 slice_bitcast_fusion.8
  2.0 0.1 pad_maximum_fusion.6.refs_0_
  2.1 0.0 copy-start.12
  2.1 1.3 collective-permute-start.10
  3.4 5.6 %collective-permute-start.9 = (bf16[2,128,1280]{2,1,0:T(8,128)(2,1)S(1)}, bf16[2,128,1280]{2,1,0:T(8,128)(2,1)S(1)}, u32[]{:S(2)}, u32[]{:S(2)}) collective-permute-start(bf16[2,128,1280]{2,1,0:T(8,128)(2,1)S(1)} %pad_maximum_fusion.6.refs_0_), channel_id=1, source_target_pairs={{0,4},{1,5},{2,6},{3,7},{4,8},{5,9},{6,10},{7,11},{8,12},{9,13},{1... | collective-permute-start | bytes 1966088 | tf_op jit(solution)/shard_map/ppermute | solution.py:16
  9.0 2.0 %collective-permute-start.8 = (bf16[2,128,1280]{2,1,0:T(8,128)(2,1)S(1)}, bf16[2,128,1280]{2,1,0:T(8,128)(2,1)S(1)}, u32[]{:S(2)}, u32[]{:S(2)}) collective-permute-start(bf16[2,128,1280]{2,1,0:T(8,128)(2,1)S(1)} %pad_maximum_fusion.6.refs_0_), channel_id=1, source_target_pairs={{0,2},{1,3},{2,0},{3,1},{4,6},{5,7},{6,4},{7,5},{8,10},{9,11},{10,... | collective-permute-start | bytes 1966088 | tf_op jit(solution)/shard_map/ppermute | solution.py:16
  11.0 0.1 pad_maximum_fusion.5.refs_0_
  11.1 0.0 copy-start.11
  11.1 1.3 collective-permute-start.3
  12.4 5.4 %collective-permute-start.2 = (bf16[2,128,1280]{2,1,0:T(8,128)(2,1)S(1)}, bf16[2,128,1280]{2,1,0:T(8,128)(2,1)}, u32[]{:S(2)}, u32[]{:S(2)}) collective-permute-start(bf16[2,128,1280]{2,1,0:T(8,128)(2,1)S(1)} %pad_maximum_fusion.5.refs_0_), channel_id=1, source_target_pairs={{0,4},{1,5},{2,6},{3,7},{4,8},{5,9},{6,10},{7,11},{8,12},{9,13},{1... | collective-permute-start | bytes 1966088 | tf_op jit(solution)/shard_map/ppermute | solution.py:16
  17.9 4.7 %collective-permute-done.10.refs_4_ = bf16[2,128,1280]{2,1,0:T(8,128)(2,1)S(1)} collective-permute-done((bf16[2,128,1280]{2,1,0:T(8,128)(2,1)S(1)}, bf16[2,128,1280]{2,1,0:T(8,128)(2,1)S(1)}, u32[]{:S(2)}, u32[]{:S(2)}) %collective-permute-start.10) | collective-permute-done | bytes 655392 | tf_op jit(solution)/shard_map/ppermute | solution.py:16
  22.6 2.0 %collective-permute-start.1 = (bf16[2,128,1280]{2,1,0:T(8,128)(2,1)S(1)}, bf16[2,128,1280]{2,1,0:T(8,128)(2,1)}, u32[]{:S(2)}, u32[]{:S(2)}) collective-permute-start(bf16[2,128,1280]{2,1,0:T(8,128)(2,1)S(1)} %pad_maximum_fusion.5.refs_0_), channel_id=1, source_target_pairs={{0,2},{1,3},{2,0},{3,1},{4,6},{5,7},{6,4},{7,5},{8,10},{9,11},{10,... | collective-permute-start | bytes 1966088 | tf_op jit(solution)/shard_map/ppermute | solution.py:16
  24.6 0.0 collective-permute-done.9.refs_3_
  24.6 0.1 collective-permute-start.7
  24.7 2.0 %collective-permute-done.8.refs_2_ = bf16[2,128,1280]{2,1,0:T(8,128)(2,1)S(1)} collective-permute-done((bf16[2,128,1280]{2,1,0:T(8,128)(2,1)S(1)}, bf16[2,128,1280]{2,1,0:T(8,128)(2,1)S(1)}, u32[]{:S(2)}, u32[]{:S(2)}) %collective-permute-start.8) | collective-permute-done | bytes 655392 | tf_op jit(solution)/shard_map/ppermute | solution.py:16
  26.7 0.8 copy-done.15
  27.5 1.7 %pad_maximum_fusion.2 = bf16[3,2,128,1280]{3,2,1,0:T(8,128)(2,1)S(1)} fusion(bf16[1,2,128,1280]{3,2,1,0:T(8,128)(2,1)} %bitcast.44, bf16[1,2,128,1280]{3,2,1,0:T(8,128)(2,1)} %bitcast.45, bf16[1,2,128,1280]{3,2,1,0:T(8,128)(2,1)} %bitcast.46), kind=kLoop, calls=%fused_computation.15 | loop fusion | flops 1966080 | bytes 3932160 | tf_op jit(solution)/shard_map/stack | solution.py:156
  29.2 0.1 collective-permute-start.11
  29.3 6.6 %collective-permute-done.3.refs_4_ = bf16[2,128,1280]{2,1,0:T(8,128)(2,1)} collective-permute-done((bf16[2,128,1280]{2,1,0:T(8,128)(2,1)S(1)}, bf16[2,128,1280]{2,1,0:T(8,128)(2,1)}, u32[]{:S(2)}, u32[]{:S(2)}) %collective-permute-start.3) | collective-permute-done | bytes 655392 | tf_op jit(solution)/shard_map/ppermute | solution.py:16
  35.9 1.1 collective-permute-done.2.refs_3_
  37.0 2.4 %collective-permute-done.1.refs_2_ = bf16[2,128,1280]{2,1,0:T(8,128)(2,1)} collective-permute-done((bf16[2,128,1280]{2,1,0:T(8,128)(2,1)S(1)}, bf16[2,128,1280]{2,1,0:T(8,128)(2,1)}, u32[]{:S(2)}, u32[]{:S(2)}) %collective-permute-start.1) | collective-permute-done | bytes 655392 | tf_op jit(solution)/shard_map/ppermute | solution.py:16
  39.4 3.0 %pad_maximum_fusion.1 = bf16[3,2,128,1280]{3,2,1,0:T(8,128)(2,1)} fusion(bf16[1,2,128,1280]{3,2,1,0:T(8,128)(2,1)} %bitcast.7, bf16[1,2,128,1280]{3,2,1,0:T(8,128)(2,1)} %bitcast.6, bf16[1,2,128,1280]{3,2,1,0:T(8,128)(2,1)} %bitcast.5), kind=kLoop, calls=%fused_computation.14 | loop fusion | flops 1966080 | bytes 3932160 | tf_op jit(solution)/shard_map/stack | solution.py:156
  42.5 0.0 collective-permute-start.4
  42.5 0.1 copy.9
  42.6 0.1 select_reduce_fusion
  42.7 0.1 multiply_reduce_fusion
  42.8 1.5 collective-permute-start.13
  44.3 4.3 %collective-permute-start.12 = (bf16[2,128,1280]{2,1,0:T(8,128)(2,1)}, bf16[2,128,1280]{2,1,0:T(8,128)(2,1)}, u32[]{:S(2)}, u32[]{:S(2)}) collective-permute-start(bf16[2,128,1280]{2,1,0:T(8,128)(2,1)} %copy-done.15), channel_id=1, source_target_pairs={{0,5},{3,6},{4,9},{7,10},{8,13},{11,14},{16,21},{19,22},{20,25},{2... | collective-permute-start | bytes 1966088 | tf_op jit(solution)/shard_map/ppermute | solution.py:16
  48.6 0.0 collective-permute-done.7.refs_1_
  48.7 0.1 collective-permute-start
  48.7 0.0 collective-permute-done.13.refs_7_
  48.8 1.5 collective-permute-start.6
  50.3 5.9 %collective-permute-done.12.refs_6_ = bf16[2,128,1280]{2,1,0:T(8,128)(2,1)} collective-permute-done((bf16[2,128,1280]{2,1,0:T(8,128)(2,1)}, bf16[2,128,1280]{2,1,0:T(8,128)(2,1)}, u32[]{:S(2)}, u32[]{:S(2)}) %collective-permute-start.12) | collective-permute-done | bytes 655392 | tf_op jit(solution)/shard_map/ppermute | solution.py:16
  56.2 4.7 %collective-permute-start.5 = (bf16[2,128,1280]{2,1,0:T(8,128)(2,1)}, bf16[2,128,1280]{2,1,0:T(8,128)(2,1)}, u32[]{:S(2)}, u32[]{:S(2)}) collective-permute-start(bf16[2,128,1280]{2,1,0:T(8,128)(2,1)} %collective-permute-done.1.refs_2_), channel_id=1, source_target_pairs={{0,5},{3,6},{4,9},{7,10},{8,13},{11,14},{16,21},{19,22},{20,25},{2... | collective-permute-start | bytes 1966088 | tf_op jit(solution)/shard_map/ppermute | solution.py:16
  60.8 1.4 fusion.15.mask_ref
  62.2 0.0 collective-permute-done.11.refs_5_
  62.2 14.1 %shard_map.86 = (bf16[128,1280]{1,0:T(8,128)(2,1)}, bf16[2,128,1280]{2,1,0:T(8,128)(2,1)}, bf16[4,2,128,1280]{3,2,1,0:T(8,128)(2,1)}, bf16[2,128,1280]{2,1,0:T(8...) custom-call(s32[128,1280]{1,0:T(8,128)} %fusion.15.mask_ref, ...), custom_call_target="tpu_custom_call" | custom-call | flops 2516582400 | bytes 14745600 | tf_op jit(solution)/shard_map/pallas_call | solution.py:127
  76.3 0.0 collective-permute-done.refs_1_
  76.4 0.0 collective-permute-done.6.refs_7_
  76.4 0.0 collective-permute-done.5.refs_6_
  76.4 0.0 collective-permute-done.4.refs_5_
  76.4 14.1 %shard_map.85 = (bf16[128,1280]{1,0:T(8,128)(2,1)}, bf16[2,128,1280]{2,1,0:T(8,128)(2,1)}, bf16[4,2,128,1280]{3,2,1,0:T(8,128)(2,1)}, bf16[2,128,1280]{2,1,0:T(8...) custom-call(s32[128,1280]{1,0:T(8,128)} %fusion.15.mask_ref, ...), custom_call_target="tpu_custom_call" | custom-call | flops 2516582400 | bytes 14745600 | tf_op jit(solution)/shard_map/pallas_call | solution.py:127
  90.5 2.3 %pad_maximum_fusion = bf16[4,2,128,2560]{3,2,1,0:T(8,128)(2,1)S(1)} fusion(bf16[4,2,128,1280]{3,2,1,0:T(8,128)(2,1)S(1)} %copy-done, bf16[4,2,128,1280]{3,2,1,0:T(8,128)(2,1)} %get-tuple-element.23), kind=kLoop, calls=%fused_computation | loop fusion | flops 10485760 | bytes 10485760 | tf_op jit(solution)/shard_map/concatenate | solution.py:247
  92.8 0.1 collective-permute-start.14
  92.9 0.1 pad_maximum_fusion.4
  93.1 0.0 copy-start.4
  93.1 0.9 collective-permute-start.16
  94.0 0.1 copy-done.9
  94.1 0.1 pad_maximum_fusion.3
  94.2 1.4 collective-permute-start.15
  95.6 0.0 collective-permute-done.16
  95.6 19.0 %collective-permute-done.15 = bf16[2,128,2560]{2,1,0:T(8,128)(2,1)S(1)} collective-permute-done((bf16[2,128,2560]{2,1,0:T(8,128)(2,1)S(1)}, bf16[2,128,2560]{2,1,0:T(8,128)(2,1)S(1)}, u32[]{:S(2)}, u32[]{:S(2)}) %collective-permute-start.15) | collective-permute-done | bytes 1310752 | tf_op jit(solution)/shard_map/ppermute | solution.py:16
  114.6 0.0 collective-permute-done.14
  114.7 0.0 copy-start.17
  114.7 1.3 fusion.4
  116.0 0.1 collective-permute-start.17
  116.1 3.2 %collective-permute-start.19 = (bf16[2,128,2560]{2,1,0:T(8,128)(2,1)S(1)}, bf16[2,128,2560]{2,1,0:T(8,128)(2,1)S(1)}, u32[]{:S(2)}, u32[]{:S(2)}) collective-permute-start(bf16[2,128,2560]{2,1,0:T(8,128)(2,1)S(1)} %get-tuple-element.36), channel_id=1, source_target_pairs={{0,4},{1,5},{2,6},{3,7},{4,8},{5,9},{6,10},{7,11},{8,12},{9,13},{1... | collective-permute-start | bytes 3932168 | tf_op jit(solution)/shard_map/ppermute | solution.py:16
  119.3 1.3 collective-permute-start.18
  120.6 0.9 pad_maximum_fusion.7
  121.5 25.0 %collective-permute-done.17 = bf16[2,128,2560]{2,1,0:T(8,128)(2,1)S(1)} collective-permute-done((bf16[2,128,2560]{2,1,0:T(8,128)(2,1)S(1)}, bf16[2,128,2560]{2,1,0:T(8,128)(2,1)S(1)}, u32[]{:S(2)}, u32[]{:S(2)}) %collective-permute-start.17) | collective-permute-done | bytes 1310752 | tf_op jit(solution)/shard_map/ppermute | solution.py:16
  146.6 1.8 %collective-permute-done.19 = bf16[2,128,2560]{2,1,0:T(8,128)(2,1)S(1)} collective-permute-done((bf16[2,128,2560]{2,1,0:T(8,128)(2,1)S(1)}, bf16[2,128,2560]{2,1,0:T(8,128)(2,1)S(1)}, u32[]{:S(2)}, u32[]{:S(2)}) %collective-permute-start.19) | collective-permute-done | bytes 1310752 | tf_op jit(solution)/shard_map/ppermute | solution.py:16
  148.4 4.2 %collective-permute-done.18 = bf16[2,128,2560]{2,1,0:T(8,128)(2,1)S(1)} collective-permute-done((bf16[2,128,2560]{2,1,0:T(8,128)(2,1)S(1)}, bf16[2,128,2560]{2,1,0:T(8,128)(2,1)S(1)}, u32[]{:S(2)}, u32[]{:S(2)}) %collective-permute-start.18) | collective-permute-done | bytes 1310752 | tf_op jit(solution)/shard_map/ppermute | solution.py:16
  152.6 0.8 fusion.8
  153.4 1.1 slice_bitcast_fusion.4
  (55 shorter events, 0.2 us)
Async XLA Ops:
  2.1 27.2 %copy-start.12 = (bf16[2,128,1280]{2,1,0:T(8,128)(2,1)}, bf16[2,128,1280]{2,1,0:T(8,128)(2,1)S(1)}, u32[]{:S(2)}) copy-start(bf16[2,128,1280]{2,1,0:T(8,128)(2,1)S(1)} %pad_maximum_fusion.6.refs_0_) | copy-start | bytes 1966084
  2.1 20.5 %collective-permute-start.10 = (bf16[2,128,1280]{2,1,0:T(8,128)(2,1)S(1)}, bf16[2,128,1280]{2,1,0:T(8,128)(2,1)S(1)}, u32[]{:S(2)}, u32[]{:S(2)}) collective-permute-start(bf16[2,128,1280]{2,1,0:T(8,128)(2,1)S(1)} %pad_maximum_fusion.6.refs_0_), channel_id=1, source_target_pairs={{4,0},{5,1},{6,2},{7,3},{8,4},{9,5},{10,6},{11,7},{12,8},{13,9},{1... | collective-permute-start | bytes 1966088 | tf_op jit(solution)/shard_map/ppermute | solution.py:16
  3.4 21.2 %collective-permute-start.9 = (bf16[2,128,1280]{2,1,0:T(8,128)(2,1)S(1)}, bf16[2,128,1280]{2,1,0:T(8,128)(2,1)S(1)}, u32[]{:S(2)}, u32[]{:S(2)}) collective-permute-start(bf16[2,128,1280]{2,1,0:T(8,128)(2,1)S(1)} %pad_maximum_fusion.6.refs_0_), channel_id=1, source_target_pairs={{0,4},{1,5},{2,6},{3,7},{4,8},{5,9},{6,10},{7,11},{8,12},{9,13},{1... | collective-permute-start | bytes 1966088 | tf_op jit(solution)/shard_map/ppermute | solution.py:16
  9.0 17.7 %collective-permute-start.8 = (bf16[2,128,1280]{2,1,0:T(8,128)(2,1)S(1)}, bf16[2,128,1280]{2,1,0:T(8,128)(2,1)S(1)}, u32[]{:S(2)}, u32[]{:S(2)}) collective-permute-start(bf16[2,128,1280]{2,1,0:T(8,128)(2,1)S(1)} %pad_maximum_fusion.6.refs_0_), channel_id=1, source_target_pairs={{0,2},{1,3},{2,0},{3,1},{4,6},{5,7},{6,4},{7,5},{8,10},{9,11},{10,... | collective-permute-start | bytes 1966088 | tf_op jit(solution)/shard_map/ppermute | solution.py:16
  11.1 37.6 %copy-start.11 = (bf16[2,128,1280]{2,1,0:T(8,128)(2,1)}, bf16[2,128,1280]{2,1,0:T(8,128)(2,1)S(1)}, u32[]{:S(2)}) copy-start(bf16[2,128,1280]{2,1,0:T(8,128)(2,1)S(1)} %pad_maximum_fusion.5.refs_0_) | copy-start | bytes 1966084
  11.1 24.8 %collective-permute-start.3 = (bf16[2,128,1280]{2,1,0:T(8,128)(2,1)S(1)}, bf16[2,128,1280]{2,1,0:T(8,128)(2,1)}, u32[]{:S(2)}, u32[]{:S(2)}) collective-permute-start(bf16[2,128,1280]{2,1,0:T(8,128)(2,1)S(1)} %pad_maximum_fusion.5.refs_0_), channel_id=1, source_target_pairs={{4,0},{5,1},{6,2},{7,3},{8,4},{9,5},{10,6},{11,7},{12,8},{13,9},{1... | collective-permute-start | bytes 1966088 | tf_op jit(solution)/shard_map/ppermute | solution.py:16
  12.4 24.6 %collective-permute-start.2 = (bf16[2,128,1280]{2,1,0:T(8,128)(2,1)S(1)}, bf16[2,128,1280]{2,1,0:T(8,128)(2,1)}, u32[]{:S(2)}, u32[]{:S(2)}) collective-permute-start(bf16[2,128,1280]{2,1,0:T(8,128)(2,1)S(1)} %pad_maximum_fusion.5.refs_0_), channel_id=1, source_target_pairs={{0,4},{1,5},{2,6},{3,7},{4,8},{5,9},{6,10},{7,11},{8,12},{9,13},{1... | collective-permute-start | bytes 1966088 | tf_op jit(solution)/shard_map/ppermute | solution.py:16
  22.6 4.1 %copy-start.13 = (bf16[2,128,1280]{2,1,0:T(8,128)(2,1)}, bf16[2,128,1280]{2,1,0:T(8,128)(2,1)S(1)}, u32[]{:S(2)}) copy-start(bf16[2,128,1280]{2,1,0:T(8,128)(2,1)S(1)} %collective-permute-done.10.refs_4_) | copy-start | bytes 1966084
  22.6 16.8 %collective-permute-start.1 = (bf16[2,128,1280]{2,1,0:T(8,128)(2,1)S(1)}, bf16[2,128,1280]{2,1,0:T(8,128)(2,1)}, u32[]{:S(2)}, u32[]{:S(2)}) collective-permute-start(bf16[2,128,1280]{2,1,0:T(8,128)(2,1)S(1)} %pad_maximum_fusion.5.refs_0_), channel_id=1, source_target_pairs={{0,2},{1,3},{2,0},{3,1},{4,6},{5,7},{6,4},{7,5},{8,10},{9,11},{10,... | collective-permute-start | bytes 1966088 | tf_op jit(solution)/shard_map/ppermute | solution.py:16
  24.6 2.1 %copy-start.14 = (bf16[2,128,1280]{2,1,0:T(8,128)(2,1)}, bf16[2,128,1280]{2,1,0:T(8,128)(2,1)S(1)}, u32[]{:S(2)}) copy-start(bf16[2,128,1280]{2,1,0:T(8,128)(2,1)S(1)} %collective-permute-done.9.refs_3_) | copy-start | bytes 1966084
  24.6 24.0 %collective-permute-start.7 = (bf16[2,128,1280]{2,1,0:T(8,128)(2,1)S(1)}, bf16[2,128,1280]{2,1,0:T(8,128)(2,1)}, u32[]{:S(2)}, u32[]{:S(2)}) collective-permute-start(bf16[2,128,1280]{2,1,0:T(8,128)(2,1)S(1)} %pad_maximum_fusion.6.refs_0_), channel_id=1, source_target_pairs={{0,1},{1,0},{2,3},{3,2},{4,5},{5,4},{6,7},{7,6},{8,9},{9,8},{10,11... | collective-permute-start | bytes 1966088 | tf_op jit(solution)/shard_map/ppermute | solution.py:16
  26.7 0.8 copy-start.15
  29.2 33.0 %collective-permute-start.11 = (bf16[3,2,128,1280]{3,2,1,0:T(8,128)(2,1)S(1)}, bf16[3,2,128,1280]{3,2,1,0:T(8,128)(2,1)}, u32[]{:S(2)}, u32[]{:S(2)}) collective-permute-start(bf16[3,2,128,1280]{3,2,1,0:T(8,128)(2,1)S(1)} %pad_maximum_fusion.2), channel_id=1, source_target_pairs={{0,1},{1,0},{2,3},{3,2},{4,5},{5,4},{6,7},{7,6},{8,9},{9,8},{10,11... | collective-permute-start | bytes 5898248 | tf_op jit(solution)/shard_map/ppermute | solution.py:16
  39.4 3.0 %copy-start.20 = (s32[4,3]{1,0:T(4,128)S(1)}, s32[4,3]{1,0:T(4,128)}, u32[]{:S(2)}) copy-start(s32[4,3]{1,0:T(4,128)} %param.10) | copy-start | bytes 148
  39.4 3.2 %copy-start.21 = (s32[4]{0:T(128)S(1)}, s32[4]{0:T(128)}, u32[]{:S(2)}) copy-start(s32[4]{0:T(128)} %param.11) | copy-start | bytes 52
  42.5 33.9 %collective-permute-start.4 = (bf16[3,2,128,1280]{3,2,1,0:T(8,128)(2,1)}, bf16[3,2,128,1280]{3,2,1,0:T(8,128)(2,1)}, u32[]{:S(2)}, u32[]{:S(2)}) collective-permute-start(bf16[3,2,128,1280]{3,2,1,0:T(8,128)(2,1)} %pad_maximum_fusion.1), channel_id=1, source_target_pairs={{0,1},{1,0},{2,3},{3,2},{4,5},{5,4},{6,7},{7,6},{8,9},{9,8},{10,11... | collective-permute-start | bytes 5898248 | tf_op jit(solution)/shard_map/ppermute | solution.py:16
  42.8 6.0 %collective-permute-start.13 = (bf16[2,128,1280]{2,1,0:T(8,128)(2,1)}, bf16[2,128,1280]{2,1,0:T(8,128)(2,1)}, u32[]{:S(2)}, u32[]{:S(2)}) collective-permute-start(bf16[2,128,1280]{2,1,0:T(8,128)(2,1)} %copy-done.15), channel_id=1, source_target_pairs={{4,1},{7,2},{8,5},{11,6},{12,9},{15,10},{20,17},{23,18},{24,21},{2... | collective-permute-start | bytes 1966088 | tf_op jit(solution)/shard_map/ppermute | solution.py:16
  44.3 11.9 %collective-permute-start.12 = (bf16[2,128,1280]{2,1,0:T(8,128)(2,1)}, bf16[2,128,1280]{2,1,0:T(8,128)(2,1)}, u32[]{:S(2)}, u32[]{:S(2)}) collective-permute-start(bf16[2,128,1280]{2,1,0:T(8,128)(2,1)} %copy-done.15), channel_id=1, source_target_pairs={{0,5},{3,6},{4,9},{7,10},{8,13},{11,14},{16,21},{19,22},{20,25},{2... | collective-permute-start | bytes 1966088 | tf_op jit(solution)/shard_map/ppermute | solution.py:16
  48.7 27.7 %collective-permute-start = (bf16[2,128,1280]{2,1,0:T(8,128)(2,1)S(1)}, bf16[2,128,1280]{2,1,0:T(8,128)(2,1)}, u32[]{:S(2)}, u32[]{:S(2)}) collective-permute-start(bf16[2,128,1280]{2,1,0:T(8,128)(2,1)S(1)} %pad_maximum_fusion.5.refs_0_), channel_id=1, source_target_pairs={{0,1},{1,0},{2,3},{3,2},{4,5},{5,4},{6,7},{7,6},{8,9},{9,8},{10,11... | collective-permute-start | bytes 1966088 | tf_op jit(solution)/shard_map/ppermute | solution.py:16
  48.8 27.6 %collective-permute-start.6 = (bf16[2,128,1280]{2,1,0:T(8,128)(2,1)}, bf16[2,128,1280]{2,1,0:T(8,128)(2,1)}, u32[]{:S(2)}, u32[]{:S(2)}) collective-permute-start(bf16[2,128,1280]{2,1,0:T(8,128)(2,1)} %collective-permute-done.1.refs_2_), channel_id=1, source_target_pairs={{4,1},{7,2},{8,5},{11,6},{12,9},{15,10},{20,17},{23,18},{24,21},{2... | collective-permute-start | bytes 1966088 | tf_op jit(solution)/shard_map/ppermute | solution.py:16
  56.2 20.2 %collective-permute-start.5 = (bf16[2,128,1280]{2,1,0:T(8,128)(2,1)}, bf16[2,128,1280]{2,1,0:T(8,128)(2,1)}, u32[]{:S(2)}, u32[]{:S(2)}) collective-permute-start(bf16[2,128,1280]{2,1,0:T(8,128)(2,1)} %collective-permute-done.1.refs_2_), channel_id=1, source_target_pairs={{0,5},{3,6},{4,9},{7,10},{8,13},{11,14},{16,21},{19,22},{20,25},{2... | collective-permute-start | bytes 1966088 | tf_op jit(solution)/shard_map/ppermute | solution.py:16
  76.3 14.2 %copy-start = (bf16[4,2,128,1280]{3,2,1,0:T(8,128)(2,1)S(1)}, bf16[4,2,128,1280]{3,2,1,0:T(8,128)(2,1)}, u32[]{:S(2)}) copy-start(bf16[4,2,128,1280]{3,2,1,0:T(8,128)(2,1)} %get-tuple-element.24) | copy-start | bytes 7864324
  90.5 2.4 %copy-start.8 = (bf16[2,128,1280]{2,1,0:T(8,128)(2,1)S(1)}, bf16[2,128,1280]{2,1,0:T(8,128)(2,1)}, u32[]{:S(2)}) copy-start(bf16[2,128,1280]{2,1,0:T(8,128)(2,1)} %get-tuple-element.30) | copy-start | bytes 1966084
  90.5 2.4 %copy-start.10 = (bf16[2,128,1280]{2,1,0:T(8,128)(2,1)S(1)}, bf16[2,128,1280]{2,1,0:T(8,128)(2,1)}, u32[]{:S(2)}) copy-start(bf16[2,128,1280]{2,1,0:T(8,128)(2,1)} %get-tuple-element.29) | copy-start | bytes 1966084
  92.8 1.2 copy-start.7
  92.8 1.3 copy-start.9
  92.8 21.8 %collective-permute-start.14 = (bf16[4,2,128,2560]{3,2,1,0:T(8,128)(2,1)S(1)}, bf16[4,2,128,2560]{3,2,1,0:T(8,128)(2,1)S(1)}, u32[]{:S(2)}, u32[]{:S(2)}) collective-permute-start(bf16[4,2,128,2560]{3,2,1,0:T(8,128)(2,1)S(1)} %pad_maximum_fusion), channel_id=1, source_target_pairs={{0,1},{1,0},{2,3},{3,2},{4,5},{5,4},{6,7},{7,6},{8,9},{9,8},{10,11... | collective-permute-start | bytes 15728648 | tf_op jit(solution)/shard_map/ppermute | solution.py:16
  92.9 21.7 %copy-start.5 = (bf16[2,128,1280]{2,1,0:T(8,128)(2,1)S(1)}, bf16[2,128,1280]{2,1,0:T(8,128)(2,1)}, u32[]{:S(2)}) copy-start(bf16[2,128,1280]{2,1,0:T(8,128)(2,1)} %get-tuple-element.31) | copy-start | bytes 1966084
  92.9 21.7 %copy-start.6 = (bf16[2,128,1280]{2,1,0:T(8,128)(2,1)S(1)}, bf16[2,128,1280]{2,1,0:T(8,128)(2,1)}, u32[]{:S(2)}) copy-start(bf16[2,128,1280]{2,1,0:T(8,128)(2,1)} %get-tuple-element.33) | copy-start | bytes 1966084
  93.0 21.6 %copy-start.1 = (bf16[2,128,1280]{2,1,0:T(8,128)(2,1)S(1)}, bf16[2,128,1280]{2,1,0:T(8,128)(2,1)}, u32[]{:S(2)}) copy-start(bf16[2,128,1280]{2,1,0:T(8,128)(2,1)} %get-tuple-element.26) | copy-start | bytes 1966084
  93.0 21.6 %copy-start.2 = (bf16[2,128,1280]{2,1,0:T(8,128)(2,1)S(1)}, bf16[2,128,1280]{2,1,0:T(8,128)(2,1)}, u32[]{:S(2)}) copy-start(bf16[2,128,1280]{2,1,0:T(8,128)(2,1)} %get-tuple-element.32) | copy-start | bytes 1966084
  93.0 21.6 %copy-start.3 = (bf16[2,128,1280]{2,1,0:T(8,128)(2,1)S(1)}, bf16[2,128,1280]{2,1,0:T(8,128)(2,1)}, u32[]{:S(2)}) copy-start(bf16[2,128,1280]{2,1,0:T(8,128)(2,1)} %get-tuple-element.34) | copy-start | bytes 1966084
  93.1 21.6 %copy-start.4 = (bf16[2,128,1280]{2,1,0:T(8,128)(2,1)S(1)}, bf16[2,128,1280]{2,1,0:T(8,128)(2,1)}, u32[]{:S(2)}) copy-start(bf16[2,128,1280]{2,1,0:T(8,128)(2,1)} %get-tuple-element.25) | copy-start | bytes 1966084
  93.1 2.5 %collective-permute-start.16 = (bf16[2,128,2560]{2,1,0:T(8,128)(2,1)S(1)}, bf16[2,128,2560]{2,1,0:T(8,128)(2,1)S(1)}, u32[]{:S(2)}, u32[]{:S(2)}) collective-permute-start(bf16[2,128,2560]{2,1,0:T(8,128)(2,1)S(1)} %pad_maximum_fusion.4), channel_id=1, source_target_pairs={{1,4},{2,7},{5,8},{6,11},{9,12},{10,15},{17,20},{18,23},{21,24},{2... | collective-permute-start | bytes 3932168 | tf_op jit(solution)/shard_map/ppermute | solution.py:16
  94.2 20.4 %collective-permute-start.15 = (bf16[2,128,2560]{2,1,0:T(8,128)(2,1)S(1)}, bf16[2,128,2560]{2,1,0:T(8,128)(2,1)S(1)}, u32[]{:S(2)}, u32[]{:S(2)}) collective-permute-start(bf16[2,128,2560]{2,1,0:T(8,128)(2,1)S(1)} %pad_maximum_fusion.3), channel_id=1, source_target_pairs={{5,0},{6,3},{9,4},{10,7},{13,8},{14,11},{21,16},{22,19},{25,20},{2... | collective-permute-start | bytes 3932168 | tf_op jit(solution)/shard_map/ppermute | solution.py:16
  114.6 6.0 %copy-start.18 = (bf16[128,1280]{1,0:T(8,128)(2,1)S(1)}, bf16[128,1280]{1,0:T(8,128)(2,1)}, u32[]{:S(2)}) copy-start(bf16[128,1280]{1,0:T(8,128)(2,1)} %get-tuple-element.20) | copy-start | bytes 983044
  114.7 6.0 %copy-start.19 = (bf16[128,1280]{1,0:T(8,128)(2,1)S(1)}, bf16[128,1280]{1,0:T(8,128)(2,1)}, u32[]{:S(2)}) copy-start(bf16[128,1280]{1,0:T(8,128)(2,1)} %get-tuple-element.19) | copy-start | bytes 983044
  114.7 37.9 %copy-start.16 = (bf16[2,128,1280]{2,1,0:T(8,128)(2,1)S(1)}, bf16[2,128,1280]{2,1,0:T(8,128)(2,1)}, u32[]{:S(2)}) copy-start(bf16[2,128,1280]{2,1,0:T(8,128)(2,1)} %get-tuple-element.22) | copy-start | bytes 1966084
  114.7 37.9 %copy-start.17 = (bf16[2,128,1280]{2,1,0:T(8,128)(2,1)S(1)}, bf16[2,128,1280]{2,1,0:T(8,128)(2,1)}, u32[]{:S(2)}) copy-start(bf16[2,128,1280]{2,1,0:T(8,128)(2,1)} %get-tuple-element.21) | copy-start | bytes 1966084
  116.0 30.5 %collective-permute-start.17 = (bf16[2,128,2560]{2,1,0:T(8,128)(2,1)S(1)}, bf16[2,128,2560]{2,1,0:T(8,128)(2,1)S(1)}, u32[]{:S(2)}, u32[]{:S(2)}) collective-permute-start(bf16[2,128,2560]{2,1,0:T(8,128)(2,1)S(1)} %get-tuple-element.35), channel_id=1, source_target_pairs={{0,2},{1,3},{2,0},{3,1},{4,6},{5,7},{6,4},{7,5},{8,10},{9,11},{10,... | collective-permute-start | bytes 3932168 | tf_op jit(solution)/shard_map/ppermute | solution.py:16
  116.1 32.3 %collective-permute-start.19 = (bf16[2,128,2560]{2,1,0:T(8,128)(2,1)S(1)}, bf16[2,128,2560]{2,1,0:T(8,128)(2,1)S(1)}, u32[]{:S(2)}, u32[]{:S(2)}) collective-permute-start(bf16[2,128,2560]{2,1,0:T(8,128)(2,1)S(1)} %get-tuple-element.36), channel_id=1, source_target_pairs={{0,4},{1,5},{2,6},{3,7},{4,8},{5,9},{6,10},{7,11},{8,12},{9,13},{1... | collective-permute-start | bytes 3932168 | tf_op jit(solution)/shard_map/ppermute | solution.py:16
  119.3 33.3 %collective-permute-start.18 = (bf16[2,128,2560]{2,1,0:T(8,128)(2,1)S(1)}, bf16[2,128,2560]{2,1,0:T(8,128)(2,1)S(1)}, u32[]{:S(2)}, u32[]{:S(2)}) collective-permute-start(bf16[2,128,2560]{2,1,0:T(8,128)(2,1)S(1)} %get-tuple-element.37), channel_id=1, source_target_pairs={{4,0},{5,1},{6,2},{7,3},{8,4},{9,5},{10,6},{11,7},{12,8},{13,9},{1... | collective-permute-start | bytes 3932168 | tf_op jit(solution)/shard_map/ppermute | solution.py:16

commit v12 on v7

--- a/solution.py
+++ b/solution.py
@@ -143,17 +143,16 @@
     core, cross, down, up, diag_up, diag_down, back = route(count)
     if after is not None:
         own, _ = lax.optimization_barrier((own, after))
-    from_core = send(own, core)
     from_cross = send(own, cross)
     from_below = send(own, up)
     from_above = send(own, down)
-    return [own, from_core, from_cross, from_below, from_above]
+    return [own, from_cross, from_below, from_above]
 
 
 def forward_second(first, count, after):
     core, cross, down, up, diag_up, diag_down, back = route(count)
-    own, from_core, from_cross, from_below, from_above = first
-    ahead = jnp.stack([from_cross, from_below, from_above])
+    own, from_cross, from_below, from_above = first
+    ahead = jnp.stack([own, from_cross, from_below, from_above])
     if after is not None:
         (ahead, from_cross), _ = lax.optimization_barrier(((ahead, from_cross), after))
     relayed = send(ahead, core)
@@ -163,7 +162,7 @@
 
 
 def chunk_kernel(forward_mask, queries, out_grad, inputs, head_offset, inv_root):
-    slot_in = [(0, ()), (1, ()), (2, ()), (3, ()), (4, ()), (5, (0,)), (5, (1,)), (5, (2,)), (6, ()), (7, ())]
+    slot_in = [(0, ()), (4, (0,)), (1, ()), (2, ()), (3, ()), (4, (1,)), (4, (2,)), (4, (3,)), (5, ()), (6, ())]
     out_lead = [(), (4,), (), (), (), (), ()]
     slot_out = [(0, ()), (1, (0,)), (2, ()), (3, ()), (4, ()), (1, (1,)), (1, (2,)), (1, (3,)), (5, ()), (6, ())]
     return attention_backward(

time: 146 us -> 144 us (0.986)
  starting transfers between devices: 47.2 us -> 42.9 us
  other arithmetic: 12.5 us -> 15.5 us
  waiting for transfers between devices: 54.5 us -> 51.9 us
  local copies, waits for them, and re-layouts: 1.6 us -> 3.31 us
    ppermute x26 -> x24, starting transfers between devices: 47.2 us -> 42.9 us  [send(): return lax.ppermute(value, 'tm', pairs)]
    ppermute x26 -> x24, waiting for transfers between devices: 54.5 us -> 51.9 us  [send(): return lax.ppermute(value, 'tm', pairs)]
    unnamed x25 -> x37, local copies, waits for them, and re-layouts: 0.15 us -> 1.85 us
    convert_element_type x2, other arithmetic: 1.4 us -> 3.01 us  [return_second(): cross_sum.astype(jnp.bfloat16)]
  transfers between devices with their start and end apart: 26 -> 24, of which waited for: 15 -> 14; matrix products, arithmetic and copies ran while one was open for 7% -> 9% of each run, Pallas kernels for 19% -> 20%
where the time goes in v12:
time: 144 us; the launch traced here: 143 us
  waiting for transfers between devices  51.9 us (36%)
  starting transfers between devices  42.9 us (30%)
  Pallas kernels  28.1 us (20%)
  other arithmetic  15.5 us (11%)
  local copies, waits for them, and re-layouts  3.31 us (2%)
    ppermute x24, waiting for transfers between devices, send(): return lax.ppermute(value, 'tm', pairs)  51.9 us
    ppermute x24, starting transfers between devices, send(): return lax.ppermute(value, 'tm', pairs)  42.9 us
    pallas_call x2, Pallas kernels, attention_backward(): pl.pallas_call(kernel, grid=(heads // STEP_HEADS,), in_specs=in_specs, ou...  28.1 us
    another operation x4, other arithmetic, forward_second(): ahead = jnp.stack([own, from_cross, from_below, from_above])  5.2 us
    convert_element_type x2, other arithmetic, return_second(): cross_sum.astype(jnp.bfloat16)  3.01 us
  transfers between devices with their start and end apart: 24, of which 14 were waited for; matrix products, arithmetic and copies ran while one was open for 9% of the time, Pallas kernels for 20%

profile of v12, /device:TPU:0, one launch (start us, length us, event | category | flops | bytes accessed | tf_op | source)
XLA Modules:
  0.0 143.0 jit_solution(12483553636562422120)
XLA Ops:
  0.6 1.4 slice_bitcast_fusion.14
  2.0 1.0 fusion.30
  3.0 3.0 %collective-permute-start = (bf16[2,128,1280]{2,1,0:T(8,128)(2,1)}, bf16[2,128,1280]{2,1,0:T(8,128)(2,1)S(1)}, u32[]{:S(2)}, u32[]{:S(2)}) collective-permute-start(bf16[2,128,1280]{2,1,0:T(8,128)(2,1)} %get-tuple-element.46.refs_0_), channel_id=1, source_target_pairs={{0,2},{1,3},{2,0},{3,1},{4,6},{5,7},{6,4},{7,5},{8,10},{9,11},{10,... | collective-permute-start | bytes 1966088 | tf_op jit(solution)/shard_map/ppermute | solution.py:16
  6.0 3.5 %collective-permute-start.1 = (bf16[2,128,1280]{2,1,0:T(8,128)(2,1)}, bf16[2,128,1280]{2,1,0:T(8,128)(2,1)S(1)}, u32[]{:S(2)}, u32[]{:S(2)}) collective-permute-start(bf16[2,128,1280]{2,1,0:T(8,128)(2,1)} %get-tuple-element.46.refs_0_), channel_id=1, source_target_pairs={{0,4},{1,5},{2,6},{3,7},{4,8},{5,9},{6,10},{7,11},{8,12},{9,13},{1... | collective-permute-start | bytes 1966088 | tf_op jit(solution)/shard_map/ppermute | solution.py:16
  9.5 1.3 collective-permute-start.2
  10.8 0.9 fusion.29
  11.7 0.5 collective-permute-start.6
  12.2 4.6 %collective-permute-start.7 = (bf16[2,128,1280]{2,1,0:T(8,128)(2,1)}, bf16[2,128,1280]{2,1,0:T(8,128)(2,1)S(1)}, u32[]{:S(2)}, u32[]{:S(2)}) collective-permute-start(bf16[2,128,1280]{2,1,0:T(8,128)(2,1)} %get-tuple-element.52.refs_0_), channel_id=1, source_target_pairs={{0,4},{1,5},{2,6},{3,7},{4,8},{5,9},{6,10},{7,11},{8,12},{9,13},{1... | collective-permute-start | bytes 1966088 | tf_op jit(solution)/shard_map/ppermute | solution.py:16
  16.9 0.1 copy.9
  17.1 4.7 %collective-permute-done.refs_1_ = bf16[2,128,1280]{2,1,0:T(8,128)(2,1)S(1)} collective-permute-done((bf16[2,128,1280]{2,1,0:T(8,128)(2,1)}, bf16[2,128,1280]{2,1,0:T(8,128)(2,1)S(1)}, u32[]{:S(2)}, u32[]{:S(2)}) %collective-permute-start) | collective-permute-done | bytes 655392 | tf_op jit(solution)/shard_map/ppermute | solution.py:16
  21.8 1.3 collective-permute-start.8
  23.1 1.8 %collective-permute-done.1.refs_2_ = bf16[2,128,1280]{2,1,0:T(8,128)(2,1)S(1)} collective-permute-done((bf16[2,128,1280]{2,1,0:T(8,128)(2,1)}, bf16[2,128,1280]{2,1,0:T(8,128)(2,1)S(1)}, u32[]{:S(2)}, u32[]{:S(2)}) %collective-permute-start.1) | collective-permute-done | bytes 655392 | tf_op jit(solution)/shard_map/ppermute | solution.py:16
  24.9 4.4 %collective-permute-done.2.refs_3_ = bf16[2,128,1280]{2,1,0:T(8,128)(2,1)} collective-permute-done((bf16[2,128,1280]{2,1,0:T(8,128)(2,1)}, bf16[2,128,1280]{2,1,0:T(8,128)(2,1)}, u32[]{:S(2)}, u32[]{:S(2)}) %collective-permute-start.2) | collective-permute-done | bytes 655392 | tf_op jit(solution)/shard_map/ppermute | solution.py:16
  29.3 1.4 pad_maximum_fusion
  30.8 0.1 collective-permute-start.3
  30.9 4.2 %collective-permute-done.6.refs_1_ = bf16[2,128,1280]{2,1,0:T(8,128)(2,1)} collective-permute-done((bf16[2,128,1280]{2,1,0:T(8,128)(2,1)}, bf16[2,128,1280]{2,1,0:T(8,128)(2,1)}, u32[]{:S(2)}, u32[]{:S(2)}) %collective-permute-start.6) | collective-permute-done | bytes 655392 | tf_op jit(solution)/shard_map/ppermute | solution.py:16
  35.1 2.4 %collective-permute-done.7.refs_2_ = bf16[2,128,1280]{2,1,0:T(8,128)(2,1)S(1)} collective-permute-done((bf16[2,128,1280]{2,1,0:T(8,128)(2,1)}, bf16[2,128,1280]{2,1,0:T(8,128)(2,1)S(1)}, u32[]{:S(2)}, u32[]{:S(2)}) %collective-permute-start.7) | collective-permute-done | bytes 655392 | tf_op jit(solution)/shard_map/ppermute | solution.py:16
  37.5 4.0 %collective-permute-done.8.refs_3_ = bf16[2,128,1280]{2,1,0:T(8,128)(2,1)S(1)} collective-permute-done((bf16[2,128,1280]{2,1,0:T(8,128)(2,1)}, bf16[2,128,1280]{2,1,0:T(8,128)(2,1)S(1)}, u32[]{:S(2)}, u32[]{:S(2)}) %collective-permute-start.8) | collective-permute-done | bytes 655392 | tf_op jit(solution)/shard_map/ppermute | solution.py:16
  41.6 1.9 %pad_maximum_fusion.1 = bf16[4,2,128,1280]{3,2,1,0:T(8,128)(2,1)S(1)} fusion(bf16[1,2,128,1280]{3,2,1,0:T(8,128)(2,1)S(1)} %bitcast.75, bf16[1,2,128,1280]{3,2,1,0:T(8,128)(2,1)} %bitcast.72, bf16[1,2,128,1280]{3,2,1,0:T(8,128)(2,1)} %bitcast.12, bf16[1,2,128,1280]{3,2,1,0:T(8,128)(2,1)S(1)} %get-tuple-element.51), kind=kLoop, calls=%fused_computation.1 | loop fusion | flops 3932160 | bytes 5242880 | tf_op jit(solution)/shard_map/stack | solution.py:155
  43.5 0.1 collective-permute-start.9
  43.6 0.1 select_reduce_fusion
  43.7 0.1 multiply_reduce_fusion
  43.8 3.6 %collective-permute-start.4 = (bf16[2,128,1280]{2,1,0:T(8,128)(2,1)S(1)}, bf16[2,128,1280]{2,1,0:T(8,128)(2,1)S(1)}, u32[]{:S(2)}, u32[]{:S(2)}) collective-permute-start(bf16[2,128,1280]{2,1,0:T(8,128)(2,1)S(1)} %copy-done.2), channel_id=1, source_target_pairs={{0,5},{3,6},{4,9},{7,10},{8,13},{11,14},{16,21},{19,22},{20,25},{2... | collective-permute-start | bytes 1966088 | tf_op jit(solution)/shard_map/ppermute | solution.py:16
  47.4 0.7 collective-permute-start.5
  48.1 1.4 fusion.24.mask_ref
  49.5 1.9 %collective-permute-start.10 = (bf16[2,128,1280]{2,1,0:T(8,128)(2,1)}, bf16[2,128,1280]{2,1,0:T(8,128)(2,1)S(1)}, u32[]{:S(2)}, u32[]{:S(2)}) collective-permute-start(bf16[2,128,1280]{2,1,0:T(8,128)(2,1)} %collective-permute-done.6.refs_1_), channel_id=1, source_target_pairs={{0,5},{3,6},{4,9},{7,10},{8,13},{11,14},{16,21},{19,22},{20,25},{2... | collective-permute-start | bytes 1966088 | tf_op jit(solution)/shard_map/ppermute | solution.py:16
  51.4 4.0 %collective-permute-done.4.refs_5_ = bf16[2,128,1280]{2,1,0:T(8,128)(2,1)S(1)} collective-permute-done((bf16[2,128,1280]{2,1,0:T(8,128)(2,1)S(1)}, bf16[2,128,1280]{2,1,0:T(8,128)(2,1)S(1)}, u32[]{:S(2)}, u32[]{:S(2)}) %collective-permute-start.4) | collective-permute-done | bytes 655392 | tf_op jit(solution)/shard_map/ppermute | solution.py:16
  55.4 1.5 %collective-permute-start.11 = (bf16[2,128,1280]{2,1,0:T(8,128)(2,1)}, bf16[2,128,1280]{2,1,0:T(8,128)(2,1)}, u32[]{:S(2)}, u32[]{:S(2)}) collective-permute-start(bf16[2,128,1280]{2,1,0:T(8,128)(2,1)} %collective-permute-done.6.refs_1_), channel_id=1, source_target_pairs={{4,1},{7,2},{8,5},{11,6},{12,9},{15,10},{20,17},{23,18},{24,21},{2... | collective-permute-start | bytes 1966088 | tf_op jit(solution)/shard_map/ppermute | solution.py:16
  56.9 0.0 collective-permute-done.5.refs_6_
  56.9 0.9 copy-done.16
  57.8 14.0 %shard_map.85 = (bf16[128,1280]{1,0:T(8,128)(2,1)}, bf16[2,128,1280]{2,1,0:T(8,128)(2,1)}, bf16[4,2,128,1280]{3,2,1,0:T(8,128)(2,1)}, bf16[2,128,1280]{2,1,0:T(8...) custom-call(s32[128,1280]{1,0:T(8,128)} %fusion.24.mask_ref, ...), custom_call_target="tpu_custom_call" | custom-call | flops 2516582400 | bytes 14745600 | tf_op jit(solution)/shard_map/pallas_call | solution.py:127
  71.8 1.7 %collective-permute-start.12 = (bf16[4,2,128,1280]{3,2,1,0:T(8,128)(2,1)}, bf16[4,2,128,1280]{3,2,1,0:T(8,128)(2,1)}, u32[]{:S(2)}, u32[]{:S(2)}) collective-permute-start(bf16[4,2,128,1280]{3,2,1,0:T(8,128)(2,1)} %get-tuple-element.22), channel_id=1, source_target_pairs={{0,1},{1,0},{2,3},{3,2},{4,5},{5,4},{6,7},{7,6},{8,9},{9,8},{10,11... | collective-permute-start | bytes 7864328 | tf_op jit(solution)/shard_map/ppermute | solution.py:16
  73.6 0.0 collective-permute-done.10.refs_5_
  73.6 0.0 collective-permute-done.11.refs_6_
  73.6 0.8 copy-done.14
  74.4 14.1 %shard_map.86 = (bf16[128,1280]{1,0:T(8,128)(2,1)}, bf16[2,128,1280]{2,1,0:T(8,128)(2,1)}, bf16[4,2,128,1280]{3,2,1,0:T(8,128)(2,1)}, bf16[2,128,1280]{2,1,0:T(8...) custom-call(s32[128,1280]{1,0:T(8,128)} %fusion.24.mask_ref, ...), custom_call_target="tpu_custom_call" | custom-call | flops 2516582400 | bytes 14745600 | tf_op jit(solution)/shard_map/pallas_call | solution.py:127
  88.5 0.1 collective-permute-start.18
  88.6 1.4 collective-permute-start.13
  90.1 0.7 collective-permute-start.14
  90.8 1.3 collective-permute-start.19
  92.1 2.0 %pad_maximum_fusion.4 = bf16[128,2560]{1,0:T(8,128)(2,1)} fusion(bf16[128,1280]{1,0:T(8,128)(2,1)} %get-tuple-element.20, bf16[128,1280]{1,0:T(8,128)(2,1)} %get-tuple-element.19), kind=kLoop, calls=%fused_computation.46 | loop fusion | flops 1310720 | bytes 1310720 | tf_op jit(solution)/shard_map/concatenate | solution.py:253
  94.0 6.9 %collective-permute-done.13 = bf16[2,128,1280]{2,1,0:T(8,128)(2,1)S(1)} collective-permute-done((bf16[2,128,1280]{2,1,0:T(8,128)(2,1)}, bf16[2,128,1280]{2,1,0:T(8,128)(2,1)S(1)}, u32[]{:S(2)}, u32[]{:S(2)}) %collective-permute-start.13) | collective-permute-done | bytes 655392 | tf_op jit(solution)/shard_map/ppermute | solution.py:16
  100.9 0.7 collective-permute-start.20
  101.6 0.0 collective-permute-done.12
  101.7 2.3 %fusion.13 = (bf16[2,128,1280]{2,1,0:T(8,128)(2,1)S(1)}, bf16[2,128,1280]{2,1,0:T(8,128)(2,1)S(1)}, bf16[2,128,1280]{2,1,0:T(8,128)(2,1)S(1)}) fusion(bf16[2,128,1280]{2,1,0:T(8,128)(2,1)S(1)} %collective-permute-done.14, bf16[2,128,1280]{2,1,0:T(8,128)(2,1)S(1)} %collective-permute-done.13, bf16[2,128,1280]{2,1,0:T(8,128)(2,1)S(1)} %copy-done.8, ...), kind=kLoop, calls=%fused_computation.22 | loop fusion | flops 5242880 | bytes 7208960 | tf_op jit(solution)/shard_map/convert_element_type | solution.py:194
  104.0 2.7 %collective-permute-start.15 = (bf16[2,128,1280]{2,1,0:T(8,128)(2,1)S(1)}, bf16[2,128,1280]{2,1,0:T(8,128)(2,1)S(1)}, u32[]{:S(2)}, u32[]{:S(2)}) collective-permute-start(bf16[2,128,1280]{2,1,0:T(8,128)(2,1)S(1)} %get-tuple-element.35), channel_id=1, source_target_pairs={{0,2},{1,3},{2,0},{3,1},{4,6},{5,7},{6,4},{7,5},{8,10},{9,11},{10,... | collective-permute-start | bytes 1966088 | tf_op jit(solution)/shard_map/ppermute | solution.py:16
  106.7 1.3 collective-permute-start.16
  108.0 5.2 %collective-permute-start.17 = (bf16[2,128,1280]{2,1,0:T(8,128)(2,1)S(1)}, bf16[2,128,1280]{2,1,0:T(8,128)(2,1)S(1)}, u32[]{:S(2)}, u32[]{:S(2)}) collective-permute-start(bf16[2,128,1280]{2,1,0:T(8,128)(2,1)S(1)} %get-tuple-element.36), channel_id=1, source_target_pairs={{0,4},{1,5},{2,6},{3,7},{4,8},{5,9},{6,10},{7,11},{8,12},{9,13},{1... | collective-permute-start | bytes 1966088 | tf_op jit(solution)/shard_map/ppermute | solution.py:16
  113.2 0.0 collective-permute-done.20
  113.2 0.0 collective-permute-done.18
  113.2 0.7 fusion.4
  113.9 0.1 collective-permute-start.21
  114.0 1.3 collective-permute-start.22
  115.3 6.5 %collective-permute-done.15 = bf16[2,128,1280]{2,1,0:T(8,128)(2,1)S(1)} collective-permute-done((bf16[2,128,1280]{2,1,0:T(8,128)(2,1)S(1)}, bf16[2,128,1280]{2,1,0:T(8,128)(2,1)S(1)}, u32[]{:S(2)}, u32[]{:S(2)}) %collective-permute-start.15) | collective-permute-done | bytes 655392 | tf_op jit(solution)/shard_map/ppermute | solution.py:16
  121.8 4.5 %collective-permute-start.23 = (bf16[2,128,1280]{2,1,0:T(8,128)(2,1)S(1)}, bf16[2,128,1280]{2,1,0:T(8,128)(2,1)S(1)}, u32[]{:S(2)}, u32[]{:S(2)}) collective-permute-start(bf16[2,128,1280]{2,1,0:T(8,128)(2,1)S(1)} %get-tuple-element.39), channel_id=1, source_target_pairs={{0,4},{1,5},{2,6},{3,7},{4,8},{5,9},{6,10},{7,11},{8,12},{9,13},{1... | collective-permute-start | bytes 1966088 | tf_op jit(solution)/shard_map/ppermute | solution.py:16
  126.3 0.4 collective-permute-done.16
  126.7 0.5 collective-permute-done.17
  127.2 1.5 %fusion.17 = bf16[2,128,1280]{2,1,0:T(8,128)(2,1)S(1)} fusion(bf16[2,128,1280]{2,1,0:T(8,128)(2,1)S(1)} %collective-permute-done.17, bf16[2,128,1280]{2,1,0:T(8,128)(2,1)S(1)} %collective-permute-done.16, bf16[2,128,1280]{2,1,0:T(8,128)(2,1)S(1)} %collective-permute-done.15, bf16[2,128,1280]{2,1,0:T(8,128)(2,1)S(1)} %copy-done.11, ...), kind=kLoop, calls=%fused_computation.27 | loop fusion | flops 3276800 | bytes 3932160 | tf_op jit(solution)/shard_map/convert.11
  128.8 6.5 %collective-permute-done.21 = bf16[2,128,1280]{2,1,0:T(8,128)(2,1)S(1)} collective-permute-done((bf16[2,128,1280]{2,1,0:T(8,128)(2,1)S(1)}, bf16[2,128,1280]{2,1,0:T(8,128)(2,1)S(1)}, u32[]{:S(2)}, u32[]{:S(2)}) %collective-permute-start.21) | collective-permute-done | bytes 655392 | tf_op jit(solution)/shard_map/ppermute | solution.py:16
  135.3 4.8 %collective-permute-done.22 = bf16[2,128,1280]{2,1,0:T(8,128)(2,1)S(1)} collective-permute-done((bf16[2,128,1280]{2,1,0:T(8,128)(2,1)S(1)}, bf16[2,128,1280]{2,1,0:T(8,128)(2,1)S(1)}, u32[]{:S(2)}, u32[]{:S(2)}) %collective-permute-start.22) | collective-permute-done | bytes 655392 | tf_op jit(solution)/shard_map/ppermute | solution.py:16
  140.1 0.7 collective-permute-done.23
  140.8 0.4 fusion.8
  141.2 0.9 pad_maximum_fusion.6
  142.1 0.9 pad_maximum_fusion.5
  (57 shorter events, 0.3 us)
Async XLA Ops:
  3.0 13.9 %copy-start.13 = (s32[4,3]{1,0:T(4,128)S(1)}, s32[4,3]{1,0:T(4,128)}, u32[]{:S(2)}) copy-start(s32[4,3]{1,0:T(4,128)} %param.10) | copy-start | bytes 148
  3.0 18.8 %collective-permute-start = (bf16[2,128,1280]{2,1,0:T(8,128)(2,1)}, bf16[2,128,1280]{2,1,0:T(8,128)(2,1)S(1)}, u32[]{:S(2)}, u32[]{:S(2)}) collective-permute-start(bf16[2,128,1280]{2,1,0:T(8,128)(2,1)} %get-tuple-element.46.refs_0_), channel_id=1, source_target_pairs={{0,2},{1,3},{2,0},{3,1},{4,6},{5,7},{6,4},{7,5},{8,10},{9,11},{10,... | collective-permute-start | bytes 1966088 | tf_op jit(solution)/shard_map/ppermute | solution.py:16
  6.0 18.9 %collective-permute-start.1 = (bf16[2,128,1280]{2,1,0:T(8,128)(2,1)}, bf16[2,128,1280]{2,1,0:T(8,128)(2,1)S(1)}, u32[]{:S(2)}, u32[]{:S(2)}) collective-permute-start(bf16[2,128,1280]{2,1,0:T(8,128)(2,1)} %get-tuple-element.46.refs_0_), channel_id=1, source_target_pairs={{0,4},{1,5},{2,6},{3,7},{4,8},{5,9},{6,10},{7,11},{8,12},{9,13},{1... | collective-permute-start | bytes 1966088 | tf_op jit(solution)/shard_map/ppermute | solution.py:16
  9.5 19.8 %collective-permute-start.2 = (bf16[2,128,1280]{2,1,0:T(8,128)(2,1)}, bf16[2,128,1280]{2,1,0:T(8,128)(2,1)}, u32[]{:S(2)}, u32[]{:S(2)}) collective-permute-start(bf16[2,128,1280]{2,1,0:T(8,128)(2,1)} %get-tuple-element.46.refs_0_), channel_id=1, source_target_pairs={{4,0},{5,1},{6,2},{7,3},{8,4},{9,5},{10,6},{11,7},{12,8},{13,9},{1... | collective-permute-start | bytes 1966088 | tf_op jit(solution)/shard_map/ppermute | solution.py:16
  11.7 23.3 %collective-permute-start.6 = (bf16[2,128,1280]{2,1,0:T(8,128)(2,1)}, bf16[2,128,1280]{2,1,0:T(8,128)(2,1)}, u32[]{:S(2)}, u32[]{:S(2)}) collective-permute-start(bf16[2,128,1280]{2,1,0:T(8,128)(2,1)} %get-tuple-element.52.refs_0_), channel_id=1, source_target_pairs={{0,2},{1,3},{2,0},{3,1},{4,6},{5,7},{6,4},{7,5},{8,10},{9,11},{10,... | collective-permute-start | bytes 1966088 | tf_op jit(solution)/shard_map/ppermute | solution.py:16
  12.2 25.3 %collective-permute-start.7 = (bf16[2,128,1280]{2,1,0:T(8,128)(2,1)}, bf16[2,128,1280]{2,1,0:T(8,128)(2,1)S(1)}, u32[]{:S(2)}, u32[]{:S(2)}) collective-permute-start(bf16[2,128,1280]{2,1,0:T(8,128)(2,1)} %get-tuple-element.52.refs_0_), channel_id=1, source_target_pairs={{0,4},{1,5},{2,6},{3,7},{4,8},{5,9},{6,10},{7,11},{8,12},{9,13},{1... | collective-permute-start | bytes 1966088 | tf_op jit(solution)/shard_map/ppermute | solution.py:16
  21.8 9.0 %copy-start.1 = (bf16[2,128,1280]{2,1,0:T(8,128)(2,1)}, bf16[2,128,1280]{2,1,0:T(8,128)(2,1)S(1)}, u32[]{:S(2)}) copy-start(bf16[2,128,1280]{2,1,0:T(8,128)(2,1)S(1)} %collective-permute-done.refs_1_) | copy-start | bytes 1966084
  21.8 19.8 %collective-permute-start.8 = (bf16[2,128,1280]{2,1,0:T(8,128)(2,1)}, bf16[2,128,1280]{2,1,0:T(8,128)(2,1)S(1)}, u32[]{:S(2)}, u32[]{:S(2)}) collective-permute-start(bf16[2,128,1280]{2,1,0:T(8,128)(2,1)} %get-tuple-element.52.refs_0_), channel_id=1, source_target_pairs={{4,0},{5,1},{6,2},{7,3},{8,4},{9,5},{10,6},{11,7},{12,8},{13,9},{1... | collective-permute-start | bytes 1966088 | tf_op jit(solution)/shard_map/ppermute | solution.py:16
  24.9 5.9 %copy-start.3 = (bf16[2,128,1280]{2,1,0:T(8,128)(2,1)}, bf16[2,128,1280]{2,1,0:T(8,128)(2,1)S(1)}, u32[]{:S(2)}) copy-start(bf16[2,128,1280]{2,1,0:T(8,128)(2,1)S(1)} %collective-permute-done.1.refs_2_) | copy-start | bytes 1966084
  30.8 27.0 %collective-permute-start.3 = (bf16[4,2,128,1280]{3,2,1,0:T(8,128)(2,1)S(1)}, bf16[4,2,128,1280]{3,2,1,0:T(8,128)(2,1)}, u32[]{:S(2)}, u32[]{:S(2)}) collective-permute-start(bf16[4,2,128,1280]{3,2,1,0:T(8,128)(2,1)S(1)} %pad_maximum_fusion), channel_id=1, source_target_pairs={{0,1},{1,0},{2,3},{3,2},{4,5},{5,4},{6,7},{7,6},{8,9},{9,8},{10,11... | collective-permute-start | bytes 7864328 | tf_op jit(solution)/shard_map/ppermute | solution.py:16
  37.5 4.1 %copy-start = (bf16[2,128,1280]{2,1,0:T(8,128)(2,1)}, bf16[2,128,1280]{2,1,0:T(8,128)(2,1)S(1)}, u32[]{:S(2)}) copy-start(bf16[2,128,1280]{2,1,0:T(8,128)(2,1)S(1)} %collective-permute-done.7.refs_2_) | copy-start | bytes 1966084
  41.6 1.9 %copy-start.4 = (bf16[2,128,1280]{2,1,0:T(8,128)(2,1)}, bf16[2,128,1280]{2,1,0:T(8,128)(2,1)S(1)}, u32[]{:S(2)}) copy-start(bf16[2,128,1280]{2,1,0:T(8,128)(2,1)S(1)} %collective-permute-done.8.refs_3_) | copy-start | bytes 1966084
  41.6 2.0 %copy-start.17 = (s32[4]{0:T(128)S(1)}, s32[4]{0:T(128)}, u32[]{:S(2)}) copy-start(s32[4]{0:T(128)} %param.11) | copy-start | bytes 52
  41.6 2.2 %copy-start.2 = (bf16[2,128,1280]{2,1,0:T(8,128)(2,1)S(1)}, bf16[2,128,1280]{2,1,0:T(8,128)(2,1)}, u32[]{:S(2)}) copy-start(bf16[2,128,1280]{2,1,0:T(8,128)(2,1)} %copy-done.1) | copy-start | bytes 1966084
  43.5 31.0 %collective-permute-start.9 = (bf16[4,2,128,1280]{3,2,1,0:T(8,128)(2,1)S(1)}, bf16[4,2,128,1280]{3,2,1,0:T(8,128)(2,1)}, u32[]{:S(2)}, u32[]{:S(2)}) collective-permute-start(bf16[4,2,128,1280]{3,2,1,0:T(8,128)(2,1)S(1)} %pad_maximum_fusion.1), channel_id=1, source_target_pairs={{0,1},{1,0},{2,3},{3,2},{4,5},{5,4},{6,7},{7,6},{8,9},{9,8},{10,11... | collective-permute-start | bytes 7864328 | tf_op jit(solution)/shard_map/ppermute | solution.py:16
  43.8 11.6 %collective-permute-start.4 = (bf16[2,128,1280]{2,1,0:T(8,128)(2,1)S(1)}, bf16[2,128,1280]{2,1,0:T(8,128)(2,1)S(1)}, u32[]{:S(2)}, u32[]{:S(2)}) collective-permute-start(bf16[2,128,1280]{2,1,0:T(8,128)(2,1)S(1)} %copy-done.2), channel_id=1, source_target_pairs={{0,5},{3,6},{4,9},{7,10},{8,13},{11,14},{16,21},{19,22},{20,25},{2... | collective-permute-start | bytes 1966088 | tf_op jit(solution)/shard_map/ppermute | solution.py:16
  47.4 9.6 %collective-permute-start.5 = (bf16[2,128,1280]{2,1,0:T(8,128)(2,1)S(1)}, bf16[2,128,1280]{2,1,0:T(8,128)(2,1)S(1)}, u32[]{:S(2)}, u32[]{:S(2)}) collective-permute-start(bf16[2,128,1280]{2,1,0:T(8,128)(2,1)S(1)} %copy-done.2), channel_id=1, source_target_pairs={{4,1},{7,2},{8,5},{11,6},{12,9},{15,10},{20,17},{23,18},{24,21},{2... | collective-permute-start | bytes 1966088 | tf_op jit(solution)/shard_map/ppermute | solution.py:16
  49.5 24.1 %collective-permute-start.10 = (bf16[2,128,1280]{2,1,0:T(8,128)(2,1)}, bf16[2,128,1280]{2,1,0:T(8,128)(2,1)S(1)}, u32[]{:S(2)}, u32[]{:S(2)}) collective-permute-start(bf16[2,128,1280]{2,1,0:T(8,128)(2,1)} %collective-permute-done.6.refs_1_), channel_id=1, source_target_pairs={{0,5},{3,6},{4,9},{7,10},{8,13},{11,14},{16,21},{19,22},{20,25},{2... | collective-permute-start | bytes 1966088 | tf_op jit(solution)/shard_map/ppermute | solution.py:16
  55.4 1.5 %copy-start.15 = (bf16[2,128,1280]{2,1,0:T(8,128)(2,1)}, bf16[2,128,1280]{2,1,0:T(8,128)(2,1)S(1)}, u32[]{:S(2)}) copy-start(bf16[2,128,1280]{2,1,0:T(8,128)(2,1)S(1)} %collective-permute-done.4.refs_5_) | copy-start | bytes 1966084
  55.4 18.1 %collective-permute-start.11 = (bf16[2,128,1280]{2,1,0:T(8,128)(2,1)}, bf16[2,128,1280]{2,1,0:T(8,128)(2,1)}, u32[]{:S(2)}, u32[]{:S(2)}) collective-permute-start(bf16[2,128,1280]{2,1,0:T(8,128)(2,1)} %collective-permute-done.6.refs_1_), channel_id=1, source_target_pairs={{4,1},{7,2},{8,5},{11,6},{12,9},{15,10},{20,17},{23,18},{24,21},{2... | collective-permute-start | bytes 1966088 | tf_op jit(solution)/shard_map/ppermute | solution.py:16
  56.9 0.9 copy-start.16
  71.8 29.8 %collective-permute-start.12 = (bf16[4,2,128,1280]{3,2,1,0:T(8,128)(2,1)}, bf16[4,2,128,1280]{3,2,1,0:T(8,128)(2,1)}, u32[]{:S(2)}, u32[]{:S(2)}) collective-permute-start(bf16[4,2,128,1280]{3,2,1,0:T(8,128)(2,1)} %get-tuple-element.22), channel_id=1, source_target_pairs={{0,1},{1,0},{2,3},{3,2},{4,5},{5,4},{6,7},{7,6},{8,9},{9,8},{10,11... | collective-permute-start | bytes 7864328 | tf_op jit(solution)/shard_map/ppermute | solution.py:16
  73.6 0.8 copy-start.14
  74.4 27.2 %copy-start.10 = (bf16[2,128,1280]{2,1,0:T(8,128)(2,1)S(1)}, bf16[2,128,1280]{2,1,0:T(8,128)(2,1)}, u32[]{:S(2)}) copy-start(bf16[2,128,1280]{2,1,0:T(8,128)(2,1)} %get-tuple-element.27) | copy-start | bytes 1966084
  88.5 13.1 %copy-start.8 = (bf16[2,128,1280]{2,1,0:T(8,128)(2,1)S(1)}, bf16[2,128,1280]{2,1,0:T(8,128)(2,1)}, u32[]{:S(2)}) copy-start(bf16[2,128,1280]{2,1,0:T(8,128)(2,1)} %get-tuple-element.23) | copy-start | bytes 1966084
  88.5 13.1 %copy-start.9 = (bf16[2,128,1280]{2,1,0:T(8,128)(2,1)S(1)}, bf16[2,128,1280]{2,1,0:T(8,128)(2,1)}, u32[]{:S(2)}) copy-start(bf16[2,128,1280]{2,1,0:T(8,128)(2,1)} %get-tuple-element.26) | copy-start | bytes 1966084
  88.5 24.6 %collective-permute-start.18 = (bf16[4,2,128,1280]{3,2,1,0:T(8,128)(2,1)}, bf16[4,2,128,1280]{3,2,1,0:T(8,128)(2,1)S(1)}, u32[]{:S(2)}, u32[]{:S(2)}) collective-permute-start(bf16[4,2,128,1280]{3,2,1,0:T(8,128)(2,1)} %get-tuple-element.29), channel_id=1, source_target_pairs={{0,1},{1,0},{2,3},{3,2},{4,5},{5,4},{6,7},{7,6},{8,9},{9,8},{10,11... | collective-permute-start | bytes 7864328 | tf_op jit(solution)/shard_map/ppermute | solution.py:16
  88.6 12.2 %collective-permute-start.13 = (bf16[2,128,1280]{2,1,0:T(8,128)(2,1)}, bf16[2,128,1280]{2,1,0:T(8,128)(2,1)S(1)}, u32[]{:S(2)}, u32[]{:S(2)}) collective-permute-start(bf16[2,128,1280]{2,1,0:T(8,128)(2,1)} %get-tuple-element.24), channel_id=1, source_target_pairs={{5,0},{6,3},{9,4},{10,7},{13,8},{14,11},{21,16},{22,19},{25,20},{2... | collective-permute-start | bytes 1966088 | tf_op jit(solution)/shard_map/ppermute | solution.py:16
  90.1 11.5 %collective-permute-start.14 = (bf16[2,128,1280]{2,1,0:T(8,128)(2,1)}, bf16[2,128,1280]{2,1,0:T(8,128)(2,1)S(1)}, u32[]{:S(2)}, u32[]{:S(2)}) collective-permute-start(bf16[2,128,1280]{2,1,0:T(8,128)(2,1)} %get-tuple-element.25), channel_id=1, source_target_pairs={{1,4},{2,7},{5,8},{6,11},{9,12},{10,15},{17,20},{18,23},{21,24},{2... | collective-permute-start | bytes 1966088 | tf_op jit(solution)/shard_map/ppermute | solution.py:16
  90.8 17.2 %collective-permute-start.19 = (bf16[2,128,1280]{2,1,0:T(8,128)(2,1)}, bf16[2,128,1280]{2,1,0:T(8,128)(2,1)S(1)}, u32[]{:S(2)}, u32[]{:S(2)}) collective-permute-start(bf16[2,128,1280]{2,1,0:T(8,128)(2,1)} %get-tuple-element.31), channel_id=1, source_target_pairs={{5,0},{6,3},{9,4},{10,7},{13,8},{14,11},{21,16},{22,19},{25,20},{2... | collective-permute-start | bytes 1966088 | tf_op jit(solution)/shard_map/ppermute | solution.py:16
  100.9 12.3 %collective-permute-start.20 = (bf16[2,128,1280]{2,1,0:T(8,128)(2,1)}, bf16[2,128,1280]{2,1,0:T(8,128)(2,1)S(1)}, u32[]{:S(2)}, u32[]{:S(2)}) collective-permute-start(bf16[2,128,1280]{2,1,0:T(8,128)(2,1)} %get-tuple-element.32), channel_id=1, source_target_pairs={{1,4},{2,7},{5,8},{6,11},{9,12},{10,15},{17,20},{18,23},{21,24},{2... | collective-permute-start | bytes 1966088 | tf_op jit(solution)/shard_map/ppermute | solution.py:16
  101.6 11.6 %copy-start.5 = (bf16[2,128,1280]{2,1,0:T(8,128)(2,1)S(1)}, bf16[2,128,1280]{2,1,0:T(8,128)(2,1)}, u32[]{:S(2)}) copy-start(bf16[2,128,1280]{2,1,0:T(8,128)(2,1)} %get-tuple-element.30) | copy-start | bytes 1966084
  101.6 11.6 %copy-start.6 = (bf16[2,128,1280]{2,1,0:T(8,128)(2,1)S(1)}, bf16[2,128,1280]{2,1,0:T(8,128)(2,1)}, u32[]{:S(2)}) copy-start(bf16[2,128,1280]{2,1,0:T(8,128)(2,1)} %get-tuple-element.33) | copy-start | bytes 1966084
  101.6 11.6 %copy-start.7 = (bf16[2,128,1280]{2,1,0:T(8,128)(2,1)S(1)}, bf16[2,128,1280]{2,1,0:T(8,128)(2,1)}, u32[]{:S(2)}) copy-start(bf16[2,128,1280]{2,1,0:T(8,128)(2,1)} %get-tuple-element.34) | copy-start | bytes 1966084
  104.0 17.8 %collective-permute-start.15 = (bf16[2,128,1280]{2,1,0:T(8,128)(2,1)S(1)}, bf16[2,128,1280]{2,1,0:T(8,128)(2,1)S(1)}, u32[]{:S(2)}, u32[]{:S(2)}) collective-permute-start(bf16[2,128,1280]{2,1,0:T(8,128)(2,1)S(1)} %get-tuple-element.35), channel_id=1, source_target_pairs={{0,2},{1,3},{2,0},{3,1},{4,6},{5,7},{6,4},{7,5},{8,10},{9,11},{10,... | collective-permute-start | bytes 1966088 | tf_op jit(solution)/shard_map/ppermute | solution.py:16
  106.7 20.1 %collective-permute-start.16 = (bf16[2,128,1280]{2,1,0:T(8,128)(2,1)S(1)}, bf16[2,128,1280]{2,1,0:T(8,128)(2,1)S(1)}, u32[]{:S(2)}, u32[]{:S(2)}) collective-permute-start(bf16[2,128,1280]{2,1,0:T(8,128)(2,1)S(1)} %get-tuple-element.37), channel_id=1, source_target_pairs={{4,0},{5,1},{6,2},{7,3},{8,4},{9,5},{10,6},{11,7},{12,8},{13,9},{1... | collective-permute-start | bytes 1966088 | tf_op jit(solution)/shard_map/ppermute | solution.py:16
  108.0 19.3 %collective-permute-start.17 = (bf16[2,128,1280]{2,1,0:T(8,128)(2,1)S(1)}, bf16[2,128,1280]{2,1,0:T(8,128)(2,1)S(1)}, u32[]{:S(2)}, u32[]{:S(2)}) collective-permute-start(bf16[2,128,1280]{2,1,0:T(8,128)(2,1)S(1)} %get-tuple-element.36), channel_id=1, source_target_pairs={{0,4},{1,5},{2,6},{3,7},{4,8},{5,9},{6,10},{7,11},{8,12},{9,13},{1... | collective-permute-start | bytes 1966088 | tf_op jit(solution)/shard_map/ppermute | solution.py:16
  113.2 14.0 %copy-start.11 = (bf16[2,128,1280]{2,1,0:T(8,128)(2,1)S(1)}, bf16[2,128,1280]{2,1,0:T(8,128)(2,1)}, u32[]{:S(2)}) copy-start(bf16[2,128,1280]{2,1,0:T(8,128)(2,1)} %get-tuple-element.21) | copy-start | bytes 1966084
  113.9 21.4 %collective-permute-start.21 = (bf16[2,128,1280]{2,1,0:T(8,128)(2,1)S(1)}, bf16[2,128,1280]{2,1,0:T(8,128)(2,1)S(1)}, u32[]{:S(2)}, u32[]{:S(2)}) collective-permute-start(bf16[2,128,1280]{2,1,0:T(8,128)(2,1)S(1)} %get-tuple-element.38), channel_id=1, source_target_pairs={{0,2},{1,3},{2,0},{3,1},{4,6},{5,7},{6,4},{7,5},{8,10},{9,11},{10,... | collective-permute-start | bytes 1966088 | tf_op jit(solution)/shard_map/ppermute | solution.py:16
  114.0 26.1 %collective-permute-start.22 = (bf16[2,128,1280]{2,1,0:T(8,128)(2,1)S(1)}, bf16[2,128,1280]{2,1,0:T(8,128)(2,1)S(1)}, u32[]{:S(2)}, u32[]{:S(2)}) collective-permute-start(bf16[2,128,1280]{2,1,0:T(8,128)(2,1)S(1)} %get-tuple-element.40), channel_id=1, source_target_pairs={{4,0},{5,1},{6,2},{7,3},{8,4},{9,5},{10,6},{11,7},{12,8},{13,9},{1... | collective-permute-start | bytes 1966088 | tf_op jit(solution)/shard_map/ppermute | solution.py:16
  121.8 19.0 %collective-permute-start.23 = (bf16[2,128,1280]{2,1,0:T(8,128)(2,1)S(1)}, bf16[2,128,1280]{2,1,0:T(8,128)(2,1)S(1)}, u32[]{:S(2)}, u32[]{:S(2)}) collective-permute-start(bf16[2,128,1280]{2,1,0:T(8,128)(2,1)S(1)} %get-tuple-element.39), channel_id=1, source_target_pairs={{0,4},{1,5},{2,6},{3,7},{4,8},{5,9},{6,10},{7,11},{8,12},{9,13},{1... | collective-permute-start | bytes 1966088 | tf_op jit(solution)/shard_map/ppermute | solution.py:16
  128.8 12.0 %copy-start.12 = (bf16[2,128,1280]{2,1,0:T(8,128)(2,1)S(1)}, bf16[2,128,1280]{2,1,0:T(8,128)(2,1)}, u32[]{:S(2)}) copy-start(bf16[2,128,1280]{2,1,0:T(8,128)(2,1)} %get-tuple-element.28) | copy-start | bytes 1966084

commit v13 on v12

--- a/solution.py
+++ b/solution.py
@@ -237,9 +237,8 @@
     for c, first in enumerate(starts):
         own = jnp.stack([keys[:, first : first + width], values[:, first : first + width]])
         firsts.append(forward_relay(own, count, None))
-    for c in range(len(starts)):
-        seconds.append(forward_second(firsts[c], count, None))
     for c, first in enumerate(starts):
+        seconds.append(forward_second(firsts[c], count, dqs[c - 1] if c else None))
         dq, parts = chunk_kernel(forward_mask, queries, out_grad, seconds[c], first // HD, inv_root)
         dqs.append(dq)
         outs.append(parts)

time: 144 us -> 148 us (1.028)
  starting transfers between devices: 42.9 us -> 45.6 us
  local copies, waits for them, and re-layouts: 3.31 us -> 5.03 us
    ppermute x24, starting transfers between devices: 42.9 us -> 45.6 us  [send(): return lax.ppermute(value, 'tm', pairs)]
    unnamed x37, local copies, waits for them, and re-layouts: 1.85 us -> 3.58 us
  transfers between devices with their start and end apart: 24 -> 24, of which waited for: 14 -> 14; matrix products, arithmetic and copies ran while one was open for 9% -> 8% of each run, Pallas kernels for 20% -> 9%
where the time goes in v13:
time: 148 us
  waiting for transfers between devices  52.7 us (36%)
  starting transfers between devices  45.6 us (31%)
  Pallas kernels  28 us (19%)
  other arithmetic  15.2 us (10%)
  local copies, waits for them, and re-layouts  5.03 us (3%)
    ppermute x24, waiting for transfers between devices, send(): return lax.ppermute(value, 'tm', pairs)  52.7 us
    ppermute x24, starting transfers between devices, send(): return lax.ppermute(value, 'tm', pairs)  45.6 us
    pallas_call x2, Pallas kernels, attention_backward(): pl.pallas_call(kernel, grid=(heads // STEP_HEADS,), in_specs=in_specs, ou...  28 us
    another operation x4, other arithmetic, forward_second(): ahead = jnp.stack([own, from_cross, from_below, from_above])  5.33 us
    unnamed x37, local copies, waits for them, and re-layouts  3.58 us
    convert_element_type x2, other arithmetic, return_second(): cross_sum.astype(jnp.bfloat16)  3.55 us
  transfers between devices with their start and end apart: 24, of which 14 were waited for; matrix products, arithmetic and copies ran while one was open for 8% of the time, Pallas kernels for 9%

profile of v13, /device:TPU:0, one launch (start us, length us, event | category | flops | bytes accessed | tf_op | source)
XLA Modules:
  0.0 147.7 jit_solution(216206030630655722)
XLA Ops:
  0.6 1.4 slice_bitcast_fusion.14
  2.0 0.9 fusion.30
  2.9 3.0 %collective-permute-start = (bf16[2,128,1280]{2,1,0:T(8,128)(2,1)}, bf16[2,128,1280]{2,1,0:T(8,128)(2,1)}, u32[]{:S(2)}, u32[]{:S(2)}) collective-permute-start(bf16[2,128,1280]{2,1,0:T(8,128)(2,1)} %get-tuple-element.50.refs_0_), channel_id=1, source_target_pairs={{0,2},{1,3},{2,0},{3,1},{4,6},{5,7},{6,4},{7,5},{8,10},{9,11},{10,... | collective-permute-start | bytes 1966088 | tf_op jit(solution)/shard_map/ppermute | solution.py:16
  5.9 3.5 %collective-permute-start.1 = (bf16[2,128,1280]{2,1,0:T(8,128)(2,1)}, bf16[2,128,1280]{2,1,0:T(8,128)(2,1)S(1)}, u32[]{:S(2)}, u32[]{:S(2)}) collective-permute-start(bf16[2,128,1280]{2,1,0:T(8,128)(2,1)} %get-tuple-element.50.refs_0_), channel_id=1, source_target_pairs={{0,4},{1,5},{2,6},{3,7},{4,8},{5,9},{6,10},{7,11},{8,12},{9,13},{1... | collective-permute-start | bytes 1966088 | tf_op jit(solution)/shard_map/ppermute | solution.py:16
  9.4 1.3 collective-permute-start.2
  10.7 0.9 fusion.29
  11.7 0.5 collective-permute-start.6
  12.2 4.6 %collective-permute-start.7 = (bf16[2,128,1280]{2,1,0:T(8,128)(2,1)}, bf16[2,128,1280]{2,1,0:T(8,128)(2,1)S(1)}, u32[]{:S(2)}, u32[]{:S(2)}) collective-permute-start(bf16[2,128,1280]{2,1,0:T(8,128)(2,1)} %get-tuple-element.56.refs_0_), channel_id=1, source_target_pairs={{0,4},{1,5},{2,6},{3,7},{4,8},{5,9},{6,10},{7,11},{8,12},{9,13},{1... | collective-permute-start | bytes 1966088 | tf_op jit(solution)/shard_map/ppermute | solution.py:16
  16.8 0.1 copy.9
  17.0 4.8 %collective-permute-done.refs_1_ = bf16[2,128,1280]{2,1,0:T(8,128)(2,1)} collective-permute-done((bf16[2,128,1280]{2,1,0:T(8,128)(2,1)}, bf16[2,128,1280]{2,1,0:T(8,128)(2,1)}, u32[]{:S(2)}, u32[]{:S(2)}) %collective-permute-start) | collective-permute-done | bytes 655392 | tf_op jit(solution)/shard_map/ppermute | solution.py:16
  21.8 1.3 collective-permute-start.8
  23.1 1.7 %collective-permute-done.1.refs_2_ = bf16[2,128,1280]{2,1,0:T(8,128)(2,1)S(1)} collective-permute-done((bf16[2,128,1280]{2,1,0:T(8,128)(2,1)}, bf16[2,128,1280]{2,1,0:T(8,128)(2,1)S(1)}, u32[]{:S(2)}, u32[]{:S(2)}) %collective-permute-start.1) | collective-permute-done | bytes 655392 | tf_op jit(solution)/shard_map/ppermute | solution.py:16
  24.8 4.4 %collective-permute-done.2.refs_3_ = bf16[2,128,1280]{2,1,0:T(8,128)(2,1)} collective-permute-done((bf16[2,128,1280]{2,1,0:T(8,128)(2,1)}, bf16[2,128,1280]{2,1,0:T(8,128)(2,1)}, u32[]{:S(2)}, u32[]{:S(2)}) %collective-permute-start.2) | collective-permute-done | bytes 655392 | tf_op jit(solution)/shard_map/ppermute | solution.py:16
  29.3 1.6 %pad_maximum_fusion = bf16[4,2,128,1280]{3,2,1,0:T(8,128)(2,1)S(1)} fusion(bf16[1,2,128,1280]{3,2,1,0:T(8,128)(2,1)} %bitcast.8, bf16[1,2,128,1280]{3,2,1,0:T(8,128)(2,1)S(1)} %bitcast.74, bf16[1,2,128,1280]{3,2,1,0:T(8,128)(2,1)} %bitcast.6, bf16[1,2,128,1280]{3,2,1,0:T(8,128)(2,1)S(1)} %get-tuple-element.49), kind=kLoop, calls=%fused_computation | loop fusion | flops 3932160 | bytes 5242880 | tf_op jit(solution)/shard_map/stack | solution.py:155
  30.9 0.1 collective-permute-start.3
  31.1 0.1 select_reduce_fusion
  31.2 0.1 multiply_reduce_fusion
  31.3 3.6 %collective-permute-start.4 = (bf16[2,128,1280]{2,1,0:T(8,128)(2,1)}, bf16[2,128,1280]{2,1,0:T(8,128)(2,1)S(1)}, u32[]{:S(2)}, u32[]{:S(2)}) collective-permute-start(bf16[2,128,1280]{2,1,0:T(8,128)(2,1)} %collective-permute-done.refs_1_), channel_id=1, source_target_pairs={{0,5},{3,6},{4,9},{7,10},{8,13},{11,14},{16,21},{19,22},{20,25},{2... | collective-permute-start | bytes 1966088 | tf_op jit(solution)/shard_map/ppermute | solution.py:16
  34.9 0.0 collective-permute-done.6.refs_1_
  34.9 0.7 collective-permute-start.5
  35.6 1.4 fusion.24.mask_ref
  37.0 0.4 collective-permute-done.7.refs_2_
  37.5 4.0 %collective-permute-done.8.refs_3_ = bf16[2,128,1280]{2,1,0:T(8,128)(2,1)S(1)} collective-permute-done((bf16[2,128,1280]{2,1,0:T(8,128)(2,1)}, bf16[2,128,1280]{2,1,0:T(8,128)(2,1)S(1)}, u32[]{:S(2)}, u32[]{:S(2)}) %collective-permute-start.8) | collective-permute-done | bytes 655392 | tf_op jit(solution)/shard_map/ppermute | solution.py:16
  41.5 1.8 %pad_maximum_fusion.1 = bf16[4,2,128,1280]{3,2,1,0:T(8,128)(2,1)S(1)} fusion(bf16[1,2,128,1280]{3,2,1,0:T(8,128)(2,1)S(1)} %bitcast.75, bf16[1,2,128,1280]{3,2,1,0:T(8,128)(2,1)} %bitcast.73, bf16[1,2,128,1280]{3,2,1,0:T(8,128)(2,1)} %bitcast.72, bf16[1,2,128,1280]{3,2,1,0:T(8,128)(2,1)S(1)} %get-tuple-element.55), kind=kLoop, calls=%fused_computation.1 | loop fusion | flops 3932160 | bytes 5242880 | tf_op jit(solution)/shard_map/stack | solution.py:155
  43.4 0.0 copy-start.1
  43.4 1.1 collective-permute-done.4.refs_5_
  44.5 0.9 copy-done.13
  45.4 0.8 copy-done.14
  46.2 0.0 collective-permute-done.3.refs_4_
  46.2 14.0 %shard_map.85 = (bf16[128,1280]{1,0:T(8,128)(2,1)}, bf16[2,128,1280]{2,1,0:T(8,128)(2,1)}, bf16[4,2,128,1280]{3,2,1,0:T(8,128)(2,1)}, bf16[2,128,1280]{2,1,0:T(8...) custom-call(s32[128,1280]{1,0:T(8,128)} %fusion.24.mask_ref, ...), custom_call_target="tpu_custom_call" | custom-call | flops 2516582400 | bytes 14745600 | tf_op jit(solution)/shard_map/pallas_call | solution.py:127
  60.2 3.0 %collective-permute-start.9 = (bf16[4,2,128,1280]{3,2,1,0:T(8,128)(2,1)S(1)}, bf16[4,2,128,1280]{3,2,1,0:T(8,128)(2,1)}, u32[]{:S(2)}, u32[]{:S(2)}) collective-permute-start(bf16[4,2,128,1280]{3,2,1,0:T(8,128)(2,1)S(1)} %pad_maximum_fusion.1), channel_id=1, source_target_pairs={{0,1},{1,0},{2,3},{3,2},{4,5},{5,4},{6,7},{7,6},{8,9},{9,8},{10,11... | collective-permute-start | bytes 7864328 | tf_op jit(solution)/shard_map/ppermute | solution.py:16
  63.3 0.1 collective-permute-start.12
  63.3 3.5 %collective-permute-start.10 = (bf16[2,128,1280]{2,1,0:T(8,128)(2,1)S(1)}, bf16[2,128,1280]{2,1,0:T(8,128)(2,1)S(1)}, u32[]{:S(2)}, u32[]{:S(2)}) collective-permute-start(bf16[2,128,1280]{2,1,0:T(8,128)(2,1)S(1)} %copy-done.1), channel_id=1, source_target_pairs={{0,5},{3,6},{4,9},{7,10},{8,13},{11,14},{16,21},{19,22},{20,25},{2... | collective-permute-start | bytes 1966088 | tf_op jit(solution)/shard_map/ppermute | solution.py:16
  66.9 0.7 collective-permute-start.11
  67.6 7.3 %collective-permute-done.10.refs_5_ = bf16[2,128,1280]{2,1,0:T(8,128)(2,1)S(1)} collective-permute-done((bf16[2,128,1280]{2,1,0:T(8,128)(2,1)S(1)}, bf16[2,128,1280]{2,1,0:T(8,128)(2,1)S(1)}, u32[]{:S(2)}, u32[]{:S(2)}) %collective-permute-start.10) | collective-permute-done | bytes 655392 | tf_op jit(solution)/shard_map/ppermute | solution.py:16
  74.9 0.0 collective-permute-done.11.refs_6_
  74.9 0.8 copy-done.15
  75.7 0.8 copy-done.16
  76.6 14.0 %shard_map.86 = (bf16[128,1280]{1,0:T(8,128)(2,1)}, bf16[2,128,1280]{2,1,0:T(8,128)(2,1)}, bf16[4,2,128,1280]{3,2,1,0:T(8,128)(2,1)}, bf16[2,128,1280]{2,1,0:T(8...) custom-call(s32[128,1280]{1,0:T(8,128)} %fusion.24.mask_ref, ...), custom_call_target="tpu_custom_call" | custom-call | flops 2516582400 | bytes 14745600 | tf_op jit(solution)/shard_map/pallas_call | solution.py:127
  90.6 2.4 %collective-permute-start.18 = (bf16[4,2,128,1280]{3,2,1,0:T(8,128)(2,1)}, bf16[4,2,128,1280]{3,2,1,0:T(8,128)(2,1)S(1)}, u32[]{:S(2)}, u32[]{:S(2)}) collective-permute-start(bf16[4,2,128,1280]{3,2,1,0:T(8,128)(2,1)} %get-tuple-element.33), channel_id=1, source_target_pairs={{0,1},{1,0},{2,3},{3,2},{4,5},{5,4},{6,7},{7,6},{8,9},{9,8},{10,11... | collective-permute-start | bytes 7864328 | tf_op jit(solution)/shard_map/ppermute | solution.py:16
  93.0 1.3 collective-permute-start.13
  94.3 0.7 collective-permute-start.14
  95.0 1.3 collective-permute-start.19
  96.3 8.8 %collective-permute-done.13 = bf16[2,128,1280]{2,1,0:T(8,128)(2,1)S(1)} collective-permute-done((bf16[2,128,1280]{2,1,0:T(8,128)(2,1)}, bf16[2,128,1280]{2,1,0:T(8,128)(2,1)S(1)}, u32[]{:S(2)}, u32[]{:S(2)}) %collective-permute-start.13) | collective-permute-done | bytes 655392 | tf_op jit(solution)/shard_map/ppermute | solution.py:16
  105.1 0.7 collective-permute-start.20
  105.9 2.9 %fusion.13 = (bf16[2,128,1280]{2,1,0:T(8,128)(2,1)S(1)}, bf16[2,128,1280]{2,1,0:T(8,128)(2,1)S(1)}, bf16[2,128,1280]{2,1,0:T(8,128)(2,1)S(1)}) fusion(bf16[2,128,1280]{2,1,0:T(8,128)(2,1)S(1)} %collective-permute-done.14, bf16[2,128,1280]{2,1,0:T(8,128)(2,1)S(1)} %collective-permute-done.13, bf16[2,128,1280]{2,1,0:T(8,128)(2,1)} %get-tuple-element.27, ...), kind=kLoop, calls=%fused_computation.22 | loop fusion | flops 5242880 | bytes 7208960 | tf_op jit(solution)/shard_map/convert_element_type | solution.py:194
  108.8 2.5 %collective-permute-start.15 = (bf16[2,128,1280]{2,1,0:T(8,128)(2,1)S(1)}, bf16[2,128,1280]{2,1,0:T(8,128)(2,1)S(1)}, u32[]{:S(2)}, u32[]{:S(2)}) collective-permute-start(bf16[2,128,1280]{2,1,0:T(8,128)(2,1)S(1)} %get-tuple-element.39), channel_id=1, source_target_pairs={{0,2},{1,3},{2,0},{3,1},{4,6},{5,7},{6,4},{7,5},{8,10},{9,11},{10,... | collective-permute-start | bytes 1966088 | tf_op jit(solution)/shard_map/ppermute | solution.py:16
  111.3 1.3 collective-permute-start.16
  112.6 0.9 pad_maximum_fusion.4
  113.5 4.6 %collective-permute-start.17 = (bf16[2,128,1280]{2,1,0:T(8,128)(2,1)S(1)}, bf16[2,128,1280]{2,1,0:T(8,128)(2,1)S(1)}, u32[]{:S(2)}, u32[]{:S(2)}) collective-permute-start(bf16[2,128,1280]{2,1,0:T(8,128)(2,1)S(1)} %get-tuple-element.40), channel_id=1, source_target_pairs={{0,4},{1,5},{2,6},{3,7},{4,8},{5,9},{6,10},{7,11},{8,12},{9,13},{1... | collective-permute-start | bytes 1966088 | tf_op jit(solution)/shard_map/ppermute | solution.py:16
  118.1 0.7 fusion.4
  118.8 0.2 collective-permute-start.21
  119.0 1.3 collective-permute-start.22
  120.3 6.2 %collective-permute-done.15 = bf16[2,128,1280]{2,1,0:T(8,128)(2,1)S(1)} collective-permute-done((bf16[2,128,1280]{2,1,0:T(8,128)(2,1)S(1)}, bf16[2,128,1280]{2,1,0:T(8,128)(2,1)S(1)}, u32[]{:S(2)}, u32[]{:S(2)}) %collective-permute-start.15) | collective-permute-done | bytes 655392 | tf_op jit(solution)/shard_map/ppermute | solution.py:16
  126.5 3.5 %collective-permute-start.23 = (bf16[2,128,1280]{2,1,0:T(8,128)(2,1)S(1)}, bf16[2,128,1280]{2,1,0:T(8,128)(2,1)S(1)}, u32[]{:S(2)}, u32[]{:S(2)}) collective-permute-start(bf16[2,128,1280]{2,1,0:T(8,128)(2,1)S(1)} %get-tuple-element.43), channel_id=1, source_target_pairs={{0,4},{1,5},{2,6},{3,7},{4,8},{5,9},{6,10},{7,11},{8,12},{9,13},{1... | collective-permute-start | bytes 1966088 | tf_op jit(solution)/shard_map/ppermute | solution.py:16
  130.0 0.8 collective-permute-done.16
  130.8 1.0 collective-permute-done.17
  131.8 1.5 %fusion.17 = bf16[2,128,1280]{2,1,0:T(8,128)(2,1)S(1)} fusion(bf16[2,128,1280]{2,1,0:T(8,128)(2,1)S(1)} %collective-permute-done.17, bf16[2,128,1280]{2,1,0:T(8,128)(2,1)S(1)} %collective-permute-done.16, bf16[2,128,1280]{2,1,0:T(8,128)(2,1)S(1)} %collective-permute-done.15, bf16[2,128,1280]{2,1,0:T(8,128)(2,1)S(1)} %copy-done.8, ...), kind=kLoop, calls=%fused_computation.27 | loop fusion | flops 3276800 | bytes 3932160 | tf_op jit(solution)/shard_map/convert.11
  133.4 7.2 %collective-permute-done.21 = bf16[2,128,1280]{2,1,0:T(8,128)(2,1)S(1)} collective-permute-done((bf16[2,128,1280]{2,1,0:T(8,128)(2,1)S(1)}, bf16[2,128,1280]{2,1,0:T(8,128)(2,1)S(1)}, u32[]{:S(2)}, u32[]{:S(2)}) %collective-permute-start.21) | collective-permute-done | bytes 655392 | tf_op jit(solution)/shard_map/ppermute | solution.py:16
  140.6 2.8 %collective-permute-done.22 = bf16[2,128,1280]{2,1,0:T(8,128)(2,1)S(1)} collective-permute-done((bf16[2,128,1280]{2,1,0:T(8,128)(2,1)S(1)}, bf16[2,128,1280]{2,1,0:T(8,128)(2,1)S(1)}, u32[]{:S(2)}, u32[]{:S(2)}) %collective-permute-start.22) | collective-permute-done | bytes 655392 | tf_op jit(solution)/shard_map/ppermute | solution.py:16
  143.3 2.1 %collective-permute-done.23 = bf16[2,128,1280]{2,1,0:T(8,128)(2,1)S(1)} collective-permute-done((bf16[2,128,1280]{2,1,0:T(8,128)(2,1)S(1)}, bf16[2,128,1280]{2,1,0:T(8,128)(2,1)S(1)}, u32[]{:S(2)}, u32[]{:S(2)}) %collective-permute-start.23) | collective-permute-done | bytes 655392 | tf_op jit(solution)/shard_map/ppermute | solution.py:16
  145.4 0.4 fusion.8
  145.9 0.9 pad_maximum_fusion.6
  146.8 0.9 pad_maximum_fusion.5
  (57 shorter events, 0.3 us)
Async XLA Ops:
  2.9 13.9 %copy-start.12 = (s32[4,3]{1,0:T(4,128)S(1)}, s32[4,3]{1,0:T(4,128)}, u32[]{:S(2)}) copy-start(s32[4,3]{1,0:T(4,128)} %param.10) | copy-start | bytes 148
  2.9 18.9 %collective-permute-start = (bf16[2,128,1280]{2,1,0:T(8,128)(2,1)}, bf16[2,128,1280]{2,1,0:T(8,128)(2,1)}, u32[]{:S(2)}, u32[]{:S(2)}) collective-permute-start(bf16[2,128,1280]{2,1,0:T(8,128)(2,1)} %get-tuple-element.50.refs_0_), channel_id=1, source_target_pairs={{0,2},{1,3},{2,0},{3,1},{4,6},{5,7},{6,4},{7,5},{8,10},{9,11},{10,... | collective-permute-start | bytes 1966088 | tf_op jit(solution)/shard_map/ppermute | solution.py:16
  5.9 18.9 %collective-permute-start.1 = (bf16[2,128,1280]{2,1,0:T(8,128)(2,1)}, bf16[2,128,1280]{2,1,0:T(8,128)(2,1)S(1)}, u32[]{:S(2)}, u32[]{:S(2)}) collective-permute-start(bf16[2,128,1280]{2,1,0:T(8,128)(2,1)} %get-tuple-element.50.refs_0_), channel_id=1, source_target_pairs={{0,4},{1,5},{2,6},{3,7},{4,8},{5,9},{6,10},{7,11},{8,12},{9,13},{1... | collective-permute-start | bytes 1966088 | tf_op jit(solution)/shard_map/ppermute | solution.py:16
  9.4 19.8 %collective-permute-start.2 = (bf16[2,128,1280]{2,1,0:T(8,128)(2,1)}, bf16[2,128,1280]{2,1,0:T(8,128)(2,1)}, u32[]{:S(2)}, u32[]{:S(2)}) collective-permute-start(bf16[2,128,1280]{2,1,0:T(8,128)(2,1)} %get-tuple-element.50.refs_0_), channel_id=1, source_target_pairs={{4,0},{5,1},{6,2},{7,3},{8,4},{9,5},{10,6},{11,7},{12,8},{13,9},{1... | collective-permute-start | bytes 1966088 | tf_op jit(solution)/shard_map/ppermute | solution.py:16
  11.7 23.2 %collective-permute-start.6 = (bf16[2,128,1280]{2,1,0:T(8,128)(2,1)}, bf16[2,128,1280]{2,1,0:T(8,128)(2,1)S(1)}, u32[]{:S(2)}, u32[]{:S(2)}) collective-permute-start(bf16[2,128,1280]{2,1,0:T(8,128)(2,1)} %get-tuple-element.56.refs_0_), channel_id=1, source_target_pairs={{0,2},{1,3},{2,0},{3,1},{4,6},{5,7},{6,4},{7,5},{8,10},{9,11},{10,... | collective-permute-start | bytes 1966088 | tf_op jit(solution)/shard_map/ppermute | solution.py:16
  12.2 25.3 %collective-permute-start.7 = (bf16[2,128,1280]{2,1,0:T(8,128)(2,1)}, bf16[2,128,1280]{2,1,0:T(8,128)(2,1)S(1)}, u32[]{:S(2)}, u32[]{:S(2)}) collective-permute-start(bf16[2,128,1280]{2,1,0:T(8,128)(2,1)} %get-tuple-element.56.refs_0_), channel_id=1, source_target_pairs={{0,4},{1,5},{2,6},{3,7},{4,8},{5,9},{6,10},{7,11},{8,12},{9,13},{1... | collective-permute-start | bytes 1966088 | tf_op jit(solution)/shard_map/ppermute | solution.py:16
  21.8 19.7 %collective-permute-start.8 = (bf16[2,128,1280]{2,1,0:T(8,128)(2,1)}, bf16[2,128,1280]{2,1,0:T(8,128)(2,1)S(1)}, u32[]{:S(2)}, u32[]{:S(2)}) collective-permute-start(bf16[2,128,1280]{2,1,0:T(8,128)(2,1)} %get-tuple-element.56.refs_0_), channel_id=1, source_target_pairs={{4,0},{5,1},{6,2},{7,3},{8,4},{9,5},{10,6},{11,7},{12,8},{13,9},{1... | collective-permute-start | bytes 1966088 | tf_op jit(solution)/shard_map/ppermute | solution.py:16
  24.8 6.1 %copy-start.3 = (bf16[2,128,1280]{2,1,0:T(8,128)(2,1)}, bf16[2,128,1280]{2,1,0:T(8,128)(2,1)S(1)}, u32[]{:S(2)}) copy-start(bf16[2,128,1280]{2,1,0:T(8,128)(2,1)S(1)} %collective-permute-done.1.refs_2_) | copy-start | bytes 1966084
  29.3 1.8 %copy-start.17 = (s32[4]{0:T(128)S(1)}, s32[4]{0:T(128)}, u32[]{:S(2)}) copy-start(s32[4]{0:T(128)} %param.11) | copy-start | bytes 52
  30.9 15.3 %collective-permute-start.3 = (bf16[4,2,128,1280]{3,2,1,0:T(8,128)(2,1)S(1)}, bf16[4,2,128,1280]{3,2,1,0:T(8,128)(2,1)}, u32[]{:S(2)}, u32[]{:S(2)}) collective-permute-start(bf16[4,2,128,1280]{3,2,1,0:T(8,128)(2,1)S(1)} %pad_maximum_fusion), channel_id=1, source_target_pairs={{0,1},{1,0},{2,3},{3,2},{4,5},{5,4},{6,7},{7,6},{8,9},{9,8},{10,11... | collective-permute-start | bytes 7864328 | tf_op jit(solution)/shard_map/ppermute | solution.py:16
  31.3 13.2 %collective-permute-start.4 = (bf16[2,128,1280]{2,1,0:T(8,128)(2,1)}, bf16[2,128,1280]{2,1,0:T(8,128)(2,1)S(1)}, u32[]{:S(2)}, u32[]{:S(2)}) collective-permute-start(bf16[2,128,1280]{2,1,0:T(8,128)(2,1)} %collective-permute-done.refs_1_), channel_id=1, source_target_pairs={{0,5},{3,6},{4,9},{7,10},{8,13},{11,14},{16,21},{19,22},{20,25},{2... | collective-permute-start | bytes 1966088 | tf_op jit(solution)/shard_map/ppermute | solution.py:16
  34.9 6.6 %copy-start = (bf16[2,128,1280]{2,1,0:T(8,128)(2,1)}, bf16[2,128,1280]{2,1,0:T(8,128)(2,1)S(1)}, u32[]{:S(2)}) copy-start(bf16[2,128,1280]{2,1,0:T(8,128)(2,1)S(1)} %collective-permute-done.6.refs_1_) | copy-start | bytes 1966084
  34.9 10.5 %collective-permute-start.5 = (bf16[2,128,1280]{2,1,0:T(8,128)(2,1)}, bf16[2,128,1280]{2,1,0:T(8,128)(2,1)S(1)}, u32[]{:S(2)}, u32[]{:S(2)}) collective-permute-start(bf16[2,128,1280]{2,1,0:T(8,128)(2,1)} %collective-permute-done.refs_1_), channel_id=1, source_target_pairs={{4,1},{7,2},{8,5},{11,6},{12,9},{15,10},{20,17},{23,18},{24,21},{2... | collective-permute-start | bytes 1966088 | tf_op jit(solution)/shard_map/ppermute | solution.py:16
  37.5 4.1 %copy-start.2 = (bf16[2,128,1280]{2,1,0:T(8,128)(2,1)}, bf16[2,128,1280]{2,1,0:T(8,128)(2,1)S(1)}, u32[]{:S(2)}) copy-start(bf16[2,128,1280]{2,1,0:T(8,128)(2,1)S(1)} %collective-permute-done.7.refs_2_) | copy-start | bytes 1966084
  41.5 1.9 %copy-start.4 = (bf16[2,128,1280]{2,1,0:T(8,128)(2,1)}, bf16[2,128,1280]{2,1,0:T(8,128)(2,1)S(1)}, u32[]{:S(2)}) copy-start(bf16[2,128,1280]{2,1,0:T(8,128)(2,1)S(1)} %collective-permute-done.8.refs_3_) | copy-start | bytes 1966084
  43.4 20.0 %copy-start.1 = (bf16[2,128,1280]{2,1,0:T(8,128)(2,1)S(1)}, bf16[2,128,1280]{2,1,0:T(8,128)(2,1)}, u32[]{:S(2)}) copy-start(bf16[2,128,1280]{2,1,0:T(8,128)(2,1)} %copy-done) | copy-start | bytes 1966084
  44.5 0.9 copy-start.13
  45.4 0.8 copy-start.14
  60.2 16.3 %collective-permute-start.9 = (bf16[4,2,128,1280]{3,2,1,0:T(8,128)(2,1)S(1)}, bf16[4,2,128,1280]{3,2,1,0:T(8,128)(2,1)}, u32[]{:S(2)}, u32[]{:S(2)}) collective-permute-start(bf16[4,2,128,1280]{3,2,1,0:T(8,128)(2,1)S(1)} %pad_maximum_fusion.1), channel_id=1, source_target_pairs={{0,1},{1,0},{2,3},{3,2},{4,5},{5,4},{6,7},{7,6},{8,9},{9,8},{10,11... | collective-permute-start | bytes 7864328 | tf_op jit(solution)/shard_map/ppermute | solution.py:16
  63.3 42.6 %collective-permute-start.12 = (bf16[4,2,128,1280]{3,2,1,0:T(8,128)(2,1)}, bf16[4,2,128,1280]{3,2,1,0:T(8,128)(2,1)}, u32[]{:S(2)}, u32[]{:S(2)}) collective-permute-start(bf16[4,2,128,1280]{3,2,1,0:T(8,128)(2,1)} %get-tuple-element.26), channel_id=1, source_target_pairs={{0,1},{1,0},{2,3},{3,2},{4,5},{5,4},{6,7},{7,6},{8,9},{9,8},{10,11... | collective-permute-start | bytes 7864328 | tf_op jit(solution)/shard_map/ppermute | solution.py:16
  63.3 11.6 %collective-permute-start.10 = (bf16[2,128,1280]{2,1,0:T(8,128)(2,1)S(1)}, bf16[2,128,1280]{2,1,0:T(8,128)(2,1)S(1)}, u32[]{:S(2)}, u32[]{:S(2)}) collective-permute-start(bf16[2,128,1280]{2,1,0:T(8,128)(2,1)S(1)} %copy-done.1), channel_id=1, source_target_pairs={{0,5},{3,6},{4,9},{7,10},{8,13},{11,14},{16,21},{19,22},{20,25},{2... | collective-permute-start | bytes 1966088 | tf_op jit(solution)/shard_map/ppermute | solution.py:16
  66.9 8.1 %collective-permute-start.11 = (bf16[2,128,1280]{2,1,0:T(8,128)(2,1)S(1)}, bf16[2,128,1280]{2,1,0:T(8,128)(2,1)S(1)}, u32[]{:S(2)}, u32[]{:S(2)}) collective-permute-start(bf16[2,128,1280]{2,1,0:T(8,128)(2,1)S(1)} %copy-done.1), channel_id=1, source_target_pairs={{4,1},{7,2},{8,5},{11,6},{12,9},{15,10},{20,17},{23,18},{24,21},{2... | collective-permute-start | bytes 1966088 | tf_op jit(solution)/shard_map/ppermute | solution.py:16
  74.9 0.8 copy-start.15
  75.7 0.8 copy-start.16
  90.6 27.5 %collective-permute-start.18 = (bf16[4,2,128,1280]{3,2,1,0:T(8,128)(2,1)}, bf16[4,2,128,1280]{3,2,1,0:T(8,128)(2,1)S(1)}, u32[]{:S(2)}, u32[]{:S(2)}) collective-permute-start(bf16[4,2,128,1280]{3,2,1,0:T(8,128)(2,1)} %get-tuple-element.33), channel_id=1, source_target_pairs={{0,1},{1,0},{2,3},{3,2},{4,5},{5,4},{6,7},{7,6},{8,9},{9,8},{10,11... | collective-permute-start | bytes 7864328 | tf_op jit(solution)/shard_map/ppermute | solution.py:16
  93.0 12.1 %collective-permute-start.13 = (bf16[2,128,1280]{2,1,0:T(8,128)(2,1)}, bf16[2,128,1280]{2,1,0:T(8,128)(2,1)S(1)}, u32[]{:S(2)}, u32[]{:S(2)}) collective-permute-start(bf16[2,128,1280]{2,1,0:T(8,128)(2,1)} %get-tuple-element.28), channel_id=1, source_target_pairs={{5,0},{6,3},{9,4},{10,7},{13,8},{14,11},{21,16},{22,19},{25,20},{2... | collective-permute-start | bytes 1966088 | tf_op jit(solution)/shard_map/ppermute | solution.py:16
  94.3 11.5 %collective-permute-start.14 = (bf16[2,128,1280]{2,1,0:T(8,128)(2,1)}, bf16[2,128,1280]{2,1,0:T(8,128)(2,1)S(1)}, u32[]{:S(2)}, u32[]{:S(2)}) collective-permute-start(bf16[2,128,1280]{2,1,0:T(8,128)(2,1)} %get-tuple-element.29), channel_id=1, source_target_pairs={{1,4},{2,7},{5,8},{6,11},{9,12},{10,15},{17,20},{18,23},{21,24},{2... | collective-permute-start | bytes 1966088 | tf_op jit(solution)/shard_map/ppermute | solution.py:16
  95.0 18.4 %collective-permute-start.19 = (bf16[2,128,1280]{2,1,0:T(8,128)(2,1)}, bf16[2,128,1280]{2,1,0:T(8,128)(2,1)S(1)}, u32[]{:S(2)}, u32[]{:S(2)}) collective-permute-start(bf16[2,128,1280]{2,1,0:T(8,128)(2,1)} %get-tuple-element.35), channel_id=1, source_target_pairs={{5,0},{6,3},{9,4},{10,7},{13,8},{14,11},{21,16},{22,19},{25,20},{2... | collective-permute-start | bytes 1966088 | tf_op jit(solution)/shard_map/ppermute | solution.py:16
  105.1 12.9 %collective-permute-start.20 = (bf16[2,128,1280]{2,1,0:T(8,128)(2,1)}, bf16[2,128,1280]{2,1,0:T(8,128)(2,1)S(1)}, u32[]{:S(2)}, u32[]{:S(2)}) collective-permute-start(bf16[2,128,1280]{2,1,0:T(8,128)(2,1)} %get-tuple-element.36), channel_id=1, source_target_pairs={{1,4},{2,7},{5,8},{6,11},{9,12},{10,15},{17,20},{18,23},{21,24},{2... | collective-permute-start | bytes 1966088 | tf_op jit(solution)/shard_map/ppermute | solution.py:16
  105.9 6.7 %copy-start.10 = (bf16[128,1280]{1,0:T(8,128)(2,1)S(1)}, bf16[128,1280]{1,0:T(8,128)(2,1)}, u32[]{:S(2)}) copy-start(bf16[128,1280]{1,0:T(8,128)(2,1)} %get-tuple-element.21) | copy-start | bytes 983044
  105.9 6.7 %copy-start.11 = (bf16[128,1280]{1,0:T(8,128)(2,1)S(1)}, bf16[128,1280]{1,0:T(8,128)(2,1)}, u32[]{:S(2)}) copy-start(bf16[128,1280]{1,0:T(8,128)(2,1)} %get-tuple-element.24) | copy-start | bytes 983044
  105.9 12.2 %copy-start.7 = (bf16[2,128,1280]{2,1,0:T(8,128)(2,1)S(1)}, bf16[2,128,1280]{2,1,0:T(8,128)(2,1)}, u32[]{:S(2)}) copy-start(bf16[2,128,1280]{2,1,0:T(8,128)(2,1)} %get-tuple-element.38) | copy-start | bytes 1966084
  108.8 9.4 %copy-start.5 = (bf16[2,128,1280]{2,1,0:T(8,128)(2,1)S(1)}, bf16[2,128,1280]{2,1,0:T(8,128)(2,1)}, u32[]{:S(2)}) copy-start(bf16[2,128,1280]{2,1,0:T(8,128)(2,1)} %get-tuple-element.34) | copy-start | bytes 1966084
  108.8 9.4 %copy-start.6 = (bf16[2,128,1280]{2,1,0:T(8,128)(2,1)S(1)}, bf16[2,128,1280]{2,1,0:T(8,128)(2,1)}, u32[]{:S(2)}) copy-start(bf16[2,128,1280]{2,1,0:T(8,128)(2,1)} %get-tuple-element.37) | copy-start | bytes 1966084
  108.8 17.7 %collective-permute-start.15 = (bf16[2,128,1280]{2,1,0:T(8,128)(2,1)S(1)}, bf16[2,128,1280]{2,1,0:T(8,128)(2,1)S(1)}, u32[]{:S(2)}, u32[]{:S(2)}) collective-permute-start(bf16[2,128,1280]{2,1,0:T(8,128)(2,1)S(1)} %get-tuple-element.39), channel_id=1, source_target_pairs={{0,2},{1,3},{2,0},{3,1},{4,6},{5,7},{6,4},{7,5},{8,10},{9,11},{10,... | collective-permute-start | bytes 1966088 | tf_op jit(solution)/shard_map/ppermute | solution.py:16
  111.3 19.5 %collective-permute-start.16 = (bf16[2,128,1280]{2,1,0:T(8,128)(2,1)S(1)}, bf16[2,128,1280]{2,1,0:T(8,128)(2,1)S(1)}, u32[]{:S(2)}, u32[]{:S(2)}) collective-permute-start(bf16[2,128,1280]{2,1,0:T(8,128)(2,1)S(1)} %get-tuple-element.41), channel_id=1, source_target_pairs={{4,0},{5,1},{6,2},{7,3},{8,4},{9,5},{10,6},{11,7},{12,8},{13,9},{1... | collective-permute-start | bytes 1966088 | tf_op jit(solution)/shard_map/ppermute | solution.py:16
  113.5 18.3 %collective-permute-start.17 = (bf16[2,128,1280]{2,1,0:T(8,128)(2,1)S(1)}, bf16[2,128,1280]{2,1,0:T(8,128)(2,1)S(1)}, u32[]{:S(2)}, u32[]{:S(2)}) collective-permute-start(bf16[2,128,1280]{2,1,0:T(8,128)(2,1)S(1)} %get-tuple-element.40), channel_id=1, source_target_pairs={{0,4},{1,5},{2,6},{3,7},{4,8},{5,9},{6,10},{7,11},{8,12},{9,13},{1... | collective-permute-start | bytes 1966088 | tf_op jit(solution)/shard_map/ppermute | solution.py:16
  118.1 13.7 %copy-start.8 = (bf16[2,128,1280]{2,1,0:T(8,128)(2,1)S(1)}, bf16[2,128,1280]{2,1,0:T(8,128)(2,1)}, u32[]{:S(2)}) copy-start(bf16[2,128,1280]{2,1,0:T(8,128)(2,1)} %get-tuple-element.25) | copy-start | bytes 1966084
  118.8 21.7 %collective-permute-start.21 = (bf16[2,128,1280]{2,1,0:T(8,128)(2,1)S(1)}, bf16[2,128,1280]{2,1,0:T(8,128)(2,1)S(1)}, u32[]{:S(2)}, u32[]{:S(2)}) collective-permute-start(bf16[2,128,1280]{2,1,0:T(8,128)(2,1)S(1)} %get-tuple-element.42), channel_id=1, source_target_pairs={{0,2},{1,3},{2,0},{3,1},{4,6},{5,7},{6,4},{7,5},{8,10},{9,11},{10,... | collective-permute-start | bytes 1966088 | tf_op jit(solution)/shard_map/ppermute | solution.py:16
  119.0 24.3 %collective-permute-start.22 = (bf16[2,128,1280]{2,1,0:T(8,128)(2,1)S(1)}, bf16[2,128,1280]{2,1,0:T(8,128)(2,1)S(1)}, u32[]{:S(2)}, u32[]{:S(2)}) collective-permute-start(bf16[2,128,1280]{2,1,0:T(8,128)(2,1)S(1)} %get-tuple-element.44), channel_id=1, source_target_pairs={{4,0},{5,1},{6,2},{7,3},{8,4},{9,5},{10,6},{11,7},{12,8},{13,9},{1... | collective-permute-start | bytes 1966088 | tf_op jit(solution)/shard_map/ppermute | solution.py:16
  126.5 18.9 %collective-permute-start.23 = (bf16[2,128,1280]{2,1,0:T(8,128)(2,1)S(1)}, bf16[2,128,1280]{2,1,0:T(8,128)(2,1)S(1)}, u32[]{:S(2)}, u32[]{:S(2)}) collective-permute-start(bf16[2,128,1280]{2,1,0:T(8,128)(2,1)S(1)} %get-tuple-element.43), channel_id=1, source_target_pairs={{0,4},{1,5},{2,6},{3,7},{4,8},{5,9},{6,10},{7,11},{8,12},{9,13},{1... | collective-permute-start | bytes 1966088 | tf_op jit(solution)/shard_map/ppermute | solution.py:16
  133.3 12.1 %copy-start.9 = (bf16[2,128,1280]{2,1,0:T(8,128)(2,1)S(1)}, bf16[2,128,1280]{2,1,0:T(8,128)(2,1)}, u32[]{:S(2)}) copy-start(bf16[2,128,1280]{2,1,0:T(8,128)(2,1)} %get-tuple-element.32) | copy-start | bytes 1966084

commit v14 on v12

--- a/solution.py
+++ b/solution.py
@@ -183,15 +183,23 @@
     return [to_partner, diag_back_below, diag_back_above]
 
 
-def return_second(outs, first, count, after):
-    core, cross, down, up, diag_up, diag_down, back = route(count)
+def return_sums(outs, first):
     own_part, to_core, cross_part, below_part, above_part, diag_b_part, diag_a_part = outs
     to_partner, diag_back_below, diag_back_above = first
     wide = lambda tensor: tensor.astype(jnp.float32)
     cross_sum = wide(cross_part) + wide(to_partner[1]) + wide(diag_back_below) + wide(diag_back_above)
     below_sum = wide(below_part) + wide(to_partner[2])
     above_sum = wide(above_part) + wide(to_partner[3])
-    sums = (cross_sum.astype(jnp.bfloat16), below_sum.astype(jnp.bfloat16), above_sum.astype(jnp.bfloat16))
+    return (cross_sum.astype(jnp.bfloat16), below_sum.astype(jnp.bfloat16), above_sum.astype(jnp.bfloat16))
+
+
+def return_second(outs, first, count, after, sums=None):
+    core, cross, down, up, diag_up, diag_down, back = route(count)
+    own_part, to_core, cross_part, below_part, above_part, diag_b_part, diag_a_part = outs
+    to_partner, diag_back_below, diag_back_above = first
+    wide = lambda tensor: tensor.astype(jnp.float32)
+    if sums is None:
+        sums = return_sums(outs, first)
     if after is not None:
         sums, _ = lax.optimization_barrier((sums, after))
     got_cross = send(sums[0], cross)
@@ -240,15 +248,21 @@
     for c in range(len(starts)):
         seconds.append(forward_second(firsts[c], count, None))
     for c, first in enumerate(starts):
-        dq, parts = chunk_kernel(forward_mask, queries, out_grad, seconds[c], first // HD, inv_root)
+        inputs = seconds[c]
+        if c:
+            done_back = return_first(outs[c - 1], count, None)
+            backs.append(done_back)
+            (inputs, ready), _ = lax.optimization_barrier(((inputs, return_sums(outs[c - 1], done_back)), 0))
+        dq, parts = chunk_kernel(forward_mask, queries, out_grad, inputs, first // HD, inv_root)
+        if c:
+            got, summed = return_second(outs[c - 1], done_back, count, None, ready)
+            (dq, parts, summed), _ = lax.optimization_barrier(((dq, parts, summed), 0))
+            sums.append(summed)
         dqs.append(dq)
         outs.append(parts)
-    for c in range(len(starts)):
-        backs.append(return_first(outs[c], count, None))
-    got = None
-    for c in range(len(starts)):
-        got, summed = return_second(outs[c], backs[c], count, None)
-        sums.append(summed)
+    last = len(starts) - 1
+    backs.append(return_first(outs[last], count, None))
+    sums.append(return_second(outs[last], backs[last], count, None)[1])
     grads = [(dqs[c], sums[c][0].astype(jnp.bfloat16), sums[c][1].astype(jnp.bfloat16)) for c in range(len(starts))]
     query_grad = jnp.concatenate([grad[0] for grad in grads], axis=1)
     key_grad = jnp.concatenate([grad[1] for grad in grads], axis=1)

time: 144 us -> 151 us (1.049)
  starting transfers between devices: 42.9 us -> 51.2 us
    ppermute x24, starting transfers between devices: 42.9 us -> 51.2 us  [send(): return lax.ppermute(value, 'tm', pairs)]
    add x0 -> x1, other arithmetic: none -> 2.24 us  [return_second(): wide(own_part) + wide(to_partner[0]) + wide(got_cross) + wide(got_below)]
  transfers between devices with their start and end apart: 24 -> 24, of which waited for: 14 -> 12; matrix products, arithmetic and copies ran while one was open for 9% -> 6% of each run, Pallas kernels for 20% -> 19%
where the time goes in v14:
time: 151 us; the launch traced here: 150 us
  waiting for transfers between devices  52 us (34%)
  starting transfers between devices  51.2 us (34%)
  Pallas kernels  28 us (19%)
  other arithmetic  15.3 us (10%)
  local copies, waits for them, and re-layouts  2.46 us (2%)
    ppermute x24, waiting for transfers between devices, send(): return lax.ppermute(value, 'tm', pairs)  52 us
    ppermute x24, starting transfers between devices, send(): return lax.ppermute(value, 'tm', pairs)  51.2 us
    pallas_call x2, Pallas kernels, attention_backward(): pl.pallas_call(kernel, grid=(heads // STEP_HEADS,), in_specs=in_specs, ou...  28 us
    another operation x4, other arithmetic, forward_second(): ahead = jnp.stack([own, from_cross, from_below, from_above])  5.84 us
  transfers between devices with their start and end apart: 24, of which 12 were waited for; matrix products, arithmetic and copies ran while one was open for 6% of the time, Pallas kernels for 19%

profile of v14, /device:TPU:0, one launch (start us, length us, event | category | flops | bytes accessed | tf_op | source)
XLA Modules:
  0.0 150.1 jit_solution(4409384749491860547)
XLA Ops:
  0.6 1.4 slice_bitcast_fusion.14
  2.0 0.9 fusion.29
  2.9 3.0 %collective-permute-start = (bf16[2,128,1280]{2,1,0:T(8,128)(2,1)S(1)}, bf16[2,128,1280]{2,1,0:T(8,128)(2,1)S(1)}, u32[]{:S(2)}, u32[]{:S(2)}) collective-permute-start(bf16[2,128,1280]{2,1,0:T(8,128)(2,1)S(1)} %get-tuple-element.84.refs_0_), channel_id=1, source_target_pairs={{0,2},{1,3},{2,0},{3,1},{4,6},{5,7},{6,4},{7,5},{8,10},{9,11},{10,... | collective-permute-start | bytes 1966088 | tf_op jit(solution)/shard_map/ppermute | solution.py:16
  5.9 3.5 %collective-permute-start.1 = (bf16[2,128,1280]{2,1,0:T(8,128)(2,1)S(1)}, bf16[2,128,1280]{2,1,0:T(8,128)(2,1)S(1)}, u32[]{:S(2)}, u32[]{:S(2)}) collective-permute-start(bf16[2,128,1280]{2,1,0:T(8,128)(2,1)S(1)} %get-tuple-element.84.refs_0_), channel_id=1, source_target_pairs={{0,4},{1,5},{2,6},{3,7},{4,8},{5,9},{6,10},{7,11},{8,12},{9,13},{1... | collective-permute-start | bytes 1966088 | tf_op jit(solution)/shard_map/ppermute | solution.py:16
  9.4 1.3 collective-permute-start.2
  10.7 0.9 fusion.28
  11.7 0.5 collective-permute-start.6
  12.2 5.4 %collective-permute-start.7 = (bf16[2,128,1280]{2,1,0:T(8,128)(2,1)}, bf16[2,128,1280]{2,1,0:T(8,128)(2,1)}, u32[]{:S(2)}, u32[]{:S(2)}) collective-permute-start(bf16[2,128,1280]{2,1,0:T(8,128)(2,1)} %get-tuple-element.45.refs_0_), channel_id=1, source_target_pairs={{0,4},{1,5},{2,6},{3,7},{4,8},{5,9},{6,10},{7,11},{8,12},{9,13},{1... | collective-permute-start | bytes 1966088 | tf_op jit(solution)/shard_map/ppermute | solution.py:16
  17.6 3.9 %collective-permute-done.refs_1_ = bf16[2,128,1280]{2,1,0:T(8,128)(2,1)S(1)} collective-permute-done((bf16[2,128,1280]{2,1,0:T(8,128)(2,1)S(1)}, bf16[2,128,1280]{2,1,0:T(8,128)(2,1)S(1)}, u32[]{:S(2)}, u32[]{:S(2)}) %collective-permute-start) | collective-permute-done | bytes 655392 | tf_op jit(solution)/shard_map/ppermute | solution.py:16
  21.5 3.0 %collective-permute-done.1.refs_2_ = bf16[2,128,1280]{2,1,0:T(8,128)(2,1)S(1)} collective-permute-done((bf16[2,128,1280]{2,1,0:T(8,128)(2,1)S(1)}, bf16[2,128,1280]{2,1,0:T(8,128)(2,1)S(1)}, u32[]{:S(2)}, u32[]{:S(2)}) %collective-permute-start.1) | collective-permute-done | bytes 655392 | tf_op jit(solution)/shard_map/ppermute | solution.py:16
  24.5 2.7 %collective-permute-done.2.refs_3_ = bf16[2,128,1280]{2,1,0:T(8,128)(2,1)S(1)} collective-permute-done((bf16[2,128,1280]{2,1,0:T(8,128)(2,1)S(1)}, bf16[2,128,1280]{2,1,0:T(8,128)(2,1)S(1)}, u32[]{:S(2)}, u32[]{:S(2)}) %collective-permute-start.2) | collective-permute-done | bytes 655392 | tf_op jit(solution)/shard_map/ppermute | solution.py:16
  27.2 0.8 copy-done.2
  28.1 2.0 %pad_maximum_fusion = bf16[4,2,128,1280]{3,2,1,0:T(8,128)(2,1)S(1)} fusion(bf16[1,2,128,1280]{3,2,1,0:T(8,128)(2,1)} %bitcast.74, bf16[1,2,128,1280]{3,2,1,0:T(8,128)(2,1)} %bitcast.73, bf16[1,2,128,1280]{3,2,1,0:T(8,128)(2,1)} %bitcast.72, bf16[1,2,128,1280]{3,2,1,0:T(8,128)(2,1)} %get-tuple-element.83), kind=kLoop, calls=%fused_computation | loop fusion | flops 3932160 | bytes 5242880 | tf_op jit(solution)/shard_map/stack | solution.py:155
  30.1 0.1 collective-permute-start.3
  30.3 0.1 copy.9
  30.5 0.1 select_reduce_fusion
  30.6 0.1 multiply_reduce_fusion
  30.7 4.3 %collective-permute-start.4 = (bf16[2,128,1280]{2,1,0:T(8,128)(2,1)}, bf16[2,128,1280]{2,1,0:T(8,128)(2,1)}, u32[]{:S(2)}, u32[]{:S(2)}) collective-permute-start(bf16[2,128,1280]{2,1,0:T(8,128)(2,1)} %copy-done), channel_id=1, source_target_pairs={{0,5},{3,6},{4,9},{7,10},{8,13},{11,14},{16,21},{19,22},{20,25},{2... | collective-permute-start | bytes 1966088 | tf_op jit(solution)/shard_map/ppermute | solution.py:16
  35.0 1.5 collective-permute-start.5
  36.5 7.7 %collective-permute-done.4.refs_5_ = bf16[2,128,1280]{2,1,0:T(8,128)(2,1)} collective-permute-done((bf16[2,128,1280]{2,1,0:T(8,128)(2,1)}, bf16[2,128,1280]{2,1,0:T(8,128)(2,1)}, u32[]{:S(2)}, u32[]{:S(2)}) %collective-permute-start.4) | collective-permute-done | bytes 655392 | tf_op jit(solution)/shard_map/ppermute | solution.py:16
  44.3 1.3 collective-permute-start.8
  45.5 1.4 fusion.23.mask_ref
  47.0 0.0 collective-permute-done.5.refs_6_
  47.0 0.0 collective-permute-done.3.refs_4_
  47.0 14.0 %shard_map.85 = (bf16[128,1280]{1,0:T(8,128)(2,1)}, bf16[2,128,1280]{2,1,0:T(8,128)(2,1)}, bf16[4,2,128,1280]{3,2,1,0:T(8,128)(2,1)}, bf16[2,128,1280]{2,1,0:T(8...) custom-call(s32[128,1280]{1,0:T(8,128)} %fusion.23.mask_ref, ...), custom_call_target="tpu_custom_call" | custom-call | flops 2516582400 | bytes 14745600 | tf_op jit(solution)/shard_map/pallas_call | solution.py:127
  61.0 0.1 collective-permute-start.12
  61.0 0.0 collective-permute-done.6.refs_1_
  61.1 0.0 collective-permute-done.7.refs_2_
  61.1 2.6 %collective-permute-done.8.refs_3_ = bf16[2,128,1280]{2,1,0:T(8,128)(2,1)} collective-permute-done((bf16[2,128,1280]{2,1,0:T(8,128)(2,1)}, bf16[2,128,1280]{2,1,0:T(8,128)(2,1)}, u32[]{:S(2)}, u32[]{:S(2)}) %collective-permute-start.8) | collective-permute-done | bytes 655392 | tf_op jit(solution)/shard_map/ppermute | solution.py:16
  63.7 2.0 %pad_maximum_fusion.1 = bf16[4,2,128,1280]{3,2,1,0:T(8,128)(2,1)S(1)} fusion(bf16[1,2,128,1280]{3,2,1,0:T(8,128)(2,1)} %bitcast.14, bf16[1,2,128,1280]{3,2,1,0:T(8,128)(2,1)} %bitcast.13, bf16[1,2,128,1280]{3,2,1,0:T(8,128)(2,1)} %bitcast.12, bf16[1,2,128,1280]{3,2,1,0:T(8,128)(2,1)S(1)} %get-tuple-element.89), kind=kLoop, calls=%fused_computation.1 | loop fusion | flops 3932160 | bytes 5242880 | tf_op jit(solution)/shard_map/stack | solution.py:155
  65.6 0.1 collective-permute-start.9
  65.7 1.3 collective-permute-start.13
  67.0 0.7 collective-permute-start.14
  67.8 6.2 %collective-permute-start.10 = (bf16[2,128,1280]{2,1,0:T(8,128)(2,1)}, bf16[2,128,1280]{2,1,0:T(8,128)(2,1)S(1)}, u32[]{:S(2)}, u32[]{:S(2)}) collective-permute-start(bf16[2,128,1280]{2,1,0:T(8,128)(2,1)} %collective-permute-done.6.refs_1_), channel_id=1, source_target_pairs={{0,5},{3,6},{4,9},{7,10},{8,13},{11,14},{16,21},{19,22},{20,25},{2... | collective-permute-start | bytes 1966088 | tf_op jit(solution)/shard_map/ppermute | solution.py:16
  74.0 3.7 %collective-permute-done.13 = bf16[2,128,1280]{2,1,0:T(8,128)(2,1)S(1)} collective-permute-done((bf16[2,128,1280]{2,1,0:T(8,128)(2,1)S(1)}, bf16[2,128,1280]{2,1,0:T(8,128)(2,1)S(1)}, u32[]{:S(2)}, u32[]{:S(2)}) %collective-permute-start.13) | collective-permute-done | bytes 655392 | tf_op jit(solution)/shard_map/ppermute | solution.py:16
  77.6 0.7 collective-permute-start.11
  78.3 0.0 collective-permute-done.14
  78.3 0.0 collective-permute-done.12
  78.4 1.8 %fusion.12 = (bf16[2,128,1280]{2,1,0:T(8,128)(2,1)S(1)}, bf16[2,128,1280]{2,1,0:T(8,128)(2,1)}, bf16[2,128,1280]{2,1,0:T(8,128)(2,1)}) fusion(bf16[2,128,1280]{2,1,0:T(8,128)(2,1)S(1)} %copy-done.5, bf16[4,2,128,1280]{3,2,1,0:T(8,128)(2,1)S(1)} %collective-permute-done.12, bf16[2,128,1280]{2,1,0:T(8,128)(2,1)S(1)} %copy-done.4, ...), kind=kLoop, calls=%fused_computation.20 | loop fusion | flops 5242880 | bytes 7208960 | tf_op jit(solution)/shard_map/convert_element_type | solution.py:193
  80.1 5.2 %collective-permute-done.10.refs_5_ = bf16[2,128,1280]{2,1,0:T(8,128)(2,1)S(1)} collective-permute-done((bf16[2,128,1280]{2,1,0:T(8,128)(2,1)}, bf16[2,128,1280]{2,1,0:T(8,128)(2,1)S(1)}, u32[]{:S(2)}, u32[]{:S(2)}) %collective-permute-start.10) | collective-permute-done | bytes 655392 | tf_op jit(solution)/shard_map/ppermute | solution.py:16
  85.3 0.0 collective-permute-done.11.refs_6_
  85.4 4.1 %collective-permute-start.15 = (bf16[2,128,1280]{2,1,0:T(8,128)(2,1)}, bf16[2,128,1280]{2,1,0:T(8,128)(2,1)}, u32[]{:S(2)}, u32[]{:S(2)}) collective-permute-start(bf16[2,128,1280]{2,1,0:T(8,128)(2,1)} %get-tuple-element.61), channel_id=1, source_target_pairs={{0,2},{1,3},{2,0},{3,1},{4,6},{5,7},{6,4},{7,5},{8,10},{9,11},{10,... | collective-permute-start | bytes 1966088 | tf_op jit(solution)/shard_map/ppermute | solution.py:16
  89.5 1.3 collective-permute-start.16
  90.8 5.4 %collective-permute-start.17 = (bf16[2,128,1280]{2,1,0:T(8,128)(2,1)S(1)}, bf16[2,128,1280]{2,1,0:T(8,128)(2,1)}, u32[]{:S(2)}, u32[]{:S(2)}) collective-permute-start(bf16[2,128,1280]{2,1,0:T(8,128)(2,1)S(1)} %get-tuple-element.63), channel_id=1, source_target_pairs={{0,4},{1,5},{2,6},{3,7},{4,8},{5,9},{6,10},{7,11},{8,12},{9,13},{1... | collective-permute-start | bytes 1966088 | tf_op jit(solution)/shard_map/ppermute | solution.py:16
  96.2 14.0 %shard_map.86 = (bf16[128,1280]{1,0:T(8,128)(2,1)}, bf16[2,128,1280]{2,1,0:T(8,128)(2,1)}, bf16[4,2,128,1280]{3,2,1,0:T(8,128)(2,1)}, bf16[2,128,1280]{2,1,0:T(8...) custom-call(s32[128,1280]{1,0:T(8,128)} %fusion.23.mask_ref, ...), custom_call_target="tpu_custom_call" | custom-call | flops 2516582400 | bytes 14745600 | tf_op jit(solution)/shard_map/pallas_call | solution.py:127
  110.2 0.1 collective-permute-done.17
  110.4 2.2 %fusion.11 = bf16[2,128,1280]{2,1,0:T(8,128)(2,1)S(1)} fusion(bf16[2,128,1280]{2,1,0:T(8,128)(2,1)} %collective-permute-done.17, bf16[2,128,1280]{2,1,0:T(8,128)(2,1)} %collective-permute-done.16, bf16[2,128,1280]{2,1,0:T(8,128)(2,1)} %collective-permute-done.15, bf16[2,128,1280]{2,1,0:T(8,128)(2,1)} %get-tuple-element.60, ...), kind=kLoop, calls=%fused_computation.18 | loop fusion | flops 3276800 | bytes 3932160 | tf_op jit(solution)/shard_map/add | solution.py:208
  112.6 0.7 collective-permute-start.18
  113.4 1.3 collective-permute-start.19
  114.7 0.7 collective-permute-start.20
  115.4 9.9 %collective-permute-done.19 = bf16[2,128,1280]{2,1,0:T(8,128)(2,1)S(1)} collective-permute-done((bf16[2,128,1280]{2,1,0:T(8,128)(2,1)S(1)}, bf16[2,128,1280]{2,1,0:T(8,128)(2,1)S(1)}, u32[]{:S(2)}, u32[]{:S(2)}) %collective-permute-start.19) | collective-permute-done | bytes 655392 | tf_op jit(solution)/shard_map/ppermute | solution.py:16
  125.3 0.0 collective-permute-done.20
  125.3 0.0 collective-permute-done.18
  125.3 0.7 fusion.4
  126.0 1.9 %collective-permute-start.21 = (bf16[2,128,1280]{2,1,0:T(8,128)(2,1)S(1)}, bf16[2,128,1280]{2,1,0:T(8,128)(2,1)S(1)}, u32[]{:S(2)}, u32[]{:S(2)}) collective-permute-start(bf16[2,128,1280]{2,1,0:T(8,128)(2,1)S(1)} %get-tuple-element.73), channel_id=1, source_target_pairs={{0,2},{1,3},{2,0},{3,1},{4,6},{5,7},{6,4},{7,5},{8,10},{9,11},{10,... | collective-permute-start | bytes 1966088 | tf_op jit(solution)/shard_map/ppermute | solution.py:16
  127.9 1.3 collective-permute-start.22
  129.2 4.6 %collective-permute-start.23 = (bf16[2,128,1280]{2,1,0:T(8,128)(2,1)S(1)}, bf16[2,128,1280]{2,1,0:T(8,128)(2,1)S(1)}, u32[]{:S(2)}, u32[]{:S(2)}) collective-permute-start(bf16[2,128,1280]{2,1,0:T(8,128)(2,1)S(1)} %get-tuple-element.74), channel_id=1, source_target_pairs={{0,4},{1,5},{2,6},{3,7},{4,8},{5,9},{6,10},{7,11},{8,12},{9,13},{1... | collective-permute-start | bytes 1966088 | tf_op jit(solution)/shard_map/ppermute | solution.py:16
  133.8 0.9 pad_maximum_fusion.4
  134.7 8.9 %collective-permute-done.21 = bf16[2,128,1280]{2,1,0:T(8,128)(2,1)S(1)} collective-permute-done((bf16[2,128,1280]{2,1,0:T(8,128)(2,1)S(1)}, bf16[2,128,1280]{2,1,0:T(8,128)(2,1)S(1)}, u32[]{:S(2)}, u32[]{:S(2)}) %collective-permute-start.21) | collective-permute-done | bytes 655392 | tf_op jit(solution)/shard_map/ppermute | solution.py:16
  143.7 3.1 %collective-permute-done.22 = bf16[2,128,1280]{2,1,0:T(8,128)(2,1)S(1)} collective-permute-done((bf16[2,128,1280]{2,1,0:T(8,128)(2,1)S(1)}, bf16[2,128,1280]{2,1,0:T(8,128)(2,1)S(1)}, u32[]{:S(2)}, u32[]{:S(2)}) %collective-permute-start.22) | collective-permute-done | bytes 655392 | tf_op jit(solution)/shard_map/ppermute | solution.py:16
  146.7 1.2 collective-permute-done.23
  147.9 0.4 fusion.8
  148.4 0.9 pad_maximum_fusion.6
  149.3 0.9 pad_maximum_fusion.5
  (65 shorter events, 0.3 us)
Async XLA Ops:
  2.9 24.3 %copy-start.9 = (bf16[2,128,1280]{2,1,0:T(8,128)(2,1)}, bf16[2,128,1280]{2,1,0:T(8,128)(2,1)S(1)}, u32[]{:S(2)}) copy-start(bf16[2,128,1280]{2,1,0:T(8,128)(2,1)S(1)} %get-tuple-element.84.refs_0_) | copy-start | bytes 1966084
  2.9 18.6 %collective-permute-start = (bf16[2,128,1280]{2,1,0:T(8,128)(2,1)S(1)}, bf16[2,128,1280]{2,1,0:T(8,128)(2,1)S(1)}, u32[]{:S(2)}, u32[]{:S(2)}) collective-permute-start(bf16[2,128,1280]{2,1,0:T(8,128)(2,1)S(1)} %get-tuple-element.84.refs_0_), channel_id=1, source_target_pairs={{0,2},{1,3},{2,0},{3,1},{4,6},{5,7},{6,4},{7,5},{8,10},{9,11},{10,... | collective-permute-start | bytes 1966088 | tf_op jit(solution)/shard_map/ppermute | solution.py:16
  5.9 18.6 %collective-permute-start.1 = (bf16[2,128,1280]{2,1,0:T(8,128)(2,1)S(1)}, bf16[2,128,1280]{2,1,0:T(8,128)(2,1)S(1)}, u32[]{:S(2)}, u32[]{:S(2)}) collective-permute-start(bf16[2,128,1280]{2,1,0:T(8,128)(2,1)S(1)} %get-tuple-element.84.refs_0_), channel_id=1, source_target_pairs={{0,4},{1,5},{2,6},{3,7},{4,8},{5,9},{6,10},{7,11},{8,12},{9,13},{1... | collective-permute-start | bytes 1966088 | tf_op jit(solution)/shard_map/ppermute | solution.py:16
  9.4 17.8 %collective-permute-start.2 = (bf16[2,128,1280]{2,1,0:T(8,128)(2,1)S(1)}, bf16[2,128,1280]{2,1,0:T(8,128)(2,1)S(1)}, u32[]{:S(2)}, u32[]{:S(2)}) collective-permute-start(bf16[2,128,1280]{2,1,0:T(8,128)(2,1)S(1)} %get-tuple-element.84.refs_0_), channel_id=1, source_target_pairs={{4,0},{5,1},{6,2},{7,3},{8,4},{9,5},{10,6},{11,7},{12,8},{13,9},{1... | collective-permute-start | bytes 1966088 | tf_op jit(solution)/shard_map/ppermute | solution.py:16
  11.7 49.4 %collective-permute-start.6 = (bf16[2,128,1280]{2,1,0:T(8,128)(2,1)}, bf16[2,128,1280]{2,1,0:T(8,128)(2,1)}, u32[]{:S(2)}, u32[]{:S(2)}) collective-permute-start(bf16[2,128,1280]{2,1,0:T(8,128)(2,1)} %get-tuple-element.45.refs_0_), channel_id=1, source_target_pairs={{0,2},{1,3},{2,0},{3,1},{4,6},{5,7},{6,4},{7,5},{8,10},{9,11},{10,... | collective-permute-start | bytes 1966088 | tf_op jit(solution)/shard_map/ppermute | solution.py:16
  12.2 48.9 %collective-permute-start.7 = (bf16[2,128,1280]{2,1,0:T(8,128)(2,1)}, bf16[2,128,1280]{2,1,0:T(8,128)(2,1)}, u32[]{:S(2)}, u32[]{:S(2)}) collective-permute-start(bf16[2,128,1280]{2,1,0:T(8,128)(2,1)} %get-tuple-element.45.refs_0_), channel_id=1, source_target_pairs={{0,4},{1,5},{2,6},{3,7},{4,8},{5,9},{6,10},{7,11},{8,12},{9,13},{1... | collective-permute-start | bytes 1966088 | tf_op jit(solution)/shard_map/ppermute | solution.py:16
  21.5 5.8 %copy-start = (bf16[2,128,1280]{2,1,0:T(8,128)(2,1)}, bf16[2,128,1280]{2,1,0:T(8,128)(2,1)S(1)}, u32[]{:S(2)}) copy-start(bf16[2,128,1280]{2,1,0:T(8,128)(2,1)S(1)} %collective-permute-done.refs_1_) | copy-start | bytes 1966084
  24.5 2.8 %copy-start.1 = (bf16[2,128,1280]{2,1,0:T(8,128)(2,1)}, bf16[2,128,1280]{2,1,0:T(8,128)(2,1)S(1)}, u32[]{:S(2)}) copy-start(bf16[2,128,1280]{2,1,0:T(8,128)(2,1)S(1)} %collective-permute-done.1.refs_2_) | copy-start | bytes 1966084
  27.2 0.8 copy-start.2
  28.1 2.2 %copy-start.13 = (s32[4,3]{1,0:T(4,128)S(1)}, s32[4,3]{1,0:T(4,128)}, u32[]{:S(2)}) copy-start(s32[4,3]{1,0:T(4,128)} %param.10) | copy-start | bytes 148
  28.1 2.4 %copy-start.21 = (s32[4]{0:T(128)S(1)}, s32[4]{0:T(128)}, u32[]{:S(2)}) copy-start(s32[4]{0:T(128)} %param.11) | copy-start | bytes 52
  30.1 16.8 %collective-permute-start.3 = (bf16[4,2,128,1280]{3,2,1,0:T(8,128)(2,1)S(1)}, bf16[4,2,128,1280]{3,2,1,0:T(8,128)(2,1)}, u32[]{:S(2)}, u32[]{:S(2)}) collective-permute-start(bf16[4,2,128,1280]{3,2,1,0:T(8,128)(2,1)S(1)} %pad_maximum_fusion), channel_id=1, source_target_pairs={{0,1},{1,0},{2,3},{3,2},{4,5},{5,4},{6,7},{7,6},{8,9},{9,8},{10,11... | collective-permute-start | bytes 7864328 | tf_op jit(solution)/shard_map/ppermute | solution.py:16
  30.7 13.6 %collective-permute-start.4 = (bf16[2,128,1280]{2,1,0:T(8,128)(2,1)}, bf16[2,128,1280]{2,1,0:T(8,128)(2,1)}, u32[]{:S(2)}, u32[]{:S(2)}) collective-permute-start(bf16[2,128,1280]{2,1,0:T(8,128)(2,1)} %copy-done), channel_id=1, source_target_pairs={{0,5},{3,6},{4,9},{7,10},{8,13},{11,14},{16,21},{19,22},{20,25},{2... | collective-permute-start | bytes 1966088 | tf_op jit(solution)/shard_map/ppermute | solution.py:16
  35.0 11.9 %collective-permute-start.5 = (bf16[2,128,1280]{2,1,0:T(8,128)(2,1)}, bf16[2,128,1280]{2,1,0:T(8,128)(2,1)}, u32[]{:S(2)}, u32[]{:S(2)}) collective-permute-start(bf16[2,128,1280]{2,1,0:T(8,128)(2,1)} %copy-done), channel_id=1, source_target_pairs={{4,1},{7,2},{8,5},{11,6},{12,9},{15,10},{20,17},{23,18},{24,21},{2... | collective-permute-start | bytes 1966088 | tf_op jit(solution)/shard_map/ppermute | solution.py:16
  44.3 19.4 %collective-permute-start.8 = (bf16[2,128,1280]{2,1,0:T(8,128)(2,1)}, bf16[2,128,1280]{2,1,0:T(8,128)(2,1)}, u32[]{:S(2)}, u32[]{:S(2)}) collective-permute-start(bf16[2,128,1280]{2,1,0:T(8,128)(2,1)} %get-tuple-element.45.refs_0_), channel_id=1, source_target_pairs={{4,0},{5,1},{6,2},{7,3},{8,4},{9,5},{10,6},{11,7},{12,8},{13,9},{1... | collective-permute-start | bytes 1966088 | tf_op jit(solution)/shard_map/ppermute | solution.py:16
  61.0 17.4 %collective-permute-start.12 = (bf16[4,2,128,1280]{3,2,1,0:T(8,128)(2,1)}, bf16[4,2,128,1280]{3,2,1,0:T(8,128)(2,1)S(1)}, u32[]{:S(2)}, u32[]{:S(2)}) collective-permute-start(bf16[4,2,128,1280]{3,2,1,0:T(8,128)(2,1)} %get-tuple-element.40), channel_id=1, source_target_pairs={{0,1},{1,0},{2,3},{3,2},{4,5},{5,4},{6,7},{7,6},{8,9},{9,8},{10,11... | collective-permute-start | bytes 7864328 | tf_op jit(solution)/shard_map/ppermute | solution.py:16
  63.7 2.1 %copy-start.19 = (bf16[2,128,1280]{2,1,0:T(8,128)(2,1)S(1)}, bf16[2,128,1280]{2,1,0:T(8,128)(2,1)}, u32[]{:S(2)}) copy-start(bf16[2,128,1280]{2,1,0:T(8,128)(2,1)} %get-tuple-element.41) | copy-start | bytes 1966084
  63.7 3.4 %copy-start.17 = (bf16[2,128,1280]{2,1,0:T(8,128)(2,1)S(1)}, bf16[2,128,1280]{2,1,0:T(8,128)(2,1)}, u32[]{:S(2)}) copy-start(bf16[2,128,1280]{2,1,0:T(8,128)(2,1)} %get-tuple-element.42) | copy-start | bytes 1966084
  63.7 14.7 %copy-start.3 = (bf16[2,128,1280]{2,1,0:T(8,128)(2,1)S(1)}, bf16[2,128,1280]{2,1,0:T(8,128)(2,1)}, u32[]{:S(2)}) copy-start(bf16[2,128,1280]{2,1,0:T(8,128)(2,1)} %get-tuple-element.39) | copy-start | bytes 1966084
  63.7 14.7 %copy-start.4 = (bf16[2,128,1280]{2,1,0:T(8,128)(2,1)S(1)}, bf16[2,128,1280]{2,1,0:T(8,128)(2,1)}, u32[]{:S(2)}) copy-start(bf16[2,128,1280]{2,1,0:T(8,128)(2,1)} %get-tuple-element.43) | copy-start | bytes 1966084
  63.7 14.7 %copy-start.5 = (bf16[2,128,1280]{2,1,0:T(8,128)(2,1)S(1)}, bf16[2,128,1280]{2,1,0:T(8,128)(2,1)}, u32[]{:S(2)}) copy-start(bf16[2,128,1280]{2,1,0:T(8,128)(2,1)} %get-tuple-element.44) | copy-start | bytes 1966084
  65.6 19.7 %collective-permute-start.9 = (bf16[4,2,128,1280]{3,2,1,0:T(8,128)(2,1)S(1)}, bf16[4,2,128,1280]{3,2,1,0:T(8,128)(2,1)S(1)}, u32[]{:S(2)}, u32[]{:S(2)}) collective-permute-start(bf16[4,2,128,1280]{3,2,1,0:T(8,128)(2,1)S(1)} %pad_maximum_fusion.1), channel_id=1, source_target_pairs={{0,1},{1,0},{2,3},{3,2},{4,5},{5,4},{6,7},{7,6},{8,9},{9,8},{10,11... | collective-permute-start | bytes 7864328 | tf_op jit(solution)/shard_map/ppermute | solution.py:16
  65.7 11.9 %collective-permute-start.13 = (bf16[2,128,1280]{2,1,0:T(8,128)(2,1)S(1)}, bf16[2,128,1280]{2,1,0:T(8,128)(2,1)S(1)}, u32[]{:S(2)}, u32[]{:S(2)}) collective-permute-start(bf16[2,128,1280]{2,1,0:T(8,128)(2,1)S(1)} %copy-done.19), channel_id=1, source_target_pairs={{5,0},{6,3},{9,4},{10,7},{13,8},{14,11},{21,16},{22,19},{25,20},{2... | collective-permute-start | bytes 1966088 | tf_op jit(solution)/shard_map/ppermute | solution.py:16
  67.0 11.3 %collective-permute-start.14 = (bf16[2,128,1280]{2,1,0:T(8,128)(2,1)S(1)}, bf16[2,128,1280]{2,1,0:T(8,128)(2,1)S(1)}, u32[]{:S(2)}, u32[]{:S(2)}) collective-permute-start(bf16[2,128,1280]{2,1,0:T(8,128)(2,1)S(1)} %copy-done.17), channel_id=1, source_target_pairs={{1,4},{2,7},{5,8},{6,11},{9,12},{10,15},{17,20},{18,23},{21,24},{2... | collective-permute-start | bytes 1966088 | tf_op jit(solution)/shard_map/ppermute | solution.py:16
  67.8 17.6 %collective-permute-start.10 = (bf16[2,128,1280]{2,1,0:T(8,128)(2,1)}, bf16[2,128,1280]{2,1,0:T(8,128)(2,1)S(1)}, u32[]{:S(2)}, u32[]{:S(2)}) collective-permute-start(bf16[2,128,1280]{2,1,0:T(8,128)(2,1)} %collective-permute-done.6.refs_1_), channel_id=1, source_target_pairs={{0,5},{3,6},{4,9},{7,10},{8,13},{11,14},{16,21},{19,22},{20,25},{2... | collective-permute-start | bytes 1966088 | tf_op jit(solution)/shard_map/ppermute | solution.py:16
  77.6 7.7 %collective-permute-start.11 = (bf16[2,128,1280]{2,1,0:T(8,128)(2,1)}, bf16[2,128,1280]{2,1,0:T(8,128)(2,1)S(1)}, u32[]{:S(2)}, u32[]{:S(2)}) collective-permute-start(bf16[2,128,1280]{2,1,0:T(8,128)(2,1)} %collective-permute-done.6.refs_1_), channel_id=1, source_target_pairs={{4,1},{7,2},{8,5},{11,6},{12,9},{15,10},{20,17},{23,18},{24,21},{2... | collective-permute-start | bytes 1966088 | tf_op jit(solution)/shard_map/ppermute | solution.py:16
  85.3 5.4 %copy-start.15 = (bf16[2,128,1280]{2,1,0:T(8,128)(2,1)}, bf16[2,128,1280]{2,1,0:T(8,128)(2,1)S(1)}, u32[]{:S(2)}) copy-start(bf16[2,128,1280]{2,1,0:T(8,128)(2,1)S(1)} %collective-permute-done.10.refs_5_) | copy-start | bytes 1966084
  85.3 5.4 %copy-start.16 = (bf16[2,128,1280]{2,1,0:T(8,128)(2,1)}, bf16[2,128,1280]{2,1,0:T(8,128)(2,1)S(1)}, u32[]{:S(2)}) copy-start(bf16[2,128,1280]{2,1,0:T(8,128)(2,1)S(1)} %collective-permute-done.11.refs_6_) | copy-start | bytes 1966084
  85.3 4.1 %copy-start.14 = (bf16[4,2,128,1280]{3,2,1,0:T(8,128)(2,1)}, bf16[4,2,128,1280]{3,2,1,0:T(8,128)(2,1)S(1)}, u32[]{:S(2)}) copy-start(bf16[4,2,128,1280]{3,2,1,0:T(8,128)(2,1)S(1)} %collective-permute-done.9.refs_4_) | copy-start | bytes 7864324
  85.4 24.8 %collective-permute-start.15 = (bf16[2,128,1280]{2,1,0:T(8,128)(2,1)}, bf16[2,128,1280]{2,1,0:T(8,128)(2,1)}, u32[]{:S(2)}, u32[]{:S(2)}) collective-permute-start(bf16[2,128,1280]{2,1,0:T(8,128)(2,1)} %get-tuple-element.61), channel_id=1, source_target_pairs={{0,2},{1,3},{2,0},{3,1},{4,6},{5,7},{6,4},{7,5},{8,10},{9,11},{10,... | collective-permute-start | bytes 1966088 | tf_op jit(solution)/shard_map/ppermute | solution.py:16
  89.5 20.7 %collective-permute-start.16 = (bf16[2,128,1280]{2,1,0:T(8,128)(2,1)}, bf16[2,128,1280]{2,1,0:T(8,128)(2,1)}, u32[]{:S(2)}, u32[]{:S(2)}) collective-permute-start(bf16[2,128,1280]{2,1,0:T(8,128)(2,1)} %get-tuple-element.62), channel_id=1, source_target_pairs={{4,0},{5,1},{6,2},{7,3},{8,4},{9,5},{10,6},{11,7},{12,8},{13,9},{1... | collective-permute-start | bytes 1966088 | tf_op jit(solution)/shard_map/ppermute | solution.py:16
  90.8 19.6 %collective-permute-start.17 = (bf16[2,128,1280]{2,1,0:T(8,128)(2,1)S(1)}, bf16[2,128,1280]{2,1,0:T(8,128)(2,1)}, u32[]{:S(2)}, u32[]{:S(2)}) collective-permute-start(bf16[2,128,1280]{2,1,0:T(8,128)(2,1)S(1)} %get-tuple-element.63), channel_id=1, source_target_pairs={{0,4},{1,5},{2,6},{3,7},{4,8},{5,9},{6,10},{7,11},{8,12},{9,13},{1... | collective-permute-start | bytes 1966088 | tf_op jit(solution)/shard_map/ppermute | solution.py:16
  110.4 3.0 %copy-start.20 = (bf16[2,128,1280]{2,1,0:T(8,128)(2,1)S(1)}, bf16[2,128,1280]{2,1,0:T(8,128)(2,1)}, u32[]{:S(2)}) copy-start(bf16[2,128,1280]{2,1,0:T(8,128)(2,1)} %get-tuple-element.69) | copy-start | bytes 1966084
  110.4 4.3 %copy-start.18 = (bf16[2,128,1280]{2,1,0:T(8,128)(2,1)S(1)}, bf16[2,128,1280]{2,1,0:T(8,128)(2,1)}, u32[]{:S(2)}) copy-start(bf16[2,128,1280]{2,1,0:T(8,128)(2,1)} %get-tuple-element.70) | copy-start | bytes 1966084
  110.4 14.9 %copy-start.6 = (bf16[2,128,1280]{2,1,0:T(8,128)(2,1)S(1)}, bf16[2,128,1280]{2,1,0:T(8,128)(2,1)}, u32[]{:S(2)}) copy-start(bf16[2,128,1280]{2,1,0:T(8,128)(2,1)} %get-tuple-element.68) | copy-start | bytes 1966084
  110.4 14.9 %copy-start.7 = (bf16[2,128,1280]{2,1,0:T(8,128)(2,1)S(1)}, bf16[2,128,1280]{2,1,0:T(8,128)(2,1)}, u32[]{:S(2)}) copy-start(bf16[2,128,1280]{2,1,0:T(8,128)(2,1)} %get-tuple-element.71) | copy-start | bytes 1966084
  110.4 14.9 %copy-start.8 = (bf16[2,128,1280]{2,1,0:T(8,128)(2,1)S(1)}, bf16[2,128,1280]{2,1,0:T(8,128)(2,1)}, u32[]{:S(2)}) copy-start(bf16[2,128,1280]{2,1,0:T(8,128)(2,1)} %get-tuple-element.72) | copy-start | bytes 1966084
  112.6 21.2 %copy-start.11 = (bf16[128,1280]{1,0:T(8,128)(2,1)S(1)}, bf16[128,1280]{1,0:T(8,128)(2,1)}, u32[]{:S(2)}) copy-start(bf16[128,1280]{1,0:T(8,128)(2,1)} %get-tuple-element.38) | copy-start | bytes 983044
  112.6 21.2 %copy-start.12 = (bf16[128,1280]{1,0:T(8,128)(2,1)S(1)}, bf16[128,1280]{1,0:T(8,128)(2,1)}, u32[]{:S(2)}) copy-start(bf16[128,1280]{1,0:T(8,128)(2,1)} %get-tuple-element.64) | copy-start | bytes 983044
  112.6 12.6 %collective-permute-start.18 = (bf16[4,2,128,1280]{3,2,1,0:T(8,128)(2,1)}, bf16[4,2,128,1280]{3,2,1,0:T(8,128)(2,1)S(1)}, u32[]{:S(2)}, u32[]{:S(2)}) collective-permute-start(bf16[4,2,128,1280]{3,2,1,0:T(8,128)(2,1)} %get-tuple-element.67), channel_id=1, source_target_pairs={{0,1},{1,0},{2,3},{3,2},{4,5},{5,4},{6,7},{7,6},{8,9},{9,8},{10,11... | collective-permute-start | bytes 7864328 | tf_op jit(solution)/shard_map/ppermute | solution.py:16
  113.4 11.9 %collective-permute-start.19 = (bf16[2,128,1280]{2,1,0:T(8,128)(2,1)S(1)}, bf16[2,128,1280]{2,1,0:T(8,128)(2,1)S(1)}, u32[]{:S(2)}, u32[]{:S(2)}) collective-permute-start(bf16[2,128,1280]{2,1,0:T(8,128)(2,1)S(1)} %copy-done.20), channel_id=1, source_target_pairs={{5,0},{6,3},{9,4},{10,7},{13,8},{14,11},{21,16},{22,19},{25,20},{2... | collective-permute-start | bytes 1966088 | tf_op jit(solution)/shard_map/ppermute | solution.py:16
  114.7 10.6 %collective-permute-start.20 = (bf16[2,128,1280]{2,1,0:T(8,128)(2,1)S(1)}, bf16[2,128,1280]{2,1,0:T(8,128)(2,1)S(1)}, u32[]{:S(2)}, u32[]{:S(2)}) collective-permute-start(bf16[2,128,1280]{2,1,0:T(8,128)(2,1)S(1)} %copy-done.18), channel_id=1, source_target_pairs={{1,4},{2,7},{5,8},{6,11},{9,12},{10,15},{17,20},{18,23},{21,24},{2... | collective-permute-start | bytes 1966088 | tf_op jit(solution)/shard_map/ppermute | solution.py:16
  126.0 17.7 %collective-permute-start.21 = (bf16[2,128,1280]{2,1,0:T(8,128)(2,1)S(1)}, bf16[2,128,1280]{2,1,0:T(8,128)(2,1)S(1)}, u32[]{:S(2)}, u32[]{:S(2)}) collective-permute-start(bf16[2,128,1280]{2,1,0:T(8,128)(2,1)S(1)} %get-tuple-element.73), channel_id=1, source_target_pairs={{0,2},{1,3},{2,0},{3,1},{4,6},{5,7},{6,4},{7,5},{8,10},{9,11},{10,... | collective-permute-start | bytes 1966088 | tf_op jit(solution)/shard_map/ppermute | solution.py:16
  127.9 18.8 %collective-permute-start.22 = (bf16[2,128,1280]{2,1,0:T(8,128)(2,1)S(1)}, bf16[2,128,1280]{2,1,0:T(8,128)(2,1)S(1)}, u32[]{:S(2)}, u32[]{:S(2)}) collective-permute-start(bf16[2,128,1280]{2,1,0:T(8,128)(2,1)S(1)} %get-tuple-element.75), channel_id=1, source_target_pairs={{4,0},{5,1},{6,2},{7,3},{8,4},{9,5},{10,6},{11,7},{12,8},{13,9},{1... | collective-permute-start | bytes 1966088 | tf_op jit(solution)/shard_map/ppermute | solution.py:16
  129.2 18.7 %collective-permute-start.23 = (bf16[2,128,1280]{2,1,0:T(8,128)(2,1)S(1)}, bf16[2,128,1280]{2,1,0:T(8,128)(2,1)S(1)}, u32[]{:S(2)}, u32[]{:S(2)}) collective-permute-start(bf16[2,128,1280]{2,1,0:T(8,128)(2,1)S(1)} %get-tuple-element.74), channel_id=1, source_target_pairs={{0,4},{1,5},{2,6},{3,7},{4,8},{5,9},{6,10},{7,11},{8,12},{9,13},{1... | collective-permute-start | bytes 1966088 | tf_op jit(solution)/shard_map/ppermute | solution.py:16
  133.8 14.1 %copy-start.10 = (bf16[2,128,1280]{2,1,0:T(8,128)(2,1)S(1)}, bf16[2,128,1280]{2,1,0:T(8,128)(2,1)}, u32[]{:S(2)}) copy-start(bf16[2,128,1280]{2,1,0:T(8,128)(2,1)} %get-tuple-element.66) | copy-start | bytes 1966084

commit v15 on v12

--- a/solution.py
+++ b/solution.py
@@ -8,7 +8,6 @@
 
 HD = 128
 QUARTERS = 4
-CHUNKS = 2
 STEP_HEADS = 2
 
 
@@ -230,11 +229,15 @@
     own_rows = device * rows_own + base_rows
     forward_mask = allowed(own_rows, far_rows, frame_keep, band_window, frame_len).astype(jnp.int32)
     heads = channel_total // HD
-    chunk_heads = heads // CHUNKS if heads % CHUNKS == 0 else heads
-    width = chunk_heads * HD
-    starts = list(range(0, channel_total, width))
+    lead_heads = (heads * 3 // 10) // STEP_HEADS * STEP_HEADS
+    if lead_heads < STEP_HEADS or heads % STEP_HEADS:
+        lead_heads = heads
+    bounds = [0, lead_heads * HD, channel_total] if lead_heads < heads else [0, channel_total]
+    starts = bounds[:-1]
+    widths = [b - a for a, b in zip(bounds[:-1], bounds[1:])]
     firsts, seconds, outs, backs, sums, dqs = [], [], [], [], [], []
     for c, first in enumerate(starts):
+        width = widths[c]
         own = jnp.stack([keys[:, first : first + width], values[:, first : first + width]])
         firsts.append(forward_relay(own, count, None))
     for c in range(len(starts)):

time: 144 us -> 171 us (1.19)
  waiting for transfers between devices: 51.9 us -> 78.7 us
  local copies, waits for them, and re-layouts: 3.31 us -> 5.58 us
  other arithmetic: 15.5 us -> 13.4 us
    ppermute x24, waiting for transfers between devices: 51.9 us -> 78.7 us  [send(): return lax.ppermute(value, 'tm', pairs)]
    another operation x4, other arithmetic: 5.2 us -> 2.48 us  [forward_second(): ahead = jnp.stack([own, from_cross, from_below, from_above])]
  transfers between devices with their start and end apart: 24 -> 24, of which waited for: 14 -> 9; matrix products, arithmetic and copies ran while one was open for 9% -> 5% of each run, Pallas kernels for 20% -> 16%
where the time goes in v15:
time: 171 us
  waiting for transfers between devices  78.7 us (46%)
  starting transfers between devices  44 us (26%)
  Pallas kernels  28 us (16%)
  other arithmetic  13.4 us (8%)
  local copies, waits for them, and re-layouts  5.58 us (3%)
    ppermute x24, waiting for transfers between devices, send(): return lax.ppermute(value, 'tm', pairs)  78.7 us
    ppermute x24, starting transfers between devices, send(): return lax.ppermute(value, 'tm', pairs)  44 us
    pallas_call x2, Pallas kernels, attention_backward(): pl.pallas_call(kernel, grid=(heads // STEP_HEADS,), in_specs=in_specs, ou...  28 us
    convert_element_type x2, other arithmetic, return_second(): cross_sum.astype(jnp.bfloat16)  4.57 us
  transfers between devices with their start and end apart: 24, of which 9 were waited for; matrix products, arithmetic and copies ran while one was open for 5% of the time, Pallas kernels for 16%

profile of v15, /device:TPU:0, one launch (start us, length us, event | category | flops | bytes accessed | tf_op | source)
XLA Modules:
  0.0 170.8 jit_solution(3963146038106050934)
XLA Ops:
  0.6 1.2 slice_bitcast_fusion.6
  1.9 0.1 fusion.30
  2.0 3.1 %collective-permute-start.6 = (bf16[2,128,1792]{2,1,0:T(8,128)(2,1)S(1)}, bf16[2,128,1792]{2,1,0:T(8,128)(2,1)S(1)}, u32[]{:S(2)}, u32[]{:S(2)}) collective-permute-start(bf16[2,128,1792]{2,1,0:T(8,128)(2,1)S(1)} %get-tuple-element.44.refs_0_), channel_id=1, source_target_pairs={{0,2},{1,3},{2,0},{3,1},{4,6},{5,7},{6,4},{7,5},{8,10},{9,11},{10,... | collective-permute-start | bytes 2752520 | tf_op jit(solution)/shard_map/ppermute | solution.py:15
  5.1 3.5 %collective-permute-start.7 = (bf16[2,128,1792]{2,1,0:T(8,128)(2,1)S(1)}, bf16[2,128,1792]{2,1,0:T(8,128)(2,1)S(1)}, u32[]{:S(2)}, u32[]{:S(2)}) collective-permute-start(bf16[2,128,1792]{2,1,0:T(8,128)(2,1)S(1)} %get-tuple-element.44.refs_0_), channel_id=1, source_target_pairs={{0,4},{1,5},{2,6},{3,7},{4,8},{5,9},{6,10},{7,11},{8,12},{9,13},{1... | collective-permute-start | bytes 2752520 | tf_op jit(solution)/shard_map/ppermute | solution.py:15
  8.6 1.3 collective-permute-start.8
  9.9 15.5 %collective-permute-done.6.refs_1_ = bf16[2,128,1792]{2,1,0:T(8,128)(2,1)S(1)} collective-permute-done((bf16[2,128,1792]{2,1,0:T(8,128)(2,1)S(1)}, bf16[2,128,1792]{2,1,0:T(8,128)(2,1)S(1)}, u32[]{:S(2)}, u32[]{:S(2)}) %collective-permute-start.6) | collective-permute-done | bytes 917536 | tf_op jit(solution)/shard_map/ppermute | solution.py:15
  25.4 2.4 %collective-permute-done.7.refs_2_ = bf16[2,128,1792]{2,1,0:T(8,128)(2,1)S(1)} collective-permute-done((bf16[2,128,1792]{2,1,0:T(8,128)(2,1)S(1)}, bf16[2,128,1792]{2,1,0:T(8,128)(2,1)S(1)}, u32[]{:S(2)}, u32[]{:S(2)}) %collective-permute-start.7) | collective-permute-done | bytes 917536 | tf_op jit(solution)/shard_map/ppermute | solution.py:15
  27.8 4.2 %collective-permute-done.8.refs_3_ = bf16[2,128,1792]{2,1,0:T(8,128)(2,1)S(1)} collective-permute-done((bf16[2,128,1792]{2,1,0:T(8,128)(2,1)S(1)}, bf16[2,128,1792]{2,1,0:T(8,128)(2,1)S(1)}, u32[]{:S(2)}, u32[]{:S(2)}) %collective-permute-start.8) | collective-permute-done | bytes 917536 | tf_op jit(solution)/shard_map/ppermute | solution.py:15
  32.0 2.1 %pad_maximum_fusion = bf16[4,2,128,1792]{3,2,1,0:T(8,128)(2,1)} fusion(bf16[1,2,128,1792]{3,2,1,0:T(8,128)(2,1)S(1)} %bitcast.77, bf16[1,2,128,1792]{3,2,1,0:T(8,128)(2,1)S(1)} %bitcast.76, bf16[1,2,128,1792]{3,2,1,0:T(8,128)(2,1)S(1)} %bitcast.75, bf16[1,2,128,1792]{3,2,1,0:T(8,128)(2,1)S(1)} %get-tuple-element.43), kind=kLoop, calls=%fused_computation | loop fusion | flops 5505024 | bytes 7340032 | tf_op jit(solution)/shard_map/stack | solution.py:154
  34.1 0.1 collective-permute-start.9
  34.2 1.1 slice_bitcast_fusion.14
  35.3 0.1 fusion.29
  35.3 0.0 copy-start.3
  35.3 0.6 collective-permute-start
  35.9 3.4 %collective-permute-start.1 = (bf16[2,128,768]{2,1,0:T(8,128)(2,1)S(1)}, bf16[2,128,768]{2,1,0:T(8,128)(2,1)S(1)}, u32[]{:S(2)}, u32[]{:S(2)}) collective-permute-start(bf16[2,128,768]{2,1,0:T(8,128)(2,1)S(1)} %get-tuple-element.48.refs_0_), channel_id=1, source_target_pairs={{0,4},{1,5},{2,6},{3,7},{4,8},{5,9},{6,10},{7,11},{8,12},{9,13},{1... | collective-permute-start | bytes 1179656 | tf_op jit(solution)/shard_map/ppermute | solution.py:15
  39.6 4.0 %collective-permute-start.10 = (bf16[2,128,1792]{2,1,0:T(8,128)(2,1)S(1)}, bf16[2,128,1792]{2,1,0:T(8,128)(2,1)}, u32[]{:S(2)}, u32[]{:S(2)}) collective-permute-start(bf16[2,128,1792]{2,1,0:T(8,128)(2,1)S(1)} %collective-permute-done.6.refs_1_), channel_id=1, source_target_pairs={{0,5},{3,6},{4,9},{7,10},{8,13},{11,14},{16,21},{19,22},{20,25},{2... | collective-permute-start | bytes 2752520 | tf_op jit(solution)/shard_map/ppermute | solution.py:15
  43.6 0.1 copy.9
  43.7 0.1 select_reduce_fusion
  43.7 0.1 multiply_reduce_fusion
  43.8 0.7 collective-permute-start.11
  44.6 13.3 %collective-permute-done.10.refs_5_ = bf16[2,128,1792]{2,1,0:T(8,128)(2,1)} collective-permute-done((bf16[2,128,1792]{2,1,0:T(8,128)(2,1)S(1)}, bf16[2,128,1792]{2,1,0:T(8,128)(2,1)}, u32[]{:S(2)}, u32[]{:S(2)}) %collective-permute-start.10) | collective-permute-done | bytes 917536 | tf_op jit(solution)/shard_map/ppermute | solution.py:15
  57.9 1.3 collective-permute-start.2
  59.2 1.4 fusion.24.mask_ref
  60.6 0.0 collective-permute-done.11.refs_6_
  60.6 0.9 copy-done.19
  61.6 0.0 collective-permute-done.9.refs_4_
  61.6 18.5 %shard_map.86 = (bf16[128,1792]{1,0:T(8,128)(2,1)}, bf16[2,128,1792]{2,1,0:T(8,128)(2,1)}, bf16[4,2,128,1792]{3,2,1,0:T(8,128)(2,1)}, bf16[2,128,1792]{2,1,0:T(8...) custom-call(s32[128,1280]{1,0:T(8,128)} %fusion.24.mask_ref, ...), custom_call_target="tpu_custom_call" | custom-call | flops 3523215360 | bytes 20381696 | tf_op jit(solution)/shard_map/pallas_call | solution.py:126
  80.0 0.1 collective-permute-start.18
  80.1 0.0 collective-permute-done.1.refs_2_
  80.2 0.0 collective-permute-done.2.refs_3_
  80.2 0.2 pad_maximum_fusion.1
  80.4 0.5 collective-permute-start.3
  80.9 4.6 %collective-permute-start.4 = (bf16[2,128,768]{2,1,0:T(8,128)(2,1)S(1)}, bf16[2,128,768]{2,1,0:T(8,128)(2,1)S(1)}, u32[]{:S(2)}, u32[]{:S(2)}) collective-permute-start(bf16[2,128,768]{2,1,0:T(8,128)(2,1)S(1)} %collective-permute-done.refs_1_), channel_id=1, source_target_pairs={{0,5},{3,6},{4,9},{7,10},{8,13},{11,14},{16,21},{19,22},{20,25},{2... | collective-permute-start | bytes 1179656 | tf_op jit(solution)/shard_map/ppermute | solution.py:15
  85.5 0.7 collective-permute-start.5
  86.2 4.6 %collective-permute-done.4.refs_5_ = bf16[2,128,768]{2,1,0:T(8,128)(2,1)S(1)} collective-permute-done((bf16[2,128,768]{2,1,0:T(8,128)(2,1)S(1)}, bf16[2,128,768]{2,1,0:T(8,128)(2,1)S(1)}, u32[]{:S(2)}, u32[]{:S(2)}) %collective-permute-start.4) | collective-permute-done | bytes 393248 | tf_op jit(solution)/shard_map/ppermute | solution.py:15
  90.7 0.0 collective-permute-done.3.refs_4_
  90.8 0.7 copy-done.15
  91.5 0.1 copy-done.16
  91.6 1.3 copy-done.4
  92.9 9.5 %shard_map.85 = (bf16[128,768]{1,0:T(8,128)(2,1)}, bf16[2,128,768]{2,1,0:T(8,128)(2,1)}, bf16[4,2,128,768]{3,2,1,0:T(8,128)(2,1)}, bf16[2,128,768]{2,1,0:T(8,128...) custom-call(s32[128,1280]{1,0:T(8,128)} %fusion.24.mask_ref, ...), custom_call_target="tpu_custom_call" | custom-call | flops 1509949440 | bytes 9109504 | tf_op jit(solution)/shard_map/pallas_call | solution.py:126
  102.4 3.3 %collective-permute-start.12 = (bf16[4,2,128,768]{3,2,1,0:T(8,128)(2,1)}, bf16[4,2,128,768]{3,2,1,0:T(8,128)(2,1)S(1)}, u32[]{:S(2)}, u32[]{:S(2)}) collective-permute-start(bf16[4,2,128,768]{3,2,1,0:T(8,128)(2,1)} %get-tuple-element.22), channel_id=1, source_target_pairs={{0,1},{1,0},{2,3},{3,2},{4,5},{5,4},{6,7},{7,6},{8,9},{9,8},{10,11... | collective-permute-start | bytes 4718600 | tf_op jit(solution)/shard_map/ppermute | solution.py:15
  105.7 0.7 collective-permute-start.14
  106.4 0.7 collective-permute-start.20
  107.1 1.3 collective-permute-start.19
  108.4 1.3 collective-permute-start.13
  109.7 17.8 %collective-permute-done.13 = bf16[2,128,768]{2,1,0:T(8,128)(2,1)S(1)} collective-permute-done((bf16[2,128,768]{2,1,0:T(8,128)(2,1)}, bf16[2,128,768]{2,1,0:T(8,128)(2,1)S(1)}, u32[]{:S(2)}, u32[]{:S(2)}) %collective-permute-start.13) | collective-permute-done | bytes 393248 | tf_op jit(solution)/shard_map/ppermute | solution.py:15
  127.5 1.8 %fusion.13 = (bf16[2,128,768]{2,1,0:T(8,128)(2,1)S(1)}, bf16[2,128,768]{2,1,0:T(8,128)(2,1)S(1)}, bf16[2,128,768]{2,1,0:T(8,128)(2,1)S(1)}) fusion(bf16[2,128,768]{2,1,0:T(8,128)(2,1)S(1)} %collective-permute-done.14, bf16[2,128,768]{2,1,0:T(8,128)(2,1)S(1)} %collective-permute-done.13, bf16[2,128,768]{2,1,0:T(8,128)(2,1)} %get-tuple-element.23, ...), kind=kLoop, calls=%fused_computation.30 | loop fusion | flops 3145728 | bytes 4325376 | tf_op jit(solution)/shard_map/convert_element_type | solution.py:193
  129.3 3.5 %collective-permute-start.17 = (bf16[2,128,768]{2,1,0:T(8,128)(2,1)S(1)}, bf16[2,128,768]{2,1,0:T(8,128)(2,1)S(1)}, u32[]{:S(2)}, u32[]{:S(2)}) collective-permute-start(bf16[2,128,768]{2,1,0:T(8,128)(2,1)S(1)} %get-tuple-element.39), channel_id=1, source_target_pairs={{0,4},{1,5},{2,6},{3,7},{4,8},{5,9},{6,10},{7,11},{8,12},{9,13},{1... | collective-permute-start | bytes 1179656 | tf_op jit(solution)/shard_map/ppermute | solution.py:15
  132.8 1.3 collective-permute-start.16
  134.1 0.8 collective-permute-start.15
  134.9 2.8 %fusion.4 = (bf16[2,128,1792]{2,1,0:T(8,128)(2,1)S(1)}, bf16[2,128,1792]{2,1,0:T(8,128)(2,1)S(1)}, bf16[2,128,1792]{2,1,0:T(8,128)(2,1)S(1)}) fusion(bf16[2,128,1792]{2,1,0:T(8,128)(2,1)S(1)} %collective-permute-done.20, bf16[2,128,1792]{2,1,0:T(8,128)(2,1)S(1)} %collective-permute-done.19, bf16[2,128,1792]{2,1,0:T(8,128)(2,1)S(1)} %copy-done.5, ...), kind=kLoop, calls=%fused_computation.8 | loop fusion | flops 7340032 | bytes 10092544 | tf_op jit(solution)/shard_map/convert_element_type | solution.py:193
  137.7 0.0 copy-start.13
  137.7 4.7 %collective-permute-start.23 = (bf16[2,128,1792]{2,1,0:T(8,128)(2,1)S(1)}, bf16[2,128,1792]{2,1,0:T(8,128)(2,1)S(1)}, u32[]{:S(2)}, u32[]{:S(2)}) collective-permute-start(bf16[2,128,1792]{2,1,0:T(8,128)(2,1)S(1)} %get-tuple-element.36), channel_id=1, source_target_pairs={{0,4},{1,5},{2,6},{3,7},{4,8},{5,9},{6,10},{7,11},{8,12},{9,13},{1... | collective-permute-start | bytes 2752520 | tf_op jit(solution)/shard_map/ppermute | solution.py:15
  142.5 1.3 collective-permute-start.22
  143.8 1.3 collective-permute-start.21
  145.1 0.5 collective-permute-done.15
  145.6 0.2 fusion.17
  145.9 0.9 pad_maximum_fusion.3
  146.8 16.2 %collective-permute-done.23 = bf16[2,128,1792]{2,1,0:T(8,128)(2,1)S(1)} collective-permute-done((bf16[2,128,1792]{2,1,0:T(8,128)(2,1)S(1)}, bf16[2,128,1792]{2,1,0:T(8,128)(2,1)S(1)}, u32[]{:S(2)}, u32[]{:S(2)}) %collective-permute-start.23) | collective-permute-done | bytes 917536 | tf_op jit(solution)/shard_map/ppermute | solution.py:15
  163.1 4.2 %collective-permute-done.22 = bf16[2,128,1792]{2,1,0:T(8,128)(2,1)S(1)} collective-permute-done((bf16[2,128,1792]{2,1,0:T(8,128)(2,1)S(1)}, bf16[2,128,1792]{2,1,0:T(8,128)(2,1)S(1)}, u32[]{:S(2)}, u32[]{:S(2)}) %collective-permute-start.22) | collective-permute-done | bytes 917536 | tf_op jit(solution)/shard_map/ppermute | solution.py:15
  167.2 1.8 %fusion.8 = bf16[2,128,1792]{2,1,0:T(8,128)(2,1)S(1)} fusion(bf16[2,128,1792]{2,1,0:T(8,128)(2,1)S(1)} %collective-permute-done.23, bf16[2,128,1792]{2,1,0:T(8,128)(2,1)S(1)} %collective-permute-done.22, bf16[2,128,1792]{2,1,0:T(8,128)(2,1)S(1)} %collective-permute-done.21, bf16[2,128,1792]{2,1,0:T(8,128)(2,1)S(1)} %copy-done.12, ...), kind=kLoop, calls=%fused_computation.13 | loop fusion | flops 4587520 | bytes 5505024 | tf_op jit(solution)/shard_map/convert.10
  169.0 0.1 slice_bitcast_fusion.4
  169.1 0.9 pad_maximum_fusion.4
  170.0 0.9 pad_maximum_fusion.5
  (64 shorter events, 0.2 us)
Async XLA Ops:
  2.0 30.0 %copy-start.11 = (bf16[2,128,1792]{2,1,0:T(8,128)(2,1)}, bf16[2,128,1792]{2,1,0:T(8,128)(2,1)S(1)}, u32[]{:S(2)}) copy-start(bf16[2,128,1792]{2,1,0:T(8,128)(2,1)S(1)} %get-tuple-element.44.refs_0_) | copy-start | bytes 2752516
  2.0 23.4 %collective-permute-start.6 = (bf16[2,128,1792]{2,1,0:T(8,128)(2,1)S(1)}, bf16[2,128,1792]{2,1,0:T(8,128)(2,1)S(1)}, u32[]{:S(2)}, u32[]{:S(2)}) collective-permute-start(bf16[2,128,1792]{2,1,0:T(8,128)(2,1)S(1)} %get-tuple-element.44.refs_0_), channel_id=1, source_target_pairs={{0,2},{1,3},{2,0},{3,1},{4,6},{5,7},{6,4},{7,5},{8,10},{9,11},{10,... | collective-permute-start | bytes 2752520 | tf_op jit(solution)/shard_map/ppermute | solution.py:15
  5.1 22.8 %collective-permute-start.7 = (bf16[2,128,1792]{2,1,0:T(8,128)(2,1)S(1)}, bf16[2,128,1792]{2,1,0:T(8,128)(2,1)S(1)}, u32[]{:S(2)}, u32[]{:S(2)}) collective-permute-start(bf16[2,128,1792]{2,1,0:T(8,128)(2,1)S(1)} %get-tuple-element.44.refs_0_), channel_id=1, source_target_pairs={{0,4},{1,5},{2,6},{3,7},{4,8},{5,9},{6,10},{7,11},{8,12},{9,13},{1... | collective-permute-start | bytes 2752520 | tf_op jit(solution)/shard_map/ppermute | solution.py:15
  8.6 23.4 %collective-permute-start.8 = (bf16[2,128,1792]{2,1,0:T(8,128)(2,1)S(1)}, bf16[2,128,1792]{2,1,0:T(8,128)(2,1)S(1)}, u32[]{:S(2)}, u32[]{:S(2)}) collective-permute-start(bf16[2,128,1792]{2,1,0:T(8,128)(2,1)S(1)} %get-tuple-element.44.refs_0_), channel_id=1, source_target_pairs={{4,0},{5,1},{6,2},{7,3},{8,4},{9,5},{10,6},{11,7},{12,8},{13,9},{1... | collective-permute-start | bytes 2752520 | tf_op jit(solution)/shard_map/ppermute | solution.py:15
  25.4 18.4 %copy-start.8 = (bf16[2,128,1792]{2,1,0:T(8,128)(2,1)}, bf16[2,128,1792]{2,1,0:T(8,128)(2,1)S(1)}, u32[]{:S(2)}) copy-start(bf16[2,128,1792]{2,1,0:T(8,128)(2,1)S(1)} %collective-permute-done.6.refs_1_) | copy-start | bytes 2752516
  27.8 6.3 %copy-start.9 = (bf16[2,128,1792]{2,1,0:T(8,128)(2,1)}, bf16[2,128,1792]{2,1,0:T(8,128)(2,1)S(1)}, u32[]{:S(2)}) copy-start(bf16[2,128,1792]{2,1,0:T(8,128)(2,1)S(1)} %collective-permute-done.7.refs_2_) | copy-start | bytes 2752516
  32.0 2.1 %copy-start.10 = (bf16[2,128,1792]{2,1,0:T(8,128)(2,1)}, bf16[2,128,1792]{2,1,0:T(8,128)(2,1)S(1)}, u32[]{:S(2)}) copy-start(bf16[2,128,1792]{2,1,0:T(8,128)(2,1)S(1)} %collective-permute-done.8.refs_3_) | copy-start | bytes 2752516
  34.1 9.4 %copy-start.18 = (s32[4,3]{1,0:T(4,128)S(1)}, s32[4,3]{1,0:T(4,128)}, u32[]{:S(2)}) copy-start(s32[4,3]{1,0:T(4,128)} %param.10) | copy-start | bytes 148
  34.1 9.5 %copy-start.20 = (s32[4]{0:T(128)S(1)}, s32[4]{0:T(128)}, u32[]{:S(2)}) copy-start(s32[4]{0:T(128)} %param.11) | copy-start | bytes 52
  34.1 27.4 %collective-permute-start.9 = (bf16[4,2,128,1792]{3,2,1,0:T(8,128)(2,1)}, bf16[4,2,128,1792]{3,2,1,0:T(8,128)(2,1)}, u32[]{:S(2)}, u32[]{:S(2)}) collective-permute-start(bf16[4,2,128,1792]{3,2,1,0:T(8,128)(2,1)} %pad_maximum_fusion), channel_id=1, source_target_pairs={{0,1},{1,0},{2,3},{3,2},{4,5},{5,4},{6,7},{7,6},{8,9},{9,8},{10,11... | collective-permute-start | bytes 11010056 | tf_op jit(solution)/shard_map/ppermute | solution.py:15
  35.3 44.7 %copy-start.3 = (bf16[2,128,768]{2,1,0:T(8,128)(2,1)}, bf16[2,128,768]{2,1,0:T(8,128)(2,1)S(1)}, u32[]{:S(2)}) copy-start(bf16[2,128,768]{2,1,0:T(8,128)(2,1)S(1)} %get-tuple-element.48.refs_0_) | copy-start | bytes 1179652
  35.3 44.8 %collective-permute-start = (bf16[2,128,768]{2,1,0:T(8,128)(2,1)S(1)}, bf16[2,128,768]{2,1,0:T(8,128)(2,1)S(1)}, u32[]{:S(2)}, u32[]{:S(2)}) collective-permute-start(bf16[2,128,768]{2,1,0:T(8,128)(2,1)S(1)} %get-tuple-element.48.refs_0_), channel_id=1, source_target_pairs={{0,2},{1,3},{2,0},{3,1},{4,6},{5,7},{6,4},{7,5},{8,10},{9,11},{10,... | collective-permute-start | bytes 1179656 | tf_op jit(solution)/shard_map/ppermute | solution.py:15
  35.9 44.2 %collective-permute-start.1 = (bf16[2,128,768]{2,1,0:T(8,128)(2,1)S(1)}, bf16[2,128,768]{2,1,0:T(8,128)(2,1)S(1)}, u32[]{:S(2)}, u32[]{:S(2)}) collective-permute-start(bf16[2,128,768]{2,1,0:T(8,128)(2,1)S(1)} %get-tuple-element.48.refs_0_), channel_id=1, source_target_pairs={{0,4},{1,5},{2,6},{3,7},{4,8},{5,9},{6,10},{7,11},{8,12},{9,13},{1... | collective-permute-start | bytes 1179656 | tf_op jit(solution)/shard_map/ppermute | solution.py:15
  39.6 18.3 %collective-permute-start.10 = (bf16[2,128,1792]{2,1,0:T(8,128)(2,1)S(1)}, bf16[2,128,1792]{2,1,0:T(8,128)(2,1)}, u32[]{:S(2)}, u32[]{:S(2)}) collective-permute-start(bf16[2,128,1792]{2,1,0:T(8,128)(2,1)S(1)} %collective-permute-done.6.refs_1_), channel_id=1, source_target_pairs={{0,5},{3,6},{4,9},{7,10},{8,13},{11,14},{16,21},{19,22},{20,25},{2... | collective-permute-start | bytes 2752520 | tf_op jit(solution)/shard_map/ppermute | solution.py:15
  43.8 16.8 %collective-permute-start.11 = (bf16[2,128,1792]{2,1,0:T(8,128)(2,1)S(1)}, bf16[2,128,1792]{2,1,0:T(8,128)(2,1)S(1)}, u32[]{:S(2)}, u32[]{:S(2)}) collective-permute-start(bf16[2,128,1792]{2,1,0:T(8,128)(2,1)S(1)} %collective-permute-done.6.refs_1_), channel_id=1, source_target_pairs={{4,1},{7,2},{8,5},{11,6},{12,9},{15,10},{20,17},{23,18},{24,21},{2... | collective-permute-start | bytes 2752520 | tf_op jit(solution)/shard_map/ppermute | solution.py:15
  57.9 22.3 %collective-permute-start.2 = (bf16[2,128,768]{2,1,0:T(8,128)(2,1)S(1)}, bf16[2,128,768]{2,1,0:T(8,128)(2,1)S(1)}, u32[]{:S(2)}, u32[]{:S(2)}) collective-permute-start(bf16[2,128,768]{2,1,0:T(8,128)(2,1)S(1)} %get-tuple-element.48.refs_0_), channel_id=1, source_target_pairs={{4,0},{5,1},{6,2},{7,3},{8,4},{9,5},{10,6},{11,7},{12,8},{13,9},{1... | collective-permute-start | bytes 1179656 | tf_op jit(solution)/shard_map/ppermute | solution.py:15
  60.6 0.9 copy-start.19
  80.0 54.9 %collective-permute-start.18 = (bf16[4,2,128,1792]{3,2,1,0:T(8,128)(2,1)}, bf16[4,2,128,1792]{3,2,1,0:T(8,128)(2,1)}, u32[]{:S(2)}, u32[]{:S(2)}) collective-permute-start(bf16[4,2,128,1792]{3,2,1,0:T(8,128)(2,1)} %get-tuple-element.29), channel_id=1, source_target_pairs={{0,1},{1,0},{2,3},{3,2},{4,5},{5,4},{6,7},{7,6},{8,9},{9,8},{10,11... | collective-permute-start | bytes 11010056 | tf_op jit(solution)/shard_map/ppermute | solution.py:15
  80.1 10.6 %copy-start = (bf16[2,128,768]{2,1,0:T(8,128)(2,1)}, bf16[2,128,768]{2,1,0:T(8,128)(2,1)S(1)}, u32[]{:S(2)}) copy-start(bf16[2,128,768]{2,1,0:T(8,128)(2,1)S(1)} %collective-permute-done.refs_1_) | copy-start | bytes 1179652
  80.1 10.6 %copy-start.1 = (bf16[2,128,768]{2,1,0:T(8,128)(2,1)}, bf16[2,128,768]{2,1,0:T(8,128)(2,1)S(1)}, u32[]{:S(2)}) copy-start(bf16[2,128,768]{2,1,0:T(8,128)(2,1)S(1)} %collective-permute-done.1.refs_2_) | copy-start | bytes 1179652
  80.2 10.6 %copy-start.2 = (bf16[2,128,768]{2,1,0:T(8,128)(2,1)}, bf16[2,128,768]{2,1,0:T(8,128)(2,1)S(1)}, u32[]{:S(2)}) copy-start(bf16[2,128,768]{2,1,0:T(8,128)(2,1)S(1)} %collective-permute-done.2.refs_3_) | copy-start | bytes 1179652
  80.4 10.4 %collective-permute-start.3 = (bf16[4,2,128,768]{3,2,1,0:T(8,128)(2,1)S(1)}, bf16[4,2,128,768]{3,2,1,0:T(8,128)(2,1)S(1)}, u32[]{:S(2)}, u32[]{:S(2)}) collective-permute-start(bf16[4,2,128,768]{3,2,1,0:T(8,128)(2,1)S(1)} %pad_maximum_fusion.1), channel_id=1, source_target_pairs={{0,1},{1,0},{2,3},{3,2},{4,5},{5,4},{6,7},{7,6},{8,9},{9,8},{10,11... | collective-permute-start | bytes 4718600 | tf_op jit(solution)/shard_map/ppermute | solution.py:15
  80.9 9.8 %collective-permute-start.4 = (bf16[2,128,768]{2,1,0:T(8,128)(2,1)S(1)}, bf16[2,128,768]{2,1,0:T(8,128)(2,1)S(1)}, u32[]{:S(2)}, u32[]{:S(2)}) collective-permute-start(bf16[2,128,768]{2,1,0:T(8,128)(2,1)S(1)} %collective-permute-done.refs_1_), channel_id=1, source_target_pairs={{0,5},{3,6},{4,9},{7,10},{8,13},{11,14},{16,21},{19,22},{20,25},{2... | collective-permute-start | bytes 1179656 | tf_op jit(solution)/shard_map/ppermute | solution.py:15
  85.5 5.3 %collective-permute-start.5 = (bf16[2,128,768]{2,1,0:T(8,128)(2,1)S(1)}, bf16[2,128,768]{2,1,0:T(8,128)(2,1)S(1)}, u32[]{:S(2)}, u32[]{:S(2)}) collective-permute-start(bf16[2,128,768]{2,1,0:T(8,128)(2,1)S(1)} %collective-permute-done.refs_1_), channel_id=1, source_target_pairs={{4,1},{7,2},{8,5},{11,6},{12,9},{15,10},{20,17},{23,18},{24,21},{2... | collective-permute-start | bytes 1179656 | tf_op jit(solution)/shard_map/ppermute | solution.py:15
  90.7 0.8 copy-start.15
  90.7 0.9 copy-start.16
  91.6 1.3 copy-start.4
  102.4 25.1 %collective-permute-start.12 = (bf16[4,2,128,768]{3,2,1,0:T(8,128)(2,1)}, bf16[4,2,128,768]{3,2,1,0:T(8,128)(2,1)S(1)}, u32[]{:S(2)}, u32[]{:S(2)}) collective-permute-start(bf16[4,2,128,768]{3,2,1,0:T(8,128)(2,1)} %get-tuple-element.22), channel_id=1, source_target_pairs={{0,1},{1,0},{2,3},{3,2},{4,5},{5,4},{6,7},{7,6},{8,9},{9,8},{10,11... | collective-permute-start | bytes 4718600 | tf_op jit(solution)/shard_map/ppermute | solution.py:15
  105.7 2.7 %collective-permute-start.14 = (bf16[2,128,768]{2,1,0:T(8,128)(2,1)}, bf16[2,128,768]{2,1,0:T(8,128)(2,1)S(1)}, u32[]{:S(2)}, u32[]{:S(2)}) collective-permute-start(bf16[2,128,768]{2,1,0:T(8,128)(2,1)} %get-tuple-element.25), channel_id=1, source_target_pairs={{1,4},{2,7},{5,8},{6,11},{9,12},{10,15},{17,20},{18,23},{21,24},{2... | collective-permute-start | bytes 1179656 | tf_op jit(solution)/shard_map/ppermute | solution.py:15
  106.4 27.7 %collective-permute-start.20 = (bf16[2,128,1792]{2,1,0:T(8,128)(2,1)}, bf16[2,128,1792]{2,1,0:T(8,128)(2,1)S(1)}, u32[]{:S(2)}, u32[]{:S(2)}) collective-permute-start(bf16[2,128,1792]{2,1,0:T(8,128)(2,1)} %get-tuple-element.32), channel_id=1, source_target_pairs={{1,4},{2,7},{5,8},{6,11},{9,12},{10,15},{17,20},{18,23},{21,24},{2... | collective-permute-start | bytes 2752520 | tf_op jit(solution)/shard_map/ppermute | solution.py:15
  107.1 27.8 %collective-permute-start.19 = (bf16[2,128,1792]{2,1,0:T(8,128)(2,1)}, bf16[2,128,1792]{2,1,0:T(8,128)(2,1)S(1)}, u32[]{:S(2)}, u32[]{:S(2)}) collective-permute-start(bf16[2,128,1792]{2,1,0:T(8,128)(2,1)} %get-tuple-element.31), channel_id=1, source_target_pairs={{5,0},{6,3},{9,4},{10,7},{13,8},{14,11},{21,16},{22,19},{25,20},{2... | collective-permute-start | bytes 2752520 | tf_op jit(solution)/shard_map/ppermute | solution.py:15
  108.4 19.1 %collective-permute-start.13 = (bf16[2,128,768]{2,1,0:T(8,128)(2,1)}, bf16[2,128,768]{2,1,0:T(8,128)(2,1)S(1)}, u32[]{:S(2)}, u32[]{:S(2)}) collective-permute-start(bf16[2,128,768]{2,1,0:T(8,128)(2,1)} %get-tuple-element.24), channel_id=1, source_target_pairs={{5,0},{6,3},{9,4},{10,7},{13,8},{14,11},{21,16},{22,19},{25,20},{2... | collective-permute-start | bytes 1179656 | tf_op jit(solution)/shard_map/ppermute | solution.py:15
  127.5 7.5 %copy-start.5 = (bf16[2,128,1792]{2,1,0:T(8,128)(2,1)S(1)}, bf16[2,128,1792]{2,1,0:T(8,128)(2,1)}, u32[]{:S(2)}) copy-start(bf16[2,128,1792]{2,1,0:T(8,128)(2,1)} %get-tuple-element.30) | copy-start | bytes 2752516
  127.5 7.5 %copy-start.6 = (bf16[2,128,1792]{2,1,0:T(8,128)(2,1)S(1)}, bf16[2,128,1792]{2,1,0:T(8,128)(2,1)}, u32[]{:S(2)}) copy-start(bf16[2,128,1792]{2,1,0:T(8,128)(2,1)} %get-tuple-element.33) | copy-start | bytes 2752516
  127.5 7.5 %copy-start.7 = (bf16[2,128,1792]{2,1,0:T(8,128)(2,1)S(1)}, bf16[2,128,1792]{2,1,0:T(8,128)(2,1)}, u32[]{:S(2)}) copy-start(bf16[2,128,1792]{2,1,0:T(8,128)(2,1)} %get-tuple-element.34) | copy-start | bytes 2752516
  129.3 14.5 %collective-permute-start.17 = (bf16[2,128,768]{2,1,0:T(8,128)(2,1)S(1)}, bf16[2,128,768]{2,1,0:T(8,128)(2,1)S(1)}, u32[]{:S(2)}, u32[]{:S(2)}) collective-permute-start(bf16[2,128,768]{2,1,0:T(8,128)(2,1)S(1)} %get-tuple-element.39), channel_id=1, source_target_pairs={{0,4},{1,5},{2,6},{3,7},{4,8},{5,9},{6,10},{7,11},{8,12},{9,13},{1... | collective-permute-start | bytes 1179656 | tf_op jit(solution)/shard_map/ppermute | solution.py:15
  132.8 12.4 %collective-permute-start.16 = (bf16[2,128,768]{2,1,0:T(8,128)(2,1)S(1)}, bf16[2,128,768]{2,1,0:T(8,128)(2,1)S(1)}, u32[]{:S(2)}, u32[]{:S(2)}) collective-permute-start(bf16[2,128,768]{2,1,0:T(8,128)(2,1)S(1)} %get-tuple-element.40), channel_id=1, source_target_pairs={{4,0},{5,1},{6,2},{7,3},{8,4},{9,5},{10,6},{11,7},{12,8},{13,9},{1... | collective-permute-start | bytes 1179656 | tf_op jit(solution)/shard_map/ppermute | solution.py:15
  134.1 11.6 %collective-permute-start.15 = (bf16[2,128,768]{2,1,0:T(8,128)(2,1)S(1)}, bf16[2,128,768]{2,1,0:T(8,128)(2,1)S(1)}, u32[]{:S(2)}, u32[]{:S(2)}) collective-permute-start(bf16[2,128,768]{2,1,0:T(8,128)(2,1)S(1)} %get-tuple-element.38), channel_id=1, source_target_pairs={{0,2},{1,3},{2,0},{3,1},{4,6},{5,7},{6,4},{7,5},{8,10},{9,11},{10,... | collective-permute-start | bytes 1179656 | tf_op jit(solution)/shard_map/ppermute | solution.py:15
  134.9 10.7 %copy-start.14 = (bf16[2,128,768]{2,1,0:T(8,128)(2,1)S(1)}, bf16[2,128,768]{2,1,0:T(8,128)(2,1)}, u32[]{:S(2)}) copy-start(bf16[2,128,768]{2,1,0:T(8,128)(2,1)} %get-tuple-element.21) | copy-start | bytes 1179652
  137.7 8.2 %copy-start.13 = (bf16[128,1792]{1,0:T(8,128)(2,1)S(1)}, bf16[128,1792]{1,0:T(8,128)(2,1)}, u32[]{:S(2)}) copy-start(bf16[128,1792]{1,0:T(8,128)(2,1)} %get-tuple-element.20) | copy-start | bytes 1376260
  137.7 8.2 %copy-start.17 = (bf16[128,768]{1,0:T(8,128)(2,1)S(1)}, bf16[128,768]{1,0:T(8,128)(2,1)}, u32[]{:S(2)}) copy-start(bf16[128,768]{1,0:T(8,128)(2,1)} %get-tuple-element.19) | copy-start | bytes 589828
  137.7 25.3 %collective-permute-start.23 = (bf16[2,128,1792]{2,1,0:T(8,128)(2,1)S(1)}, bf16[2,128,1792]{2,1,0:T(8,128)(2,1)S(1)}, u32[]{:S(2)}, u32[]{:S(2)}) collective-permute-start(bf16[2,128,1792]{2,1,0:T(8,128)(2,1)S(1)} %get-tuple-element.36), channel_id=1, source_target_pairs={{0,4},{1,5},{2,6},{3,7},{4,8},{5,9},{6,10},{7,11},{8,12},{9,13},{1... | collective-permute-start | bytes 2752520 | tf_op jit(solution)/shard_map/ppermute | solution.py:15
  142.5 24.7 %collective-permute-start.22 = (bf16[2,128,1792]{2,1,0:T(8,128)(2,1)S(1)}, bf16[2,128,1792]{2,1,0:T(8,128)(2,1)S(1)}, u32[]{:S(2)}, u32[]{:S(2)}) collective-permute-start(bf16[2,128,1792]{2,1,0:T(8,128)(2,1)S(1)} %get-tuple-element.37), channel_id=1, source_target_pairs={{4,0},{5,1},{6,2},{7,3},{8,4},{9,5},{10,6},{11,7},{12,8},{13,9},{1... | collective-permute-start | bytes 2752520 | tf_op jit(solution)/shard_map/ppermute | solution.py:15
  143.8 23.4 %collective-permute-start.21 = (bf16[2,128,1792]{2,1,0:T(8,128)(2,1)S(1)}, bf16[2,128,1792]{2,1,0:T(8,128)(2,1)S(1)}, u32[]{:S(2)}, u32[]{:S(2)}) collective-permute-start(bf16[2,128,1792]{2,1,0:T(8,128)(2,1)S(1)} %get-tuple-element.35), channel_id=1, source_target_pairs={{0,2},{1,3},{2,0},{3,1},{4,6},{5,7},{6,4},{7,5},{8,10},{9,11},{10,... | collective-permute-start | bytes 2752520 | tf_op jit(solution)/shard_map/ppermute | solution.py:15
  145.6 21.6 %copy-start.12 = (bf16[2,128,1792]{2,1,0:T(8,128)(2,1)S(1)}, bf16[2,128,1792]{2,1,0:T(8,128)(2,1)}, u32[]{:S(2)}) copy-start(bf16[2,128,1792]{2,1,0:T(8,128)(2,1)} %get-tuple-element.28) | copy-start | bytes 2752516

commit v16 on v12

--- a/solution.py
+++ b/solution.py
@@ -8,7 +8,7 @@
 
 HD = 128
 QUARTERS = 4
-CHUNKS = 2
+CHUNKS = 3
 STEP_HEADS = 2
 
 
@@ -230,11 +230,14 @@
     own_rows = device * rows_own + base_rows
     forward_mask = allowed(own_rows, far_rows, frame_keep, band_window, frame_len).astype(jnp.int32)
     heads = channel_total // HD
-    chunk_heads = heads // CHUNKS if heads % CHUNKS == 0 else heads
-    width = chunk_heads * HD
-    starts = list(range(0, channel_total, width))
+    units = heads // STEP_HEADS if heads % STEP_HEADS == 0 else 0
+    pieces = min(CHUNKS, units) if units else 1
+    cuts = [(units * k // pieces) * STEP_HEADS * HD for k in range(pieces + 1)] if units else [0, channel_total]
+    starts = cuts[:-1]
+    widths = [b - a for a, b in zip(cuts[:-1], cuts[1:])]
     firsts, seconds, outs, backs, sums, dqs = [], [], [], [], [], []
     for c, first in enumerate(starts):
+        width = widths[c]
         own = jnp.stack([keys[:, first : first + width], values[:, first : first + width]])
         firsts.append(forward_relay(own, count, None))
     for c in range(len(starts)):

time: 144 us -> 160 us (1.11)
  starting transfers between devices: 42.9 us -> 67.9 us
  waiting for transfers between devices: 51.9 us -> 37.7 us
  Pallas kernels: 28.1 us -> 31 us
  other arithmetic: 15.5 us -> 17.7 us
    ppermute x24 -> x36, starting transfers between devices: 42.9 us -> 67.9 us  [send(): return lax.ppermute(value, 'tm', pairs)]
    ppermute x24 -> x36, waiting for transfers between devices: 51.9 us -> 37.7 us  [send(): return lax.ppermute(value, 'tm', pairs)]
    pallas_call x2 -> x3, Pallas kernels: 28.1 us -> 31 us  [attention_backward(): pl.pallas_call(kernel, grid=(heads // STEP_HEADS,), in_specs=in_specs, ou...]
    convert_element_type x2 -> x3, other arithmetic: 3.01 us -> 4.61 us  [return_second(): cross_sum.astype(jnp.bfloat16)]
    another operation x4 -> x6, other arithmetic: 5.2 us -> 5.2 us  [forward_second(): ahead = jnp.stack([own, from_cross, from_below, from_above])]
  transfers between devices with their start and end apart: 24 -> 36, of which waited for: 14 -> 12; matrix products, arithmetic and copies ran while one was open for 9% -> 10% of each run, Pallas kernels for 20% -> 19%
where the time goes in v16:
time: 160 us; the launch traced here: 159 us
  starting transfers between devices  67.9 us (42%)
  waiting for transfers between devices  37.7 us (24%)
  Pallas kernels  31 us (19%)
  other arithmetic  17.7 us (11%)
  local copies, waits for them, and re-layouts  3.41 us (2%)
    ppermute x36, starting transfers between devices, send(): return lax.ppermute(value, 'tm', pairs)  67.9 us
    ppermute x36, waiting for transfers between devices, send(): return lax.ppermute(value, 'tm', pairs)  37.7 us
    pallas_call x3, Pallas kernels, attention_backward(): pl.pallas_call(kernel, grid=(heads // STEP_HEADS,), in_specs=in_specs, ou...  31 us
    another operation x6, other arithmetic, forward_second(): ahead = jnp.stack([own, from_cross, from_below, from_above])  5.2 us
    convert_element_type x3, other arithmetic, return_second(): cross_sum.astype(jnp.bfloat16)  4.61 us
  transfers between devices with their start and end apart: 36, of which 12 were waited for; matrix products, arithmetic and copies ran while one was open for 10% of the time, Pallas kernels for 19%

profile of v16, /device:TPU:0, one launch (start us, length us, event | category | flops | bytes accessed | tf_op | source)
XLA Modules:
  0.0 159.2 jit_solution(16379726075285500562)
XLA Ops:
  0.6 1.3 slice_bitcast_fusion.22
  2.0 3.1 %collective-permute-start = (bf16[2,128,768]{2,1,0:T(8,128)(2,1)S(1)}, bf16[2,128,768]{2,1,0:T(8,128)(2,1)S(1)}, u32[]{:S(2)}, u32[]{:S(2)}) collective-permute-start(bf16[2,128,768]{2,1,0:T(8,128)(2,1)S(1)} %get-tuple-element.73.refs_0_), channel_id=1, source_target_pairs={{0,2},{1,3},{2,0},{3,1},{4,6},{5,7},{6,4},{7,5},{8,10},{9,11},{10,... | collective-permute-start | bytes 1179656 | tf_op jit(solution)/shard_map/ppermute | solution.py:16
  5.1 3.5 %collective-permute-start.1 = (bf16[2,128,768]{2,1,0:T(8,128)(2,1)S(1)}, bf16[2,128,768]{2,1,0:T(8,128)(2,1)S(1)}, u32[]{:S(2)}, u32[]{:S(2)}) collective-permute-start(bf16[2,128,768]{2,1,0:T(8,128)(2,1)S(1)} %get-tuple-element.73.refs_0_), channel_id=1, source_target_pairs={{0,4},{1,5},{2,6},{3,7},{4,8},{5,9},{6,10},{7,11},{8,12},{9,13},{1... | collective-permute-start | bytes 1179656 | tf_op jit(solution)/shard_map/ppermute | solution.py:16
  8.6 1.3 collective-permute-start.2
  9.9 1.1 slice_bitcast_fusion.14
  10.9 0.9 fusion.40
  11.8 0.5 collective-permute-start.12
  12.3 5.3 %collective-permute-start.13 = (bf16[2,128,1024]{2,1,0:T(8,128)(2,1)}, bf16[2,128,1024]{2,1,0:T(8,128)(2,1)}, u32[]{:S(2)}, u32[]{:S(2)}) collective-permute-start(bf16[2,128,1024]{2,1,0:T(8,128)(2,1)} %get-tuple-element.67.refs_0_), channel_id=1, source_target_pairs={{0,4},{1,5},{2,6},{3,7},{4,8},{5,9},{6,10},{7,11},{8,12},{9,13},{1... | collective-permute-start | bytes 1572872 | tf_op jit(solution)/shard_map/ppermute | solution.py:16
  17.7 0.5 and_select_fusion
  18.3 1.3 collective-permute-start.14
  19.9 1.6 collective-permute-start.6
  21.4 4.6 %collective-permute-start.7 = (bf16[2,128,768]{2,1,0:T(8,128)(2,1)S(1)}, bf16[2,128,768]{2,1,0:T(8,128)(2,1)S(1)}, u32[]{:S(2)}, u32[]{:S(2)}) collective-permute-start(bf16[2,128,768]{2,1,0:T(8,128)(2,1)S(1)} %get-tuple-element.75.refs_0_), channel_id=1, source_target_pairs={{0,4},{1,5},{2,6},{3,7},{4,8},{5,9},{6,10},{7,11},{8,12},{9,13},{1... | collective-permute-start | bytes 1179656 | tf_op jit(solution)/shard_map/ppermute | solution.py:16
  26.0 0.8 collective-permute-done.12.refs_1_
  26.8 1.3 collective-permute-start.8
  28.1 0.2 pad_maximum_fusion.1
  28.3 1.1 collective-permute-done.13.refs_2_
  29.5 5.9 %collective-permute-done.14.refs_3_ = bf16[2,128,1024]{2,1,0:T(8,128)(2,1)} collective-permute-done((bf16[2,128,1024]{2,1,0:T(8,128)(2,1)}, bf16[2,128,1024]{2,1,0:T(8,128)(2,1)}, u32[]{:S(2)}, u32[]{:S(2)}) %collective-permute-start.14) | collective-permute-done | bytes 524320 | tf_op jit(solution)/shard_map/ppermute | solution.py:16
  35.3 1.5 pad_maximum_fusion
  37.0 4.1 %collective-permute-done.8.refs_3_ = bf16[2,128,768]{2,1,0:T(8,128)(2,1)S(1)} collective-permute-done((bf16[2,128,768]{2,1,0:T(8,128)(2,1)S(1)}, bf16[2,128,768]{2,1,0:T(8,128)(2,1)S(1)}, u32[]{:S(2)}, u32[]{:S(2)}) %collective-permute-start.8) | collective-permute-done | bytes 393248 | tf_op jit(solution)/shard_map/ppermute | solution.py:16
  41.1 2.6 %pad_maximum_fusion.2 = bf16[4,2,128,768]{3,2,1,0:T(8,128)(2,1)} fusion(bf16[1,2,128,768]{3,2,1,0:T(8,128)(2,1)S(1)} %bitcast.109, bf16[1,2,128,768]{3,2,1,0:T(8,128)(2,1)S(1)} %bitcast.108, bf16[1,2,128,768]{3,2,1,0:T(8,128)(2,1)} %bitcast.12, bf16[1,2,128,768]{3,2,1,0:T(8,128)(2,1)S(1)} %get-tuple-element.74), kind=kLoop, calls=%fused_computation.2 | loop fusion | flops 2359296 | bytes 3145728 | tf_op jit(solution)/shard_map/stack | solution.py:155
  43.7 3.6 %collective-permute-start.4 = (bf16[2,128,768]{2,1,0:T(8,128)(2,1)S(1)}, bf16[2,128,768]{2,1,0:T(8,128)(2,1)}, u32[]{:S(2)}, u32[]{:S(2)}) collective-permute-start(bf16[2,128,768]{2,1,0:T(8,128)(2,1)S(1)} %collective-permute-done.refs_1_), channel_id=1, source_target_pairs={{0,5},{3,6},{4,9},{7,10},{8,13},{11,14},{16,21},{19,22},{20,25},{2... | collective-permute-start | bytes 1179656 | tf_op jit(solution)/shard_map/ppermute | solution.py:16
  47.3 0.7 collective-permute-start.5
  48.1 3.7 %collective-permute-done.4.refs_5_ = bf16[2,128,768]{2,1,0:T(8,128)(2,1)} collective-permute-done((bf16[2,128,768]{2,1,0:T(8,128)(2,1)S(1)}, bf16[2,128,768]{2,1,0:T(8,128)(2,1)}, u32[]{:S(2)}, u32[]{:S(2)}) %collective-permute-start.4) | collective-permute-done | bytes 393248 | tf_op jit(solution)/shard_map/ppermute | solution.py:16
  51.8 3.9 %collective-permute-start.10 = (bf16[2,128,768]{2,1,0:T(8,128)(2,1)}, bf16[2,128,768]{2,1,0:T(8,128)(2,1)S(1)}, u32[]{:S(2)}, u32[]{:S(2)}) collective-permute-start(bf16[2,128,768]{2,1,0:T(8,128)(2,1)} %collective-permute-done.6.refs_1_), channel_id=1, source_target_pairs={{0,5},{3,6},{4,9},{7,10},{8,13},{11,14},{16,21},{19,22},{20,25},{2... | collective-permute-start | bytes 1179656 | tf_op jit(solution)/shard_map/ppermute | solution.py:16
  55.8 0.7 copy-done.21
  56.5 0.7 collective-permute-start.11
  57.2 1.4 fusion.33.mask_ref
  58.7 9.6 %shard_map.85 = (bf16[128,768]{1,0:T(8,128)(2,1)}, bf16[2,128,768]{2,1,0:T(8,128)(2,1)}, bf16[4,2,128,768]{3,2,1,0:T(8,128)(2,1)}, bf16[2,128,768]{2,1,0:T(8,128...) custom-call(s32[128,1280]{1,0:T(8,128)} %fusion.33.mask_ref, ...), custom_call_target="tpu_custom_call" | custom-call | flops 1509949440 | bytes 9109504 | tf_op jit(solution)/shard_map/pallas_call | solution.py:127
  68.2 0.6 collective-permute-start.18
  68.9 5.1 %collective-permute-start.16 = (bf16[2,128,1024]{2,1,0:T(8,128)(2,1)S(1)}, bf16[2,128,1024]{2,1,0:T(8,128)(2,1)}, u32[]{:S(2)}, u32[]{:S(2)}) collective-permute-start(bf16[2,128,1024]{2,1,0:T(8,128)(2,1)S(1)} %collective-permute-done.12.refs_1_), channel_id=1, source_target_pairs={{0,5},{3,6},{4,9},{7,10},{8,13},{11,14},{16,21},{19,22},{20,25},{2... | collective-permute-start | bytes 1572872 | tf_op jit(solution)/shard_map/ppermute | solution.py:16
  74.0 1.5 collective-permute-start.17
  75.4 9.5 %shard_map.86 = (bf16[128,768]{1,0:T(8,128)(2,1)}, bf16[2,128,768]{2,1,0:T(8,128)(2,1)}, bf16[4,2,128,768]{3,2,1,0:T(8,128)(2,1)}, bf16[2,128,768]{2,1,0:T(8,128...) custom-call(s32[128,1280]{1,0:T(8,128)} %fusion.33.mask_ref, ...), custom_call_target="tpu_custom_call" | custom-call | flops 1509949440 | bytes 9109504 | tf_op jit(solution)/shard_map/pallas_call | solution.py:127
  85.1 11.9 %shard_map.87 = (bf16[128,1024]{1,0:T(8,128)(2,1)}, bf16[2,128,1024]{2,1,0:T(8,128)(2,1)}, bf16[4,2,128,1024]{3,2,1,0:T(8,128)(2,1)}, bf16[2,128,1024]{2,1,0:T(8...) custom-call(s32[128,1280]{1,0:T(8,128)} %fusion.33.mask_ref, ...), custom_call_target="tpu_custom_call" | custom-call | flops 2013265920 | bytes 11927552 | tf_op jit(solution)/shard_map/pallas_call | solution.py:127
  97.0 0.5 collective-permute-start.30
  97.5 1.3 collective-permute-start.19
  98.8 0.7 collective-permute-start.20
  99.5 7.3 %collective-permute-done.19 = bf16[2,128,768]{2,1,0:T(8,128)(2,1)S(1)} collective-permute-done((bf16[2,128,768]{2,1,0:T(8,128)(2,1)}, bf16[2,128,768]{2,1,0:T(8,128)(2,1)S(1)}, u32[]{:S(2)}, u32[]{:S(2)}) %collective-permute-start.19) | collective-permute-done | bytes 393248 | tf_op jit(solution)/shard_map/ppermute | solution.py:16
  106.8 1.3 collective-permute-start.25
  108.1 0.7 collective-permute-start.26
  108.8 1.9 %fusion.22 = (bf16[2,128,768]{2,1,0:T(8,128)(2,1)S(1)}, bf16[2,128,768]{2,1,0:T(8,128)(2,1)S(1)}, bf16[2,128,768]{2,1,0:T(8,128)(2,1)S(1)}) fusion(bf16[2,128,768]{2,1,0:T(8,128)(2,1)S(1)} %collective-permute-done.20, bf16[2,128,768]{2,1,0:T(8,128)(2,1)S(1)} %collective-permute-done.19, bf16[2,128,768]{2,1,0:T(8,128)(2,1)S(1)} %copy-done.17, ...), kind=kLoop, calls=%fused_computation.39 | loop fusion | flops 3145728 | bytes 4325376 | tf_op jit(solution)/shard_map/convert_element_type | solution.py:194
  110.8 2.9 %collective-permute-start.21 = (bf16[2,128,768]{2,1,0:T(8,128)(2,1)S(1)}, bf16[2,128,768]{2,1,0:T(8,128)(2,1)S(1)}, u32[]{:S(2)}, u32[]{:S(2)}) collective-permute-start(bf16[2,128,768]{2,1,0:T(8,128)(2,1)S(1)} %get-tuple-element.54), channel_id=1, source_target_pairs={{0,2},{1,3},{2,0},{3,1},{4,6},{5,7},{6,4},{7,5},{8,10},{9,11},{10,... | collective-permute-start | bytes 1179656 | tf_op jit(solution)/shard_map/ppermute | solution.py:16
  113.6 2.4 %collective-permute-done.25 = bf16[2,128,768]{2,1,0:T(8,128)(2,1)S(1)} collective-permute-done((bf16[2,128,768]{2,1,0:T(8,128)(2,1)}, bf16[2,128,768]{2,1,0:T(8,128)(2,1)S(1)}, u32[]{:S(2)}, u32[]{:S(2)}) %collective-permute-start.25) | collective-permute-done | bytes 393248 | tf_op jit(solution)/shard_map/ppermute | solution.py:16
  116.1 1.3 collective-permute-start.22
  117.4 4.6 %collective-permute-start.23 = (bf16[2,128,768]{2,1,0:T(8,128)(2,1)S(1)}, bf16[2,128,768]{2,1,0:T(8,128)(2,1)S(1)}, u32[]{:S(2)}, u32[]{:S(2)}) collective-permute-start(bf16[2,128,768]{2,1,0:T(8,128)(2,1)S(1)} %get-tuple-element.55), channel_id=1, source_target_pairs={{0,4},{1,5},{2,6},{3,7},{4,8},{5,9},{6,10},{7,11},{8,12},{9,13},{1... | collective-permute-start | bytes 1179656 | tf_op jit(solution)/shard_map/ppermute | solution.py:16
  122.0 0.9 pad_maximum_fusion.3
  122.9 1.3 collective-permute-start.31
  124.2 0.9 collective-permute-start.32
  125.1 1.7 %fusion.13 = (bf16[2,128,768]{2,1,0:T(8,128)(2,1)S(1)}, bf16[2,128,768]{2,1,0:T(8,128)(2,1)S(1)}, bf16[2,128,768]{2,1,0:T(8,128)(2,1)S(1)}) fusion(bf16[2,128,768]{2,1,0:T(8,128)(2,1)S(1)} %collective-permute-done.26, bf16[2,128,768]{2,1,0:T(8,128)(2,1)S(1)} %collective-permute-done.25, bf16[2,128,768]{2,1,0:T(8,128)(2,1)S(1)} %copy-done.14, ...), kind=kLoop, calls=%fused_computation.26 | loop fusion | flops 3145728 | bytes 4325376 | tf_op jit(solution)/shard_map/convert_element_type | solution.py:194
  127.0 2.3 %collective-permute-start.27 = (bf16[2,128,768]{2,1,0:T(8,128)(2,1)S(1)}, bf16[2,128,768]{2,1,0:T(8,128)(2,1)S(1)}, u32[]{:S(2)}, u32[]{:S(2)}) collective-permute-start(bf16[2,128,768]{2,1,0:T(8,128)(2,1)S(1)} %get-tuple-element.57), channel_id=1, source_target_pairs={{0,2},{1,3},{2,0},{3,1},{4,6},{5,7},{6,4},{7,5},{8,10},{9,11},{10,... | collective-permute-start | bytes 1179656 | tf_op jit(solution)/shard_map/ppermute | solution.py:16
  129.3 1.3 collective-permute-start.28
  130.6 1.3 fusion.26
  131.8 1.5 collective-permute-done.31
  133.3 3.1 %collective-permute-start.29 = (bf16[2,128,768]{2,1,0:T(8,128)(2,1)S(1)}, bf16[2,128,768]{2,1,0:T(8,128)(2,1)S(1)}, u32[]{:S(2)}, u32[]{:S(2)}) collective-permute-start(bf16[2,128,768]{2,1,0:T(8,128)(2,1)S(1)} %get-tuple-element.58), channel_id=1, source_target_pairs={{0,4},{1,5},{2,6},{3,7},{4,8},{5,9},{6,10},{7,11},{8,12},{9,13},{1... | collective-permute-start | bytes 1179656 | tf_op jit(solution)/shard_map/ppermute | solution.py:16
  136.5 1.0 fusion.4
  137.5 1.0 collective-permute-start.33
  138.5 1.3 collective-permute-start.34
  139.8 5.0 %collective-permute-start.35 = (bf16[2,128,1024]{2,1,0:T(8,128)(2,1)S(1)}, bf16[2,128,1024]{2,1,0:T(8,128)(2,1)S(1)}, u32[]{:S(2)}, u32[]{:S(2)}) collective-permute-start(bf16[2,128,1024]{2,1,0:T(8,128)(2,1)S(1)} %get-tuple-element.52), channel_id=1, source_target_pairs={{0,4},{1,5},{2,6},{3,7},{4,8},{5,9},{6,10},{7,11},{8,12},{9,13},{1... | collective-permute-start | bytes 1572872 | tf_op jit(solution)/shard_map/ppermute | solution.py:16
  144.9 1.3 fusion.17
  146.3 6.1 %collective-permute-done.33 = bf16[2,128,1024]{2,1,0:T(8,128)(2,1)S(1)} collective-permute-done((bf16[2,128,1024]{2,1,0:T(8,128)(2,1)S(1)}, bf16[2,128,1024]{2,1,0:T(8,128)(2,1)S(1)}, u32[]{:S(2)}, u32[]{:S(2)}) %collective-permute-start.33) | collective-permute-done | bytes 524320 | tf_op jit(solution)/shard_map/ppermute | solution.py:16
  152.3 3.3 %collective-permute-done.34 = bf16[2,128,1024]{2,1,0:T(8,128)(2,1)S(1)} collective-permute-done((bf16[2,128,1024]{2,1,0:T(8,128)(2,1)S(1)}, bf16[2,128,1024]{2,1,0:T(8,128)(2,1)S(1)}, u32[]{:S(2)}, u32[]{:S(2)}) %collective-permute-start.34) | collective-permute-done | bytes 524320 | tf_op jit(solution)/shard_map/ppermute | solution.py:16
  155.6 1.3 collective-permute-done.35
  156.9 0.5 fusion.8
  157.4 0.9 pad_maximum_fusion.5
  158.3 0.9 pad_maximum_fusion.4
  (116 shorter events, 1.1 us)
Async XLA Ops:
  2.0 17.8 %copy-start.5 = (bf16[2,128,768]{2,1,0:T(8,128)(2,1)}, bf16[2,128,768]{2,1,0:T(8,128)(2,1)S(1)}, u32[]{:S(2)}) copy-start(bf16[2,128,768]{2,1,0:T(8,128)(2,1)S(1)} %get-tuple-element.73.refs_0_) | copy-start | bytes 1179652
  2.0 17.7 %copy-start.27 = (s32[4,3]{1,0:T(4,128)S(1)}, s32[4,3]{1,0:T(4,128)}, u32[]{:S(2)}) copy-start(s32[4,3]{1,0:T(4,128)} %param.10) | copy-start | bytes 148
  2.0 16.3 %collective-permute-start = (bf16[2,128,768]{2,1,0:T(8,128)(2,1)S(1)}, bf16[2,128,768]{2,1,0:T(8,128)(2,1)S(1)}, u32[]{:S(2)}, u32[]{:S(2)}) collective-permute-start(bf16[2,128,768]{2,1,0:T(8,128)(2,1)S(1)} %get-tuple-element.73.refs_0_), channel_id=1, source_target_pairs={{0,2},{1,3},{2,0},{3,1},{4,6},{5,7},{6,4},{7,5},{8,10},{9,11},{10,... | collective-permute-start | bytes 1179656 | tf_op jit(solution)/shard_map/ppermute | solution.py:16
  5.1 14.8 %collective-permute-start.1 = (bf16[2,128,768]{2,1,0:T(8,128)(2,1)S(1)}, bf16[2,128,768]{2,1,0:T(8,128)(2,1)S(1)}, u32[]{:S(2)}, u32[]{:S(2)}) collective-permute-start(bf16[2,128,768]{2,1,0:T(8,128)(2,1)S(1)} %get-tuple-element.73.refs_0_), channel_id=1, source_target_pairs={{0,4},{1,5},{2,6},{3,7},{4,8},{5,9},{6,10},{7,11},{8,12},{9,13},{1... | collective-permute-start | bytes 1179656 | tf_op jit(solution)/shard_map/ppermute | solution.py:16
  8.6 12.9 %collective-permute-start.2 = (bf16[2,128,768]{2,1,0:T(8,128)(2,1)S(1)}, bf16[2,128,768]{2,1,0:T(8,128)(2,1)S(1)}, u32[]{:S(2)}, u32[]{:S(2)}) collective-permute-start(bf16[2,128,768]{2,1,0:T(8,128)(2,1)S(1)} %get-tuple-element.73.refs_0_), channel_id=1, source_target_pairs={{4,0},{5,1},{6,2},{7,3},{8,4},{9,5},{10,6},{11,7},{12,8},{13,9},{1... | collective-permute-start | bytes 1179656 | tf_op jit(solution)/shard_map/ppermute | solution.py:16
  11.8 15.0 %collective-permute-start.12 = (bf16[2,128,1024]{2,1,0:T(8,128)(2,1)}, bf16[2,128,1024]{2,1,0:T(8,128)(2,1)S(1)}, u32[]{:S(2)}, u32[]{:S(2)}) collective-permute-start(bf16[2,128,1024]{2,1,0:T(8,128)(2,1)} %get-tuple-element.67.refs_0_), channel_id=1, source_target_pairs={{0,2},{1,3},{2,0},{3,1},{4,6},{5,7},{6,4},{7,5},{8,10},{9,11},{10,... | collective-permute-start | bytes 1572872 | tf_op jit(solution)/shard_map/ppermute | solution.py:16
  12.3 17.2 %collective-permute-start.13 = (bf16[2,128,1024]{2,1,0:T(8,128)(2,1)}, bf16[2,128,1024]{2,1,0:T(8,128)(2,1)}, u32[]{:S(2)}, u32[]{:S(2)}) collective-permute-start(bf16[2,128,1024]{2,1,0:T(8,128)(2,1)} %get-tuple-element.67.refs_0_), channel_id=1, source_target_pairs={{0,4},{1,5},{2,6},{3,7},{4,8},{5,9},{6,10},{7,11},{8,12},{9,13},{1... | collective-permute-start | bytes 1572872 | tf_op jit(solution)/shard_map/ppermute | solution.py:16
  18.2 10.1 %copy-start.25 = (s32[128]{0:T(128)}, s32[128]{0:T(128)S(1)}, u32[]{:S(2)}) copy-start(s32[128]{0:T(128)S(1)} %get-tuple-element.81) | copy-start | bytes 1540
  18.3 29.0 %copy-start = (bf16[2,128,768]{2,1,0:T(8,128)(2,1)}, bf16[2,128,768]{2,1,0:T(8,128)(2,1)S(1)}, u32[]{:S(2)}) copy-start(bf16[2,128,768]{2,1,0:T(8,128)(2,1)S(1)} %collective-permute-done.refs_1_) | copy-start | bytes 1179652
  18.3 17.0 %collective-permute-start.14 = (bf16[2,128,1024]{2,1,0:T(8,128)(2,1)}, bf16[2,128,1024]{2,1,0:T(8,128)(2,1)}, u32[]{:S(2)}, u32[]{:S(2)}) collective-permute-start(bf16[2,128,1024]{2,1,0:T(8,128)(2,1)} %get-tuple-element.67.refs_0_), channel_id=1, source_target_pairs={{4,0},{5,1},{6,2},{7,3},{8,4},{9,5},{10,6},{11,7},{12,8},{13,9},{1... | collective-permute-start | bytes 1572872 | tf_op jit(solution)/shard_map/ppermute | solution.py:16
  19.8 8.5 %copy-start.6 = (bf16[2,128,768]{2,1,0:T(8,128)(2,1)}, bf16[2,128,768]{2,1,0:T(8,128)(2,1)S(1)}, u32[]{:S(2)}) copy-start(bf16[2,128,768]{2,1,0:T(8,128)(2,1)S(1)} %get-tuple-element.75.refs_0_) | copy-start | bytes 1179652
  19.8 8.5 %copy-start.1 = (bf16[2,128,768]{2,1,0:T(8,128)(2,1)}, bf16[2,128,768]{2,1,0:T(8,128)(2,1)S(1)}, u32[]{:S(2)}) copy-start(bf16[2,128,768]{2,1,0:T(8,128)(2,1)S(1)} %collective-permute-done.1.refs_2_) | copy-start | bytes 1179652
  19.9 17.1 %collective-permute-start.6 = (bf16[2,128,768]{2,1,0:T(8,128)(2,1)S(1)}, bf16[2,128,768]{2,1,0:T(8,128)(2,1)}, u32[]{:S(2)}, u32[]{:S(2)}) collective-permute-start(bf16[2,128,768]{2,1,0:T(8,128)(2,1)S(1)} %get-tuple-element.75.refs_0_), channel_id=1, source_target_pairs={{0,2},{1,3},{2,0},{3,1},{4,6},{5,7},{6,4},{7,5},{8,10},{9,11},{10,... | collective-permute-start | bytes 1179656 | tf_op jit(solution)/shard_map/ppermute | solution.py:16
  21.4 6.9 %copy-start.2 = (bf16[2,128,768]{2,1,0:T(8,128)(2,1)}, bf16[2,128,768]{2,1,0:T(8,128)(2,1)S(1)}, u32[]{:S(2)}) copy-start(bf16[2,128,768]{2,1,0:T(8,128)(2,1)S(1)} %collective-permute-done.2.refs_3_) | copy-start | bytes 1179652
  21.4 15.5 %collective-permute-start.7 = (bf16[2,128,768]{2,1,0:T(8,128)(2,1)S(1)}, bf16[2,128,768]{2,1,0:T(8,128)(2,1)S(1)}, u32[]{:S(2)}, u32[]{:S(2)}) collective-permute-start(bf16[2,128,768]{2,1,0:T(8,128)(2,1)S(1)} %get-tuple-element.75.refs_0_), channel_id=1, source_target_pairs={{0,4},{1,5},{2,6},{3,7},{4,8},{5,9},{6,10},{7,11},{8,12},{9,13},{1... | collective-permute-start | bytes 1179656 | tf_op jit(solution)/shard_map/ppermute | solution.py:16
  26.8 47.2 %copy-start.8 = (bf16[2,128,1024]{2,1,0:T(8,128)(2,1)}, bf16[2,128,1024]{2,1,0:T(8,128)(2,1)S(1)}, u32[]{:S(2)}) copy-start(bf16[2,128,1024]{2,1,0:T(8,128)(2,1)S(1)} %collective-permute-done.12.refs_1_) | copy-start | bytes 1572868
  26.8 14.3 %collective-permute-start.8 = (bf16[2,128,768]{2,1,0:T(8,128)(2,1)S(1)}, bf16[2,128,768]{2,1,0:T(8,128)(2,1)S(1)}, u32[]{:S(2)}, u32[]{:S(2)}) collective-permute-start(bf16[2,128,768]{2,1,0:T(8,128)(2,1)S(1)} %get-tuple-element.75.refs_0_), channel_id=1, source_target_pairs={{4,0},{5,1},{6,2},{7,3},{8,4},{9,5},{10,6},{11,7},{12,8},{13,9},{1... | collective-permute-start | bytes 1179656 | tf_op jit(solution)/shard_map/ppermute | solution.py:16
  29.5 29.2 %collective-permute-start.3 = (bf16[4,2,128,768]{3,2,1,0:T(8,128)(2,1)S(1)}, bf16[4,2,128,768]{3,2,1,0:T(8,128)(2,1)}, u32[]{:S(2)}, u32[]{:S(2)}) collective-permute-start(bf16[4,2,128,768]{3,2,1,0:T(8,128)(2,1)S(1)} %pad_maximum_fusion.1), channel_id=1, source_target_pairs={{0,1},{1,0},{2,3},{3,2},{4,5},{5,4},{6,7},{7,6},{8,9},{9,8},{10,11... | collective-permute-start | bytes 4718600 | tf_op jit(solution)/shard_map/ppermute | solution.py:16
  36.8 48.3 %collective-permute-start.15 = (bf16[4,2,128,1024]{3,2,1,0:T(8,128)(2,1)S(1)}, bf16[4,2,128,1024]{3,2,1,0:T(8,128)(2,1)}, u32[]{:S(2)}, u32[]{:S(2)}) collective-permute-start(bf16[4,2,128,1024]{3,2,1,0:T(8,128)(2,1)S(1)} %pad_maximum_fusion), channel_id=1, source_target_pairs={{0,1},{1,0},{2,3},{3,2},{4,5},{5,4},{6,7},{7,6},{8,9},{9,8},{10,11... | collective-permute-start | bytes 6291464 | tf_op jit(solution)/shard_map/ppermute | solution.py:16
  37.0 6.7 %copy-start.3 = (bf16[2,128,768]{2,1,0:T(8,128)(2,1)}, bf16[2,128,768]{2,1,0:T(8,128)(2,1)S(1)}, u32[]{:S(2)}) copy-start(bf16[2,128,768]{2,1,0:T(8,128)(2,1)S(1)} %collective-permute-done.7.refs_2_) | copy-start | bytes 1179652
  41.1 6.9 %copy-start.26 = (s32[128]{0:T(128)S(1)}, s32[128]{0:T(128)}, u32[]{:S(2)}) copy-start(s32[128]{0:T(128)} %copy-done.25) | copy-start | bytes 1540
  41.1 6.9 %copy-start.31 = (s32[4]{0:T(128)S(1)}, s32[4]{0:T(128)}, u32[]{:S(2)}) copy-start(s32[4]{0:T(128)} %param.11) | copy-start | bytes 52
  41.1 16.1 %copy-start.28 = (s32[128]{0:T(128)S(1)}, s32[128]{0:T(128)}, u32[]{:S(2)}) copy-start(s32[128]{0:T(128)} %get-tuple-element.82) | copy-start | bytes 1540
  43.7 31.7 %collective-permute-start.9 = (bf16[4,2,128,768]{3,2,1,0:T(8,128)(2,1)}, bf16[4,2,128,768]{3,2,1,0:T(8,128)(2,1)}, u32[]{:S(2)}, u32[]{:S(2)}) collective-permute-start(bf16[4,2,128,768]{3,2,1,0:T(8,128)(2,1)} %pad_maximum_fusion.2), channel_id=1, source_target_pairs={{0,1},{1,0},{2,3},{3,2},{4,5},{5,4},{6,7},{7,6},{8,9},{9,8},{10,11... | collective-permute-start | bytes 4718600 | tf_op jit(solution)/shard_map/ppermute | solution.py:16
  43.7 8.1 %collective-permute-start.4 = (bf16[2,128,768]{2,1,0:T(8,128)(2,1)S(1)}, bf16[2,128,768]{2,1,0:T(8,128)(2,1)}, u32[]{:S(2)}, u32[]{:S(2)}) collective-permute-start(bf16[2,128,768]{2,1,0:T(8,128)(2,1)S(1)} %collective-permute-done.refs_1_), channel_id=1, source_target_pairs={{0,5},{3,6},{4,9},{7,10},{8,13},{11,14},{16,21},{19,22},{20,25},{2... | collective-permute-start | bytes 1179656 | tf_op jit(solution)/shard_map/ppermute | solution.py:16
  47.3 8.5 %collective-permute-start.5 = (bf16[2,128,768]{2,1,0:T(8,128)(2,1)S(1)}, bf16[2,128,768]{2,1,0:T(8,128)(2,1)S(1)}, u32[]{:S(2)}, u32[]{:S(2)}) collective-permute-start(bf16[2,128,768]{2,1,0:T(8,128)(2,1)S(1)} %collective-permute-done.refs_1_), channel_id=1, source_target_pairs={{4,1},{7,2},{8,5},{11,6},{12,9},{15,10},{20,17},{23,18},{24,21},{2... | collective-permute-start | bytes 1179656 | tf_op jit(solution)/shard_map/ppermute | solution.py:16
  51.8 17.0 %collective-permute-start.10 = (bf16[2,128,768]{2,1,0:T(8,128)(2,1)}, bf16[2,128,768]{2,1,0:T(8,128)(2,1)S(1)}, u32[]{:S(2)}, u32[]{:S(2)}) collective-permute-start(bf16[2,128,768]{2,1,0:T(8,128)(2,1)} %collective-permute-done.6.refs_1_), channel_id=1, source_target_pairs={{0,5},{3,6},{4,9},{7,10},{8,13},{11,14},{16,21},{19,22},{20,25},{2... | collective-permute-start | bytes 1179656 | tf_op jit(solution)/shard_map/ppermute | solution.py:16
  56.5 17.4 %collective-permute-start.11 = (bf16[2,128,768]{2,1,0:T(8,128)(2,1)}, bf16[2,128,768]{2,1,0:T(8,128)(2,1)S(1)}, u32[]{:S(2)}, u32[]{:S(2)}) collective-permute-start(bf16[2,128,768]{2,1,0:T(8,128)(2,1)} %collective-permute-done.6.refs_1_), channel_id=1, source_target_pairs={{4,1},{7,2},{8,5},{11,6},{12,9},{15,10},{20,17},{23,18},{24,21},{2... | collective-permute-start | bytes 1179656 | tf_op jit(solution)/shard_map/ppermute | solution.py:16
  68.2 40.5 %collective-permute-start.18 = (bf16[4,2,128,768]{3,2,1,0:T(8,128)(2,1)}, bf16[4,2,128,768]{3,2,1,0:T(8,128)(2,1)}, u32[]{:S(2)}, u32[]{:S(2)}) collective-permute-start(bf16[4,2,128,768]{3,2,1,0:T(8,128)(2,1)} %get-tuple-element.31), channel_id=1, source_target_pairs={{0,1},{1,0},{2,3},{3,2},{4,5},{5,4},{6,7},{7,6},{8,9},{9,8},{10,11... | collective-permute-start | bytes 4718600 | tf_op jit(solution)/shard_map/ppermute | solution.py:16
  68.8 6.6 %copy-start.19 = (bf16[2,128,768]{2,1,0:T(8,128)(2,1)}, bf16[2,128,768]{2,1,0:T(8,128)(2,1)S(1)}, u32[]{:S(2)}) copy-start(bf16[2,128,768]{2,1,0:T(8,128)(2,1)S(1)} %collective-permute-done.10.refs_5_) | copy-start | bytes 1179652
  68.9 16.2 %collective-permute-start.16 = (bf16[2,128,1024]{2,1,0:T(8,128)(2,1)S(1)}, bf16[2,128,1024]{2,1,0:T(8,128)(2,1)}, u32[]{:S(2)}, u32[]{:S(2)}) collective-permute-start(bf16[2,128,1024]{2,1,0:T(8,128)(2,1)S(1)} %collective-permute-done.12.refs_1_), channel_id=1, source_target_pairs={{0,5},{3,6},{4,9},{7,10},{8,13},{11,14},{16,21},{19,22},{20,25},{2... | collective-permute-start | bytes 1572872 | tf_op jit(solution)/shard_map/ppermute | solution.py:16
  74.0 11.1 %collective-permute-start.17 = (bf16[2,128,1024]{2,1,0:T(8,128)(2,1)S(1)}, bf16[2,128,1024]{2,1,0:T(8,128)(2,1)}, u32[]{:S(2)}, u32[]{:S(2)}) collective-permute-start(bf16[2,128,1024]{2,1,0:T(8,128)(2,1)S(1)} %collective-permute-done.12.refs_1_), channel_id=1, source_target_pairs={{4,1},{7,2},{8,5},{11,6},{12,9},{15,10},{20,17},{23,18},{24,21},{2... | collective-permute-start | bytes 1572872 | tf_op jit(solution)/shard_map/ppermute | solution.py:16
  85.0 23.8 %copy-start.17 = (bf16[2,128,768]{2,1,0:T(8,128)(2,1)S(1)}, bf16[2,128,768]{2,1,0:T(8,128)(2,1)}, u32[]{:S(2)}) copy-start(bf16[2,128,768]{2,1,0:T(8,128)(2,1)} %get-tuple-element.32) | copy-start | bytes 1179652
  85.0 23.8 %copy-start.18 = (bf16[2,128,768]{2,1,0:T(8,128)(2,1)S(1)}, bf16[2,128,768]{2,1,0:T(8,128)(2,1)}, u32[]{:S(2)}) copy-start(bf16[2,128,768]{2,1,0:T(8,128)(2,1)} %get-tuple-element.35) | copy-start | bytes 1179652
  85.0 37.8 %collective-permute-start.24 = (bf16[4,2,128,768]{3,2,1,0:T(8,128)(2,1)}, bf16[4,2,128,768]{3,2,1,0:T(8,128)(2,1)}, u32[]{:S(2)}, u32[]{:S(2)}) collective-permute-start(bf16[4,2,128,768]{3,2,1,0:T(8,128)(2,1)} %get-tuple-element.38), channel_id=1, source_target_pairs={{0,1},{1,0},{2,3},{3,2},{4,5},{5,4},{6,7},{7,6},{8,9},{9,8},{10,11... | collective-permute-start | bytes 4718600 | tf_op jit(solution)/shard_map/ppermute | solution.py:16
  97.0 39.5 %collective-permute-start.30 = (bf16[4,2,128,1024]{3,2,1,0:T(8,128)(2,1)}, bf16[4,2,128,1024]{3,2,1,0:T(8,128)(2,1)S(1)}, u32[]{:S(2)}, u32[]{:S(2)}) collective-permute-start(bf16[4,2,128,1024]{3,2,1,0:T(8,128)(2,1)} %get-tuple-element.45), channel_id=1, source_target_pairs={{0,1},{1,0},{2,3},{3,2},{4,5},{5,4},{6,7},{7,6},{8,9},{9,8},{10,11... | collective-permute-start | bytes 6291464 | tf_op jit(solution)/shard_map/ppermute | solution.py:16
  97.5 9.3 %collective-permute-start.19 = (bf16[2,128,768]{2,1,0:T(8,128)(2,1)}, bf16[2,128,768]{2,1,0:T(8,128)(2,1)S(1)}, u32[]{:S(2)}, u32[]{:S(2)}) collective-permute-start(bf16[2,128,768]{2,1,0:T(8,128)(2,1)} %get-tuple-element.33), channel_id=1, source_target_pairs={{5,0},{6,3},{9,4},{10,7},{13,8},{14,11},{21,16},{22,19},{25,20},{2... | collective-permute-start | bytes 1179656 | tf_op jit(solution)/shard_map/ppermute | solution.py:16
  98.8 9.3 %collective-permute-start.20 = (bf16[2,128,768]{2,1,0:T(8,128)(2,1)}, bf16[2,128,768]{2,1,0:T(8,128)(2,1)S(1)}, u32[]{:S(2)}, u32[]{:S(2)}) collective-permute-start(bf16[2,128,768]{2,1,0:T(8,128)(2,1)} %get-tuple-element.34), channel_id=1, source_target_pairs={{1,4},{2,7},{5,8},{6,11},{9,12},{10,15},{17,20},{18,23},{21,24},{2... | collective-permute-start | bytes 1179656 | tf_op jit(solution)/shard_map/ppermute | solution.py:16
  106.8 9.3 %collective-permute-start.25 = (bf16[2,128,768]{2,1,0:T(8,128)(2,1)}, bf16[2,128,768]{2,1,0:T(8,128)(2,1)S(1)}, u32[]{:S(2)}, u32[]{:S(2)}) collective-permute-start(bf16[2,128,768]{2,1,0:T(8,128)(2,1)} %get-tuple-element.40), channel_id=1, source_target_pairs={{5,0},{6,3},{9,4},{10,7},{13,8},{14,11},{21,16},{22,19},{25,20},{2... | collective-permute-start | bytes 1179656 | tf_op jit(solution)/shard_map/ppermute | solution.py:16
  108.1 9.3 %collective-permute-start.26 = (bf16[2,128,768]{2,1,0:T(8,128)(2,1)}, bf16[2,128,768]{2,1,0:T(8,128)(2,1)S(1)}, u32[]{:S(2)}, u32[]{:S(2)}) collective-permute-start(bf16[2,128,768]{2,1,0:T(8,128)(2,1)} %get-tuple-element.41), channel_id=1, source_target_pairs={{1,4},{2,7},{5,8},{6,11},{9,12},{10,15},{17,20},{18,23},{21,24},{2... | collective-permute-start | bytes 1179656 | tf_op jit(solution)/shard_map/ppermute | solution.py:16
  108.8 13.2 %copy-start.22 = (bf16[128,1024]{1,0:T(8,128)(2,1)S(1)}, bf16[128,1024]{1,0:T(8,128)(2,1)}, u32[]{:S(2)}) copy-start(bf16[128,1024]{1,0:T(8,128)(2,1)} %get-tuple-element.29) | copy-start | bytes 786436
  108.8 13.2 %copy-start.23 = (bf16[128,768]{1,0:T(8,128)(2,1)S(1)}, bf16[128,768]{1,0:T(8,128)(2,1)}, u32[]{:S(2)}) copy-start(bf16[128,768]{1,0:T(8,128)(2,1)} %get-tuple-element.27) | copy-start | bytes 589828
  108.8 13.2 %copy-start.24 = (bf16[128,768]{1,0:T(8,128)(2,1)S(1)}, bf16[128,768]{1,0:T(8,128)(2,1)}, u32[]{:S(2)}) copy-start(bf16[128,768]{1,0:T(8,128)(2,1)} %get-tuple-element.28) | copy-start | bytes 589828
  108.8 14.0 %copy-start.30 = (bf16[2,128,1024]{2,1,0:T(8,128)(2,1)S(1)}, bf16[2,128,1024]{2,1,0:T(8,128)(2,1)}, u32[]{:S(2)}) copy-start(bf16[2,128,1024]{2,1,0:T(8,128)(2,1)} %get-tuple-element.47) | copy-start | bytes 1572868
  108.8 15.3 %copy-start.29 = (bf16[2,128,1024]{2,1,0:T(8,128)(2,1)S(1)}, bf16[2,128,1024]{2,1,0:T(8,128)(2,1)}, u32[]{:S(2)}) copy-start(bf16[2,128,1024]{2,1,0:T(8,128)(2,1)} %get-tuple-element.48) | copy-start | bytes 1572868
  110.7 14.3 %copy-start.14 = (bf16[2,128,768]{2,1,0:T(8,128)(2,1)S(1)}, bf16[2,128,768]{2,1,0:T(8,128)(2,1)}, u32[]{:S(2)}) copy-start(bf16[2,128,768]{2,1,0:T(8,128)(2,1)} %get-tuple-element.39) | copy-start | bytes 1179652
  110.7 14.3 %copy-start.15 = (bf16[2,128,768]{2,1,0:T(8,128)(2,1)S(1)}, bf16[2,128,768]{2,1,0:T(8,128)(2,1)}, u32[]{:S(2)}) copy-start(bf16[2,128,768]{2,1,0:T(8,128)(2,1)} %get-tuple-element.42) | copy-start | bytes 1179652
  110.7 14.3 %copy-start.16 = (bf16[2,128,768]{2,1,0:T(8,128)(2,1)S(1)}, bf16[2,128,768]{2,1,0:T(8,128)(2,1)}, u32[]{:S(2)}) copy-start(bf16[2,128,768]{2,1,0:T(8,128)(2,1)} %get-tuple-element.43) | copy-start | bytes 1179652
  110.8 13.4 %collective-permute-start.21 = (bf16[2,128,768]{2,1,0:T(8,128)(2,1)S(1)}, bf16[2,128,768]{2,1,0:T(8,128)(2,1)S(1)}, u32[]{:S(2)}, u32[]{:S(2)}) collective-permute-start(bf16[2,128,768]{2,1,0:T(8,128)(2,1)S(1)} %get-tuple-element.54), channel_id=1, source_target_pairs={{0,2},{1,3},{2,0},{3,1},{4,6},{5,7},{6,4},{7,5},{8,10},{9,11},{10,... | collective-permute-start | bytes 1179656 | tf_op jit(solution)/shard_map/ppermute | solution.py:16
  116.1 10.9 %collective-permute-start.22 = (bf16[2,128,768]{2,1,0:T(8,128)(2,1)S(1)}, bf16[2,128,768]{2,1,0:T(8,128)(2,1)S(1)}, u32[]{:S(2)}, u32[]{:S(2)}) collective-permute-start(bf16[2,128,768]{2,1,0:T(8,128)(2,1)S(1)} %get-tuple-element.56), channel_id=1, source_target_pairs={{4,0},{5,1},{6,2},{7,3},{8,4},{9,5},{10,6},{11,7},{12,8},{13,9},{1... | collective-permute-start | bytes 1179656 | tf_op jit(solution)/shard_map/ppermute | solution.py:16
  117.4 11.9 %collective-permute-start.23 = (bf16[2,128,768]{2,1,0:T(8,128)(2,1)S(1)}, bf16[2,128,768]{2,1,0:T(8,128)(2,1)S(1)}, u32[]{:S(2)}, u32[]{:S(2)}) collective-permute-start(bf16[2,128,768]{2,1,0:T(8,128)(2,1)S(1)} %get-tuple-element.55), channel_id=1, source_target_pairs={{0,4},{1,5},{2,6},{3,7},{4,8},{5,9},{6,10},{7,11},{8,12},{9,13},{1... | collective-permute-start | bytes 1179656 | tf_op jit(solution)/shard_map/ppermute | solution.py:16
  122.9 10.5 %collective-permute-start.31 = (bf16[2,128,1024]{2,1,0:T(8,128)(2,1)S(1)}, bf16[2,128,1024]{2,1,0:T(8,128)(2,1)S(1)}, u32[]{:S(2)}, u32[]{:S(2)}) collective-permute-start(bf16[2,128,1024]{2,1,0:T(8,128)(2,1)S(1)} %copy-done.30), channel_id=1, source_target_pairs={{5,0},{6,3},{9,4},{10,7},{13,8},{14,11},{21,16},{22,19},{25,20},{2... | collective-permute-start | bytes 1572872 | tf_op jit(solution)/shard_map/ppermute | solution.py:16
  124.2 12.3 %collective-permute-start.32 = (bf16[2,128,1024]{2,1,0:T(8,128)(2,1)S(1)}, bf16[2,128,1024]{2,1,0:T(8,128)(2,1)S(1)}, u32[]{:S(2)}, u32[]{:S(2)}) collective-permute-start(bf16[2,128,1024]{2,1,0:T(8,128)(2,1)S(1)} %copy-done.29), channel_id=1, source_target_pairs={{1,4},{2,7},{5,8},{6,11},{9,12},{10,15},{17,20},{18,23},{21,24},{2... | collective-permute-start | bytes 1572872 | tf_op jit(solution)/shard_map/ppermute | solution.py:16
  126.8 9.6 %copy-start.9 = (bf16[2,128,1024]{2,1,0:T(8,128)(2,1)S(1)}, bf16[2,128,1024]{2,1,0:T(8,128)(2,1)}, u32[]{:S(2)}) copy-start(bf16[2,128,1024]{2,1,0:T(8,128)(2,1)} %get-tuple-element.46) | copy-start | bytes 1572868
  126.8 9.6 %copy-start.10 = (bf16[2,128,1024]{2,1,0:T(8,128)(2,1)S(1)}, bf16[2,128,1024]{2,1,0:T(8,128)(2,1)}, u32[]{:S(2)}) copy-start(bf16[2,128,1024]{2,1,0:T(8,128)(2,1)} %get-tuple-element.49) | copy-start | bytes 1572868
  126.8 9.6 %copy-start.11 = (bf16[2,128,1024]{2,1,0:T(8,128)(2,1)S(1)}, bf16[2,128,1024]{2,1,0:T(8,128)(2,1)}, u32[]{:S(2)}) copy-start(bf16[2,128,1024]{2,1,0:T(8,128)(2,1)} %get-tuple-element.50) | copy-start | bytes 1572868
  127.0 12.8 %collective-permute-start.27 = (bf16[2,128,768]{2,1,0:T(8,128)(2,1)S(1)}, bf16[2,128,768]{2,1,0:T(8,128)(2,1)S(1)}, u32[]{:S(2)}, u32[]{:S(2)}) collective-permute-start(bf16[2,128,768]{2,1,0:T(8,128)(2,1)S(1)} %get-tuple-element.57), channel_id=1, source_target_pairs={{0,2},{1,3},{2,0},{3,1},{4,6},{5,7},{6,4},{7,5},{8,10},{9,11},{10,... | collective-permute-start | bytes 1179656 | tf_op jit(solution)/shard_map/ppermute | solution.py:16
  129.3 15.6 %collective-permute-start.28 = (bf16[2,128,768]{2,1,0:T(8,128)(2,1)S(1)}, bf16[2,128,768]{2,1,0:T(8,128)(2,1)S(1)}, u32[]{:S(2)}, u32[]{:S(2)}) collective-permute-start(bf16[2,128,768]{2,1,0:T(8,128)(2,1)S(1)} %get-tuple-element.59), channel_id=1, source_target_pairs={{4,0},{5,1},{6,2},{7,3},{8,4},{9,5},{10,6},{11,7},{12,8},{13,9},{1... | collective-permute-start | bytes 1179656 | tf_op jit(solution)/shard_map/ppermute | solution.py:16
  133.3 11.6 %collective-permute-start.29 = (bf16[2,128,768]{2,1,0:T(8,128)(2,1)S(1)}, bf16[2,128,768]{2,1,0:T(8,128)(2,1)S(1)}, u32[]{:S(2)}, u32[]{:S(2)}) collective-permute-start(bf16[2,128,768]{2,1,0:T(8,128)(2,1)S(1)} %get-tuple-element.58), channel_id=1, source_target_pairs={{0,4},{1,5},{2,6},{3,7},{4,8},{5,9},{6,10},{7,11},{8,12},{9,13},{1... | collective-permute-start | bytes 1179656 | tf_op jit(solution)/shard_map/ppermute | solution.py:16
  136.5 8.4 %copy-start.12 = (bf16[2,128,768]{2,1,0:T(8,128)(2,1)S(1)}, bf16[2,128,768]{2,1,0:T(8,128)(2,1)}, u32[]{:S(2)}) copy-start(bf16[2,128,768]{2,1,0:T(8,128)(2,1)} %get-tuple-element.37) | copy-start | bytes 1179652
  137.5 14.8 %collective-permute-start.33 = (bf16[2,128,1024]{2,1,0:T(8,128)(2,1)S(1)}, bf16[2,128,1024]{2,1,0:T(8,128)(2,1)S(1)}, u32[]{:S(2)}, u32[]{:S(2)}) collective-permute-start(bf16[2,128,1024]{2,1,0:T(8,128)(2,1)S(1)} %get-tuple-element.51), channel_id=1, source_target_pairs={{0,2},{1,3},{2,0},{3,1},{4,6},{5,7},{6,4},{7,5},{8,10},{9,11},{10,... | collective-permute-start | bytes 1572872 | tf_op jit(solution)/shard_map/ppermute | solution.py:16
  138.5 17.1 %collective-permute-start.34 = (bf16[2,128,1024]{2,1,0:T(8,128)(2,1)S(1)}, bf16[2,128,1024]{2,1,0:T(8,128)(2,1)S(1)}, u32[]{:S(2)}, u32[]{:S(2)}) collective-permute-start(bf16[2,128,1024]{2,1,0:T(8,128)(2,1)S(1)} %get-tuple-element.53), channel_id=1, source_target_pairs={{4,0},{5,1},{6,2},{7,3},{8,4},{9,5},{10,6},{11,7},{12,8},{13,9},{1... | collective-permute-start | bytes 1572872 | tf_op jit(solution)/shard_map/ppermute | solution.py:16
  139.8 17.1 %collective-permute-start.35 = (bf16[2,128,1024]{2,1,0:T(8,128)(2,1)S(1)}, bf16[2,128,1024]{2,1,0:T(8,128)(2,1)S(1)}, u32[]{:S(2)}, u32[]{:S(2)}) collective-permute-start(bf16[2,128,1024]{2,1,0:T(8,128)(2,1)S(1)} %get-tuple-element.52), channel_id=1, source_target_pairs={{0,4},{1,5},{2,6},{3,7},{4,8},{5,9},{6,10},{7,11},{8,12},{9,13},{1... | collective-permute-start | bytes 1572872 | tf_op jit(solution)/shard_map/ppermute | solution.py:16
  144.9 12.0 %copy-start.7 = (bf16[2,128,1024]{2,1,0:T(8,128)(2,1)S(1)}, bf16[2,128,1024]{2,1,0:T(8,128)(2,1)}, u32[]{:S(2)}) copy-start(bf16[2,128,1024]{2,1,0:T(8,128)(2,1)} %get-tuple-element.44) | copy-start | bytes 1572868
  (4 other events, 10.3 us)

commit v17 on v12

--- a/solution.py
+++ b/solution.py
@@ -152,17 +152,14 @@
 def forward_second(first, count, after):
     core, cross, down, up, diag_up, diag_down, back = route(count)
     own, from_cross, from_below, from_above = first
-    ahead = jnp.stack([own, from_cross, from_below, from_above])
-    if after is not None:
-        (ahead, from_cross), _ = lax.optimization_barrier(((ahead, from_cross), after))
-    relayed = send(ahead, core)
+    relayed = [send(block, core) for block in first]
     diag_from_below = send(from_cross, diag_up)
     diag_from_above = send(from_cross, diag_down)
-    return first + [relayed, diag_from_below, diag_from_above]
+    return first + relayed + [diag_from_below, diag_from_above]
 
 
 def chunk_kernel(forward_mask, queries, out_grad, inputs, head_offset, inv_root):
-    slot_in = [(0, ()), (4, (0,)), (1, ()), (2, ()), (3, ()), (4, (1,)), (4, (2,)), (4, (3,)), (5, ()), (6, ())]
+    slot_in = [(0, ()), (4, ()), (1, ()), (2, ()), (3, ()), (5, ()), (6, ()), (7, ()), (8, ()), (9, ())]
     out_lead = [(), (4,), (), (), (), (), ()]
     slot_out = [(0, ()), (1, (0,)), (2, ()), (3, ()), (4, ()), (1, (1,)), (1, (2,)), (1, (3,)), (5, ()), (6, ())]
     return attention_backward(

time: 144 us -> 137 us (0.951)
  other arithmetic: 15.5 us -> 7.77 us
  starting transfers between devices: 42.9 us -> 50 us
  waiting for transfers between devices: 51.9 us -> 45.5 us
    ppermute x24 -> x30, starting transfers between devices: 42.9 us -> 50 us  [send(): return lax.ppermute(value, 'tm', pairs)]
    ppermute x24 -> x30, waiting for transfers between devices: 51.9 us -> 45.5 us  [send(): return lax.ppermute(value, 'tm', pairs)]
    another operation x6 -> x4, other arithmetic: 7.12 us -> 0.97 us  [the longest x4 5.2 us: forward_second(): ahead = jnp.stack([own, from_cross, from_below, from_above])]
    convert_element_type x2, other arithmetic: 3.01 us -> 1.4 us  [return_second(): cross_sum.astype(jnp.bfloat16)]
  transfers between devices with their start and end apart: 24 -> 30, of which waited for: 14 -> 11; matrix products, arithmetic and copies ran while one was open for 9% -> 4% of each run, Pallas kernels for 20% -> 21%
where the time goes in v17:
time: 137 us; the launch traced here: 136 us
  starting transfers between devices  50 us (36%)
  waiting for transfers between devices  45.5 us (33%)
  Pallas kernels  28.2 us (21%)
  other arithmetic  7.77 us (6%)
  local copies, waits for them, and re-layouts  3.2 us (2%)
    ppermute x30, starting transfers between devices, send(): return lax.ppermute(value, 'tm', pairs)  50 us
    ppermute x30, waiting for transfers between devices, send(): return lax.ppermute(value, 'tm', pairs)  45.5 us
    pallas_call x2, Pallas kernels, attention_backward(): pl.pallas_call(kernel, grid=(heads // STEP_HEADS,), in_specs=in_specs, ou...  28.2 us
  transfers between devices with their start and end apart: 30, of which 11 were waited for; matrix products, arithmetic and copies ran while one was open for 4% of the time, Pallas kernels for 21%

profile of v17, /device:TPU:0, one launch (start us, length us, event | category | flops | bytes accessed | tf_op | source)
XLA Modules:
  0.0 135.8 jit_solution(12819675097636018094)
XLA Ops:
  0.6 1.4 slice_bitcast_fusion.14
  2.0 0.0 copy-start.10
  2.0 0.0 copy-start.18
  2.0 0.1 pad_maximum_fusion.refs_0_
  2.1 3.1 %collective-permute-start = (bf16[2,128,1280]{2,1,0:T(8,128)(2,1)S(1)}, bf16[2,128,1280]{2,1,0:T(8,128)(2,1)S(1)}, u32[]{:S(2)}, u32[]{:S(2)}) collective-permute-start(bf16[2,128,1280]{2,1,0:T(8,128)(2,1)S(1)} %pad_maximum_fusion.refs_0_), channel_id=1, source_target_pairs={{0,2},{1,3},{2,0},{3,1},{4,6},{5,7},{6,4},{7,5},{8,10},{9,11},{10,... | collective-permute-start | bytes 1966088 | tf_op jit(solution)/shard_map/ppermute | solution.py:16
  5.2 4.3 %collective-permute-start.1 = (bf16[2,128,1280]{2,1,0:T(8,128)(2,1)S(1)}, bf16[2,128,1280]{2,1,0:T(8,128)(2,1)}, u32[]{:S(2)}, u32[]{:S(2)}) collective-permute-start(bf16[2,128,1280]{2,1,0:T(8,128)(2,1)S(1)} %pad_maximum_fusion.refs_0_), channel_id=1, source_target_pairs={{0,4},{1,5},{2,6},{3,7},{4,8},{5,9},{6,10},{7,11},{8,12},{9,13},{1... | collective-permute-start | bytes 1966088 | tf_op jit(solution)/shard_map/ppermute | solution.py:16
  9.5 1.3 collective-permute-start.2
  10.8 0.1 collective-permute-start.3
  10.8 0.1 pad_maximum_fusion.1.refs_0_
  10.9 0.0 copy-start.6
  10.9 0.6 collective-permute-start.9
  11.5 0.1 copy.9
  11.8 0.1 select_reduce_fusion
  11.9 8.9 %collective-permute-done.refs_1_ = bf16[2,128,1280]{2,1,0:T(8,128)(2,1)S(1)} collective-permute-done((bf16[2,128,1280]{2,1,0:T(8,128)(2,1)S(1)}, bf16[2,128,1280]{2,1,0:T(8,128)(2,1)S(1)}, u32[]{:S(2)}, u32[]{:S(2)}) %collective-permute-start) | collective-permute-done | bytes 655392 | tf_op jit(solution)/shard_map/ppermute | solution.py:16
  20.7 4.8 %collective-permute-start.10 = (bf16[2,128,1280]{2,1,0:T(8,128)(2,1)S(1)}, bf16[2,128,1280]{2,1,0:T(8,128)(2,1)}, u32[]{:S(2)}, u32[]{:S(2)}) collective-permute-start(bf16[2,128,1280]{2,1,0:T(8,128)(2,1)S(1)} %pad_maximum_fusion.1.refs_0_), channel_id=1, source_target_pairs={{0,4},{1,5},{2,6},{3,7},{4,8},{5,9},{6,10},{7,11},{8,12},{9,13},{1... | collective-permute-start | bytes 1966088 | tf_op jit(solution)/shard_map/ppermute | solution.py:16
  25.6 1.3 collective-permute-start.11
  26.9 0.5 collective-permute-done.2.refs_3_
  27.4 0.0 collective-permute-start.12
  27.4 0.1 multiply_reduce_fusion
  27.5 0.0 collective-permute-done.3.refs_4_
  27.5 0.6 collective-permute-start.4
  28.1 5.9 %collective-permute-done.9.refs_1_ = bf16[2,128,1280]{2,1,0:T(8,128)(2,1)S(1)} collective-permute-done((bf16[2,128,1280]{2,1,0:T(8,128)(2,1)S(1)}, bf16[2,128,1280]{2,1,0:T(8,128)(2,1)S(1)}, u32[]{:S(2)}, u32[]{:S(2)}) %collective-permute-start.9) | collective-permute-done | bytes 655392 | tf_op jit(solution)/shard_map/ppermute | solution.py:16
  33.9 2.4 %collective-permute-start.7 = (bf16[2,128,1280]{2,1,0:T(8,128)(2,1)S(1)}, bf16[2,128,1280]{2,1,0:T(8,128)(2,1)S(1)}, u32[]{:S(2)}, u32[]{:S(2)}) collective-permute-start(bf16[2,128,1280]{2,1,0:T(8,128)(2,1)S(1)} %collective-permute-done.refs_1_), channel_id=1, source_target_pairs={{0,5},{3,6},{4,9},{7,10},{8,13},{11,14},{16,21},{19,22},{20,25},{2... | collective-permute-start | bytes 1966088 | tf_op jit(solution)/shard_map/ppermute | solution.py:16
  36.4 0.4 collective-permute-done.10.refs_2_
  36.8 0.7 collective-permute-start.8
  37.5 4.4 %collective-permute-done.11.refs_3_ = bf16[2,128,1280]{2,1,0:T(8,128)(2,1)} collective-permute-done((bf16[2,128,1280]{2,1,0:T(8,128)(2,1)S(1)}, bf16[2,128,1280]{2,1,0:T(8,128)(2,1)}, u32[]{:S(2)}, u32[]{:S(2)}) %collective-permute-start.11) | collective-permute-done | bytes 655392 | tf_op jit(solution)/shard_map/ppermute | solution.py:16
  41.9 0.5 collective-permute-start.6
  42.4 0.0 collective-permute-done.4.refs_5_
  42.4 0.4 copy-done.13
  42.8 0.5 collective-permute-start.13
  43.3 0.3 copy-done.14
  43.7 1.4 %fusion.24.mask_ref = s32[128,1280]{1,0:T(8,128)} fusion(s32[128]{0:T(128)S(1)} %select_reduce_fusion, s32[1280]{0:T(1024)S(1)} %get-tuple-element.50, s32[128]{0:T(128)S(1)} %get-tuple-element.55, s32[128]{0:T(128)S(1)} %get-tuple-element.52, s32[128]{0:T(128)S(1)} %get-tuple-element.53, s32[128]{0:T(128)S(1)} %get-tuple-element.51, ...), kind=kLoop, calls=%fused_computation.49 | loop fusion | flops 2949120 | bytes 670080 | tf_op jit(solution)/shard_map/convert_element_type | solution.py:228
  45.1 0.0 collective-permute-done.7.refs_8_
  45.1 4.0 %collective-permute-start.16 = (bf16[2,128,1280]{2,1,0:T(8,128)(2,1)S(1)}, bf16[2,128,1280]{2,1,0:T(8,128)(2,1)}, u32[]{:S(2)}, u32[]{:S(2)}) collective-permute-start(bf16[2,128,1280]{2,1,0:T(8,128)(2,1)S(1)} %collective-permute-done.9.refs_1_), channel_id=1, source_target_pairs={{0,5},{3,6},{4,9},{7,10},{8,13},{11,14},{16,21},{19,22},{20,25},{2... | collective-permute-start | bytes 1966088 | tf_op jit(solution)/shard_map/ppermute | solution.py:16
  49.1 1.5 %collective-permute-start.17 = (bf16[2,128,1280]{2,1,0:T(8,128)(2,1)S(1)}, bf16[2,128,1280]{2,1,0:T(8,128)(2,1)}, u32[]{:S(2)}, u32[]{:S(2)}) collective-permute-start(bf16[2,128,1280]{2,1,0:T(8,128)(2,1)S(1)} %collective-permute-done.9.refs_1_), channel_id=1, source_target_pairs={{4,1},{7,2},{8,5},{11,6},{12,9},{15,10},{20,17},{23,18},{24,21},{2... | collective-permute-start | bytes 1966088 | tf_op jit(solution)/shard_map/ppermute | solution.py:16
  50.6 0.8 copy-done.17
  51.4 0.5 collective-permute-start.15
  51.9 14.0 %shard_map.85 = (bf16[128,1280]{1,0:T(8,128)(2,1)}, bf16[2,128,1280]{2,1,0:T(8,128)(2,1)}, bf16[4,2,128,1280]{3,2,1,0:T(8,128)(2,1)}, bf16[2,128,1280]{2,1,0:T(8...) custom-call(s32[128,1280]{1,0:T(8,128)} %fusion.24.mask_ref, ...), custom_call_target="tpu_custom_call" | custom-call | flops 2516582400 | bytes 14745600 | tf_op jit(solution)/shard_map/pallas_call | solution.py:127
  66.0 0.1 collective-permute-start.18
  66.1 14.2 %shard_map.86 = (bf16[128,1280]{1,0:T(8,128)(2,1)}, bf16[2,128,1280]{2,1,0:T(8,128)(2,1)}, bf16[4,2,128,1280]{3,2,1,0:T(8,128)(2,1)}, bf16[2,128,1280]{2,1,0:T(8...) custom-call(s32[128,1280]{1,0:T(8,128)} %fusion.24.mask_ref, ...), custom_call_target="tpu_custom_call" | custom-call | flops 2516582400 | bytes 14745600 | tf_op jit(solution)/shard_map/pallas_call | solution.py:127
  80.3 0.5 collective-permute-start.24
  80.9 1.3 collective-permute-start.19
  82.2 0.7 collective-permute-start.20
  82.9 1.3 collective-permute-start.25
  84.2 2.0 %pad_maximum_fusion.2 = bf16[128,2560]{1,0:T(8,128)(2,1)} fusion(bf16[128,1280]{1,0:T(8,128)(2,1)} %get-tuple-element.20, bf16[128,1280]{1,0:T(8,128)(2,1)} %get-tuple-element.19), kind=kLoop, calls=%fused_computation.44 | loop fusion | flops 1310720 | bytes 1310720 | tf_op jit(solution)/shard_map/concatenate | solution.py:250
  86.1 7.2 %collective-permute-done.19 = bf16[2,128,1280]{2,1,0:T(8,128)(2,1)S(1)} collective-permute-done((bf16[2,128,1280]{2,1,0:T(8,128)(2,1)}, bf16[2,128,1280]{2,1,0:T(8,128)(2,1)S(1)}, u32[]{:S(2)}, u32[]{:S(2)}) %collective-permute-start.19) | collective-permute-done | bytes 655392 | tf_op jit(solution)/shard_map/ppermute | solution.py:16
  93.3 0.7 collective-permute-start.26
  94.1 0.7 fusion.13
  94.8 5.8 %collective-permute-start.21 = (bf16[2,128,1280]{2,1,0:T(8,128)(2,1)S(1)}, bf16[2,128,1280]{2,1,0:T(8,128)(2,1)S(1)}, u32[]{:S(2)}, u32[]{:S(2)}) collective-permute-start(bf16[2,128,1280]{2,1,0:T(8,128)(2,1)S(1)} %get-tuple-element.35), channel_id=1, source_target_pairs={{0,2},{1,3},{2,0},{3,1},{4,6},{5,7},{6,4},{7,5},{8,10},{9,11},{10,... | collective-permute-start | bytes 1966088 | tf_op jit(solution)/shard_map/ppermute | solution.py:16
  100.5 1.3 collective-permute-start.22
  101.8 4.6 %collective-permute-start.23 = (bf16[2,128,1280]{2,1,0:T(8,128)(2,1)S(1)}, bf16[2,128,1280]{2,1,0:T(8,128)(2,1)S(1)}, u32[]{:S(2)}, u32[]{:S(2)}) collective-permute-start(bf16[2,128,1280]{2,1,0:T(8,128)(2,1)S(1)} %get-tuple-element.36), channel_id=1, source_target_pairs={{0,4},{1,5},{2,6},{3,7},{4,8},{5,9},{6,10},{7,11},{8,12},{9,13},{1... | collective-permute-start | bytes 1966088 | tf_op jit(solution)/shard_map/ppermute | solution.py:16
  106.5 0.7 fusion.4
  107.2 2.4 %collective-permute-start.27 = (bf16[2,128,1280]{2,1,0:T(8,128)(2,1)S(1)}, bf16[2,128,1280]{2,1,0:T(8,128)(2,1)S(1)}, u32[]{:S(2)}, u32[]{:S(2)}) collective-permute-start(bf16[2,128,1280]{2,1,0:T(8,128)(2,1)S(1)} %get-tuple-element.38), channel_id=1, source_target_pairs={{0,2},{1,3},{2,0},{3,1},{4,6},{5,7},{6,4},{7,5},{8,10},{9,11},{10,... | collective-permute-start | bytes 1966088 | tf_op jit(solution)/shard_map/ppermute | solution.py:16
  109.6 1.3 collective-permute-start.28
  110.9 5.2 %collective-permute-done.21 = bf16[2,128,1280]{2,1,0:T(8,128)(2,1)S(1)} collective-permute-done((bf16[2,128,1280]{2,1,0:T(8,128)(2,1)S(1)}, bf16[2,128,1280]{2,1,0:T(8,128)(2,1)S(1)}, u32[]{:S(2)}, u32[]{:S(2)}) %collective-permute-start.21) | collective-permute-done | bytes 655392 | tf_op jit(solution)/shard_map/ppermute | solution.py:16
  116.1 3.9 %collective-permute-start.29 = (bf16[2,128,1280]{2,1,0:T(8,128)(2,1)S(1)}, bf16[2,128,1280]{2,1,0:T(8,128)(2,1)S(1)}, u32[]{:S(2)}, u32[]{:S(2)}) collective-permute-start(bf16[2,128,1280]{2,1,0:T(8,128)(2,1)S(1)} %get-tuple-element.39), channel_id=1, source_target_pairs={{0,4},{1,5},{2,6},{3,7},{4,8},{5,9},{6,10},{7,11},{8,12},{9,13},{1... | collective-permute-start | bytes 1966088 | tf_op jit(solution)/shard_map/ppermute | solution.py:16
  120.1 1.1 collective-permute-done.23
  121.1 0.4 fusion.17
  121.6 7.8 %collective-permute-done.27 = bf16[2,128,1280]{2,1,0:T(8,128)(2,1)S(1)} collective-permute-done((bf16[2,128,1280]{2,1,0:T(8,128)(2,1)S(1)}, bf16[2,128,1280]{2,1,0:T(8,128)(2,1)S(1)}, u32[]{:S(2)}, u32[]{:S(2)}) %collective-permute-start.27) | collective-permute-done | bytes 655392 | tf_op jit(solution)/shard_map/ppermute | solution.py:16
  129.5 1.9 %collective-permute-done.28 = bf16[2,128,1280]{2,1,0:T(8,128)(2,1)S(1)} collective-permute-done((bf16[2,128,1280]{2,1,0:T(8,128)(2,1)S(1)}, bf16[2,128,1280]{2,1,0:T(8,128)(2,1)S(1)}, u32[]{:S(2)}, u32[]{:S(2)}) %collective-permute-start.28) | collective-permute-done | bytes 655392 | tf_op jit(solution)/shard_map/ppermute | solution.py:16
  131.4 2.2 %collective-permute-done.29 = bf16[2,128,1280]{2,1,0:T(8,128)(2,1)S(1)} collective-permute-done((bf16[2,128,1280]{2,1,0:T(8,128)(2,1)S(1)}, bf16[2,128,1280]{2,1,0:T(8,128)(2,1)S(1)}, u32[]{:S(2)}, u32[]{:S(2)}) %collective-permute-start.29) | collective-permute-done | bytes 655392 | tf_op jit(solution)/shard_map/ppermute | solution.py:16
  133.6 0.4 fusion.8
  134.1 0.9 pad_maximum_fusion.4
  134.9 0.9 pad_maximum_fusion.3
  (69 shorter events, 0.3 us)
Async XLA Ops:
  2.0 9.5 %copy-start.10 = (s32[4,3]{1,0:T(4,128)S(1)}, s32[4,3]{1,0:T(4,128)}, u32[]{:S(2)}) copy-start(s32[4,3]{1,0:T(4,128)} %param.10) | copy-start | bytes 148
  2.0 9.8 %copy-start.18 = (s32[4]{0:T(128)S(1)}, s32[4]{0:T(128)}, u32[]{:S(2)}) copy-start(s32[4]{0:T(128)} %param.11) | copy-start | bytes 52
  2.1 49.8 %copy-start.7 = (bf16[2,128,1280]{2,1,0:T(8,128)(2,1)}, bf16[2,128,1280]{2,1,0:T(8,128)(2,1)S(1)}, u32[]{:S(2)}) copy-start(bf16[2,128,1280]{2,1,0:T(8,128)(2,1)S(1)} %pad_maximum_fusion.refs_0_) | copy-start | bytes 1966084
  2.1 18.6 %collective-permute-start = (bf16[2,128,1280]{2,1,0:T(8,128)(2,1)S(1)}, bf16[2,128,1280]{2,1,0:T(8,128)(2,1)S(1)}, u32[]{:S(2)}, u32[]{:S(2)}) collective-permute-start(bf16[2,128,1280]{2,1,0:T(8,128)(2,1)S(1)} %pad_maximum_fusion.refs_0_), channel_id=1, source_target_pairs={{0,2},{1,3},{2,0},{3,1},{4,6},{5,7},{6,4},{7,5},{8,10},{9,11},{10,... | collective-permute-start | bytes 1966088 | tf_op jit(solution)/shard_map/ppermute | solution.py:16
  5.2 20.4 %collective-permute-start.1 = (bf16[2,128,1280]{2,1,0:T(8,128)(2,1)S(1)}, bf16[2,128,1280]{2,1,0:T(8,128)(2,1)}, u32[]{:S(2)}, u32[]{:S(2)}) collective-permute-start(bf16[2,128,1280]{2,1,0:T(8,128)(2,1)S(1)} %pad_maximum_fusion.refs_0_), channel_id=1, source_target_pairs={{0,4},{1,5},{2,6},{3,7},{4,8},{5,9},{6,10},{7,11},{8,12},{9,13},{1... | collective-permute-start | bytes 1966088 | tf_op jit(solution)/shard_map/ppermute | solution.py:16
  9.5 17.9 %collective-permute-start.2 = (bf16[2,128,1280]{2,1,0:T(8,128)(2,1)S(1)}, bf16[2,128,1280]{2,1,0:T(8,128)(2,1)}, u32[]{:S(2)}, u32[]{:S(2)}) collective-permute-start(bf16[2,128,1280]{2,1,0:T(8,128)(2,1)S(1)} %pad_maximum_fusion.refs_0_), channel_id=1, source_target_pairs={{4,0},{5,1},{6,2},{7,3},{8,4},{9,5},{10,6},{11,7},{12,8},{13,9},{1... | collective-permute-start | bytes 1966088 | tf_op jit(solution)/shard_map/ppermute | solution.py:16
  10.8 16.7 %collective-permute-start.3 = (bf16[2,128,1280]{2,1,0:T(8,128)(2,1)S(1)}, bf16[2,128,1280]{2,1,0:T(8,128)(2,1)}, u32[]{:S(2)}, u32[]{:S(2)}) collective-permute-start(bf16[2,128,1280]{2,1,0:T(8,128)(2,1)S(1)} %pad_maximum_fusion.refs_0_), channel_id=1, source_target_pairs={{0,1},{1,0},{2,3},{3,2},{4,5},{5,4},{6,7},{7,6},{8,9},{9,8},{10,11... | collective-permute-start | bytes 1966088 | tf_op jit(solution)/shard_map/ppermute | solution.py:16
  10.9 55.0 %copy-start.6 = (bf16[2,128,1280]{2,1,0:T(8,128)(2,1)}, bf16[2,128,1280]{2,1,0:T(8,128)(2,1)S(1)}, u32[]{:S(2)}) copy-start(bf16[2,128,1280]{2,1,0:T(8,128)(2,1)S(1)} %pad_maximum_fusion.1.refs_0_) | copy-start | bytes 1966084
  10.9 23.0 %collective-permute-start.9 = (bf16[2,128,1280]{2,1,0:T(8,128)(2,1)S(1)}, bf16[2,128,1280]{2,1,0:T(8,128)(2,1)S(1)}, u32[]{:S(2)}, u32[]{:S(2)}) collective-permute-start(bf16[2,128,1280]{2,1,0:T(8,128)(2,1)S(1)} %pad_maximum_fusion.1.refs_0_), channel_id=1, source_target_pairs={{0,2},{1,3},{2,0},{3,1},{4,6},{5,7},{6,4},{7,5},{8,10},{9,11},{10,... | collective-permute-start | bytes 1966088 | tf_op jit(solution)/shard_map/ppermute | solution.py:16
  20.7 31.2 %copy-start.12 = (bf16[2,128,1280]{2,1,0:T(8,128)(2,1)}, bf16[2,128,1280]{2,1,0:T(8,128)(2,1)S(1)}, u32[]{:S(2)}) copy-start(bf16[2,128,1280]{2,1,0:T(8,128)(2,1)S(1)} %collective-permute-done.refs_1_) | copy-start | bytes 1966084
  20.7 16.1 %collective-permute-start.10 = (bf16[2,128,1280]{2,1,0:T(8,128)(2,1)S(1)}, bf16[2,128,1280]{2,1,0:T(8,128)(2,1)}, u32[]{:S(2)}, u32[]{:S(2)}) collective-permute-start(bf16[2,128,1280]{2,1,0:T(8,128)(2,1)S(1)} %pad_maximum_fusion.1.refs_0_), channel_id=1, source_target_pairs={{0,4},{1,5},{2,6},{3,7},{4,8},{5,9},{6,10},{7,11},{8,12},{9,13},{1... | collective-permute-start | bytes 1966088 | tf_op jit(solution)/shard_map/ppermute | solution.py:16
  25.6 16.3 %collective-permute-start.11 = (bf16[2,128,1280]{2,1,0:T(8,128)(2,1)S(1)}, bf16[2,128,1280]{2,1,0:T(8,128)(2,1)}, u32[]{:S(2)}, u32[]{:S(2)}) collective-permute-start(bf16[2,128,1280]{2,1,0:T(8,128)(2,1)S(1)} %pad_maximum_fusion.1.refs_0_), channel_id=1, source_target_pairs={{4,0},{5,1},{6,2},{7,3},{8,4},{9,5},{10,6},{11,7},{12,8},{13,9},{1... | collective-permute-start | bytes 1966088 | tf_op jit(solution)/shard_map/ppermute | solution.py:16
  27.4 14.5 %collective-permute-start.12 = (bf16[2,128,1280]{2,1,0:T(8,128)(2,1)S(1)}, bf16[2,128,1280]{2,1,0:T(8,128)(2,1)S(1)}, u32[]{:S(2)}, u32[]{:S(2)}) collective-permute-start(bf16[2,128,1280]{2,1,0:T(8,128)(2,1)S(1)} %pad_maximum_fusion.1.refs_0_), channel_id=1, source_target_pairs={{0,1},{1,0},{2,3},{3,2},{4,5},{5,4},{6,7},{7,6},{8,9},{9,8},{10,11... | collective-permute-start | bytes 1966088 | tf_op jit(solution)/shard_map/ppermute | solution.py:16
  27.5 14.9 %collective-permute-start.4 = (bf16[2,128,1280]{2,1,0:T(8,128)(2,1)S(1)}, bf16[2,128,1280]{2,1,0:T(8,128)(2,1)S(1)}, u32[]{:S(2)}, u32[]{:S(2)}) collective-permute-start(bf16[2,128,1280]{2,1,0:T(8,128)(2,1)S(1)} %collective-permute-done.refs_1_), channel_id=1, source_target_pairs={{0,1},{1,0},{2,3},{3,2},{4,5},{5,4},{6,7},{7,6},{8,9},{9,8},{10,11... | collective-permute-start | bytes 1966088 | tf_op jit(solution)/shard_map/ppermute | solution.py:16
  33.9 32.0 %copy-start.11 = (bf16[2,128,1280]{2,1,0:T(8,128)(2,1)}, bf16[2,128,1280]{2,1,0:T(8,128)(2,1)S(1)}, u32[]{:S(2)}) copy-start(bf16[2,128,1280]{2,1,0:T(8,128)(2,1)S(1)} %collective-permute-done.9.refs_1_) | copy-start | bytes 1966084
  33.9 11.1 %collective-permute-start.7 = (bf16[2,128,1280]{2,1,0:T(8,128)(2,1)S(1)}, bf16[2,128,1280]{2,1,0:T(8,128)(2,1)S(1)}, u32[]{:S(2)}, u32[]{:S(2)}) collective-permute-start(bf16[2,128,1280]{2,1,0:T(8,128)(2,1)S(1)} %collective-permute-done.refs_1_), channel_id=1, source_target_pairs={{0,5},{3,6},{4,9},{7,10},{8,13},{11,14},{16,21},{19,22},{20,25},{2... | collective-permute-start | bytes 1966088 | tf_op jit(solution)/shard_map/ppermute | solution.py:16
  36.8 12.2 %collective-permute-start.8 = (bf16[2,128,1280]{2,1,0:T(8,128)(2,1)S(1)}, bf16[2,128,1280]{2,1,0:T(8,128)(2,1)S(1)}, u32[]{:S(2)}, u32[]{:S(2)}) collective-permute-start(bf16[2,128,1280]{2,1,0:T(8,128)(2,1)S(1)} %collective-permute-done.refs_1_), channel_id=1, source_target_pairs={{4,1},{7,2},{8,5},{11,6},{12,9},{15,10},{20,17},{23,18},{24,21},{2... | collective-permute-start | bytes 1966088 | tf_op jit(solution)/shard_map/ppermute | solution.py:16
  41.9 8.7 %collective-permute-start.5 = (bf16[2,128,1280]{2,1,0:T(8,128)(2,1)}, bf16[2,128,1280]{2,1,0:T(8,128)(2,1)S(1)}, u32[]{:S(2)}, u32[]{:S(2)}) collective-permute-start(bf16[2,128,1280]{2,1,0:T(8,128)(2,1)} %collective-permute-done.1.refs_2_), channel_id=1, source_target_pairs={{0,1},{1,0},{2,3},{3,2},{4,5},{5,4},{6,7},{7,6},{8,9},{9,8},{10,11... | collective-permute-start | bytes 1966088 | tf_op jit(solution)/shard_map/ppermute | solution.py:16
  41.9 0.9 copy-start.13
  41.9 9.5 %collective-permute-start.6 = (bf16[2,128,1280]{2,1,0:T(8,128)(2,1)}, bf16[2,128,1280]{2,1,0:T(8,128)(2,1)}, u32[]{:S(2)}, u32[]{:S(2)}) collective-permute-start(bf16[2,128,1280]{2,1,0:T(8,128)(2,1)} %collective-permute-done.2.refs_3_), channel_id=1, source_target_pairs={{0,1},{1,0},{2,3},{3,2},{4,5},{5,4},{6,7},{7,6},{8,9},{9,8},{10,11... | collective-permute-start | bytes 1966088 | tf_op jit(solution)/shard_map/ppermute | solution.py:16
  42.8 0.9 copy-start.14
  42.8 23.2 %collective-permute-start.13 = (bf16[2,128,1280]{2,1,0:T(8,128)(2,1)S(1)}, bf16[2,128,1280]{2,1,0:T(8,128)(2,1)}, u32[]{:S(2)}, u32[]{:S(2)}) collective-permute-start(bf16[2,128,1280]{2,1,0:T(8,128)(2,1)S(1)} %collective-permute-done.9.refs_1_), channel_id=1, source_target_pairs={{0,1},{1,0},{2,3},{3,2},{4,5},{5,4},{6,7},{7,6},{8,9},{9,8},{10,11... | collective-permute-start | bytes 1966088 | tf_op jit(solution)/shard_map/ppermute | solution.py:16
  45.1 4.0 %copy-start.15 = (bf16[2,128,1280]{2,1,0:T(8,128)(2,1)}, bf16[2,128,1280]{2,1,0:T(8,128)(2,1)S(1)}, u32[]{:S(2)}) copy-start(bf16[2,128,1280]{2,1,0:T(8,128)(2,1)S(1)} %collective-permute-done.7.refs_8_) | copy-start | bytes 1966084
  45.1 21.0 %collective-permute-start.16 = (bf16[2,128,1280]{2,1,0:T(8,128)(2,1)S(1)}, bf16[2,128,1280]{2,1,0:T(8,128)(2,1)}, u32[]{:S(2)}, u32[]{:S(2)}) collective-permute-start(bf16[2,128,1280]{2,1,0:T(8,128)(2,1)S(1)} %collective-permute-done.9.refs_1_), channel_id=1, source_target_pairs={{0,5},{3,6},{4,9},{7,10},{8,13},{11,14},{16,21},{19,22},{20,25},{2... | collective-permute-start | bytes 1966088 | tf_op jit(solution)/shard_map/ppermute | solution.py:16
  49.1 1.5 %copy-start.16 = (bf16[2,128,1280]{2,1,0:T(8,128)(2,1)}, bf16[2,128,1280]{2,1,0:T(8,128)(2,1)S(1)}, u32[]{:S(2)}) copy-start(bf16[2,128,1280]{2,1,0:T(8,128)(2,1)S(1)} %collective-permute-done.8.refs_9_) | copy-start | bytes 1966084
  49.1 17.0 %collective-permute-start.17 = (bf16[2,128,1280]{2,1,0:T(8,128)(2,1)S(1)}, bf16[2,128,1280]{2,1,0:T(8,128)(2,1)}, u32[]{:S(2)}, u32[]{:S(2)}) collective-permute-start(bf16[2,128,1280]{2,1,0:T(8,128)(2,1)S(1)} %collective-permute-done.9.refs_1_), channel_id=1, source_target_pairs={{4,1},{7,2},{8,5},{11,6},{12,9},{15,10},{20,17},{23,18},{24,21},{2... | collective-permute-start | bytes 1966088 | tf_op jit(solution)/shard_map/ppermute | solution.py:16
  50.6 0.8 copy-start.17
  51.4 14.7 %collective-permute-start.14 = (bf16[2,128,1280]{2,1,0:T(8,128)(2,1)}, bf16[2,128,1280]{2,1,0:T(8,128)(2,1)}, u32[]{:S(2)}, u32[]{:S(2)}) collective-permute-start(bf16[2,128,1280]{2,1,0:T(8,128)(2,1)} %collective-permute-done.10.refs_2_), channel_id=1, source_target_pairs={{0,1},{1,0},{2,3},{3,2},{4,5},{5,4},{6,7},{7,6},{8,9},{9,8},{10,11... | collective-permute-start | bytes 1966088 | tf_op jit(solution)/shard_map/ppermute | solution.py:16
  51.4 14.7 %collective-permute-start.15 = (bf16[2,128,1280]{2,1,0:T(8,128)(2,1)}, bf16[2,128,1280]{2,1,0:T(8,128)(2,1)}, u32[]{:S(2)}, u32[]{:S(2)}) collective-permute-start(bf16[2,128,1280]{2,1,0:T(8,128)(2,1)} %collective-permute-done.11.refs_3_), channel_id=1, source_target_pairs={{0,1},{1,0},{2,3},{3,2},{4,5},{5,4},{6,7},{7,6},{8,9},{9,8},{10,11... | collective-permute-start | bytes 1966088 | tf_op jit(solution)/shard_map/ppermute | solution.py:16
  66.0 28.0 %collective-permute-start.18 = (bf16[4,2,128,1280]{3,2,1,0:T(8,128)(2,1)}, bf16[4,2,128,1280]{3,2,1,0:T(8,128)(2,1)S(1)}, u32[]{:S(2)}, u32[]{:S(2)}) collective-permute-start(bf16[4,2,128,1280]{3,2,1,0:T(8,128)(2,1)} %get-tuple-element.22), channel_id=1, source_target_pairs={{0,1},{1,0},{2,3},{3,2},{4,5},{5,4},{6,7},{7,6},{8,9},{9,8},{10,11... | collective-permute-start | bytes 7864328 | tf_op jit(solution)/shard_map/ppermute | solution.py:16
  66.1 27.9 %copy-start.2 = (bf16[2,128,1280]{2,1,0:T(8,128)(2,1)S(1)}, bf16[2,128,1280]{2,1,0:T(8,128)(2,1)}, u32[]{:S(2)}) copy-start(bf16[2,128,1280]{2,1,0:T(8,128)(2,1)} %get-tuple-element.27) | copy-start | bytes 1966084
  80.3 13.7 %copy-start = (bf16[2,128,1280]{2,1,0:T(8,128)(2,1)S(1)}, bf16[2,128,1280]{2,1,0:T(8,128)(2,1)}, u32[]{:S(2)}) copy-start(bf16[2,128,1280]{2,1,0:T(8,128)(2,1)} %get-tuple-element.23) | copy-start | bytes 1966084
  80.3 13.7 %copy-start.1 = (bf16[2,128,1280]{2,1,0:T(8,128)(2,1)S(1)}, bf16[2,128,1280]{2,1,0:T(8,128)(2,1)}, u32[]{:S(2)}) copy-start(bf16[2,128,1280]{2,1,0:T(8,128)(2,1)} %get-tuple-element.26) | copy-start | bytes 1966084
  80.3 26.1 %collective-permute-start.24 = (bf16[4,2,128,1280]{3,2,1,0:T(8,128)(2,1)}, bf16[4,2,128,1280]{3,2,1,0:T(8,128)(2,1)S(1)}, u32[]{:S(2)}, u32[]{:S(2)}) collective-permute-start(bf16[4,2,128,1280]{3,2,1,0:T(8,128)(2,1)} %get-tuple-element.29), channel_id=1, source_target_pairs={{0,1},{1,0},{2,3},{3,2},{4,5},{5,4},{6,7},{7,6},{8,9},{9,8},{10,11... | collective-permute-start | bytes 7864328 | tf_op jit(solution)/shard_map/ppermute | solution.py:16
  80.9 12.4 %collective-permute-start.19 = (bf16[2,128,1280]{2,1,0:T(8,128)(2,1)}, bf16[2,128,1280]{2,1,0:T(8,128)(2,1)S(1)}, u32[]{:S(2)}, u32[]{:S(2)}) collective-permute-start(bf16[2,128,1280]{2,1,0:T(8,128)(2,1)} %get-tuple-element.24), channel_id=1, source_target_pairs={{5,0},{6,3},{9,4},{10,7},{13,8},{14,11},{21,16},{22,19},{25,20},{2... | collective-permute-start | bytes 1966088 | tf_op jit(solution)/shard_map/ppermute | solution.py:16
  82.2 11.8 %collective-permute-start.20 = (bf16[2,128,1280]{2,1,0:T(8,128)(2,1)}, bf16[2,128,1280]{2,1,0:T(8,128)(2,1)S(1)}, u32[]{:S(2)}, u32[]{:S(2)}) collective-permute-start(bf16[2,128,1280]{2,1,0:T(8,128)(2,1)} %get-tuple-element.25), channel_id=1, source_target_pairs={{1,4},{2,7},{5,8},{6,11},{9,12},{10,15},{17,20},{18,23},{21,24},{2... | collective-permute-start | bytes 1966088 | tf_op jit(solution)/shard_map/ppermute | solution.py:16
  82.9 18.9 %collective-permute-start.25 = (bf16[2,128,1280]{2,1,0:T(8,128)(2,1)}, bf16[2,128,1280]{2,1,0:T(8,128)(2,1)S(1)}, u32[]{:S(2)}, u32[]{:S(2)}) collective-permute-start(bf16[2,128,1280]{2,1,0:T(8,128)(2,1)} %get-tuple-element.31), channel_id=1, source_target_pairs={{5,0},{6,3},{9,4},{10,7},{13,8},{14,11},{21,16},{22,19},{25,20},{2... | collective-permute-start | bytes 1966088 | tf_op jit(solution)/shard_map/ppermute | solution.py:16
  93.3 13.1 %collective-permute-start.26 = (bf16[2,128,1280]{2,1,0:T(8,128)(2,1)}, bf16[2,128,1280]{2,1,0:T(8,128)(2,1)S(1)}, u32[]{:S(2)}, u32[]{:S(2)}) collective-permute-start(bf16[2,128,1280]{2,1,0:T(8,128)(2,1)} %get-tuple-element.32), channel_id=1, source_target_pairs={{1,4},{2,7},{5,8},{6,11},{9,12},{10,15},{17,20},{18,23},{21,24},{2... | collective-permute-start | bytes 1966088 | tf_op jit(solution)/shard_map/ppermute | solution.py:16
  94.0 12.4 %copy-start.3 = (bf16[2,128,1280]{2,1,0:T(8,128)(2,1)S(1)}, bf16[2,128,1280]{2,1,0:T(8,128)(2,1)}, u32[]{:S(2)}) copy-start(bf16[2,128,1280]{2,1,0:T(8,128)(2,1)} %get-tuple-element.30) | copy-start | bytes 1966084
  94.0 12.4 %copy-start.4 = (bf16[2,128,1280]{2,1,0:T(8,128)(2,1)S(1)}, bf16[2,128,1280]{2,1,0:T(8,128)(2,1)}, u32[]{:S(2)}) copy-start(bf16[2,128,1280]{2,1,0:T(8,128)(2,1)} %get-tuple-element.33) | copy-start | bytes 1966084
  94.0 12.4 %copy-start.5 = (bf16[2,128,1280]{2,1,0:T(8,128)(2,1)S(1)}, bf16[2,128,1280]{2,1,0:T(8,128)(2,1)}, u32[]{:S(2)}) copy-start(bf16[2,128,1280]{2,1,0:T(8,128)(2,1)} %get-tuple-element.34) | copy-start | bytes 1966084
  94.8 21.3 %collective-permute-start.21 = (bf16[2,128,1280]{2,1,0:T(8,128)(2,1)S(1)}, bf16[2,128,1280]{2,1,0:T(8,128)(2,1)S(1)}, u32[]{:S(2)}, u32[]{:S(2)}) collective-permute-start(bf16[2,128,1280]{2,1,0:T(8,128)(2,1)S(1)} %get-tuple-element.35), channel_id=1, source_target_pairs={{0,2},{1,3},{2,0},{3,1},{4,6},{5,7},{6,4},{7,5},{8,10},{9,11},{10,... | collective-permute-start | bytes 1966088 | tf_op jit(solution)/shard_map/ppermute | solution.py:16
  100.5 19.5 %collective-permute-start.22 = (bf16[2,128,1280]{2,1,0:T(8,128)(2,1)S(1)}, bf16[2,128,1280]{2,1,0:T(8,128)(2,1)S(1)}, u32[]{:S(2)}, u32[]{:S(2)}) collective-permute-start(bf16[2,128,1280]{2,1,0:T(8,128)(2,1)S(1)} %get-tuple-element.37), channel_id=1, source_target_pairs={{4,0},{5,1},{6,2},{7,3},{8,4},{9,5},{10,6},{11,7},{12,8},{13,9},{1... | collective-permute-start | bytes 1966088 | tf_op jit(solution)/shard_map/ppermute | solution.py:16
  101.8 19.3 %collective-permute-start.23 = (bf16[2,128,1280]{2,1,0:T(8,128)(2,1)S(1)}, bf16[2,128,1280]{2,1,0:T(8,128)(2,1)S(1)}, u32[]{:S(2)}, u32[]{:S(2)}) collective-permute-start(bf16[2,128,1280]{2,1,0:T(8,128)(2,1)S(1)} %get-tuple-element.36), channel_id=1, source_target_pairs={{0,4},{1,5},{2,6},{3,7},{4,8},{5,9},{6,10},{7,11},{8,12},{9,13},{1... | collective-permute-start | bytes 1966088 | tf_op jit(solution)/shard_map/ppermute | solution.py:16
  106.5 14.7 %copy-start.8 = (bf16[2,128,1280]{2,1,0:T(8,128)(2,1)S(1)}, bf16[2,128,1280]{2,1,0:T(8,128)(2,1)}, u32[]{:S(2)}) copy-start(bf16[2,128,1280]{2,1,0:T(8,128)(2,1)} %get-tuple-element.21) | copy-start | bytes 1966084
  107.2 22.3 %collective-permute-start.27 = (bf16[2,128,1280]{2,1,0:T(8,128)(2,1)S(1)}, bf16[2,128,1280]{2,1,0:T(8,128)(2,1)S(1)}, u32[]{:S(2)}, u32[]{:S(2)}) collective-permute-start(bf16[2,128,1280]{2,1,0:T(8,128)(2,1)S(1)} %get-tuple-element.38), channel_id=1, source_target_pairs={{0,2},{1,3},{2,0},{3,1},{4,6},{5,7},{6,4},{7,5},{8,10},{9,11},{10,... | collective-permute-start | bytes 1966088 | tf_op jit(solution)/shard_map/ppermute | solution.py:16
  109.6 21.8 %collective-permute-start.28 = (bf16[2,128,1280]{2,1,0:T(8,128)(2,1)S(1)}, bf16[2,128,1280]{2,1,0:T(8,128)(2,1)S(1)}, u32[]{:S(2)}, u32[]{:S(2)}) collective-permute-start(bf16[2,128,1280]{2,1,0:T(8,128)(2,1)S(1)} %get-tuple-element.40), channel_id=1, source_target_pairs={{4,0},{5,1},{6,2},{7,3},{8,4},{9,5},{10,6},{11,7},{12,8},{13,9},{1... | collective-permute-start | bytes 1966088 | tf_op jit(solution)/shard_map/ppermute | solution.py:16
  116.1 17.5 %collective-permute-start.29 = (bf16[2,128,1280]{2,1,0:T(8,128)(2,1)S(1)}, bf16[2,128,1280]{2,1,0:T(8,128)(2,1)S(1)}, u32[]{:S(2)}, u32[]{:S(2)}) collective-permute-start(bf16[2,128,1280]{2,1,0:T(8,128)(2,1)S(1)} %get-tuple-element.39), channel_id=1, source_target_pairs={{0,4},{1,5},{2,6},{3,7},{4,8},{5,9},{6,10},{7,11},{8,12},{9,13},{1... | collective-permute-start | bytes 1966088 | tf_op jit(solution)/shard_map/ppermute | solution.py:16
  121.6 12.0 %copy-start.9 = (bf16[2,128,1280]{2,1,0:T(8,128)(2,1)S(1)}, bf16[2,128,1280]{2,1,0:T(8,128)(2,1)}, u32[]{:S(2)}) copy-start(bf16[2,128,1280]{2,1,0:T(8,128)(2,1)} %get-tuple-element.28) | copy-start | bytes 1966084

commit v18 on v17

--- a/solution.py
+++ b/solution.py
@@ -50,27 +50,22 @@
 
 def allowed(query_rows, key_rows, frame_keep, band_window, frame_len):
     frame_count = frame_keep.shape[0]
-    query_frame = jnp.floor_divide(query_rows, frame_len)
+    query_frame = jnp.floor_divide(query_rows[0], frame_len)
+    query_place = query_rows - query_frame * frame_len
     key_frame = jnp.floor_divide(key_rows, frame_len)
-    query_place = query_rows - query_frame * frame_len
     key_place = key_rows - key_frame * frame_len
     query_inside = (query_rows >= 0) & (query_rows < frame_count * frame_len)
     key_inside = (key_rows >= 0) & (key_rows < frame_count * frame_len)
-    inside = query_inside[:, None] & key_inside[None, :]
-    onehot = (query_frame[:, None] == jnp.arange(frame_count, dtype=jnp.int32)[None, :]).astype(
-        jnp.int32
-    )
-    keep_rows = jnp.sum(onehot[:, :, None] * frame_keep[None, :, :], axis=1)
-    window_rows = jnp.sum(onehot * band_window[None, :], axis=1)
-    frame_gap = key_frame[None, :] - query_frame[:, None]
+    keep = lax.dynamic_index_in_dim(frame_keep, query_frame, 0, keepdims=False)
+    window = lax.dynamic_index_in_dim(band_window, query_frame, 0, keepdims=False)
+    frame_gap = key_frame - query_frame
     kept_pair = jnp.zeros(frame_gap.shape, jnp.int32)
     for column in range(3):
-        kept_pair = kept_pair + jnp.where(
-            frame_gap == column - 1, keep_rows[:, column : column + 1], 0
-        )
+        kept_pair = kept_pair + jnp.where(frame_gap == column - 1, keep[column], 0)
+    key_ok = key_inside & (kept_pair > 0)
     place_gap = jnp.abs(query_place[:, None] - key_place[None, :])
-    nearby = (frame_gap == 0) | (place_gap <= window_rows[:, None])
-    return inside & (kept_pair > 0) & nearby
+    nearby = (frame_gap == 0)[None, :] | (place_gap <= window)
+    return query_inside[:, None] & key_ok[None, :] & nearby
 
 
 def attention_backward(mask, queries, out_grad, inputs, slot_in, out_lead, slot_out, inv_root, offset):

time: 137 us -> 137 us (level)
  other arithmetic: 7.77 us -> 9.77 us
  starting transfers between devices: 50 us -> 48.1 us
    and x1, other arithmetic: 0.01 us -> 1.97 us  [allowed(): key_ok = key_inside & (kept_pair > 0)]
    ppermute x30, starting transfers between devices: 50 us -> 48.1 us  [send(): return lax.ppermute(value, 'tm', pairs)]
  transfers between devices with their start and end apart: 30 -> 30, of which waited for: 11 -> 11; matrix products, arithmetic and copies ran while one was open for 4% -> 6% of each run, Pallas kernels for 21% -> 21%
where the time goes in v18:
time: 137 us; the launch traced here: 136 us
  starting transfers between devices  48.1 us (35%)
  waiting for transfers between devices  44.5 us (32%)
  Pallas kernels  28.2 us (21%)
  other arithmetic  9.77 us (7%)
  local copies, waits for them, and re-layouts  4.27 us (3%)
  between operations  1.4 us (1%)
    ppermute x30, starting transfers between devices, send(): return lax.ppermute(value, 'tm', pairs)  48.1 us
    ppermute x30, waiting for transfers between devices, send(): return lax.ppermute(value, 'tm', pairs)  44.5 us
    pallas_call x2, Pallas kernels, attention_backward(): pl.pallas_call(kernel, grid=(heads // STEP_HEADS,), in_specs=in_specs, ou...  28.2 us
  transfers between devices with their start and end apart: 30, of which 11 were waited for; matrix products, arithmetic and copies ran while one was open for 6% of the time, Pallas kernels for 21%

profile of v18, /device:TPU:0, one launch (start us, length us, event | category | flops | bytes accessed | tf_op | source)
XLA Modules:
  0.0 136.2 jit_solution(10420646179819184847)
XLA Ops:
  0.6 0.0 copy-start
  0.6 1.4 slice_bitcast_fusion.14
  2.0 0.0 copy-start.18
  2.0 0.1 pad_maximum_fusion.refs_0_
  2.1 3.1 %collective-permute-start = (bf16[2,128,1280]{2,1,0:T(8,128)(2,1)S(1)}, bf16[2,128,1280]{2,1,0:T(8,128)(2,1)S(1)}, u32[]{:S(2)}, u32[]{:S(2)}) collective-permute-start(bf16[2,128,1280]{2,1,0:T(8,128)(2,1)S(1)} %pad_maximum_fusion.refs_0_), channel_id=1, source_target_pairs={{0,2},{1,3},{2,0},{3,1},{4,6},{5,7},{6,4},{7,5},{8,10},{9,11},{10,... | collective-permute-start | bytes 1966088 | tf_op jit(solution)/shard_map/ppermute | solution.py:16
  5.2 4.3 %collective-permute-start.1 = (bf16[2,128,1280]{2,1,0:T(8,128)(2,1)S(1)}, bf16[2,128,1280]{2,1,0:T(8,128)(2,1)}, u32[]{:S(2)}, u32[]{:S(2)}) collective-permute-start(bf16[2,128,1280]{2,1,0:T(8,128)(2,1)S(1)} %pad_maximum_fusion.refs_0_), channel_id=1, source_target_pairs={{0,4},{1,5},{2,6},{3,7},{4,8},{5,9},{6,10},{7,11},{8,12},{9,13},{1... | collective-permute-start | bytes 1966088 | tf_op jit(solution)/shard_map/ppermute | solution.py:16
  9.5 1.3 collective-permute-start.2
  10.8 0.1 collective-permute-start.3
  10.9 0.1 pad_maximum_fusion.1.refs_0_
  10.9 0.0 copy-start.7
  10.9 0.6 collective-permute-start.9
  11.8 0.6 dynamic_slice.9
  12.4 8.3 %collective-permute-done.refs_1_ = bf16[2,128,1280]{2,1,0:T(8,128)(2,1)S(1)} collective-permute-done((bf16[2,128,1280]{2,1,0:T(8,128)(2,1)S(1)}, bf16[2,128,1280]{2,1,0:T(8,128)(2,1)S(1)}, u32[]{:S(2)}, u32[]{:S(2)}) %collective-permute-start) | collective-permute-done | bytes 655392 | tf_op jit(solution)/shard_map/ppermute | solution.py:16
  20.8 4.8 %collective-permute-start.10 = (bf16[2,128,1280]{2,1,0:T(8,128)(2,1)S(1)}, bf16[2,128,1280]{2,1,0:T(8,128)(2,1)}, u32[]{:S(2)}, u32[]{:S(2)}) collective-permute-start(bf16[2,128,1280]{2,1,0:T(8,128)(2,1)S(1)} %pad_maximum_fusion.1.refs_0_), channel_id=1, source_target_pairs={{0,4},{1,5},{2,6},{3,7},{4,8},{5,9},{6,10},{7,11},{8,12},{9,13},{1... | collective-permute-start | bytes 1966088 | tf_op jit(solution)/shard_map/ppermute | solution.py:16
  25.6 0.0 collective-permute-done.1.refs_2_
  25.6 1.3 collective-permute-start.11
  26.9 0.5 collective-permute-done.2.refs_3_
  27.4 0.0 collective-permute-start.12
  27.4 0.0 collective-permute-done.3.refs_4_
  27.4 0.6 collective-permute-start.4
  28.0 0.6 fusion.24
  28.7 5.3 %collective-permute-done.9.refs_1_ = bf16[2,128,1280]{2,1,0:T(8,128)(2,1)S(1)} collective-permute-done((bf16[2,128,1280]{2,1,0:T(8,128)(2,1)S(1)}, bf16[2,128,1280]{2,1,0:T(8,128)(2,1)S(1)}, u32[]{:S(2)}, u32[]{:S(2)}) %collective-permute-start.9) | collective-permute-done | bytes 655392 | tf_op jit(solution)/shard_map/ppermute | solution.py:16
  33.9 2.4 %collective-permute-start.7 = (bf16[2,128,1280]{2,1,0:T(8,128)(2,1)S(1)}, bf16[2,128,1280]{2,1,0:T(8,128)(2,1)S(1)}, u32[]{:S(2)}, u32[]{:S(2)}) collective-permute-start(bf16[2,128,1280]{2,1,0:T(8,128)(2,1)S(1)} %collective-permute-done.refs_1_), channel_id=1, source_target_pairs={{0,5},{3,6},{4,9},{7,10},{8,13},{11,14},{16,21},{19,22},{20,25},{2... | collective-permute-start | bytes 1966088 | tf_op jit(solution)/shard_map/ppermute | solution.py:16
  36.4 0.4 collective-permute-done.10.refs_2_
  36.8 0.7 collective-permute-start.8
  37.5 4.4 %collective-permute-done.11.refs_3_ = bf16[2,128,1280]{2,1,0:T(8,128)(2,1)} collective-permute-done((bf16[2,128,1280]{2,1,0:T(8,128)(2,1)S(1)}, bf16[2,128,1280]{2,1,0:T(8,128)(2,1)}, u32[]{:S(2)}, u32[]{:S(2)}) %collective-permute-start.11) | collective-permute-done | bytes 655392 | tf_op jit(solution)/shard_map/ppermute | solution.py:16
  41.9 0.5 collective-permute-start.6
  42.4 2.0 %fusion.23 = (pred[1280]{0:T(1024)(128)(4,1)S(1)}, pred[1280]{0:T(1024)(128)(4,1)S(1)}) fusion(s32[1280]{0:T(1024)S(1)} %constant_dynamic-update-slice_fusion, s32[]{:T(128)} %bitcast.3, s32[]{:T(128)} %bitcast.2, s32[]{:T(128)} %bitcast.1, s32[]{:T(128)S(6)} %select_n.64), kind=kLoop, calls=%fused_computation.60 | loop fusion | flops 37120 | bytes 7696 | tf_op jit(solution)/shard_map/and | solution.py:65
  44.4 0.2 collective-permute-start.13
  44.6 0.7 copy-done.14
  45.2 1.7 %fusion.20.mask_ref = s32[128,1280]{1,0:T(8,128)} fusion(s32[]{:T(128)} %bitcast.4, s32[1280]{0:T(1024)S(1)} %multiply_subtract_fusion, s32[128]{0:T(128)S(1)} %broadcast_subtract_fusion, pred[1280]{0:T(1024)(128)(4,1)S(1)} %get-tuple-element.36, pred[1280]{0:T(1024)(128)(4,1)S(1)} %get-tuple-element.35, pred[128]{0:T(512)(128)(4,1)S(1)} %compare_and_fusion), kind=kLoop, calls=%fused_computation.42 | loop fusion | flops 1146880 | bytes 663684 | tf_op jit(solution)/shard_map/convert_element_type | solution.py:223
  46.9 3.2 %collective-permute-start.16 = (bf16[2,128,1280]{2,1,0:T(8,128)(2,1)S(1)}, bf16[2,128,1280]{2,1,0:T(8,128)(2,1)}, u32[]{:S(2)}, u32[]{:S(2)}) collective-permute-start(bf16[2,128,1280]{2,1,0:T(8,128)(2,1)S(1)} %collective-permute-done.9.refs_1_), channel_id=1, source_target_pairs={{0,5},{3,6},{4,9},{7,10},{8,13},{11,14},{16,21},{19,22},{20,25},{2... | collective-permute-start | bytes 1966088 | tf_op jit(solution)/shard_map/ppermute | solution.py:16
  50.1 1.5 %collective-permute-start.17 = (bf16[2,128,1280]{2,1,0:T(8,128)(2,1)S(1)}, bf16[2,128,1280]{2,1,0:T(8,128)(2,1)}, u32[]{:S(2)}, u32[]{:S(2)}) collective-permute-start(bf16[2,128,1280]{2,1,0:T(8,128)(2,1)S(1)} %collective-permute-done.9.refs_1_), channel_id=1, source_target_pairs={{4,1},{7,2},{8,5},{11,6},{12,9},{15,10},{20,17},{23,18},{24,21},{2... | collective-permute-start | bytes 1966088 | tf_op jit(solution)/shard_map/ppermute | solution.py:16
  51.6 0.0 collective-permute-done.5.refs_6_
  51.6 0.8 copy-done.17
  52.4 0.0 collective-permute-start.14
  52.4 0.5 collective-permute-start.15
  53.0 14.0 %shard_map.85 = (bf16[128,1280]{1,0:T(8,128)(2,1)}, bf16[2,128,1280]{2,1,0:T(8,128)(2,1)}, bf16[4,2,128,1280]{3,2,1,0:T(8,128)(2,1)}, bf16[2,128,1280]{2,1,0:T(8...) custom-call(s32[128,1280]{1,0:T(8,128)} %fusion.20.mask_ref, ...), custom_call_target="tpu_custom_call" | custom-call | flops 2516582400 | bytes 14745600 | tf_op jit(solution)/shard_map/pallas_call | solution.py:122
  67.0 0.1 collective-permute-start.18
  67.1 14.2 %shard_map.86 = (bf16[128,1280]{1,0:T(8,128)(2,1)}, bf16[2,128,1280]{2,1,0:T(8,128)(2,1)}, bf16[4,2,128,1280]{3,2,1,0:T(8,128)(2,1)}, bf16[2,128,1280]{2,1,0:T(8...) custom-call(s32[128,1280]{1,0:T(8,128)} %fusion.20.mask_ref, ...), custom_call_target="tpu_custom_call" | custom-call | flops 2516582400 | bytes 14745600 | tf_op jit(solution)/shard_map/pallas_call | solution.py:122
  81.3 0.6 collective-permute-start.24
  81.9 1.3 collective-permute-start.19
  83.2 0.7 collective-permute-start.20
  83.9 1.3 collective-permute-start.25
  85.2 2.0 %pad_maximum_fusion.2 = bf16[128,2560]{1,0:T(8,128)(2,1)} fusion(bf16[128,1280]{1,0:T(8,128)(2,1)} %get-tuple-element.20, bf16[128,1280]{1,0:T(8,128)(2,1)} %get-tuple-element.19), kind=kLoop, calls=%fused_computation.36 | loop fusion | flops 1310720 | bytes 1310720 | tf_op jit(solution)/shard_map/concatenate | solution.py:245
  87.1 6.9 %collective-permute-done.19 = bf16[2,128,1280]{2,1,0:T(8,128)(2,1)S(1)} collective-permute-done((bf16[2,128,1280]{2,1,0:T(8,128)(2,1)}, bf16[2,128,1280]{2,1,0:T(8,128)(2,1)S(1)}, u32[]{:S(2)}, u32[]{:S(2)}) %collective-permute-start.19) | collective-permute-done | bytes 655392 | tf_op jit(solution)/shard_map/ppermute | solution.py:16
  94.0 0.7 collective-permute-start.26
  94.8 0.7 fusion.13
  95.5 5.0 %collective-permute-start.21 = (bf16[2,128,1280]{2,1,0:T(8,128)(2,1)S(1)}, bf16[2,128,1280]{2,1,0:T(8,128)(2,1)S(1)}, u32[]{:S(2)}, u32[]{:S(2)}) collective-permute-start(bf16[2,128,1280]{2,1,0:T(8,128)(2,1)S(1)} %get-tuple-element.37), channel_id=1, source_target_pairs={{0,2},{1,3},{2,0},{3,1},{4,6},{5,7},{6,4},{7,5},{8,10},{9,11},{10,... | collective-permute-start | bytes 1966088 | tf_op jit(solution)/shard_map/ppermute | solution.py:16
  100.5 1.3 collective-permute-start.22
  101.8 4.6 %collective-permute-start.23 = (bf16[2,128,1280]{2,1,0:T(8,128)(2,1)S(1)}, bf16[2,128,1280]{2,1,0:T(8,128)(2,1)S(1)}, u32[]{:S(2)}, u32[]{:S(2)}) collective-permute-start(bf16[2,128,1280]{2,1,0:T(8,128)(2,1)S(1)} %get-tuple-element.38), channel_id=1, source_target_pairs={{0,4},{1,5},{2,6},{3,7},{4,8},{5,9},{6,10},{7,11},{8,12},{9,13},{1... | collective-permute-start | bytes 1966088 | tf_op jit(solution)/shard_map/ppermute | solution.py:16
  106.5 0.7 fusion.4
  107.1 2.4 %collective-permute-start.27 = (bf16[2,128,1280]{2,1,0:T(8,128)(2,1)S(1)}, bf16[2,128,1280]{2,1,0:T(8,128)(2,1)S(1)}, u32[]{:S(2)}, u32[]{:S(2)}) collective-permute-start(bf16[2,128,1280]{2,1,0:T(8,128)(2,1)S(1)} %get-tuple-element.40), channel_id=1, source_target_pairs={{0,2},{1,3},{2,0},{3,1},{4,6},{5,7},{6,4},{7,5},{8,10},{9,11},{10,... | collective-permute-start | bytes 1966088 | tf_op jit(solution)/shard_map/ppermute | solution.py:16
  109.6 1.3 collective-permute-start.28
  110.9 5.2 %collective-permute-done.21 = bf16[2,128,1280]{2,1,0:T(8,128)(2,1)S(1)} collective-permute-done((bf16[2,128,1280]{2,1,0:T(8,128)(2,1)S(1)}, bf16[2,128,1280]{2,1,0:T(8,128)(2,1)S(1)}, u32[]{:S(2)}, u32[]{:S(2)}) %collective-permute-start.21) | collective-permute-done | bytes 655392 | tf_op jit(solution)/shard_map/ppermute | solution.py:16
  116.1 3.9 %collective-permute-start.29 = (bf16[2,128,1280]{2,1,0:T(8,128)(2,1)S(1)}, bf16[2,128,1280]{2,1,0:T(8,128)(2,1)S(1)}, u32[]{:S(2)}, u32[]{:S(2)}) collective-permute-start(bf16[2,128,1280]{2,1,0:T(8,128)(2,1)S(1)} %get-tuple-element.41), channel_id=1, source_target_pairs={{0,4},{1,5},{2,6},{3,7},{4,8},{5,9},{6,10},{7,11},{8,12},{9,13},{1... | collective-permute-start | bytes 1966088 | tf_op jit(solution)/shard_map/ppermute | solution.py:16
  120.0 1.4 %collective-permute-done.23 = bf16[2,128,1280]{2,1,0:T(8,128)(2,1)S(1)} collective-permute-done((bf16[2,128,1280]{2,1,0:T(8,128)(2,1)S(1)}, bf16[2,128,1280]{2,1,0:T(8,128)(2,1)S(1)}, u32[]{:S(2)}, u32[]{:S(2)}) %collective-permute-start.23) | collective-permute-done | bytes 655392 | tf_op jit(solution)/shard_map/ppermute | solution.py:16
  121.5 0.4 fusion.17
  121.9 7.9 %collective-permute-done.27 = bf16[2,128,1280]{2,1,0:T(8,128)(2,1)S(1)} collective-permute-done((bf16[2,128,1280]{2,1,0:T(8,128)(2,1)S(1)}, bf16[2,128,1280]{2,1,0:T(8,128)(2,1)S(1)}, u32[]{:S(2)}, u32[]{:S(2)}) %collective-permute-start.27) | collective-permute-done | bytes 655392 | tf_op jit(solution)/shard_map/ppermute | solution.py:16
  129.8 1.9 %collective-permute-done.28 = bf16[2,128,1280]{2,1,0:T(8,128)(2,1)S(1)} collective-permute-done((bf16[2,128,1280]{2,1,0:T(8,128)(2,1)S(1)}, bf16[2,128,1280]{2,1,0:T(8,128)(2,1)S(1)}, u32[]{:S(2)}, u32[]{:S(2)}) %collective-permute-start.28) | collective-permute-done | bytes 655392 | tf_op jit(solution)/shard_map/ppermute | solution.py:16
  131.7 2.2 %collective-permute-done.29 = bf16[2,128,1280]{2,1,0:T(8,128)(2,1)S(1)} collective-permute-done((bf16[2,128,1280]{2,1,0:T(8,128)(2,1)S(1)}, bf16[2,128,1280]{2,1,0:T(8,128)(2,1)S(1)}, u32[]{:S(2)}, u32[]{:S(2)}) %collective-permute-start.29) | collective-permute-done | bytes 655392 | tf_op jit(solution)/shard_map/ppermute | solution.py:16
  133.9 0.4 fusion.8
  134.4 0.9 pad_maximum_fusion.4
  135.3 0.9 pad_maximum_fusion.3
  (67 shorter events, 0.3 us)
Async XLA Ops:
  0.6 11.1 %copy-start = (s32[4,3]{1,0:T(4,128)S(1)}, s32[4,3]{1,0:T(4,128)}, u32[]{:S(2)}) copy-start(s32[4,3]{1,0:T(4,128)} %param.10) | copy-start | bytes 148
  2.0 9.8 %copy-start.18 = (s32[4]{0:T(128)S(1)}, s32[4]{0:T(128)}, u32[]{:S(2)}) copy-start(s32[4]{0:T(128)} %param.11) | copy-start | bytes 52
  2.1 50.9 %copy-start.8 = (bf16[2,128,1280]{2,1,0:T(8,128)(2,1)}, bf16[2,128,1280]{2,1,0:T(8,128)(2,1)S(1)}, u32[]{:S(2)}) copy-start(bf16[2,128,1280]{2,1,0:T(8,128)(2,1)S(1)} %pad_maximum_fusion.refs_0_) | copy-start | bytes 1966084
  2.1 18.6 %collective-permute-start = (bf16[2,128,1280]{2,1,0:T(8,128)(2,1)S(1)}, bf16[2,128,1280]{2,1,0:T(8,128)(2,1)S(1)}, u32[]{:S(2)}, u32[]{:S(2)}) collective-permute-start(bf16[2,128,1280]{2,1,0:T(8,128)(2,1)S(1)} %pad_maximum_fusion.refs_0_), channel_id=1, source_target_pairs={{0,2},{1,3},{2,0},{3,1},{4,6},{5,7},{6,4},{7,5},{8,10},{9,11},{10,... | collective-permute-start | bytes 1966088 | tf_op jit(solution)/shard_map/ppermute | solution.py:16
  5.2 20.4 %collective-permute-start.1 = (bf16[2,128,1280]{2,1,0:T(8,128)(2,1)S(1)}, bf16[2,128,1280]{2,1,0:T(8,128)(2,1)}, u32[]{:S(2)}, u32[]{:S(2)}) collective-permute-start(bf16[2,128,1280]{2,1,0:T(8,128)(2,1)S(1)} %pad_maximum_fusion.refs_0_), channel_id=1, source_target_pairs={{0,4},{1,5},{2,6},{3,7},{4,8},{5,9},{6,10},{7,11},{8,12},{9,13},{1... | collective-permute-start | bytes 1966088 | tf_op jit(solution)/shard_map/ppermute | solution.py:16
  9.5 17.9 %collective-permute-start.2 = (bf16[2,128,1280]{2,1,0:T(8,128)(2,1)S(1)}, bf16[2,128,1280]{2,1,0:T(8,128)(2,1)}, u32[]{:S(2)}, u32[]{:S(2)}) collective-permute-start(bf16[2,128,1280]{2,1,0:T(8,128)(2,1)S(1)} %pad_maximum_fusion.refs_0_), channel_id=1, source_target_pairs={{4,0},{5,1},{6,2},{7,3},{8,4},{9,5},{10,6},{11,7},{12,8},{13,9},{1... | collective-permute-start | bytes 1966088 | tf_op jit(solution)/shard_map/ppermute | solution.py:16
  10.8 16.6 %collective-permute-start.3 = (bf16[2,128,1280]{2,1,0:T(8,128)(2,1)S(1)}, bf16[2,128,1280]{2,1,0:T(8,128)(2,1)}, u32[]{:S(2)}, u32[]{:S(2)}) collective-permute-start(bf16[2,128,1280]{2,1,0:T(8,128)(2,1)S(1)} %pad_maximum_fusion.refs_0_), channel_id=1, source_target_pairs={{0,1},{1,0},{2,3},{3,2},{4,5},{5,4},{6,7},{7,6},{8,9},{9,8},{10,11... | collective-permute-start | bytes 1966088 | tf_op jit(solution)/shard_map/ppermute | solution.py:16
  10.9 56.1 %copy-start.7 = (bf16[2,128,1280]{2,1,0:T(8,128)(2,1)}, bf16[2,128,1280]{2,1,0:T(8,128)(2,1)S(1)}, u32[]{:S(2)}) copy-start(bf16[2,128,1280]{2,1,0:T(8,128)(2,1)S(1)} %pad_maximum_fusion.1.refs_0_) | copy-start | bytes 1966084
  10.9 23.0 %collective-permute-start.9 = (bf16[2,128,1280]{2,1,0:T(8,128)(2,1)S(1)}, bf16[2,128,1280]{2,1,0:T(8,128)(2,1)S(1)}, u32[]{:S(2)}, u32[]{:S(2)}) collective-permute-start(bf16[2,128,1280]{2,1,0:T(8,128)(2,1)S(1)} %pad_maximum_fusion.1.refs_0_), channel_id=1, source_target_pairs={{0,2},{1,3},{2,0},{3,1},{4,6},{5,7},{6,4},{7,5},{8,10},{9,11},{10,... | collective-permute-start | bytes 1966088 | tf_op jit(solution)/shard_map/ppermute | solution.py:16
  20.7 32.2 %copy-start.12 = (bf16[2,128,1280]{2,1,0:T(8,128)(2,1)}, bf16[2,128,1280]{2,1,0:T(8,128)(2,1)S(1)}, u32[]{:S(2)}) copy-start(bf16[2,128,1280]{2,1,0:T(8,128)(2,1)S(1)} %collective-permute-done.refs_1_) | copy-start | bytes 1966084
  20.8 16.1 %collective-permute-start.10 = (bf16[2,128,1280]{2,1,0:T(8,128)(2,1)S(1)}, bf16[2,128,1280]{2,1,0:T(8,128)(2,1)}, u32[]{:S(2)}, u32[]{:S(2)}) collective-permute-start(bf16[2,128,1280]{2,1,0:T(8,128)(2,1)S(1)} %pad_maximum_fusion.1.refs_0_), channel_id=1, source_target_pairs={{0,4},{1,5},{2,6},{3,7},{4,8},{5,9},{6,10},{7,11},{8,12},{9,13},{1... | collective-permute-start | bytes 1966088 | tf_op jit(solution)/shard_map/ppermute | solution.py:16
  25.6 16.3 %collective-permute-start.11 = (bf16[2,128,1280]{2,1,0:T(8,128)(2,1)S(1)}, bf16[2,128,1280]{2,1,0:T(8,128)(2,1)}, u32[]{:S(2)}, u32[]{:S(2)}) collective-permute-start(bf16[2,128,1280]{2,1,0:T(8,128)(2,1)S(1)} %pad_maximum_fusion.1.refs_0_), channel_id=1, source_target_pairs={{4,0},{5,1},{6,2},{7,3},{8,4},{9,5},{10,6},{11,7},{12,8},{13,9},{1... | collective-permute-start | bytes 1966088 | tf_op jit(solution)/shard_map/ppermute | solution.py:16
  27.4 14.5 %collective-permute-start.12 = (bf16[2,128,1280]{2,1,0:T(8,128)(2,1)S(1)}, bf16[2,128,1280]{2,1,0:T(8,128)(2,1)S(1)}, u32[]{:S(2)}, u32[]{:S(2)}) collective-permute-start(bf16[2,128,1280]{2,1,0:T(8,128)(2,1)S(1)} %pad_maximum_fusion.1.refs_0_), channel_id=1, source_target_pairs={{0,1},{1,0},{2,3},{3,2},{4,5},{5,4},{6,7},{7,6},{8,9},{9,8},{10,11... | collective-permute-start | bytes 1966088 | tf_op jit(solution)/shard_map/ppermute | solution.py:16
  27.4 16.9 %collective-permute-start.4 = (bf16[2,128,1280]{2,1,0:T(8,128)(2,1)S(1)}, bf16[2,128,1280]{2,1,0:T(8,128)(2,1)S(1)}, u32[]{:S(2)}, u32[]{:S(2)}) collective-permute-start(bf16[2,128,1280]{2,1,0:T(8,128)(2,1)S(1)} %collective-permute-done.refs_1_), channel_id=1, source_target_pairs={{0,1},{1,0},{2,3},{3,2},{4,5},{5,4},{6,7},{7,6},{8,9},{9,8},{10,11... | collective-permute-start | bytes 1966088 | tf_op jit(solution)/shard_map/ppermute | solution.py:16
  33.9 33.1 %copy-start.11 = (bf16[2,128,1280]{2,1,0:T(8,128)(2,1)}, bf16[2,128,1280]{2,1,0:T(8,128)(2,1)S(1)}, u32[]{:S(2)}) copy-start(bf16[2,128,1280]{2,1,0:T(8,128)(2,1)S(1)} %collective-permute-done.9.refs_1_) | copy-start | bytes 1966084
  33.9 12.9 %collective-permute-start.7 = (bf16[2,128,1280]{2,1,0:T(8,128)(2,1)S(1)}, bf16[2,128,1280]{2,1,0:T(8,128)(2,1)S(1)}, u32[]{:S(2)}, u32[]{:S(2)}) collective-permute-start(bf16[2,128,1280]{2,1,0:T(8,128)(2,1)S(1)} %collective-permute-done.refs_1_), channel_id=1, source_target_pairs={{0,5},{3,6},{4,9},{7,10},{8,13},{11,14},{16,21},{19,22},{20,25},{2... | collective-permute-start | bytes 1966088 | tf_op jit(solution)/shard_map/ppermute | solution.py:16
  36.8 13.3 %collective-permute-start.8 = (bf16[2,128,1280]{2,1,0:T(8,128)(2,1)S(1)}, bf16[2,128,1280]{2,1,0:T(8,128)(2,1)S(1)}, u32[]{:S(2)}, u32[]{:S(2)}) collective-permute-start(bf16[2,128,1280]{2,1,0:T(8,128)(2,1)S(1)} %collective-permute-done.refs_1_), channel_id=1, source_target_pairs={{4,1},{7,2},{8,5},{11,6},{12,9},{15,10},{20,17},{23,18},{24,21},{2... | collective-permute-start | bytes 1966088 | tf_op jit(solution)/shard_map/ppermute | solution.py:16
  41.9 9.7 %collective-permute-start.5 = (bf16[2,128,1280]{2,1,0:T(8,128)(2,1)}, bf16[2,128,1280]{2,1,0:T(8,128)(2,1)S(1)}, u32[]{:S(2)}, u32[]{:S(2)}) collective-permute-start(bf16[2,128,1280]{2,1,0:T(8,128)(2,1)} %collective-permute-done.1.refs_2_), channel_id=1, source_target_pairs={{0,1},{1,0},{2,3},{3,2},{4,5},{5,4},{6,7},{7,6},{8,9},{9,8},{10,11... | collective-permute-start | bytes 1966088 | tf_op jit(solution)/shard_map/ppermute | solution.py:16
  41.9 2.5 %copy-start.13 = (bf16[2,128,1280]{2,1,0:T(8,128)(2,1)}, bf16[2,128,1280]{2,1,0:T(8,128)(2,1)S(1)}, u32[]{:S(2)}) copy-start(bf16[2,128,1280]{2,1,0:T(8,128)(2,1)S(1)} %collective-permute-done.12.refs_4_) | copy-start | bytes 1966084
  41.9 10.6 %collective-permute-start.6 = (bf16[2,128,1280]{2,1,0:T(8,128)(2,1)}, bf16[2,128,1280]{2,1,0:T(8,128)(2,1)}, u32[]{:S(2)}, u32[]{:S(2)}) collective-permute-start(bf16[2,128,1280]{2,1,0:T(8,128)(2,1)} %collective-permute-done.2.refs_3_), channel_id=1, source_target_pairs={{0,1},{1,0},{2,3},{3,2},{4,5},{5,4},{6,7},{7,6},{8,9},{9,8},{10,11... | collective-permute-start | bytes 1966088 | tf_op jit(solution)/shard_map/ppermute | solution.py:16
  44.4 0.8 copy-start.14
  44.4 22.6 %collective-permute-start.13 = (bf16[2,128,1280]{2,1,0:T(8,128)(2,1)S(1)}, bf16[2,128,1280]{2,1,0:T(8,128)(2,1)}, u32[]{:S(2)}, u32[]{:S(2)}) collective-permute-start(bf16[2,128,1280]{2,1,0:T(8,128)(2,1)S(1)} %collective-permute-done.9.refs_1_), channel_id=1, source_target_pairs={{0,1},{1,0},{2,3},{3,2},{4,5},{5,4},{6,7},{7,6},{8,9},{9,8},{10,11... | collective-permute-start | bytes 1966088 | tf_op jit(solution)/shard_map/ppermute | solution.py:16
  46.9 3.2 %copy-start.15 = (bf16[2,128,1280]{2,1,0:T(8,128)(2,1)}, bf16[2,128,1280]{2,1,0:T(8,128)(2,1)S(1)}, u32[]{:S(2)}) copy-start(bf16[2,128,1280]{2,1,0:T(8,128)(2,1)S(1)} %collective-permute-done.7.refs_8_) | copy-start | bytes 1966084
  46.9 20.2 %collective-permute-start.16 = (bf16[2,128,1280]{2,1,0:T(8,128)(2,1)S(1)}, bf16[2,128,1280]{2,1,0:T(8,128)(2,1)}, u32[]{:S(2)}, u32[]{:S(2)}) collective-permute-start(bf16[2,128,1280]{2,1,0:T(8,128)(2,1)S(1)} %collective-permute-done.9.refs_1_), channel_id=1, source_target_pairs={{0,5},{3,6},{4,9},{7,10},{8,13},{11,14},{16,21},{19,22},{20,25},{2... | collective-permute-start | bytes 1966088 | tf_op jit(solution)/shard_map/ppermute | solution.py:16
  50.1 1.5 %copy-start.16 = (bf16[2,128,1280]{2,1,0:T(8,128)(2,1)}, bf16[2,128,1280]{2,1,0:T(8,128)(2,1)S(1)}, u32[]{:S(2)}) copy-start(bf16[2,128,1280]{2,1,0:T(8,128)(2,1)S(1)} %collective-permute-done.8.refs_9_) | copy-start | bytes 1966084
  50.1 17.0 %collective-permute-start.17 = (bf16[2,128,1280]{2,1,0:T(8,128)(2,1)S(1)}, bf16[2,128,1280]{2,1,0:T(8,128)(2,1)}, u32[]{:S(2)}, u32[]{:S(2)}) collective-permute-start(bf16[2,128,1280]{2,1,0:T(8,128)(2,1)S(1)} %collective-permute-done.9.refs_1_), channel_id=1, source_target_pairs={{4,1},{7,2},{8,5},{11,6},{12,9},{15,10},{20,17},{23,18},{24,21},{2... | collective-permute-start | bytes 1966088 | tf_op jit(solution)/shard_map/ppermute | solution.py:16
  51.6 0.8 copy-start.17
  52.4 14.7 %collective-permute-start.14 = (bf16[2,128,1280]{2,1,0:T(8,128)(2,1)}, bf16[2,128,1280]{2,1,0:T(8,128)(2,1)}, u32[]{:S(2)}, u32[]{:S(2)}) collective-permute-start(bf16[2,128,1280]{2,1,0:T(8,128)(2,1)} %collective-permute-done.10.refs_2_), channel_id=1, source_target_pairs={{0,1},{1,0},{2,3},{3,2},{4,5},{5,4},{6,7},{7,6},{8,9},{9,8},{10,11... | collective-permute-start | bytes 1966088 | tf_op jit(solution)/shard_map/ppermute | solution.py:16
  52.4 14.7 %collective-permute-start.15 = (bf16[2,128,1280]{2,1,0:T(8,128)(2,1)}, bf16[2,128,1280]{2,1,0:T(8,128)(2,1)}, u32[]{:S(2)}, u32[]{:S(2)}) collective-permute-start(bf16[2,128,1280]{2,1,0:T(8,128)(2,1)} %collective-permute-done.11.refs_3_), channel_id=1, source_target_pairs={{0,1},{1,0},{2,3},{3,2},{4,5},{5,4},{6,7},{7,6},{8,9},{9,8},{10,11... | collective-permute-start | bytes 1966088 | tf_op jit(solution)/shard_map/ppermute | solution.py:16
  67.0 27.7 %collective-permute-start.18 = (bf16[4,2,128,1280]{3,2,1,0:T(8,128)(2,1)}, bf16[4,2,128,1280]{3,2,1,0:T(8,128)(2,1)S(1)}, u32[]{:S(2)}, u32[]{:S(2)}) collective-permute-start(bf16[4,2,128,1280]{3,2,1,0:T(8,128)(2,1)} %get-tuple-element.22), channel_id=1, source_target_pairs={{0,1},{1,0},{2,3},{3,2},{4,5},{5,4},{6,7},{7,6},{8,9},{9,8},{10,11... | collective-permute-start | bytes 7864328 | tf_op jit(solution)/shard_map/ppermute | solution.py:16
  67.1 27.6 %copy-start.3 = (bf16[2,128,1280]{2,1,0:T(8,128)(2,1)S(1)}, bf16[2,128,1280]{2,1,0:T(8,128)(2,1)}, u32[]{:S(2)}) copy-start(bf16[2,128,1280]{2,1,0:T(8,128)(2,1)} %get-tuple-element.27) | copy-start | bytes 1966084
  81.3 13.4 %copy-start.1 = (bf16[2,128,1280]{2,1,0:T(8,128)(2,1)S(1)}, bf16[2,128,1280]{2,1,0:T(8,128)(2,1)}, u32[]{:S(2)}) copy-start(bf16[2,128,1280]{2,1,0:T(8,128)(2,1)} %get-tuple-element.23) | copy-start | bytes 1966084
  81.3 13.4 %copy-start.2 = (bf16[2,128,1280]{2,1,0:T(8,128)(2,1)S(1)}, bf16[2,128,1280]{2,1,0:T(8,128)(2,1)}, u32[]{:S(2)}) copy-start(bf16[2,128,1280]{2,1,0:T(8,128)(2,1)} %get-tuple-element.26) | copy-start | bytes 1966084
  81.3 25.1 %collective-permute-start.24 = (bf16[4,2,128,1280]{3,2,1,0:T(8,128)(2,1)}, bf16[4,2,128,1280]{3,2,1,0:T(8,128)(2,1)S(1)}, u32[]{:S(2)}, u32[]{:S(2)}) collective-permute-start(bf16[4,2,128,1280]{3,2,1,0:T(8,128)(2,1)} %get-tuple-element.29), channel_id=1, source_target_pairs={{0,1},{1,0},{2,3},{3,2},{4,5},{5,4},{6,7},{7,6},{8,9},{9,8},{10,11... | collective-permute-start | bytes 7864328 | tf_op jit(solution)/shard_map/ppermute | solution.py:16
  81.9 12.1 %collective-permute-start.19 = (bf16[2,128,1280]{2,1,0:T(8,128)(2,1)}, bf16[2,128,1280]{2,1,0:T(8,128)(2,1)S(1)}, u32[]{:S(2)}, u32[]{:S(2)}) collective-permute-start(bf16[2,128,1280]{2,1,0:T(8,128)(2,1)} %get-tuple-element.24), channel_id=1, source_target_pairs={{5,0},{6,3},{9,4},{10,7},{13,8},{14,11},{21,16},{22,19},{25,20},{2... | collective-permute-start | bytes 1966088 | tf_op jit(solution)/shard_map/ppermute | solution.py:16
  83.2 11.5 %collective-permute-start.20 = (bf16[2,128,1280]{2,1,0:T(8,128)(2,1)}, bf16[2,128,1280]{2,1,0:T(8,128)(2,1)S(1)}, u32[]{:S(2)}, u32[]{:S(2)}) collective-permute-start(bf16[2,128,1280]{2,1,0:T(8,128)(2,1)} %get-tuple-element.25), channel_id=1, source_target_pairs={{1,4},{2,7},{5,8},{6,11},{9,12},{10,15},{17,20},{18,23},{21,24},{2... | collective-permute-start | bytes 1966088 | tf_op jit(solution)/shard_map/ppermute | solution.py:16
  83.9 17.9 %collective-permute-start.25 = (bf16[2,128,1280]{2,1,0:T(8,128)(2,1)}, bf16[2,128,1280]{2,1,0:T(8,128)(2,1)S(1)}, u32[]{:S(2)}, u32[]{:S(2)}) collective-permute-start(bf16[2,128,1280]{2,1,0:T(8,128)(2,1)} %get-tuple-element.31), channel_id=1, source_target_pairs={{5,0},{6,3},{9,4},{10,7},{13,8},{14,11},{21,16},{22,19},{25,20},{2... | collective-permute-start | bytes 1966088 | tf_op jit(solution)/shard_map/ppermute | solution.py:16
  94.0 12.4 %collective-permute-start.26 = (bf16[2,128,1280]{2,1,0:T(8,128)(2,1)}, bf16[2,128,1280]{2,1,0:T(8,128)(2,1)S(1)}, u32[]{:S(2)}, u32[]{:S(2)}) collective-permute-start(bf16[2,128,1280]{2,1,0:T(8,128)(2,1)} %get-tuple-element.32), channel_id=1, source_target_pairs={{1,4},{2,7},{5,8},{6,11},{9,12},{10,15},{17,20},{18,23},{21,24},{2... | collective-permute-start | bytes 1966088 | tf_op jit(solution)/shard_map/ppermute | solution.py:16
  94.7 11.7 %copy-start.4 = (bf16[2,128,1280]{2,1,0:T(8,128)(2,1)S(1)}, bf16[2,128,1280]{2,1,0:T(8,128)(2,1)}, u32[]{:S(2)}) copy-start(bf16[2,128,1280]{2,1,0:T(8,128)(2,1)} %get-tuple-element.30) | copy-start | bytes 1966084
  94.8 11.7 %copy-start.5 = (bf16[2,128,1280]{2,1,0:T(8,128)(2,1)S(1)}, bf16[2,128,1280]{2,1,0:T(8,128)(2,1)}, u32[]{:S(2)}) copy-start(bf16[2,128,1280]{2,1,0:T(8,128)(2,1)} %get-tuple-element.33) | copy-start | bytes 1966084
  94.8 11.7 %copy-start.6 = (bf16[2,128,1280]{2,1,0:T(8,128)(2,1)S(1)}, bf16[2,128,1280]{2,1,0:T(8,128)(2,1)}, u32[]{:S(2)}) copy-start(bf16[2,128,1280]{2,1,0:T(8,128)(2,1)} %get-tuple-element.34) | copy-start | bytes 1966084
  95.5 20.6 %collective-permute-start.21 = (bf16[2,128,1280]{2,1,0:T(8,128)(2,1)S(1)}, bf16[2,128,1280]{2,1,0:T(8,128)(2,1)S(1)}, u32[]{:S(2)}, u32[]{:S(2)}) collective-permute-start(bf16[2,128,1280]{2,1,0:T(8,128)(2,1)S(1)} %get-tuple-element.37), channel_id=1, source_target_pairs={{0,2},{1,3},{2,0},{3,1},{4,6},{5,7},{6,4},{7,5},{8,10},{9,11},{10,... | collective-permute-start | bytes 1966088 | tf_op jit(solution)/shard_map/ppermute | solution.py:16
  100.5 19.5 %collective-permute-start.22 = (bf16[2,128,1280]{2,1,0:T(8,128)(2,1)S(1)}, bf16[2,128,1280]{2,1,0:T(8,128)(2,1)S(1)}, u32[]{:S(2)}, u32[]{:S(2)}) collective-permute-start(bf16[2,128,1280]{2,1,0:T(8,128)(2,1)S(1)} %get-tuple-element.39), channel_id=1, source_target_pairs={{4,0},{5,1},{6,2},{7,3},{8,4},{9,5},{10,6},{11,7},{12,8},{13,9},{1... | collective-permute-start | bytes 1966088 | tf_op jit(solution)/shard_map/ppermute | solution.py:16
  101.8 19.7 %collective-permute-start.23 = (bf16[2,128,1280]{2,1,0:T(8,128)(2,1)S(1)}, bf16[2,128,1280]{2,1,0:T(8,128)(2,1)S(1)}, u32[]{:S(2)}, u32[]{:S(2)}) collective-permute-start(bf16[2,128,1280]{2,1,0:T(8,128)(2,1)S(1)} %get-tuple-element.38), channel_id=1, source_target_pairs={{0,4},{1,5},{2,6},{3,7},{4,8},{5,9},{6,10},{7,11},{8,12},{9,13},{1... | collective-permute-start | bytes 1966088 | tf_op jit(solution)/shard_map/ppermute | solution.py:16
  106.4 15.0 %copy-start.9 = (bf16[2,128,1280]{2,1,0:T(8,128)(2,1)S(1)}, bf16[2,128,1280]{2,1,0:T(8,128)(2,1)}, u32[]{:S(2)}) copy-start(bf16[2,128,1280]{2,1,0:T(8,128)(2,1)} %get-tuple-element.21) | copy-start | bytes 1966084
  107.1 22.6 %collective-permute-start.27 = (bf16[2,128,1280]{2,1,0:T(8,128)(2,1)S(1)}, bf16[2,128,1280]{2,1,0:T(8,128)(2,1)S(1)}, u32[]{:S(2)}, u32[]{:S(2)}) collective-permute-start(bf16[2,128,1280]{2,1,0:T(8,128)(2,1)S(1)} %get-tuple-element.40), channel_id=1, source_target_pairs={{0,2},{1,3},{2,0},{3,1},{4,6},{5,7},{6,4},{7,5},{8,10},{9,11},{10,... | collective-permute-start | bytes 1966088 | tf_op jit(solution)/shard_map/ppermute | solution.py:16
  109.6 22.1 %collective-permute-start.28 = (bf16[2,128,1280]{2,1,0:T(8,128)(2,1)S(1)}, bf16[2,128,1280]{2,1,0:T(8,128)(2,1)S(1)}, u32[]{:S(2)}, u32[]{:S(2)}) collective-permute-start(bf16[2,128,1280]{2,1,0:T(8,128)(2,1)S(1)} %get-tuple-element.42), channel_id=1, source_target_pairs={{4,0},{5,1},{6,2},{7,3},{8,4},{9,5},{10,6},{11,7},{12,8},{13,9},{1... | collective-permute-start | bytes 1966088 | tf_op jit(solution)/shard_map/ppermute | solution.py:16
  116.1 17.8 %collective-permute-start.29 = (bf16[2,128,1280]{2,1,0:T(8,128)(2,1)S(1)}, bf16[2,128,1280]{2,1,0:T(8,128)(2,1)S(1)}, u32[]{:S(2)}, u32[]{:S(2)}) collective-permute-start(bf16[2,128,1280]{2,1,0:T(8,128)(2,1)S(1)} %get-tuple-element.41), channel_id=1, source_target_pairs={{0,4},{1,5},{2,6},{3,7},{4,8},{5,9},{6,10},{7,11},{8,12},{9,13},{1... | collective-permute-start | bytes 1966088 | tf_op jit(solution)/shard_map/ppermute | solution.py:16
  121.9 12.0 %copy-start.10 = (bf16[2,128,1280]{2,1,0:T(8,128)(2,1)S(1)}, bf16[2,128,1280]{2,1,0:T(8,128)(2,1)}, u32[]{:S(2)}) copy-start(bf16[2,128,1280]{2,1,0:T(8,128)(2,1)} %get-tuple-element.28) | copy-start | bytes 1966084

commit v19 on v18

--- a/solution.py
+++ b/solution.py
@@ -68,7 +68,7 @@
     return query_inside[:, None] & key_ok[None, :] & nearby
 
 
-def attention_backward(mask, queries, out_grad, inputs, slot_in, out_lead, slot_out, inv_root, offset):
+def attention_backward(mask, queries, out_grad, inputs, slot_in, out_lead, slot_out, inv_root, offset, dq_into):
     rows, channels = inputs[0].shape[-2:]
     heads = channels // HD
     slots = len(slot_in)
@@ -76,8 +76,9 @@
 
     def kernel(mask_ref, q_ref, g_ref, *refs):
         in_refs = refs[:n_in]
-        dq_ref = refs[n_in]
-        out_refs = refs[n_in + 1 :]
+        skip = 0 if dq_into is None else 1
+        dq_ref = refs[n_in + skip]
+        out_refs = refs[n_in + skip + 1 :]
         nt = (((1,), (1,)), ((), ()))
         tn = (((0,), (0,)), ((), ()))
         for j in range(STEP_HEADS):
@@ -115,13 +116,17 @@
         pl.BlockSpec((rows, STEP_HEADS * HD), lambda h: (0, h + offset // STEP_HEADS)),
         pl.BlockSpec((rows, STEP_HEADS * HD), lambda h: (0, h + offset // STEP_HEADS)),
     ] + [head_spec(tuple(x.shape[:-3])) for x in inputs]
-    out_specs = [pl.BlockSpec((rows, STEP_HEADS * HD), lambda h: (0, h))] + [head_spec(lead) for lead in out_lead]
-    out_shape = [jax.ShapeDtypeStruct((rows, channels), jnp.bfloat16)] + [
+    out_specs = [pl.BlockSpec((rows, STEP_HEADS * HD), lambda h: (0, h + offset // STEP_HEADS))] + [head_spec(lead) for lead in out_lead]
+    out_shape = [jax.ShapeDtypeStruct(queries.shape, jnp.bfloat16)] + [
         jax.ShapeDtypeStruct(lead + (2, rows, channels), jnp.bfloat16) for lead in out_lead
     ]
+    extra = [] if dq_into is None else [dq_into]
+    if dq_into is not None:
+        in_specs = in_specs + [pl.BlockSpec(memory_space=pl.ANY)]
     results = pl.pallas_call(
         kernel,
         grid=(heads // STEP_HEADS,),
+        input_output_aliases={} if dq_into is None else {3 + n_in: 0},
         in_specs=in_specs,
         out_specs=out_specs,
         out_shape=out_shape,
@@ -130,7 +135,7 @@
             transcendentals=2 * heads * rows * slots * rows,
             bytes_accessed=2 * 4 * slots * rows * channels + 6 * rows * channels + 4 * rows * slots * rows,
         ),
-    )(mask, queries, out_grad, *inputs)
+    )(mask, queries, out_grad, *inputs, *extra)
     return results[0], results[1:]
 
 
@@ -153,12 +158,12 @@
     return first + relayed + [diag_from_below, diag_from_above]
 
 
-def chunk_kernel(forward_mask, queries, out_grad, inputs, head_offset, inv_root):
+def chunk_kernel(forward_mask, queries, out_grad, inputs, head_offset, inv_root, dq_into):
     slot_in = [(0, ()), (4, ()), (1, ()), (2, ()), (3, ()), (5, ()), (6, ()), (7, ()), (8, ()), (9, ())]
     out_lead = [(), (4,), (), (), (), (), ()]
     slot_out = [(0, ()), (1, (0,)), (2, ()), (3, ()), (4, ()), (1, (1,)), (1, (2,)), (1, (3,)), (5, ()), (6, ())]
     return attention_backward(
-        forward_mask, queries, out_grad, inputs, slot_in, out_lead, slot_out, inv_root, head_offset
+        forward_mask, queries, out_grad, inputs, slot_in, out_lead, slot_out, inv_root, head_offset, dq_into
     )
 
 
@@ -232,7 +237,9 @@
     for c in range(len(starts)):
         seconds.append(forward_second(firsts[c], count, None))
     for c, first in enumerate(starts):
-        dq, parts = chunk_kernel(forward_mask, queries, out_grad, seconds[c], first // HD, inv_root)
+        dq, parts = chunk_kernel(
+            forward_mask, queries, out_grad, seconds[c], first // HD, inv_root, dqs[-1] if dqs else None
+        )
         dqs.append(dq)
         outs.append(parts)
     for c in range(len(starts)):
@@ -242,7 +249,7 @@
         got, summed = return_second(outs[c], backs[c], count, None)
         sums.append(summed)
     grads = [(dqs[c], sums[c][0].astype(jnp.bfloat16), sums[c][1].astype(jnp.bfloat16)) for c in range(len(starts))]
-    query_grad = jnp.concatenate([grad[0] for grad in grads], axis=1)
+    query_grad = dqs[-1]
     key_grad = jnp.concatenate([grad[1] for grad in grads], axis=1)
     value_grad = jnp.concatenate([grad[2] for grad in grads], axis=1)
     return (query_grad, key_grad, value_grad)

time: 137 us -> 137 us (level)
  waiting for transfers between devices: 44.5 us -> 47.6 us
  starting transfers between devices: 48.1 us -> 45.8 us
    ppermute x30, waiting for transfers between devices: 44.5 us -> 47.6 us  [send(): return lax.ppermute(value, 'tm', pairs)]
    ppermute x30, starting transfers between devices: 48.1 us -> 45.8 us  [send(): return lax.ppermute(value, 'tm', pairs)]
    concatenate x1 -> x0, other arithmetic: 1.95 us -> none  [body(): query_grad = jnp.concatenate([grad[0] for grad in grads], axis=1)]
    convert_element_type x2, other arithmetic: 1.38 us -> 2.86 us  [return_second(): cross_sum.astype(jnp.bfloat16)]
where the time goes in v19:
time: 137 us
  waiting for transfers between devices  47.6 us (35%)
  starting transfers between devices  45.8 us (33%)
  Pallas kernels  28.1 us (21%)
  other arithmetic  9.38 us (7%)
  local copies, waits for them, and re-layouts  4.3 us (3%)
    ppermute x30, waiting for transfers between devices, send(): return lax.ppermute(value, 'tm', pairs)  47.6 us
    ppermute x30, starting transfers between devices, send(): return lax.ppermute(value, 'tm', pairs)  45.8 us
    pallas_call x2, Pallas kernels, attention_backward(): pl.pallas_call(kernel, grid=(heads // STEP_HEADS,), input_output_aliases=...  28.1 us
    convert_element_type x2, other arithmetic, return_second(): cross_sum.astype(jnp.bfloat16)  2.86 us
  transfers between devices with their start and end apart: 30, of which 11 were waited for; matrix products, arithmetic and copies ran while one was open for 6% of the time, Pallas kernels for 21%

profile of v19, /device:TPU:0, one launch (start us, length us, event | category | flops | bytes accessed | tf_op | source)
XLA Modules:
  0.0 136.6 jit_solution(14258770662885554801)
XLA Ops:
  0.6 0.0 copy-start
  0.6 1.4 slice_bitcast_fusion.12
  2.0 0.0 copy-start.16
  2.0 0.1 pad_maximum_fusion.1.refs_0_
  2.1 3.1 %collective-permute-start.9 = (bf16[2,128,1280]{2,1,0:T(8,128)(2,1)S(1)}, bf16[2,128,1280]{2,1,0:T(8,128)(2,1)S(1)}, u32[]{:S(2)}, u32[]{:S(2)}) collective-permute-start(bf16[2,128,1280]{2,1,0:T(8,128)(2,1)S(1)} %pad_maximum_fusion.1.refs_0_), channel_id=1, source_target_pairs={{0,2},{1,3},{2,0},{3,1},{4,6},{5,7},{6,4},{7,5},{8,10},{9,11},{10,... | collective-permute-start | bytes 1966088 | tf_op jit(solution)/shard_map/ppermute | solution.py:16
  5.2 4.3 %collective-permute-start.10 = (bf16[2,128,1280]{2,1,0:T(8,128)(2,1)S(1)}, bf16[2,128,1280]{2,1,0:T(8,128)(2,1)}, u32[]{:S(2)}, u32[]{:S(2)}) collective-permute-start(bf16[2,128,1280]{2,1,0:T(8,128)(2,1)S(1)} %pad_maximum_fusion.1.refs_0_), channel_id=1, source_target_pairs={{0,4},{1,5},{2,6},{3,7},{4,8},{5,9},{6,10},{7,11},{8,12},{9,13},{1... | collective-permute-start | bytes 1966088 | tf_op jit(solution)/shard_map/ppermute | solution.py:16
  9.5 1.3 collective-permute-start.11
  10.8 0.1 collective-permute-start.12
  10.9 0.1 pad_maximum_fusion.refs_0_
  10.9 0.0 copy-start.5
  10.9 0.6 collective-permute-start
  11.8 0.6 dynamic_slice.9
  12.5 8.3 %collective-permute-done.9.refs_1_ = bf16[2,128,1280]{2,1,0:T(8,128)(2,1)S(1)} collective-permute-done((bf16[2,128,1280]{2,1,0:T(8,128)(2,1)S(1)}, bf16[2,128,1280]{2,1,0:T(8,128)(2,1)S(1)}, u32[]{:S(2)}, u32[]{:S(2)}) %collective-permute-start.9) | collective-permute-done | bytes 655392 | tf_op jit(solution)/shard_map/ppermute | solution.py:16
  20.8 4.8 %collective-permute-start.1 = (bf16[2,128,1280]{2,1,0:T(8,128)(2,1)S(1)}, bf16[2,128,1280]{2,1,0:T(8,128)(2,1)}, u32[]{:S(2)}, u32[]{:S(2)}) collective-permute-start(bf16[2,128,1280]{2,1,0:T(8,128)(2,1)S(1)} %pad_maximum_fusion.refs_0_), channel_id=1, source_target_pairs={{0,4},{1,5},{2,6},{3,7},{4,8},{5,9},{6,10},{7,11},{8,12},{9,13},{1... | collective-permute-start | bytes 1966088 | tf_op jit(solution)/shard_map/ppermute | solution.py:16
  25.6 0.0 collective-permute-done.10.refs_2_
  25.6 1.3 collective-permute-start.2
  26.9 0.5 collective-permute-done.11.refs_3_
  27.4 0.0 collective-permute-start.3
  27.4 0.6 collective-permute-start.13
  28.0 0.6 fusion.24
  28.7 5.3 %collective-permute-done.refs_1_ = bf16[2,128,1280]{2,1,0:T(8,128)(2,1)S(1)} collective-permute-done((bf16[2,128,1280]{2,1,0:T(8,128)(2,1)S(1)}, bf16[2,128,1280]{2,1,0:T(8,128)(2,1)S(1)}, u32[]{:S(2)}, u32[]{:S(2)}) %collective-permute-start) | collective-permute-done | bytes 655392 | tf_op jit(solution)/shard_map/ppermute | solution.py:16
  33.9 2.4 %collective-permute-start.16 = (bf16[2,128,1280]{2,1,0:T(8,128)(2,1)S(1)}, bf16[2,128,1280]{2,1,0:T(8,128)(2,1)S(1)}, u32[]{:S(2)}, u32[]{:S(2)}) collective-permute-start(bf16[2,128,1280]{2,1,0:T(8,128)(2,1)S(1)} %collective-permute-done.9.refs_1_), channel_id=1, source_target_pairs={{0,5},{3,6},{4,9},{7,10},{8,13},{11,14},{16,21},{19,22},{20,25},{2... | collective-permute-start | bytes 1966088 | tf_op jit(solution)/shard_map/ppermute | solution.py:16
  36.4 0.4 collective-permute-done.1.refs_2_
  36.8 0.7 collective-permute-start.17
  37.5 4.4 %collective-permute-done.2.refs_3_ = bf16[2,128,1280]{2,1,0:T(8,128)(2,1)} collective-permute-done((bf16[2,128,1280]{2,1,0:T(8,128)(2,1)S(1)}, bf16[2,128,1280]{2,1,0:T(8,128)(2,1)}, u32[]{:S(2)}, u32[]{:S(2)}) %collective-permute-start.2) | collective-permute-done | bytes 655392 | tf_op jit(solution)/shard_map/ppermute | solution.py:16
  41.9 0.0 collective-permute-done.3.refs_4_
  41.9 0.5 collective-permute-start.15
  42.4 2.0 %fusion.23 = (pred[1280]{0:T(1024)(128)(4,1)S(1)}, pred[1280]{0:T(1024)(128)(4,1)S(1)}) fusion(s32[1280]{0:T(1024)S(1)} %constant_dynamic-update-slice_fusion, s32[]{:T(128)} %bitcast.3, s32[]{:T(128)} %bitcast.2, s32[]{:T(128)} %bitcast.1, s32[]{:T(128)S(6)} %select_n.64), kind=kLoop, calls=%fused_computation.59 | loop fusion | flops 37120 | bytes 7696 | tf_op jit(solution)/shard_map/and | solution.py:65
  44.4 0.0 collective-permute-done.13.refs_5_
  44.4 0.2 collective-permute-start.4
  44.5 0.7 copy-done.12
  45.2 1.7 %fusion.20.mask_ref = s32[128,1280]{1,0:T(8,128)} fusion(s32[]{:T(128)} %bitcast.4, s32[1280]{0:T(1024)S(1)} %multiply_subtract_fusion, s32[128]{0:T(128)S(1)} %broadcast_subtract_fusion, pred[1280]{0:T(1024)(128)(4,1)S(1)} %get-tuple-element.36, pred[1280]{0:T(1024)(128)(4,1)S(1)} %get-tuple-element.35, pred[128]{0:T(512)(128)(4,1)S(1)} %compare_and_fusion), kind=kLoop, calls=%fused_computation.41 | loop fusion | flops 1146880 | bytes 663684 | tf_op jit(solution)/shard_map/convert_element_type | solution.py:228
  47.0 0.0 collective-permute-done.16.refs_8_
  47.0 3.2 %collective-permute-start.7 = (bf16[2,128,1280]{2,1,0:T(8,128)(2,1)S(1)}, bf16[2,128,1280]{2,1,0:T(8,128)(2,1)}, u32[]{:S(2)}, u32[]{:S(2)}) collective-permute-start(bf16[2,128,1280]{2,1,0:T(8,128)(2,1)S(1)} %collective-permute-done.refs_1_), channel_id=1, source_target_pairs={{0,5},{3,6},{4,9},{7,10},{8,13},{11,14},{16,21},{19,22},{20,25},{2... | collective-permute-start | bytes 1966088 | tf_op jit(solution)/shard_map/ppermute | solution.py:16
  50.2 0.0 collective-permute-done.17.refs_9_
  50.2 1.5 %collective-permute-start.8 = (bf16[2,128,1280]{2,1,0:T(8,128)(2,1)S(1)}, bf16[2,128,1280]{2,1,0:T(8,128)(2,1)}, u32[]{:S(2)}, u32[]{:S(2)}) collective-permute-start(bf16[2,128,1280]{2,1,0:T(8,128)(2,1)S(1)} %collective-permute-done.refs_1_), channel_id=1, source_target_pairs={{4,1},{7,2},{8,5},{11,6},{12,9},{15,10},{20,17},{23,18},{24,21},{2... | collective-permute-start | bytes 1966088 | tf_op jit(solution)/shard_map/ppermute | solution.py:16
  51.7 0.8 copy-done.15
  52.6 0.5 collective-permute-start.6
  53.1 14.0 %shard_map.85 = (bf16[128,2560]{1,0:T(8,128)(2,1)}, bf16[2,128,1280]{2,1,0:T(8,128)(2,1)}, bf16[4,2,128,1280]{3,2,1,0:T(8,128)(2,1)}, bf16[2,128,1280]{2,1,0:T(8...) custom-call(s32[128,1280]{1,0:T(8,128)} %fusion.20.mask_ref, ...), custom_call_target="tpu_custom_call" | custom-call | flops 2516582400 | bytes 14745600 | tf_op jit(solution)/shard_map/pallas_call | solution.py:126
  67.1 0.1 collective-permute-start.18
  67.2 14.1 %shard_map.86 = (bf16[128,2560]{1,0:T(8,128)(2,1)}, bf16[2,128,1280]{2,1,0:T(8,128)(2,1)}, bf16[4,2,128,1280]{3,2,1,0:T(8,128)(2,1)}, bf16[2,128,1280]{2,1,0:T(8...) custom-call(s32[128,1280]{1,0:T(8,128)} %fusion.20.mask_ref, ...), custom_call_target="tpu_custom_call", output_to_operand_aliasing={{0}: (13, {})} | custom-call | flops 2516582400 | bytes 14745600 | tf_op jit(solution)/shard_map/pallas_call | solution.py:126
  81.4 0.5 collective-permute-start.24
  81.9 1.3 collective-permute-start.19
  83.2 0.7 collective-permute-start.20
  83.9 1.3 collective-permute-start.25
  85.2 8.8 %collective-permute-done.19 = bf16[2,128,1280]{2,1,0:T(8,128)(2,1)S(1)} collective-permute-done((bf16[2,128,1280]{2,1,0:T(8,128)(2,1)}, bf16[2,128,1280]{2,1,0:T(8,128)(2,1)S(1)}, u32[]{:S(2)}, u32[]{:S(2)}) %collective-permute-start.19) | collective-permute-done | bytes 655392 | tf_op jit(solution)/shard_map/ppermute | solution.py:16
  94.0 0.7 collective-permute-start.26
  94.8 2.1 %fusion.13 = (bf16[2,128,1280]{2,1,0:T(8,128)(2,1)S(1)}, bf16[2,128,1280]{2,1,0:T(8,128)(2,1)S(1)}, bf16[2,128,1280]{2,1,0:T(8,128)(2,1)S(1)}) fusion(bf16[2,128,1280]{2,1,0:T(8,128)(2,1)S(1)} %collective-permute-done.20, bf16[2,128,1280]{2,1,0:T(8,128)(2,1)S(1)} %collective-permute-done.19, bf16[2,128,1280]{2,1,0:T(8,128)(2,1)S(1)} %copy-done.1, ...), kind=kLoop, calls=%fused_computation.20 | loop fusion | flops 5242880 | bytes 7208960 | tf_op jit(solution)/shard_map/convert_element_type | solution.py:191
  96.9 5.0 %collective-permute-start.21 = (bf16[2,128,1280]{2,1,0:T(8,128)(2,1)S(1)}, bf16[2,128,1280]{2,1,0:T(8,128)(2,1)S(1)}, u32[]{:S(2)}, u32[]{:S(2)}) collective-permute-start(bf16[2,128,1280]{2,1,0:T(8,128)(2,1)S(1)} %get-tuple-element.37), channel_id=1, source_target_pairs={{0,2},{1,3},{2,0},{3,1},{4,6},{5,7},{6,4},{7,5},{8,10},{9,11},{10,... | collective-permute-start | bytes 1966088 | tf_op jit(solution)/shard_map/ppermute | solution.py:16
  101.9 1.3 collective-permute-start.22
  103.2 4.6 %collective-permute-start.23 = (bf16[2,128,1280]{2,1,0:T(8,128)(2,1)S(1)}, bf16[2,128,1280]{2,1,0:T(8,128)(2,1)S(1)}, u32[]{:S(2)}, u32[]{:S(2)}) collective-permute-start(bf16[2,128,1280]{2,1,0:T(8,128)(2,1)S(1)} %get-tuple-element.38), channel_id=1, source_target_pairs={{0,4},{1,5},{2,6},{3,7},{4,8},{5,9},{6,10},{7,11},{8,12},{9,13},{1... | collective-permute-start | bytes 1966088 | tf_op jit(solution)/shard_map/ppermute | solution.py:16
  107.9 0.7 fusion.4
  108.6 0.2 collective-permute-start.27
  108.9 1.3 collective-permute-start.28
  110.1 7.4 %collective-permute-done.21 = bf16[2,128,1280]{2,1,0:T(8,128)(2,1)S(1)} collective-permute-done((bf16[2,128,1280]{2,1,0:T(8,128)(2,1)S(1)}, bf16[2,128,1280]{2,1,0:T(8,128)(2,1)S(1)}, u32[]{:S(2)}, u32[]{:S(2)}) %collective-permute-start.21) | collective-permute-done | bytes 655392 | tf_op jit(solution)/shard_map/ppermute | solution.py:16
  117.5 3.8 %collective-permute-start.29 = (bf16[2,128,1280]{2,1,0:T(8,128)(2,1)S(1)}, bf16[2,128,1280]{2,1,0:T(8,128)(2,1)S(1)}, u32[]{:S(2)}, u32[]{:S(2)}) collective-permute-start(bf16[2,128,1280]{2,1,0:T(8,128)(2,1)S(1)} %get-tuple-element.41), channel_id=1, source_target_pairs={{0,4},{1,5},{2,6},{3,7},{4,8},{5,9},{6,10},{7,11},{8,12},{9,13},{1... | collective-permute-start | bytes 1966088 | tf_op jit(solution)/shard_map/ppermute | solution.py:16
  121.3 0.1 collective-permute-done.22
  121.4 0.4 fusion.17
  121.9 9.3 %collective-permute-done.27 = bf16[2,128,1280]{2,1,0:T(8,128)(2,1)S(1)} collective-permute-done((bf16[2,128,1280]{2,1,0:T(8,128)(2,1)S(1)}, bf16[2,128,1280]{2,1,0:T(8,128)(2,1)S(1)}, u32[]{:S(2)}, u32[]{:S(2)}) %collective-permute-start.27) | collective-permute-done | bytes 655392 | tf_op jit(solution)/shard_map/ppermute | solution.py:16
  131.2 1.9 %collective-permute-done.28 = bf16[2,128,1280]{2,1,0:T(8,128)(2,1)S(1)} collective-permute-done((bf16[2,128,1280]{2,1,0:T(8,128)(2,1)S(1)}, bf16[2,128,1280]{2,1,0:T(8,128)(2,1)S(1)}, u32[]{:S(2)}, u32[]{:S(2)}) %collective-permute-start.28) | collective-permute-done | bytes 655392 | tf_op jit(solution)/shard_map/ppermute | solution.py:16
  133.1 1.2 collective-permute-done.29
  134.3 0.4 fusion.8
  134.8 0.9 pad_maximum_fusion.3
  135.7 0.9 pad_maximum_fusion.2
  (62 shorter events, 0.3 us)
Async XLA Ops:
  0.6 11.1 %copy-start = (s32[4,3]{1,0:T(4,128)S(1)}, s32[4,3]{1,0:T(4,128)}, u32[]{:S(2)}) copy-start(s32[4,3]{1,0:T(4,128)} %param.10) | copy-start | bytes 148
  2.0 9.8 %copy-start.16 = (s32[4]{0:T(128)S(1)}, s32[4]{0:T(128)}, u32[]{:S(2)}) copy-start(s32[4]{0:T(128)} %param.11) | copy-start | bytes 52
  2.1 51.0 %copy-start.6 = (bf16[2,128,1280]{2,1,0:T(8,128)(2,1)}, bf16[2,128,1280]{2,1,0:T(8,128)(2,1)S(1)}, u32[]{:S(2)}) copy-start(bf16[2,128,1280]{2,1,0:T(8,128)(2,1)S(1)} %pad_maximum_fusion.1.refs_0_) | copy-start | bytes 1966084
  2.1 18.6 %collective-permute-start.9 = (bf16[2,128,1280]{2,1,0:T(8,128)(2,1)S(1)}, bf16[2,128,1280]{2,1,0:T(8,128)(2,1)S(1)}, u32[]{:S(2)}, u32[]{:S(2)}) collective-permute-start(bf16[2,128,1280]{2,1,0:T(8,128)(2,1)S(1)} %pad_maximum_fusion.1.refs_0_), channel_id=1, source_target_pairs={{0,2},{1,3},{2,0},{3,1},{4,6},{5,7},{6,4},{7,5},{8,10},{9,11},{10,... | collective-permute-start | bytes 1966088 | tf_op jit(solution)/shard_map/ppermute | solution.py:16
  5.2 20.4 %collective-permute-start.10 = (bf16[2,128,1280]{2,1,0:T(8,128)(2,1)S(1)}, bf16[2,128,1280]{2,1,0:T(8,128)(2,1)}, u32[]{:S(2)}, u32[]{:S(2)}) collective-permute-start(bf16[2,128,1280]{2,1,0:T(8,128)(2,1)S(1)} %pad_maximum_fusion.1.refs_0_), channel_id=1, source_target_pairs={{0,4},{1,5},{2,6},{3,7},{4,8},{5,9},{6,10},{7,11},{8,12},{9,13},{1... | collective-permute-start | bytes 1966088 | tf_op jit(solution)/shard_map/ppermute | solution.py:16
  9.5 17.9 %collective-permute-start.11 = (bf16[2,128,1280]{2,1,0:T(8,128)(2,1)S(1)}, bf16[2,128,1280]{2,1,0:T(8,128)(2,1)}, u32[]{:S(2)}, u32[]{:S(2)}) collective-permute-start(bf16[2,128,1280]{2,1,0:T(8,128)(2,1)S(1)} %pad_maximum_fusion.1.refs_0_), channel_id=1, source_target_pairs={{4,0},{5,1},{6,2},{7,3},{8,4},{9,5},{10,6},{11,7},{12,8},{13,9},{1... | collective-permute-start | bytes 1966088 | tf_op jit(solution)/shard_map/ppermute | solution.py:16
  10.8 16.6 %collective-permute-start.12 = (bf16[2,128,1280]{2,1,0:T(8,128)(2,1)S(1)}, bf16[2,128,1280]{2,1,0:T(8,128)(2,1)}, u32[]{:S(2)}, u32[]{:S(2)}) collective-permute-start(bf16[2,128,1280]{2,1,0:T(8,128)(2,1)S(1)} %pad_maximum_fusion.1.refs_0_), channel_id=1, source_target_pairs={{0,1},{1,0},{2,3},{3,2},{4,5},{5,4},{6,7},{7,6},{8,9},{9,8},{10,11... | collective-permute-start | bytes 1966088 | tf_op jit(solution)/shard_map/ppermute | solution.py:16
  10.9 56.1 %copy-start.5 = (bf16[2,128,1280]{2,1,0:T(8,128)(2,1)}, bf16[2,128,1280]{2,1,0:T(8,128)(2,1)S(1)}, u32[]{:S(2)}) copy-start(bf16[2,128,1280]{2,1,0:T(8,128)(2,1)S(1)} %pad_maximum_fusion.refs_0_) | copy-start | bytes 1966084
  10.9 23.0 %collective-permute-start = (bf16[2,128,1280]{2,1,0:T(8,128)(2,1)S(1)}, bf16[2,128,1280]{2,1,0:T(8,128)(2,1)S(1)}, u32[]{:S(2)}, u32[]{:S(2)}) collective-permute-start(bf16[2,128,1280]{2,1,0:T(8,128)(2,1)S(1)} %pad_maximum_fusion.refs_0_), channel_id=1, source_target_pairs={{0,2},{1,3},{2,0},{3,1},{4,6},{5,7},{6,4},{7,5},{8,10},{9,11},{10,... | collective-permute-start | bytes 1966088 | tf_op jit(solution)/shard_map/ppermute | solution.py:16
  20.7 32.3 %copy-start.10 = (bf16[2,128,1280]{2,1,0:T(8,128)(2,1)}, bf16[2,128,1280]{2,1,0:T(8,128)(2,1)S(1)}, u32[]{:S(2)}) copy-start(bf16[2,128,1280]{2,1,0:T(8,128)(2,1)S(1)} %collective-permute-done.9.refs_1_) | copy-start | bytes 1966084
  20.8 16.1 %collective-permute-start.1 = (bf16[2,128,1280]{2,1,0:T(8,128)(2,1)S(1)}, bf16[2,128,1280]{2,1,0:T(8,128)(2,1)}, u32[]{:S(2)}, u32[]{:S(2)}) collective-permute-start(bf16[2,128,1280]{2,1,0:T(8,128)(2,1)S(1)} %pad_maximum_fusion.refs_0_), channel_id=1, source_target_pairs={{0,4},{1,5},{2,6},{3,7},{4,8},{5,9},{6,10},{7,11},{8,12},{9,13},{1... | collective-permute-start | bytes 1966088 | tf_op jit(solution)/shard_map/ppermute | solution.py:16
  25.6 16.3 %collective-permute-start.2 = (bf16[2,128,1280]{2,1,0:T(8,128)(2,1)S(1)}, bf16[2,128,1280]{2,1,0:T(8,128)(2,1)}, u32[]{:S(2)}, u32[]{:S(2)}) collective-permute-start(bf16[2,128,1280]{2,1,0:T(8,128)(2,1)S(1)} %pad_maximum_fusion.refs_0_), channel_id=1, source_target_pairs={{4,0},{5,1},{6,2},{7,3},{8,4},{9,5},{10,6},{11,7},{12,8},{13,9},{1... | collective-permute-start | bytes 1966088 | tf_op jit(solution)/shard_map/ppermute | solution.py:16
  27.4 14.5 %collective-permute-start.3 = (bf16[2,128,1280]{2,1,0:T(8,128)(2,1)S(1)}, bf16[2,128,1280]{2,1,0:T(8,128)(2,1)S(1)}, u32[]{:S(2)}, u32[]{:S(2)}) collective-permute-start(bf16[2,128,1280]{2,1,0:T(8,128)(2,1)S(1)} %pad_maximum_fusion.refs_0_), channel_id=1, source_target_pairs={{0,1},{1,0},{2,3},{3,2},{4,5},{5,4},{6,7},{7,6},{8,9},{9,8},{10,11... | collective-permute-start | bytes 1966088 | tf_op jit(solution)/shard_map/ppermute | solution.py:16
  27.4 16.9 %collective-permute-start.13 = (bf16[2,128,1280]{2,1,0:T(8,128)(2,1)S(1)}, bf16[2,128,1280]{2,1,0:T(8,128)(2,1)S(1)}, u32[]{:S(2)}, u32[]{:S(2)}) collective-permute-start(bf16[2,128,1280]{2,1,0:T(8,128)(2,1)S(1)} %collective-permute-done.9.refs_1_), channel_id=1, source_target_pairs={{0,1},{1,0},{2,3},{3,2},{4,5},{5,4},{6,7},{7,6},{8,9},{9,8},{10,11... | collective-permute-start | bytes 1966088 | tf_op jit(solution)/shard_map/ppermute | solution.py:16
  33.9 33.1 %copy-start.9 = (bf16[2,128,1280]{2,1,0:T(8,128)(2,1)}, bf16[2,128,1280]{2,1,0:T(8,128)(2,1)S(1)}, u32[]{:S(2)}) copy-start(bf16[2,128,1280]{2,1,0:T(8,128)(2,1)S(1)} %collective-permute-done.refs_1_) | copy-start | bytes 1966084
  33.9 13.0 %collective-permute-start.16 = (bf16[2,128,1280]{2,1,0:T(8,128)(2,1)S(1)}, bf16[2,128,1280]{2,1,0:T(8,128)(2,1)S(1)}, u32[]{:S(2)}, u32[]{:S(2)}) collective-permute-start(bf16[2,128,1280]{2,1,0:T(8,128)(2,1)S(1)} %collective-permute-done.9.refs_1_), channel_id=1, source_target_pairs={{0,5},{3,6},{4,9},{7,10},{8,13},{11,14},{16,21},{19,22},{20,25},{2... | collective-permute-start | bytes 1966088 | tf_op jit(solution)/shard_map/ppermute | solution.py:16
  36.8 13.4 %collective-permute-start.17 = (bf16[2,128,1280]{2,1,0:T(8,128)(2,1)S(1)}, bf16[2,128,1280]{2,1,0:T(8,128)(2,1)S(1)}, u32[]{:S(2)}, u32[]{:S(2)}) collective-permute-start(bf16[2,128,1280]{2,1,0:T(8,128)(2,1)S(1)} %collective-permute-done.9.refs_1_), channel_id=1, source_target_pairs={{4,1},{7,2},{8,5},{11,6},{12,9},{15,10},{20,17},{23,18},{24,21},{2... | collective-permute-start | bytes 1966088 | tf_op jit(solution)/shard_map/ppermute | solution.py:16
  41.9 9.8 %collective-permute-start.14 = (bf16[2,128,1280]{2,1,0:T(8,128)(2,1)}, bf16[2,128,1280]{2,1,0:T(8,128)(2,1)S(1)}, u32[]{:S(2)}, u32[]{:S(2)}) collective-permute-start(bf16[2,128,1280]{2,1,0:T(8,128)(2,1)} %collective-permute-done.10.refs_2_), channel_id=1, source_target_pairs={{0,1},{1,0},{2,3},{3,2},{4,5},{5,4},{6,7},{7,6},{8,9},{9,8},{10,11... | collective-permute-start | bytes 1966088 | tf_op jit(solution)/shard_map/ppermute | solution.py:16
  41.9 2.5 %copy-start.11 = (bf16[2,128,1280]{2,1,0:T(8,128)(2,1)}, bf16[2,128,1280]{2,1,0:T(8,128)(2,1)S(1)}, u32[]{:S(2)}) copy-start(bf16[2,128,1280]{2,1,0:T(8,128)(2,1)S(1)} %collective-permute-done.3.refs_4_) | copy-start | bytes 1966084
  41.9 10.7 %collective-permute-start.15 = (bf16[2,128,1280]{2,1,0:T(8,128)(2,1)}, bf16[2,128,1280]{2,1,0:T(8,128)(2,1)}, u32[]{:S(2)}, u32[]{:S(2)}) collective-permute-start(bf16[2,128,1280]{2,1,0:T(8,128)(2,1)} %collective-permute-done.11.refs_3_), channel_id=1, source_target_pairs={{0,1},{1,0},{2,3},{3,2},{4,5},{5,4},{6,7},{7,6},{8,9},{9,8},{10,11... | collective-permute-start | bytes 1966088 | tf_op jit(solution)/shard_map/ppermute | solution.py:16
  44.4 0.8 copy-start.12
  44.4 22.7 %collective-permute-start.4 = (bf16[2,128,1280]{2,1,0:T(8,128)(2,1)S(1)}, bf16[2,128,1280]{2,1,0:T(8,128)(2,1)}, u32[]{:S(2)}, u32[]{:S(2)}) collective-permute-start(bf16[2,128,1280]{2,1,0:T(8,128)(2,1)S(1)} %collective-permute-done.refs_1_), channel_id=1, source_target_pairs={{0,1},{1,0},{2,3},{3,2},{4,5},{5,4},{6,7},{7,6},{8,9},{9,8},{10,11... | collective-permute-start | bytes 1966088 | tf_op jit(solution)/shard_map/ppermute | solution.py:16
  47.0 3.2 %copy-start.13 = (bf16[2,128,1280]{2,1,0:T(8,128)(2,1)}, bf16[2,128,1280]{2,1,0:T(8,128)(2,1)S(1)}, u32[]{:S(2)}) copy-start(bf16[2,128,1280]{2,1,0:T(8,128)(2,1)S(1)} %collective-permute-done.16.refs_8_) | copy-start | bytes 1966084
  47.0 20.2 %collective-permute-start.7 = (bf16[2,128,1280]{2,1,0:T(8,128)(2,1)S(1)}, bf16[2,128,1280]{2,1,0:T(8,128)(2,1)}, u32[]{:S(2)}, u32[]{:S(2)}) collective-permute-start(bf16[2,128,1280]{2,1,0:T(8,128)(2,1)S(1)} %collective-permute-done.refs_1_), channel_id=1, source_target_pairs={{0,5},{3,6},{4,9},{7,10},{8,13},{11,14},{16,21},{19,22},{20,25},{2... | collective-permute-start | bytes 1966088 | tf_op jit(solution)/shard_map/ppermute | solution.py:16
  50.2 1.5 %copy-start.14 = (bf16[2,128,1280]{2,1,0:T(8,128)(2,1)}, bf16[2,128,1280]{2,1,0:T(8,128)(2,1)S(1)}, u32[]{:S(2)}) copy-start(bf16[2,128,1280]{2,1,0:T(8,128)(2,1)S(1)} %collective-permute-done.17.refs_9_) | copy-start | bytes 1966084
  50.2 17.0 %collective-permute-start.8 = (bf16[2,128,1280]{2,1,0:T(8,128)(2,1)S(1)}, bf16[2,128,1280]{2,1,0:T(8,128)(2,1)}, u32[]{:S(2)}, u32[]{:S(2)}) collective-permute-start(bf16[2,128,1280]{2,1,0:T(8,128)(2,1)S(1)} %collective-permute-done.refs_1_), channel_id=1, source_target_pairs={{4,1},{7,2},{8,5},{11,6},{12,9},{15,10},{20,17},{23,18},{24,21},{2... | collective-permute-start | bytes 1966088 | tf_op jit(solution)/shard_map/ppermute | solution.py:16
  51.7 0.9 copy-start.15
  52.5 14.7 %collective-permute-start.5 = (bf16[2,128,1280]{2,1,0:T(8,128)(2,1)}, bf16[2,128,1280]{2,1,0:T(8,128)(2,1)}, u32[]{:S(2)}, u32[]{:S(2)}) collective-permute-start(bf16[2,128,1280]{2,1,0:T(8,128)(2,1)} %collective-permute-done.1.refs_2_), channel_id=1, source_target_pairs={{0,1},{1,0},{2,3},{3,2},{4,5},{5,4},{6,7},{7,6},{8,9},{9,8},{10,11... | collective-permute-start | bytes 1966088 | tf_op jit(solution)/shard_map/ppermute | solution.py:16
  52.6 14.7 %collective-permute-start.6 = (bf16[2,128,1280]{2,1,0:T(8,128)(2,1)}, bf16[2,128,1280]{2,1,0:T(8,128)(2,1)}, u32[]{:S(2)}, u32[]{:S(2)}) collective-permute-start(bf16[2,128,1280]{2,1,0:T(8,128)(2,1)} %collective-permute-done.2.refs_3_), channel_id=1, source_target_pairs={{0,1},{1,0},{2,3},{3,2},{4,5},{5,4},{6,7},{7,6},{8,9},{9,8},{10,11... | collective-permute-start | bytes 1966088 | tf_op jit(solution)/shard_map/ppermute | solution.py:16
  67.1 27.6 %collective-permute-start.18 = (bf16[4,2,128,1280]{3,2,1,0:T(8,128)(2,1)}, bf16[4,2,128,1280]{3,2,1,0:T(8,128)(2,1)S(1)}, u32[]{:S(2)}, u32[]{:S(2)}) collective-permute-start(bf16[4,2,128,1280]{3,2,1,0:T(8,128)(2,1)} %get-tuple-element.22), channel_id=1, source_target_pairs={{0,1},{1,0},{2,3},{3,2},{4,5},{5,4},{6,7},{7,6},{8,9},{9,8},{10,11... | collective-permute-start | bytes 7864328 | tf_op jit(solution)/shard_map/ppermute | solution.py:16
  67.2 27.5 %copy-start.1 = (bf16[2,128,1280]{2,1,0:T(8,128)(2,1)S(1)}, bf16[2,128,1280]{2,1,0:T(8,128)(2,1)}, u32[]{:S(2)}) copy-start(bf16[2,128,1280]{2,1,0:T(8,128)(2,1)} %get-tuple-element.23) | copy-start | bytes 1966084
  81.4 26.5 %collective-permute-start.24 = (bf16[4,2,128,1280]{3,2,1,0:T(8,128)(2,1)}, bf16[4,2,128,1280]{3,2,1,0:T(8,128)(2,1)S(1)}, u32[]{:S(2)}, u32[]{:S(2)}) collective-permute-start(bf16[4,2,128,1280]{3,2,1,0:T(8,128)(2,1)} %get-tuple-element.29), channel_id=1, source_target_pairs={{0,1},{1,0},{2,3},{3,2},{4,5},{5,4},{6,7},{7,6},{8,9},{9,8},{10,11... | collective-permute-start | bytes 7864328 | tf_op jit(solution)/shard_map/ppermute | solution.py:16
  81.9 12.1 %collective-permute-start.19 = (bf16[2,128,1280]{2,1,0:T(8,128)(2,1)}, bf16[2,128,1280]{2,1,0:T(8,128)(2,1)S(1)}, u32[]{:S(2)}, u32[]{:S(2)}) collective-permute-start(bf16[2,128,1280]{2,1,0:T(8,128)(2,1)} %get-tuple-element.24), channel_id=1, source_target_pairs={{5,0},{6,3},{9,4},{10,7},{13,8},{14,11},{21,16},{22,19},{25,20},{2... | collective-permute-start | bytes 1966088 | tf_op jit(solution)/shard_map/ppermute | solution.py:16
  83.2 11.5 %collective-permute-start.20 = (bf16[2,128,1280]{2,1,0:T(8,128)(2,1)}, bf16[2,128,1280]{2,1,0:T(8,128)(2,1)S(1)}, u32[]{:S(2)}, u32[]{:S(2)}) collective-permute-start(bf16[2,128,1280]{2,1,0:T(8,128)(2,1)} %get-tuple-element.25), channel_id=1, source_target_pairs={{1,4},{2,7},{5,8},{6,11},{9,12},{10,15},{17,20},{18,23},{21,24},{2... | collective-permute-start | bytes 1966088 | tf_op jit(solution)/shard_map/ppermute | solution.py:16
  83.9 19.3 %collective-permute-start.25 = (bf16[2,128,1280]{2,1,0:T(8,128)(2,1)}, bf16[2,128,1280]{2,1,0:T(8,128)(2,1)S(1)}, u32[]{:S(2)}, u32[]{:S(2)}) collective-permute-start(bf16[2,128,1280]{2,1,0:T(8,128)(2,1)} %get-tuple-element.31), channel_id=1, source_target_pairs={{5,0},{6,3},{9,4},{10,7},{13,8},{14,11},{21,16},{22,19},{25,20},{2... | collective-permute-start | bytes 1966088 | tf_op jit(solution)/shard_map/ppermute | solution.py:16
  94.0 13.8 %collective-permute-start.26 = (bf16[2,128,1280]{2,1,0:T(8,128)(2,1)}, bf16[2,128,1280]{2,1,0:T(8,128)(2,1)S(1)}, u32[]{:S(2)}, u32[]{:S(2)}) collective-permute-start(bf16[2,128,1280]{2,1,0:T(8,128)(2,1)} %get-tuple-element.32), channel_id=1, source_target_pairs={{1,4},{2,7},{5,8},{6,11},{9,12},{10,15},{17,20},{18,23},{21,24},{2... | collective-permute-start | bytes 1966088 | tf_op jit(solution)/shard_map/ppermute | solution.py:16
  94.7 13.1 %copy-start.2 = (bf16[2,128,1280]{2,1,0:T(8,128)(2,1)S(1)}, bf16[2,128,1280]{2,1,0:T(8,128)(2,1)}, u32[]{:S(2)}) copy-start(bf16[2,128,1280]{2,1,0:T(8,128)(2,1)} %get-tuple-element.30) | copy-start | bytes 1966084
  94.7 13.1 %copy-start.3 = (bf16[2,128,1280]{2,1,0:T(8,128)(2,1)S(1)}, bf16[2,128,1280]{2,1,0:T(8,128)(2,1)}, u32[]{:S(2)}) copy-start(bf16[2,128,1280]{2,1,0:T(8,128)(2,1)} %get-tuple-element.33) | copy-start | bytes 1966084
  94.8 13.1 %copy-start.4 = (bf16[2,128,1280]{2,1,0:T(8,128)(2,1)S(1)}, bf16[2,128,1280]{2,1,0:T(8,128)(2,1)}, u32[]{:S(2)}) copy-start(bf16[2,128,1280]{2,1,0:T(8,128)(2,1)} %get-tuple-element.34) | copy-start | bytes 1966084
  96.9 20.6 %collective-permute-start.21 = (bf16[2,128,1280]{2,1,0:T(8,128)(2,1)S(1)}, bf16[2,128,1280]{2,1,0:T(8,128)(2,1)S(1)}, u32[]{:S(2)}, u32[]{:S(2)}) collective-permute-start(bf16[2,128,1280]{2,1,0:T(8,128)(2,1)S(1)} %get-tuple-element.37), channel_id=1, source_target_pairs={{0,2},{1,3},{2,0},{3,1},{4,6},{5,7},{6,4},{7,5},{8,10},{9,11},{10,... | collective-permute-start | bytes 1966088 | tf_op jit(solution)/shard_map/ppermute | solution.py:16
  101.9 19.5 %collective-permute-start.22 = (bf16[2,128,1280]{2,1,0:T(8,128)(2,1)S(1)}, bf16[2,128,1280]{2,1,0:T(8,128)(2,1)S(1)}, u32[]{:S(2)}, u32[]{:S(2)}) collective-permute-start(bf16[2,128,1280]{2,1,0:T(8,128)(2,1)S(1)} %get-tuple-element.39), channel_id=1, source_target_pairs={{4,0},{5,1},{6,2},{7,3},{8,4},{9,5},{10,6},{11,7},{12,8},{13,9},{1... | collective-permute-start | bytes 1966088 | tf_op jit(solution)/shard_map/ppermute | solution.py:16
  103.2 18.2 %collective-permute-start.23 = (bf16[2,128,1280]{2,1,0:T(8,128)(2,1)S(1)}, bf16[2,128,1280]{2,1,0:T(8,128)(2,1)S(1)}, u32[]{:S(2)}, u32[]{:S(2)}) collective-permute-start(bf16[2,128,1280]{2,1,0:T(8,128)(2,1)S(1)} %get-tuple-element.38), channel_id=1, source_target_pairs={{0,4},{1,5},{2,6},{3,7},{4,8},{5,9},{6,10},{7,11},{8,12},{9,13},{1... | collective-permute-start | bytes 1966088 | tf_op jit(solution)/shard_map/ppermute | solution.py:16
  107.9 13.5 %copy-start.7 = (bf16[2,128,1280]{2,1,0:T(8,128)(2,1)S(1)}, bf16[2,128,1280]{2,1,0:T(8,128)(2,1)}, u32[]{:S(2)}) copy-start(bf16[2,128,1280]{2,1,0:T(8,128)(2,1)} %get-tuple-element.21) | copy-start | bytes 1966084
  108.6 22.6 %collective-permute-start.27 = (bf16[2,128,1280]{2,1,0:T(8,128)(2,1)S(1)}, bf16[2,128,1280]{2,1,0:T(8,128)(2,1)S(1)}, u32[]{:S(2)}, u32[]{:S(2)}) collective-permute-start(bf16[2,128,1280]{2,1,0:T(8,128)(2,1)S(1)} %get-tuple-element.40), channel_id=1, source_target_pairs={{0,2},{1,3},{2,0},{3,1},{4,6},{5,7},{6,4},{7,5},{8,10},{9,11},{10,... | collective-permute-start | bytes 1966088 | tf_op jit(solution)/shard_map/ppermute | solution.py:16
  108.9 24.3 %collective-permute-start.28 = (bf16[2,128,1280]{2,1,0:T(8,128)(2,1)S(1)}, bf16[2,128,1280]{2,1,0:T(8,128)(2,1)S(1)}, u32[]{:S(2)}, u32[]{:S(2)}) collective-permute-start(bf16[2,128,1280]{2,1,0:T(8,128)(2,1)S(1)} %get-tuple-element.42), channel_id=1, source_target_pairs={{4,0},{5,1},{6,2},{7,3},{8,4},{9,5},{10,6},{11,7},{12,8},{13,9},{1... | collective-permute-start | bytes 1966088 | tf_op jit(solution)/shard_map/ppermute | solution.py:16
  117.5 16.8 %collective-permute-start.29 = (bf16[2,128,1280]{2,1,0:T(8,128)(2,1)S(1)}, bf16[2,128,1280]{2,1,0:T(8,128)(2,1)S(1)}, u32[]{:S(2)}, u32[]{:S(2)}) collective-permute-start(bf16[2,128,1280]{2,1,0:T(8,128)(2,1)S(1)} %get-tuple-element.41), channel_id=1, source_target_pairs={{0,4},{1,5},{2,6},{3,7},{4,8},{5,9},{6,10},{7,11},{8,12},{9,13},{1... | collective-permute-start | bytes 1966088 | tf_op jit(solution)/shard_map/ppermute | solution.py:16
  121.9 12.4 %copy-start.8 = (bf16[2,128,1280]{2,1,0:T(8,128)(2,1)S(1)}, bf16[2,128,1280]{2,1,0:T(8,128)(2,1)}, u32[]{:S(2)}) copy-start(bf16[2,128,1280]{2,1,0:T(8,128)(2,1)} %get-tuple-element.28) | copy-start | bytes 1966084

commit v20 on v18

--- a/solution.py
+++ b/solution.py
@@ -228,6 +228,8 @@
     firsts, seconds, outs, backs, sums, dqs = [], [], [], [], [], []
     for c, first in enumerate(starts):
         own = jnp.stack([keys[:, first : first + width], values[:, first : first + width]])
+        if c == 0:
+            (keys, values), _ = lax.optimization_barrier(((keys, values), own))
         firsts.append(forward_relay(own, count, None))
     for c in range(len(starts)):
         seconds.append(forward_second(firsts[c], count, None))

time: 137 us -> 138 us (level)
  transfers between devices with their start and end apart: 30 -> 30, of which waited for: 11 -> 12; matrix products, arithmetic and copies ran while one was open for 6% -> 7% of each run, Pallas kernels for 21% -> 21%
where the time goes in v20:
time: 138 us; the launch traced here: 137 us
  starting transfers between devices  48.1 us (35%)
  waiting for transfers between devices  44.4 us (32%)
  Pallas kernels  28.2 us (20%)
  other arithmetic  9.84 us (7%)
  local copies, waits for them, and re-layouts  5.05 us (4%)
  between operations  1.42 us (1%)
    ppermute x30, starting transfers between devices, send(): return lax.ppermute(value, 'tm', pairs)  48.1 us
    ppermute x30, waiting for transfers between devices, send(): return lax.ppermute(value, 'tm', pairs)  44.4 us
    pallas_call x2, Pallas kernels, attention_backward(): pl.pallas_call(kernel, grid=(heads // STEP_HEADS,), in_specs=in_specs, ou...  28.2 us
  transfers between devices with their start and end apart: 30, of which 12 were waited for; matrix products, arithmetic and copies ran while one was open for 7% of the time, Pallas kernels for 21%

profile of v20, /device:TPU:0, one launch (start us, length us, event | category | flops | bytes accessed | tf_op | source)
XLA Modules:
  0.0 137.0 jit_solution(3685348554005679364)
XLA Ops:
  0.6 0.0 copy-start
  0.7 1.2 slice_bitcast_fusion.14
  1.8 0.0 copy-start.8
  1.9 0.1 pad_maximum_fusion.refs_0_
  1.9 0.0 copy-start.21
  1.9 3.1 %collective-permute-start = (bf16[2,128,1280]{2,1,0:T(8,128)(2,1)S(1)}, bf16[2,128,1280]{2,1,0:T(8,128)(2,1)S(1)}, u32[]{:S(2)}, u32[]{:S(2)}) collective-permute-start(bf16[2,128,1280]{2,1,0:T(8,128)(2,1)S(1)} %pad_maximum_fusion.refs_0_), channel_id=1, source_target_pairs={{0,2},{1,3},{2,0},{3,1},{4,6},{5,7},{6,4},{7,5},{8,10},{9,11},{10,... | collective-permute-start | bytes 1966088 | tf_op jit(solution)/shard_map/ppermute | solution.py:16
  5.0 4.3 %collective-permute-start.1 = (bf16[2,128,1280]{2,1,0:T(8,128)(2,1)S(1)}, bf16[2,128,1280]{2,1,0:T(8,128)(2,1)}, u32[]{:S(2)}, u32[]{:S(2)}) collective-permute-start(bf16[2,128,1280]{2,1,0:T(8,128)(2,1)S(1)} %pad_maximum_fusion.refs_0_), channel_id=1, source_target_pairs={{0,4},{1,5},{2,6},{3,7},{4,8},{5,9},{6,10},{7,11},{8,12},{9,13},{1... | collective-permute-start | bytes 1966088 | tf_op jit(solution)/shard_map/ppermute | solution.py:16
  9.3 1.3 collective-permute-start.2
  10.6 0.1 collective-permute-start.3
  10.8 0.1 pad_maximum_fusion.1.refs_0_
  10.8 0.0 copy-start.9
  10.8 0.7 collective-permute-start.9
  11.8 0.6 dynamic_slice.9
  12.5 8.1 %collective-permute-done.refs_1_ = bf16[2,128,1280]{2,1,0:T(8,128)(2,1)S(1)} collective-permute-done((bf16[2,128,1280]{2,1,0:T(8,128)(2,1)S(1)}, bf16[2,128,1280]{2,1,0:T(8,128)(2,1)S(1)}, u32[]{:S(2)}, u32[]{:S(2)}) %collective-permute-start) | collective-permute-done | bytes 655392 | tf_op jit(solution)/shard_map/ppermute | solution.py:16
  20.6 4.8 %collective-permute-start.10 = (bf16[2,128,1280]{2,1,0:T(8,128)(2,1)S(1)}, bf16[2,128,1280]{2,1,0:T(8,128)(2,1)}, u32[]{:S(2)}, u32[]{:S(2)}) collective-permute-start(bf16[2,128,1280]{2,1,0:T(8,128)(2,1)S(1)} %pad_maximum_fusion.1.refs_0_), channel_id=1, source_target_pairs={{0,4},{1,5},{2,6},{3,7},{4,8},{5,9},{6,10},{7,11},{8,12},{9,13},{1... | collective-permute-start | bytes 1966088 | tf_op jit(solution)/shard_map/ppermute | solution.py:16
  25.4 1.3 collective-permute-start.11
  26.7 0.5 collective-permute-done.2.refs_3_
  27.3 0.6 collective-permute-start.4
  27.8 0.7 fusion.24
  28.5 5.3 %collective-permute-done.9.refs_1_ = bf16[2,128,1280]{2,1,0:T(8,128)(2,1)S(1)} collective-permute-done((bf16[2,128,1280]{2,1,0:T(8,128)(2,1)S(1)}, bf16[2,128,1280]{2,1,0:T(8,128)(2,1)S(1)}, u32[]{:S(2)}, u32[]{:S(2)}) %collective-permute-start.9) | collective-permute-done | bytes 655392 | tf_op jit(solution)/shard_map/ppermute | solution.py:16
  33.8 2.4 %collective-permute-start.7 = (bf16[2,128,1280]{2,1,0:T(8,128)(2,1)S(1)}, bf16[2,128,1280]{2,1,0:T(8,128)(2,1)S(1)}, u32[]{:S(2)}, u32[]{:S(2)}) collective-permute-start(bf16[2,128,1280]{2,1,0:T(8,128)(2,1)S(1)} %collective-permute-done.refs_1_), channel_id=1, source_target_pairs={{0,5},{3,6},{4,9},{7,10},{8,13},{11,14},{16,21},{19,22},{20,25},{2... | collective-permute-start | bytes 1966088 | tf_op jit(solution)/shard_map/ppermute | solution.py:16
  36.2 0.4 collective-permute-done.10.refs_2_
  36.7 0.7 collective-permute-start.8
  37.4 4.4 %collective-permute-done.11.refs_3_ = bf16[2,128,1280]{2,1,0:T(8,128)(2,1)} collective-permute-done((bf16[2,128,1280]{2,1,0:T(8,128)(2,1)S(1)}, bf16[2,128,1280]{2,1,0:T(8,128)(2,1)}, u32[]{:S(2)}, u32[]{:S(2)}) %collective-permute-start.11) | collective-permute-done | bytes 655392 | tf_op jit(solution)/shard_map/ppermute | solution.py:16
  41.7 0.0 collective-permute-start.5
  41.7 0.0 collective-permute-done.12.refs_4_
  41.7 0.5 collective-permute-start.6
  42.2 2.0 %fusion.23 = (pred[1280]{0:T(1024)(128)(4,1)S(1)}, pred[1280]{0:T(1024)(128)(4,1)S(1)}) fusion(s32[1280]{0:T(1024)S(1)} %constant_dynamic-update-slice_fusion, s32[]{:T(128)} %bitcast.3, s32[]{:T(128)} %bitcast.2, s32[]{:T(128)} %bitcast.1, s32[]{:T(128)S(6)} %select_n.64), kind=kLoop, calls=%fused_computation.60 | loop fusion | flops 37120 | bytes 7696 | tf_op jit(solution)/shard_map/and | solution.py:65
  44.3 0.2 collective-permute-start.13
  44.5 0.7 copy-done.16
  45.2 1.7 %fusion.20.mask_ref = s32[128,1280]{1,0:T(8,128)} fusion(s32[]{:T(128)} %bitcast.4, s32[1280]{0:T(1024)S(1)} %multiply_subtract_fusion, s32[128]{0:T(128)S(1)} %broadcast_subtract_fusion, pred[1280]{0:T(1024)(128)(4,1)S(1)} %get-tuple-element.40, pred[1280]{0:T(1024)(128)(4,1)S(1)} %get-tuple-element.39, pred[128]{0:T(512)(128)(4,1)S(1)} %compare_and_fusion), kind=kLoop, calls=%fused_computation.42 | loop fusion | flops 1146880 | bytes 663684 | tf_op jit(solution)/shard_map/convert_element_type | solution.py:223
  46.8 3.2 %collective-permute-start.16 = (bf16[2,128,1280]{2,1,0:T(8,128)(2,1)S(1)}, bf16[2,128,1280]{2,1,0:T(8,128)(2,1)}, u32[]{:S(2)}, u32[]{:S(2)}) collective-permute-start(bf16[2,128,1280]{2,1,0:T(8,128)(2,1)S(1)} %collective-permute-done.9.refs_1_), channel_id=1, source_target_pairs={{0,5},{3,6},{4,9},{7,10},{8,13},{11,14},{16,21},{19,22},{20,25},{2... | collective-permute-start | bytes 1966088 | tf_op jit(solution)/shard_map/ppermute | solution.py:16
  50.1 1.6 %collective-permute-start.17 = (bf16[2,128,1280]{2,1,0:T(8,128)(2,1)S(1)}, bf16[2,128,1280]{2,1,0:T(8,128)(2,1)}, u32[]{:S(2)}, u32[]{:S(2)}) collective-permute-start(bf16[2,128,1280]{2,1,0:T(8,128)(2,1)S(1)} %collective-permute-done.9.refs_1_), channel_id=1, source_target_pairs={{4,1},{7,2},{8,5},{11,6},{12,9},{15,10},{20,17},{23,18},{24,21},{2... | collective-permute-start | bytes 1966088 | tf_op jit(solution)/shard_map/ppermute | solution.py:16
  51.7 0.9 copy-done.20
  52.5 0.5 collective-permute-start.15
  53.0 14.0 %shard_map.85 = (bf16[128,1280]{1,0:T(8,128)(2,1)}, bf16[2,128,1280]{2,1,0:T(8,128)(2,1)}, bf16[4,2,128,1280]{3,2,1,0:T(8,128)(2,1)}, bf16[2,128,1280]{2,1,0:T(8...) custom-call(s32[128,1280]{1,0:T(8,128)} %fusion.20.mask_ref, ...), custom_call_target="tpu_custom_call" | custom-call | flops 2516582400 | bytes 14745600 | tf_op jit(solution)/shard_map/pallas_call | solution.py:122
  67.1 0.8 copy-done.18
  67.9 0.0 collective-permute-start.18
  68.0 14.2 %shard_map.86 = (bf16[128,1280]{1,0:T(8,128)(2,1)}, bf16[2,128,1280]{2,1,0:T(8,128)(2,1)}, bf16[4,2,128,1280]{3,2,1,0:T(8,128)(2,1)}, bf16[2,128,1280]{2,1,0:T(8...) custom-call(s32[128,1280]{1,0:T(8,128)} %fusion.20.mask_ref, ...), custom_call_target="tpu_custom_call" | custom-call | flops 2516582400 | bytes 14745600 | tf_op jit(solution)/shard_map/pallas_call | solution.py:122
  82.2 0.6 collective-permute-start.24
  82.8 1.3 collective-permute-start.19
  84.0 0.7 collective-permute-start.20
  84.8 1.3 collective-permute-start.25
  86.1 2.0 %pad_maximum_fusion.2 = bf16[128,2560]{1,0:T(8,128)(2,1)} fusion(bf16[128,1280]{1,0:T(8,128)(2,1)} %get-tuple-element.24, bf16[128,1280]{1,0:T(8,128)(2,1)} %get-tuple-element.21), kind=kLoop, calls=%fused_computation.36 | loop fusion | flops 1310720 | bytes 1310720 | tf_op jit(solution)/shard_map/concatenate | solution.py:247
  88.0 6.9 %collective-permute-done.19 = bf16[2,128,1280]{2,1,0:T(8,128)(2,1)S(1)} collective-permute-done((bf16[2,128,1280]{2,1,0:T(8,128)(2,1)}, bf16[2,128,1280]{2,1,0:T(8,128)(2,1)S(1)}, u32[]{:S(2)}, u32[]{:S(2)}) %collective-permute-start.19) | collective-permute-done | bytes 655392 | tf_op jit(solution)/shard_map/ppermute | solution.py:16
  94.9 0.7 collective-permute-start.26
  95.6 0.7 fusion.13
  96.3 5.1 %collective-permute-start.21 = (bf16[2,128,1280]{2,1,0:T(8,128)(2,1)S(1)}, bf16[2,128,1280]{2,1,0:T(8,128)(2,1)S(1)}, u32[]{:S(2)}, u32[]{:S(2)}) collective-permute-start(bf16[2,128,1280]{2,1,0:T(8,128)(2,1)S(1)} %get-tuple-element.41), channel_id=1, source_target_pairs={{0,2},{1,3},{2,0},{3,1},{4,6},{5,7},{6,4},{7,5},{8,10},{9,11},{10,... | collective-permute-start | bytes 1966088 | tf_op jit(solution)/shard_map/ppermute | solution.py:16
  101.4 1.3 collective-permute-start.22
  102.7 4.6 %collective-permute-start.23 = (bf16[2,128,1280]{2,1,0:T(8,128)(2,1)S(1)}, bf16[2,128,1280]{2,1,0:T(8,128)(2,1)S(1)}, u32[]{:S(2)}, u32[]{:S(2)}) collective-permute-start(bf16[2,128,1280]{2,1,0:T(8,128)(2,1)S(1)} %get-tuple-element.42), channel_id=1, source_target_pairs={{0,4},{1,5},{2,6},{3,7},{4,8},{5,9},{6,10},{7,11},{8,12},{9,13},{1... | collective-permute-start | bytes 1966088 | tf_op jit(solution)/shard_map/ppermute | solution.py:16
  107.3 0.7 fusion.4
  108.0 2.4 %collective-permute-start.27 = (bf16[2,128,1280]{2,1,0:T(8,128)(2,1)S(1)}, bf16[2,128,1280]{2,1,0:T(8,128)(2,1)S(1)}, u32[]{:S(2)}, u32[]{:S(2)}) collective-permute-start(bf16[2,128,1280]{2,1,0:T(8,128)(2,1)S(1)} %get-tuple-element.44), channel_id=1, source_target_pairs={{0,2},{1,3},{2,0},{3,1},{4,6},{5,7},{6,4},{7,5},{8,10},{9,11},{10,... | collective-permute-start | bytes 1966088 | tf_op jit(solution)/shard_map/ppermute | solution.py:16
  110.5 1.3 collective-permute-start.28
  111.8 5.2 %collective-permute-done.21 = bf16[2,128,1280]{2,1,0:T(8,128)(2,1)S(1)} collective-permute-done((bf16[2,128,1280]{2,1,0:T(8,128)(2,1)S(1)}, bf16[2,128,1280]{2,1,0:T(8,128)(2,1)S(1)}, u32[]{:S(2)}, u32[]{:S(2)}) %collective-permute-start.21) | collective-permute-done | bytes 655392 | tf_op jit(solution)/shard_map/ppermute | solution.py:16
  117.0 3.8 %collective-permute-start.29 = (bf16[2,128,1280]{2,1,0:T(8,128)(2,1)S(1)}, bf16[2,128,1280]{2,1,0:T(8,128)(2,1)S(1)}, u32[]{:S(2)}, u32[]{:S(2)}) collective-permute-start(bf16[2,128,1280]{2,1,0:T(8,128)(2,1)S(1)} %get-tuple-element.45), channel_id=1, source_target_pairs={{0,4},{1,5},{2,6},{3,7},{4,8},{5,9},{6,10},{7,11},{8,12},{9,13},{1... | collective-permute-start | bytes 1966088 | tf_op jit(solution)/shard_map/ppermute | solution.py:16
  120.7 0.1 collective-permute-done.22
  120.9 1.5 %collective-permute-done.23 = bf16[2,128,1280]{2,1,0:T(8,128)(2,1)S(1)} collective-permute-done((bf16[2,128,1280]{2,1,0:T(8,128)(2,1)S(1)}, bf16[2,128,1280]{2,1,0:T(8,128)(2,1)S(1)}, u32[]{:S(2)}, u32[]{:S(2)}) %collective-permute-start.23) | collective-permute-done | bytes 655392 | tf_op jit(solution)/shard_map/ppermute | solution.py:16
  122.3 0.4 fusion.17
  122.8 7.8 %collective-permute-done.27 = bf16[2,128,1280]{2,1,0:T(8,128)(2,1)S(1)} collective-permute-done((bf16[2,128,1280]{2,1,0:T(8,128)(2,1)S(1)}, bf16[2,128,1280]{2,1,0:T(8,128)(2,1)S(1)}, u32[]{:S(2)}, u32[]{:S(2)}) %collective-permute-start.27) | collective-permute-done | bytes 655392 | tf_op jit(solution)/shard_map/ppermute | solution.py:16
  130.6 1.9 %collective-permute-done.28 = bf16[2,128,1280]{2,1,0:T(8,128)(2,1)S(1)} collective-permute-done((bf16[2,128,1280]{2,1,0:T(8,128)(2,1)S(1)}, bf16[2,128,1280]{2,1,0:T(8,128)(2,1)S(1)}, u32[]{:S(2)}, u32[]{:S(2)}) %collective-permute-start.28) | collective-permute-done | bytes 655392 | tf_op jit(solution)/shard_map/ppermute | solution.py:16
  132.5 2.2 %collective-permute-done.29 = bf16[2,128,1280]{2,1,0:T(8,128)(2,1)S(1)} collective-permute-done((bf16[2,128,1280]{2,1,0:T(8,128)(2,1)S(1)}, bf16[2,128,1280]{2,1,0:T(8,128)(2,1)S(1)}, u32[]{:S(2)}, u32[]{:S(2)}) %collective-permute-start.29) | collective-permute-done | bytes 655392 | tf_op jit(solution)/shard_map/ppermute | solution.py:16
  134.8 0.4 fusion.8
  135.3 0.9 pad_maximum_fusion.4
  136.1 0.9 pad_maximum_fusion.3
  (75 shorter events, 0.4 us)
Async XLA Ops:
  0.6 11.2 %copy-start = (s32[4,3]{1,0:T(4,128)S(1)}, s32[4,3]{1,0:T(4,128)}, u32[]{:S(2)}) copy-start(s32[4,3]{1,0:T(4,128)} %param.10) | copy-start | bytes 148
  0.6 10.0 %copy-start.7 = (bf16[128,2560]{1,0:T(8,128)(2,1)S(1)}, bf16[128,2560]{1,0:T(8,128)(2,1)}, u32[]{:S(2)}) copy-start(bf16[128,2560]{1,0:T(8,128)(2,1)} %param.8) | copy-start | bytes 1966084
  1.8 8.9 %copy-start.8 = (bf16[128,2560]{1,0:T(8,128)(2,1)S(1)}, bf16[128,2560]{1,0:T(8,128)(2,1)}, u32[]{:S(2)}) copy-start(bf16[128,2560]{1,0:T(8,128)(2,1)} %param.7) | copy-start | bytes 1966084
  1.9 9.6 %copy-start.10 = (bf16[2,128,1280]{2,1,0:T(8,128)(2,1)}, bf16[2,128,1280]{2,1,0:T(8,128)(2,1)S(1)}, u32[]{:S(2)}) copy-start(bf16[2,128,1280]{2,1,0:T(8,128)(2,1)S(1)} %pad_maximum_fusion.refs_0_) | copy-start | bytes 1966084
  1.9 9.9 %copy-start.21 = (s32[4]{0:T(128)S(1)}, s32[4]{0:T(128)}, u32[]{:S(2)}) copy-start(s32[4]{0:T(128)} %param.11) | copy-start | bytes 52
  1.9 18.6 %collective-permute-start = (bf16[2,128,1280]{2,1,0:T(8,128)(2,1)S(1)}, bf16[2,128,1280]{2,1,0:T(8,128)(2,1)S(1)}, u32[]{:S(2)}, u32[]{:S(2)}) collective-permute-start(bf16[2,128,1280]{2,1,0:T(8,128)(2,1)S(1)} %pad_maximum_fusion.refs_0_), channel_id=1, source_target_pairs={{0,2},{1,3},{2,0},{3,1},{4,6},{5,7},{6,4},{7,5},{8,10},{9,11},{10,... | collective-permute-start | bytes 1966088 | tf_op jit(solution)/shard_map/ppermute | solution.py:16
  5.0 20.4 %collective-permute-start.1 = (bf16[2,128,1280]{2,1,0:T(8,128)(2,1)S(1)}, bf16[2,128,1280]{2,1,0:T(8,128)(2,1)}, u32[]{:S(2)}, u32[]{:S(2)}) collective-permute-start(bf16[2,128,1280]{2,1,0:T(8,128)(2,1)S(1)} %pad_maximum_fusion.refs_0_), channel_id=1, source_target_pairs={{0,4},{1,5},{2,6},{3,7},{4,8},{5,9},{6,10},{7,11},{8,12},{9,13},{1... | collective-permute-start | bytes 1966088 | tf_op jit(solution)/shard_map/ppermute | solution.py:16
  9.3 17.9 %collective-permute-start.2 = (bf16[2,128,1280]{2,1,0:T(8,128)(2,1)S(1)}, bf16[2,128,1280]{2,1,0:T(8,128)(2,1)}, u32[]{:S(2)}, u32[]{:S(2)}) collective-permute-start(bf16[2,128,1280]{2,1,0:T(8,128)(2,1)S(1)} %pad_maximum_fusion.refs_0_), channel_id=1, source_target_pairs={{4,0},{5,1},{6,2},{7,3},{8,4},{9,5},{10,6},{11,7},{12,8},{13,9},{1... | collective-permute-start | bytes 1966088 | tf_op jit(solution)/shard_map/ppermute | solution.py:16
  10.6 16.6 %collective-permute-start.3 = (bf16[2,128,1280]{2,1,0:T(8,128)(2,1)S(1)}, bf16[2,128,1280]{2,1,0:T(8,128)(2,1)}, u32[]{:S(2)}, u32[]{:S(2)}) collective-permute-start(bf16[2,128,1280]{2,1,0:T(8,128)(2,1)S(1)} %pad_maximum_fusion.refs_0_), channel_id=1, source_target_pairs={{0,1},{1,0},{2,3},{3,2},{4,5},{5,4},{6,7},{7,6},{8,9},{9,8},{10,11... | collective-permute-start | bytes 1966088 | tf_op jit(solution)/shard_map/ppermute | solution.py:16
  10.8 56.2 %copy-start.9 = (bf16[2,128,1280]{2,1,0:T(8,128)(2,1)}, bf16[2,128,1280]{2,1,0:T(8,128)(2,1)S(1)}, u32[]{:S(2)}) copy-start(bf16[2,128,1280]{2,1,0:T(8,128)(2,1)S(1)} %pad_maximum_fusion.1.refs_0_) | copy-start | bytes 1966084
  10.8 22.9 %collective-permute-start.9 = (bf16[2,128,1280]{2,1,0:T(8,128)(2,1)S(1)}, bf16[2,128,1280]{2,1,0:T(8,128)(2,1)S(1)}, u32[]{:S(2)}, u32[]{:S(2)}) collective-permute-start(bf16[2,128,1280]{2,1,0:T(8,128)(2,1)S(1)} %pad_maximum_fusion.1.refs_0_), channel_id=1, source_target_pairs={{0,2},{1,3},{2,0},{3,1},{4,6},{5,7},{6,4},{7,5},{8,10},{9,11},{10,... | collective-permute-start | bytes 1966088 | tf_op jit(solution)/shard_map/ppermute | solution.py:16
  20.6 32.4 %copy-start.14 = (bf16[2,128,1280]{2,1,0:T(8,128)(2,1)}, bf16[2,128,1280]{2,1,0:T(8,128)(2,1)S(1)}, u32[]{:S(2)}) copy-start(bf16[2,128,1280]{2,1,0:T(8,128)(2,1)S(1)} %collective-permute-done.refs_1_) | copy-start | bytes 1966084
  20.6 16.1 %collective-permute-start.10 = (bf16[2,128,1280]{2,1,0:T(8,128)(2,1)S(1)}, bf16[2,128,1280]{2,1,0:T(8,128)(2,1)}, u32[]{:S(2)}, u32[]{:S(2)}) collective-permute-start(bf16[2,128,1280]{2,1,0:T(8,128)(2,1)S(1)} %pad_maximum_fusion.1.refs_0_), channel_id=1, source_target_pairs={{0,4},{1,5},{2,6},{3,7},{4,8},{5,9},{6,10},{7,11},{8,12},{9,13},{1... | collective-permute-start | bytes 1966088 | tf_op jit(solution)/shard_map/ppermute | solution.py:16
  25.4 16.3 %collective-permute-start.11 = (bf16[2,128,1280]{2,1,0:T(8,128)(2,1)S(1)}, bf16[2,128,1280]{2,1,0:T(8,128)(2,1)}, u32[]{:S(2)}, u32[]{:S(2)}) collective-permute-start(bf16[2,128,1280]{2,1,0:T(8,128)(2,1)S(1)} %pad_maximum_fusion.1.refs_0_), channel_id=1, source_target_pairs={{4,0},{5,1},{6,2},{7,3},{8,4},{9,5},{10,6},{11,7},{12,8},{13,9},{1... | collective-permute-start | bytes 1966088 | tf_op jit(solution)/shard_map/ppermute | solution.py:16
  27.2 14.5 %collective-permute-start.12 = (bf16[2,128,1280]{2,1,0:T(8,128)(2,1)S(1)}, bf16[2,128,1280]{2,1,0:T(8,128)(2,1)S(1)}, u32[]{:S(2)}, u32[]{:S(2)}) collective-permute-start(bf16[2,128,1280]{2,1,0:T(8,128)(2,1)S(1)} %pad_maximum_fusion.1.refs_0_), channel_id=1, source_target_pairs={{0,1},{1,0},{2,3},{3,2},{4,5},{5,4},{6,7},{7,6},{8,9},{9,8},{10,11... | collective-permute-start | bytes 1966088 | tf_op jit(solution)/shard_map/ppermute | solution.py:16
  27.3 17.0 %collective-permute-start.4 = (bf16[2,128,1280]{2,1,0:T(8,128)(2,1)S(1)}, bf16[2,128,1280]{2,1,0:T(8,128)(2,1)S(1)}, u32[]{:S(2)}, u32[]{:S(2)}) collective-permute-start(bf16[2,128,1280]{2,1,0:T(8,128)(2,1)S(1)} %collective-permute-done.refs_1_), channel_id=1, source_target_pairs={{0,1},{1,0},{2,3},{3,2},{4,5},{5,4},{6,7},{7,6},{8,9},{9,8},{10,11... | collective-permute-start | bytes 1966088 | tf_op jit(solution)/shard_map/ppermute | solution.py:16
  33.8 33.3 %copy-start.13 = (bf16[2,128,1280]{2,1,0:T(8,128)(2,1)}, bf16[2,128,1280]{2,1,0:T(8,128)(2,1)S(1)}, u32[]{:S(2)}) copy-start(bf16[2,128,1280]{2,1,0:T(8,128)(2,1)S(1)} %collective-permute-done.9.refs_1_) | copy-start | bytes 1966084
  33.8 13.0 %collective-permute-start.7 = (bf16[2,128,1280]{2,1,0:T(8,128)(2,1)S(1)}, bf16[2,128,1280]{2,1,0:T(8,128)(2,1)S(1)}, u32[]{:S(2)}, u32[]{:S(2)}) collective-permute-start(bf16[2,128,1280]{2,1,0:T(8,128)(2,1)S(1)} %collective-permute-done.refs_1_), channel_id=1, source_target_pairs={{0,5},{3,6},{4,9},{7,10},{8,13},{11,14},{16,21},{19,22},{20,25},{2... | collective-permute-start | bytes 1966088 | tf_op jit(solution)/shard_map/ppermute | solution.py:16
  36.7 13.4 %collective-permute-start.8 = (bf16[2,128,1280]{2,1,0:T(8,128)(2,1)S(1)}, bf16[2,128,1280]{2,1,0:T(8,128)(2,1)S(1)}, u32[]{:S(2)}, u32[]{:S(2)}) collective-permute-start(bf16[2,128,1280]{2,1,0:T(8,128)(2,1)S(1)} %collective-permute-done.refs_1_), channel_id=1, source_target_pairs={{4,1},{7,2},{8,5},{11,6},{12,9},{15,10},{20,17},{23,18},{24,21},{2... | collective-permute-start | bytes 1966088 | tf_op jit(solution)/shard_map/ppermute | solution.py:16
  41.7 9.9 %collective-permute-start.5 = (bf16[2,128,1280]{2,1,0:T(8,128)(2,1)}, bf16[2,128,1280]{2,1,0:T(8,128)(2,1)S(1)}, u32[]{:S(2)}, u32[]{:S(2)}) collective-permute-start(bf16[2,128,1280]{2,1,0:T(8,128)(2,1)} %collective-permute-done.1.refs_2_), channel_id=1, source_target_pairs={{0,1},{1,0},{2,3},{3,2},{4,5},{5,4},{6,7},{7,6},{8,9},{9,8},{10,11... | collective-permute-start | bytes 1966088 | tf_op jit(solution)/shard_map/ppermute | solution.py:16
  41.7 2.6 %copy-start.15 = (bf16[2,128,1280]{2,1,0:T(8,128)(2,1)}, bf16[2,128,1280]{2,1,0:T(8,128)(2,1)S(1)}, u32[]{:S(2)}) copy-start(bf16[2,128,1280]{2,1,0:T(8,128)(2,1)S(1)} %collective-permute-done.12.refs_4_) | copy-start | bytes 1966084
  41.7 10.8 %collective-permute-start.6 = (bf16[2,128,1280]{2,1,0:T(8,128)(2,1)}, bf16[2,128,1280]{2,1,0:T(8,128)(2,1)}, u32[]{:S(2)}, u32[]{:S(2)}) collective-permute-start(bf16[2,128,1280]{2,1,0:T(8,128)(2,1)} %collective-permute-done.2.refs_3_), channel_id=1, source_target_pairs={{0,1},{1,0},{2,3},{3,2},{4,5},{5,4},{6,7},{7,6},{8,9},{9,8},{10,11... | collective-permute-start | bytes 1966088 | tf_op jit(solution)/shard_map/ppermute | solution.py:16
  44.3 0.9 copy-start.16
  44.3 22.8 %collective-permute-start.13 = (bf16[2,128,1280]{2,1,0:T(8,128)(2,1)S(1)}, bf16[2,128,1280]{2,1,0:T(8,128)(2,1)S(1)}, u32[]{:S(2)}, u32[]{:S(2)}) collective-permute-start(bf16[2,128,1280]{2,1,0:T(8,128)(2,1)S(1)} %collective-permute-done.9.refs_1_), channel_id=1, source_target_pairs={{0,1},{1,0},{2,3},{3,2},{4,5},{5,4},{6,7},{7,6},{8,9},{9,8},{10,11... | collective-permute-start | bytes 1966088 | tf_op jit(solution)/shard_map/ppermute | solution.py:16
  46.8 3.3 %copy-start.17 = (bf16[2,128,1280]{2,1,0:T(8,128)(2,1)}, bf16[2,128,1280]{2,1,0:T(8,128)(2,1)S(1)}, u32[]{:S(2)}) copy-start(bf16[2,128,1280]{2,1,0:T(8,128)(2,1)S(1)} %collective-permute-done.7.refs_8_) | copy-start | bytes 1966084
  46.8 21.1 %collective-permute-start.16 = (bf16[2,128,1280]{2,1,0:T(8,128)(2,1)S(1)}, bf16[2,128,1280]{2,1,0:T(8,128)(2,1)}, u32[]{:S(2)}, u32[]{:S(2)}) collective-permute-start(bf16[2,128,1280]{2,1,0:T(8,128)(2,1)S(1)} %collective-permute-done.9.refs_1_), channel_id=1, source_target_pairs={{0,5},{3,6},{4,9},{7,10},{8,13},{11,14},{16,21},{19,22},{20,25},{2... | collective-permute-start | bytes 1966088 | tf_op jit(solution)/shard_map/ppermute | solution.py:16
  50.1 1.6 %copy-start.19 = (bf16[2,128,1280]{2,1,0:T(8,128)(2,1)}, bf16[2,128,1280]{2,1,0:T(8,128)(2,1)S(1)}, u32[]{:S(2)}) copy-start(bf16[2,128,1280]{2,1,0:T(8,128)(2,1)S(1)} %collective-permute-done.8.refs_9_) | copy-start | bytes 1966084
  50.1 17.8 %collective-permute-start.17 = (bf16[2,128,1280]{2,1,0:T(8,128)(2,1)S(1)}, bf16[2,128,1280]{2,1,0:T(8,128)(2,1)}, u32[]{:S(2)}, u32[]{:S(2)}) collective-permute-start(bf16[2,128,1280]{2,1,0:T(8,128)(2,1)S(1)} %collective-permute-done.9.refs_1_), channel_id=1, source_target_pairs={{4,1},{7,2},{8,5},{11,6},{12,9},{15,10},{20,17},{23,18},{24,21},{2... | collective-permute-start | bytes 1966088 | tf_op jit(solution)/shard_map/ppermute | solution.py:16
  51.7 0.9 copy-start.20
  52.5 15.4 %collective-permute-start.14 = (bf16[2,128,1280]{2,1,0:T(8,128)(2,1)}, bf16[2,128,1280]{2,1,0:T(8,128)(2,1)}, u32[]{:S(2)}, u32[]{:S(2)}) collective-permute-start(bf16[2,128,1280]{2,1,0:T(8,128)(2,1)} %collective-permute-done.10.refs_2_), channel_id=1, source_target_pairs={{0,1},{1,0},{2,3},{3,2},{4,5},{5,4},{6,7},{7,6},{8,9},{9,8},{10,11... | collective-permute-start | bytes 1966088 | tf_op jit(solution)/shard_map/ppermute | solution.py:16
  52.5 15.4 %collective-permute-start.15 = (bf16[2,128,1280]{2,1,0:T(8,128)(2,1)}, bf16[2,128,1280]{2,1,0:T(8,128)(2,1)}, u32[]{:S(2)}, u32[]{:S(2)}) collective-permute-start(bf16[2,128,1280]{2,1,0:T(8,128)(2,1)} %collective-permute-done.11.refs_3_), channel_id=1, source_target_pairs={{0,1},{1,0},{2,3},{3,2},{4,5},{5,4},{6,7},{7,6},{8,9},{9,8},{10,11... | collective-permute-start | bytes 1966088 | tf_op jit(solution)/shard_map/ppermute | solution.py:16
  67.1 0.8 copy-start.18
  67.9 27.7 %collective-permute-start.18 = (bf16[4,2,128,1280]{3,2,1,0:T(8,128)(2,1)}, bf16[4,2,128,1280]{3,2,1,0:T(8,128)(2,1)S(1)}, u32[]{:S(2)}, u32[]{:S(2)}) collective-permute-start(bf16[4,2,128,1280]{3,2,1,0:T(8,128)(2,1)} %get-tuple-element.26), channel_id=1, source_target_pairs={{0,1},{1,0},{2,3},{3,2},{4,5},{5,4},{6,7},{7,6},{8,9},{9,8},{10,11... | collective-permute-start | bytes 7864328 | tf_op jit(solution)/shard_map/ppermute | solution.py:16
  68.0 27.6 %copy-start.3 = (bf16[2,128,1280]{2,1,0:T(8,128)(2,1)S(1)}, bf16[2,128,1280]{2,1,0:T(8,128)(2,1)}, u32[]{:S(2)}) copy-start(bf16[2,128,1280]{2,1,0:T(8,128)(2,1)} %get-tuple-element.31) | copy-start | bytes 1966084
  82.2 13.4 %copy-start.1 = (bf16[2,128,1280]{2,1,0:T(8,128)(2,1)S(1)}, bf16[2,128,1280]{2,1,0:T(8,128)(2,1)}, u32[]{:S(2)}) copy-start(bf16[2,128,1280]{2,1,0:T(8,128)(2,1)} %get-tuple-element.27) | copy-start | bytes 1966084
  82.2 13.4 %copy-start.2 = (bf16[2,128,1280]{2,1,0:T(8,128)(2,1)S(1)}, bf16[2,128,1280]{2,1,0:T(8,128)(2,1)}, u32[]{:S(2)}) copy-start(bf16[2,128,1280]{2,1,0:T(8,128)(2,1)} %get-tuple-element.30) | copy-start | bytes 1966084
  82.2 25.1 %collective-permute-start.24 = (bf16[4,2,128,1280]{3,2,1,0:T(8,128)(2,1)}, bf16[4,2,128,1280]{3,2,1,0:T(8,128)(2,1)S(1)}, u32[]{:S(2)}, u32[]{:S(2)}) collective-permute-start(bf16[4,2,128,1280]{3,2,1,0:T(8,128)(2,1)} %get-tuple-element.33), channel_id=1, source_target_pairs={{0,1},{1,0},{2,3},{3,2},{4,5},{5,4},{6,7},{7,6},{8,9},{9,8},{10,11... | collective-permute-start | bytes 7864328 | tf_op jit(solution)/shard_map/ppermute | solution.py:16
  82.8 12.1 %collective-permute-start.19 = (bf16[2,128,1280]{2,1,0:T(8,128)(2,1)}, bf16[2,128,1280]{2,1,0:T(8,128)(2,1)S(1)}, u32[]{:S(2)}, u32[]{:S(2)}) collective-permute-start(bf16[2,128,1280]{2,1,0:T(8,128)(2,1)} %get-tuple-element.28), channel_id=1, source_target_pairs={{5,0},{6,3},{9,4},{10,7},{13,8},{14,11},{21,16},{22,19},{25,20},{2... | collective-permute-start | bytes 1966088 | tf_op jit(solution)/shard_map/ppermute | solution.py:16
  84.0 11.5 %collective-permute-start.20 = (bf16[2,128,1280]{2,1,0:T(8,128)(2,1)}, bf16[2,128,1280]{2,1,0:T(8,128)(2,1)S(1)}, u32[]{:S(2)}, u32[]{:S(2)}) collective-permute-start(bf16[2,128,1280]{2,1,0:T(8,128)(2,1)} %get-tuple-element.29), channel_id=1, source_target_pairs={{1,4},{2,7},{5,8},{6,11},{9,12},{10,15},{17,20},{18,23},{21,24},{2... | collective-permute-start | bytes 1966088 | tf_op jit(solution)/shard_map/ppermute | solution.py:16
  84.8 17.9 %collective-permute-start.25 = (bf16[2,128,1280]{2,1,0:T(8,128)(2,1)}, bf16[2,128,1280]{2,1,0:T(8,128)(2,1)S(1)}, u32[]{:S(2)}, u32[]{:S(2)}) collective-permute-start(bf16[2,128,1280]{2,1,0:T(8,128)(2,1)} %get-tuple-element.35), channel_id=1, source_target_pairs={{5,0},{6,3},{9,4},{10,7},{13,8},{14,11},{21,16},{22,19},{25,20},{2... | collective-permute-start | bytes 1966088 | tf_op jit(solution)/shard_map/ppermute | solution.py:16
  94.9 12.4 %collective-permute-start.26 = (bf16[2,128,1280]{2,1,0:T(8,128)(2,1)}, bf16[2,128,1280]{2,1,0:T(8,128)(2,1)S(1)}, u32[]{:S(2)}, u32[]{:S(2)}) collective-permute-start(bf16[2,128,1280]{2,1,0:T(8,128)(2,1)} %get-tuple-element.36), channel_id=1, source_target_pairs={{1,4},{2,7},{5,8},{6,11},{9,12},{10,15},{17,20},{18,23},{21,24},{2... | collective-permute-start | bytes 1966088 | tf_op jit(solution)/shard_map/ppermute | solution.py:16
  95.6 11.7 %copy-start.4 = (bf16[2,128,1280]{2,1,0:T(8,128)(2,1)S(1)}, bf16[2,128,1280]{2,1,0:T(8,128)(2,1)}, u32[]{:S(2)}) copy-start(bf16[2,128,1280]{2,1,0:T(8,128)(2,1)} %get-tuple-element.34) | copy-start | bytes 1966084
  95.6 11.7 %copy-start.5 = (bf16[2,128,1280]{2,1,0:T(8,128)(2,1)S(1)}, bf16[2,128,1280]{2,1,0:T(8,128)(2,1)}, u32[]{:S(2)}) copy-start(bf16[2,128,1280]{2,1,0:T(8,128)(2,1)} %get-tuple-element.37) | copy-start | bytes 1966084
  95.6 11.7 %copy-start.6 = (bf16[2,128,1280]{2,1,0:T(8,128)(2,1)S(1)}, bf16[2,128,1280]{2,1,0:T(8,128)(2,1)}, u32[]{:S(2)}) copy-start(bf16[2,128,1280]{2,1,0:T(8,128)(2,1)} %get-tuple-element.38) | copy-start | bytes 1966084
  96.3 20.6 %collective-permute-start.21 = (bf16[2,128,1280]{2,1,0:T(8,128)(2,1)S(1)}, bf16[2,128,1280]{2,1,0:T(8,128)(2,1)S(1)}, u32[]{:S(2)}, u32[]{:S(2)}) collective-permute-start(bf16[2,128,1280]{2,1,0:T(8,128)(2,1)S(1)} %get-tuple-element.41), channel_id=1, source_target_pairs={{0,2},{1,3},{2,0},{3,1},{4,6},{5,7},{6,4},{7,5},{8,10},{9,11},{10,... | collective-permute-start | bytes 1966088 | tf_op jit(solution)/shard_map/ppermute | solution.py:16
  101.4 19.5 %collective-permute-start.22 = (bf16[2,128,1280]{2,1,0:T(8,128)(2,1)S(1)}, bf16[2,128,1280]{2,1,0:T(8,128)(2,1)S(1)}, u32[]{:S(2)}, u32[]{:S(2)}) collective-permute-start(bf16[2,128,1280]{2,1,0:T(8,128)(2,1)S(1)} %get-tuple-element.43), channel_id=1, source_target_pairs={{4,0},{5,1},{6,2},{7,3},{8,4},{9,5},{10,6},{11,7},{12,8},{13,9},{1... | collective-permute-start | bytes 1966088 | tf_op jit(solution)/shard_map/ppermute | solution.py:16
  102.7 19.7 %collective-permute-start.23 = (bf16[2,128,1280]{2,1,0:T(8,128)(2,1)S(1)}, bf16[2,128,1280]{2,1,0:T(8,128)(2,1)S(1)}, u32[]{:S(2)}, u32[]{:S(2)}) collective-permute-start(bf16[2,128,1280]{2,1,0:T(8,128)(2,1)S(1)} %get-tuple-element.42), channel_id=1, source_target_pairs={{0,4},{1,5},{2,6},{3,7},{4,8},{5,9},{6,10},{7,11},{8,12},{9,13},{1... | collective-permute-start | bytes 1966088 | tf_op jit(solution)/shard_map/ppermute | solution.py:16
  107.3 15.0 %copy-start.11 = (bf16[2,128,1280]{2,1,0:T(8,128)(2,1)S(1)}, bf16[2,128,1280]{2,1,0:T(8,128)(2,1)}, u32[]{:S(2)}) copy-start(bf16[2,128,1280]{2,1,0:T(8,128)(2,1)} %get-tuple-element.25) | copy-start | bytes 1966084
  108.0 22.6 %collective-permute-start.27 = (bf16[2,128,1280]{2,1,0:T(8,128)(2,1)S(1)}, bf16[2,128,1280]{2,1,0:T(8,128)(2,1)S(1)}, u32[]{:S(2)}, u32[]{:S(2)}) collective-permute-start(bf16[2,128,1280]{2,1,0:T(8,128)(2,1)S(1)} %get-tuple-element.44), channel_id=1, source_target_pairs={{0,2},{1,3},{2,0},{3,1},{4,6},{5,7},{6,4},{7,5},{8,10},{9,11},{10,... | collective-permute-start | bytes 1966088 | tf_op jit(solution)/shard_map/ppermute | solution.py:16
  110.5 22.1 %collective-permute-start.28 = (bf16[2,128,1280]{2,1,0:T(8,128)(2,1)S(1)}, bf16[2,128,1280]{2,1,0:T(8,128)(2,1)S(1)}, u32[]{:S(2)}, u32[]{:S(2)}) collective-permute-start(bf16[2,128,1280]{2,1,0:T(8,128)(2,1)S(1)} %get-tuple-element.46), channel_id=1, source_target_pairs={{4,0},{5,1},{6,2},{7,3},{8,4},{9,5},{10,6},{11,7},{12,8},{13,9},{1... | collective-permute-start | bytes 1966088 | tf_op jit(solution)/shard_map/ppermute | solution.py:16
  117.0 17.8 %collective-permute-start.29 = (bf16[2,128,1280]{2,1,0:T(8,128)(2,1)S(1)}, bf16[2,128,1280]{2,1,0:T(8,128)(2,1)S(1)}, u32[]{:S(2)}, u32[]{:S(2)}) collective-permute-start(bf16[2,128,1280]{2,1,0:T(8,128)(2,1)S(1)} %get-tuple-element.45), channel_id=1, source_target_pairs={{0,4},{1,5},{2,6},{3,7},{4,8},{5,9},{6,10},{7,11},{8,12},{9,13},{1... | collective-permute-start | bytes 1966088 | tf_op jit(solution)/shard_map/ppermute | solution.py:16
  122.8 12.0 %copy-start.12 = (bf16[2,128,1280]{2,1,0:T(8,128)(2,1)S(1)}, bf16[2,128,1280]{2,1,0:T(8,128)(2,1)}, u32[]{:S(2)}) copy-start(bf16[2,128,1280]{2,1,0:T(8,128)(2,1)} %get-tuple-element.32) | copy-start | bytes 1966084

commit v21 on v18

--- a/solution.py
+++ b/solution.py
@@ -9,7 +9,7 @@
 HD = 128
 QUARTERS = 4
 CHUNKS = 2
-STEP_HEADS = 2
+STEP_HEADS = 5
 
 
 def send(value, pairs):

time: 137 us -> 139 us (1.015)
  Pallas kernels: 28.2 us -> 29.7 us
    pallas_call x2, Pallas kernels: 28.2 us -> 29.7 us  [attention_backward(): pl.pallas_call(kernel, grid=(heads // STEP_HEADS,), in_specs=in_specs, ou...]
  transfers between devices with their start and end apart: 30 -> 30, of which waited for: 11 -> 11; matrix products, arithmetic and copies ran while one was open for 6% -> 6% of each run, Pallas kernels for 21% -> 22%
where the time goes in v21:
time: 139 us; the launch traced here: 138 us
  starting transfers between devices  48.1 us (35%)
  waiting for transfers between devices  44.4 us (32%)
  Pallas kernels  29.7 us (21%)
  other arithmetic  9.77 us (7%)
  local copies, waits for them, and re-layouts  4.27 us (3%)
    ppermute x30, starting transfers between devices, send(): return lax.ppermute(value, 'tm', pairs)  48.1 us
    ppermute x30, waiting for transfers between devices, send(): return lax.ppermute(value, 'tm', pairs)  44.4 us
    pallas_call x2, Pallas kernels, attention_backward(): pl.pallas_call(kernel, grid=(heads // STEP_HEADS,), in_specs=in_specs, ou...  29.7 us
  transfers between devices with their start and end apart: 30, of which 11 were waited for; matrix products, arithmetic and copies ran while one was open for 6% of the time, Pallas kernels for 22%

profile of v21, /device:TPU:0, one launch (start us, length us, event | category | flops | bytes accessed | tf_op | source)
XLA Modules:
  0.0 137.7 jit_solution(18039881106553767581)
XLA Ops:
  0.6 0.0 copy-start
  0.6 1.4 slice_bitcast_fusion.14
  2.0 0.0 copy-start.18
  2.0 0.1 pad_maximum_fusion.refs_0_
  2.1 3.1 %collective-permute-start = (bf16[2,128,1280]{2,1,0:T(8,128)(2,1)S(1)}, bf16[2,128,1280]{2,1,0:T(8,128)(2,1)S(1)}, u32[]{:S(2)}, u32[]{:S(2)}) collective-permute-start(bf16[2,128,1280]{2,1,0:T(8,128)(2,1)S(1)} %pad_maximum_fusion.refs_0_), channel_id=1, source_target_pairs={{0,2},{1,3},{2,0},{3,1},{4,6},{5,7},{6,4},{7,5},{8,10},{9,11},{10,... | collective-permute-start | bytes 1966088 | tf_op jit(solution)/shard_map/ppermute | solution.py:16
  5.2 4.3 %collective-permute-start.1 = (bf16[2,128,1280]{2,1,0:T(8,128)(2,1)S(1)}, bf16[2,128,1280]{2,1,0:T(8,128)(2,1)}, u32[]{:S(2)}, u32[]{:S(2)}) collective-permute-start(bf16[2,128,1280]{2,1,0:T(8,128)(2,1)S(1)} %pad_maximum_fusion.refs_0_), channel_id=1, source_target_pairs={{0,4},{1,5},{2,6},{3,7},{4,8},{5,9},{6,10},{7,11},{8,12},{9,13},{1... | collective-permute-start | bytes 1966088 | tf_op jit(solution)/shard_map/ppermute | solution.py:16
  9.5 1.3 collective-permute-start.2
  10.8 0.1 collective-permute-start.3
  10.9 0.1 pad_maximum_fusion.1.refs_0_
  10.9 0.0 copy-start.7
  10.9 0.6 collective-permute-start.9
  11.8 0.6 dynamic_slice.9
  12.4 8.3 %collective-permute-done.refs_1_ = bf16[2,128,1280]{2,1,0:T(8,128)(2,1)S(1)} collective-permute-done((bf16[2,128,1280]{2,1,0:T(8,128)(2,1)S(1)}, bf16[2,128,1280]{2,1,0:T(8,128)(2,1)S(1)}, u32[]{:S(2)}, u32[]{:S(2)}) %collective-permute-start) | collective-permute-done | bytes 655392 | tf_op jit(solution)/shard_map/ppermute | solution.py:16
  20.8 4.8 %collective-permute-start.10 = (bf16[2,128,1280]{2,1,0:T(8,128)(2,1)S(1)}, bf16[2,128,1280]{2,1,0:T(8,128)(2,1)}, u32[]{:S(2)}, u32[]{:S(2)}) collective-permute-start(bf16[2,128,1280]{2,1,0:T(8,128)(2,1)S(1)} %pad_maximum_fusion.1.refs_0_), channel_id=1, source_target_pairs={{0,4},{1,5},{2,6},{3,7},{4,8},{5,9},{6,10},{7,11},{8,12},{9,13},{1... | collective-permute-start | bytes 1966088 | tf_op jit(solution)/shard_map/ppermute | solution.py:16
  25.6 1.3 collective-permute-start.11
  26.9 0.5 collective-permute-done.2.refs_3_
  27.4 0.0 collective-permute-start.12
  27.4 0.0 collective-permute-done.3.refs_4_
  27.4 0.6 collective-permute-start.4
  28.0 0.6 fusion.24
  28.7 5.3 %collective-permute-done.9.refs_1_ = bf16[2,128,1280]{2,1,0:T(8,128)(2,1)S(1)} collective-permute-done((bf16[2,128,1280]{2,1,0:T(8,128)(2,1)S(1)}, bf16[2,128,1280]{2,1,0:T(8,128)(2,1)S(1)}, u32[]{:S(2)}, u32[]{:S(2)}) %collective-permute-start.9) | collective-permute-done | bytes 655392 | tf_op jit(solution)/shard_map/ppermute | solution.py:16
  33.9 2.4 %collective-permute-start.7 = (bf16[2,128,1280]{2,1,0:T(8,128)(2,1)S(1)}, bf16[2,128,1280]{2,1,0:T(8,128)(2,1)S(1)}, u32[]{:S(2)}, u32[]{:S(2)}) collective-permute-start(bf16[2,128,1280]{2,1,0:T(8,128)(2,1)S(1)} %collective-permute-done.refs_1_), channel_id=1, source_target_pairs={{0,5},{3,6},{4,9},{7,10},{8,13},{11,14},{16,21},{19,22},{20,25},{2... | collective-permute-start | bytes 1966088 | tf_op jit(solution)/shard_map/ppermute | solution.py:16
  36.4 0.4 collective-permute-done.10.refs_2_
  36.8 0.7 collective-permute-start.8
  37.5 4.4 %collective-permute-done.11.refs_3_ = bf16[2,128,1280]{2,1,0:T(8,128)(2,1)} collective-permute-done((bf16[2,128,1280]{2,1,0:T(8,128)(2,1)S(1)}, bf16[2,128,1280]{2,1,0:T(8,128)(2,1)}, u32[]{:S(2)}, u32[]{:S(2)}) %collective-permute-start.11) | collective-permute-done | bytes 655392 | tf_op jit(solution)/shard_map/ppermute | solution.py:16
  41.9 0.5 collective-permute-start.6
  42.4 2.0 %fusion.23 = (pred[1280]{0:T(1024)(128)(4,1)S(1)}, pred[1280]{0:T(1024)(128)(4,1)S(1)}) fusion(s32[1280]{0:T(1024)S(1)} %constant_dynamic-update-slice_fusion, s32[]{:T(128)} %bitcast.3, s32[]{:T(128)} %bitcast.2, s32[]{:T(128)} %bitcast.1, s32[]{:T(128)S(6)} %select_n.64), kind=kLoop, calls=%fused_computation.60 | loop fusion | flops 37120 | bytes 7696 | tf_op jit(solution)/shard_map/and | solution.py:65
  44.4 0.0 collective-permute-done.4.refs_5_
  44.4 0.2 collective-permute-start.13
  44.6 0.7 copy-done.14
  45.2 1.7 %fusion.20.mask_ref = s32[128,1280]{1,0:T(8,128)} fusion(s32[]{:T(128)} %bitcast.4, s32[1280]{0:T(1024)S(1)} %multiply_subtract_fusion, s32[128]{0:T(128)S(1)} %broadcast_subtract_fusion, pred[1280]{0:T(1024)(128)(4,1)S(1)} %get-tuple-element.36, pred[1280]{0:T(1024)(128)(4,1)S(1)} %get-tuple-element.35, pred[128]{0:T(512)(128)(4,1)S(1)} %compare_and_fusion), kind=kLoop, calls=%fused_computation.42 | loop fusion | flops 1146880 | bytes 663684 | tf_op jit(solution)/shard_map/convert_element_type | solution.py:223
  46.9 3.2 %collective-permute-start.16 = (bf16[2,128,1280]{2,1,0:T(8,128)(2,1)S(1)}, bf16[2,128,1280]{2,1,0:T(8,128)(2,1)}, u32[]{:S(2)}, u32[]{:S(2)}) collective-permute-start(bf16[2,128,1280]{2,1,0:T(8,128)(2,1)S(1)} %collective-permute-done.9.refs_1_), channel_id=1, source_target_pairs={{0,5},{3,6},{4,9},{7,10},{8,13},{11,14},{16,21},{19,22},{20,25},{2... | collective-permute-start | bytes 1966088 | tf_op jit(solution)/shard_map/ppermute | solution.py:16
  50.1 0.0 collective-permute-done.8.refs_9_
  50.1 1.5 %collective-permute-start.17 = (bf16[2,128,1280]{2,1,0:T(8,128)(2,1)S(1)}, bf16[2,128,1280]{2,1,0:T(8,128)(2,1)}, u32[]{:S(2)}, u32[]{:S(2)}) collective-permute-start(bf16[2,128,1280]{2,1,0:T(8,128)(2,1)S(1)} %collective-permute-done.9.refs_1_), channel_id=1, source_target_pairs={{4,1},{7,2},{8,5},{11,6},{12,9},{15,10},{20,17},{23,18},{24,21},{2... | collective-permute-start | bytes 1966088 | tf_op jit(solution)/shard_map/ppermute | solution.py:16
  51.6 0.0 collective-permute-done.5.refs_6_
  51.6 0.8 copy-done.17
  52.4 0.5 collective-permute-start.15
  53.0 14.8 %shard_map.85 = (bf16[128,1280]{1,0:T(8,128)(2,1)}, bf16[2,128,1280]{2,1,0:T(8,128)(2,1)}, bf16[4,2,128,1280]{3,2,1,0:T(8,128)(2,1)}, bf16[2,128,1280]{2,1,0:T(8...) custom-call(s32[128,1280]{1,0:T(8,128)} %fusion.20.mask_ref, ...), custom_call_target="tpu_custom_call" | custom-call | flops 2516582400 | bytes 14745600 | tf_op jit(solution)/shard_map/pallas_call | solution.py:122
  67.8 0.1 collective-permute-start.18
  67.9 14.9 %shard_map.86 = (bf16[128,1280]{1,0:T(8,128)(2,1)}, bf16[2,128,1280]{2,1,0:T(8,128)(2,1)}, bf16[4,2,128,1280]{3,2,1,0:T(8,128)(2,1)}, bf16[2,128,1280]{2,1,0:T(8...) custom-call(s32[128,1280]{1,0:T(8,128)} %fusion.20.mask_ref, ...), custom_call_target="tpu_custom_call" | custom-call | flops 2516582400 | bytes 14745600 | tf_op jit(solution)/shard_map/pallas_call | solution.py:122
  82.9 0.5 collective-permute-start.24
  83.4 1.3 collective-permute-start.19
  84.7 0.7 collective-permute-start.20
  85.4 1.3 collective-permute-start.25
  86.7 2.0 %pad_maximum_fusion.2 = bf16[128,2560]{1,0:T(8,128)(2,1)} fusion(bf16[128,1280]{1,0:T(8,128)(2,1)} %get-tuple-element.20, bf16[128,1280]{1,0:T(8,128)(2,1)} %get-tuple-element.19), kind=kLoop, calls=%fused_computation.36 | loop fusion | flops 1310720 | bytes 1310720 | tf_op jit(solution)/shard_map/concatenate | solution.py:245
  88.7 6.9 %collective-permute-done.19 = bf16[2,128,1280]{2,1,0:T(8,128)(2,1)S(1)} collective-permute-done((bf16[2,128,1280]{2,1,0:T(8,128)(2,1)}, bf16[2,128,1280]{2,1,0:T(8,128)(2,1)S(1)}, u32[]{:S(2)}, u32[]{:S(2)}) %collective-permute-start.19) | collective-permute-done | bytes 655392 | tf_op jit(solution)/shard_map/ppermute | solution.py:16
  95.5 0.7 collective-permute-start.26
  96.3 0.7 fusion.13
  97.0 5.1 %collective-permute-start.21 = (bf16[2,128,1280]{2,1,0:T(8,128)(2,1)S(1)}, bf16[2,128,1280]{2,1,0:T(8,128)(2,1)S(1)}, u32[]{:S(2)}, u32[]{:S(2)}) collective-permute-start(bf16[2,128,1280]{2,1,0:T(8,128)(2,1)S(1)} %get-tuple-element.37), channel_id=1, source_target_pairs={{0,2},{1,3},{2,0},{3,1},{4,6},{5,7},{6,4},{7,5},{8,10},{9,11},{10,... | collective-permute-start | bytes 1966088 | tf_op jit(solution)/shard_map/ppermute | solution.py:16
  102.0 1.3 collective-permute-start.22
  103.3 4.6 %collective-permute-start.23 = (bf16[2,128,1280]{2,1,0:T(8,128)(2,1)S(1)}, bf16[2,128,1280]{2,1,0:T(8,128)(2,1)S(1)}, u32[]{:S(2)}, u32[]{:S(2)}) collective-permute-start(bf16[2,128,1280]{2,1,0:T(8,128)(2,1)S(1)} %get-tuple-element.38), channel_id=1, source_target_pairs={{0,4},{1,5},{2,6},{3,7},{4,8},{5,9},{6,10},{7,11},{8,12},{9,13},{1... | collective-permute-start | bytes 1966088 | tf_op jit(solution)/shard_map/ppermute | solution.py:16
  108.0 0.7 fusion.4
  108.7 2.4 %collective-permute-start.27 = (bf16[2,128,1280]{2,1,0:T(8,128)(2,1)S(1)}, bf16[2,128,1280]{2,1,0:T(8,128)(2,1)S(1)}, u32[]{:S(2)}, u32[]{:S(2)}) collective-permute-start(bf16[2,128,1280]{2,1,0:T(8,128)(2,1)S(1)} %get-tuple-element.40), channel_id=1, source_target_pairs={{0,2},{1,3},{2,0},{3,1},{4,6},{5,7},{6,4},{7,5},{8,10},{9,11},{10,... | collective-permute-start | bytes 1966088 | tf_op jit(solution)/shard_map/ppermute | solution.py:16
  111.1 1.3 collective-permute-start.28
  112.4 5.2 %collective-permute-done.21 = bf16[2,128,1280]{2,1,0:T(8,128)(2,1)S(1)} collective-permute-done((bf16[2,128,1280]{2,1,0:T(8,128)(2,1)S(1)}, bf16[2,128,1280]{2,1,0:T(8,128)(2,1)S(1)}, u32[]{:S(2)}, u32[]{:S(2)}) %collective-permute-start.21) | collective-permute-done | bytes 655392 | tf_op jit(solution)/shard_map/ppermute | solution.py:16
  117.6 3.9 %collective-permute-start.29 = (bf16[2,128,1280]{2,1,0:T(8,128)(2,1)S(1)}, bf16[2,128,1280]{2,1,0:T(8,128)(2,1)S(1)}, u32[]{:S(2)}, u32[]{:S(2)}) collective-permute-start(bf16[2,128,1280]{2,1,0:T(8,128)(2,1)S(1)} %get-tuple-element.41), channel_id=1, source_target_pairs={{0,4},{1,5},{2,6},{3,7},{4,8},{5,9},{6,10},{7,11},{8,12},{9,13},{1... | collective-permute-start | bytes 1966088 | tf_op jit(solution)/shard_map/ppermute | solution.py:16
  121.5 1.4 %collective-permute-done.23 = bf16[2,128,1280]{2,1,0:T(8,128)(2,1)S(1)} collective-permute-done((bf16[2,128,1280]{2,1,0:T(8,128)(2,1)S(1)}, bf16[2,128,1280]{2,1,0:T(8,128)(2,1)S(1)}, u32[]{:S(2)}, u32[]{:S(2)}) %collective-permute-start.23) | collective-permute-done | bytes 655392 | tf_op jit(solution)/shard_map/ppermute | solution.py:16
  123.0 0.4 fusion.17
  123.5 7.8 %collective-permute-done.27 = bf16[2,128,1280]{2,1,0:T(8,128)(2,1)S(1)} collective-permute-done((bf16[2,128,1280]{2,1,0:T(8,128)(2,1)S(1)}, bf16[2,128,1280]{2,1,0:T(8,128)(2,1)S(1)}, u32[]{:S(2)}, u32[]{:S(2)}) %collective-permute-start.27) | collective-permute-done | bytes 655392 | tf_op jit(solution)/shard_map/ppermute | solution.py:16
  131.3 1.9 %collective-permute-done.28 = bf16[2,128,1280]{2,1,0:T(8,128)(2,1)S(1)} collective-permute-done((bf16[2,128,1280]{2,1,0:T(8,128)(2,1)S(1)}, bf16[2,128,1280]{2,1,0:T(8,128)(2,1)S(1)}, u32[]{:S(2)}, u32[]{:S(2)}) %collective-permute-start.28) | collective-permute-done | bytes 655392 | tf_op jit(solution)/shard_map/ppermute | solution.py:16
  133.2 2.2 %collective-permute-done.29 = bf16[2,128,1280]{2,1,0:T(8,128)(2,1)S(1)} collective-permute-done((bf16[2,128,1280]{2,1,0:T(8,128)(2,1)S(1)}, bf16[2,128,1280]{2,1,0:T(8,128)(2,1)S(1)}, u32[]{:S(2)}, u32[]{:S(2)}) %collective-permute-start.29) | collective-permute-done | bytes 655392 | tf_op jit(solution)/shard_map/ppermute | solution.py:16
  135.4 0.4 fusion.8
  135.9 0.9 pad_maximum_fusion.4
  136.8 0.9 pad_maximum_fusion.3
  (67 shorter events, 0.3 us)
Async XLA Ops:
  0.6 11.1 %copy-start = (s32[4,3]{1,0:T(4,128)S(1)}, s32[4,3]{1,0:T(4,128)}, u32[]{:S(2)}) copy-start(s32[4,3]{1,0:T(4,128)} %param.10) | copy-start | bytes 148
  2.0 9.8 %copy-start.18 = (s32[4]{0:T(128)S(1)}, s32[4]{0:T(128)}, u32[]{:S(2)}) copy-start(s32[4]{0:T(128)} %param.11) | copy-start | bytes 52
  2.1 50.9 %copy-start.8 = (bf16[2,128,1280]{2,1,0:T(8,128)(2,1)}, bf16[2,128,1280]{2,1,0:T(8,128)(2,1)S(1)}, u32[]{:S(2)}) copy-start(bf16[2,128,1280]{2,1,0:T(8,128)(2,1)S(1)} %pad_maximum_fusion.refs_0_) | copy-start | bytes 1966084
  2.1 18.6 %collective-permute-start = (bf16[2,128,1280]{2,1,0:T(8,128)(2,1)S(1)}, bf16[2,128,1280]{2,1,0:T(8,128)(2,1)S(1)}, u32[]{:S(2)}, u32[]{:S(2)}) collective-permute-start(bf16[2,128,1280]{2,1,0:T(8,128)(2,1)S(1)} %pad_maximum_fusion.refs_0_), channel_id=1, source_target_pairs={{0,2},{1,3},{2,0},{3,1},{4,6},{5,7},{6,4},{7,5},{8,10},{9,11},{10,... | collective-permute-start | bytes 1966088 | tf_op jit(solution)/shard_map/ppermute | solution.py:16
  5.2 20.4 %collective-permute-start.1 = (bf16[2,128,1280]{2,1,0:T(8,128)(2,1)S(1)}, bf16[2,128,1280]{2,1,0:T(8,128)(2,1)}, u32[]{:S(2)}, u32[]{:S(2)}) collective-permute-start(bf16[2,128,1280]{2,1,0:T(8,128)(2,1)S(1)} %pad_maximum_fusion.refs_0_), channel_id=1, source_target_pairs={{0,4},{1,5},{2,6},{3,7},{4,8},{5,9},{6,10},{7,11},{8,12},{9,13},{1... | collective-permute-start | bytes 1966088 | tf_op jit(solution)/shard_map/ppermute | solution.py:16
  9.5 17.9 %collective-permute-start.2 = (bf16[2,128,1280]{2,1,0:T(8,128)(2,1)S(1)}, bf16[2,128,1280]{2,1,0:T(8,128)(2,1)}, u32[]{:S(2)}, u32[]{:S(2)}) collective-permute-start(bf16[2,128,1280]{2,1,0:T(8,128)(2,1)S(1)} %pad_maximum_fusion.refs_0_), channel_id=1, source_target_pairs={{4,0},{5,1},{6,2},{7,3},{8,4},{9,5},{10,6},{11,7},{12,8},{13,9},{1... | collective-permute-start | bytes 1966088 | tf_op jit(solution)/shard_map/ppermute | solution.py:16
  10.8 16.6 %collective-permute-start.3 = (bf16[2,128,1280]{2,1,0:T(8,128)(2,1)S(1)}, bf16[2,128,1280]{2,1,0:T(8,128)(2,1)}, u32[]{:S(2)}, u32[]{:S(2)}) collective-permute-start(bf16[2,128,1280]{2,1,0:T(8,128)(2,1)S(1)} %pad_maximum_fusion.refs_0_), channel_id=1, source_target_pairs={{0,1},{1,0},{2,3},{3,2},{4,5},{5,4},{6,7},{7,6},{8,9},{9,8},{10,11... | collective-permute-start | bytes 1966088 | tf_op jit(solution)/shard_map/ppermute | solution.py:16
  10.9 56.8 %copy-start.7 = (bf16[2,128,1280]{2,1,0:T(8,128)(2,1)}, bf16[2,128,1280]{2,1,0:T(8,128)(2,1)S(1)}, u32[]{:S(2)}) copy-start(bf16[2,128,1280]{2,1,0:T(8,128)(2,1)S(1)} %pad_maximum_fusion.1.refs_0_) | copy-start | bytes 1966084
  10.9 23.0 %collective-permute-start.9 = (bf16[2,128,1280]{2,1,0:T(8,128)(2,1)S(1)}, bf16[2,128,1280]{2,1,0:T(8,128)(2,1)S(1)}, u32[]{:S(2)}, u32[]{:S(2)}) collective-permute-start(bf16[2,128,1280]{2,1,0:T(8,128)(2,1)S(1)} %pad_maximum_fusion.1.refs_0_), channel_id=1, source_target_pairs={{0,2},{1,3},{2,0},{3,1},{4,6},{5,7},{6,4},{7,5},{8,10},{9,11},{10,... | collective-permute-start | bytes 1966088 | tf_op jit(solution)/shard_map/ppermute | solution.py:16
  20.7 32.2 %copy-start.12 = (bf16[2,128,1280]{2,1,0:T(8,128)(2,1)}, bf16[2,128,1280]{2,1,0:T(8,128)(2,1)S(1)}, u32[]{:S(2)}) copy-start(bf16[2,128,1280]{2,1,0:T(8,128)(2,1)S(1)} %collective-permute-done.refs_1_) | copy-start | bytes 1966084
  20.8 16.1 %collective-permute-start.10 = (bf16[2,128,1280]{2,1,0:T(8,128)(2,1)S(1)}, bf16[2,128,1280]{2,1,0:T(8,128)(2,1)}, u32[]{:S(2)}, u32[]{:S(2)}) collective-permute-start(bf16[2,128,1280]{2,1,0:T(8,128)(2,1)S(1)} %pad_maximum_fusion.1.refs_0_), channel_id=1, source_target_pairs={{0,4},{1,5},{2,6},{3,7},{4,8},{5,9},{6,10},{7,11},{8,12},{9,13},{1... | collective-permute-start | bytes 1966088 | tf_op jit(solution)/shard_map/ppermute | solution.py:16
  25.6 16.3 %collective-permute-start.11 = (bf16[2,128,1280]{2,1,0:T(8,128)(2,1)S(1)}, bf16[2,128,1280]{2,1,0:T(8,128)(2,1)}, u32[]{:S(2)}, u32[]{:S(2)}) collective-permute-start(bf16[2,128,1280]{2,1,0:T(8,128)(2,1)S(1)} %pad_maximum_fusion.1.refs_0_), channel_id=1, source_target_pairs={{4,0},{5,1},{6,2},{7,3},{8,4},{9,5},{10,6},{11,7},{12,8},{13,9},{1... | collective-permute-start | bytes 1966088 | tf_op jit(solution)/shard_map/ppermute | solution.py:16
  27.4 14.5 %collective-permute-start.12 = (bf16[2,128,1280]{2,1,0:T(8,128)(2,1)S(1)}, bf16[2,128,1280]{2,1,0:T(8,128)(2,1)S(1)}, u32[]{:S(2)}, u32[]{:S(2)}) collective-permute-start(bf16[2,128,1280]{2,1,0:T(8,128)(2,1)S(1)} %pad_maximum_fusion.1.refs_0_), channel_id=1, source_target_pairs={{0,1},{1,0},{2,3},{3,2},{4,5},{5,4},{6,7},{7,6},{8,9},{9,8},{10,11... | collective-permute-start | bytes 1966088 | tf_op jit(solution)/shard_map/ppermute | solution.py:16
  27.4 16.9 %collective-permute-start.4 = (bf16[2,128,1280]{2,1,0:T(8,128)(2,1)S(1)}, bf16[2,128,1280]{2,1,0:T(8,128)(2,1)S(1)}, u32[]{:S(2)}, u32[]{:S(2)}) collective-permute-start(bf16[2,128,1280]{2,1,0:T(8,128)(2,1)S(1)} %collective-permute-done.refs_1_), channel_id=1, source_target_pairs={{0,1},{1,0},{2,3},{3,2},{4,5},{5,4},{6,7},{7,6},{8,9},{9,8},{10,11... | collective-permute-start | bytes 1966088 | tf_op jit(solution)/shard_map/ppermute | solution.py:16
  33.9 33.8 %copy-start.11 = (bf16[2,128,1280]{2,1,0:T(8,128)(2,1)}, bf16[2,128,1280]{2,1,0:T(8,128)(2,1)S(1)}, u32[]{:S(2)}) copy-start(bf16[2,128,1280]{2,1,0:T(8,128)(2,1)S(1)} %collective-permute-done.9.refs_1_) | copy-start | bytes 1966084
  33.9 12.9 %collective-permute-start.7 = (bf16[2,128,1280]{2,1,0:T(8,128)(2,1)S(1)}, bf16[2,128,1280]{2,1,0:T(8,128)(2,1)S(1)}, u32[]{:S(2)}, u32[]{:S(2)}) collective-permute-start(bf16[2,128,1280]{2,1,0:T(8,128)(2,1)S(1)} %collective-permute-done.refs_1_), channel_id=1, source_target_pairs={{0,5},{3,6},{4,9},{7,10},{8,13},{11,14},{16,21},{19,22},{20,25},{2... | collective-permute-start | bytes 1966088 | tf_op jit(solution)/shard_map/ppermute | solution.py:16
  36.8 13.3 %collective-permute-start.8 = (bf16[2,128,1280]{2,1,0:T(8,128)(2,1)S(1)}, bf16[2,128,1280]{2,1,0:T(8,128)(2,1)S(1)}, u32[]{:S(2)}, u32[]{:S(2)}) collective-permute-start(bf16[2,128,1280]{2,1,0:T(8,128)(2,1)S(1)} %collective-permute-done.refs_1_), channel_id=1, source_target_pairs={{4,1},{7,2},{8,5},{11,6},{12,9},{15,10},{20,17},{23,18},{24,21},{2... | collective-permute-start | bytes 1966088 | tf_op jit(solution)/shard_map/ppermute | solution.py:16
  41.9 9.7 %collective-permute-start.5 = (bf16[2,128,1280]{2,1,0:T(8,128)(2,1)}, bf16[2,128,1280]{2,1,0:T(8,128)(2,1)S(1)}, u32[]{:S(2)}, u32[]{:S(2)}) collective-permute-start(bf16[2,128,1280]{2,1,0:T(8,128)(2,1)} %collective-permute-done.1.refs_2_), channel_id=1, source_target_pairs={{0,1},{1,0},{2,3},{3,2},{4,5},{5,4},{6,7},{7,6},{8,9},{9,8},{10,11... | collective-permute-start | bytes 1966088 | tf_op jit(solution)/shard_map/ppermute | solution.py:16
  41.9 2.5 %copy-start.13 = (bf16[2,128,1280]{2,1,0:T(8,128)(2,1)}, bf16[2,128,1280]{2,1,0:T(8,128)(2,1)S(1)}, u32[]{:S(2)}) copy-start(bf16[2,128,1280]{2,1,0:T(8,128)(2,1)S(1)} %collective-permute-done.12.refs_4_) | copy-start | bytes 1966084
  41.9 10.6 %collective-permute-start.6 = (bf16[2,128,1280]{2,1,0:T(8,128)(2,1)}, bf16[2,128,1280]{2,1,0:T(8,128)(2,1)}, u32[]{:S(2)}, u32[]{:S(2)}) collective-permute-start(bf16[2,128,1280]{2,1,0:T(8,128)(2,1)} %collective-permute-done.2.refs_3_), channel_id=1, source_target_pairs={{0,1},{1,0},{2,3},{3,2},{4,5},{5,4},{6,7},{7,6},{8,9},{9,8},{10,11... | collective-permute-start | bytes 1966088 | tf_op jit(solution)/shard_map/ppermute | solution.py:16
  44.4 0.8 copy-start.14
  44.4 23.4 %collective-permute-start.13 = (bf16[2,128,1280]{2,1,0:T(8,128)(2,1)S(1)}, bf16[2,128,1280]{2,1,0:T(8,128)(2,1)}, u32[]{:S(2)}, u32[]{:S(2)}) collective-permute-start(bf16[2,128,1280]{2,1,0:T(8,128)(2,1)S(1)} %collective-permute-done.9.refs_1_), channel_id=1, source_target_pairs={{0,1},{1,0},{2,3},{3,2},{4,5},{5,4},{6,7},{7,6},{8,9},{9,8},{10,11... | collective-permute-start | bytes 1966088 | tf_op jit(solution)/shard_map/ppermute | solution.py:16
  46.9 3.2 %copy-start.15 = (bf16[2,128,1280]{2,1,0:T(8,128)(2,1)}, bf16[2,128,1280]{2,1,0:T(8,128)(2,1)S(1)}, u32[]{:S(2)}) copy-start(bf16[2,128,1280]{2,1,0:T(8,128)(2,1)S(1)} %collective-permute-done.7.refs_8_) | copy-start | bytes 1966084
  46.9 21.0 %collective-permute-start.16 = (bf16[2,128,1280]{2,1,0:T(8,128)(2,1)S(1)}, bf16[2,128,1280]{2,1,0:T(8,128)(2,1)}, u32[]{:S(2)}, u32[]{:S(2)}) collective-permute-start(bf16[2,128,1280]{2,1,0:T(8,128)(2,1)S(1)} %collective-permute-done.9.refs_1_), channel_id=1, source_target_pairs={{0,5},{3,6},{4,9},{7,10},{8,13},{11,14},{16,21},{19,22},{20,25},{2... | collective-permute-start | bytes 1966088 | tf_op jit(solution)/shard_map/ppermute | solution.py:16
  50.1 1.5 %copy-start.16 = (bf16[2,128,1280]{2,1,0:T(8,128)(2,1)}, bf16[2,128,1280]{2,1,0:T(8,128)(2,1)S(1)}, u32[]{:S(2)}) copy-start(bf16[2,128,1280]{2,1,0:T(8,128)(2,1)S(1)} %collective-permute-done.8.refs_9_) | copy-start | bytes 1966084
  50.1 17.8 %collective-permute-start.17 = (bf16[2,128,1280]{2,1,0:T(8,128)(2,1)S(1)}, bf16[2,128,1280]{2,1,0:T(8,128)(2,1)}, u32[]{:S(2)}, u32[]{:S(2)}) collective-permute-start(bf16[2,128,1280]{2,1,0:T(8,128)(2,1)S(1)} %collective-permute-done.9.refs_1_), channel_id=1, source_target_pairs={{4,1},{7,2},{8,5},{11,6},{12,9},{15,10},{20,17},{23,18},{24,21},{2... | collective-permute-start | bytes 1966088 | tf_op jit(solution)/shard_map/ppermute | solution.py:16
  51.6 0.8 copy-start.17
  52.4 15.5 %collective-permute-start.14 = (bf16[2,128,1280]{2,1,0:T(8,128)(2,1)}, bf16[2,128,1280]{2,1,0:T(8,128)(2,1)}, u32[]{:S(2)}, u32[]{:S(2)}) collective-permute-start(bf16[2,128,1280]{2,1,0:T(8,128)(2,1)} %collective-permute-done.10.refs_2_), channel_id=1, source_target_pairs={{0,1},{1,0},{2,3},{3,2},{4,5},{5,4},{6,7},{7,6},{8,9},{9,8},{10,11... | collective-permute-start | bytes 1966088 | tf_op jit(solution)/shard_map/ppermute | solution.py:16
  52.4 15.5 %collective-permute-start.15 = (bf16[2,128,1280]{2,1,0:T(8,128)(2,1)}, bf16[2,128,1280]{2,1,0:T(8,128)(2,1)}, u32[]{:S(2)}, u32[]{:S(2)}) collective-permute-start(bf16[2,128,1280]{2,1,0:T(8,128)(2,1)} %collective-permute-done.11.refs_3_), channel_id=1, source_target_pairs={{0,1},{1,0},{2,3},{3,2},{4,5},{5,4},{6,7},{7,6},{8,9},{9,8},{10,11... | collective-permute-start | bytes 1966088 | tf_op jit(solution)/shard_map/ppermute | solution.py:16
  67.8 28.4 %collective-permute-start.18 = (bf16[4,2,128,1280]{3,2,1,0:T(8,128)(2,1)}, bf16[4,2,128,1280]{3,2,1,0:T(8,128)(2,1)S(1)}, u32[]{:S(2)}, u32[]{:S(2)}) collective-permute-start(bf16[4,2,128,1280]{3,2,1,0:T(8,128)(2,1)} %get-tuple-element.22), channel_id=1, source_target_pairs={{0,1},{1,0},{2,3},{3,2},{4,5},{5,4},{6,7},{7,6},{8,9},{9,8},{10,11... | collective-permute-start | bytes 7864328 | tf_op jit(solution)/shard_map/ppermute | solution.py:16
  67.9 28.3 %copy-start.3 = (bf16[2,128,1280]{2,1,0:T(8,128)(2,1)S(1)}, bf16[2,128,1280]{2,1,0:T(8,128)(2,1)}, u32[]{:S(2)}) copy-start(bf16[2,128,1280]{2,1,0:T(8,128)(2,1)} %get-tuple-element.27) | copy-start | bytes 1966084
  82.8 13.4 %copy-start.1 = (bf16[2,128,1280]{2,1,0:T(8,128)(2,1)S(1)}, bf16[2,128,1280]{2,1,0:T(8,128)(2,1)}, u32[]{:S(2)}) copy-start(bf16[2,128,1280]{2,1,0:T(8,128)(2,1)} %get-tuple-element.23) | copy-start | bytes 1966084
  82.8 13.4 %copy-start.2 = (bf16[2,128,1280]{2,1,0:T(8,128)(2,1)S(1)}, bf16[2,128,1280]{2,1,0:T(8,128)(2,1)}, u32[]{:S(2)}) copy-start(bf16[2,128,1280]{2,1,0:T(8,128)(2,1)} %get-tuple-element.26) | copy-start | bytes 1966084
  82.9 25.1 %collective-permute-start.24 = (bf16[4,2,128,1280]{3,2,1,0:T(8,128)(2,1)}, bf16[4,2,128,1280]{3,2,1,0:T(8,128)(2,1)S(1)}, u32[]{:S(2)}, u32[]{:S(2)}) collective-permute-start(bf16[4,2,128,1280]{3,2,1,0:T(8,128)(2,1)} %get-tuple-element.29), channel_id=1, source_target_pairs={{0,1},{1,0},{2,3},{3,2},{4,5},{5,4},{6,7},{7,6},{8,9},{9,8},{10,11... | collective-permute-start | bytes 7864328 | tf_op jit(solution)/shard_map/ppermute | solution.py:16
  83.4 12.1 %collective-permute-start.19 = (bf16[2,128,1280]{2,1,0:T(8,128)(2,1)}, bf16[2,128,1280]{2,1,0:T(8,128)(2,1)S(1)}, u32[]{:S(2)}, u32[]{:S(2)}) collective-permute-start(bf16[2,128,1280]{2,1,0:T(8,128)(2,1)} %get-tuple-element.24), channel_id=1, source_target_pairs={{5,0},{6,3},{9,4},{10,7},{13,8},{14,11},{21,16},{22,19},{25,20},{2... | collective-permute-start | bytes 1966088 | tf_op jit(solution)/shard_map/ppermute | solution.py:16
  84.7 11.5 %collective-permute-start.20 = (bf16[2,128,1280]{2,1,0:T(8,128)(2,1)}, bf16[2,128,1280]{2,1,0:T(8,128)(2,1)S(1)}, u32[]{:S(2)}, u32[]{:S(2)}) collective-permute-start(bf16[2,128,1280]{2,1,0:T(8,128)(2,1)} %get-tuple-element.25), channel_id=1, source_target_pairs={{1,4},{2,7},{5,8},{6,11},{9,12},{10,15},{17,20},{18,23},{21,24},{2... | collective-permute-start | bytes 1966088 | tf_op jit(solution)/shard_map/ppermute | solution.py:16
  85.4 17.9 %collective-permute-start.25 = (bf16[2,128,1280]{2,1,0:T(8,128)(2,1)}, bf16[2,128,1280]{2,1,0:T(8,128)(2,1)S(1)}, u32[]{:S(2)}, u32[]{:S(2)}) collective-permute-start(bf16[2,128,1280]{2,1,0:T(8,128)(2,1)} %get-tuple-element.31), channel_id=1, source_target_pairs={{5,0},{6,3},{9,4},{10,7},{13,8},{14,11},{21,16},{22,19},{25,20},{2... | collective-permute-start | bytes 1966088 | tf_op jit(solution)/shard_map/ppermute | solution.py:16
  95.5 12.4 %collective-permute-start.26 = (bf16[2,128,1280]{2,1,0:T(8,128)(2,1)}, bf16[2,128,1280]{2,1,0:T(8,128)(2,1)S(1)}, u32[]{:S(2)}, u32[]{:S(2)}) collective-permute-start(bf16[2,128,1280]{2,1,0:T(8,128)(2,1)} %get-tuple-element.32), channel_id=1, source_target_pairs={{1,4},{2,7},{5,8},{6,11},{9,12},{10,15},{17,20},{18,23},{21,24},{2... | collective-permute-start | bytes 1966088 | tf_op jit(solution)/shard_map/ppermute | solution.py:16
  96.3 11.7 %copy-start.4 = (bf16[2,128,1280]{2,1,0:T(8,128)(2,1)S(1)}, bf16[2,128,1280]{2,1,0:T(8,128)(2,1)}, u32[]{:S(2)}) copy-start(bf16[2,128,1280]{2,1,0:T(8,128)(2,1)} %get-tuple-element.30) | copy-start | bytes 1966084
  96.3 11.7 %copy-start.5 = (bf16[2,128,1280]{2,1,0:T(8,128)(2,1)S(1)}, bf16[2,128,1280]{2,1,0:T(8,128)(2,1)}, u32[]{:S(2)}) copy-start(bf16[2,128,1280]{2,1,0:T(8,128)(2,1)} %get-tuple-element.33) | copy-start | bytes 1966084
  96.3 11.7 %copy-start.6 = (bf16[2,128,1280]{2,1,0:T(8,128)(2,1)S(1)}, bf16[2,128,1280]{2,1,0:T(8,128)(2,1)}, u32[]{:S(2)}) copy-start(bf16[2,128,1280]{2,1,0:T(8,128)(2,1)} %get-tuple-element.34) | copy-start | bytes 1966084
  97.0 20.6 %collective-permute-start.21 = (bf16[2,128,1280]{2,1,0:T(8,128)(2,1)S(1)}, bf16[2,128,1280]{2,1,0:T(8,128)(2,1)S(1)}, u32[]{:S(2)}, u32[]{:S(2)}) collective-permute-start(bf16[2,128,1280]{2,1,0:T(8,128)(2,1)S(1)} %get-tuple-element.37), channel_id=1, source_target_pairs={{0,2},{1,3},{2,0},{3,1},{4,6},{5,7},{6,4},{7,5},{8,10},{9,11},{10,... | collective-permute-start | bytes 1966088 | tf_op jit(solution)/shard_map/ppermute | solution.py:16
  102.0 19.5 %collective-permute-start.22 = (bf16[2,128,1280]{2,1,0:T(8,128)(2,1)S(1)}, bf16[2,128,1280]{2,1,0:T(8,128)(2,1)S(1)}, u32[]{:S(2)}, u32[]{:S(2)}) collective-permute-start(bf16[2,128,1280]{2,1,0:T(8,128)(2,1)S(1)} %get-tuple-element.39), channel_id=1, source_target_pairs={{4,0},{5,1},{6,2},{7,3},{8,4},{9,5},{10,6},{11,7},{12,8},{13,9},{1... | collective-permute-start | bytes 1966088 | tf_op jit(solution)/shard_map/ppermute | solution.py:16
  103.3 19.7 %collective-permute-start.23 = (bf16[2,128,1280]{2,1,0:T(8,128)(2,1)S(1)}, bf16[2,128,1280]{2,1,0:T(8,128)(2,1)S(1)}, u32[]{:S(2)}, u32[]{:S(2)}) collective-permute-start(bf16[2,128,1280]{2,1,0:T(8,128)(2,1)S(1)} %get-tuple-element.38), channel_id=1, source_target_pairs={{0,4},{1,5},{2,6},{3,7},{4,8},{5,9},{6,10},{7,11},{8,12},{9,13},{1... | collective-permute-start | bytes 1966088 | tf_op jit(solution)/shard_map/ppermute | solution.py:16
  108.0 15.0 %copy-start.9 = (bf16[2,128,1280]{2,1,0:T(8,128)(2,1)S(1)}, bf16[2,128,1280]{2,1,0:T(8,128)(2,1)}, u32[]{:S(2)}) copy-start(bf16[2,128,1280]{2,1,0:T(8,128)(2,1)} %get-tuple-element.21) | copy-start | bytes 1966084
  108.7 22.6 %collective-permute-start.27 = (bf16[2,128,1280]{2,1,0:T(8,128)(2,1)S(1)}, bf16[2,128,1280]{2,1,0:T(8,128)(2,1)S(1)}, u32[]{:S(2)}, u32[]{:S(2)}) collective-permute-start(bf16[2,128,1280]{2,1,0:T(8,128)(2,1)S(1)} %get-tuple-element.40), channel_id=1, source_target_pairs={{0,2},{1,3},{2,0},{3,1},{4,6},{5,7},{6,4},{7,5},{8,10},{9,11},{10,... | collective-permute-start | bytes 1966088 | tf_op jit(solution)/shard_map/ppermute | solution.py:16
  111.1 22.1 %collective-permute-start.28 = (bf16[2,128,1280]{2,1,0:T(8,128)(2,1)S(1)}, bf16[2,128,1280]{2,1,0:T(8,128)(2,1)S(1)}, u32[]{:S(2)}, u32[]{:S(2)}) collective-permute-start(bf16[2,128,1280]{2,1,0:T(8,128)(2,1)S(1)} %get-tuple-element.42), channel_id=1, source_target_pairs={{4,0},{5,1},{6,2},{7,3},{8,4},{9,5},{10,6},{11,7},{12,8},{13,9},{1... | collective-permute-start | bytes 1966088 | tf_op jit(solution)/shard_map/ppermute | solution.py:16
  117.6 17.8 %collective-permute-start.29 = (bf16[2,128,1280]{2,1,0:T(8,128)(2,1)S(1)}, bf16[2,128,1280]{2,1,0:T(8,128)(2,1)S(1)}, u32[]{:S(2)}, u32[]{:S(2)}) collective-permute-start(bf16[2,128,1280]{2,1,0:T(8,128)(2,1)S(1)} %get-tuple-element.41), channel_id=1, source_target_pairs={{0,4},{1,5},{2,6},{3,7},{4,8},{5,9},{6,10},{7,11},{8,12},{9,13},{1... | collective-permute-start | bytes 1966088 | tf_op jit(solution)/shard_map/ppermute | solution.py:16
  123.4 12.0 %copy-start.10 = (bf16[2,128,1280]{2,1,0:T(8,128)(2,1)S(1)}, bf16[2,128,1280]{2,1,0:T(8,128)(2,1)}, u32[]{:S(2)}) copy-start(bf16[2,128,1280]{2,1,0:T(8,128)(2,1)} %get-tuple-element.28) | copy-start | bytes 1966084

commit v22 on v18

--- a/solution.py
+++ b/solution.py
@@ -87,7 +87,7 @@
             q = q_ref[:, cols]
             g = g_ref[:, cols]
             scores = lax.dot_general(q, k, nt, preferred_element_type=jnp.float32) * inv_root
-            masked = jnp.where(mask_ref[...] != 0, scores, -1e30)
+            masked = scores + mask_ref[...]
             highest = jnp.max(masked, axis=1, keepdims=True)
             total_mass = jnp.sum(jnp.exp(masked - highest), axis=1, keepdims=True)
             log_total = highest + jnp.log(total_mass)
@@ -220,7 +220,7 @@
     base_rows = jnp.arange(rows_own, dtype=jnp.int32)
     far_rows = jnp.concatenate([source * rows_own + base_rows for source in sources])
     own_rows = device * rows_own + base_rows
-    forward_mask = allowed(own_rows, far_rows, frame_keep, band_window, frame_len).astype(jnp.int32)
+    forward_mask = jnp.where(allowed(own_rows, far_rows, frame_keep, band_window, frame_len), 0.0, -1e30)
     heads = channel_total // HD
     chunk_heads = heads // CHUNKS if heads % CHUNKS == 0 else heads
     width = chunk_heads * HD

time: 137 us -> 137 us (level)
    select_n x0 -> x1, other arithmetic: none -> 1.7 us  [body(): jnp.where(allowed(own_rows, far_rows, frame_keep, band_window, frame_len)...]
    convert_element_type x1 -> x0, other arithmetic: 1.66 us -> none  [body(): allowed(own_rows, far_rows, frame_keep, band_window, frame_len)]
where the time goes in v22:
time: 137 us; the launch traced here: 136 us
  starting transfers between devices  48.1 us (35%)
  waiting for transfers between devices  44.5 us (32%)
  Pallas kernels  28.1 us (21%)
  other arithmetic  9.81 us (7%)
  local copies, waits for them, and re-layouts  4.27 us (3%)
  between operations  1.37 us (1%)
    ppermute x30, starting transfers between devices, send(): return lax.ppermute(value, 'tm', pairs)  48.1 us
    ppermute x30, waiting for transfers between devices, send(): return lax.ppermute(value, 'tm', pairs)  44.5 us
    pallas_call x2, Pallas kernels, attention_backward(): pl.pallas_call(kernel, grid=(heads // STEP_HEADS,), in_specs=in_specs, ou...  28.1 us
  transfers between devices with their start and end apart: 30, of which 11 were waited for; matrix products, arithmetic and copies ran while one was open for 6% of the time, Pallas kernels for 21%

profile of v22, /device:TPU:0, one launch (start us, length us, event | category | flops | bytes accessed | tf_op | source)
XLA Modules:
  0.0 136.1 jit_solution(8549650236195847747)
XLA Ops:
  0.6 0.0 copy-start
  0.6 1.4 slice_bitcast_fusion.14
  2.0 0.0 copy-start.18
  2.0 0.1 pad_maximum_fusion.refs_0_
  2.1 3.1 %collective-permute-start = (bf16[2,128,1280]{2,1,0:T(8,128)(2,1)S(1)}, bf16[2,128,1280]{2,1,0:T(8,128)(2,1)S(1)}, u32[]{:S(2)}, u32[]{:S(2)}) collective-permute-start(bf16[2,128,1280]{2,1,0:T(8,128)(2,1)S(1)} %pad_maximum_fusion.refs_0_), channel_id=1, source_target_pairs={{0,2},{1,3},{2,0},{3,1},{4,6},{5,7},{6,4},{7,5},{8,10},{9,11},{10,... | collective-permute-start | bytes 1966088 | tf_op jit(solution)/shard_map/ppermute | solution.py:16
  5.2 4.3 %collective-permute-start.1 = (bf16[2,128,1280]{2,1,0:T(8,128)(2,1)S(1)}, bf16[2,128,1280]{2,1,0:T(8,128)(2,1)}, u32[]{:S(2)}, u32[]{:S(2)}) collective-permute-start(bf16[2,128,1280]{2,1,0:T(8,128)(2,1)S(1)} %pad_maximum_fusion.refs_0_), channel_id=1, source_target_pairs={{0,4},{1,5},{2,6},{3,7},{4,8},{5,9},{6,10},{7,11},{8,12},{9,13},{1... | collective-permute-start | bytes 1966088 | tf_op jit(solution)/shard_map/ppermute | solution.py:16
  9.5 1.3 collective-permute-start.2
  10.8 0.1 collective-permute-start.3
  10.9 0.1 pad_maximum_fusion.1.refs_0_
  10.9 0.0 copy-start.7
  10.9 0.6 collective-permute-start.9
  11.8 0.6 dynamic_slice.9
  12.4 8.3 %collective-permute-done.refs_1_ = bf16[2,128,1280]{2,1,0:T(8,128)(2,1)S(1)} collective-permute-done((bf16[2,128,1280]{2,1,0:T(8,128)(2,1)S(1)}, bf16[2,128,1280]{2,1,0:T(8,128)(2,1)S(1)}, u32[]{:S(2)}, u32[]{:S(2)}) %collective-permute-start) | collective-permute-done | bytes 655392 | tf_op jit(solution)/shard_map/ppermute | solution.py:16
  20.8 4.8 %collective-permute-start.10 = (bf16[2,128,1280]{2,1,0:T(8,128)(2,1)S(1)}, bf16[2,128,1280]{2,1,0:T(8,128)(2,1)}, u32[]{:S(2)}, u32[]{:S(2)}) collective-permute-start(bf16[2,128,1280]{2,1,0:T(8,128)(2,1)S(1)} %pad_maximum_fusion.1.refs_0_), channel_id=1, source_target_pairs={{0,4},{1,5},{2,6},{3,7},{4,8},{5,9},{6,10},{7,11},{8,12},{9,13},{1... | collective-permute-start | bytes 1966088 | tf_op jit(solution)/shard_map/ppermute | solution.py:16
  25.6 0.0 collective-permute-done.1.refs_2_
  25.6 1.3 collective-permute-start.11
  26.9 0.5 collective-permute-done.2.refs_3_
  27.4 0.0 collective-permute-start.12
  27.4 0.6 collective-permute-start.4
  28.0 0.6 fusion.24
  28.7 5.3 %collective-permute-done.9.refs_1_ = bf16[2,128,1280]{2,1,0:T(8,128)(2,1)S(1)} collective-permute-done((bf16[2,128,1280]{2,1,0:T(8,128)(2,1)S(1)}, bf16[2,128,1280]{2,1,0:T(8,128)(2,1)S(1)}, u32[]{:S(2)}, u32[]{:S(2)}) %collective-permute-start.9) | collective-permute-done | bytes 655392 | tf_op jit(solution)/shard_map/ppermute | solution.py:16
  33.9 2.4 %collective-permute-start.7 = (bf16[2,128,1280]{2,1,0:T(8,128)(2,1)S(1)}, bf16[2,128,1280]{2,1,0:T(8,128)(2,1)S(1)}, u32[]{:S(2)}, u32[]{:S(2)}) collective-permute-start(bf16[2,128,1280]{2,1,0:T(8,128)(2,1)S(1)} %collective-permute-done.refs_1_), channel_id=1, source_target_pairs={{0,5},{3,6},{4,9},{7,10},{8,13},{11,14},{16,21},{19,22},{20,25},{2... | collective-permute-start | bytes 1966088 | tf_op jit(solution)/shard_map/ppermute | solution.py:16
  36.4 0.4 collective-permute-done.10.refs_2_
  36.8 0.7 collective-permute-start.8
  37.5 4.4 %collective-permute-done.11.refs_3_ = bf16[2,128,1280]{2,1,0:T(8,128)(2,1)} collective-permute-done((bf16[2,128,1280]{2,1,0:T(8,128)(2,1)S(1)}, bf16[2,128,1280]{2,1,0:T(8,128)(2,1)}, u32[]{:S(2)}, u32[]{:S(2)}) %collective-permute-start.11) | collective-permute-done | bytes 655392 | tf_op jit(solution)/shard_map/ppermute | solution.py:16
  41.9 0.0 collective-permute-start.5
  41.9 0.0 collective-permute-done.12.refs_4_
  41.9 0.5 collective-permute-start.6
  42.4 2.0 %fusion.23 = (pred[1280]{0:T(1024)(128)(4,1)S(1)}, pred[1280]{0:T(1024)(128)(4,1)S(1)}) fusion(s32[1280]{0:T(1024)S(1)} %constant_dynamic-update-slice_fusion, s32[]{:T(128)} %bitcast.3, s32[]{:T(128)} %bitcast.2, s32[]{:T(128)} %bitcast.1, s32[]{:T(128)S(6)} %select_n.68), kind=kLoop, calls=%fused_computation.60 | loop fusion | flops 37120 | bytes 7696 | tf_op jit(solution)/shard_map/and | solution.py:65
  44.4 0.2 collective-permute-start.13
  44.6 0.7 copy-done.14
  45.2 1.7 %fusion.20.mask_ref = f32[128,1280]{1,0:T(8,128)} fusion(s32[]{:T(128)} %bitcast.4, s32[1280]{0:T(1024)S(1)} %multiply_subtract_fusion, s32[128]{0:T(128)S(1)} %broadcast_subtract_fusion, pred[1280]{0:T(1024)(128)(4,1)S(1)} %get-tuple-element.36, pred[1280]{0:T(1024)(128)(4,1)S(1)} %get-tuple-element.35, pred[128]{0:T(512)(128)(4,1)S(1)} %compare_and_fusion), kind=kLoop, calls=%fused_computation.42 | loop fusion | flops 1146880 | bytes 663684 | tf_op jit(solution)/shard_map/jit(_where)/select_n | solution.py:223
  46.9 3.2 %collective-permute-start.16 = (bf16[2,128,1280]{2,1,0:T(8,128)(2,1)S(1)}, bf16[2,128,1280]{2,1,0:T(8,128)(2,1)}, u32[]{:S(2)}, u32[]{:S(2)}) collective-permute-start(bf16[2,128,1280]{2,1,0:T(8,128)(2,1)S(1)} %collective-permute-done.9.refs_1_), channel_id=1, source_target_pairs={{0,5},{3,6},{4,9},{7,10},{8,13},{11,14},{16,21},{19,22},{20,25},{2... | collective-permute-start | bytes 1966088 | tf_op jit(solution)/shard_map/ppermute | solution.py:16
  50.1 1.5 %collective-permute-start.17 = (bf16[2,128,1280]{2,1,0:T(8,128)(2,1)S(1)}, bf16[2,128,1280]{2,1,0:T(8,128)(2,1)}, u32[]{:S(2)}, u32[]{:S(2)}) collective-permute-start(bf16[2,128,1280]{2,1,0:T(8,128)(2,1)S(1)} %collective-permute-done.9.refs_1_), channel_id=1, source_target_pairs={{4,1},{7,2},{8,5},{11,6},{12,9},{15,10},{20,17},{23,18},{24,21},{2... | collective-permute-start | bytes 1966088 | tf_op jit(solution)/shard_map/ppermute | solution.py:16
  51.7 0.8 copy-done.17
  52.5 0.5 collective-permute-start.15
  53.0 14.0 %shard_map.85 = (bf16[128,1280]{1,0:T(8,128)(2,1)}, bf16[2,128,1280]{2,1,0:T(8,128)(2,1)}, bf16[4,2,128,1280]{3,2,1,0:T(8,128)(2,1)}, bf16[2,128,1280]{2,1,0:T(8...) custom-call(f32[128,1280]{1,0:T(8,128)} %fusion.20.mask_ref, ...), custom_call_target="tpu_custom_call" | custom-call | flops 2516582400 | bytes 14745600 | tf_op jit(solution)/shard_map/pallas_call | solution.py:122
  67.0 0.1 collective-permute-start.18
  67.1 14.2 %shard_map.86 = (bf16[128,1280]{1,0:T(8,128)(2,1)}, bf16[2,128,1280]{2,1,0:T(8,128)(2,1)}, bf16[4,2,128,1280]{3,2,1,0:T(8,128)(2,1)}, bf16[2,128,1280]{2,1,0:T(8...) custom-call(f32[128,1280]{1,0:T(8,128)} %fusion.20.mask_ref, ...), custom_call_target="tpu_custom_call" | custom-call | flops 2516582400 | bytes 14745600 | tf_op jit(solution)/shard_map/pallas_call | solution.py:122
  81.3 0.5 collective-permute-start.24
  81.8 1.3 collective-permute-start.19
  83.1 0.7 collective-permute-start.20
  83.8 1.3 collective-permute-start.25
  85.1 2.0 %pad_maximum_fusion.2 = bf16[128,2560]{1,0:T(8,128)(2,1)} fusion(bf16[128,1280]{1,0:T(8,128)(2,1)} %get-tuple-element.20, bf16[128,1280]{1,0:T(8,128)(2,1)} %get-tuple-element.19), kind=kLoop, calls=%fused_computation.36 | loop fusion | flops 1310720 | bytes 1310720 | tf_op jit(solution)/shard_map/concatenate | solution.py:245
  87.1 6.9 %collective-permute-done.19 = bf16[2,128,1280]{2,1,0:T(8,128)(2,1)S(1)} collective-permute-done((bf16[2,128,1280]{2,1,0:T(8,128)(2,1)}, bf16[2,128,1280]{2,1,0:T(8,128)(2,1)S(1)}, u32[]{:S(2)}, u32[]{:S(2)}) %collective-permute-start.19) | collective-permute-done | bytes 655392 | tf_op jit(solution)/shard_map/ppermute | solution.py:16
  93.9 0.7 collective-permute-start.26
  94.7 0.7 fusion.13
  95.4 5.1 %collective-permute-start.21 = (bf16[2,128,1280]{2,1,0:T(8,128)(2,1)S(1)}, bf16[2,128,1280]{2,1,0:T(8,128)(2,1)S(1)}, u32[]{:S(2)}, u32[]{:S(2)}) collective-permute-start(bf16[2,128,1280]{2,1,0:T(8,128)(2,1)S(1)} %get-tuple-element.37), channel_id=1, source_target_pairs={{0,2},{1,3},{2,0},{3,1},{4,6},{5,7},{6,4},{7,5},{8,10},{9,11},{10,... | collective-permute-start | bytes 1966088 | tf_op jit(solution)/shard_map/ppermute | solution.py:16
  100.5 1.3 collective-permute-start.22
  101.8 4.6 %collective-permute-start.23 = (bf16[2,128,1280]{2,1,0:T(8,128)(2,1)S(1)}, bf16[2,128,1280]{2,1,0:T(8,128)(2,1)S(1)}, u32[]{:S(2)}, u32[]{:S(2)}) collective-permute-start(bf16[2,128,1280]{2,1,0:T(8,128)(2,1)S(1)} %get-tuple-element.38), channel_id=1, source_target_pairs={{0,4},{1,5},{2,6},{3,7},{4,8},{5,9},{6,10},{7,11},{8,12},{9,13},{1... | collective-permute-start | bytes 1966088 | tf_op jit(solution)/shard_map/ppermute | solution.py:16
  106.4 0.7 fusion.4
  107.1 2.4 %collective-permute-start.27 = (bf16[2,128,1280]{2,1,0:T(8,128)(2,1)S(1)}, bf16[2,128,1280]{2,1,0:T(8,128)(2,1)S(1)}, u32[]{:S(2)}, u32[]{:S(2)}) collective-permute-start(bf16[2,128,1280]{2,1,0:T(8,128)(2,1)S(1)} %get-tuple-element.40), channel_id=1, source_target_pairs={{0,2},{1,3},{2,0},{3,1},{4,6},{5,7},{6,4},{7,5},{8,10},{9,11},{10,... | collective-permute-start | bytes 1966088 | tf_op jit(solution)/shard_map/ppermute | solution.py:16
  109.6 1.3 collective-permute-start.28
  110.9 5.2 %collective-permute-done.21 = bf16[2,128,1280]{2,1,0:T(8,128)(2,1)S(1)} collective-permute-done((bf16[2,128,1280]{2,1,0:T(8,128)(2,1)S(1)}, bf16[2,128,1280]{2,1,0:T(8,128)(2,1)S(1)}, u32[]{:S(2)}, u32[]{:S(2)}) %collective-permute-start.21) | collective-permute-done | bytes 655392 | tf_op jit(solution)/shard_map/ppermute | solution.py:16
  116.1 3.9 %collective-permute-start.29 = (bf16[2,128,1280]{2,1,0:T(8,128)(2,1)S(1)}, bf16[2,128,1280]{2,1,0:T(8,128)(2,1)S(1)}, u32[]{:S(2)}, u32[]{:S(2)}) collective-permute-start(bf16[2,128,1280]{2,1,0:T(8,128)(2,1)S(1)} %get-tuple-element.41), channel_id=1, source_target_pairs={{0,4},{1,5},{2,6},{3,7},{4,8},{5,9},{6,10},{7,11},{8,12},{9,13},{1... | collective-permute-start | bytes 1966088 | tf_op jit(solution)/shard_map/ppermute | solution.py:16
  119.9 0.0 collective-permute-done.22
  120.0 1.5 %collective-permute-done.23 = bf16[2,128,1280]{2,1,0:T(8,128)(2,1)S(1)} collective-permute-done((bf16[2,128,1280]{2,1,0:T(8,128)(2,1)S(1)}, bf16[2,128,1280]{2,1,0:T(8,128)(2,1)S(1)}, u32[]{:S(2)}, u32[]{:S(2)}) %collective-permute-start.23) | collective-permute-done | bytes 655392 | tf_op jit(solution)/shard_map/ppermute | solution.py:16
  121.4 0.4 fusion.17
  121.9 7.8 %collective-permute-done.27 = bf16[2,128,1280]{2,1,0:T(8,128)(2,1)S(1)} collective-permute-done((bf16[2,128,1280]{2,1,0:T(8,128)(2,1)S(1)}, bf16[2,128,1280]{2,1,0:T(8,128)(2,1)S(1)}, u32[]{:S(2)}, u32[]{:S(2)}) %collective-permute-start.27) | collective-permute-done | bytes 655392 | tf_op jit(solution)/shard_map/ppermute | solution.py:16
  129.7 1.9 %collective-permute-done.28 = bf16[2,128,1280]{2,1,0:T(8,128)(2,1)S(1)} collective-permute-done((bf16[2,128,1280]{2,1,0:T(8,128)(2,1)S(1)}, bf16[2,128,1280]{2,1,0:T(8,128)(2,1)S(1)}, u32[]{:S(2)}, u32[]{:S(2)}) %collective-permute-start.28) | collective-permute-done | bytes 655392 | tf_op jit(solution)/shard_map/ppermute | solution.py:16
  131.6 2.2 %collective-permute-done.29 = bf16[2,128,1280]{2,1,0:T(8,128)(2,1)S(1)} collective-permute-done((bf16[2,128,1280]{2,1,0:T(8,128)(2,1)S(1)}, bf16[2,128,1280]{2,1,0:T(8,128)(2,1)S(1)}, u32[]{:S(2)}, u32[]{:S(2)}) %collective-permute-start.29) | collective-permute-done | bytes 655392 | tf_op jit(solution)/shard_map/ppermute | solution.py:16
  133.9 0.4 fusion.8
  134.3 0.9 pad_maximum_fusion.4
  135.2 0.9 pad_maximum_fusion.3
  (67 shorter events, 0.3 us)
Async XLA Ops:
  0.6 11.1 %copy-start = (s32[4,3]{1,0:T(4,128)S(1)}, s32[4,3]{1,0:T(4,128)}, u32[]{:S(2)}) copy-start(s32[4,3]{1,0:T(4,128)} %param.10) | copy-start | bytes 148
  2.0 9.8 %copy-start.18 = (s32[4]{0:T(128)S(1)}, s32[4]{0:T(128)}, u32[]{:S(2)}) copy-start(s32[4]{0:T(128)} %param.11) | copy-start | bytes 52
  2.1 50.9 %copy-start.8 = (bf16[2,128,1280]{2,1,0:T(8,128)(2,1)}, bf16[2,128,1280]{2,1,0:T(8,128)(2,1)S(1)}, u32[]{:S(2)}) copy-start(bf16[2,128,1280]{2,1,0:T(8,128)(2,1)S(1)} %pad_maximum_fusion.refs_0_) | copy-start | bytes 1966084
  2.1 18.6 %collective-permute-start = (bf16[2,128,1280]{2,1,0:T(8,128)(2,1)S(1)}, bf16[2,128,1280]{2,1,0:T(8,128)(2,1)S(1)}, u32[]{:S(2)}, u32[]{:S(2)}) collective-permute-start(bf16[2,128,1280]{2,1,0:T(8,128)(2,1)S(1)} %pad_maximum_fusion.refs_0_), channel_id=1, source_target_pairs={{0,2},{1,3},{2,0},{3,1},{4,6},{5,7},{6,4},{7,5},{8,10},{9,11},{10,... | collective-permute-start | bytes 1966088 | tf_op jit(solution)/shard_map/ppermute | solution.py:16
  5.2 20.4 %collective-permute-start.1 = (bf16[2,128,1280]{2,1,0:T(8,128)(2,1)S(1)}, bf16[2,128,1280]{2,1,0:T(8,128)(2,1)}, u32[]{:S(2)}, u32[]{:S(2)}) collective-permute-start(bf16[2,128,1280]{2,1,0:T(8,128)(2,1)S(1)} %pad_maximum_fusion.refs_0_), channel_id=1, source_target_pairs={{0,4},{1,5},{2,6},{3,7},{4,8},{5,9},{6,10},{7,11},{8,12},{9,13},{1... | collective-permute-start | bytes 1966088 | tf_op jit(solution)/shard_map/ppermute | solution.py:16
  9.5 17.9 %collective-permute-start.2 = (bf16[2,128,1280]{2,1,0:T(8,128)(2,1)S(1)}, bf16[2,128,1280]{2,1,0:T(8,128)(2,1)}, u32[]{:S(2)}, u32[]{:S(2)}) collective-permute-start(bf16[2,128,1280]{2,1,0:T(8,128)(2,1)S(1)} %pad_maximum_fusion.refs_0_), channel_id=1, source_target_pairs={{4,0},{5,1},{6,2},{7,3},{8,4},{9,5},{10,6},{11,7},{12,8},{13,9},{1... | collective-permute-start | bytes 1966088 | tf_op jit(solution)/shard_map/ppermute | solution.py:16
  10.8 16.6 %collective-permute-start.3 = (bf16[2,128,1280]{2,1,0:T(8,128)(2,1)S(1)}, bf16[2,128,1280]{2,1,0:T(8,128)(2,1)}, u32[]{:S(2)}, u32[]{:S(2)}) collective-permute-start(bf16[2,128,1280]{2,1,0:T(8,128)(2,1)S(1)} %pad_maximum_fusion.refs_0_), channel_id=1, source_target_pairs={{0,1},{1,0},{2,3},{3,2},{4,5},{5,4},{6,7},{7,6},{8,9},{9,8},{10,11... | collective-permute-start | bytes 1966088 | tf_op jit(solution)/shard_map/ppermute | solution.py:16
  10.9 56.0 %copy-start.7 = (bf16[2,128,1280]{2,1,0:T(8,128)(2,1)}, bf16[2,128,1280]{2,1,0:T(8,128)(2,1)S(1)}, u32[]{:S(2)}) copy-start(bf16[2,128,1280]{2,1,0:T(8,128)(2,1)S(1)} %pad_maximum_fusion.1.refs_0_) | copy-start | bytes 1966084
  10.9 23.0 %collective-permute-start.9 = (bf16[2,128,1280]{2,1,0:T(8,128)(2,1)S(1)}, bf16[2,128,1280]{2,1,0:T(8,128)(2,1)S(1)}, u32[]{:S(2)}, u32[]{:S(2)}) collective-permute-start(bf16[2,128,1280]{2,1,0:T(8,128)(2,1)S(1)} %pad_maximum_fusion.1.refs_0_), channel_id=1, source_target_pairs={{0,2},{1,3},{2,0},{3,1},{4,6},{5,7},{6,4},{7,5},{8,10},{9,11},{10,... | collective-permute-start | bytes 1966088 | tf_op jit(solution)/shard_map/ppermute | solution.py:16
  20.7 32.3 %copy-start.12 = (bf16[2,128,1280]{2,1,0:T(8,128)(2,1)}, bf16[2,128,1280]{2,1,0:T(8,128)(2,1)S(1)}, u32[]{:S(2)}) copy-start(bf16[2,128,1280]{2,1,0:T(8,128)(2,1)S(1)} %collective-permute-done.refs_1_) | copy-start | bytes 1966084
  20.8 16.1 %collective-permute-start.10 = (bf16[2,128,1280]{2,1,0:T(8,128)(2,1)S(1)}, bf16[2,128,1280]{2,1,0:T(8,128)(2,1)}, u32[]{:S(2)}, u32[]{:S(2)}) collective-permute-start(bf16[2,128,1280]{2,1,0:T(8,128)(2,1)S(1)} %pad_maximum_fusion.1.refs_0_), channel_id=1, source_target_pairs={{0,4},{1,5},{2,6},{3,7},{4,8},{5,9},{6,10},{7,11},{8,12},{9,13},{1... | collective-permute-start | bytes 1966088 | tf_op jit(solution)/shard_map/ppermute | solution.py:16
  25.6 16.3 %collective-permute-start.11 = (bf16[2,128,1280]{2,1,0:T(8,128)(2,1)S(1)}, bf16[2,128,1280]{2,1,0:T(8,128)(2,1)}, u32[]{:S(2)}, u32[]{:S(2)}) collective-permute-start(bf16[2,128,1280]{2,1,0:T(8,128)(2,1)S(1)} %pad_maximum_fusion.1.refs_0_), channel_id=1, source_target_pairs={{4,0},{5,1},{6,2},{7,3},{8,4},{9,5},{10,6},{11,7},{12,8},{13,9},{1... | collective-permute-start | bytes 1966088 | tf_op jit(solution)/shard_map/ppermute | solution.py:16
  27.4 14.5 %collective-permute-start.12 = (bf16[2,128,1280]{2,1,0:T(8,128)(2,1)S(1)}, bf16[2,128,1280]{2,1,0:T(8,128)(2,1)S(1)}, u32[]{:S(2)}, u32[]{:S(2)}) collective-permute-start(bf16[2,128,1280]{2,1,0:T(8,128)(2,1)S(1)} %pad_maximum_fusion.1.refs_0_), channel_id=1, source_target_pairs={{0,1},{1,0},{2,3},{3,2},{4,5},{5,4},{6,7},{7,6},{8,9},{9,8},{10,11... | collective-permute-start | bytes 1966088 | tf_op jit(solution)/shard_map/ppermute | solution.py:16
  27.4 16.9 %collective-permute-start.4 = (bf16[2,128,1280]{2,1,0:T(8,128)(2,1)S(1)}, bf16[2,128,1280]{2,1,0:T(8,128)(2,1)S(1)}, u32[]{:S(2)}, u32[]{:S(2)}) collective-permute-start(bf16[2,128,1280]{2,1,0:T(8,128)(2,1)S(1)} %collective-permute-done.refs_1_), channel_id=1, source_target_pairs={{0,1},{1,0},{2,3},{3,2},{4,5},{5,4},{6,7},{7,6},{8,9},{9,8},{10,11... | collective-permute-start | bytes 1966088 | tf_op jit(solution)/shard_map/ppermute | solution.py:16
  33.9 33.0 %copy-start.11 = (bf16[2,128,1280]{2,1,0:T(8,128)(2,1)}, bf16[2,128,1280]{2,1,0:T(8,128)(2,1)S(1)}, u32[]{:S(2)}) copy-start(bf16[2,128,1280]{2,1,0:T(8,128)(2,1)S(1)} %collective-permute-done.9.refs_1_) | copy-start | bytes 1966084
  33.9 13.0 %collective-permute-start.7 = (bf16[2,128,1280]{2,1,0:T(8,128)(2,1)S(1)}, bf16[2,128,1280]{2,1,0:T(8,128)(2,1)S(1)}, u32[]{:S(2)}, u32[]{:S(2)}) collective-permute-start(bf16[2,128,1280]{2,1,0:T(8,128)(2,1)S(1)} %collective-permute-done.refs_1_), channel_id=1, source_target_pairs={{0,5},{3,6},{4,9},{7,10},{8,13},{11,14},{16,21},{19,22},{20,25},{2... | collective-permute-start | bytes 1966088 | tf_op jit(solution)/shard_map/ppermute | solution.py:16
  36.8 13.3 %collective-permute-start.8 = (bf16[2,128,1280]{2,1,0:T(8,128)(2,1)S(1)}, bf16[2,128,1280]{2,1,0:T(8,128)(2,1)S(1)}, u32[]{:S(2)}, u32[]{:S(2)}) collective-permute-start(bf16[2,128,1280]{2,1,0:T(8,128)(2,1)S(1)} %collective-permute-done.refs_1_), channel_id=1, source_target_pairs={{4,1},{7,2},{8,5},{11,6},{12,9},{15,10},{20,17},{23,18},{24,21},{2... | collective-permute-start | bytes 1966088 | tf_op jit(solution)/shard_map/ppermute | solution.py:16
  41.9 9.8 %collective-permute-start.5 = (bf16[2,128,1280]{2,1,0:T(8,128)(2,1)}, bf16[2,128,1280]{2,1,0:T(8,128)(2,1)S(1)}, u32[]{:S(2)}, u32[]{:S(2)}) collective-permute-start(bf16[2,128,1280]{2,1,0:T(8,128)(2,1)} %collective-permute-done.1.refs_2_), channel_id=1, source_target_pairs={{0,1},{1,0},{2,3},{3,2},{4,5},{5,4},{6,7},{7,6},{8,9},{9,8},{10,11... | collective-permute-start | bytes 1966088 | tf_op jit(solution)/shard_map/ppermute | solution.py:16
  41.9 2.5 %copy-start.13 = (bf16[2,128,1280]{2,1,0:T(8,128)(2,1)}, bf16[2,128,1280]{2,1,0:T(8,128)(2,1)S(1)}, u32[]{:S(2)}) copy-start(bf16[2,128,1280]{2,1,0:T(8,128)(2,1)S(1)} %collective-permute-done.12.refs_4_) | copy-start | bytes 1966084
  41.9 10.6 %collective-permute-start.6 = (bf16[2,128,1280]{2,1,0:T(8,128)(2,1)}, bf16[2,128,1280]{2,1,0:T(8,128)(2,1)}, u32[]{:S(2)}, u32[]{:S(2)}) collective-permute-start(bf16[2,128,1280]{2,1,0:T(8,128)(2,1)} %collective-permute-done.2.refs_3_), channel_id=1, source_target_pairs={{0,1},{1,0},{2,3},{3,2},{4,5},{5,4},{6,7},{7,6},{8,9},{9,8},{10,11... | collective-permute-start | bytes 1966088 | tf_op jit(solution)/shard_map/ppermute | solution.py:16
  44.4 0.8 copy-start.14
  44.4 22.6 %collective-permute-start.13 = (bf16[2,128,1280]{2,1,0:T(8,128)(2,1)S(1)}, bf16[2,128,1280]{2,1,0:T(8,128)(2,1)}, u32[]{:S(2)}, u32[]{:S(2)}) collective-permute-start(bf16[2,128,1280]{2,1,0:T(8,128)(2,1)S(1)} %collective-permute-done.9.refs_1_), channel_id=1, source_target_pairs={{0,1},{1,0},{2,3},{3,2},{4,5},{5,4},{6,7},{7,6},{8,9},{9,8},{10,11... | collective-permute-start | bytes 1966088 | tf_op jit(solution)/shard_map/ppermute | solution.py:16
  46.9 3.2 %copy-start.15 = (bf16[2,128,1280]{2,1,0:T(8,128)(2,1)}, bf16[2,128,1280]{2,1,0:T(8,128)(2,1)S(1)}, u32[]{:S(2)}) copy-start(bf16[2,128,1280]{2,1,0:T(8,128)(2,1)S(1)} %collective-permute-done.7.refs_8_) | copy-start | bytes 1966084
  46.9 20.2 %collective-permute-start.16 = (bf16[2,128,1280]{2,1,0:T(8,128)(2,1)S(1)}, bf16[2,128,1280]{2,1,0:T(8,128)(2,1)}, u32[]{:S(2)}, u32[]{:S(2)}) collective-permute-start(bf16[2,128,1280]{2,1,0:T(8,128)(2,1)S(1)} %collective-permute-done.9.refs_1_), channel_id=1, source_target_pairs={{0,5},{3,6},{4,9},{7,10},{8,13},{11,14},{16,21},{19,22},{20,25},{2... | collective-permute-start | bytes 1966088 | tf_op jit(solution)/shard_map/ppermute | solution.py:16
  50.1 1.5 %copy-start.16 = (bf16[2,128,1280]{2,1,0:T(8,128)(2,1)}, bf16[2,128,1280]{2,1,0:T(8,128)(2,1)S(1)}, u32[]{:S(2)}) copy-start(bf16[2,128,1280]{2,1,0:T(8,128)(2,1)S(1)} %collective-permute-done.8.refs_9_) | copy-start | bytes 1966084
  50.1 17.0 %collective-permute-start.17 = (bf16[2,128,1280]{2,1,0:T(8,128)(2,1)S(1)}, bf16[2,128,1280]{2,1,0:T(8,128)(2,1)}, u32[]{:S(2)}, u32[]{:S(2)}) collective-permute-start(bf16[2,128,1280]{2,1,0:T(8,128)(2,1)S(1)} %collective-permute-done.9.refs_1_), channel_id=1, source_target_pairs={{4,1},{7,2},{8,5},{11,6},{12,9},{15,10},{20,17},{23,18},{24,21},{2... | collective-permute-start | bytes 1966088 | tf_op jit(solution)/shard_map/ppermute | solution.py:16
  51.6 0.8 copy-start.17
  52.5 14.6 %collective-permute-start.14 = (bf16[2,128,1280]{2,1,0:T(8,128)(2,1)}, bf16[2,128,1280]{2,1,0:T(8,128)(2,1)}, u32[]{:S(2)}, u32[]{:S(2)}) collective-permute-start(bf16[2,128,1280]{2,1,0:T(8,128)(2,1)} %collective-permute-done.10.refs_2_), channel_id=1, source_target_pairs={{0,1},{1,0},{2,3},{3,2},{4,5},{5,4},{6,7},{7,6},{8,9},{9,8},{10,11... | collective-permute-start | bytes 1966088 | tf_op jit(solution)/shard_map/ppermute | solution.py:16
  52.5 14.6 %collective-permute-start.15 = (bf16[2,128,1280]{2,1,0:T(8,128)(2,1)}, bf16[2,128,1280]{2,1,0:T(8,128)(2,1)}, u32[]{:S(2)}, u32[]{:S(2)}) collective-permute-start(bf16[2,128,1280]{2,1,0:T(8,128)(2,1)} %collective-permute-done.11.refs_3_), channel_id=1, source_target_pairs={{0,1},{1,0},{2,3},{3,2},{4,5},{5,4},{6,7},{7,6},{8,9},{9,8},{10,11... | collective-permute-start | bytes 1966088 | tf_op jit(solution)/shard_map/ppermute | solution.py:16
  67.0 27.7 %collective-permute-start.18 = (bf16[4,2,128,1280]{3,2,1,0:T(8,128)(2,1)}, bf16[4,2,128,1280]{3,2,1,0:T(8,128)(2,1)S(1)}, u32[]{:S(2)}, u32[]{:S(2)}) collective-permute-start(bf16[4,2,128,1280]{3,2,1,0:T(8,128)(2,1)} %get-tuple-element.22), channel_id=1, source_target_pairs={{0,1},{1,0},{2,3},{3,2},{4,5},{5,4},{6,7},{7,6},{8,9},{9,8},{10,11... | collective-permute-start | bytes 7864328 | tf_op jit(solution)/shard_map/ppermute | solution.py:16
  67.1 27.6 %copy-start.3 = (bf16[2,128,1280]{2,1,0:T(8,128)(2,1)S(1)}, bf16[2,128,1280]{2,1,0:T(8,128)(2,1)}, u32[]{:S(2)}) copy-start(bf16[2,128,1280]{2,1,0:T(8,128)(2,1)} %get-tuple-element.27) | copy-start | bytes 1966084
  81.3 13.4 %copy-start.1 = (bf16[2,128,1280]{2,1,0:T(8,128)(2,1)S(1)}, bf16[2,128,1280]{2,1,0:T(8,128)(2,1)}, u32[]{:S(2)}) copy-start(bf16[2,128,1280]{2,1,0:T(8,128)(2,1)} %get-tuple-element.23) | copy-start | bytes 1966084
  81.3 13.4 %copy-start.2 = (bf16[2,128,1280]{2,1,0:T(8,128)(2,1)S(1)}, bf16[2,128,1280]{2,1,0:T(8,128)(2,1)}, u32[]{:S(2)}) copy-start(bf16[2,128,1280]{2,1,0:T(8,128)(2,1)} %get-tuple-element.26) | copy-start | bytes 1966084
  81.3 25.1 %collective-permute-start.24 = (bf16[4,2,128,1280]{3,2,1,0:T(8,128)(2,1)}, bf16[4,2,128,1280]{3,2,1,0:T(8,128)(2,1)S(1)}, u32[]{:S(2)}, u32[]{:S(2)}) collective-permute-start(bf16[4,2,128,1280]{3,2,1,0:T(8,128)(2,1)} %get-tuple-element.29), channel_id=1, source_target_pairs={{0,1},{1,0},{2,3},{3,2},{4,5},{5,4},{6,7},{7,6},{8,9},{9,8},{10,11... | collective-permute-start | bytes 7864328 | tf_op jit(solution)/shard_map/ppermute | solution.py:16
  81.8 12.1 %collective-permute-start.19 = (bf16[2,128,1280]{2,1,0:T(8,128)(2,1)}, bf16[2,128,1280]{2,1,0:T(8,128)(2,1)S(1)}, u32[]{:S(2)}, u32[]{:S(2)}) collective-permute-start(bf16[2,128,1280]{2,1,0:T(8,128)(2,1)} %get-tuple-element.24), channel_id=1, source_target_pairs={{5,0},{6,3},{9,4},{10,7},{13,8},{14,11},{21,16},{22,19},{25,20},{2... | collective-permute-start | bytes 1966088 | tf_op jit(solution)/shard_map/ppermute | solution.py:16
  83.1 11.5 %collective-permute-start.20 = (bf16[2,128,1280]{2,1,0:T(8,128)(2,1)}, bf16[2,128,1280]{2,1,0:T(8,128)(2,1)S(1)}, u32[]{:S(2)}, u32[]{:S(2)}) collective-permute-start(bf16[2,128,1280]{2,1,0:T(8,128)(2,1)} %get-tuple-element.25), channel_id=1, source_target_pairs={{1,4},{2,7},{5,8},{6,11},{9,12},{10,15},{17,20},{18,23},{21,24},{2... | collective-permute-start | bytes 1966088 | tf_op jit(solution)/shard_map/ppermute | solution.py:16
  83.8 17.9 %collective-permute-start.25 = (bf16[2,128,1280]{2,1,0:T(8,128)(2,1)}, bf16[2,128,1280]{2,1,0:T(8,128)(2,1)S(1)}, u32[]{:S(2)}, u32[]{:S(2)}) collective-permute-start(bf16[2,128,1280]{2,1,0:T(8,128)(2,1)} %get-tuple-element.31), channel_id=1, source_target_pairs={{5,0},{6,3},{9,4},{10,7},{13,8},{14,11},{21,16},{22,19},{25,20},{2... | collective-permute-start | bytes 1966088 | tf_op jit(solution)/shard_map/ppermute | solution.py:16
  93.9 12.4 %collective-permute-start.26 = (bf16[2,128,1280]{2,1,0:T(8,128)(2,1)}, bf16[2,128,1280]{2,1,0:T(8,128)(2,1)S(1)}, u32[]{:S(2)}, u32[]{:S(2)}) collective-permute-start(bf16[2,128,1280]{2,1,0:T(8,128)(2,1)} %get-tuple-element.32), channel_id=1, source_target_pairs={{1,4},{2,7},{5,8},{6,11},{9,12},{10,15},{17,20},{18,23},{21,24},{2... | collective-permute-start | bytes 1966088 | tf_op jit(solution)/shard_map/ppermute | solution.py:16
  94.7 11.7 %copy-start.4 = (bf16[2,128,1280]{2,1,0:T(8,128)(2,1)S(1)}, bf16[2,128,1280]{2,1,0:T(8,128)(2,1)}, u32[]{:S(2)}) copy-start(bf16[2,128,1280]{2,1,0:T(8,128)(2,1)} %get-tuple-element.30) | copy-start | bytes 1966084
  94.7 11.7 %copy-start.5 = (bf16[2,128,1280]{2,1,0:T(8,128)(2,1)S(1)}, bf16[2,128,1280]{2,1,0:T(8,128)(2,1)}, u32[]{:S(2)}) copy-start(bf16[2,128,1280]{2,1,0:T(8,128)(2,1)} %get-tuple-element.33) | copy-start | bytes 1966084
  94.7 11.7 %copy-start.6 = (bf16[2,128,1280]{2,1,0:T(8,128)(2,1)S(1)}, bf16[2,128,1280]{2,1,0:T(8,128)(2,1)}, u32[]{:S(2)}) copy-start(bf16[2,128,1280]{2,1,0:T(8,128)(2,1)} %get-tuple-element.34) | copy-start | bytes 1966084
  95.4 20.7 %collective-permute-start.21 = (bf16[2,128,1280]{2,1,0:T(8,128)(2,1)S(1)}, bf16[2,128,1280]{2,1,0:T(8,128)(2,1)S(1)}, u32[]{:S(2)}, u32[]{:S(2)}) collective-permute-start(bf16[2,128,1280]{2,1,0:T(8,128)(2,1)S(1)} %get-tuple-element.37), channel_id=1, source_target_pairs={{0,2},{1,3},{2,0},{3,1},{4,6},{5,7},{6,4},{7,5},{8,10},{9,11},{10,... | collective-permute-start | bytes 1966088 | tf_op jit(solution)/shard_map/ppermute | solution.py:16
  100.5 19.5 %collective-permute-start.22 = (bf16[2,128,1280]{2,1,0:T(8,128)(2,1)S(1)}, bf16[2,128,1280]{2,1,0:T(8,128)(2,1)S(1)}, u32[]{:S(2)}, u32[]{:S(2)}) collective-permute-start(bf16[2,128,1280]{2,1,0:T(8,128)(2,1)S(1)} %get-tuple-element.39), channel_id=1, source_target_pairs={{4,0},{5,1},{6,2},{7,3},{8,4},{9,5},{10,6},{11,7},{12,8},{13,9},{1... | collective-permute-start | bytes 1966088 | tf_op jit(solution)/shard_map/ppermute | solution.py:16
  101.8 19.7 %collective-permute-start.23 = (bf16[2,128,1280]{2,1,0:T(8,128)(2,1)S(1)}, bf16[2,128,1280]{2,1,0:T(8,128)(2,1)S(1)}, u32[]{:S(2)}, u32[]{:S(2)}) collective-permute-start(bf16[2,128,1280]{2,1,0:T(8,128)(2,1)S(1)} %get-tuple-element.38), channel_id=1, source_target_pairs={{0,4},{1,5},{2,6},{3,7},{4,8},{5,9},{6,10},{7,11},{8,12},{9,13},{1... | collective-permute-start | bytes 1966088 | tf_op jit(solution)/shard_map/ppermute | solution.py:16
  106.4 15.0 %copy-start.9 = (bf16[2,128,1280]{2,1,0:T(8,128)(2,1)S(1)}, bf16[2,128,1280]{2,1,0:T(8,128)(2,1)}, u32[]{:S(2)}) copy-start(bf16[2,128,1280]{2,1,0:T(8,128)(2,1)} %get-tuple-element.21) | copy-start | bytes 1966084
  107.1 22.6 %collective-permute-start.27 = (bf16[2,128,1280]{2,1,0:T(8,128)(2,1)S(1)}, bf16[2,128,1280]{2,1,0:T(8,128)(2,1)S(1)}, u32[]{:S(2)}, u32[]{:S(2)}) collective-permute-start(bf16[2,128,1280]{2,1,0:T(8,128)(2,1)S(1)} %get-tuple-element.40), channel_id=1, source_target_pairs={{0,2},{1,3},{2,0},{3,1},{4,6},{5,7},{6,4},{7,5},{8,10},{9,11},{10,... | collective-permute-start | bytes 1966088 | tf_op jit(solution)/shard_map/ppermute | solution.py:16
  109.6 22.1 %collective-permute-start.28 = (bf16[2,128,1280]{2,1,0:T(8,128)(2,1)S(1)}, bf16[2,128,1280]{2,1,0:T(8,128)(2,1)S(1)}, u32[]{:S(2)}, u32[]{:S(2)}) collective-permute-start(bf16[2,128,1280]{2,1,0:T(8,128)(2,1)S(1)} %get-tuple-element.42), channel_id=1, source_target_pairs={{4,0},{5,1},{6,2},{7,3},{8,4},{9,5},{10,6},{11,7},{12,8},{13,9},{1... | collective-permute-start | bytes 1966088 | tf_op jit(solution)/shard_map/ppermute | solution.py:16
  116.1 17.8 %collective-permute-start.29 = (bf16[2,128,1280]{2,1,0:T(8,128)(2,1)S(1)}, bf16[2,128,1280]{2,1,0:T(8,128)(2,1)S(1)}, u32[]{:S(2)}, u32[]{:S(2)}) collective-permute-start(bf16[2,128,1280]{2,1,0:T(8,128)(2,1)S(1)} %get-tuple-element.41), channel_id=1, source_target_pairs={{0,4},{1,5},{2,6},{3,7},{4,8},{5,9},{6,10},{7,11},{8,12},{9,13},{1... | collective-permute-start | bytes 1966088 | tf_op jit(solution)/shard_map/ppermute | solution.py:16
  121.8 12.0 %copy-start.10 = (bf16[2,128,1280]{2,1,0:T(8,128)(2,1)S(1)}, bf16[2,128,1280]{2,1,0:T(8,128)(2,1)}, u32[]{:S(2)}) copy-start(bf16[2,128,1280]{2,1,0:T(8,128)(2,1)} %get-tuple-element.28) | copy-start | bytes 1966084
